TPU v7x, 128 devices: a whole 4x4x4 slice. The times are simulated.
128 devices in a mesh: box: 16 (over x, z_hi, core), group: 8 (over y, z_lo).
Axes of the slice: x: 4, y: 4, z: 4 (z_hi: 2, z_lo: 2; z = z_hi * 2 + z_lo), core: 2. Of those that a mesh axis runs over, the one named last changes fastest.
Arguments:
- right_side: float32 [256, 256, 512], P('box', 'group'), may hold values from -6 to 6
- inv_density: float32 [256, 256, 512], P('box', 'group'), may hold values from 0.2 to 5
- pressure: float32 [256, 256, 512], P('box', 'group'), may hold values from -6 to 6
Outputs:
- corrected: float32 [256, 256, 512], P('box', 'group')
All inputs are finite; a program needn't handle non-finite values.
Results may differ from a plain program's by a relative error of at most 0.0003.
Values sent between devices are 32-bit elements; how exact they have to be, the bound alone decides.
No kernel may reach another device: no remote copies, remote signals or barrier semaphores. Data moves between devices by JAX's collectives and lax.ppermute only.
A program may use at most 128 MiB of HBM per device.

v0:
```python
import jax
import jax.numpy as jnp
from jax import lax
from jax.sharding import PartitionSpec as P

SWEEPS = 2
CHEB = 8


def extended(block, sides, width):
    for axis, dim in sides:
        count = lax.axis_size(axis)
        forward = [(i, i + 1) for i in range(count - 1)]
        backward = [(target, source) for source, target in forward]
        low = lax.ppermute(
            lax.slice_in_dim(block, block.shape[dim] - width, None, axis=dim), axis, forward
        )
        high = lax.ppermute(lax.slice_in_dim(block, 0, width, axis=dim), axis, backward)
        block = jnp.concatenate([low, block, high], axis=dim)
    return block


def neighbours(padded):
    return [
        padded[:-2, 1:-1, 1:-1],
        padded[2:, 1:-1, 1:-1],
        padded[1:-1, :-2, 1:-1],
        padded[1:-1, 2:, 1:-1],
        padded[1:-1, 1:-1, :-2],
        padded[1:-1, 1:-1, 2:],
    ]


def face_coefs(field, padded):
    return [
        jnp.where(near > 0, 2.0 * field * near / (field + near), field)
        for near in neighbours(padded)
    ]


def stencil(field, padded, coefs):
    total = jnp.zeros_like(field)
    for coef, near in zip(coefs, neighbours(padded)):
        total = total + coef * (field - near)
    return total


def block_mean(field):
    sx, sy, sz = field.shape
    return field.reshape(sx // 4, 4, sy // 4, 4, sz // 4, 4).mean(axis=(1, 3, 5))


def chebyshev(rhs_c, coefs, diag, padder):
    low, high = (0.05, 2.0)
    theta = (high + low) / 2.0
    delta = (high - low) / 2.0
    sigma = theta / delta
    rho = 1.0 / sigma
    solution = jnp.zeros_like(rhs_c)
    remain = rhs_c
    direction = remain / (diag * theta)
    for step in range(CHEB):
        solution = solution + direction
        if step + 1 < CHEB:
            remain = remain - stencil(direction, padder(direction), coefs)
            rho_next = 1.0 / (2.0 * sigma - rho)
            direction = rho_next * rho * direction + 2.0 * rho_next / delta * remain / diag
            rho = rho_next
    return solution


def depth_pad(field):
    return jnp.pad(field, ((0, 0), (0, 0), (1, 1)))


def pressure_pad(field):
    return depth_pad(extended(field, (("box", 0), ("group", 1)), 1))


def direction_pad(field):
    return depth_pad(extended(field, (("box", 0), ("group", 1)), 1))


def per_device(right_side, inv_density, pressure):
    density_padded = depth_pad(extended(inv_density, (("box", 0), ("group", 1)), 1))
    coefs = face_coefs(inv_density, density_padded)
    diag = sum(coefs)
    fine = pressure
    for sweep in range(SWEEPS):
        fine = fine + 2.0 / 3.0 * (right_side - stencil(fine, pressure_pad(fine), coefs)) / diag
    res = right_side - stencil(fine, pressure_pad(fine), coefs)
    coarse_rhs = block_mean(res)
    coarse_b = block_mean(inv_density)
    coarse_padded = depth_pad(extended(coarse_b, (("box", 0), ("group", 1)), 1))
    coarse_coefs = [c * 0.0625 for c in face_coefs(coarse_b, coarse_padded)]
    corr = chebyshev(coarse_rhs, coarse_coefs, sum(coarse_coefs), direction_pad)
    expanded = jnp.repeat(jnp.repeat(jnp.repeat(corr, 4, axis=0), 4, axis=1), 4, axis=2)
    return fine + expanded


def solution(mesh):
    return jax.shard_map(
        per_device,
        mesh=mesh,
        in_specs=(P("box", "group", None), P("box", "group", None), P("box", "group", None)),
        out_specs=P("box", "group", None),
        check_vma=False,
    )
```

profile of v0, /device:TPU:34, one launch (start us, length us, event | category | flops | bytes accessed | tf_op | source)
XLA Modules:
  0.0 328.5 jit_solution(14946584273614158975)
XLA Ops:
  3.7 6.0 %collective-permute-start.3 = (f32[1,32,512]{2,1,0:T(8,128)S(1)}, f32[1,32,512]{2,1,0:T(8,128)S(1)}, u32[]{:S(2)}, u32[]{:S(2)}) collective-permute-start(f32[1,32,512]{2,1,0:T(8,128)S(1)} %get-tuple-element.40), channel_id=1, source_target_pairs={{8,0},{16,8},{24,16},{32,24},{40,32},{48,40},{56,48},{64,56},{72,6... | collective-permute-start | bytes 196616 | tf_op jit(solution)/shard_map/ppermute | solution.py:18
  11.7 6.0 %collective-permute-start.2 = (f32[1,32,512]{2,1,0:T(8,128)S(1)}, f32[1,32,512]{2,1,0:T(8,128)S(1)}, u32[]{:S(2)}, u32[]{:S(2)}) collective-permute-start(f32[1,32,512]{2,1,0:T(8,128)S(1)} %get-tuple-element.38), channel_id=1, source_target_pairs={{8,0},{16,8},{24,16},{32,24},{40,32},{48,40},{56,48},{64,56},{72,6... | collective-permute-start | bytes 196616 | tf_op jit(solution)/shard_map/ppermute | solution.py:18
  17.7 36.8 %reshape.16 = f32[4,4,8,4,128,4]{5,4,3,2,1,0:T(8,128)} reshape(f32[16,32,512]{2,1,0:T(8,128)} %param.4) | data formatting | bytes 2097152 | tf_op jit(solution)/shard_map/reshape | solution.py:50
  54.5 12.3 %reduce_sum.19 = f32[4,8,128]{2,1,0:T(8,128)S(1)} reduce(f32[4,4,8,4,128,4]{5,4,3,2,1,0:T(8,128)} %reshape.16, f32[]{:T(128)} %constant.21.clone.1), dimensions={1,3,5}, to_apply=%region_1.2 | reduce | flops 258048 | bytes 1064964 | tf_op jit(solution)/shard_map/reduce_sum | solution.py:50
  67.0 3.2 collective-permute-start.4
  70.2 2.8 collective-permute-start.6
  73.2 3.9 %collective-permute-start.5 = (f32[18,1,512]{2,1,0:T(1,128)S(1)}, f32[18,1,512]{2,1,0:T(1,128)S(1)}, u32[]{:S(2)}, u32[]{:S(2)}) collective-permute-start(f32[18,1,512]{2,1,0:T(1,128)S(1)} %get-tuple-element.32), channel_id=1, source_target_pairs={{0,1},{1,2},{2,3},{3,4},{4,5},{5,6},{6,7},{8,9},{9,10},{10,11},{11... | collective-permute-start | bytes 110600 | tf_op jit(solution)/shard_map/ppermute | solution.py:15
  80.0 3.9 %collective-permute-done.7 = f32[18,1,512]{2,1,0:T(1,128)S(1)} collective-permute-done((f32[18,1,512]{2,1,0:T(1,128)S(1)}, f32[18,1,512]{2,1,0:T(1,128)S(1)}, u32[]{:S(2)}, u32[]{:S(2)}) %collective-permute-start.7) | collective-permute-done | bytes 36896 | tf_op jit(solution)/shard_map/ppermute | solution.py:18
  84.8 4.6 %fusion.41 = (f32[16,32,512]{2,1,0:T(8,128)S(1)}, f32[16,32,512]{2,1,0:T(8,128)S(1)}, f32[16,32,512]{2,1,0:T(8,128)S(1)}) fusion(f32[16,32,512]{2,1,0:T(8,128)S(1)} %copy-done.2, f32[16,32,512]{2,1,0:T(8,128)S(1)} %copy-done.1, f32[18,34,514]{2,1,0:T(8,128)S(1)} %select_maximum_fusion.8, f32[18,1,512]{2,1,0:T(1,128)S(1)} %collective-permute-done.7, ...), kind=kLoop, calls=%fused_computation.76 | loop fusion | flops 17039360 | bytes 13254656 | tf_op jit(solution)/shard_map/add | solution.py:90
  91.3 6.0 %collective-permute-start.9 = (f32[1,32,512]{2,1,0:T(8,128)S(1)}, f32[1,32,512]{2,1,0:T(8,128)S(1)}, u32[]{:S(2)}, u32[]{:S(2)}) collective-permute-start(f32[1,32,512]{2,1,0:T(8,128)S(1)} %get-tuple-element.37), channel_id=1, source_target_pairs={{8,0},{16,8},{24,16},{32,24},{40,32},{48,40},{56,48},{64,56},{72,6... | collective-permute-start | bytes 196616 | tf_op jit(solution)/shard_map/ppermute | solution.py:18
  101.4 3.8 %collective-permute-start.11 = (f32[18,1,512]{2,1,0:T(1,128)S(1)}, f32[18,1,512]{2,1,0:T(1,128)S(1)}, u32[]{:S(2)}, u32[]{:S(2)}) collective-permute-start(f32[18,1,512]{2,1,0:T(1,128)S(1)} %get-tuple-element.29), channel_id=1, source_target_pairs={{1,0},{2,1},{3,2},{4,3},{5,4},{6,5},{7,6},{9,8},{10,9},{11,10},{12... | collective-permute-start | bytes 110600 | tf_op jit(solution)/shard_map/ppermute | solution.py:18
  107.3 5.9 %collective-permute-start.17 = (f32[1,8,128]{2,1,0:T(8,128)S(1)}, f32[1,8,128]{2,1,0:T(8,128)S(1)}, u32[]{:S(2)}, u32[]{:S(2)}) collective-permute-start(f32[1,8,128]{2,1,0:T(8,128)S(1)} %get-tuple-element.73), channel_id=1, source_target_pairs={{8,0},{16,8},{24,16},{32,24},{40,32},{48,40},{56,48},{64,56},{72,6... | collective-permute-start | bytes 12296 | tf_op jit(solution)/shard_map/ppermute | solution.py:18
  114.1 2.9 fusion.22
  118.9 6.0 %collective-permute-start.13 = (f32[1,32,512]{2,1,0:T(8,128)S(1)}, f32[1,32,512]{2,1,0:T(8,128)S(1)}, u32[]{:S(2)}, u32[]{:S(2)}) collective-permute-start(f32[1,32,512]{2,1,0:T(8,128)S(1)} %get-tuple-element.35), channel_id=1, source_target_pairs={{8,0},{16,8},{24,16},{32,24},{40,32},{48,40},{56,48},{64,56},{72,6... | collective-permute-start | bytes 196616 | tf_op jit(solution)/shard_map/ppermute | solution.py:18
  126.9 4.8 %collective-permute-start.18 = (f32[6,1,128]{2,1,0:T(1,128)S(1)}, f32[6,1,128]{2,1,0:T(1,128)S(1)}, u32[]{:S(2)}, u32[]{:S(2)}) collective-permute-start(f32[6,1,128]{2,1,0:T(1,128)S(1)} %get-tuple-element.57), channel_id=1, source_target_pairs={{0,1},{1,2},{2,3},{3,4},{4,5},{5,6},{6,7},{8,9},{9,10},{10,11},{11... | collective-permute-start | bytes 9224 | tf_op jit(solution)/shard_map/ppermute | solution.py:15
  131.8 2.7 collective-permute-start.14
  134.5 3.4 %collective-permute-start.15 = (f32[18,1,512]{2,1,0:T(1,128)S(1)}, f32[18,1,512]{2,1,0:T(1,128)S(1)}, u32[]{:S(2)}, u32[]{:S(2)}) collective-permute-start(f32[18,1,512]{2,1,0:T(1,128)S(1)} %get-tuple-element.27), channel_id=1, source_target_pairs={{1,0},{2,1},{3,2},{4,3},{5,4},{6,5},{7,6},{9,8},{10,9},{11,10},{12... | collective-permute-start | bytes 110600 | tf_op jit(solution)/shard_map/ppermute | solution.py:18
  138.0 3.2 collective-permute-done.15
  142.1 2.6 fusion.3
  144.7 36.0 %reshape.15 = f32[4,4,8,4,128,4]{5,4,3,2,1,0:T(8,128)} reshape(f32[16,32,512]{2,1,0:T(8,128)S(1)} %fusion.3) | data formatting | bytes 2097152 | tf_op jit(solution)/shard_map/reshape | solution.py:50
  180.6 12.2 %reduce_sum.18 = f32[4,8,128]{2,1,0:T(8,128)S(1)} reduce(f32[4,4,8,4,128,4]{5,4,3,2,1,0:T(8,128)} %reshape.15, f32[]{:T(128)} %constant.21.clone.1), dimensions={1,3,5}, to_apply=%region_0.1 | reduce | flops 258048 | bytes 1064964 | tf_op jit(solution)/shard_map/reduce_sum | solution.py:50
  194.9 6.0 %collective-permute-start.21 = (f32[1,8,128]{2,1,0:T(8,128)S(1)}, f32[1,8,128]{2,1,0:T(8,128)S(1)}, u32[]{:S(2)}, u32[]{:S(2)}) collective-permute-start(f32[1,8,128]{2,1,0:T(8,128)S(1)} %get-tuple-element.71), channel_id=1, source_target_pairs={{8,0},{16,8},{24,16},{32,24},{40,32},{48,40},{56,48},{64,56},{72,6... | collective-permute-start | bytes 12296 | tf_op jit(solution)/shard_map/ppermute | solution.py:18
  202.2 3.3 %collective-permute-start.22 = (f32[6,1,128]{2,1,0:T(1,128)S(1)}, f32[6,1,128]{2,1,0:T(1,128)S(1)}, u32[]{:S(2)}, u32[]{:S(2)}) collective-permute-start(f32[6,1,128]{2,1,0:T(1,128)S(1)} %get-tuple-element.54), channel_id=1, source_target_pairs={{0,1},{1,2},{2,3},{3,4},{4,5},{5,6},{6,7},{8,9},{9,10},{10,11},{11... | collective-permute-start | bytes 9224 | tf_op jit(solution)/shard_map/ppermute | solution.py:15
  205.5 2.5 collective-permute-start.23
  208.1 3.8 %collective-permute-done.23 = f32[6,1,128]{2,1,0:T(1,128)S(1)} collective-permute-done((f32[6,1,128]{2,1,0:T(1,128)S(1)}, f32[6,1,128]{2,1,0:T(1,128)S(1)}, u32[]{:S(2)}, u32[]{:S(2)}) %collective-permute-start.23) | collective-permute-done | bytes 3104 | tf_op jit(solution)/shard_map/ppermute | solution.py:18
  214.1 6.0 %collective-permute-start.25 = (f32[1,8,128]{2,1,0:T(8,128)S(1)}, f32[1,8,128]{2,1,0:T(8,128)S(1)}, u32[]{:S(2)}, u32[]{:S(2)}) collective-permute-start(f32[1,8,128]{2,1,0:T(8,128)S(1)} %get-tuple-element.69), channel_id=1, source_target_pairs={{8,0},{16,8},{24,16},{32,24},{40,32},{48,40},{56,48},{64,56},{72,6... | collective-permute-start | bytes 12296 | tf_op jit(solution)/shard_map/ppermute | solution.py:18
  221.5 2.5 collective-permute-start.26
  224.0 3.3 %collective-permute-start.27 = (f32[6,1,128]{2,1,0:T(1,128)S(1)}, f32[6,1,128]{2,1,0:T(1,128)S(1)}, u32[]{:S(2)}, u32[]{:S(2)}) collective-permute-start(f32[6,1,128]{2,1,0:T(1,128)S(1)} %get-tuple-element.53), channel_id=1, source_target_pairs={{1,0},{2,1},{3,2},{4,3},{5,4},{6,5},{7,6},{9,8},{10,9},{11,10},{12... | collective-permute-start | bytes 9224 | tf_op jit(solution)/shard_map/ppermute | solution.py:18
  227.3 3.1 collective-permute-done.27
  232.5 6.0 %collective-permute-start.29 = (f32[1,8,128]{2,1,0:T(8,128)S(1)}, f32[1,8,128]{2,1,0:T(8,128)S(1)}, u32[]{:S(2)}, u32[]{:S(2)}) collective-permute-start(f32[1,8,128]{2,1,0:T(8,128)S(1)} %get-tuple-element.67), channel_id=1, source_target_pairs={{8,0},{16,8},{24,16},{32,24},{40,32},{48,40},{56,48},{64,56},{72,6... | collective-permute-start | bytes 12296 | tf_op jit(solution)/shard_map/ppermute | solution.py:18
  239.9 3.1 collective-permute-start.30
  243.0 2.7 collective-permute-start.31
  245.8 3.7 %collective-permute-done.31 = f32[6,1,128]{2,1,0:T(1,128)S(1)} collective-permute-done((f32[6,1,128]{2,1,0:T(1,128)S(1)}, f32[6,1,128]{2,1,0:T(1,128)S(1)}, u32[]{:S(2)}, u32[]{:S(2)}) %collective-permute-start.31) | collective-permute-done | bytes 3104 | tf_op jit(solution)/shard_map/ppermute | solution.py:18
  251.6 6.0 %collective-permute-start.33 = (f32[1,8,128]{2,1,0:T(8,128)S(1)}, f32[1,8,128]{2,1,0:T(8,128)S(1)}, u32[]{:S(2)}, u32[]{:S(2)}) collective-permute-start(f32[1,8,128]{2,1,0:T(8,128)S(1)} %get-tuple-element.65), channel_id=1, source_target_pairs={{8,0},{16,8},{24,16},{32,24},{40,32},{48,40},{56,48},{64,56},{72,6... | collective-permute-start | bytes 12296 | tf_op jit(solution)/shard_map/ppermute | solution.py:18
  258.9 2.5 collective-permute-start.34
  261.5 3.3 %collective-permute-start.35 = (f32[6,1,128]{2,1,0:T(1,128)S(1)}, f32[6,1,128]{2,1,0:T(1,128)S(1)}, u32[]{:S(2)}, u32[]{:S(2)}) collective-permute-start(f32[6,1,128]{2,1,0:T(1,128)S(1)} %get-tuple-element.49), channel_id=1, source_target_pairs={{1,0},{2,1},{3,2},{4,3},{5,4},{6,5},{7,6},{9,8},{10,9},{11,10},{12... | collective-permute-start | bytes 9224 | tf_op jit(solution)/shard_map/ppermute | solution.py:18
  264.8 3.1 collective-permute-done.35
  270.0 6.0 %collective-permute-start.37 = (f32[1,8,128]{2,1,0:T(8,128)S(1)}, f32[1,8,128]{2,1,0:T(8,128)S(1)}, u32[]{:S(2)}, u32[]{:S(2)}) collective-permute-start(f32[1,8,128]{2,1,0:T(8,128)S(1)} %get-tuple-element.63), channel_id=1, source_target_pairs={{8,0},{16,8},{24,16},{32,24},{40,32},{48,40},{56,48},{64,56},{72,6... | collective-permute-start | bytes 12296 | tf_op jit(solution)/shard_map/ppermute | solution.py:18
  279.3 3.9 %collective-permute-start.39 = (f32[6,1,128]{2,1,0:T(1,128)S(1)}, f32[6,1,128]{2,1,0:T(1,128)S(1)}, u32[]{:S(2)}, u32[]{:S(2)}) collective-permute-start(f32[6,1,128]{2,1,0:T(1,128)S(1)} %get-tuple-element.47), channel_id=1, source_target_pairs={{1,0},{2,1},{3,2},{4,3},{5,4},{6,5},{7,6},{9,8},{10,9},{11,10},{12... | collective-permute-start | bytes 9224 | tf_op jit(solution)/shard_map/ppermute | solution.py:18
  283.2 2.5 collective-permute-done.39
  287.9 6.0 %collective-permute-start.41 = (f32[1,8,128]{2,1,0:T(8,128)S(1)}, f32[1,8,128]{2,1,0:T(8,128)S(1)}, u32[]{:S(2)}, u32[]{:S(2)}) collective-permute-start(f32[1,8,128]{2,1,0:T(8,128)S(1)} %get-tuple-element.61), channel_id=1, source_target_pairs={{8,0},{16,8},{24,16},{32,24},{40,32},{48,40},{56,48},{64,56},{72,6... | collective-permute-start | bytes 12296 | tf_op jit(solution)/shard_map/ppermute | solution.py:18
  297.1 3.9 %collective-permute-start.43 = (f32[6,1,128]{2,1,0:T(1,128)S(1)}, f32[6,1,128]{2,1,0:T(1,128)S(1)}, u32[]{:S(2)}, u32[]{:S(2)}) collective-permute-start(f32[6,1,128]{2,1,0:T(1,128)S(1)} %get-tuple-element.45), channel_id=1, source_target_pairs={{1,0},{2,1},{3,2},{4,3},{5,4},{6,5},{7,6},{9,8},{10,9},{11,10},{12... | collective-permute-start | bytes 9224 | tf_op jit(solution)/shard_map/ppermute | solution.py:18
  301.1 2.5 collective-permute-done.43
  305.7 6.0 %collective-permute-start.45 = (f32[1,8,128]{2,1,0:T(8,128)S(1)}, f32[1,8,128]{2,1,0:T(8,128)S(1)}, u32[]{:S(2)}, u32[]{:S(2)}) collective-permute-start(f32[1,8,128]{2,1,0:T(8,128)S(1)} %get-tuple-element.59), channel_id=1, source_target_pairs={{8,0},{16,8},{24,16},{32,24},{40,32},{48,40},{56,48},{64,56},{72,6... | collective-permute-start | bytes 12296 | tf_op jit(solution)/shard_map/ppermute | solution.py:18
  315.0 3.9 %collective-permute-start.47 = (f32[6,1,128]{2,1,0:T(1,128)S(1)}, f32[6,1,128]{2,1,0:T(1,128)S(1)}, u32[]{:S(2)}, u32[]{:S(2)}) collective-permute-start(f32[6,1,128]{2,1,0:T(1,128)S(1)} %get-tuple-element.43), channel_id=1, source_target_pairs={{1,0},{2,1},{3,2},{4,3},{5,4},{6,5},{7,6},{9,8},{10,9},{11,10},{12... | collective-permute-start | bytes 9224 | tf_op jit(solution)/shard_map/ppermute | solution.py:18
  318.9 2.5 collective-permute-done.47
  322.2 2.3 broadcast_in_dim.11
  324.5 2.8 copy.187
  (119 shorter events, 55.0 us)
Async XLA Ops:
  0.9 65.9 %collective-permute-start = (f32[1,32,512]{2,1,0:T(8,128)S(1)}, f32[1,32,512]{2,1,0:T(8,128)S(1)}, u32[]{:S(2)}, u32[]{:S(2)}) collective-permute-start(f32[1,32,512]{2,1,0:T(8,128)S(1)} %get-tuple-element.39), channel_id=1, source_target_pairs={{0,8},{8,16},{16,24},{24,32},{32,40},{40,48},{48,56},{56,64},{64,7... | collective-permute-start | bytes 196616 | tf_op jit(solution)/shard_map/ppermute | solution.py:15
  3.7 69.5 %collective-permute-start.3 = (f32[1,32,512]{2,1,0:T(8,128)S(1)}, f32[1,32,512]{2,1,0:T(8,128)S(1)}, u32[]{:S(2)}, u32[]{:S(2)}) collective-permute-start(f32[1,32,512]{2,1,0:T(8,128)S(1)} %get-tuple-element.40), channel_id=1, source_target_pairs={{8,0},{16,8},{24,16},{32,24},{40,32},{48,40},{56,48},{64,56},{72,6... | collective-permute-start | bytes 196616 | tf_op jit(solution)/shard_map/ppermute | solution.py:18
  9.8 63.3 %collective-permute-start.1 = (f32[1,32,512]{2,1,0:T(8,128)S(1)}, f32[1,32,512]{2,1,0:T(8,128)S(1)}, u32[]{:S(2)}, u32[]{:S(2)}) collective-permute-start(f32[1,32,512]{2,1,0:T(8,128)S(1)} %get-tuple-element.41), channel_id=1, source_target_pairs={{0,8},{8,16},{16,24},{24,32},{32,40},{40,48},{48,56},{56,64},{64,7... | collective-permute-start | bytes 196616 | tf_op jit(solution)/shard_map/ppermute | solution.py:15
  11.7 55.3 %collective-permute-start.2 = (f32[1,32,512]{2,1,0:T(8,128)S(1)}, f32[1,32,512]{2,1,0:T(8,128)S(1)}, u32[]{:S(2)}, u32[]{:S(2)}) collective-permute-start(f32[1,32,512]{2,1,0:T(8,128)S(1)} %get-tuple-element.38), channel_id=1, source_target_pairs={{8,0},{16,8},{24,16},{32,24},{40,32},{48,40},{56,48},{64,56},{72,6... | collective-permute-start | bytes 196616 | tf_op jit(solution)/shard_map/ppermute | solution.py:18
  67.0 12.1 %collective-permute-start.4 = (f32[18,1,512]{2,1,0:T(1,128)S(1)}, f32[18,1,512]{2,1,0:T(1,128)S(1)}, u32[]{:S(2)}, u32[]{:S(2)}) collective-permute-start(f32[18,1,512]{2,1,0:T(1,128)S(1)} %get-tuple-element.30), channel_id=1, source_target_pairs={{0,1},{1,2},{2,3},{3,4},{4,5},{5,6},{6,7},{8,9},{9,10},{10,11},{11... | collective-permute-start | bytes 110600 | tf_op jit(solution)/shard_map/ppermute | solution.py:15
  70.2 8.9 %collective-permute-start.6 = (f32[18,1,512]{2,1,0:T(1,128)S(1)}, f32[18,1,512]{2,1,0:T(1,128)S(1)}, u32[]{:S(2)}, u32[]{:S(2)}) collective-permute-start(f32[18,1,512]{2,1,0:T(1,128)S(1)} %get-tuple-element.31), channel_id=1, source_target_pairs={{1,0},{2,1},{3,2},{4,3},{5,4},{6,5},{7,6},{9,8},{10,9},{11,10},{12... | collective-permute-start | bytes 110600 | tf_op jit(solution)/shard_map/ppermute | solution.py:18
  73.2 6.8 %collective-permute-start.5 = (f32[18,1,512]{2,1,0:T(1,128)S(1)}, f32[18,1,512]{2,1,0:T(1,128)S(1)}, u32[]{:S(2)}, u32[]{:S(2)}) collective-permute-start(f32[18,1,512]{2,1,0:T(1,128)S(1)} %get-tuple-element.32), channel_id=1, source_target_pairs={{0,1},{1,2},{2,3},{3,4},{4,5},{5,6},{6,7},{8,9},{9,10},{10,11},{11... | collective-permute-start | bytes 110600 | tf_op jit(solution)/shard_map/ppermute | solution.py:15
  77.2 6.8 %collective-permute-start.7 = (f32[18,1,512]{2,1,0:T(1,128)S(1)}, f32[18,1,512]{2,1,0:T(1,128)S(1)}, u32[]{:S(2)}, u32[]{:S(2)}) collective-permute-start(f32[18,1,512]{2,1,0:T(1,128)S(1)} %get-tuple-element.33), channel_id=1, source_target_pairs={{1,0},{2,1},{3,2},{4,3},{5,4},{6,5},{7,6},{9,8},{10,9},{11,10},{12... | collective-permute-start | bytes 110600 | tf_op jit(solution)/shard_map/ppermute | solution.py:18
  89.4 8.0 %collective-permute-start.8 = (f32[1,32,512]{2,1,0:T(8,128)S(1)}, f32[1,32,512]{2,1,0:T(8,128)S(1)}, u32[]{:S(2)}, u32[]{:S(2)}) collective-permute-start(f32[1,32,512]{2,1,0:T(8,128)S(1)} %get-tuple-element.36), channel_id=1, source_target_pairs={{0,8},{8,16},{16,24},{24,32},{32,40},{40,48},{48,56},{56,64},{64,7... | collective-permute-start | bytes 196616 | tf_op jit(solution)/shard_map/ppermute | solution.py:15
  91.3 7.9 %collective-permute-start.9 = (f32[1,32,512]{2,1,0:T(8,128)S(1)}, f32[1,32,512]{2,1,0:T(8,128)S(1)}, u32[]{:S(2)}, u32[]{:S(2)}) collective-permute-start(f32[1,32,512]{2,1,0:T(8,128)S(1)} %get-tuple-element.37), channel_id=1, source_target_pairs={{8,0},{16,8},{24,16},{32,24},{40,32},{48,40},{56,48},{64,56},{72,6... | collective-permute-start | bytes 196616 | tf_op jit(solution)/shard_map/ppermute | solution.py:18
  99.3 13.9 %collective-permute-start.10 = (f32[18,1,512]{2,1,0:T(1,128)S(1)}, f32[18,1,512]{2,1,0:T(1,128)S(1)}, u32[]{:S(2)}, u32[]{:S(2)}) collective-permute-start(f32[18,1,512]{2,1,0:T(1,128)S(1)} %get-tuple-element.28), channel_id=1, source_target_pairs={{0,1},{1,2},{2,3},{3,4},{4,5},{5,6},{6,7},{8,9},{9,10},{10,11},{11... | collective-permute-start | bytes 110600 | tf_op jit(solution)/shard_map/ppermute | solution.py:15
  101.4 11.8 %collective-permute-start.11 = (f32[18,1,512]{2,1,0:T(1,128)S(1)}, f32[18,1,512]{2,1,0:T(1,128)S(1)}, u32[]{:S(2)}, u32[]{:S(2)}) collective-permute-start(f32[18,1,512]{2,1,0:T(1,128)S(1)} %get-tuple-element.29), channel_id=1, source_target_pairs={{1,0},{2,1},{3,2},{4,3},{5,4},{6,5},{7,6},{9,8},{10,9},{11,10},{12... | collective-permute-start | bytes 110600 | tf_op jit(solution)/shard_map/ppermute | solution.py:18
  105.2 19.7 %collective-permute-start.16 = (f32[1,8,128]{2,1,0:T(8,128)S(1)}, f32[1,8,128]{2,1,0:T(8,128)S(1)}, u32[]{:S(2)}, u32[]{:S(2)}) collective-permute-start(f32[1,8,128]{2,1,0:T(8,128)S(1)} %get-tuple-element.72), channel_id=1, source_target_pairs={{0,8},{8,16},{16,24},{24,32},{32,40},{40,48},{48,56},{56,64},{64,7... | collective-permute-start | bytes 12296 | tf_op jit(solution)/shard_map/ppermute | solution.py:15
  107.3 17.6 %collective-permute-start.17 = (f32[1,8,128]{2,1,0:T(8,128)S(1)}, f32[1,8,128]{2,1,0:T(8,128)S(1)}, u32[]{:S(2)}, u32[]{:S(2)}) collective-permute-start(f32[1,8,128]{2,1,0:T(8,128)S(1)} %get-tuple-element.73), channel_id=1, source_target_pairs={{8,0},{16,8},{24,16},{32,24},{40,32},{48,40},{56,48},{64,56},{72,6... | collective-permute-start | bytes 12296 | tf_op jit(solution)/shard_map/ppermute | solution.py:18
  116.9 14.8 %collective-permute-start.12 = (f32[1,32,512]{2,1,0:T(8,128)S(1)}, f32[1,32,512]{2,1,0:T(8,128)S(1)}, u32[]{:S(2)}, u32[]{:S(2)}) collective-permute-start(f32[1,32,512]{2,1,0:T(8,128)S(1)} %get-tuple-element.34), channel_id=1, source_target_pairs={{0,8},{8,16},{16,24},{24,32},{32,40},{40,48},{48,56},{56,64},{64,7... | collective-permute-start | bytes 196616 | tf_op jit(solution)/shard_map/ppermute | solution.py:15
  118.9 12.9 %collective-permute-start.13 = (f32[1,32,512]{2,1,0:T(8,128)S(1)}, f32[1,32,512]{2,1,0:T(8,128)S(1)}, u32[]{:S(2)}, u32[]{:S(2)}) collective-permute-start(f32[1,32,512]{2,1,0:T(8,128)S(1)} %get-tuple-element.35), channel_id=1, source_target_pairs={{8,0},{16,8},{24,16},{32,24},{40,32},{48,40},{56,48},{64,56},{72,6... | collective-permute-start | bytes 196616 | tf_op jit(solution)/shard_map/ppermute | solution.py:18
  125.0 12.9 %collective-permute-start.19 = (f32[6,1,128]{2,1,0:T(1,128)S(1)}, f32[6,1,128]{2,1,0:T(1,128)S(1)}, u32[]{:S(2)}, u32[]{:S(2)}) collective-permute-start(f32[6,1,128]{2,1,0:T(1,128)S(1)} %get-tuple-element.56), channel_id=1, source_target_pairs={{1,0},{2,1},{3,2},{4,3},{5,4},{6,5},{7,6},{9,8},{10,9},{11,10},{12... | collective-permute-start | bytes 9224 | tf_op jit(solution)/shard_map/ppermute | solution.py:18
  126.9 11.0 %collective-permute-start.18 = (f32[6,1,128]{2,1,0:T(1,128)S(1)}, f32[6,1,128]{2,1,0:T(1,128)S(1)}, u32[]{:S(2)}, u32[]{:S(2)}) collective-permute-start(f32[6,1,128]{2,1,0:T(1,128)S(1)} %get-tuple-element.57), channel_id=1, source_target_pairs={{0,1},{1,2},{2,3},{3,4},{4,5},{5,6},{6,7},{8,9},{9,10},{10,11},{11... | collective-permute-start | bytes 9224 | tf_op jit(solution)/shard_map/ppermute | solution.py:15
  131.8 6.2 %collective-permute-start.14 = (f32[18,1,512]{2,1,0:T(1,128)S(1)}, f32[18,1,512]{2,1,0:T(1,128)S(1)}, u32[]{:S(2)}, u32[]{:S(2)}) collective-permute-start(f32[18,1,512]{2,1,0:T(1,128)S(1)} %get-tuple-element.26), channel_id=1, source_target_pairs={{0,1},{1,2},{2,3},{3,4},{4,5},{5,6},{6,7},{8,9},{9,10},{10,11},{11... | collective-permute-start | bytes 110600 | tf_op jit(solution)/shard_map/ppermute | solution.py:15
  134.5 6.8 %collective-permute-start.15 = (f32[18,1,512]{2,1,0:T(1,128)S(1)}, f32[18,1,512]{2,1,0:T(1,128)S(1)}, u32[]{:S(2)}, u32[]{:S(2)}) collective-permute-start(f32[18,1,512]{2,1,0:T(1,128)S(1)} %get-tuple-element.27), channel_id=1, source_target_pairs={{1,0},{2,1},{3,2},{4,3},{5,4},{6,5},{7,6},{9,8},{10,9},{11,10},{12... | collective-permute-start | bytes 110600 | tf_op jit(solution)/shard_map/ppermute | solution.py:18
  193.0 8.0 %collective-permute-start.20 = (f32[1,8,128]{2,1,0:T(8,128)S(1)}, f32[1,8,128]{2,1,0:T(8,128)S(1)}, u32[]{:S(2)}, u32[]{:S(2)}) collective-permute-start(f32[1,8,128]{2,1,0:T(8,128)S(1)} %get-tuple-element.70), channel_id=1, source_target_pairs={{0,8},{8,16},{16,24},{24,32},{32,40},{40,48},{48,56},{56,64},{64,7... | collective-permute-start | bytes 12296 | tf_op jit(solution)/shard_map/ppermute | solution.py:15
  194.9 7.4 %collective-permute-start.21 = (f32[1,8,128]{2,1,0:T(8,128)S(1)}, f32[1,8,128]{2,1,0:T(8,128)S(1)}, u32[]{:S(2)}, u32[]{:S(2)}) collective-permute-start(f32[1,8,128]{2,1,0:T(8,128)S(1)} %get-tuple-element.71), channel_id=1, source_target_pairs={{8,0},{16,8},{24,16},{32,24},{40,32},{48,40},{56,48},{64,56},{72,6... | collective-permute-start | bytes 12296 | tf_op jit(solution)/shard_map/ppermute | solution.py:18
  202.2 5.8 %collective-permute-start.22 = (f32[6,1,128]{2,1,0:T(1,128)S(1)}, f32[6,1,128]{2,1,0:T(1,128)S(1)}, u32[]{:S(2)}, u32[]{:S(2)}) collective-permute-start(f32[6,1,128]{2,1,0:T(1,128)S(1)} %get-tuple-element.54), channel_id=1, source_target_pairs={{0,1},{1,2},{2,3},{3,4},{4,5},{5,6},{6,7},{8,9},{9,10},{10,11},{11... | collective-permute-start | bytes 9224 | tf_op jit(solution)/shard_map/ppermute | solution.py:15
  205.5 6.4 %collective-permute-start.23 = (f32[6,1,128]{2,1,0:T(1,128)S(1)}, f32[6,1,128]{2,1,0:T(1,128)S(1)}, u32[]{:S(2)}, u32[]{:S(2)}) collective-permute-start(f32[6,1,128]{2,1,0:T(1,128)S(1)} %get-tuple-element.55), channel_id=1, source_target_pairs={{1,0},{2,1},{3,2},{4,3},{5,4},{6,5},{7,6},{9,8},{10,9},{11,10},{12... | collective-permute-start | bytes 9224 | tf_op jit(solution)/shard_map/ppermute | solution.py:18
  212.2 8.0 %collective-permute-start.24 = (f32[1,8,128]{2,1,0:T(8,128)S(1)}, f32[1,8,128]{2,1,0:T(8,128)S(1)}, u32[]{:S(2)}, u32[]{:S(2)}) collective-permute-start(f32[1,8,128]{2,1,0:T(8,128)S(1)} %get-tuple-element.68), channel_id=1, source_target_pairs={{0,8},{8,16},{16,24},{24,32},{32,40},{40,48},{48,56},{56,64},{64,7... | collective-permute-start | bytes 12296 | tf_op jit(solution)/shard_map/ppermute | solution.py:15
  214.1 7.4 %collective-permute-start.25 = (f32[1,8,128]{2,1,0:T(8,128)S(1)}, f32[1,8,128]{2,1,0:T(8,128)S(1)}, u32[]{:S(2)}, u32[]{:S(2)}) collective-permute-start(f32[1,8,128]{2,1,0:T(8,128)S(1)} %get-tuple-element.69), channel_id=1, source_target_pairs={{8,0},{16,8},{24,16},{32,24},{40,32},{48,40},{56,48},{64,56},{72,6... | collective-permute-start | bytes 12296 | tf_op jit(solution)/shard_map/ppermute | solution.py:18
  221.5 5.8 %collective-permute-start.26 = (f32[6,1,128]{2,1,0:T(1,128)S(1)}, f32[6,1,128]{2,1,0:T(1,128)S(1)}, u32[]{:S(2)}, u32[]{:S(2)}) collective-permute-start(f32[6,1,128]{2,1,0:T(1,128)S(1)} %get-tuple-element.52), channel_id=1, source_target_pairs={{0,1},{1,2},{2,3},{3,4},{4,5},{5,6},{6,7},{8,9},{9,10},{10,11},{11... | collective-permute-start | bytes 9224 | tf_op jit(solution)/shard_map/ppermute | solution.py:15
  224.0 6.4 %collective-permute-start.27 = (f32[6,1,128]{2,1,0:T(1,128)S(1)}, f32[6,1,128]{2,1,0:T(1,128)S(1)}, u32[]{:S(2)}, u32[]{:S(2)}) collective-permute-start(f32[6,1,128]{2,1,0:T(1,128)S(1)} %get-tuple-element.53), channel_id=1, source_target_pairs={{1,0},{2,1},{3,2},{4,3},{5,4},{6,5},{7,6},{9,8},{10,9},{11,10},{12... | collective-permute-start | bytes 9224 | tf_op jit(solution)/shard_map/ppermute | solution.py:18
  230.6 8.0 %collective-permute-start.28 = (f32[1,8,128]{2,1,0:T(8,128)S(1)}, f32[1,8,128]{2,1,0:T(8,128)S(1)}, u32[]{:S(2)}, u32[]{:S(2)}) collective-permute-start(f32[1,8,128]{2,1,0:T(8,128)S(1)} %get-tuple-element.66), channel_id=1, source_target_pairs={{0,8},{8,16},{16,24},{24,32},{32,40},{40,48},{48,56},{56,64},{64,7... | collective-permute-start | bytes 12296 | tf_op jit(solution)/shard_map/ppermute | solution.py:15
  232.5 7.4 %collective-permute-start.29 = (f32[1,8,128]{2,1,0:T(8,128)S(1)}, f32[1,8,128]{2,1,0:T(8,128)S(1)}, u32[]{:S(2)}, u32[]{:S(2)}) collective-permute-start(f32[1,8,128]{2,1,0:T(8,128)S(1)} %get-tuple-element.67), channel_id=1, source_target_pairs={{8,0},{16,8},{24,16},{32,24},{40,32},{48,40},{56,48},{64,56},{72,6... | collective-permute-start | bytes 12296 | tf_op jit(solution)/shard_map/ppermute | solution.py:18
  239.9 5.8 %collective-permute-start.30 = (f32[6,1,128]{2,1,0:T(1,128)S(1)}, f32[6,1,128]{2,1,0:T(1,128)S(1)}, u32[]{:S(2)}, u32[]{:S(2)}) collective-permute-start(f32[6,1,128]{2,1,0:T(1,128)S(1)} %get-tuple-element.50), channel_id=1, source_target_pairs={{0,1},{1,2},{2,3},{3,4},{4,5},{5,6},{6,7},{8,9},{9,10},{10,11},{11... | collective-permute-start | bytes 9224 | tf_op jit(solution)/shard_map/ppermute | solution.py:15
  243.0 6.4 %collective-permute-start.31 = (f32[6,1,128]{2,1,0:T(1,128)S(1)}, f32[6,1,128]{2,1,0:T(1,128)S(1)}, u32[]{:S(2)}, u32[]{:S(2)}) collective-permute-start(f32[6,1,128]{2,1,0:T(1,128)S(1)} %get-tuple-element.51), channel_id=1, source_target_pairs={{1,0},{2,1},{3,2},{4,3},{5,4},{6,5},{7,6},{9,8},{10,9},{11,10},{12... | collective-permute-start | bytes 9224 | tf_op jit(solution)/shard_map/ppermute | solution.py:18
  249.7 8.0 %collective-permute-start.32 = (f32[1,8,128]{2,1,0:T(8,128)S(1)}, f32[1,8,128]{2,1,0:T(8,128)S(1)}, u32[]{:S(2)}, u32[]{:S(2)}) collective-permute-start(f32[1,8,128]{2,1,0:T(8,128)S(1)} %get-tuple-element.64), channel_id=1, source_target_pairs={{0,8},{8,16},{16,24},{24,32},{32,40},{40,48},{48,56},{56,64},{64,7... | collective-permute-start | bytes 12296 | tf_op jit(solution)/shard_map/ppermute | solution.py:15
  251.6 7.4 %collective-permute-start.33 = (f32[1,8,128]{2,1,0:T(8,128)S(1)}, f32[1,8,128]{2,1,0:T(8,128)S(1)}, u32[]{:S(2)}, u32[]{:S(2)}) collective-permute-start(f32[1,8,128]{2,1,0:T(8,128)S(1)} %get-tuple-element.65), channel_id=1, source_target_pairs={{8,0},{16,8},{24,16},{32,24},{40,32},{48,40},{56,48},{64,56},{72,6... | collective-permute-start | bytes 12296 | tf_op jit(solution)/shard_map/ppermute | solution.py:18
  258.9 5.8 %collective-permute-start.34 = (f32[6,1,128]{2,1,0:T(1,128)S(1)}, f32[6,1,128]{2,1,0:T(1,128)S(1)}, u32[]{:S(2)}, u32[]{:S(2)}) collective-permute-start(f32[6,1,128]{2,1,0:T(1,128)S(1)} %get-tuple-element.48), channel_id=1, source_target_pairs={{0,1},{1,2},{2,3},{3,4},{4,5},{5,6},{6,7},{8,9},{9,10},{10,11},{11... | collective-permute-start | bytes 9224 | tf_op jit(solution)/shard_map/ppermute | solution.py:15
  261.5 6.4 %collective-permute-start.35 = (f32[6,1,128]{2,1,0:T(1,128)S(1)}, f32[6,1,128]{2,1,0:T(1,128)S(1)}, u32[]{:S(2)}, u32[]{:S(2)}) collective-permute-start(f32[6,1,128]{2,1,0:T(1,128)S(1)} %get-tuple-element.49), channel_id=1, source_target_pairs={{1,0},{2,1},{3,2},{4,3},{5,4},{6,5},{7,6},{9,8},{10,9},{11,10},{12... | collective-permute-start | bytes 9224 | tf_op jit(solution)/shard_map/ppermute | solution.py:18
  268.1 8.0 %collective-permute-start.36 = (f32[1,8,128]{2,1,0:T(8,128)S(1)}, f32[1,8,128]{2,1,0:T(8,128)S(1)}, u32[]{:S(2)}, u32[]{:S(2)}) collective-permute-start(f32[1,8,128]{2,1,0:T(8,128)S(1)} %get-tuple-element.62), channel_id=1, source_target_pairs={{0,8},{8,16},{16,24},{24,32},{32,40},{40,48},{48,56},{56,64},{64,7... | collective-permute-start | bytes 12296 | tf_op jit(solution)/shard_map/ppermute | solution.py:15
  270.0 7.4 %collective-permute-start.37 = (f32[1,8,128]{2,1,0:T(8,128)S(1)}, f32[1,8,128]{2,1,0:T(8,128)S(1)}, u32[]{:S(2)}, u32[]{:S(2)}) collective-permute-start(f32[1,8,128]{2,1,0:T(8,128)S(1)} %get-tuple-element.63), channel_id=1, source_target_pairs={{8,0},{16,8},{24,16},{32,24},{40,32},{48,40},{56,48},{64,56},{72,6... | collective-permute-start | bytes 12296 | tf_op jit(solution)/shard_map/ppermute | solution.py:18
  277.4 5.8 %collective-permute-start.38 = (f32[6,1,128]{2,1,0:T(1,128)S(1)}, f32[6,1,128]{2,1,0:T(1,128)S(1)}, u32[]{:S(2)}, u32[]{:S(2)}) collective-permute-start(f32[6,1,128]{2,1,0:T(1,128)S(1)} %get-tuple-element.46), channel_id=1, source_target_pairs={{0,1},{1,2},{2,3},{3,4},{4,5},{5,6},{6,7},{8,9},{9,10},{10,11},{11... | collective-permute-start | bytes 9224 | tf_op jit(solution)/shard_map/ppermute | solution.py:15
  279.3 6.4 %collective-permute-start.39 = (f32[6,1,128]{2,1,0:T(1,128)S(1)}, f32[6,1,128]{2,1,0:T(1,128)S(1)}, u32[]{:S(2)}, u32[]{:S(2)}) collective-permute-start(f32[6,1,128]{2,1,0:T(1,128)S(1)} %get-tuple-element.47), channel_id=1, source_target_pairs={{1,0},{2,1},{3,2},{4,3},{5,4},{6,5},{7,6},{9,8},{10,9},{11,10},{12... | collective-permute-start | bytes 9224 | tf_op jit(solution)/shard_map/ppermute | solution.py:18
  285.9 8.0 %collective-permute-start.40 = (f32[1,8,128]{2,1,0:T(8,128)S(1)}, f32[1,8,128]{2,1,0:T(8,128)S(1)}, u32[]{:S(2)}, u32[]{:S(2)}) collective-permute-start(f32[1,8,128]{2,1,0:T(8,128)S(1)} %get-tuple-element.60), channel_id=1, source_target_pairs={{0,8},{8,16},{16,24},{24,32},{32,40},{40,48},{48,56},{56,64},{64,7... | collective-permute-start | bytes 12296 | tf_op jit(solution)/shard_map/ppermute | solution.py:15
  287.9 7.4 %collective-permute-start.41 = (f32[1,8,128]{2,1,0:T(8,128)S(1)}, f32[1,8,128]{2,1,0:T(8,128)S(1)}, u32[]{:S(2)}, u32[]{:S(2)}) collective-permute-start(f32[1,8,128]{2,1,0:T(8,128)S(1)} %get-tuple-element.61), channel_id=1, source_target_pairs={{8,0},{16,8},{24,16},{32,24},{40,32},{48,40},{56,48},{64,56},{72,6... | collective-permute-start | bytes 12296 | tf_op jit(solution)/shard_map/ppermute | solution.py:18
  295.2 5.8 %collective-permute-start.42 = (f32[6,1,128]{2,1,0:T(1,128)S(1)}, f32[6,1,128]{2,1,0:T(1,128)S(1)}, u32[]{:S(2)}, u32[]{:S(2)}) collective-permute-start(f32[6,1,128]{2,1,0:T(1,128)S(1)} %get-tuple-element.44), channel_id=1, source_target_pairs={{0,1},{1,2},{2,3},{3,4},{4,5},{5,6},{6,7},{8,9},{9,10},{10,11},{11... | collective-permute-start | bytes 9224 | tf_op jit(solution)/shard_map/ppermute | solution.py:15
  297.1 6.4 %collective-permute-start.43 = (f32[6,1,128]{2,1,0:T(1,128)S(1)}, f32[6,1,128]{2,1,0:T(1,128)S(1)}, u32[]{:S(2)}, u32[]{:S(2)}) collective-permute-start(f32[6,1,128]{2,1,0:T(1,128)S(1)} %get-tuple-element.45), channel_id=1, source_target_pairs={{1,0},{2,1},{3,2},{4,3},{5,4},{6,5},{7,6},{9,8},{10,9},{11,10},{12... | collective-permute-start | bytes 9224 | tf_op jit(solution)/shard_map/ppermute | solution.py:18
  303.8 8.0 %collective-permute-start.44 = (f32[1,8,128]{2,1,0:T(8,128)S(1)}, f32[1,8,128]{2,1,0:T(8,128)S(1)}, u32[]{:S(2)}, u32[]{:S(2)}) collective-permute-start(f32[1,8,128]{2,1,0:T(8,128)S(1)} %get-tuple-element.58), channel_id=1, source_target_pairs={{0,8},{8,16},{16,24},{24,32},{32,40},{40,48},{48,56},{56,64},{64,7... | collective-permute-start | bytes 12296 | tf_op jit(solution)/shard_map/ppermute | solution.py:15
  305.7 7.4 %collective-permute-start.45 = (f32[1,8,128]{2,1,0:T(8,128)S(1)}, f32[1,8,128]{2,1,0:T(8,128)S(1)}, u32[]{:S(2)}, u32[]{:S(2)}) collective-permute-start(f32[1,8,128]{2,1,0:T(8,128)S(1)} %get-tuple-element.59), channel_id=1, source_target_pairs={{8,0},{16,8},{24,16},{32,24},{40,32},{48,40},{56,48},{64,56},{72,6... | collective-permute-start | bytes 12296 | tf_op jit(solution)/shard_map/ppermute | solution.py:18
  313.1 5.8 %collective-permute-start.46 = (f32[6,1,128]{2,1,0:T(1,128)S(1)}, f32[6,1,128]{2,1,0:T(1,128)S(1)}, u32[]{:S(2)}, u32[]{:S(2)}) collective-permute-start(f32[6,1,128]{2,1,0:T(1,128)S(1)} %get-tuple-element.42), channel_id=1, source_target_pairs={{0,1},{1,2},{2,3},{3,4},{4,5},{5,6},{6,7},{8,9},{9,10},{10,11},{11... | collective-permute-start | bytes 9224 | tf_op jit(solution)/shard_map/ppermute | solution.py:15
  315.0 6.4 %collective-permute-start.47 = (f32[6,1,128]{2,1,0:T(1,128)S(1)}, f32[6,1,128]{2,1,0:T(1,128)S(1)}, u32[]{:S(2)}, u32[]{:S(2)}) collective-permute-start(f32[6,1,128]{2,1,0:T(1,128)S(1)} %get-tuple-element.43), channel_id=1, source_target_pairs={{1,0},{2,1},{3,2},{4,3},{5,4},{6,5},{7,6},{9,8},{10,9},{11,10},{12... | collective-permute-start | bytes 9224 | tf_op jit(solution)/shard_map/ppermute | solution.py:18
  (3 other events, 23.4 us)
where the time goes:
time: 331 us; the launch traced here: 329 us
  starting transfers between devices  167 us (50%)
  local copies, waits for them, and re-layouts  80.6 us (24%)
  other arithmetic  41 us (12%)
  waiting for transfers between devices  39.1 us (12%)
    ppermute x24, starting transfers between devices, extended(): lax.ppermute(lax.slice_in_dim(block, 0, width, axis=dim), axis, backward)  110 us
    reshape x2, local copies, waits for them, and re-layouts, block_mean(): field.reshape(sx // 4, 4, sy // 4, 4, sz // 4, 4).mean(axis=(1, 3, 5))  72.8 us
    ppermute x24, starting transfers between devices, extended(): lax.ppermute(lax.slice_in_dim(block, block.shape[dim] - width, None, axis...  57 us
    ppermute x24, waiting for transfers between devices, extended(): lax.ppermute(lax.slice_in_dim(block, 0, width, axis=dim), axis, backward)  39.1 us
    reduce_sum x2, other arithmetic, block_mean(): field.reshape(sx // 4, 4, sy // 4, 4, sz // 4, 4).mean(axis=(1, 3, 5))  24.5 us
    add x2, other arithmetic, per_device(): fine + 2.0 / 3.0 * (right_side - stencil(fine, pressure_pad(fine), coefs)...  7.44 us
  transfers between devices with their start and end apart: 48, of which 17 were waited for; matrix products, arithmetic and copies ran while one was open for 17% of the time, Pallas kernels for 0%

commit v1 on v0

v1 whole, which is shorter than its diff:
```python
import jax
import jax.numpy as jnp
from jax import lax
from jax.sharding import PartitionSpec as P

SWEEPS = 2
CHEB = 8
HIGHEST = lax.Precision.HIGHEST


def shifted_pairs(count, hop):
    return [(i, i + hop) for i in range(count - hop)]


def halo_from(block, axis, dim, width, hop):
    count = lax.axis_size(axis)
    n = block.shape[dim]
    if hop >= count:
        shape = list(block.shape)
        shape[dim] = width
        zeros = jnp.zeros(shape, block.dtype)
        return zeros, zeros
    forward = shifted_pairs(count, hop)
    backward = [(t, s) for s, t in forward]
    low = lax.ppermute(lax.slice_in_dim(block, n - width, n, axis=dim), axis, forward)
    high = lax.ppermute(lax.slice_in_dim(block, 0, width, axis=dim), axis, backward)
    return low, high


def deep_extend(block, axis, dim, depth):
    n = block.shape[dim]
    lows, highs = [], []
    need, hop = depth, 1
    while need > 0:
        width = min(n, need)
        low, high = halo_from(block, axis, dim, width, hop)
        lows.insert(0, low)
        highs.append(high)
        need -= width
        hop += 1
    return jnp.concatenate(lows + [block] + highs, axis=dim)


def shift_z(field, side):
    zeros = jnp.zeros_like(field[:, :, :1])
    if side < 0:
        return jnp.concatenate([zeros, field[:, :, :-1]], axis=2)
    return jnp.concatenate([field[:, :, 1:], zeros], axis=2)


def fine_neighbours(field):
    xl, xh = halo_from(field, "box", 0, 1, 1)
    yl, yh = halo_from(field, "group", 1, 1, 1)
    return [
        jnp.concatenate([xl, field[:-1]], axis=0),
        jnp.concatenate([field[1:], xh], axis=0),
        jnp.concatenate([yl, field[:, :-1]], axis=1),
        jnp.concatenate([field[:, 1:], yh], axis=1),
        shift_z(field, -1),
        shift_z(field, 1),
    ]


def padded_neighbours(padded):
    return [
        padded[:-2, 1:-1, 1:-1],
        padded[2:, 1:-1, 1:-1],
        padded[1:-1, :-2, 1:-1],
        padded[1:-1, 2:, 1:-1],
        padded[1:-1, 1:-1, :-2],
        padded[1:-1, 1:-1, 2:],
    ]


def coefs_of(field, nears):
    return [jnp.where(near > 0, 2.0 * field * near / (field + near), field) for near in nears]


def apply_op(field, nears, coefs):
    total = jnp.zeros_like(field)
    for coef, near in zip(coefs, nears):
        total = total + coef * (field - near)
    return total


def group_matrix(n, k):
    rows = lax.broadcasted_iota(jnp.int32, (n, n // k), 0) // k
    cols = lax.broadcasted_iota(jnp.int32, (n, n // k), 1)
    return (rows == cols).astype(jnp.float32)


def block_mean(field):
    sx, sy, sz = field.shape
    fx = field.reshape(sx // 4, 4, sy, sz).sum(axis=1)
    fz = jnp.einsum("xyz,zc->xyc", fx, group_matrix(sz, 4), precision=HIGHEST)
    fy = jnp.einsum("xyc,yb->xbc", fz, group_matrix(sy, 4), precision=HIGHEST)
    return fy * (1.0 / 64.0)


def expand(coarse, shape):
    sx, sy, sz = shape
    cz = jnp.einsum("xbc,zc->xbz", coarse, group_matrix(sz, 4), precision=HIGHEST)
    cy = jnp.einsum("xbz,yb->xyz", cz, group_matrix(sy, 4), precision=HIGHEST)
    return jnp.broadcast_to(cy[:, None], (sx // 4, 4, sy, sz)).reshape(sx, sy, sz)


def inside_mask(shape, depth, totals):
    ex, ey, ez = shape
    cx, cy = ex - 2 * depth, ey - 2 * depth
    gx = lax.axis_index("box") * cx - depth + lax.broadcasted_iota(jnp.int32, shape, 0)
    gy = lax.axis_index("group") * cy - depth + lax.broadcasted_iota(jnp.int32, shape, 1)
    return (gx >= 0) & (gx < totals[0]) & (gy >= 0) & (gy < totals[1])


def chebyshev_local(rhs_c, b_c):
    depth = CHEB
    cx, cy, cz = rhs_c.shape
    both = jnp.stack([b_c, rhs_c])
    both = deep_extend(both, "box", 1, depth)
    both = deep_extend(both, "group", 2, depth)
    b_ext, rhs_ext = both[0], both[1]
    totals = (cx * lax.axis_size("box"), cy * lax.axis_size("group"))
    inside = inside_mask(b_ext.shape, depth, totals)
    coefs = [c * 0.0625 for c in coefs_of(b_ext, padded_neighbours(jnp.pad(b_ext, 1)))]
    diag = sum(coefs)
    inv_diag = jnp.where(inside, 1.0 / jnp.where(inside, diag, 1.0), 0.0)

    low, high = (0.05, 2.0)
    theta = (high + low) / 2.0
    delta = (high - low) / 2.0
    sigma = theta / delta
    rho = 1.0 / sigma
    solution = jnp.zeros_like(rhs_ext)
    remain = jnp.where(inside, rhs_ext, 0.0)
    direction = remain * inv_diag / theta
    for step in range(CHEB):
        solution = solution + direction
        if step + 1 < CHEB:
            nears = padded_neighbours(jnp.pad(direction, 1))
            remain = remain - apply_op(direction, nears, coefs)
            rho_next = 1.0 / (2.0 * sigma - rho)
            direction = rho_next * rho * direction + 2.0 * rho_next / delta * remain * inv_diag
            rho = rho_next
    return solution[depth:depth + cx, depth:depth + cy]


def per_device(right_side, inv_density, pressure):
    coefs = coefs_of(inv_density, fine_neighbours(inv_density))
    diag = sum(coefs)
    fine = pressure
    for sweep in range(SWEEPS):
        fine = fine + 2.0 / 3.0 * (right_side - apply_op(fine, fine_neighbours(fine), coefs)) / diag
    res = right_side - apply_op(fine, fine_neighbours(fine), coefs)
    coarse_rhs = block_mean(res)
    coarse_b = block_mean(inv_density)
    corr = chebyshev_local(coarse_rhs, coarse_b)
    return fine + expand(corr, fine.shape)


def solution(mesh):
    return jax.shard_map(
        per_device,
        mesh=mesh,
        in_specs=(P("box", "group", None), P("box", "group", None), P("box", "group", None)),
        out_specs=P("box", "group", None),
        check_vma=False,
    )
```

time: 331 us -> 121 us (0.37)
  starting transfers between devices: 167 us -> 75.7 us
  local copies, waits for them, and re-layouts: 80.6 us -> 9.19 us
  other arithmetic: 41 us -> 12.1 us
  waiting for transfers between devices: 39.1 us -> 19.6 us
    ppermute x48 -> x22, starting transfers between devices: 167 us -> 75.7 us  [the longest x11 47.4 us: halo_from(): lax.ppermute(lax.slice_in_dim(block, 0, width, axis=dim), axis, backward)]
    reshape x4 -> x0, local copies, waits for them, and re-layouts: 76.1 us -> none  [the longest x2 72.8 us: block_mean(): field.reshape(sx // 4, 4, sy // 4, 4, sz // 4, 4).mean(axis=(1, 3, 5))]
    reduce_sum x2, other arithmetic: 24.5 us -> 2.61 us  [block_mean(): fx = field.reshape(sx // 4, 4, sy, sz).sum(axis=1)]
    ppermute x48 -> x22, waiting for transfers between devices: 39.1 us -> 19.6 us  [the longest x11 18.4 us: halo_from(): lax.ppermute(lax.slice_in_dim(block, 0, width, axis=dim), axis, backward)]
    slice x14 -> x17, local copies, waits for them, and re-layouts: 1.93 us -> 9.14 us  [the longest x1 3.07 us: shift_z(): return jnp.concatenate([field[:, :, 1:], zeros], axis=2)]
    concatenate x13 -> x1, other arithmetic: 4.33 us -> 0.03 us  [deep_extend(): return jnp.concatenate(lows + [block] + highs, axis=dim)]
  transfers between devices with their start and end apart: 48 -> 22, of which waited for: 17 -> 6; matrix products, arithmetic and copies ran while one was open for 17% -> 6% of each run, Pallas kernels for 0% -> 0%
where the time goes in v1:
time: 121 us; the launch traced here: 119 us
  starting transfers between devices  75.7 us (63%)
  waiting for transfers between devices  19.6 us (16%)
  other arithmetic  12.1 us (10%)
  local copies, waits for them, and re-layouts  9.19 us (8%)
  matrix products  2.05 us (2%)
    ppermute x11, starting transfers between devices, halo_from(): lax.ppermute(lax.slice_in_dim(block, 0, width, axis=dim), axis, backward)  47.4 us
    ppermute x11, starting transfers between devices, halo_from(): lax.ppermute(lax.slice_in_dim(block, n - width, n, axis=dim), axis, forward)  28.2 us
    ppermute x11, waiting for transfers between devices, halo_from(): lax.ppermute(lax.slice_in_dim(block, 0, width, axis=dim), axis, backward)  18.4 us
    add x2, other arithmetic, per_device(): fine + 2.0 / 3.0 * (right_side - apply_op(fine, fine_neighbours(fine), co...  5.76 us
    slice x1, local copies, waits for them, and re-layouts, shift_z(): return jnp.concatenate([field[:, :, 1:], zeros], axis=2)  3.07 us
    reduce_sum x2, other arithmetic, block_mean(): fx = field.reshape(sx // 4, 4, sy, sz).sum(axis=1)  2.61 us
  transfers between devices with their start and end apart: 22, of which 6 were waited for; matrix products, arithmetic and copies ran while one was open for 6% of the time, Pallas kernels for 0%

profile of v1, /device:TPU:34, one launch (start us, length us, event | category | flops | bytes accessed | tf_op | source)
XLA Modules:
  0.0 119.2 jit_solution(18291635492255421998)
XLA Ops:
  0.0 0.9 fusion.216
  0.9 1.9 %collective-permute-start = (f32[1,32,512]{2,1,0:T(8,128)S(1)}, f32[1,32,512]{2,1,0:T(8,128)S(1)}, u32[]{:S(2)}, u32[]{:S(2)}) collective-permute-start(f32[1,32,512]{2,1,0:T(8,128)S(1)} %get-tuple-element.56), channel_id=1, source_target_pairs={{0,8},{8,16},{16,24},{24,32},{32,40},{40,48},{48,56},{56,64},{64,7... | collective-permute-start | bytes 196616 | tf_op jit(solution)/shard_map/ppermute | solution.py:25
  2.8 6.0 %collective-permute-start.2 = (f32[1,32,512]{2,1,0:T(8,128)S(1)}, f32[1,32,512]{2,1,0:T(8,128)S(1)}, u32[]{:S(2)}, u32[]{:S(2)}) collective-permute-start(f32[1,32,512]{2,1,0:T(8,128)S(1)} %get-tuple-element.55), channel_id=1, source_target_pairs={{8,0},{16,8},{24,16},{32,24},{40,32},{48,40},{56,48},{64,56},{72,6... | collective-permute-start | bytes 196616 | tf_op jit(solution)/shard_map/ppermute | solution.py:26
  8.9 1.1 fusion.213
  10.0 3.0 %collective-permute-start.4 = (f32[16,1,512]{2,1,0:T(1,128)S(1)}, f32[16,1,512]{2,1,0:T(1,128)S(1)}, u32[]{:S(2)}, u32[]{:S(2)}) collective-permute-start(f32[16,1,512]{2,1,0:T(1,128)S(1)} %get-tuple-element.49), channel_id=1, source_target_pairs={{0,1},{1,2},{2,3},{3,4},{4,5},{5,6},{6,7},{8,9},{9,10},{10,11},{11... | collective-permute-start | bytes 98312 | tf_op jit(solution)/shard_map/ppermute | solution.py:25
  13.0 1.1 fusion.220
  14.1 3.8 %collective-permute-start.5 = (f32[16,1,512]{2,1,0:T(1,128)S(1)}, f32[16,1,512]{2,1,0:T(1,128)S(1)}, u32[]{:S(2)}, u32[]{:S(2)}) collective-permute-start(f32[16,1,512]{2,1,0:T(1,128)S(1)} %get-tuple-element.64), channel_id=1, source_target_pairs={{0,1},{1,2},{2,3},{3,4},{4,5},{5,6},{6,7},{8,9},{9,10},{10,11},{11... | collective-permute-start | bytes 98312 | tf_op jit(solution)/shard_map/ppermute | solution.py:25
  17.9 2.0 %collective-permute-start.6 = (f32[16,1,512]{2,1,0:T(1,128)S(1)}, f32[16,1,512]{2,1,0:T(1,128)S(1)}, u32[]{:S(2)}, u32[]{:S(2)}) collective-permute-start(f32[16,1,512]{2,1,0:T(1,128)S(1)} %get-tuple-element.50), channel_id=1, source_target_pairs={{1,0},{2,1},{3,2},{4,3},{5,4},{6,5},{7,6},{9,8},{10,9},{11,10},{12... | collective-permute-start | bytes 98312 | tf_op jit(solution)/shard_map/ppermute | solution.py:26
  20.0 3.1 %fusion.217 = (f32[16,32,511]{2,1,0:T(8,128)S(1)}, f32[16,32,511]{2,1,0:T(8,128)S(1)}, f32[16,32,511]{2,1,0:T(8,128)S(1)}, f32[16,32,511]{2,1,0:T(8,128)S(1)}) fusion(f32[16,32,512]{2,1,0:T(8,128)} %param.4, f32[16,32,512]{2,1,0:T(8,128)} %param.5), kind=kLoop, calls=%fused_computation.322 | loop fusion | bytes 8372224 | tf_op jit(solution)/shard_map/slice | solution.py:48
  23.1 0.6 fusion.215
  23.7 0.6 fusion.214
  24.4 0.5 fusion.182
  25.0 1.9 %collective-permute-start.1 = (f32[1,32,512]{2,1,0:T(8,128)S(1)}, f32[1,32,512]{2,1,0:T(8,128)S(1)}, u32[]{:S(2)}, u32[]{:S(2)}) collective-permute-start(f32[1,32,512]{2,1,0:T(8,128)S(1)} %get-tuple-element.68), channel_id=1, source_target_pairs={{0,8},{8,16},{16,24},{24,32},{32,40},{40,48},{48,56},{56,64},{64,7... | collective-permute-start | bytes 196616 | tf_op jit(solution)/shard_map/ppermute | solution.py:25
  26.9 6.0 %collective-permute-start.3 = (f32[1,32,512]{2,1,0:T(8,128)S(1)}, f32[1,32,512]{2,1,0:T(8,128)S(1)}, u32[]{:S(2)}, u32[]{:S(2)}) collective-permute-start(f32[1,32,512]{2,1,0:T(8,128)S(1)} %get-tuple-element.67), channel_id=1, source_target_pairs={{8,0},{16,8},{24,16},{32,24},{40,32},{48,40},{56,48},{64,56},{72,6... | collective-permute-start | bytes 196616 | tf_op jit(solution)/shard_map/ppermute | solution.py:26
  33.0 1.9 %collective-permute-start.7 = (f32[16,1,512]{2,1,0:T(1,128)S(1)}, f32[16,1,512]{2,1,0:T(1,128)S(1)}, u32[]{:S(2)}, u32[]{:S(2)}) collective-permute-start(f32[16,1,512]{2,1,0:T(1,128)S(1)} %get-tuple-element.63), channel_id=1, source_target_pairs={{1,0},{2,1},{3,2},{4,3},{5,4},{6,5},{7,6},{9,8},{10,9},{11,10},{12... | collective-permute-start | bytes 98312 | tf_op jit(solution)/shard_map/ppermute | solution.py:26
  35.0 4.6 %collective-permute-done.7 = f32[16,1,512]{2,1,0:T(1,128)S(1)} collective-permute-done((f32[16,1,512]{2,1,0:T(1,128)S(1)}, f32[16,1,512]{2,1,0:T(1,128)S(1)}, u32[]{:S(2)}, u32[]{:S(2)}) %collective-permute-start.7) | collective-permute-done | bytes 32800 | tf_op jit(solution)/shard_map/ppermute | solution.py:26
  39.7 3.2 %fusion.11 = (f32[16,32,512]{2,1,0:T(8,128)S(1)}, f32[16,32,512]{2,1,0:T(8,128)S(1)}, f32[16,32,512]{2,1,0:T(8,128)S(1)}) fusion(f32[16,32,512]{2,1,0:T(8,128)S(1)} %copy-done.1, f32[16,32,512]{2,1,0:T(8,128)S(1)} %copy-done.2, f32[15,32,512]{2,1,0:T(8,128)S(1)} %get-tuple-element.73, f32[1,32,512]{2,1,0:T(8,128)S(1)} %collective-permute-done.1, ...), kind=kLoop, calls=%fused_computation.64 | loop fusion | flops 17039360 | bytes 18866176 | tf_op jit(solution)/shard_map/add | solution.py:152
  42.9 0.4 fusion.208
  43.6 1.9 %collective-permute-start.8 = (f32[1,32,512]{2,1,0:T(8,128)S(1)}, f32[1,32,512]{2,1,0:T(8,128)S(1)}, u32[]{:S(2)}, u32[]{:S(2)}) collective-permute-start(f32[1,32,512]{2,1,0:T(8,128)S(1)} %get-tuple-element.48), channel_id=1, source_target_pairs={{0,8},{8,16},{16,24},{24,32},{32,40},{40,48},{48,56},{56,64},{64,7... | collective-permute-start | bytes 196616 | tf_op jit(solution)/shard_map/ppermute | solution.py:25
  45.5 6.0 %collective-permute-start.9 = (f32[1,32,512]{2,1,0:T(8,128)S(1)}, f32[1,32,512]{2,1,0:T(8,128)S(1)}, u32[]{:S(2)}, u32[]{:S(2)}) collective-permute-start(f32[1,32,512]{2,1,0:T(8,128)S(1)} %get-tuple-element.47), channel_id=1, source_target_pairs={{8,0},{16,8},{24,16},{32,24},{40,32},{48,40},{56,48},{64,56},{72,6... | collective-permute-start | bytes 196616 | tf_op jit(solution)/shard_map/ppermute | solution.py:26
  51.6 3.8 %collective-permute-start.10 = (f32[16,1,512]{2,1,0:T(1,128)S(1)}, f32[16,1,512]{2,1,0:T(1,128)S(1)}, u32[]{:S(2)}, u32[]{:S(2)}) collective-permute-start(f32[16,1,512]{2,1,0:T(1,128)S(1)} %get-tuple-element.44), channel_id=1, source_target_pairs={{0,1},{1,2},{2,3},{3,4},{4,5},{5,6},{6,7},{8,9},{9,10},{10,11},{11... | collective-permute-start | bytes 98312 | tf_op jit(solution)/shard_map/ppermute | solution.py:25
  55.4 2.0 %collective-permute-start.11 = (f32[16,1,512]{2,1,0:T(1,128)S(1)}, f32[16,1,512]{2,1,0:T(1,128)S(1)}, u32[]{:S(2)}, u32[]{:S(2)}) collective-permute-start(f32[16,1,512]{2,1,0:T(1,128)S(1)} %get-tuple-element.43), channel_id=1, source_target_pairs={{1,0},{2,1},{3,2},{4,3},{5,4},{6,5},{7,6},{9,8},{10,9},{11,10},{12... | collective-permute-start | bytes 98312 | tf_op jit(solution)/shard_map/ppermute | solution.py:26
  57.7 4.4 %collective-permute-done.11 = f32[16,1,512]{2,1,0:T(1,128)S(1)} collective-permute-done((f32[16,1,512]{2,1,0:T(1,128)S(1)}, f32[16,1,512]{2,1,0:T(1,128)S(1)}, u32[]{:S(2)}, u32[]{:S(2)}) %collective-permute-start.11) | collective-permute-done | bytes 32800 | tf_op jit(solution)/shard_map/ppermute | solution.py:26
  62.1 2.6 %fusion.24 = f32[16,32,512]{2,1,0:T(8,128)S(1)} fusion(f32[16,32,512]{2,1,0:T(8,128)S(1)} %get-tuple-element.26, f32[16,32,512]{2,1,0:T(8,128)S(1)} %copy-done.2, f32[15,32,512]{2,1,0:T(8,128)S(1)} %get-tuple-element.46, f32[1,32,512]{2,1,0:T(8,128)S(1)} %collective-permute-done.8, f32[1,32,512]{2,1,0:T(8,128)S(1)} %collective-permute-done.9, ...), kind=kLoop, calls=%fused_computation.84 | loop fusion | flops 13893632 | bytes 16769024 | tf_op jit(solution)/shard_map/add | solution.py:152
  64.9 0.4 fusion.207
  65.4 1.9 %collective-permute-start.12 = (f32[1,32,512]{2,1,0:T(8,128)S(1)}, f32[1,32,512]{2,1,0:T(8,128)S(1)}, u32[]{:S(2)}, u32[]{:S(2)}) collective-permute-start(f32[1,32,512]{2,1,0:T(8,128)S(1)} %get-tuple-element.29), channel_id=1, source_target_pairs={{0,8},{8,16},{16,24},{24,32},{32,40},{40,48},{48,56},{56,64},{64,7... | collective-permute-start | bytes 196616 | tf_op jit(solution)/shard_map/ppermute | solution.py:25
  67.3 6.0 %collective-permute-start.13 = (f32[1,32,512]{2,1,0:T(8,128)S(1)}, f32[1,32,512]{2,1,0:T(8,128)S(1)}, u32[]{:S(2)}, u32[]{:S(2)}) collective-permute-start(f32[1,32,512]{2,1,0:T(8,128)S(1)} %get-tuple-element.30), channel_id=1, source_target_pairs={{8,0},{16,8},{24,16},{32,24},{40,32},{48,40},{56,48},{64,56},{72,6... | collective-permute-start | bytes 196616 | tf_op jit(solution)/shard_map/ppermute | solution.py:26
  73.4 2.1 %collective-permute-start.14 = (f32[16,1,512]{2,1,0:T(1,128)S(1)}, f32[16,1,512]{2,1,0:T(1,128)S(1)}, u32[]{:S(2)}, u32[]{:S(2)}) collective-permute-start(f32[16,1,512]{2,1,0:T(1,128)S(1)} %get-tuple-element.33), channel_id=1, source_target_pairs={{0,1},{1,2},{2,3},{3,4},{4,5},{5,6},{6,7},{8,9},{9,10},{10,11},{11... | collective-permute-start | bytes 98312 | tf_op jit(solution)/shard_map/ppermute | solution.py:25
  75.5 3.7 %collective-permute-start.15 = (f32[16,1,512]{2,1,0:T(1,128)S(1)}, f32[16,1,512]{2,1,0:T(1,128)S(1)}, u32[]{:S(2)}, u32[]{:S(2)}) collective-permute-start(f32[16,1,512]{2,1,0:T(1,128)S(1)} %get-tuple-element.34), channel_id=1, source_target_pairs={{1,0},{2,1},{3,2},{4,3},{5,4},{6,5},{7,6},{9,8},{10,9},{11,10},{12... | collective-permute-start | bytes 98312 | tf_op jit(solution)/shard_map/ppermute | solution.py:26
  79.5 2.7 %collective-permute-done.15 = f32[16,1,512]{2,1,0:T(1,128)S(1)} collective-permute-done((f32[16,1,512]{2,1,0:T(1,128)S(1)}, f32[16,1,512]{2,1,0:T(1,128)S(1)}, u32[]{:S(2)}, u32[]{:S(2)}) %collective-permute-start.15) | collective-permute-done | bytes 32800 | tf_op jit(solution)/shard_map/ppermute | solution.py:26
  82.2 2.5 %bitcast_reduce_fusion = f32[4,32,512]{2,1,0:T(8,128)S(1)} fusion(f32[16,32,512]{2,1,0:T(8,128)S(1)} %copy-done.2, f32[16,32,512]{2,1,0:T(8,128)S(1)} %fusion.24, f32[16,32,511]{2,1,0:T(8,128)S(1)} %get-tuple-element.38, f32[16,32,511]{2,1,0:T(8,128)S(1)} %get-tuple-element.37, f32[16,32,512]{2,1,0:T(8,128)S(1)} %get-tuple-element.27, ...), kind=kLoop, calls=%fused_computation.106 | loop fusion | flops 11993088 | bytes 15982592 | tf_op jit(solution)/shard_map/reduce_sum | solution.py:94
  84.8 0.5 fusion.180
  85.4 1.9 %collective-permute-start.16 = (f32[2,4,8,128]{3,2,1,0:T(8,128)S(1)}, f32[2,4,8,128]{3,2,1,0:T(8,128)S(1)}, u32[]{:S(2)}, u32[]{:S(2)}) collective-permute-start(f32[2,4,8,128]{3,2,1,0:T(8,128)S(1)} %pad_maximum_fusion.5), channel_id=1, source_target_pairs={{0,16},{8,24},{16,32},{24,40},{32,48},{40,56},{48,64},{56,72},{64,... | collective-permute-start | bytes 98312 | tf_op jit(solution)/shard_map/ppermute | solution.py:25
  87.3 1.9 %collective-permute-start.17 = (f32[2,4,8,128]{3,2,1,0:T(8,128)S(1)}, f32[2,4,8,128]{3,2,1,0:T(8,128)S(1)}, u32[]{:S(2)}, u32[]{:S(2)}) collective-permute-start(f32[2,4,8,128]{3,2,1,0:T(8,128)S(1)} %pad_maximum_fusion.5), channel_id=1, source_target_pairs={{0,8},{8,16},{16,24},{24,32},{32,40},{40,48},{48,56},{56,64},{64,7... | collective-permute-start | bytes 98312 | tf_op jit(solution)/shard_map/ppermute | solution.py:25
  89.3 6.0 %collective-permute-start.18 = (f32[2,4,8,128]{3,2,1,0:T(8,128)S(1)}, f32[2,4,8,128]{3,2,1,0:T(8,128)S(1)}, u32[]{:S(2)}, u32[]{:S(2)}) collective-permute-start(f32[2,4,8,128]{3,2,1,0:T(8,128)S(1)} %pad_maximum_fusion.5), channel_id=1, source_target_pairs={{8,0},{16,8},{24,16},{32,24},{40,32},{48,40},{56,48},{64,56},{72,6... | collective-permute-start | bytes 98312 | tf_op jit(solution)/shard_map/ppermute | solution.py:26
  95.3 5.4 %collective-permute-start.19 = (f32[2,4,8,128]{3,2,1,0:T(8,128)S(1)}, f32[2,4,8,128]{3,2,1,0:T(8,128)S(1)}, u32[]{:S(2)}, u32[]{:S(2)}) collective-permute-start(f32[2,4,8,128]{3,2,1,0:T(8,128)S(1)} %pad_maximum_fusion.5), channel_id=1, source_target_pairs={{16,0},{24,8},{32,16},{40,24},{48,32},{56,40},{64,48},{72,56},{80,... | collective-permute-start | bytes 98312 | tf_op jit(solution)/shard_map/ppermute | solution.py:26
  100.8 1.8 %collective-permute-done.19 = f32[2,4,8,128]{3,2,1,0:T(8,128)S(1)} collective-permute-done((f32[2,4,8,128]{3,2,1,0:T(8,128)S(1)}, f32[2,4,8,128]{3,2,1,0:T(8,128)S(1)}, u32[]{:S(2)}, u32[]{:S(2)}) %collective-permute-start.19) | collective-permute-done | bytes 32800 | tf_op jit(solution)/shard_map/ppermute | solution.py:26
  102.7 3.9 %collective-permute-start.20 = (f32[2,20,8,128]{3,2,1,0:T(8,128)S(1)}, f32[2,20,8,128]{3,2,1,0:T(8,128)S(1)}, u32[]{:S(2)}, u32[]{:S(2)}) collective-permute-start(f32[2,20,8,128]{3,2,1,0:T(8,128)S(1)} %constant_dynamic-update-slice_fusion), channel_id=1, source_target_pairs={{0,1},{1,2},{2,3},{3,4},{4,5},{5,6},{6,7},{8,9},{9,10},{10,11},{11... | collective-permute-start | bytes 491528 | tf_op jit(solution)/shard_map/ppermute | solution.py:25
  106.6 2.1 %collective-permute-start.21 = (f32[2,20,8,128]{3,2,1,0:T(8,128)S(1)}, f32[2,20,8,128]{3,2,1,0:T(8,128)S(1)}, u32[]{:S(2)}, u32[]{:S(2)}) collective-permute-start(f32[2,20,8,128]{3,2,1,0:T(8,128)S(1)} %constant_dynamic-update-slice_fusion), channel_id=1, source_target_pairs={{1,0},{2,1},{3,2},{4,3},{5,4},{6,5},{7,6},{9,8},{10,9},{11,10},{12... | collective-permute-start | bytes 491528 | tf_op jit(solution)/shard_map/ppermute | solution.py:26
  108.7 1.2 collective-permute-done.20
  109.9 4.8 %collective-permute-done.21 = f32[2,20,8,128]{3,2,1,0:T(8,128)S(1)} collective-permute-done((f32[2,20,8,128]{3,2,1,0:T(8,128)S(1)}, f32[2,20,8,128]{3,2,1,0:T(8,128)S(1)}, u32[]{:S(2)}, u32[]{:S(2)}) %collective-permute-start.21) | collective-permute-done | bytes 163872 | tf_op jit(solution)/shard_map/ppermute | solution.py:26
  114.8 0.5 fusion.165
  115.3 0.3 fusion.166
  116.2 0.3 multiply_add_fusion.2
  116.7 0.3 multiply_add_fusion
  117.2 0.5 fusion.169
  117.7 0.3 convolution_bitcast_fusion
  118.0 1.1 bitcast_add_fusion
  (52 shorter events, 2.6 us)
Async XLA Ops:
  0.9 38.8 %collective-permute-start = (f32[1,32,512]{2,1,0:T(8,128)S(1)}, f32[1,32,512]{2,1,0:T(8,128)S(1)}, u32[]{:S(2)}, u32[]{:S(2)}) collective-permute-start(f32[1,32,512]{2,1,0:T(8,128)S(1)} %get-tuple-element.56), channel_id=1, source_target_pairs={{0,8},{8,16},{16,24},{24,32},{32,40},{40,48},{48,56},{56,64},{64,7... | collective-permute-start | bytes 196616 | tf_op jit(solution)/shard_map/ppermute | solution.py:25
  2.8 36.9 %collective-permute-start.2 = (f32[1,32,512]{2,1,0:T(8,128)S(1)}, f32[1,32,512]{2,1,0:T(8,128)S(1)}, u32[]{:S(2)}, u32[]{:S(2)}) collective-permute-start(f32[1,32,512]{2,1,0:T(8,128)S(1)} %get-tuple-element.55), channel_id=1, source_target_pairs={{8,0},{16,8},{24,16},{32,24},{40,32},{48,40},{56,48},{64,56},{72,6... | collective-permute-start | bytes 196616 | tf_op jit(solution)/shard_map/ppermute | solution.py:26
  10.0 15.0 %collective-permute-start.4 = (f32[16,1,512]{2,1,0:T(1,128)S(1)}, f32[16,1,512]{2,1,0:T(1,128)S(1)}, u32[]{:S(2)}, u32[]{:S(2)}) collective-permute-start(f32[16,1,512]{2,1,0:T(1,128)S(1)} %get-tuple-element.49), channel_id=1, source_target_pairs={{0,1},{1,2},{2,3},{3,4},{4,5},{5,6},{6,7},{8,9},{9,10},{10,11},{11... | collective-permute-start | bytes 98312 | tf_op jit(solution)/shard_map/ppermute | solution.py:25
  14.1 12.8 %collective-permute-start.5 = (f32[16,1,512]{2,1,0:T(1,128)S(1)}, f32[16,1,512]{2,1,0:T(1,128)S(1)}, u32[]{:S(2)}, u32[]{:S(2)}) collective-permute-start(f32[16,1,512]{2,1,0:T(1,128)S(1)} %get-tuple-element.64), channel_id=1, source_target_pairs={{0,1},{1,2},{2,3},{3,4},{4,5},{5,6},{6,7},{8,9},{9,10},{10,11},{11... | collective-permute-start | bytes 98312 | tf_op jit(solution)/shard_map/ppermute | solution.py:25
  17.9 15.0 %collective-permute-start.6 = (f32[16,1,512]{2,1,0:T(1,128)S(1)}, f32[16,1,512]{2,1,0:T(1,128)S(1)}, u32[]{:S(2)}, u32[]{:S(2)}) collective-permute-start(f32[16,1,512]{2,1,0:T(1,128)S(1)} %get-tuple-element.50), channel_id=1, source_target_pairs={{1,0},{2,1},{3,2},{4,3},{5,4},{6,5},{7,6},{9,8},{10,9},{11,10},{12... | collective-permute-start | bytes 98312 | tf_op jit(solution)/shard_map/ppermute | solution.py:26
  19.9 3.1 %copy-start = (f32[16,32,512]{2,1,0:T(8,128)S(1)}, f32[16,32,512]{2,1,0:T(8,128)}, u32[]{:S(2)}) copy-start(f32[16,32,512]{2,1,0:T(8,128)} %param.4) | copy-start | bytes 3145732
  19.9 3.1 %copy-start.1 = (f32[16,32,512]{2,1,0:T(8,128)S(1)}, f32[16,32,512]{2,1,0:T(8,128)}, u32[]{:S(2)}) copy-start(f32[16,32,512]{2,1,0:T(8,128)} %param.5) | copy-start | bytes 3145732
  24.3 15.4 %copy-start.2 = (f32[16,32,512]{2,1,0:T(8,128)S(1)}, f32[16,32,512]{2,1,0:T(8,128)}, u32[]{:S(2)}) copy-start(f32[16,32,512]{2,1,0:T(8,128)} %param.3) | copy-start | bytes 3145732
  25.0 14.7 %collective-permute-start.1 = (f32[1,32,512]{2,1,0:T(8,128)S(1)}, f32[1,32,512]{2,1,0:T(8,128)S(1)}, u32[]{:S(2)}, u32[]{:S(2)}) collective-permute-start(f32[1,32,512]{2,1,0:T(8,128)S(1)} %get-tuple-element.68), channel_id=1, source_target_pairs={{0,8},{8,16},{16,24},{24,32},{32,40},{40,48},{48,56},{56,64},{64,7... | collective-permute-start | bytes 196616 | tf_op jit(solution)/shard_map/ppermute | solution.py:25
  26.9 12.8 %collective-permute-start.3 = (f32[1,32,512]{2,1,0:T(8,128)S(1)}, f32[1,32,512]{2,1,0:T(8,128)S(1)}, u32[]{:S(2)}, u32[]{:S(2)}) collective-permute-start(f32[1,32,512]{2,1,0:T(8,128)S(1)} %get-tuple-element.67), channel_id=1, source_target_pairs={{8,0},{16,8},{24,16},{32,24},{40,32},{48,40},{56,48},{64,56},{72,6... | collective-permute-start | bytes 196616 | tf_op jit(solution)/shard_map/ppermute | solution.py:26
  33.0 6.7 %collective-permute-start.7 = (f32[16,1,512]{2,1,0:T(1,128)S(1)}, f32[16,1,512]{2,1,0:T(1,128)S(1)}, u32[]{:S(2)}, u32[]{:S(2)}) collective-permute-start(f32[16,1,512]{2,1,0:T(1,128)S(1)} %get-tuple-element.63), channel_id=1, source_target_pairs={{1,0},{2,1},{3,2},{4,3},{5,4},{6,5},{7,6},{9,8},{10,9},{11,10},{12... | collective-permute-start | bytes 98312 | tf_op jit(solution)/shard_map/ppermute | solution.py:26
  43.6 18.5 %collective-permute-start.8 = (f32[1,32,512]{2,1,0:T(8,128)S(1)}, f32[1,32,512]{2,1,0:T(8,128)S(1)}, u32[]{:S(2)}, u32[]{:S(2)}) collective-permute-start(f32[1,32,512]{2,1,0:T(8,128)S(1)} %get-tuple-element.48), channel_id=1, source_target_pairs={{0,8},{8,16},{16,24},{24,32},{32,40},{40,48},{48,56},{56,64},{64,7... | collective-permute-start | bytes 196616 | tf_op jit(solution)/shard_map/ppermute | solution.py:25
  45.5 16.6 %collective-permute-start.9 = (f32[1,32,512]{2,1,0:T(8,128)S(1)}, f32[1,32,512]{2,1,0:T(8,128)S(1)}, u32[]{:S(2)}, u32[]{:S(2)}) collective-permute-start(f32[1,32,512]{2,1,0:T(8,128)S(1)} %get-tuple-element.47), channel_id=1, source_target_pairs={{8,0},{16,8},{24,16},{32,24},{40,32},{48,40},{56,48},{64,56},{72,6... | collective-permute-start | bytes 196616 | tf_op jit(solution)/shard_map/ppermute | solution.py:26
  51.6 6.1 %collective-permute-start.10 = (f32[16,1,512]{2,1,0:T(1,128)S(1)}, f32[16,1,512]{2,1,0:T(1,128)S(1)}, u32[]{:S(2)}, u32[]{:S(2)}) collective-permute-start(f32[16,1,512]{2,1,0:T(1,128)S(1)} %get-tuple-element.44), channel_id=1, source_target_pairs={{0,1},{1,2},{2,3},{3,4},{4,5},{5,6},{6,7},{8,9},{9,10},{10,11},{11... | collective-permute-start | bytes 98312 | tf_op jit(solution)/shard_map/ppermute | solution.py:25
  55.4 6.7 %collective-permute-start.11 = (f32[16,1,512]{2,1,0:T(1,128)S(1)}, f32[16,1,512]{2,1,0:T(1,128)S(1)}, u32[]{:S(2)}, u32[]{:S(2)}) collective-permute-start(f32[16,1,512]{2,1,0:T(1,128)S(1)} %get-tuple-element.43), channel_id=1, source_target_pairs={{1,0},{2,1},{3,2},{4,3},{5,4},{6,5},{7,6},{9,8},{10,9},{11,10},{12... | collective-permute-start | bytes 98312 | tf_op jit(solution)/shard_map/ppermute | solution.py:26
  65.4 16.8 %collective-permute-start.12 = (f32[1,32,512]{2,1,0:T(8,128)S(1)}, f32[1,32,512]{2,1,0:T(8,128)S(1)}, u32[]{:S(2)}, u32[]{:S(2)}) collective-permute-start(f32[1,32,512]{2,1,0:T(8,128)S(1)} %get-tuple-element.29), channel_id=1, source_target_pairs={{0,8},{8,16},{16,24},{24,32},{32,40},{40,48},{48,56},{56,64},{64,7... | collective-permute-start | bytes 196616 | tf_op jit(solution)/shard_map/ppermute | solution.py:25
  67.3 14.9 %collective-permute-start.13 = (f32[1,32,512]{2,1,0:T(8,128)S(1)}, f32[1,32,512]{2,1,0:T(8,128)S(1)}, u32[]{:S(2)}, u32[]{:S(2)}) collective-permute-start(f32[1,32,512]{2,1,0:T(8,128)S(1)} %get-tuple-element.30), channel_id=1, source_target_pairs={{8,0},{16,8},{24,16},{32,24},{40,32},{48,40},{56,48},{64,56},{72,6... | collective-permute-start | bytes 196616 | tf_op jit(solution)/shard_map/ppermute | solution.py:26
  73.4 6.1 %collective-permute-start.14 = (f32[16,1,512]{2,1,0:T(1,128)S(1)}, f32[16,1,512]{2,1,0:T(1,128)S(1)}, u32[]{:S(2)}, u32[]{:S(2)}) collective-permute-start(f32[16,1,512]{2,1,0:T(1,128)S(1)} %get-tuple-element.33), channel_id=1, source_target_pairs={{0,1},{1,2},{2,3},{3,4},{4,5},{5,6},{6,7},{8,9},{9,10},{10,11},{11... | collective-permute-start | bytes 98312 | tf_op jit(solution)/shard_map/ppermute | solution.py:25
  75.5 6.7 %collective-permute-start.15 = (f32[16,1,512]{2,1,0:T(1,128)S(1)}, f32[16,1,512]{2,1,0:T(1,128)S(1)}, u32[]{:S(2)}, u32[]{:S(2)}) collective-permute-start(f32[16,1,512]{2,1,0:T(1,128)S(1)} %get-tuple-element.34), channel_id=1, source_target_pairs={{1,0},{2,1},{3,2},{4,3},{5,4},{6,5},{7,6},{9,8},{10,9},{11,10},{12... | collective-permute-start | bytes 98312 | tf_op jit(solution)/shard_map/ppermute | solution.py:26
  85.4 15.3 %collective-permute-start.16 = (f32[2,4,8,128]{3,2,1,0:T(8,128)S(1)}, f32[2,4,8,128]{3,2,1,0:T(8,128)S(1)}, u32[]{:S(2)}, u32[]{:S(2)}) collective-permute-start(f32[2,4,8,128]{3,2,1,0:T(8,128)S(1)} %pad_maximum_fusion.5), channel_id=1, source_target_pairs={{0,16},{8,24},{16,32},{24,40},{32,48},{40,56},{48,64},{56,72},{64,... | collective-permute-start | bytes 98312 | tf_op jit(solution)/shard_map/ppermute | solution.py:25
  87.3 13.4 %collective-permute-start.17 = (f32[2,4,8,128]{3,2,1,0:T(8,128)S(1)}, f32[2,4,8,128]{3,2,1,0:T(8,128)S(1)}, u32[]{:S(2)}, u32[]{:S(2)}) collective-permute-start(f32[2,4,8,128]{3,2,1,0:T(8,128)S(1)} %pad_maximum_fusion.5), channel_id=1, source_target_pairs={{0,8},{8,16},{16,24},{24,32},{32,40},{40,48},{48,56},{56,64},{64,7... | collective-permute-start | bytes 98312 | tf_op jit(solution)/shard_map/ppermute | solution.py:25
  89.3 11.5 %collective-permute-start.18 = (f32[2,4,8,128]{3,2,1,0:T(8,128)S(1)}, f32[2,4,8,128]{3,2,1,0:T(8,128)S(1)}, u32[]{:S(2)}, u32[]{:S(2)}) collective-permute-start(f32[2,4,8,128]{3,2,1,0:T(8,128)S(1)} %pad_maximum_fusion.5), channel_id=1, source_target_pairs={{8,0},{16,8},{24,16},{32,24},{40,32},{48,40},{56,48},{64,56},{72,6... | collective-permute-start | bytes 98312 | tf_op jit(solution)/shard_map/ppermute | solution.py:26
  95.3 7.3 %collective-permute-start.19 = (f32[2,4,8,128]{3,2,1,0:T(8,128)S(1)}, f32[2,4,8,128]{3,2,1,0:T(8,128)S(1)}, u32[]{:S(2)}, u32[]{:S(2)}) collective-permute-start(f32[2,4,8,128]{3,2,1,0:T(8,128)S(1)} %pad_maximum_fusion.5), channel_id=1, source_target_pairs={{16,0},{24,8},{32,16},{40,24},{48,32},{56,40},{64,48},{72,56},{80,... | collective-permute-start | bytes 98312 | tf_op jit(solution)/shard_map/ppermute | solution.py:26
  102.7 7.2 %collective-permute-start.20 = (f32[2,20,8,128]{3,2,1,0:T(8,128)S(1)}, f32[2,20,8,128]{3,2,1,0:T(8,128)S(1)}, u32[]{:S(2)}, u32[]{:S(2)}) collective-permute-start(f32[2,20,8,128]{3,2,1,0:T(8,128)S(1)} %constant_dynamic-update-slice_fusion), channel_id=1, source_target_pairs={{0,1},{1,2},{2,3},{3,4},{4,5},{5,6},{6,7},{8,9},{9,10},{10,11},{11... | collective-permute-start | bytes 491528 | tf_op jit(solution)/shard_map/ppermute | solution.py:25
  106.6 8.1 %collective-permute-start.21 = (f32[2,20,8,128]{3,2,1,0:T(8,128)S(1)}, f32[2,20,8,128]{3,2,1,0:T(8,128)S(1)}, u32[]{:S(2)}, u32[]{:S(2)}) collective-permute-start(f32[2,20,8,128]{3,2,1,0:T(8,128)S(1)} %constant_dynamic-update-slice_fusion), channel_id=1, source_target_pairs={{1,0},{2,1},{3,2},{4,3},{5,4},{6,5},{7,6},{9,8},{10,9},{11,10},{12... | collective-permute-start | bytes 491528 | tf_op jit(solution)/shard_map/ppermute | solution.py:26

commit v2 on v1

--- a/solution.py
+++ b/solution.py
@@ -144,13 +144,33 @@
     return solution[depth:depth + cx, depth:depth + cy]
 
 
+def grid_mask(shape, depth, axes, totals):
+    inside = None
+    for dim, (axis, total) in enumerate(zip(axes, totals)):
+        own = shape[dim] - 2 * depth
+        g = lax.axis_index(axis) * own - depth + lax.broadcasted_iota(jnp.int32, shape, dim)
+        ok = (g >= 0) & (g < total)
+        inside = ok if inside is None else inside & ok
+    return inside
+
+
 def per_device(right_side, inv_density, pressure):
-    coefs = coefs_of(inv_density, fine_neighbours(inv_density))
+    depth = SWEEPS + 1
+    sx, sy, sz = pressure.shape
+    both = jnp.stack([right_side, inv_density, pressure])
+    both = deep_extend(both, "box", 1, depth)
+    both = deep_extend(both, "group", 2, depth)
+    rhs_e, b_e, fine = both[0], both[1], both[2]
+    totals = (sx * lax.axis_size("box"), sy * lax.axis_size("group"))
+    inside = grid_mask(fine.shape, depth, ("box", "group"), totals)
+    coefs = coefs_of(b_e, padded_neighbours(jnp.pad(b_e, 1)))
     diag = sum(coefs)
-    fine = pressure
     for sweep in range(SWEEPS):
-        fine = fine + 2.0 / 3.0 * (right_side - apply_op(fine, fine_neighbours(fine), coefs)) / diag
-    res = right_side - apply_op(fine, fine_neighbours(fine), coefs)
+        step = 2.0 / 3.0 * (rhs_e - apply_op(fine, padded_neighbours(jnp.pad(fine, 1)), coefs)) / diag
+        fine = jnp.where(inside, fine + step, 0.0)
+    res = rhs_e - apply_op(fine, padded_neighbours(jnp.pad(fine, 1)), coefs)
+    own = (slice(depth, depth + sx), slice(depth, depth + sy))
+    fine, res = fine[own], res[own]
     coarse_rhs = block_mean(res)
     coarse_b = block_mean(inv_density)
     corr = chebyshev_local(coarse_rhs, coarse_b)

time: 121 us -> 114 us (0.942); the launches traced: 119 us -> 114 us
  starting transfers between devices: 75.7 us -> 38.9 us
  other arithmetic: 12.1 us -> 37 us
  waiting for transfers between devices: 19.6 us -> 32.8 us
  local copies, waits for them, and re-layouts: 9.19 us -> 2.75 us
    ppermute x11 -> x5, starting transfers between devices: 47.4 us -> 19.2 us  [halo_from(): lax.ppermute(lax.slice_in_dim(block, 0, width, axis=dim), axis, backward)]
    ppermute x11 -> x5, waiting for transfers between devices: 1.21 us -> 22.1 us  [halo_from(): lax.ppermute(lax.slice_in_dim(block, n - width, n, axis=dim), axis, forward)]
    select_n x0 -> x2, other arithmetic: none -> 18.4 us  [per_device(): fine = jnp.where(inside, fine + step, 0.0)]
    ppermute x11 -> x5, starting transfers between devices: 28.2 us -> 19.6 us  [halo_from(): lax.ppermute(lax.slice_in_dim(block, n - width, n, axis=dim), axis, forward)]
    ppermute x11 -> x5, waiting for transfers between devices: 18.4 us -> 10.7 us  [halo_from(): lax.ppermute(lax.slice_in_dim(block, 0, width, axis=dim), axis, backward)]
    slice x9 -> x0, local copies, waits for them, and re-layouts: 5.95 us -> none  [the longest x1 3.07 us: shift_z(): return jnp.concatenate([field[:, :, 1:], zeros], axis=2)]
    add x2 -> x0, other arithmetic: 5.76 us -> none  [per_device(): fine + 2.0 / 3.0 * (right_side - apply_op(fine, fine_neighbours(fine), co...]
    slice x0 -> x2, other arithmetic: none -> 4.03 us  [halo_from(): lax.slice_in_dim(block, n - width, n, axis=dim)]
  transfers between devices with their start and end apart: 22 -> 10, of which waited for: 6 -> 6; matrix products, arithmetic and copies ran while one was open for 6% -> 1% of each run, Pallas kernels for 0% -> 0%
where the time goes in v2:
time: 114 us
  starting transfers between devices  38.9 us (34%)
  other arithmetic  37 us (32%)
  waiting for transfers between devices  32.8 us (29%)
  local copies, waits for them, and re-layouts  2.75 us (2%)
  matrix products  2.04 us (2%)
    ppermute x5, waiting for transfers between devices, halo_from(): lax.ppermute(lax.slice_in_dim(block, n - width, n, axis=dim), axis, forward)  22.1 us
    ppermute x5, starting transfers between devices, halo_from(): lax.ppermute(lax.slice_in_dim(block, n - width, n, axis=dim), axis, forward)  19.6 us
    ppermute x5, starting transfers between devices, halo_from(): lax.ppermute(lax.slice_in_dim(block, 0, width, axis=dim), axis, backward)  19.2 us
    select_n x2, other arithmetic, per_device(): fine = jnp.where(inside, fine + step, 0.0)  18.4 us
    ppermute x5, waiting for transfers between devices, halo_from(): lax.ppermute(lax.slice_in_dim(block, 0, width, axis=dim), axis, backward)  10.7 us
    reduce_sum x2, other arithmetic, block_mean(): fx = field.reshape(sx // 4, 4, sy, sz).sum(axis=1)  5.05 us
    slice x2, other arithmetic, halo_from(): lax.slice_in_dim(block, n - width, n, axis=dim)  4.03 us
    mul x1, other arithmetic, apply_op(): total = total + coef * (field - near)  3.51 us
  transfers between devices with their start and end apart: 10, of which 6 were waited for; matrix products, arithmetic and copies ran while one was open for 1% of the time, Pallas kernels for 0%

profile of v2, /device:TPU:34, one launch (start us, length us, event | category | flops | bytes accessed | tf_op | source)
XLA Modules:
  0.0 113.9 jit_solution(13637036079624470104)
XLA Ops:
  0.0 2.6 %pad_maximum_fusion.3 = (f32[3,3,32,512]{3,2,1,0:T(8,128)}, f32[3,3,32,512]{3,2,1,0:T(8,128)}) fusion(f32[1,16,32,512]{3,2,1,0:T(8,128)} %bitcast.65, f32[1,16,32,512]{3,2,1,0:T(8,128)} %bitcast.62, f32[1,16,32,512]{3,2,1,0:T(8,128)} %bitcast.68), kind=kLoop, calls=%fused_computation.155 | loop fusion | flops 589824 | bytes 4325376 | tf_op jit(solution)/shard_map/slice | solution.py:25
  2.7 1.9 %collective-permute-start = (f32[3,3,32,512]{3,2,1,0:T(8,128)}, f32[3,3,32,512]{3,2,1,0:T(8,128)}, u32[]{:S(2)}, u32[]{:S(2)}) collective-permute-start(f32[3,3,32,512]{3,2,1,0:T(8,128)} %get-tuple-element.38), channel_id=1, source_target_pairs={{0,8},{8,16},{16,24},{24,32},{32,40},{40,48},{48,56},{56,64},{64,7... | collective-permute-start | bytes 1769480 | tf_op jit(solution)/shard_map/ppermute | solution.py:25
  4.6 6.0 %collective-permute-start.1 = (f32[3,3,32,512]{3,2,1,0:T(8,128)}, f32[3,3,32,512]{3,2,1,0:T(8,128)}, u32[]{:S(2)}, u32[]{:S(2)}) collective-permute-start(f32[3,3,32,512]{3,2,1,0:T(8,128)} %get-tuple-element.39), channel_id=1, source_target_pairs={{8,0},{16,8},{24,16},{32,24},{40,32},{48,40},{56,48},{64,56},{72,6... | collective-permute-start | bytes 1769480 | tf_op jit(solution)/shard_map/ppermute | solution.py:26
  10.7 0.1 bitcast_reduce_fusion.1
  10.8 5.9 %collective-permute-done = f32[3,3,32,512]{3,2,1,0:T(8,128)} collective-permute-done((f32[3,3,32,512]{3,2,1,0:T(8,128)}, f32[3,3,32,512]{3,2,1,0:T(8,128)}, u32[]{:S(2)}, u32[]{:S(2)}) %collective-permute-start) | collective-permute-done | bytes 589856 | tf_op jit(solution)/shard_map/ppermute | solution.py:25
  16.7 1.7 %collective-permute-done.1 = f32[3,3,32,512]{3,2,1,0:T(8,128)} collective-permute-done((f32[3,3,32,512]{3,2,1,0:T(8,128)}, f32[3,3,32,512]{3,2,1,0:T(8,128)}, u32[]{:S(2)}, u32[]{:S(2)}) %collective-permute-start.1) | collective-permute-done | bytes 589856 | tf_op jit(solution)/shard_map/ppermute | solution.py:26
  18.4 1.4 %pad_maximum_fusion.8 = (f32[3,22,3,512]{3,2,1,0:T(4,128)S(1)}, f32[3,22,3,512]{3,2,1,0:T(4,128)S(1)}) fusion(f32[3,3,32,512]{3,2,1,0:T(8,128)} %collective-permute-done.1, f32[3,3,32,512]{3,2,1,0:T(8,128)} %collective-permute-done, f32[1,16,32,512]{3,2,1,0:T(8,128)S(1)} %bitcast.66, f32[1,16,32,512]{3,2,1,0:T(8,128)S(1)} %bitcast.63, ...), kind=kLoop, calls=%fused_computation.160 | loop fusion | flops 811008 | bytes 5136384 | tf_op jit(solution)/shard_map/slice | solution.py:25
  19.8 0.1 copy.9
  19.9 3.0 %collective-permute-start.2 = (f32[3,22,3,512]{3,1,2,0:T(8,128)S(1)}, f32[3,22,3,512]{3,1,2,0:T(8,128)S(1)}, u32[]{:S(2)}, u32[]{:S(2)}) collective-permute-start(f32[3,22,3,512]{3,1,2,0:T(8,128)S(1)} %copy.9), channel_id=1, source_target_pairs={{0,1},{1,2},{2,3},{3,4},{4,5},{5,6},{6,7},{8,9},{9,10},{10,11},{11... | collective-permute-start | bytes 1216520 | tf_op jit(solution)/shard_map/ppermute | solution.py:25
  22.9 0.1 copy.10
  23.1 2.8 %collective-permute-start.3 = (f32[3,22,3,512]{3,1,2,0:T(8,128)S(1)}, f32[3,22,3,512]{3,1,2,0:T(8,128)S(1)}, u32[]{:S(2)}, u32[]{:S(2)}) collective-permute-start(f32[3,22,3,512]{3,1,2,0:T(8,128)S(1)} %copy.10), channel_id=1, source_target_pairs={{1,0},{2,1},{3,2},{4,3},{5,4},{6,5},{7,6},{9,8},{10,9},{11,10},{12... | collective-permute-start | bytes 1216520 | tf_op jit(solution)/shard_map/ppermute | solution.py:26
  25.9 0.5 fusion.197
  26.4 0.1 fusion.48
  26.6 14.3 %collective-permute-done.2 = f32[3,22,3,512]{3,1,2,0:T(8,128)S(1)} collective-permute-done((f32[3,22,3,512]{3,1,2,0:T(8,128)S(1)}, f32[3,22,3,512]{3,1,2,0:T(8,128)S(1)}, u32[]{:S(2)}, u32[]{:S(2)}) %collective-permute-start.2) | collective-permute-done | bytes 405536 | tf_op jit(solution)/shard_map/ppermute | solution.py:25
  40.9 0.3 copy.11
  41.2 0.0 collective-permute-done.3
  41.2 0.3 copy.12
  41.5 2.3 %pad_maximum_fusion = f32[3,22,38,512]{3,2,1,0:T(8,128)S(1)} fusion(f32[3,22,3,512]{3,2,1,0:T(4,128)S(1)} %copy.12, f32[3,3,32,512]{3,2,1,0:T(8,128)} %collective-permute-done.1, f32[1,16,32,512]{3,2,1,0:T(8,128)S(1)} %bitcast.67, f32[1,16,32,512]{3,2,1,0:T(8,128)S(1)} %bitcast.64, f32[1,16,32,512]{3,2,1,0:T(8,128)S(1)} %bitcast.70, ...), kind=kLoop, calls=%fused_computation | loop fusion | flops 7704576 | bytes 10272768 | tf_op jit(solution)/shard_map/concatenate | solution.py:41
  43.7 1.9 %slice_bitcast_fusion.1 = (f32[22,38,512]{2,1,0:T(8,128)}, f32[22,38,512]{2,1,0:T(8,128)S(1)}, f32[22,38,512]{2,1,0:T(8,128)S(1)}) fusion(f32[3,22,38,512]{3,2,1,0:T(8,128)S(1)} %pad_maximum_fusion), kind=kLoop, calls=%fused_computation.75 | loop fusion | bytes 10272768 | tf_op jit(solution)/shard_map/squeeze | solution.py:163
  45.6 8.2 %and_select_fusion.1 = (f32[22,38,512]{2,1,0:T(8,128)}, f32[22,38,512]{2,1,0:T(8,128)}, f32[22,38,512]{2,1,0:T(8,128)}, f32[22,38,512]{2,1,0:T(8,128)}, f32[22,38,512]{2,1,0:T(8,128)}) fusion(f32[22,38,512]{2,1,0:T(8,128)S(1)} %get-tuple-element.33, pred[38]{0:T(512)(128)(4,1)S(1)} %compare_and_fusion.2, pred[22]{0:T(512)(128)(4,1)S(1)} %compare_and_fusion.3, ...), kind=kLoop, calls=%fused_computation.26 | loop fusion | flops 25253888 | bytes 13697084 | tf_op jit(solution)/shard_map/jit(_where)/select_n | solution.py:170
  53.8 10.2 %and_select_fusion = f32[22,38,512]{2,1,0:T(8,128)S(1)} fusion(f32[22,38,512]{2,1,0:T(8,128)} %get-tuple-element.26, f32[22,38,512]{2,1,0:T(8,128)} %get-tuple-element.30, f32[22,38,512]{2,1,0:T(8,128)} %get-tuple-element.29, f32[22,38,512]{2,1,0:T(8,128)} %get-tuple-element.28, f32[22,38,512]{2,1,0:T(8,128)} %get-tuple-element.27, ...), kind=kLoop, calls=%fused_computation.25 | loop fusion | flops 16693248 | bytes 13697084 | tf_op jit(solution)/shard_map/jit(_where)/select_n | solution.py:170
  64.0 3.5 %fusion.43 = (f32[22,38,512]{2,1,0:T(8,128)S(1)}, f32[22,38,512]{2,1,0:T(8,128)S(1)}, f32[22,38,512]{2,1,0:T(8,128)S(1)}, f32[22,38,512]{2,1,0:T(8,128)S(1)}, f3...) fusion(f32[22,38,512]{2,1,0:T(8,128)S(1)} %and_select_fusion, f32[22,38,512]{2,1,0:T(8,128)S(1)} %get-tuple-element.32), kind=kLoop, calls=%fused_computation.70 | loop fusion | flops 6848512 | bytes 13697024 | tf_op jit(solution)/shard_map/mul | solution.py:82
  67.6 5.0 %bitcast_reduce_fusion = f32[4,32,512]{2,1,0:T(8,128)S(1)} fusion(f32[22,38,512]{2,1,0:T(8,128)S(1)} %get-tuple-element.41, f32[22,38,512]{2,1,0:T(8,128)S(1)} %copy-done.4, f32[22,38,512]{2,1,0:T(8,128)S(1)} %get-tuple-element.40, f32[22,38,512]{2,1,0:T(8,128)S(1)} %copy-done.3, f32[22,38,512]{2,1,0:T(8,128)} %get-tuple-element.43, ...), kind=kLoop, calls=%fused_computation.151 | loop fusion | flops 3604480 | bytes 12845056 | tf_op jit(solution)/shard_map/reduce_sum | solution.py:94
  72.5 0.5 fusion.195
  73.0 0.1 fusion.47
  73.2 9.2 %collective-permute-start.4 = (f32[2,4,8,128]{3,2,1,0:T(8,128)S(1)}, f32[2,4,8,128]{3,2,1,0:T(8,128)S(1)}, u32[]{:S(2)}, u32[]{:S(2)}) collective-permute-start(f32[2,4,8,128]{3,2,1,0:T(8,128)S(1)} %pad_maximum_fusion.10), channel_id=1, source_target_pairs={{0,16},{8,24},{16,32},{24,40},{32,48},{40,56},{48,64},{56,72},{64,... | collective-permute-start | bytes 98312 | tf_op jit(solution)/shard_map/ppermute | solution.py:25
  82.4 1.9 %collective-permute-start.5 = (f32[2,4,8,128]{3,2,1,0:T(8,128)S(1)}, f32[2,4,8,128]{3,2,1,0:T(8,128)S(1)}, u32[]{:S(2)}, u32[]{:S(2)}) collective-permute-start(f32[2,4,8,128]{3,2,1,0:T(8,128)S(1)} %pad_maximum_fusion.10), channel_id=1, source_target_pairs={{0,8},{8,16},{16,24},{24,32},{32,40},{40,48},{48,56},{56,64},{64,7... | collective-permute-start | bytes 98312 | tf_op jit(solution)/shard_map/ppermute | solution.py:25
  84.3 6.0 %collective-permute-start.6 = (f32[2,4,8,128]{3,2,1,0:T(8,128)S(1)}, f32[2,4,8,128]{3,2,1,0:T(8,128)S(1)}, u32[]{:S(2)}, u32[]{:S(2)}) collective-permute-start(f32[2,4,8,128]{3,2,1,0:T(8,128)S(1)} %pad_maximum_fusion.10), channel_id=1, source_target_pairs={{8,0},{16,8},{24,16},{32,24},{40,32},{48,40},{56,48},{64,56},{72,6... | collective-permute-start | bytes 98312 | tf_op jit(solution)/shard_map/ppermute | solution.py:26
  90.3 1.9 %collective-permute-start.7 = (f32[2,4,8,128]{3,2,1,0:T(8,128)S(1)}, f32[2,4,8,128]{3,2,1,0:T(8,128)S(1)}, u32[]{:S(2)}, u32[]{:S(2)}) collective-permute-start(f32[2,4,8,128]{3,2,1,0:T(8,128)S(1)} %pad_maximum_fusion.10), channel_id=1, source_target_pairs={{16,0},{24,8},{32,16},{40,24},{48,32},{56,40},{64,48},{72,56},{80,... | collective-permute-start | bytes 98312 | tf_op jit(solution)/shard_map/ppermute | solution.py:26
  92.3 0.0 collective-permute-done.4
  92.3 0.0 collective-permute-done.5
  92.3 0.0 collective-permute-done.6
  92.3 5.3 %collective-permute-done.7 = f32[2,4,8,128]{3,2,1,0:T(8,128)S(1)} collective-permute-done((f32[2,4,8,128]{3,2,1,0:T(8,128)S(1)}, f32[2,4,8,128]{3,2,1,0:T(8,128)S(1)}, u32[]{:S(2)}, u32[]{:S(2)}) %collective-permute-start.7) | collective-permute-done | bytes 32800 | tf_op jit(solution)/shard_map/ppermute | solution.py:26
  97.7 3.6 %collective-permute-start.8 = (f32[2,20,8,128]{3,2,1,0:T(8,128)S(1)}, f32[2,20,8,128]{3,2,1,0:T(8,128)S(1)}, u32[]{:S(2)}, u32[]{:S(2)}) collective-permute-start(f32[2,20,8,128]{3,2,1,0:T(8,128)S(1)} %constant_dynamic-update-slice_fusion), channel_id=1, source_target_pairs={{0,1},{1,2},{2,3},{3,4},{4,5},{5,6},{6,7},{8,9},{9,10},{10,11},{11... | collective-permute-start | bytes 491528 | tf_op jit(solution)/shard_map/ppermute | solution.py:25
  101.3 2.4 %collective-permute-start.9 = (f32[2,20,8,128]{3,2,1,0:T(8,128)S(1)}, f32[2,20,8,128]{3,2,1,0:T(8,128)S(1)}, u32[]{:S(2)}, u32[]{:S(2)}) collective-permute-start(f32[2,20,8,128]{3,2,1,0:T(8,128)S(1)} %constant_dynamic-update-slice_fusion), channel_id=1, source_target_pairs={{1,0},{2,1},{3,2},{4,3},{5,4},{6,5},{7,6},{9,8},{10,9},{11,10},{12... | collective-permute-start | bytes 491528 | tf_op jit(solution)/shard_map/ppermute | solution.py:26
  103.7 1.9 %collective-permute-done.8 = f32[2,20,8,128]{3,2,1,0:T(8,128)S(1)} collective-permute-done((f32[2,20,8,128]{3,2,1,0:T(8,128)S(1)}, f32[2,20,8,128]{3,2,1,0:T(8,128)S(1)}, u32[]{:S(2)}, u32[]{:S(2)}) %collective-permute-start.8) | collective-permute-done | bytes 163872 | tf_op jit(solution)/shard_map/ppermute | solution.py:25
  105.7 3.7 %collective-permute-done.9 = f32[2,20,8,128]{3,2,1,0:T(8,128)S(1)} collective-permute-done((f32[2,20,8,128]{3,2,1,0:T(8,128)S(1)}, f32[2,20,8,128]{3,2,1,0:T(8,128)S(1)}, u32[]{:S(2)}, u32[]{:S(2)}) %collective-permute-start.9) | collective-permute-done | bytes 163872 | tf_op jit(solution)/shard_map/ppermute | solution.py:26
  109.5 0.5 fusion.180
  110.0 0.3 fusion.181
  110.3 0.3 multiply_add_fusion.4
  110.6 0.3 multiply_add_fusion.3
  110.9 0.3 multiply_add_fusion.2
  111.2 0.3 multiply_add_fusion.1
  111.4 0.3 multiply_add_fusion
  111.7 0.2 fusion.167
  111.9 0.5 fusion.184
  112.4 0.3 convolution_bitcast_fusion
  112.7 1.2 %bitcast_add_fusion = f32[16,32,512]{2,1,0:T(8,128)} fusion(f32[22,38,512]{2,1,0:T(8,128)S(1)} %and_select_fusion, f32[4,32,512]{2,1,0:T(8,128)S(1)} %convolution_bitcast_fusion), kind=kLoop, calls=%fused_computation.150 | loop fusion | flops 262144 | bytes 2359296 | tf_op jit(solution)/shard_map/add | solution.py:177
  (30 shorter events, 0.2 us)
Async XLA Ops:
  0.0 10.7 %copy-start = (f32[16,32,512]{2,1,0:T(8,128)S(1)}, f32[16,32,512]{2,1,0:T(8,128)}, u32[]{:S(2)}) copy-start(f32[16,32,512]{2,1,0:T(8,128)} %param.4) | copy-start | bytes 3145732
  0.0 18.4 %copy-start.5 = (f32[16,32,512]{2,1,0:T(8,128)S(1)}, f32[16,32,512]{2,1,0:T(8,128)}, u32[]{:S(2)}) copy-start(f32[16,32,512]{2,1,0:T(8,128)} %param.5) | copy-start | bytes 3145732
  0.0 18.4 %copy-start.6 = (f32[16,32,512]{2,1,0:T(8,128)S(1)}, f32[16,32,512]{2,1,0:T(8,128)}, u32[]{:S(2)}) copy-start(f32[16,32,512]{2,1,0:T(8,128)} %param.3) | copy-start | bytes 3145732
  2.7 14.0 %collective-permute-start = (f32[3,3,32,512]{3,2,1,0:T(8,128)}, f32[3,3,32,512]{3,2,1,0:T(8,128)}, u32[]{:S(2)}, u32[]{:S(2)}) collective-permute-start(f32[3,3,32,512]{3,2,1,0:T(8,128)} %get-tuple-element.38), channel_id=1, source_target_pairs={{0,8},{8,16},{16,24},{24,32},{32,40},{40,48},{48,56},{56,64},{64,7... | collective-permute-start | bytes 1769480 | tf_op jit(solution)/shard_map/ppermute | solution.py:25
  4.6 13.8 %collective-permute-start.1 = (f32[3,3,32,512]{3,2,1,0:T(8,128)}, f32[3,3,32,512]{3,2,1,0:T(8,128)}, u32[]{:S(2)}, u32[]{:S(2)}) collective-permute-start(f32[3,3,32,512]{3,2,1,0:T(8,128)} %get-tuple-element.39), channel_id=1, source_target_pairs={{8,0},{16,8},{24,16},{32,24},{40,32},{48,40},{56,48},{64,56},{72,6... | collective-permute-start | bytes 1769480 | tf_op jit(solution)/shard_map/ppermute | solution.py:26
  19.9 21.0 %collective-permute-start.2 = (f32[3,22,3,512]{3,1,2,0:T(8,128)S(1)}, f32[3,22,3,512]{3,1,2,0:T(8,128)S(1)}, u32[]{:S(2)}, u32[]{:S(2)}) collective-permute-start(f32[3,22,3,512]{3,1,2,0:T(8,128)S(1)} %copy.9), channel_id=1, source_target_pairs={{0,1},{1,2},{2,3},{3,4},{4,5},{5,6},{6,7},{8,9},{9,10},{10,11},{11... | collective-permute-start | bytes 1216520 | tf_op jit(solution)/shard_map/ppermute | solution.py:25
  23.1 18.1 %collective-permute-start.3 = (f32[3,22,3,512]{3,1,2,0:T(8,128)S(1)}, f32[3,22,3,512]{3,1,2,0:T(8,128)S(1)}, u32[]{:S(2)}, u32[]{:S(2)}) collective-permute-start(f32[3,22,3,512]{3,1,2,0:T(8,128)S(1)} %copy.10), channel_id=1, source_target_pairs={{1,0},{2,1},{3,2},{4,3},{5,4},{6,5},{7,6},{9,8},{10,9},{11,10},{12... | collective-permute-start | bytes 1216520 | tf_op jit(solution)/shard_map/ppermute | solution.py:26
  64.0 3.6 %copy-start.1 = (f32[22,38,512]{2,1,0:T(8,128)S(1)}, f32[22,38,512]{2,1,0:T(8,128)}, u32[]{:S(2)}) copy-start(f32[22,38,512]{2,1,0:T(8,128)} %get-tuple-element.27) | copy-start | bytes 5136388
  64.0 3.5 %copy-start.2 = (f32[22,38,512]{2,1,0:T(8,128)S(1)}, f32[22,38,512]{2,1,0:T(8,128)}, u32[]{:S(2)}) copy-start(f32[22,38,512]{2,1,0:T(8,128)} %get-tuple-element.28) | copy-start | bytes 5136388
  64.0 3.5 %copy-start.3 = (f32[22,38,512]{2,1,0:T(8,128)S(1)}, f32[22,38,512]{2,1,0:T(8,128)}, u32[]{:S(2)}) copy-start(f32[22,38,512]{2,1,0:T(8,128)} %get-tuple-element.29) | copy-start | bytes 5136388
  64.0 3.5 %copy-start.4 = (f32[22,38,512]{2,1,0:T(8,128)S(1)}, f32[22,38,512]{2,1,0:T(8,128)}, u32[]{:S(2)}) copy-start(f32[22,38,512]{2,1,0:T(8,128)} %get-tuple-element.30) | copy-start | bytes 5136388
  73.2 19.1 %collective-permute-start.4 = (f32[2,4,8,128]{3,2,1,0:T(8,128)S(1)}, f32[2,4,8,128]{3,2,1,0:T(8,128)S(1)}, u32[]{:S(2)}, u32[]{:S(2)}) collective-permute-start(f32[2,4,8,128]{3,2,1,0:T(8,128)S(1)} %pad_maximum_fusion.10), channel_id=1, source_target_pairs={{0,16},{8,24},{16,32},{24,40},{32,48},{40,56},{48,64},{56,72},{64,... | collective-permute-start | bytes 98312 | tf_op jit(solution)/shard_map/ppermute | solution.py:25
  82.4 9.9 %collective-permute-start.5 = (f32[2,4,8,128]{3,2,1,0:T(8,128)S(1)}, f32[2,4,8,128]{3,2,1,0:T(8,128)S(1)}, u32[]{:S(2)}, u32[]{:S(2)}) collective-permute-start(f32[2,4,8,128]{3,2,1,0:T(8,128)S(1)} %pad_maximum_fusion.10), channel_id=1, source_target_pairs={{0,8},{8,16},{16,24},{24,32},{32,40},{40,48},{48,56},{56,64},{64,7... | collective-permute-start | bytes 98312 | tf_op jit(solution)/shard_map/ppermute | solution.py:25
  84.3 8.0 %collective-permute-start.6 = (f32[2,4,8,128]{3,2,1,0:T(8,128)S(1)}, f32[2,4,8,128]{3,2,1,0:T(8,128)S(1)}, u32[]{:S(2)}, u32[]{:S(2)}) collective-permute-start(f32[2,4,8,128]{3,2,1,0:T(8,128)S(1)} %pad_maximum_fusion.10), channel_id=1, source_target_pairs={{8,0},{16,8},{24,16},{32,24},{40,32},{48,40},{56,48},{64,56},{72,6... | collective-permute-start | bytes 98312 | tf_op jit(solution)/shard_map/ppermute | solution.py:26
  90.3 7.3 %collective-permute-start.7 = (f32[2,4,8,128]{3,2,1,0:T(8,128)S(1)}, f32[2,4,8,128]{3,2,1,0:T(8,128)S(1)}, u32[]{:S(2)}, u32[]{:S(2)}) collective-permute-start(f32[2,4,8,128]{3,2,1,0:T(8,128)S(1)} %pad_maximum_fusion.10), channel_id=1, source_target_pairs={{16,0},{24,8},{32,16},{40,24},{48,32},{56,40},{64,48},{72,56},{80,... | collective-permute-start | bytes 98312 | tf_op jit(solution)/shard_map/ppermute | solution.py:26
  97.7 8.0 %collective-permute-start.8 = (f32[2,20,8,128]{3,2,1,0:T(8,128)S(1)}, f32[2,20,8,128]{3,2,1,0:T(8,128)S(1)}, u32[]{:S(2)}, u32[]{:S(2)}) collective-permute-start(f32[2,20,8,128]{3,2,1,0:T(8,128)S(1)} %constant_dynamic-update-slice_fusion), channel_id=1, source_target_pairs={{0,1},{1,2},{2,3},{3,4},{4,5},{5,6},{6,7},{8,9},{9,10},{10,11},{11... | collective-permute-start | bytes 491528 | tf_op jit(solution)/shard_map/ppermute | solution.py:25
  101.3 8.1 %collective-permute-start.9 = (f32[2,20,8,128]{3,2,1,0:T(8,128)S(1)}, f32[2,20,8,128]{3,2,1,0:T(8,128)S(1)}, u32[]{:S(2)}, u32[]{:S(2)}) collective-permute-start(f32[2,20,8,128]{3,2,1,0:T(8,128)S(1)} %constant_dynamic-update-slice_fusion), channel_id=1, source_target_pairs={{1,0},{2,1},{3,2},{4,3},{5,4},{6,5},{7,6},{9,8},{10,9},{11,10},{12... | collective-permute-start | bytes 491528 | tf_op jit(solution)/shard_map/ppermute | solution.py:26

commit v3 on v2

--- a/solution.py
+++ b/solution.py
@@ -46,19 +46,6 @@
     if side < 0:
         return jnp.concatenate([zeros, field[:, :, :-1]], axis=2)
     return jnp.concatenate([field[:, :, 1:], zeros], axis=2)
-
-
-def fine_neighbours(field):
-    xl, xh = halo_from(field, "box", 0, 1, 1)
-    yl, yh = halo_from(field, "group", 1, 1, 1)
-    return [
-        jnp.concatenate([xl, field[:-1]], axis=0),
-        jnp.concatenate([field[1:], xh], axis=0),
-        jnp.concatenate([yl, field[:, :-1]], axis=1),
-        jnp.concatenate([field[:, 1:], yh], axis=1),
-        shift_z(field, -1),
-        shift_z(field, 1),
-    ]
 
 
 def padded_neighbours(padded):
@@ -154,16 +141,74 @@
     return inside
 
 
+def shift_both(block, dx, dy):
+    nb, ng = lax.axis_size("box"), lax.axis_size("group")
+    pairs = [
+        (i * ng + j, (i + dx) * ng + (j + dy))
+        for i in range(nb)
+        for j in range(ng)
+        if 0 <= i + dx < nb and 0 <= j + dy < ng
+    ]
+    if not pairs:
+        return jnp.zeros_like(block)
+    return lax.ppermute(block, ("box", "group"), pairs)
+
+
+def halo_ring(block, depth):
+    sx, sy = block.shape[1], block.shape[2]
+    parts = {
+        -1: slice(0, depth),
+        0: slice(0, sx),
+        1: slice(sx - depth, sx),
+    }
+    parts_y = {
+        -1: slice(0, depth),
+        0: slice(0, sy),
+        1: slice(sy - depth, sy),
+    }
+    rows = []
+    for ox in (-1, 0, 1):
+        row = []
+        for oy in (-1, 0, 1):
+            if ox == 0 and oy == 0:
+                row.append(block)
+                continue
+            piece = block[:, parts[-ox], parts_y[-oy]]
+            row.append(shift_both(piece, -ox, -oy))
+        rows.append(jnp.concatenate(row, axis=2))
+    return jnp.concatenate(rows, axis=1)
+
+
+def low_faces(b):
+    faces = []
+    for dim in range(3):
+        n = b.shape[dim]
+        lo = lax.slice_in_dim(b, 0, n - 1, axis=dim)
+        hi = lax.slice_in_dim(b, 1, n, axis=dim)
+        inner = jnp.where((lo > 0) & (hi > 0), 2.0 * hi * lo / (hi + lo), hi + lo)
+        faces.append(jnp.concatenate([lax.slice_in_dim(b, 0, 1, axis=dim), inner], axis=dim))
+    return faces
+
+
+def face_pairs(b, faces):
+    pairs = []
+    for dim, lo in enumerate(faces):
+        n = b.shape[dim]
+        hi = jnp.concatenate(
+            [lax.slice_in_dim(lo, 1, n, axis=dim), lax.slice_in_dim(b, n - 1, n, axis=dim)], axis=dim
+        )
+        pairs += [lo, hi]
+    return pairs
+
+
 def per_device(right_side, inv_density, pressure):
     depth = SWEEPS + 1
     sx, sy, sz = pressure.shape
-    both = jnp.stack([right_side, inv_density, pressure])
-    both = deep_extend(both, "box", 1, depth)
-    both = deep_extend(both, "group", 2, depth)
+    both = halo_ring(jnp.stack([right_side, inv_density, pressure]), depth)
     rhs_e, b_e, fine = both[0], both[1], both[2]
     totals = (sx * lax.axis_size("box"), sy * lax.axis_size("group"))
     inside = grid_mask(fine.shape, depth, ("box", "group"), totals)
-    coefs = coefs_of(b_e, padded_neighbours(jnp.pad(b_e, 1)))
+    coefs = face_pairs(b_e, low_faces(b_e))
     diag = sum(coefs)
     for sweep in range(SWEEPS):
         step = 2.0 / 3.0 * (rhs_e - apply_op(fine, padded_neighbours(jnp.pad(fine, 1)), coefs)) / diag

time: 114 us -> 110 us (0.965); the launches traced: 114 us -> 108 us
  starting transfers between devices: 38.9 us -> 47.5 us
  other arithmetic: 37 us -> 28.7 us
  waiting for transfers between devices: 32.8 us -> 27 us
    ppermute x0 -> x8, starting transfers between devices: none -> 26.2 us  [shift_both(): return lax.ppermute(block, ('box', 'group'), pairs)]
    ppermute x5 -> x3, waiting for transfers between devices: 22.1 us -> 1.19 us  [halo_from(): lax.ppermute(lax.slice_in_dim(block, n - width, n, axis=dim), axis, forward)]
    ppermute x0 -> x8, waiting for transfers between devices: none -> 19.3 us  [shift_both(): return lax.ppermute(block, ('box', 'group'), pairs)]
    ppermute x5 -> x3, starting transfers between devices: 19.6 us -> 7.62 us  [halo_from(): lax.ppermute(lax.slice_in_dim(block, n - width, n, axis=dim), axis, forward)]
    select_n x2, other arithmetic: 18.4 us -> 8.98 us  [per_device(): fine = jnp.where(inside, fine + step, 0.0)]
    ppermute x5 -> x3, starting transfers between devices: 19.2 us -> 13.7 us  [halo_from(): lax.ppermute(lax.slice_in_dim(block, 0, width, axis=dim), axis, backward)]
    ppermute x5 -> x3, waiting for transfers between devices: 10.7 us -> 6.48 us  [halo_from(): lax.ppermute(lax.slice_in_dim(block, 0, width, axis=dim), axis, backward)]
    concatenate x0 -> x1, other arithmetic: none -> 2.42 us  [halo_ring(): return jnp.concatenate(rows, axis=1)]
  transfers between devices with their start and end apart: 10 -> 14, of which waited for: 6 -> 5; matrix products, arithmetic and copies ran while one was open for 1% -> 4% of each run, Pallas kernels for 0% -> 0%
where the time goes in v3:
time: 110 us; the launch traced here: 108 us
  starting transfers between devices  47.5 us (43%)
  other arithmetic  28.7 us (26%)
  waiting for transfers between devices  27 us (25%)
  matrix products  2.05 us (2%)
  local copies, waits for them, and re-layouts  2.02 us (2%)
    ppermute x8, starting transfers between devices, shift_both(): return lax.ppermute(block, ('box', 'group'), pairs)  26.2 us
    ppermute x8, waiting for transfers between devices, shift_both(): return lax.ppermute(block, ('box', 'group'), pairs)  19.3 us
    ppermute x3, starting transfers between devices, halo_from(): lax.ppermute(lax.slice_in_dim(block, 0, width, axis=dim), axis, backward)  13.7 us
    select_n x2, other arithmetic, per_device(): fine = jnp.where(inside, fine + step, 0.0)  8.98 us
    ppermute x3, starting transfers between devices, halo_from(): lax.ppermute(lax.slice_in_dim(block, n - width, n, axis=dim), axis, forward)  7.62 us
    ppermute x3, waiting for transfers between devices, halo_from(): lax.ppermute(lax.slice_in_dim(block, 0, width, axis=dim), axis, backward)  6.48 us
    slice x3, other arithmetic, halo_ring(): piece = block[:, parts[-ox], parts_y[-oy]]  3.86 us
    reduce_sum x2, other arithmetic, block_mean(): fx = field.reshape(sx // 4, 4, sy, sz).sum(axis=1)  2.67 us
  transfers between devices with their start and end apart: 14, of which 5 were waited for; matrix products, arithmetic and copies ran while one was open for 4% of the time, Pallas kernels for 0%

profile of v3, /device:TPU:34, one launch (start us, length us, event | category | flops | bytes accessed | tf_op | source)
XLA Modules:
  0.0 107.9 jit_solution(7660742919218363365)
XLA Ops:
  0.0 1.9 %pad_maximum_fusion.18 = (f32[3,3,3,512]{3,2,1,0:T(4,128)S(1)}, f32[3,3,3,512]{3,2,1,0:T(4,128)}, f32[3,3,3,512]{3,2,1,0:T(4,128)}, f32[3,3,3,512]{3,2,1,0:T(4,128)}) fusion(f32[1,16,32,512]{3,2,1,0:T(8,128)} %bitcast.79, f32[1,16,32,512]{3,2,1,0:T(8,128)} %bitcast.74, f32[1,16,32,512]{3,2,1,0:T(8,128)} %bitcast.84), kind=kLoop, calls=%fused_computation.324 | loop fusion | flops 110592 | bytes 3366912 | tf_op jit(solution)/shard_map/slice | solution.py:176
  1.9 2.5 %collective-permute-start = (f32[3,3,3,512]{3,2,1,0:T(4,128)S(1)}, f32[3,3,3,512]{3,2,1,0:T(4,128)}, u32[]{:S(2)}, u32[]{:S(2)}) collective-permute-start(f32[3,3,3,512]{3,2,1,0:T(4,128)S(1)} %get-tuple-element.31), channel_id=1, source_target_pairs={{0,9},{1,10},{2,11},{3,12},{4,13},{5,14},{6,15},{8,17},{9,18},{10,... | collective-permute-start | bytes 165896 | tf_op jit(solution)/shard_map/ppermute | solution.py:154
  4.4 5.8 %collective-permute-start.2 = (f32[3,3,3,512]{3,2,1,0:T(4,128)}, f32[3,3,3,512]{3,2,1,0:T(4,128)}, u32[]{:S(2)}, u32[]{:S(2)}) collective-permute-start(f32[3,3,3,512]{3,2,1,0:T(4,128)} %get-tuple-element.34), channel_id=1, source_target_pairs={{1,8},{2,9},{3,10},{4,11},{5,12},{6,13},{7,14},{9,16},{10,17},{11,... | collective-permute-start | bytes 165896 | tf_op jit(solution)/shard_map/ppermute | solution.py:154
  10.2 0.3 pad_maximum_fusion
  10.6 0.9 slice.398
  11.4 1.9 %collective-permute-start.1 = (f32[3,3,32,512]{3,2,1,0:T(8,128)}, f32[3,3,32,512]{3,2,1,0:T(8,128)}, u32[]{:S(2)}, u32[]{:S(2)}) collective-permute-start(f32[3,3,32,512]{3,2,1,0:T(8,128)} %slice.398), channel_id=1, source_target_pairs={{0,8},{1,9},{2,10},{3,11},{4,12},{5,13},{6,14},{7,15},{8,16},{9,17... | collective-permute-start | bytes 1769480 | tf_op jit(solution)/shard_map/ppermute | solution.py:154
  13.4 1.1 pad_maximum_fusion.10
  14.4 3.4 %collective-permute-start.3 = (f32[3,16,3,512]{3,2,1,0:T(4,128)}, f32[3,16,3,512]{3,2,1,0:T(4,128)S(1)}, u32[]{:S(2)}, u32[]{:S(2)}) collective-permute-start(f32[3,16,3,512]{3,2,1,0:T(4,128)} %get-tuple-element.35), channel_id=1, source_target_pairs={{0,1},{1,2},{2,3},{3,4},{4,5},{5,6},{6,7},{8,9},{9,10},{10,11},{11... | collective-permute-start | bytes 884744 | tf_op jit(solution)/shard_map/ppermute | solution.py:154
  17.9 0.9 pad_maximum_fusion.7
  18.7 4.7 %collective-permute-start.6 = (f32[3,3,32,512]{3,2,1,0:T(8,128)}, f32[3,3,32,512]{3,2,1,0:T(8,128)}, u32[]{:S(2)}, u32[]{:S(2)}) collective-permute-start(f32[3,3,32,512]{3,2,1,0:T(8,128)} %pad_maximum_fusion.7), channel_id=1, source_target_pairs={{8,0},{9,1},{10,2},{11,3},{12,4},{13,5},{14,6},{15,7},{16,8},{17,9... | collective-permute-start | bytes 1769480 | tf_op jit(solution)/shard_map/ppermute | solution.py:154
  23.6 0.5 fusion.208
  24.2 4.1 %collective-permute-start.4 = (f32[3,16,3,512]{3,2,1,0:T(4,128)}, f32[3,16,3,512]{3,2,1,0:T(4,128)}, u32[]{:S(2)}, u32[]{:S(2)}) collective-permute-start(f32[3,16,3,512]{3,2,1,0:T(4,128)} %get-tuple-element.36), channel_id=1, source_target_pairs={{1,0},{2,1},{3,2},{4,3},{5,4},{6,5},{7,6},{9,8},{10,9},{11,10},{12... | collective-permute-start | bytes 884744 | tf_op jit(solution)/shard_map/ppermute | solution.py:154
  28.5 1.9 %collective-permute-start.5 = (f32[3,3,3,512]{3,2,1,0:T(4,128)}, f32[3,3,3,512]{3,2,1,0:T(4,128)}, u32[]{:S(2)}, u32[]{:S(2)}) collective-permute-start(f32[3,3,3,512]{3,2,1,0:T(4,128)} %get-tuple-element.33), channel_id=1, source_target_pairs={{8,1},{9,2},{10,3},{11,4},{12,5},{13,6},{14,7},{16,9},{17,10},{18,... | collective-permute-start | bytes 165896 | tf_op jit(solution)/shard_map/ppermute | solution.py:154
  30.4 0.6 compare_and_fusion.3
  31.0 14.5 %collective-permute-done.5 = f32[3,3,3,512]{3,2,1,0:T(4,128)} collective-permute-done((f32[3,3,3,512]{3,2,1,0:T(4,128)}, f32[3,3,3,512]{3,2,1,0:T(4,128)}, u32[]{:S(2)}, u32[]{:S(2)}) %collective-permute-start.5) | collective-permute-done | bytes 55328 | tf_op jit(solution)/shard_map/ppermute | solution.py:154
  45.4 1.9 %collective-permute-start.7 = (f32[3,3,3,512]{3,2,1,0:T(4,128)}, f32[3,3,3,512]{3,2,1,0:T(4,128)S(1)}, u32[]{:S(2)}, u32[]{:S(2)}) collective-permute-start(f32[3,3,3,512]{3,2,1,0:T(4,128)} %get-tuple-element.32), channel_id=1, source_target_pairs={{9,0},{10,1},{11,2},{12,3},{13,4},{14,5},{15,6},{17,8},{18,9},{19,... | collective-permute-start | bytes 165896 | tf_op jit(solution)/shard_map/ppermute | solution.py:154
  47.4 4.8 %collective-permute-done.7 = f32[3,3,3,512]{3,2,1,0:T(4,128)S(1)} collective-permute-done((f32[3,3,3,512]{3,2,1,0:T(4,128)}, f32[3,3,3,512]{3,2,1,0:T(4,128)S(1)}, u32[]{:S(2)}, u32[]{:S(2)}) %collective-permute-start.7) | collective-permute-done | bytes 55328 | tf_op jit(solution)/shard_map/ppermute | solution.py:154
  52.2 2.4 %maximum_maximum_fusion = f32[3,22,38,512]{3,2,1,0:T(8,128)S(1)} fusion(f32[3,3,3,512]{3,2,1,0:T(4,128)S(1)} %collective-permute-done.7, f32[3,3,32,512]{3,2,1,0:T(8,128)} %collective-permute-done.6, f32[3,3,3,512]{3,2,1,0:T(4,128)} %collective-permute-done.5, f32[3,16,3,512]{3,2,1,0:T(4,128)} %collective-permute-done.4, f32[1,16,32,512]{3,2,1,0:T(8,128)S(1)} %bitcast.83, ...), kind=kLoop, calls=%fused_computation | loop fusion | flops 12840960 | bytes 10272768 | tf_op jit(solution)/shard_map/concatenate | solution.py:179
  54.7 0.8 slice_bitcast_fusion.1
  55.7 0.6 divide_select_fusion
  56.4 0.6 divide_select_fusion.1
  57.0 0.5 divide_select_fusion.2
  57.5 0.9 fusion.192
  58.4 0.9 fusion.191
  59.2 4.5 %and_select_fusion.1 = f32[22,38,512]{2,1,0:T(8,128)S(1)} fusion(f32[22,38,512]{2,1,0:T(8,128)S(1)} %get-tuple-element.28, f32[22,1,512]{2,1,0:T(1,128)S(1)} %get-tuple-element.44, f32[22,37,512]{2,1,0:T(8,128)S(1)} %divide_select_fusion.1, f32[22,1,512]{2,1,0:T(1,128)S(1)} %get-tuple-element.43, f32[22,38,1]{2,1,0:T(8,128)S(1)} %get-tuple-element.42, ...), kind=kLoop, calls=%fused_computation.32 | loop fusion | flops 14553088 | bytes 10399052 | tf_op jit(solution)/shard_map/jit(_where)/select_n | solution.py:215
  63.7 4.5 %and_select_fusion = f32[22,38,512]{2,1,0:T(8,128)S(1)} fusion(f32[22,38,512]{2,1,0:T(8,128)S(1)} %and_select_fusion.1, f32[22,1,512]{2,1,0:T(1,128)S(1)} %get-tuple-element.44, f32[22,37,512]{2,1,0:T(8,128)S(1)} %divide_select_fusion.1, f32[22,1,512]{2,1,0:T(1,128)S(1)} %get-tuple-element.43, f32[22,38,1]{2,1,0:T(8,128)S(1)} %get-tuple-element.42, ...), kind=kLoop, calls=%fused_computation.31 | loop fusion | flops 14553088 | bytes 10399052 | tf_op jit(solution)/shard_map/jit(_where)/select_n | solution.py:215
  68.2 2.7 %fusion.43 = (f32[22,38,512]{2,1,0:T(8,128)S(1)}, f32[22,38,512]{2,1,0:T(8,128)S(1)}, f32[22,38,512]{2,1,0:T(8,128)S(1)}, f32[22,38,512]{2,1,0:T(8,128)S(1)}, f3...) fusion(f32[22,38,512]{2,1,0:T(8,128)S(1)} %and_select_fusion, f32[21,38,512]{2,1,0:T(8,128)S(1)} %divide_select_fusion.2, ...), kind=kLoop, calls=%fused_computation.76 | loop fusion | flops 2996224 | bytes 13774848 | tf_op jit(solution)/shard_map/mul | solution.py:69
  71.0 2.6 %bitcast_reduce_fusion = f32[4,32,512]{2,1,0:T(8,128)S(1)} fusion(f32[22,38,512]{2,1,0:T(8,128)S(1)} %get-tuple-element.38, f32[22,38,1]{2,1,0:T(8,128)S(1)} %get-tuple-element.42, f32[22,38,511]{2,1,0:T(8,128)S(1)} %divide_select_fusion, f32[22,38,512]{2,1,0:T(8,128)S(1)} %get-tuple-element.37, f32[22,38,1]{2,1,0:T(8,128)S(1)} %get-tuple-element.41, ...), kind=kLoop, calls=%fused_computation.163 | loop fusion | flops 4653056 | bytes 12123408 | tf_op jit(solution)/shard_map/reduce_sum | solution.py:81
  73.6 0.5 fusion.206
  74.3 1.9 %collective-permute-start.8 = (f32[2,4,8,128]{3,2,1,0:T(8,128)S(1)}, f32[2,4,8,128]{3,2,1,0:T(8,128)S(1)}, u32[]{:S(2)}, u32[]{:S(2)}) collective-permute-start(f32[2,4,8,128]{3,2,1,0:T(8,128)S(1)} %pad_maximum_fusion.19), channel_id=1, source_target_pairs={{0,16},{8,24},{16,32},{24,40},{32,48},{40,56},{48,64},{56,72},{64,... | collective-permute-start | bytes 98312 | tf_op jit(solution)/shard_map/ppermute | solution.py:25
  76.2 1.9 %collective-permute-start.9 = (f32[2,4,8,128]{3,2,1,0:T(8,128)S(1)}, f32[2,4,8,128]{3,2,1,0:T(8,128)S(1)}, u32[]{:S(2)}, u32[]{:S(2)}) collective-permute-start(f32[2,4,8,128]{3,2,1,0:T(8,128)S(1)} %pad_maximum_fusion.19), channel_id=1, source_target_pairs={{0,8},{8,16},{16,24},{24,32},{32,40},{40,48},{48,56},{56,64},{64,7... | collective-permute-start | bytes 98312 | tf_op jit(solution)/shard_map/ppermute | solution.py:25
  78.1 6.0 %collective-permute-start.10 = (f32[2,4,8,128]{3,2,1,0:T(8,128)S(1)}, f32[2,4,8,128]{3,2,1,0:T(8,128)S(1)}, u32[]{:S(2)}, u32[]{:S(2)}) collective-permute-start(f32[2,4,8,128]{3,2,1,0:T(8,128)S(1)} %pad_maximum_fusion.19), channel_id=1, source_target_pairs={{8,0},{16,8},{24,16},{32,24},{40,32},{48,40},{56,48},{64,56},{72,6... | collective-permute-start | bytes 98312 | tf_op jit(solution)/shard_map/ppermute | solution.py:26
  84.2 5.4 %collective-permute-start.11 = (f32[2,4,8,128]{3,2,1,0:T(8,128)S(1)}, f32[2,4,8,128]{3,2,1,0:T(8,128)S(1)}, u32[]{:S(2)}, u32[]{:S(2)}) collective-permute-start(f32[2,4,8,128]{3,2,1,0:T(8,128)S(1)} %pad_maximum_fusion.19), channel_id=1, source_target_pairs={{16,0},{24,8},{32,16},{40,24},{48,32},{56,40},{64,48},{72,56},{80,... | collective-permute-start | bytes 98312 | tf_op jit(solution)/shard_map/ppermute | solution.py:26
  89.7 1.8 %collective-permute-done.11 = f32[2,4,8,128]{3,2,1,0:T(8,128)S(1)} collective-permute-done((f32[2,4,8,128]{3,2,1,0:T(8,128)S(1)}, f32[2,4,8,128]{3,2,1,0:T(8,128)S(1)}, u32[]{:S(2)}, u32[]{:S(2)}) %collective-permute-start.11) | collective-permute-done | bytes 32800 | tf_op jit(solution)/shard_map/ppermute | solution.py:26
  91.5 3.8 %collective-permute-start.12 = (f32[2,20,8,128]{3,2,1,0:T(8,128)S(1)}, f32[2,20,8,128]{3,2,1,0:T(8,128)S(1)}, u32[]{:S(2)}, u32[]{:S(2)}) collective-permute-start(f32[2,20,8,128]{3,2,1,0:T(8,128)S(1)} %constant_dynamic-update-slice_fusion), channel_id=1, source_target_pairs={{0,1},{1,2},{2,3},{3,4},{4,5},{5,6},{6,7},{8,9},{9,10},{10,11},{11... | collective-permute-start | bytes 491528 | tf_op jit(solution)/shard_map/ppermute | solution.py:25
  95.3 2.2 %collective-permute-start.13 = (f32[2,20,8,128]{3,2,1,0:T(8,128)S(1)}, f32[2,20,8,128]{3,2,1,0:T(8,128)S(1)}, u32[]{:S(2)}, u32[]{:S(2)}) collective-permute-start(f32[2,20,8,128]{3,2,1,0:T(8,128)S(1)} %constant_dynamic-update-slice_fusion), channel_id=1, source_target_pairs={{1,0},{2,1},{3,2},{4,3},{5,4},{6,5},{7,6},{9,8},{10,9},{11,10},{12... | collective-permute-start | bytes 491528 | tf_op jit(solution)/shard_map/ppermute | solution.py:26
  97.6 1.2 %collective-permute-done.12 = f32[2,20,8,128]{3,2,1,0:T(8,128)S(1)} collective-permute-done((f32[2,20,8,128]{3,2,1,0:T(8,128)S(1)}, f32[2,20,8,128]{3,2,1,0:T(8,128)S(1)}, u32[]{:S(2)}, u32[]{:S(2)}) %collective-permute-start.12) | collective-permute-done | bytes 163872 | tf_op jit(solution)/shard_map/ppermute | solution.py:25
  98.8 4.7 %collective-permute-done.13 = f32[2,20,8,128]{3,2,1,0:T(8,128)S(1)} collective-permute-done((f32[2,20,8,128]{3,2,1,0:T(8,128)S(1)}, f32[2,20,8,128]{3,2,1,0:T(8,128)S(1)}, u32[]{:S(2)}, u32[]{:S(2)}) %collective-permute-start.13) | collective-permute-done | bytes 163872 | tf_op jit(solution)/shard_map/ppermute | solution.py:26
  103.5 0.5 fusion.189
  104.0 0.3 fusion.190
  104.3 0.3 multiply_add_fusion.4
  104.6 0.3 multiply_add_fusion.3
  104.9 0.3 multiply_add_fusion.2
  105.2 0.3 multiply_add_fusion.1
  105.4 0.3 multiply_add_fusion
  106.0 0.5 fusion.195
  106.4 0.3 convolution_bitcast_fusion
  106.8 1.2 %bitcast_add_fusion = f32[16,32,512]{2,1,0:T(8,128)} fusion(f32[22,38,512]{2,1,0:T(8,128)S(1)} %and_select_fusion, f32[4,32,512]{2,1,0:T(8,128)S(1)} %convolution_bitcast_fusion), kind=kLoop, calls=%fused_computation.162 | loop fusion | flops 262144 | bytes 2359296 | tf_op jit(solution)/shard_map/add | solution.py:222
  (62 shorter events, 1.1 us)
Async XLA Ops:
  0.0 10.2 %copy-start.2 = (f32[16,32,512]{2,1,0:T(8,128)S(1)}, f32[16,32,512]{2,1,0:T(8,128)}, u32[]{:S(2)}) copy-start(f32[16,32,512]{2,1,0:T(8,128)} %param.3) | copy-start | bytes 3145732
  0.0 10.2 %copy-start = (f32[16,32,512]{2,1,0:T(8,128)S(1)}, f32[16,32,512]{2,1,0:T(8,128)}, u32[]{:S(2)}) copy-start(f32[16,32,512]{2,1,0:T(8,128)} %param.4) | copy-start | bytes 3145732
  0.0 10.2 %copy-start.1 = (f32[16,32,512]{2,1,0:T(8,128)S(1)}, f32[16,32,512]{2,1,0:T(8,128)}, u32[]{:S(2)}) copy-start(f32[16,32,512]{2,1,0:T(8,128)} %param.5) | copy-start | bytes 3145732
  1.9 22.2 %collective-permute-start = (f32[3,3,3,512]{3,2,1,0:T(4,128)S(1)}, f32[3,3,3,512]{3,2,1,0:T(4,128)}, u32[]{:S(2)}, u32[]{:S(2)}) collective-permute-start(f32[3,3,3,512]{3,2,1,0:T(4,128)S(1)} %get-tuple-element.31), channel_id=1, source_target_pairs={{0,9},{1,10},{2,11},{3,12},{4,13},{5,14},{6,15},{8,17},{9,18},{10,... | collective-permute-start | bytes 165896 | tf_op jit(solution)/shard_map/ppermute | solution.py:154
  4.4 24.0 %collective-permute-start.2 = (f32[3,3,3,512]{3,2,1,0:T(4,128)}, f32[3,3,3,512]{3,2,1,0:T(4,128)}, u32[]{:S(2)}, u32[]{:S(2)}) collective-permute-start(f32[3,3,3,512]{3,2,1,0:T(4,128)} %get-tuple-element.34), channel_id=1, source_target_pairs={{1,8},{2,9},{3,10},{4,11},{5,12},{6,13},{7,14},{9,16},{10,17},{11,... | collective-permute-start | bytes 165896 | tf_op jit(solution)/shard_map/ppermute | solution.py:154
  11.4 40.8 %collective-permute-start.1 = (f32[3,3,32,512]{3,2,1,0:T(8,128)}, f32[3,3,32,512]{3,2,1,0:T(8,128)}, u32[]{:S(2)}, u32[]{:S(2)}) collective-permute-start(f32[3,3,32,512]{3,2,1,0:T(8,128)} %slice.398), channel_id=1, source_target_pairs={{0,8},{1,9},{2,10},{3,11},{4,12},{5,13},{6,14},{7,15},{8,16},{9,17... | collective-permute-start | bytes 1769480 | tf_op jit(solution)/shard_map/ppermute | solution.py:154
  14.4 37.8 %collective-permute-start.3 = (f32[3,16,3,512]{3,2,1,0:T(4,128)}, f32[3,16,3,512]{3,2,1,0:T(4,128)S(1)}, u32[]{:S(2)}, u32[]{:S(2)}) collective-permute-start(f32[3,16,3,512]{3,2,1,0:T(4,128)} %get-tuple-element.35), channel_id=1, source_target_pairs={{0,1},{1,2},{2,3},{3,4},{4,5},{5,6},{6,7},{8,9},{9,10},{10,11},{11... | collective-permute-start | bytes 884744 | tf_op jit(solution)/shard_map/ppermute | solution.py:154
  18.7 33.5 %collective-permute-start.6 = (f32[3,3,32,512]{3,2,1,0:T(8,128)}, f32[3,3,32,512]{3,2,1,0:T(8,128)}, u32[]{:S(2)}, u32[]{:S(2)}) collective-permute-start(f32[3,3,32,512]{3,2,1,0:T(8,128)} %pad_maximum_fusion.7), channel_id=1, source_target_pairs={{8,0},{9,1},{10,2},{11,3},{12,4},{13,5},{14,6},{15,7},{16,8},{17,9... | collective-permute-start | bytes 1769480 | tf_op jit(solution)/shard_map/ppermute | solution.py:154
  23.5 4.9 %copy-start.3 = (s32[512]{0:T(512)}, s32[512]{0:T(512)S(1)}, u32[]{:S(2)}) copy-start(s32[512]{0:T(512)S(1)} %get-tuple-element.47) | copy-start | bytes 6148
  23.5 4.9 %copy-start.5 = (s32[512]{0:T(512)}, s32[512]{0:T(512)S(1)}, u32[]{:S(2)}) copy-start(s32[512]{0:T(512)S(1)} %get-tuple-element.48) | copy-start | bytes 6148
  23.5 4.9 %copy-start.13 = (pred[512]{0:T(512)(128)(4,1)}, pred[512]{0:T(512)(128)(4,1)S(1)}, u32[]{:S(2)}) copy-start(pred[512]{0:T(512)(128)(4,1)S(1)} %fusion.215) | copy-start | bytes 1540
  24.1 4.3 %copy-start.7 = (s32[32]{0:T(128)}, s32[32]{0:T(128)S(1)}, u32[]{:S(2)}) copy-start(s32[32]{0:T(128)S(1)} %get-tuple-element.49) | copy-start | bytes 388
  24.1 4.3 %copy-start.9 = (s32[32]{0:T(128)}, s32[32]{0:T(128)S(1)}, u32[]{:S(2)}) copy-start(s32[32]{0:T(128)S(1)} %get-tuple-element.50) | copy-start | bytes 388
  24.2 4.3 %copy-start.11 = (pred[32]{0:T(512)(128)(4,1)}, pred[32]{0:T(512)(128)(4,1)S(1)}, u32[]{:S(2)}) copy-start(pred[32]{0:T(512)(128)(4,1)S(1)} %compare_and_fusion.1) | copy-start | bytes 100
  24.2 28.0 %collective-permute-start.4 = (f32[3,16,3,512]{3,2,1,0:T(4,128)}, f32[3,16,3,512]{3,2,1,0:T(4,128)}, u32[]{:S(2)}, u32[]{:S(2)}) collective-permute-start(f32[3,16,3,512]{3,2,1,0:T(4,128)} %get-tuple-element.36), channel_id=1, source_target_pairs={{1,0},{2,1},{3,2},{4,3},{5,4},{6,5},{7,6},{9,8},{10,9},{11,10},{12... | collective-permute-start | bytes 884744 | tf_op jit(solution)/shard_map/ppermute | solution.py:154
  28.5 17.0 %collective-permute-start.5 = (f32[3,3,3,512]{3,2,1,0:T(4,128)}, f32[3,3,3,512]{3,2,1,0:T(4,128)}, u32[]{:S(2)}, u32[]{:S(2)}) collective-permute-start(f32[3,3,3,512]{3,2,1,0:T(4,128)} %get-tuple-element.33), channel_id=1, source_target_pairs={{8,1},{9,2},{10,3},{11,4},{12,5},{13,6},{14,7},{16,9},{17,10},{18,... | collective-permute-start | bytes 165896 | tf_op jit(solution)/shard_map/ppermute | solution.py:154
  45.4 6.8 %collective-permute-start.7 = (f32[3,3,3,512]{3,2,1,0:T(4,128)}, f32[3,3,3,512]{3,2,1,0:T(4,128)S(1)}, u32[]{:S(2)}, u32[]{:S(2)}) collective-permute-start(f32[3,3,3,512]{3,2,1,0:T(4,128)} %get-tuple-element.32), channel_id=1, source_target_pairs={{9,0},{10,1},{11,2},{12,3},{13,4},{14,5},{15,6},{17,8},{18,9},{19,... | collective-permute-start | bytes 165896 | tf_op jit(solution)/shard_map/ppermute | solution.py:154
  57.0 2.2 %copy-start.15 = (pred[22]{0:T(512)(128)(4,1)S(1)}, pred[22]{0:T(512)(128)(4,1)}, u32[]{:S(2)}) copy-start(pred[22]{0:T(512)(128)(4,1)} %compare_and_fusion.3) | copy-start | bytes 70
  70.9 2.7 %copy-start.4 = (s32[512]{0:T(512)S(1)}, s32[512]{0:T(512)}, u32[]{:S(2)}) copy-start(s32[512]{0:T(512)} %copy-done.3) | copy-start | bytes 6148
  70.9 2.7 %copy-start.6 = (s32[512]{0:T(512)S(1)}, s32[512]{0:T(512)}, u32[]{:S(2)}) copy-start(s32[512]{0:T(512)} %copy-done.5) | copy-start | bytes 6148
  70.9 2.7 %copy-start.14 = (pred[512]{0:T(512)(128)(4,1)S(1)}, pred[512]{0:T(512)(128)(4,1)}, u32[]{:S(2)}) copy-start(pred[512]{0:T(512)(128)(4,1)} %copy-done.13) | copy-start | bytes 1540
  70.9 3.2 %copy-start.8 = (s32[32]{0:T(128)S(1)}, s32[32]{0:T(128)}, u32[]{:S(2)}) copy-start(s32[32]{0:T(128)} %copy-done.7) | copy-start | bytes 388
  70.9 3.2 %copy-start.10 = (s32[32]{0:T(128)S(1)}, s32[32]{0:T(128)}, u32[]{:S(2)}) copy-start(s32[32]{0:T(128)} %copy-done.9) | copy-start | bytes 388
  71.0 3.2 %copy-start.12 = (pred[32]{0:T(512)(128)(4,1)S(1)}, pred[32]{0:T(512)(128)(4,1)}, u32[]{:S(2)}) copy-start(pred[32]{0:T(512)(128)(4,1)} %copy-done.11) | copy-start | bytes 100
  74.3 15.3 %collective-permute-start.8 = (f32[2,4,8,128]{3,2,1,0:T(8,128)S(1)}, f32[2,4,8,128]{3,2,1,0:T(8,128)S(1)}, u32[]{:S(2)}, u32[]{:S(2)}) collective-permute-start(f32[2,4,8,128]{3,2,1,0:T(8,128)S(1)} %pad_maximum_fusion.19), channel_id=1, source_target_pairs={{0,16},{8,24},{16,32},{24,40},{32,48},{40,56},{48,64},{56,72},{64,... | collective-permute-start | bytes 98312 | tf_op jit(solution)/shard_map/ppermute | solution.py:25
  76.2 13.4 %collective-permute-start.9 = (f32[2,4,8,128]{3,2,1,0:T(8,128)S(1)}, f32[2,4,8,128]{3,2,1,0:T(8,128)S(1)}, u32[]{:S(2)}, u32[]{:S(2)}) collective-permute-start(f32[2,4,8,128]{3,2,1,0:T(8,128)S(1)} %pad_maximum_fusion.19), channel_id=1, source_target_pairs={{0,8},{8,16},{16,24},{24,32},{32,40},{40,48},{48,56},{56,64},{64,7... | collective-permute-start | bytes 98312 | tf_op jit(solution)/shard_map/ppermute | solution.py:25
  78.1 11.5 %collective-permute-start.10 = (f32[2,4,8,128]{3,2,1,0:T(8,128)S(1)}, f32[2,4,8,128]{3,2,1,0:T(8,128)S(1)}, u32[]{:S(2)}, u32[]{:S(2)}) collective-permute-start(f32[2,4,8,128]{3,2,1,0:T(8,128)S(1)} %pad_maximum_fusion.19), channel_id=1, source_target_pairs={{8,0},{16,8},{24,16},{32,24},{40,32},{48,40},{56,48},{64,56},{72,6... | collective-permute-start | bytes 98312 | tf_op jit(solution)/shard_map/ppermute | solution.py:26
  84.2 7.3 %collective-permute-start.11 = (f32[2,4,8,128]{3,2,1,0:T(8,128)S(1)}, f32[2,4,8,128]{3,2,1,0:T(8,128)S(1)}, u32[]{:S(2)}, u32[]{:S(2)}) collective-permute-start(f32[2,4,8,128]{3,2,1,0:T(8,128)S(1)} %pad_maximum_fusion.19), channel_id=1, source_target_pairs={{16,0},{24,8},{32,16},{40,24},{48,32},{56,40},{64,48},{72,56},{80,... | collective-permute-start | bytes 98312 | tf_op jit(solution)/shard_map/ppermute | solution.py:26
  91.5 7.2 %collective-permute-start.12 = (f32[2,20,8,128]{3,2,1,0:T(8,128)S(1)}, f32[2,20,8,128]{3,2,1,0:T(8,128)S(1)}, u32[]{:S(2)}, u32[]{:S(2)}) collective-permute-start(f32[2,20,8,128]{3,2,1,0:T(8,128)S(1)} %constant_dynamic-update-slice_fusion), channel_id=1, source_target_pairs={{0,1},{1,2},{2,3},{3,4},{4,5},{5,6},{6,7},{8,9},{9,10},{10,11},{11... | collective-permute-start | bytes 491528 | tf_op jit(solution)/shard_map/ppermute | solution.py:25
  95.3 8.1 %collective-permute-start.13 = (f32[2,20,8,128]{3,2,1,0:T(8,128)S(1)}, f32[2,20,8,128]{3,2,1,0:T(8,128)S(1)}, u32[]{:S(2)}, u32[]{:S(2)}) collective-permute-start(f32[2,20,8,128]{3,2,1,0:T(8,128)S(1)} %constant_dynamic-update-slice_fusion), channel_id=1, source_target_pairs={{1,0},{2,1},{3,2},{4,3},{5,4},{6,5},{7,6},{9,8},{10,9},{11,10},{12... | collective-permute-start | bytes 491528 | tf_op jit(solution)/shard_map/ppermute | solution.py:26

commit v4 on v2

--- a/solution.py
+++ b/solution.py
@@ -46,19 +46,6 @@
     if side < 0:
         return jnp.concatenate([zeros, field[:, :, :-1]], axis=2)
     return jnp.concatenate([field[:, :, 1:], zeros], axis=2)
-
-
-def fine_neighbours(field):
-    xl, xh = halo_from(field, "box", 0, 1, 1)
-    yl, yh = halo_from(field, "group", 1, 1, 1)
-    return [
-        jnp.concatenate([xl, field[:-1]], axis=0),
-        jnp.concatenate([field[1:], xh], axis=0),
-        jnp.concatenate([yl, field[:, :-1]], axis=1),
-        jnp.concatenate([field[:, 1:], yh], axis=1),
-        shift_z(field, -1),
-        shift_z(field, 1),
-    ]
 
 
 def padded_neighbours(padded):
@@ -154,16 +141,37 @@
     return inside
 
 
+def low_faces(b):
+    faces = []
+    for dim in range(3):
+        n = b.shape[dim]
+        lo = lax.slice_in_dim(b, 0, n - 1, axis=dim)
+        hi = lax.slice_in_dim(b, 1, n, axis=dim)
+        inner = jnp.where((lo > 0) & (hi > 0), 2.0 * hi * lo / (hi + lo), hi + lo)
+        faces.append(jnp.concatenate([lax.slice_in_dim(b, 0, 1, axis=dim), inner], axis=dim))
+    return faces
+
+
+def face_pairs(b, faces):
+    pairs = []
+    for dim, lo in enumerate(faces):
+        n = b.shape[dim]
+        hi = jnp.concatenate(
+            [lax.slice_in_dim(lo, 1, n, axis=dim), lax.slice_in_dim(b, n - 1, n, axis=dim)], axis=dim
+        )
+        pairs += [lo, hi]
+    return pairs
+
+
 def per_device(right_side, inv_density, pressure):
     depth = SWEEPS + 1
     sx, sy, sz = pressure.shape
     both = jnp.stack([right_side, inv_density, pressure])
-    both = deep_extend(both, "box", 1, depth)
-    both = deep_extend(both, "group", 2, depth)
+    both = deep_extend(deep_extend(both, "box", 1, depth), "group", 2, depth)
     rhs_e, b_e, fine = both[0], both[1], both[2]
     totals = (sx * lax.axis_size("box"), sy * lax.axis_size("group"))
     inside = grid_mask(fine.shape, depth, ("box", "group"), totals)
-    coefs = coefs_of(b_e, padded_neighbours(jnp.pad(b_e, 1)))
+    coefs = face_pairs(b_e, low_faces(b_e))
     diag = sum(coefs)
     for sweep in range(SWEEPS):
         step = 2.0 / 3.0 * (rhs_e - apply_op(fine, padded_neighbours(jnp.pad(fine, 1)), coefs)) / diag

time: 114 us -> 104 us (0.912)
  other arithmetic: 37 us -> 27 us
    select_n x2, other arithmetic: 18.4 us -> 8.98 us  [per_device(): fine = jnp.where(inside, fine + step, 0.0)]
    reduce_sum x2, other arithmetic: 5.05 us -> 2.67 us  [block_mean(): fx = field.reshape(sx // 4, 4, sy, sz).sum(axis=1)]
    select_n x0 -> x3, other arithmetic: none -> 1.74 us  [low_faces(): inner = jnp.where((lo > 0) & (hi > 0), 2.0 * hi * lo / (hi + lo), hi + lo)]
where the time goes in v4:
time: 104 us; the launch traced here: 103 us
  starting transfers between devices  38.9 us (37%)
  waiting for transfers between devices  33 us (32%)
  other arithmetic  27 us (26%)
  matrix products  2.05 us (2%)
  local copies, waits for them, and re-layouts  1.91 us (2%)
    ppermute x5, waiting for transfers between devices, halo_from(): lax.ppermute(lax.slice_in_dim(block, n - width, n, axis=dim), axis, forward)  22.3 us
    ppermute x5, starting transfers between devices, halo_from(): lax.ppermute(lax.slice_in_dim(block, n - width, n, axis=dim), axis, forward)  19.6 us
    ppermute x5, starting transfers between devices, halo_from(): lax.ppermute(lax.slice_in_dim(block, 0, width, axis=dim), axis, backward)  19.2 us
    ppermute x5, waiting for transfers between devices, halo_from(): lax.ppermute(lax.slice_in_dim(block, 0, width, axis=dim), axis, backward)  10.7 us
    select_n x2, other arithmetic, per_device(): fine = jnp.where(inside, fine + step, 0.0)  8.98 us
    slice x2, other arithmetic, halo_from(): lax.slice_in_dim(block, n - width, n, axis=dim)  4.02 us
    reduce_sum x2, other arithmetic, block_mean(): fx = field.reshape(sx // 4, 4, sy, sz).sum(axis=1)  2.67 us
    mul x1, other arithmetic, apply_op(): total = total + coef * (field - near)  2.65 us
  transfers between devices with their start and end apart: 10, of which 6 were waited for; matrix products, arithmetic and copies ran while one was open for 1% of the time, Pallas kernels for 0%

profile of v4, /device:TPU:34, one launch (start us, length us, event | category | flops | bytes accessed | tf_op | source)
XLA Modules:
  0.0 103.3 jit_solution(11036545883680857378)
XLA Ops:
  0.0 2.6 %pad_maximum_fusion.9 = (f32[3,3,32,512]{3,2,1,0:T(8,128)}, f32[3,3,32,512]{3,2,1,0:T(8,128)}) fusion(f32[1,16,32,512]{3,2,1,0:T(8,128)} %bitcast.78, f32[1,16,32,512]{3,2,1,0:T(8,128)} %bitcast.74, f32[1,16,32,512]{3,2,1,0:T(8,128)} %bitcast.82), kind=kLoop, calls=%fused_computation.166 | loop fusion | flops 589824 | bytes 4325376 | tf_op jit(solution)/shard_map/slice | solution.py:25
  2.6 1.9 %collective-permute-start = (f32[3,3,32,512]{3,2,1,0:T(8,128)}, f32[3,3,32,512]{3,2,1,0:T(8,128)}, u32[]{:S(2)}, u32[]{:S(2)}) collective-permute-start(f32[3,3,32,512]{3,2,1,0:T(8,128)} %get-tuple-element.35), channel_id=1, source_target_pairs={{0,8},{8,16},{16,24},{24,32},{32,40},{40,48},{48,56},{56,64},{64,7... | collective-permute-start | bytes 1769480 | tf_op jit(solution)/shard_map/ppermute | solution.py:25
  4.6 6.0 %collective-permute-start.1 = (f32[3,3,32,512]{3,2,1,0:T(8,128)}, f32[3,3,32,512]{3,2,1,0:T(8,128)}, u32[]{:S(2)}, u32[]{:S(2)}) collective-permute-start(f32[3,3,32,512]{3,2,1,0:T(8,128)} %get-tuple-element.36), channel_id=1, source_target_pairs={{8,0},{16,8},{24,16},{32,24},{40,32},{48,40},{56,48},{64,56},{72,6... | collective-permute-start | bytes 1769480 | tf_op jit(solution)/shard_map/ppermute | solution.py:26
  10.8 5.9 %collective-permute-done = f32[3,3,32,512]{3,2,1,0:T(8,128)} collective-permute-done((f32[3,3,32,512]{3,2,1,0:T(8,128)}, f32[3,3,32,512]{3,2,1,0:T(8,128)}, u32[]{:S(2)}, u32[]{:S(2)}) %collective-permute-start) | collective-permute-done | bytes 589856 | tf_op jit(solution)/shard_map/ppermute | solution.py:25
  16.7 1.7 %collective-permute-done.1 = f32[3,3,32,512]{3,2,1,0:T(8,128)} collective-permute-done((f32[3,3,32,512]{3,2,1,0:T(8,128)}, f32[3,3,32,512]{3,2,1,0:T(8,128)}, u32[]{:S(2)}, u32[]{:S(2)}) %collective-permute-start.1) | collective-permute-done | bytes 589856 | tf_op jit(solution)/shard_map/ppermute | solution.py:26
  18.4 1.4 %pad_maximum_fusion.14 = (f32[3,22,3,512]{3,2,1,0:T(4,128)S(1)}, f32[3,22,3,512]{3,2,1,0:T(4,128)S(1)}) fusion(f32[3,3,32,512]{3,2,1,0:T(8,128)} %collective-permute-done.1, f32[3,3,32,512]{3,2,1,0:T(8,128)} %collective-permute-done, f32[1,16,32,512]{3,2,1,0:T(8,128)S(1)} %bitcast.79, f32[1,16,32,512]{3,2,1,0:T(8,128)S(1)} %bitcast.75, ...), kind=kLoop, calls=%fused_computation.171 | loop fusion | flops 811008 | bytes 5136384 | tf_op jit(solution)/shard_map/slice | solution.py:25
  19.8 0.1 copy.11
  19.9 3.0 %collective-permute-start.2 = (f32[3,22,3,512]{3,1,2,0:T(8,128)S(1)}, f32[3,22,3,512]{3,1,2,0:T(8,128)S(1)}, u32[]{:S(2)}, u32[]{:S(2)}) collective-permute-start(f32[3,22,3,512]{3,1,2,0:T(8,128)S(1)} %copy.11), channel_id=1, source_target_pairs={{0,1},{1,2},{2,3},{3,4},{4,5},{5,6},{6,7},{8,9},{9,10},{10,11},{11... | collective-permute-start | bytes 1216520 | tf_op jit(solution)/shard_map/ppermute | solution.py:25
  22.9 0.1 copy.12
  23.1 2.8 %collective-permute-start.3 = (f32[3,22,3,512]{3,1,2,0:T(8,128)S(1)}, f32[3,22,3,512]{3,1,2,0:T(8,128)S(1)}, u32[]{:S(2)}, u32[]{:S(2)}) collective-permute-start(f32[3,22,3,512]{3,1,2,0:T(8,128)S(1)} %copy.12), channel_id=1, source_target_pairs={{1,0},{2,1},{3,2},{4,3},{5,4},{6,5},{7,6},{9,8},{10,9},{11,10},{12... | collective-permute-start | bytes 1216520 | tf_op jit(solution)/shard_map/ppermute | solution.py:26
  25.9 0.5 fusion.206
  26.4 0.1 fusion.48
  26.6 14.3 %collective-permute-done.2 = f32[3,22,3,512]{3,1,2,0:T(8,128)S(1)} collective-permute-done((f32[3,22,3,512]{3,1,2,0:T(8,128)S(1)}, f32[3,22,3,512]{3,1,2,0:T(8,128)S(1)}, u32[]{:S(2)}, u32[]{:S(2)}) %collective-permute-start.2) | collective-permute-done | bytes 405536 | tf_op jit(solution)/shard_map/ppermute | solution.py:25
  40.9 0.3 copy.13
  41.2 0.3 copy.14
  41.5 2.3 %pad_maximum_fusion = f32[3,22,38,512]{3,2,1,0:T(8,128)S(1)} fusion(f32[3,22,3,512]{3,2,1,0:T(4,128)S(1)} %copy.14, f32[3,3,32,512]{3,2,1,0:T(8,128)} %collective-permute-done.1, f32[1,16,32,512]{3,2,1,0:T(8,128)S(1)} %bitcast.80, f32[1,16,32,512]{3,2,1,0:T(8,128)S(1)} %bitcast.76, f32[1,16,32,512]{3,2,1,0:T(8,128)S(1)} %bitcast.84, ...), kind=kLoop, calls=%fused_computation | loop fusion | flops 7704576 | bytes 10272768 | tf_op jit(solution)/shard_map/concatenate | solution.py:41
  43.7 0.8 slice_bitcast_fusion.1
  44.5 0.2 fusion.227
  44.8 0.6 divide_select_fusion
  45.4 0.6 divide_select_fusion.1
  46.1 0.5 divide_select_fusion.2
  46.6 0.9 maximum_bitcast_fusion.1
  47.5 4.5 %and_select_fusion.1 = f32[22,38,512]{2,1,0:T(8,128)S(1)} fusion(f32[22,38,512]{2,1,0:T(8,128)S(1)} %get-tuple-element.28, f32[22,1,512]{2,1,0:T(1,128)S(1)} %get-tuple-element.44, f32[22,37,512]{2,1,0:T(8,128)S(1)} %divide_select_fusion.1, f32[22,1,512]{2,1,0:T(1,128)S(1)} %get-tuple-element.43, f32[22,38,1]{2,1,0:T(8,128)S(1)} %get-tuple-element.42, ...), kind=kLoop, calls=%fused_computation.31 | loop fusion | flops 14553088 | bytes 10399052 | tf_op jit(solution)/shard_map/jit(_where)/select_n | solution.py:178
  52.0 4.5 %and_select_fusion = f32[22,38,512]{2,1,0:T(8,128)S(1)} fusion(f32[22,38,512]{2,1,0:T(8,128)S(1)} %and_select_fusion.1, f32[22,1,512]{2,1,0:T(1,128)S(1)} %get-tuple-element.44, f32[22,37,512]{2,1,0:T(8,128)S(1)} %divide_select_fusion.1, f32[22,1,512]{2,1,0:T(1,128)S(1)} %get-tuple-element.43, f32[22,38,1]{2,1,0:T(8,128)S(1)} %get-tuple-element.42, ...), kind=kLoop, calls=%fused_computation.30 | loop fusion | flops 14553088 | bytes 10399052 | tf_op jit(solution)/shard_map/jit(_where)/select_n | solution.py:178
  56.5 2.7 %fusion.43 = (f32[22,38,512]{2,1,0:T(8,128)S(1)}, f32[22,38,512]{2,1,0:T(8,128)S(1)}, f32[22,38,512]{2,1,0:T(8,128)S(1)}, f32[22,38,512]{2,1,0:T(8,128)S(1)}, f3...) fusion(f32[22,38,512]{2,1,0:T(8,128)S(1)} %and_select_fusion, f32[21,38,512]{2,1,0:T(8,128)S(1)} %divide_select_fusion.2, ...), kind=kLoop, calls=%fused_computation.75 | loop fusion | flops 2996224 | bytes 13774848 | tf_op jit(solution)/shard_map/mul | solution.py:69
  59.1 2.6 %bitcast_reduce_fusion = f32[4,32,512]{2,1,0:T(8,128)S(1)} fusion(f32[22,38,512]{2,1,0:T(8,128)S(1)} %get-tuple-element.38, f32[22,38,1]{2,1,0:T(8,128)S(1)} %get-tuple-element.42, f32[22,38,511]{2,1,0:T(8,128)S(1)} %divide_select_fusion, f32[22,38,512]{2,1,0:T(8,128)S(1)} %get-tuple-element.37, f32[22,38,1]{2,1,0:T(8,128)S(1)} %get-tuple-element.41, ...), kind=kLoop, calls=%fused_computation.162 | loop fusion | flops 4653056 | bytes 12123408 | tf_op jit(solution)/shard_map/reduce_sum | solution.py:81
  61.7 0.5 fusion.204
  62.2 0.1 fusion.47
  62.3 9.2 %collective-permute-start.4 = (f32[2,4,8,128]{3,2,1,0:T(8,128)S(1)}, f32[2,4,8,128]{3,2,1,0:T(8,128)S(1)}, u32[]{:S(2)}, u32[]{:S(2)}) collective-permute-start(f32[2,4,8,128]{3,2,1,0:T(8,128)S(1)} %pad_maximum_fusion.16), channel_id=1, source_target_pairs={{0,16},{8,24},{16,32},{24,40},{32,48},{40,56},{48,64},{56,72},{64,... | collective-permute-start | bytes 98312 | tf_op jit(solution)/shard_map/ppermute | solution.py:25
  71.5 1.9 %collective-permute-start.5 = (f32[2,4,8,128]{3,2,1,0:T(8,128)S(1)}, f32[2,4,8,128]{3,2,1,0:T(8,128)S(1)}, u32[]{:S(2)}, u32[]{:S(2)}) collective-permute-start(f32[2,4,8,128]{3,2,1,0:T(8,128)S(1)} %pad_maximum_fusion.16), channel_id=1, source_target_pairs={{0,8},{8,16},{16,24},{24,32},{32,40},{40,48},{48,56},{56,64},{64,7... | collective-permute-start | bytes 98312 | tf_op jit(solution)/shard_map/ppermute | solution.py:25
  73.5 6.0 %collective-permute-start.6 = (f32[2,4,8,128]{3,2,1,0:T(8,128)S(1)}, f32[2,4,8,128]{3,2,1,0:T(8,128)S(1)}, u32[]{:S(2)}, u32[]{:S(2)}) collective-permute-start(f32[2,4,8,128]{3,2,1,0:T(8,128)S(1)} %pad_maximum_fusion.16), channel_id=1, source_target_pairs={{8,0},{16,8},{24,16},{32,24},{40,32},{48,40},{56,48},{64,56},{72,6... | collective-permute-start | bytes 98312 | tf_op jit(solution)/shard_map/ppermute | solution.py:26
  79.5 2.1 %collective-permute-start.7 = (f32[2,4,8,128]{3,2,1,0:T(8,128)S(1)}, f32[2,4,8,128]{3,2,1,0:T(8,128)S(1)}, u32[]{:S(2)}, u32[]{:S(2)}) collective-permute-start(f32[2,4,8,128]{3,2,1,0:T(8,128)S(1)} %pad_maximum_fusion.16), channel_id=1, source_target_pairs={{16,0},{24,8},{32,16},{40,24},{48,32},{56,40},{64,48},{72,56},{80,... | collective-permute-start | bytes 98312 | tf_op jit(solution)/shard_map/ppermute | solution.py:26
  81.7 5.3 %collective-permute-done.7 = f32[2,4,8,128]{3,2,1,0:T(8,128)S(1)} collective-permute-done((f32[2,4,8,128]{3,2,1,0:T(8,128)S(1)}, f32[2,4,8,128]{3,2,1,0:T(8,128)S(1)}, u32[]{:S(2)}, u32[]{:S(2)}) %collective-permute-start.7) | collective-permute-done | bytes 32800 | tf_op jit(solution)/shard_map/ppermute | solution.py:26
  87.0 3.6 %collective-permute-start.8 = (f32[2,20,8,128]{3,2,1,0:T(8,128)S(1)}, f32[2,20,8,128]{3,2,1,0:T(8,128)S(1)}, u32[]{:S(2)}, u32[]{:S(2)}) collective-permute-start(f32[2,20,8,128]{3,2,1,0:T(8,128)S(1)} %constant_dynamic-update-slice_fusion), channel_id=1, source_target_pairs={{0,1},{1,2},{2,3},{3,4},{4,5},{5,6},{6,7},{8,9},{9,10},{10,11},{11... | collective-permute-start | bytes 491528 | tf_op jit(solution)/shard_map/ppermute | solution.py:25
  90.6 2.2 %collective-permute-start.9 = (f32[2,20,8,128]{3,2,1,0:T(8,128)S(1)}, f32[2,20,8,128]{3,2,1,0:T(8,128)S(1)}, u32[]{:S(2)}, u32[]{:S(2)}) collective-permute-start(f32[2,20,8,128]{3,2,1,0:T(8,128)S(1)} %constant_dynamic-update-slice_fusion), channel_id=1, source_target_pairs={{1,0},{2,1},{3,2},{4,3},{5,4},{6,5},{7,6},{9,8},{10,9},{11,10},{12... | collective-permute-start | bytes 491528 | tf_op jit(solution)/shard_map/ppermute | solution.py:26
  92.9 2.1 %collective-permute-done.8 = f32[2,20,8,128]{3,2,1,0:T(8,128)S(1)} collective-permute-done((f32[2,20,8,128]{3,2,1,0:T(8,128)S(1)}, f32[2,20,8,128]{3,2,1,0:T(8,128)S(1)}, u32[]{:S(2)}, u32[]{:S(2)}) %collective-permute-start.8) | collective-permute-done | bytes 163872 | tf_op jit(solution)/shard_map/ppermute | solution.py:25
  95.0 3.7 %collective-permute-done.9 = f32[2,20,8,128]{3,2,1,0:T(8,128)S(1)} collective-permute-done((f32[2,20,8,128]{3,2,1,0:T(8,128)S(1)}, f32[2,20,8,128]{3,2,1,0:T(8,128)S(1)}, u32[]{:S(2)}, u32[]{:S(2)}) %collective-permute-start.9) | collective-permute-done | bytes 163872 | tf_op jit(solution)/shard_map/ppermute | solution.py:26
  98.8 0.5 fusion.189
  99.3 0.3 fusion.190
  99.7 0.3 multiply_add_fusion.4
  99.9 0.3 multiply_add_fusion.3
  100.2 0.3 multiply_add_fusion.2
  100.5 0.3 multiply_add_fusion.1
  100.8 0.3 multiply_add_fusion
  101.1 0.2 fusion.176
  101.3 0.5 fusion.193
  101.8 0.3 convolution_bitcast_fusion
  102.1 1.2 %bitcast_add_fusion = f32[16,32,512]{2,1,0:T(8,128)} fusion(f32[22,38,512]{2,1,0:T(8,128)S(1)} %and_select_fusion, f32[4,32,512]{2,1,0:T(8,128)S(1)} %convolution_bitcast_fusion), kind=kLoop, calls=%fused_computation.161 | loop fusion | flops 262144 | bytes 2359296 | tf_op jit(solution)/shard_map/add | solution.py:185
  (28 shorter events, 0.3 us)
Async XLA Ops:
  0.0 10.7 %copy-start = (f32[16,32,512]{2,1,0:T(8,128)S(1)}, f32[16,32,512]{2,1,0:T(8,128)}, u32[]{:S(2)}) copy-start(f32[16,32,512]{2,1,0:T(8,128)} %param.4) | copy-start | bytes 3145732
  0.0 18.4 %copy-start.1 = (f32[16,32,512]{2,1,0:T(8,128)S(1)}, f32[16,32,512]{2,1,0:T(8,128)}, u32[]{:S(2)}) copy-start(f32[16,32,512]{2,1,0:T(8,128)} %param.5) | copy-start | bytes 3145732
  0.0 18.4 %copy-start.2 = (f32[16,32,512]{2,1,0:T(8,128)S(1)}, f32[16,32,512]{2,1,0:T(8,128)}, u32[]{:S(2)}) copy-start(f32[16,32,512]{2,1,0:T(8,128)} %param.3) | copy-start | bytes 3145732
  2.6 14.0 %collective-permute-start = (f32[3,3,32,512]{3,2,1,0:T(8,128)}, f32[3,3,32,512]{3,2,1,0:T(8,128)}, u32[]{:S(2)}, u32[]{:S(2)}) collective-permute-start(f32[3,3,32,512]{3,2,1,0:T(8,128)} %get-tuple-element.35), channel_id=1, source_target_pairs={{0,8},{8,16},{16,24},{24,32},{32,40},{40,48},{48,56},{56,64},{64,7... | collective-permute-start | bytes 1769480 | tf_op jit(solution)/shard_map/ppermute | solution.py:25
  4.6 13.8 %collective-permute-start.1 = (f32[3,3,32,512]{3,2,1,0:T(8,128)}, f32[3,3,32,512]{3,2,1,0:T(8,128)}, u32[]{:S(2)}, u32[]{:S(2)}) collective-permute-start(f32[3,3,32,512]{3,2,1,0:T(8,128)} %get-tuple-element.36), channel_id=1, source_target_pairs={{8,0},{16,8},{24,16},{32,24},{40,32},{48,40},{56,48},{64,56},{72,6... | collective-permute-start | bytes 1769480 | tf_op jit(solution)/shard_map/ppermute | solution.py:26
  19.9 21.0 %collective-permute-start.2 = (f32[3,22,3,512]{3,1,2,0:T(8,128)S(1)}, f32[3,22,3,512]{3,1,2,0:T(8,128)S(1)}, u32[]{:S(2)}, u32[]{:S(2)}) collective-permute-start(f32[3,22,3,512]{3,1,2,0:T(8,128)S(1)} %copy.11), channel_id=1, source_target_pairs={{0,1},{1,2},{2,3},{3,4},{4,5},{5,6},{6,7},{8,9},{9,10},{10,11},{11... | collective-permute-start | bytes 1216520 | tf_op jit(solution)/shard_map/ppermute | solution.py:25
  23.1 18.1 %collective-permute-start.3 = (f32[3,22,3,512]{3,1,2,0:T(8,128)S(1)}, f32[3,22,3,512]{3,1,2,0:T(8,128)S(1)}, u32[]{:S(2)}, u32[]{:S(2)}) collective-permute-start(f32[3,22,3,512]{3,1,2,0:T(8,128)S(1)} %copy.12), channel_id=1, source_target_pairs={{1,0},{2,1},{3,2},{4,3},{5,4},{6,5},{7,6},{9,8},{10,9},{11,10},{12... | collective-permute-start | bytes 1216520 | tf_op jit(solution)/shard_map/ppermute | solution.py:26
  62.3 19.3 %collective-permute-start.4 = (f32[2,4,8,128]{3,2,1,0:T(8,128)S(1)}, f32[2,4,8,128]{3,2,1,0:T(8,128)S(1)}, u32[]{:S(2)}, u32[]{:S(2)}) collective-permute-start(f32[2,4,8,128]{3,2,1,0:T(8,128)S(1)} %pad_maximum_fusion.16), channel_id=1, source_target_pairs={{0,16},{8,24},{16,32},{24,40},{32,48},{40,56},{48,64},{56,72},{64,... | collective-permute-start | bytes 98312 | tf_op jit(solution)/shard_map/ppermute | solution.py:25
  71.5 10.1 %collective-permute-start.5 = (f32[2,4,8,128]{3,2,1,0:T(8,128)S(1)}, f32[2,4,8,128]{3,2,1,0:T(8,128)S(1)}, u32[]{:S(2)}, u32[]{:S(2)}) collective-permute-start(f32[2,4,8,128]{3,2,1,0:T(8,128)S(1)} %pad_maximum_fusion.16), channel_id=1, source_target_pairs={{0,8},{8,16},{16,24},{24,32},{32,40},{40,48},{48,56},{56,64},{64,7... | collective-permute-start | bytes 98312 | tf_op jit(solution)/shard_map/ppermute | solution.py:25
  73.5 8.2 %collective-permute-start.6 = (f32[2,4,8,128]{3,2,1,0:T(8,128)S(1)}, f32[2,4,8,128]{3,2,1,0:T(8,128)S(1)}, u32[]{:S(2)}, u32[]{:S(2)}) collective-permute-start(f32[2,4,8,128]{3,2,1,0:T(8,128)S(1)} %pad_maximum_fusion.16), channel_id=1, source_target_pairs={{8,0},{16,8},{24,16},{32,24},{40,32},{48,40},{56,48},{64,56},{72,6... | collective-permute-start | bytes 98312 | tf_op jit(solution)/shard_map/ppermute | solution.py:26
  79.5 7.5 %collective-permute-start.7 = (f32[2,4,8,128]{3,2,1,0:T(8,128)S(1)}, f32[2,4,8,128]{3,2,1,0:T(8,128)S(1)}, u32[]{:S(2)}, u32[]{:S(2)}) collective-permute-start(f32[2,4,8,128]{3,2,1,0:T(8,128)S(1)} %pad_maximum_fusion.16), channel_id=1, source_target_pairs={{16,0},{24,8},{32,16},{40,24},{48,32},{56,40},{64,48},{72,56},{80,... | collective-permute-start | bytes 98312 | tf_op jit(solution)/shard_map/ppermute | solution.py:26
  87.0 8.0 %collective-permute-start.8 = (f32[2,20,8,128]{3,2,1,0:T(8,128)S(1)}, f32[2,20,8,128]{3,2,1,0:T(8,128)S(1)}, u32[]{:S(2)}, u32[]{:S(2)}) collective-permute-start(f32[2,20,8,128]{3,2,1,0:T(8,128)S(1)} %constant_dynamic-update-slice_fusion), channel_id=1, source_target_pairs={{0,1},{1,2},{2,3},{3,4},{4,5},{5,6},{6,7},{8,9},{9,10},{10,11},{11... | collective-permute-start | bytes 491528 | tf_op jit(solution)/shard_map/ppermute | solution.py:25
  90.6 8.1 %collective-permute-start.9 = (f32[2,20,8,128]{3,2,1,0:T(8,128)S(1)}, f32[2,20,8,128]{3,2,1,0:T(8,128)S(1)}, u32[]{:S(2)}, u32[]{:S(2)}) collective-permute-start(f32[2,20,8,128]{3,2,1,0:T(8,128)S(1)} %constant_dynamic-update-slice_fusion), channel_id=1, source_target_pairs={{1,0},{2,1},{3,2},{4,3},{5,4},{6,5},{7,6},{9,8},{10,9},{11,10},{12... | collective-permute-start | bytes 491528 | tf_op jit(solution)/shard_map/ppermute | solution.py:26

commit v5 on v4

--- a/solution.py
+++ b/solution.py
@@ -39,6 +39,22 @@
         need -= width
         hop += 1
     return jnp.concatenate(lows + [block] + highs, axis=dim)
+
+
+def halo_with_corners(block, depth):
+    assert depth <= block.shape[1] and depth <= block.shape[2]
+    xl, xh = halo_from(block, "box", 1, depth, 1)
+    yl, yh = halo_from(block, "group", 2, depth, 1)
+    sides = jnp.concatenate([yl, yh], axis=2)
+    low, high = halo_from(sides, "box", 1, depth, 1)
+    low_l, low_h = low[:, :, :depth], low[:, :, depth:]
+    high_l, high_h = high[:, :, :depth], high[:, :, depth:]
+    rows = [
+        jnp.concatenate([low_l, xl, low_h], axis=2),
+        jnp.concatenate([yl, block, yh], axis=2),
+        jnp.concatenate([high_l, xh, high_h], axis=2),
+    ]
+    return jnp.concatenate(rows, axis=1)
 
 
 def shift_z(field, side):
@@ -166,8 +182,7 @@
 def per_device(right_side, inv_density, pressure):
     depth = SWEEPS + 1
     sx, sy, sz = pressure.shape
-    both = jnp.stack([right_side, inv_density, pressure])
-    both = deep_extend(deep_extend(both, "box", 1, depth), "group", 2, depth)
+    both = halo_with_corners(jnp.stack([right_side, inv_density, pressure]), depth)
     rhs_e, b_e, fine = both[0], both[1], both[2]
     totals = (sx * lax.axis_size("box"), sy * lax.axis_size("group"))
     inside = grid_mask(fine.shape, depth, ("box", "group"), totals)

time: 104 us -> 102 us (0.981)
  waiting for transfers between devices: 33 us -> 20.3 us
  starting transfers between devices: 38.9 us -> 44.1 us
  other arithmetic: 27 us -> 31 us
  matrix products: 2.05 us -> 3.67 us
    ppermute x5 -> x6, waiting for transfers between devices: 22.3 us -> 11.7 us  [halo_from(): lax.ppermute(lax.slice_in_dim(block, n - width, n, axis=dim), axis, forward)]
    ppermute x5 -> x6, starting transfers between devices: 19.2 us -> 24.1 us  [halo_from(): lax.ppermute(lax.slice_in_dim(block, 0, width, axis=dim), axis, backward)]
    concatenate x0 -> x1, other arithmetic: none -> 2.38 us  [halo_with_corners(): return jnp.concatenate(rows, axis=1)]
    concatenate x2 -> x1, other arithmetic: 2.3 us -> 0.03 us  [deep_extend(): return jnp.concatenate(lows + [block] + highs, axis=dim)]
    ppermute x5 -> x6, waiting for transfers between devices: 10.7 us -> 8.56 us  [halo_from(): lax.ppermute(lax.slice_in_dim(block, 0, width, axis=dim), axis, backward)]
    slice x2 -> x3, other arithmetic: 4.02 us -> 4.75 us  [halo_from(): lax.slice_in_dim(block, n - width, n, axis=dim)]
    ppermute x5 -> x6, starting transfers between devices: 19.6 us -> 20 us  [halo_from(): lax.ppermute(lax.slice_in_dim(block, n - width, n, axis=dim), axis, forward)]
  transfers between devices with their start and end apart: 10 -> 12, of which waited for: 6 -> 6; matrix products, arithmetic and copies ran while one was open for 1% -> 7% of each run, Pallas kernels for 0% -> 0%
where the time goes in v5:
time: 102 us; the launch traced here: 101 us
  starting transfers between devices  44.1 us (43%)
  other arithmetic  31 us (30%)
  waiting for transfers between devices  20.3 us (20%)
  matrix products  3.67 us (4%)
  local copies, waits for them, and re-layouts  1.26 us (1%)
    ppermute x6, starting transfers between devices, halo_from(): lax.ppermute(lax.slice_in_dim(block, 0, width, axis=dim), axis, backward)  24.1 us
    ppermute x6, starting transfers between devices, halo_from(): lax.ppermute(lax.slice_in_dim(block, n - width, n, axis=dim), axis, forward)  20 us
    ppermute x6, waiting for transfers between devices, halo_from(): lax.ppermute(lax.slice_in_dim(block, n - width, n, axis=dim), axis, forward)  11.7 us
    select_n x2, other arithmetic, per_device(): fine = jnp.where(inside, fine + step, 0.0)  8.98 us
    ppermute x6, waiting for transfers between devices, halo_from(): lax.ppermute(lax.slice_in_dim(block, 0, width, axis=dim), axis, backward)  8.56 us
    slice x3, other arithmetic, halo_from(): lax.slice_in_dim(block, n - width, n, axis=dim)  4.75 us
    reduce_sum x2, other arithmetic, block_mean(): fx = field.reshape(sx // 4, 4, sy, sz).sum(axis=1)  3.39 us
    mul x1, other arithmetic, apply_op(): total = total + coef * (field - near)  2.66 us
  transfers between devices with their start and end apart: 12, of which 6 were waited for; matrix products, arithmetic and copies ran while one was open for 7% of the time, Pallas kernels for 0%

profile of v5, /device:TPU:34, one launch (start us, length us, event | category | flops | bytes accessed | tf_op | source)
XLA Modules:
  0.0 100.9 jit_solution(18304041951253325393)
XLA Ops:
  0.0 2.6 %pad_maximum_fusion.11 = (f32[3,16,3,512]{3,2,1,0:T(4,128)}, f32[3,16,3,512]{3,2,1,0:T(4,128)}) fusion(f32[1,16,32,512]{3,2,1,0:T(8,128)} %bitcast.77, f32[1,16,32,512]{3,2,1,0:T(8,128)} %bitcast.74, f32[1,16,32,512]{3,2,1,0:T(8,128)} %bitcast.80), kind=kLoop, calls=%fused_computation.169 | loop fusion | flops 294912 | bytes 3735552 | tf_op jit(solution)/shard_map/slice | solution.py:25
  2.6 3.0 %collective-permute-start = (f32[3,16,3,512]{3,2,1,0:T(4,128)}, f32[3,16,3,512]{3,2,1,0:T(4,128)S(1)}, u32[]{:S(2)}, u32[]{:S(2)}) collective-permute-start(f32[3,16,3,512]{3,2,1,0:T(4,128)} %get-tuple-element.33), channel_id=1, source_target_pairs={{0,1},{1,2},{2,3},{3,4},{4,5},{5,6},{6,7},{8,9},{9,10},{10,11},{11... | collective-permute-start | bytes 884744 | tf_op jit(solution)/shard_map/ppermute | solution.py:25
  5.6 2.8 %collective-permute-start.1 = (f32[3,16,3,512]{3,2,1,0:T(4,128)}, f32[3,16,3,512]{3,2,1,0:T(4,128)}, u32[]{:S(2)}, u32[]{:S(2)}) collective-permute-start(f32[3,16,3,512]{3,2,1,0:T(4,128)} %get-tuple-element.34), channel_id=1, source_target_pairs={{1,0},{2,1},{3,2},{4,3},{5,4},{6,5},{7,6},{9,8},{10,9},{11,10},{12... | collective-permute-start | bytes 884744 | tf_op jit(solution)/shard_map/ppermute | solution.py:26
  8.5 1.2 %pad_maximum_fusion.8 = (f32[3,3,32,512]{3,2,1,0:T(8,128)}, f32[3,3,32,512]{3,2,1,0:T(8,128)}) fusion(f32[1,16,32,512]{3,2,1,0:T(8,128)S(1)} %bitcast.78, f32[1,16,32,512]{3,2,1,0:T(8,128)S(1)} %bitcast.75, f32[1,16,32,512]{3,2,1,0:T(8,128)S(1)} %bitcast.81), kind=kLoop, calls=%fused_computation.166 | loop fusion | flops 589824 | bytes 4325376 | tf_op jit(solution)/shard_map/slice | solution.py:25
  9.7 1.9 %collective-permute-start.3 = (f32[3,3,32,512]{3,2,1,0:T(8,128)}, f32[3,3,32,512]{3,2,1,0:T(8,128)}, u32[]{:S(2)}, u32[]{:S(2)}) collective-permute-start(f32[3,3,32,512]{3,2,1,0:T(8,128)} %get-tuple-element.31), channel_id=1, source_target_pairs={{0,8},{8,16},{16,24},{24,32},{32,40},{40,48},{48,56},{56,64},{64,7... | collective-permute-start | bytes 1769480 | tf_op jit(solution)/shard_map/ppermute | solution.py:25
  11.6 6.0 %collective-permute-start.5 = (f32[3,3,32,512]{3,2,1,0:T(8,128)}, f32[3,3,32,512]{3,2,1,0:T(8,128)}, u32[]{:S(2)}, u32[]{:S(2)}) collective-permute-start(f32[3,3,32,512]{3,2,1,0:T(8,128)} %get-tuple-element.32), channel_id=1, source_target_pairs={{8,0},{16,8},{24,16},{32,24},{40,32},{48,40},{56,48},{64,56},{72,6... | collective-permute-start | bytes 1769480 | tf_op jit(solution)/shard_map/ppermute | solution.py:26
  17.7 0.6 iota_shift-right-logical_fusion.1
  18.3 0.6 compare_and_fusion.1
  18.8 0.8 bitcast_reduce_fusion.1
  19.6 0.5 compare_and_fusion.3
  20.2 1.4 %fusion.208 = f32[4,32,128]{2,1,0:T(8,128)S(1)} fusion(f32[4,32,512]{2,1,0:T(8,128)} %bitcast_reduce_fusion.1, s32[512]{0:T(512)S(1)} %get-tuple-element.51, s32[512]{0:T(512)S(1)} %get-tuple-element.52, pred[512]{0:T(512)(128)(4,1)S(1)} %fusion.215), kind=kOutput, calls=%fused_computation.347 | convolution fusion | flops 100794368 | bytes 332288 | tf_op jit(solution)/shard_map/xyz,zc->xyc/dot_general | solution.py:98
  21.7 0.8 fusion.48
  22.5 9.0 %collective-permute-done = f32[3,16,3,512]{3,2,1,0:T(4,128)S(1)} collective-permute-done((f32[3,16,3,512]{3,2,1,0:T(4,128)}, f32[3,16,3,512]{3,2,1,0:T(4,128)S(1)}, u32[]{:S(2)}, u32[]{:S(2)}) %collective-permute-start) | collective-permute-done | bytes 294944 | tf_op jit(solution)/shard_map/ppermute | solution.py:25
  31.5 1.0 pad_maximum_fusion.13
  32.4 1.9 %collective-permute-start.2 = (f32[3,3,6,512]{3,2,1,0:T(8,128)S(1)}, f32[3,3,6,512]{3,2,1,0:T(8,128)S(1)}, u32[]{:S(2)}, u32[]{:S(2)}) collective-permute-start(f32[3,3,6,512]{3,2,1,0:T(8,128)S(1)} %get-tuple-element.43), channel_id=1, source_target_pairs={{0,8},{8,16},{16,24},{24,32},{32,40},{40,48},{48,56},{56,64},{64,7... | collective-permute-start | bytes 331784 | tf_op jit(solution)/shard_map/ppermute | solution.py:25
  34.4 6.0 %collective-permute-start.4 = (f32[3,3,6,512]{3,2,1,0:T(8,128)S(1)}, f32[3,3,6,512]{3,2,1,0:T(8,128)S(1)}, u32[]{:S(2)}, u32[]{:S(2)}) collective-permute-start(f32[3,3,6,512]{3,2,1,0:T(8,128)S(1)} %get-tuple-element.44), channel_id=1, source_target_pairs={{8,0},{16,8},{24,16},{32,24},{40,32},{48,40},{56,48},{64,56},{72,6... | collective-permute-start | bytes 331784 | tf_op jit(solution)/shard_map/ppermute | solution.py:26
  40.4 0.9 collective-permute-done.2
  41.3 1.8 %collective-permute-done.4 = f32[3,3,6,512]{3,2,1,0:T(8,128)S(1)} collective-permute-done((f32[3,3,6,512]{3,2,1,0:T(8,128)S(1)}, f32[3,3,6,512]{3,2,1,0:T(8,128)S(1)}, u32[]{:S(2)}, u32[]{:S(2)}) %collective-permute-start.4) | collective-permute-done | bytes 110624 | tf_op jit(solution)/shard_map/ppermute | solution.py:26
  43.1 2.4 %maximum_maximum_fusion = f32[3,22,38,512]{3,2,1,0:T(8,128)S(1)} fusion(f32[3,3,3,512]{3,2,1,0:T(4,128)S(1)} %get-tuple-element.50, f32[3,3,32,512]{3,2,1,0:T(8,128)} %collective-permute-done.5, f32[3,3,3,512]{3,2,1,0:T(4,128)S(1)} %get-tuple-element.49, f32[3,16,3,512]{3,2,1,0:T(4,128)} %collective-permute-done.1, f32[1,16,32,512]{3,2,1,0:T(8,128)S(1)} %bitcast.79, ...), kind=kLoop, calls=%fused_computation | loop fusion | flops 12840960 | bytes 10272768 | tf_op jit(solution)/shard_map/concatenate | solution.py:57
  45.5 0.9 slice_bitcast_fusion.1
  46.7 0.6 divide_select_fusion
  47.3 0.6 divide_select_fusion.1
  48.0 0.5 divide_select_fusion.2
  48.4 0.9 fusion.191
  49.3 0.9 fusion.192
  50.2 4.5 %and_select_fusion.1 = f32[22,38,512]{2,1,0:T(8,128)S(1)} fusion(f32[22,38,512]{2,1,0:T(8,128)S(1)} %get-tuple-element.28, f32[22,1,512]{2,1,0:T(1,128)S(1)} %get-tuple-element.42, f32[22,37,512]{2,1,0:T(8,128)S(1)} %divide_select_fusion.1, f32[22,1,512]{2,1,0:T(1,128)S(1)} %get-tuple-element.41, f32[22,38,1]{2,1,0:T(8,128)S(1)} %get-tuple-element.40, ...), kind=kLoop, calls=%fused_computation.31 | loop fusion | flops 14553088 | bytes 10399052 | tf_op jit(solution)/shard_map/jit(_where)/select_n | solution.py:193
  54.7 4.5 %and_select_fusion = f32[22,38,512]{2,1,0:T(8,128)S(1)} fusion(f32[22,38,512]{2,1,0:T(8,128)S(1)} %and_select_fusion.1, f32[22,1,512]{2,1,0:T(1,128)S(1)} %get-tuple-element.42, f32[22,37,512]{2,1,0:T(8,128)S(1)} %divide_select_fusion.1, f32[22,1,512]{2,1,0:T(1,128)S(1)} %get-tuple-element.41, f32[22,38,1]{2,1,0:T(8,128)S(1)} %get-tuple-element.40, ...), kind=kLoop, calls=%fused_computation.30 | loop fusion | flops 14553088 | bytes 10399052 | tf_op jit(solution)/shard_map/jit(_where)/select_n | solution.py:193
  59.2 2.7 %fusion.43 = (f32[22,38,512]{2,1,0:T(8,128)S(1)}, f32[22,38,512]{2,1,0:T(8,128)S(1)}, f32[22,38,512]{2,1,0:T(8,128)S(1)}, f32[22,38,512]{2,1,0:T(8,128)S(1)}, f3...) fusion(f32[22,38,512]{2,1,0:T(8,128)S(1)} %and_select_fusion, f32[21,38,512]{2,1,0:T(8,128)S(1)} %divide_select_fusion.2, ...), kind=kLoop, calls=%fused_computation.75 | loop fusion | flops 2996224 | bytes 13774848 | tf_op jit(solution)/shard_map/mul | solution.py:85
  61.9 2.6 %bitcast_reduce_fusion = f32[4,32,512]{2,1,0:T(8,128)S(1)} fusion(f32[22,38,512]{2,1,0:T(8,128)S(1)} %get-tuple-element.36, f32[22,38,1]{2,1,0:T(8,128)S(1)} %get-tuple-element.40, f32[22,38,511]{2,1,0:T(8,128)S(1)} %divide_select_fusion, f32[22,38,512]{2,1,0:T(8,128)S(1)} %get-tuple-element.35, f32[22,38,1]{2,1,0:T(8,128)S(1)} %get-tuple-element.39, ...), kind=kLoop, calls=%fused_computation.162 | loop fusion | flops 4653056 | bytes 12123408 | tf_op jit(solution)/shard_map/reduce_sum | solution.py:97
  64.5 0.5 fusion.206
  65.2 2.8 %collective-permute-start.6 = (f32[2,4,8,128]{3,2,1,0:T(8,128)S(1)}, f32[2,4,8,128]{3,2,1,0:T(8,128)S(1)}, u32[]{:S(2)}, u32[]{:S(2)}) collective-permute-start(f32[2,4,8,128]{3,2,1,0:T(8,128)S(1)} %pad_maximum_fusion.18), channel_id=1, source_target_pairs={{0,16},{8,24},{16,32},{24,40},{32,48},{40,56},{48,64},{56,72},{64,... | collective-permute-start | bytes 98312 | tf_op jit(solution)/shard_map/ppermute | solution.py:25
  68.0 5.4 %collective-permute-start.7 = (f32[2,4,8,128]{3,2,1,0:T(8,128)S(1)}, f32[2,4,8,128]{3,2,1,0:T(8,128)S(1)}, u32[]{:S(2)}, u32[]{:S(2)}) collective-permute-start(f32[2,4,8,128]{3,2,1,0:T(8,128)S(1)} %pad_maximum_fusion.18), channel_id=1, source_target_pairs={{0,8},{8,16},{16,24},{24,32},{32,40},{40,48},{48,56},{56,64},{64,7... | collective-permute-start | bytes 98312 | tf_op jit(solution)/shard_map/ppermute | solution.py:25
  73.4 2.5 %collective-permute-start.8 = (f32[2,4,8,128]{3,2,1,0:T(8,128)S(1)}, f32[2,4,8,128]{3,2,1,0:T(8,128)S(1)}, u32[]{:S(2)}, u32[]{:S(2)}) collective-permute-start(f32[2,4,8,128]{3,2,1,0:T(8,128)S(1)} %pad_maximum_fusion.18), channel_id=1, source_target_pairs={{8,0},{16,8},{24,16},{32,24},{40,32},{48,40},{56,48},{64,56},{72,6... | collective-permute-start | bytes 98312 | tf_op jit(solution)/shard_map/ppermute | solution.py:26
  76.0 4.5 %collective-permute-start.9 = (f32[2,4,8,128]{3,2,1,0:T(8,128)S(1)}, f32[2,4,8,128]{3,2,1,0:T(8,128)S(1)}, u32[]{:S(2)}, u32[]{:S(2)}) collective-permute-start(f32[2,4,8,128]{3,2,1,0:T(8,128)S(1)} %pad_maximum_fusion.18), channel_id=1, source_target_pairs={{16,0},{24,8},{32,16},{40,24},{48,32},{56,40},{64,48},{72,56},{80,... | collective-permute-start | bytes 98312 | tf_op jit(solution)/shard_map/ppermute | solution.py:26
  80.6 2.7 %collective-permute-done.9 = f32[2,4,8,128]{3,2,1,0:T(8,128)S(1)} collective-permute-done((f32[2,4,8,128]{3,2,1,0:T(8,128)S(1)}, f32[2,4,8,128]{3,2,1,0:T(8,128)S(1)}, u32[]{:S(2)}, u32[]{:S(2)}) %collective-permute-start.9) | collective-permute-done | bytes 32800 | tf_op jit(solution)/shard_map/ppermute | solution.py:26
  83.3 4.9 %collective-permute-start.10 = (f32[2,20,8,128]{3,2,1,0:T(8,128)S(1)}, f32[2,20,8,128]{3,2,1,0:T(8,128)S(1)}, u32[]{:S(2)}, u32[]{:S(2)}) collective-permute-start(f32[2,20,8,128]{3,2,1,0:T(8,128)S(1)} %constant_dynamic-update-slice_fusion), channel_id=1, source_target_pairs={{0,1},{1,2},{2,3},{3,4},{4,5},{5,6},{6,7},{8,9},{9,10},{10,11},{11... | collective-permute-start | bytes 491528 | tf_op jit(solution)/shard_map/ppermute | solution.py:25
  88.2 2.1 %collective-permute-start.11 = (f32[2,20,8,128]{3,2,1,0:T(8,128)S(1)}, f32[2,20,8,128]{3,2,1,0:T(8,128)S(1)}, u32[]{:S(2)}, u32[]{:S(2)}) collective-permute-start(f32[2,20,8,128]{3,2,1,0:T(8,128)S(1)} %constant_dynamic-update-slice_fusion), channel_id=1, source_target_pairs={{1,0},{2,1},{3,2},{4,3},{5,4},{6,5},{7,6},{9,8},{10,9},{11,10},{12... | collective-permute-start | bytes 491528 | tf_op jit(solution)/shard_map/ppermute | solution.py:26
  90.4 1.9 %collective-permute-done.10 = f32[2,20,8,128]{3,2,1,0:T(8,128)S(1)} collective-permute-done((f32[2,20,8,128]{3,2,1,0:T(8,128)S(1)}, f32[2,20,8,128]{3,2,1,0:T(8,128)S(1)}, u32[]{:S(2)}, u32[]{:S(2)}) %collective-permute-start.10) | collective-permute-done | bytes 163872 | tf_op jit(solution)/shard_map/ppermute | solution.py:25
  92.3 4.1 %collective-permute-done.11 = f32[2,20,8,128]{3,2,1,0:T(8,128)S(1)} collective-permute-done((f32[2,20,8,128]{3,2,1,0:T(8,128)S(1)}, f32[2,20,8,128]{3,2,1,0:T(8,128)S(1)}, u32[]{:S(2)}, u32[]{:S(2)}) %collective-permute-start.11) | collective-permute-done | bytes 163872 | tf_op jit(solution)/shard_map/ppermute | solution.py:26
  96.4 0.5 fusion.189
  97.0 0.3 fusion.190
  97.3 0.3 multiply_add_fusion.4
  97.8 0.3 multiply_add_fusion.2
  98.1 0.3 multiply_add_fusion.1
  98.4 0.3 multiply_add_fusion
  98.9 0.5 fusion.195
  99.4 0.3 convolution_bitcast_fusion
  99.7 1.2 %bitcast_add_fusion = f32[16,32,512]{2,1,0:T(8,128)} fusion(f32[22,38,512]{2,1,0:T(8,128)S(1)} %and_select_fusion, f32[4,32,512]{2,1,0:T(8,128)S(1)} %convolution_bitcast_fusion), kind=kLoop, calls=%fused_computation.161 | loop fusion | flops 262144 | bytes 2359296 | tf_op jit(solution)/shard_map/add | solution.py:200
  (52 shorter events, 1.1 us)
Async XLA Ops:
  0.0 8.5 %copy-start = (f32[16,32,512]{2,1,0:T(8,128)S(1)}, f32[16,32,512]{2,1,0:T(8,128)}, u32[]{:S(2)}) copy-start(f32[16,32,512]{2,1,0:T(8,128)} %param.4) | copy-start | bytes 3145732
  0.0 8.5 %copy-start.1 = (f32[16,32,512]{2,1,0:T(8,128)S(1)}, f32[16,32,512]{2,1,0:T(8,128)}, u32[]{:S(2)}) copy-start(f32[16,32,512]{2,1,0:T(8,128)} %param.5) | copy-start | bytes 3145732
  0.0 8.5 %copy-start.2 = (f32[16,32,512]{2,1,0:T(8,128)S(1)}, f32[16,32,512]{2,1,0:T(8,128)}, u32[]{:S(2)}) copy-start(f32[16,32,512]{2,1,0:T(8,128)} %param.3) | copy-start | bytes 3145732
  2.6 28.8 %collective-permute-start = (f32[3,16,3,512]{3,2,1,0:T(4,128)}, f32[3,16,3,512]{3,2,1,0:T(4,128)S(1)}, u32[]{:S(2)}, u32[]{:S(2)}) collective-permute-start(f32[3,16,3,512]{3,2,1,0:T(4,128)} %get-tuple-element.33), channel_id=1, source_target_pairs={{0,1},{1,2},{2,3},{3,4},{4,5},{5,6},{6,7},{8,9},{9,10},{10,11},{11... | collective-permute-start | bytes 884744 | tf_op jit(solution)/shard_map/ppermute | solution.py:25
  5.6 25.8 %collective-permute-start.1 = (f32[3,16,3,512]{3,2,1,0:T(4,128)}, f32[3,16,3,512]{3,2,1,0:T(4,128)}, u32[]{:S(2)}, u32[]{:S(2)}) collective-permute-start(f32[3,16,3,512]{3,2,1,0:T(4,128)} %get-tuple-element.34), channel_id=1, source_target_pairs={{1,0},{2,1},{3,2},{4,3},{5,4},{6,5},{7,6},{9,8},{10,9},{11,10},{12... | collective-permute-start | bytes 884744 | tf_op jit(solution)/shard_map/ppermute | solution.py:26
  9.7 33.5 %collective-permute-start.3 = (f32[3,3,32,512]{3,2,1,0:T(8,128)}, f32[3,3,32,512]{3,2,1,0:T(8,128)}, u32[]{:S(2)}, u32[]{:S(2)}) collective-permute-start(f32[3,3,32,512]{3,2,1,0:T(8,128)} %get-tuple-element.31), channel_id=1, source_target_pairs={{0,8},{8,16},{16,24},{24,32},{32,40},{40,48},{48,56},{56,64},{64,7... | collective-permute-start | bytes 1769480 | tf_op jit(solution)/shard_map/ppermute | solution.py:25
  11.6 31.5 %collective-permute-start.5 = (f32[3,3,32,512]{3,2,1,0:T(8,128)}, f32[3,3,32,512]{3,2,1,0:T(8,128)}, u32[]{:S(2)}, u32[]{:S(2)}) collective-permute-start(f32[3,3,32,512]{3,2,1,0:T(8,128)} %get-tuple-element.32), channel_id=1, source_target_pairs={{8,0},{16,8},{24,16},{32,24},{40,32},{48,40},{56,48},{64,56},{72,6... | collective-permute-start | bytes 1769480 | tf_op jit(solution)/shard_map/ppermute | solution.py:26
  17.7 4.0 %copy-start.3 = (s32[512]{0:T(512)}, s32[512]{0:T(512)S(1)}, u32[]{:S(2)}) copy-start(s32[512]{0:T(512)S(1)} %get-tuple-element.51) | copy-start | bytes 6148
  17.7 4.0 %copy-start.5 = (s32[512]{0:T(512)}, s32[512]{0:T(512)S(1)}, u32[]{:S(2)}) copy-start(s32[512]{0:T(512)S(1)} %get-tuple-element.52) | copy-start | bytes 6148
  17.7 4.0 %copy-start.10 = (pred[512]{0:T(512)(128)(4,1)}, pred[512]{0:T(512)(128)(4,1)S(1)}, u32[]{:S(2)}) copy-start(pred[512]{0:T(512)(128)(4,1)S(1)} %fusion.215) | copy-start | bytes 1540
  32.4 8.9 %collective-permute-start.2 = (f32[3,3,6,512]{3,2,1,0:T(8,128)S(1)}, f32[3,3,6,512]{3,2,1,0:T(8,128)S(1)}, u32[]{:S(2)}, u32[]{:S(2)}) collective-permute-start(f32[3,3,6,512]{3,2,1,0:T(8,128)S(1)} %get-tuple-element.43), channel_id=1, source_target_pairs={{0,8},{8,16},{16,24},{24,32},{32,40},{40,48},{48,56},{56,64},{64,7... | collective-permute-start | bytes 331784 | tf_op jit(solution)/shard_map/ppermute | solution.py:25
  34.4 8.7 %collective-permute-start.4 = (f32[3,3,6,512]{3,2,1,0:T(8,128)S(1)}, f32[3,3,6,512]{3,2,1,0:T(8,128)S(1)}, u32[]{:S(2)}, u32[]{:S(2)}) collective-permute-start(f32[3,3,6,512]{3,2,1,0:T(8,128)S(1)} %get-tuple-element.44), channel_id=1, source_target_pairs={{8,0},{16,8},{24,16},{32,24},{40,32},{48,40},{56,48},{64,56},{72,6... | collective-permute-start | bytes 331784 | tf_op jit(solution)/shard_map/ppermute | solution.py:26
  48.0 2.2 %copy-start.12 = (pred[22]{0:T(512)(128)(4,1)S(1)}, pred[22]{0:T(512)(128)(4,1)}, u32[]{:S(2)}) copy-start(pred[22]{0:T(512)(128)(4,1)} %compare_and_fusion.3) | copy-start | bytes 70
  61.8 2.7 %copy-start.4 = (s32[512]{0:T(512)S(1)}, s32[512]{0:T(512)}, u32[]{:S(2)}) copy-start(s32[512]{0:T(512)} %copy-done.3) | copy-start | bytes 6148
  61.8 2.7 %copy-start.6 = (s32[512]{0:T(512)S(1)}, s32[512]{0:T(512)}, u32[]{:S(2)}) copy-start(s32[512]{0:T(512)} %copy-done.5) | copy-start | bytes 6148
  61.8 2.7 %copy-start.11 = (pred[512]{0:T(512)(128)(4,1)S(1)}, pred[512]{0:T(512)(128)(4,1)}, u32[]{:S(2)}) copy-start(pred[512]{0:T(512)(128)(4,1)} %copy-done.10) | copy-start | bytes 1540
  61.8 3.2 %copy-start.7 = (s32[32]{0:T(128)S(1)}, s32[32]{0:T(128)}, u32[]{:S(2)}) copy-start(s32[32]{0:T(128)} %get-tuple-element.53) | copy-start | bytes 388
  61.9 3.2 %copy-start.8 = (s32[32]{0:T(128)S(1)}, s32[32]{0:T(128)}, u32[]{:S(2)}) copy-start(s32[32]{0:T(128)} %get-tuple-element.54) | copy-start | bytes 388
  61.9 3.2 %copy-start.9 = (pred[32]{0:T(512)(128)(4,1)S(1)}, pred[32]{0:T(512)(128)(4,1)}, u32[]{:S(2)}) copy-start(pred[32]{0:T(512)(128)(4,1)} %compare_and_fusion.1) | copy-start | bytes 100
  65.2 15.3 %collective-permute-start.6 = (f32[2,4,8,128]{3,2,1,0:T(8,128)S(1)}, f32[2,4,8,128]{3,2,1,0:T(8,128)S(1)}, u32[]{:S(2)}, u32[]{:S(2)}) collective-permute-start(f32[2,4,8,128]{3,2,1,0:T(8,128)S(1)} %pad_maximum_fusion.18), channel_id=1, source_target_pairs={{0,16},{8,24},{16,32},{24,40},{32,48},{40,56},{48,64},{56,72},{64,... | collective-permute-start | bytes 98312 | tf_op jit(solution)/shard_map/ppermute | solution.py:25
  68.0 12.5 %collective-permute-start.7 = (f32[2,4,8,128]{3,2,1,0:T(8,128)S(1)}, f32[2,4,8,128]{3,2,1,0:T(8,128)S(1)}, u32[]{:S(2)}, u32[]{:S(2)}) collective-permute-start(f32[2,4,8,128]{3,2,1,0:T(8,128)S(1)} %pad_maximum_fusion.18), channel_id=1, source_target_pairs={{0,8},{8,16},{16,24},{24,32},{32,40},{40,48},{48,56},{56,64},{64,7... | collective-permute-start | bytes 98312 | tf_op jit(solution)/shard_map/ppermute | solution.py:25
  73.4 7.1 %collective-permute-start.8 = (f32[2,4,8,128]{3,2,1,0:T(8,128)S(1)}, f32[2,4,8,128]{3,2,1,0:T(8,128)S(1)}, u32[]{:S(2)}, u32[]{:S(2)}) collective-permute-start(f32[2,4,8,128]{3,2,1,0:T(8,128)S(1)} %pad_maximum_fusion.18), channel_id=1, source_target_pairs={{8,0},{16,8},{24,16},{32,24},{40,32},{48,40},{56,48},{64,56},{72,6... | collective-permute-start | bytes 98312 | tf_op jit(solution)/shard_map/ppermute | solution.py:26
  76.0 7.3 %collective-permute-start.9 = (f32[2,4,8,128]{3,2,1,0:T(8,128)S(1)}, f32[2,4,8,128]{3,2,1,0:T(8,128)S(1)}, u32[]{:S(2)}, u32[]{:S(2)}) collective-permute-start(f32[2,4,8,128]{3,2,1,0:T(8,128)S(1)} %pad_maximum_fusion.18), channel_id=1, source_target_pairs={{16,0},{24,8},{32,16},{40,24},{48,32},{56,40},{64,48},{72,56},{80,... | collective-permute-start | bytes 98312 | tf_op jit(solution)/shard_map/ppermute | solution.py:26
  83.3 9.0 %collective-permute-start.10 = (f32[2,20,8,128]{3,2,1,0:T(8,128)S(1)}, f32[2,20,8,128]{3,2,1,0:T(8,128)S(1)}, u32[]{:S(2)}, u32[]{:S(2)}) collective-permute-start(f32[2,20,8,128]{3,2,1,0:T(8,128)S(1)} %constant_dynamic-update-slice_fusion), channel_id=1, source_target_pairs={{0,1},{1,2},{2,3},{3,4},{4,5},{5,6},{6,7},{8,9},{9,10},{10,11},{11... | collective-permute-start | bytes 491528 | tf_op jit(solution)/shard_map/ppermute | solution.py:25
  88.2 8.1 %collective-permute-start.11 = (f32[2,20,8,128]{3,2,1,0:T(8,128)S(1)}, f32[2,20,8,128]{3,2,1,0:T(8,128)S(1)}, u32[]{:S(2)}, u32[]{:S(2)}) collective-permute-start(f32[2,20,8,128]{3,2,1,0:T(8,128)S(1)} %constant_dynamic-update-slice_fusion), channel_id=1, source_target_pairs={{1,0},{2,1},{3,2},{4,3},{5,4},{6,5},{7,6},{9,8},{10,9},{11,10},{12... | collective-permute-start | bytes 491528 | tf_op jit(solution)/shard_map/ppermute | solution.py:26

commit v6 on v4

--- a/solution.py
+++ b/solution.py
@@ -39,6 +39,42 @@
         need -= width
         hop += 1
     return jnp.concatenate(lows + [block] + highs, axis=dim)
+
+
+def packed_halo(fields, depths):
+    top = max(depths)
+    assert top <= fields[0].shape[0] and top <= fields[0].shape[1]
+    offs = [sum(depths[:k]) for k in range(len(depths))]
+    up = lambda f, d, dim: lax.slice_in_dim(f, f.shape[dim] - d, f.shape[dim], axis=dim)
+    down = lambda f, d, dim: lax.slice_in_dim(f, 0, d, axis=dim)
+    nb, ng = lax.axis_size("box"), lax.axis_size("group")
+    fb, bb = shifted_pairs(nb, 1), [(t, s) for s, t in shifted_pairs(nb, 1)]
+    fg, bg = shifted_pairs(ng, 1), [(t, s) for s, t in shifted_pairs(ng, 1)]
+
+    def send(pieces, axis, pairs, dim):
+        msg = jnp.concatenate(pieces, axis=dim)
+        if not pairs:
+            return jnp.zeros_like(msg)
+        return lax.ppermute(msg, axis, pairs)
+
+    xl = send([up(f, d, 0) for f, d in zip(fields, depths)], "box", fb, 0)
+    xh = send([down(f, d, 0) for f, d in zip(fields, depths)], "box", bb, 0)
+    yl = send([up(f, d, 1) for f, d in zip(fields, depths)], "group", fg, 1)
+    yh = send([down(f, d, 1) for f, d in zip(fields, depths)], "group", bg, 1)
+    width = yl.shape[1]
+    low = send([up(yl, top, 0), up(yh, top, 0)], "box", fb, 1)
+    high = send([down(yl, top, 0), down(yh, top, 0)], "box", bb, 1)
+    out = []
+    for f, d, o in zip(fields, depths, offs):
+        ys = slice(o, o + d)
+        ys2 = slice(width + o, width + o + d)
+        rows = [
+            jnp.concatenate([low[top - d:, ys], xl[o:o + d], low[top - d:, ys2]], axis=1),
+            jnp.concatenate([yl[:, ys], f, yh[:, ys]], axis=1),
+            jnp.concatenate([high[:d, ys], xh[o:o + d], high[:d, ys2]], axis=1),
+        ]
+        out.append(jnp.concatenate(rows, axis=0))
+    return out
 
 
 def shift_z(field, side):
@@ -166,9 +202,8 @@
 def per_device(right_side, inv_density, pressure):
     depth = SWEEPS + 1
     sx, sy, sz = pressure.shape
-    both = jnp.stack([right_side, inv_density, pressure])
-    both = deep_extend(deep_extend(both, "box", 1, depth), "group", 2, depth)
-    rhs_e, b_e, fine = both[0], both[1], both[2]
+    rhs_e, b_e, fine = packed_halo([right_side, inv_density, pressure], [depth - 1, depth, depth])
+    rhs_e = jnp.pad(rhs_e, ((1, 1), (1, 1), (0, 0)))
     totals = (sx * lax.axis_size("box"), sy * lax.axis_size("group"))
     inside = grid_mask(fine.shape, depth, ("box", "group"), totals)
     coefs = face_pairs(b_e, low_faces(b_e))

time: 104 us -> 123 us (1.18)
  other arithmetic: 27 us -> 53 us
  waiting for transfers between devices: 33 us -> 12.9 us
  local copies, waits for them, and re-layouts: 1.91 us -> 8.14 us
  starting transfers between devices: 38.9 us -> 44.1 us
    ppermute x0 -> x6, starting transfers between devices: none -> 21.7 us  [send(): return lax.ppermute(msg, axis, pairs)]
    ppermute x5 -> x3, waiting for transfers between devices: 22.3 us -> 1.99 us  [halo_from(): lax.ppermute(lax.slice_in_dim(block, n - width, n, axis=dim), axis, forward)]
    select_n x2, other arithmetic: 8.98 us -> 29 us  [per_device(): fine = jnp.where(inside, fine + step, 0.0)]
    ppermute x5 -> x3, starting transfers between devices: 19.2 us -> 9.33 us  [halo_from(): lax.ppermute(lax.slice_in_dim(block, 0, width, axis=dim), axis, backward)]
    slice x2 -> x18, local copies, waits for them, and re-layouts: 0.26 us -> 7.8 us  [the longest x6 3.68 us: packed_halo(): lax.slice_in_dim(f, f.shape[dim] - d, f.shape[dim], axis=dim)]
    concatenate x0 -> x9, other arithmetic: none -> 6.83 us  [the longest x3 3.53 us: packed_halo(): out.append(jnp.concatenate(rows, axis=0))]
    ppermute x5 -> x3, starting transfers between devices: 19.6 us -> 13 us  [halo_from(): lax.ppermute(lax.slice_in_dim(block, n - width, n, axis=dim), axis, forward)]
    slice x3 -> x0, other arithmetic: 4.92 us -> none  [the longest x2 4.02 us: halo_from(): lax.slice_in_dim(block, n - width, n, axis=dim)]
  transfers between devices with their start and end apart: 10 -> 12, of which waited for: 6 -> 5; matrix products, arithmetic and copies ran while one was open for 1% -> 6% of each run, Pallas kernels for 0% -> 0%
where the time goes in v6:
time: 123 us; the launch traced here: 122 us
  other arithmetic  53 us (43%)
  starting transfers between devices  44.1 us (36%)
  waiting for transfers between devices  12.9 us (10%)
  local copies, waits for them, and re-layouts  8.14 us (7%)
  matrix products  2.65 us (2%)
    select_n x2, other arithmetic, per_device(): fine = jnp.where(inside, fine + step, 0.0)  29 us
    ppermute x6, starting transfers between devices, send(): return lax.ppermute(msg, axis, pairs)  21.7 us
    ppermute x3, starting transfers between devices, halo_from(): lax.ppermute(lax.slice_in_dim(block, n - width, n, axis=dim), axis, forward)  13 us
    ppermute x3, starting transfers between devices, halo_from(): lax.ppermute(lax.slice_in_dim(block, 0, width, axis=dim), axis, backward)  9.33 us
    ppermute x3, waiting for transfers between devices, halo_from(): lax.ppermute(lax.slice_in_dim(block, 0, width, axis=dim), axis, backward)  9.05 us
    reduce_sum x2, other arithmetic, block_mean(): fx = field.reshape(sx // 4, 4, sy, sz).sum(axis=1)  4.94 us
    mul x1, other arithmetic, apply_op(): total = total + coef * (field - near)  4.4 us
    slice x6, local copies, waits for them, and re-layouts, packed_halo(): lax.slice_in_dim(f, f.shape[dim] - d, f.shape[dim], axis=dim)  3.68 us
  transfers between devices with their start and end apart: 12, of which 5 were waited for; matrix products, arithmetic and copies ran while one was open for 6% of the time, Pallas kernels for 0%

profile of v6, /device:TPU:34, one launch (start us, length us, event | category | flops | bytes accessed | tf_op | source)
XLA Modules:
  0.0 121.6 jit_solution(18140198842542943831)
XLA Ops:
  0.0 1.2 fusion.260
  1.2 1.4 %fusion.261 = (f32[16,3,512]{2,1,0:T(4,128)S(1)}, f32[16,3,512]{2,1,0:T(4,128)S(1)}, f32[16,3,512]{2,1,0:T(4,128)S(1)}, f32[16,3,512]{2,1,0:T(4,128)S(1)}) fusion(f32[16,32,512]{2,1,0:T(8,128)} %param.4, f32[16,32,512]{2,1,0:T(8,128)} %param.5), kind=kLoop, calls=%fused_computation.430 | loop fusion | bytes 786432 | tf_op jit(solution)/shard_map/slice | solution.py:48
  2.6 0.8 pad_maximum_fusion.11
  3.4 3.0 %collective-permute-start = (f32[16,8,512]{2,1,0:T(8,128)}, f32[16,8,512]{2,1,0:T(8,128)S(1)}, u32[]{:S(2)}, u32[]{:S(2)}) collective-permute-start(f32[16,8,512]{2,1,0:T(8,128)} %pad_maximum_fusion.11), channel_id=1, source_target_pairs={{0,1},{1,2},{2,3},{3,4},{4,5},{5,6},{6,7},{8,9},{9,10},{10,11},{11... | collective-permute-start | bytes 786440 | tf_op jit(solution)/shard_map/ppermute | solution.py:58
  6.4 0.8 pad_maximum_fusion.12
  7.2 2.8 %collective-permute-start.1 = (f32[16,8,512]{2,1,0:T(8,128)}, f32[16,8,512]{2,1,0:T(8,128)S(1)}, u32[]{:S(2)}, u32[]{:S(2)}) collective-permute-start(f32[16,8,512]{2,1,0:T(8,128)} %pad_maximum_fusion.12), channel_id=1, source_target_pairs={{1,0},{2,1},{3,2},{4,3},{5,4},{6,5},{7,6},{9,8},{10,9},{11,10},{12... | collective-permute-start | bytes 786440 | tf_op jit(solution)/shard_map/ppermute | solution.py:58
  10.0 1.1 fusion.258
  11.1 0.8 pad_maximum_fusion.8
  12.0 1.9 %collective-permute-start.3 = (f32[8,32,512]{2,1,0:T(8,128)}, f32[8,32,512]{2,1,0:T(8,128)}, u32[]{:S(2)}, u32[]{:S(2)}) collective-permute-start(f32[8,32,512]{2,1,0:T(8,128)} %pad_maximum_fusion.8), channel_id=1, source_target_pairs={{0,8},{8,16},{16,24},{24,32},{32,40},{40,48},{48,56},{56,64},{64,7... | collective-permute-start | bytes 1572872 | tf_op jit(solution)/shard_map/ppermute | solution.py:58
  13.9 0.8 pad_maximum_fusion.9
  14.8 6.0 %collective-permute-start.5 = (f32[8,32,512]{2,1,0:T(8,128)}, f32[8,32,512]{2,1,0:T(8,128)}, u32[]{:S(2)}, u32[]{:S(2)}) collective-permute-start(f32[8,32,512]{2,1,0:T(8,128)} %pad_maximum_fusion.9), channel_id=1, source_target_pairs={{8,0},{16,8},{24,16},{32,24},{40,32},{48,40},{56,48},{64,56},{72,6... | collective-permute-start | bytes 1572872 | tf_op jit(solution)/shard_map/ppermute | solution.py:58
  21.0 0.5 fusion.233
  21.5 0.6 compare_and_fusion.3
  22.1 0.7 fusion.79
  22.9 0.6 compare_and_fusion.2
  23.5 1.9 %collective-permute-start.2 = (f32[3,16,512]{2,1,0:T(8,128)S(1)}, f32[3,16,512]{2,1,0:T(8,128)S(1)}, u32[]{:S(2)}, u32[]{:S(2)}) collective-permute-start(f32[3,16,512]{2,1,0:T(8,128)S(1)} %pad_maximum_fusion.13), channel_id=1, source_target_pairs={{0,8},{8,16},{16,24},{24,32},{32,40},{40,48},{48,56},{56,64},{64,7... | collective-permute-start | bytes 294920 | tf_op jit(solution)/shard_map/ppermute | solution.py:58
  25.4 6.0 %collective-permute-start.4 = (f32[3,16,512]{2,1,0:T(8,128)S(1)}, f32[3,16,512]{2,1,0:T(8,128)S(1)}, u32[]{:S(2)}, u32[]{:S(2)}) collective-permute-start(f32[3,16,512]{2,1,0:T(8,128)S(1)} %pad_maximum_fusion.14), channel_id=1, source_target_pairs={{8,0},{16,8},{24,16},{32,24},{40,32},{48,40},{56,48},{64,56},{72,6... | collective-permute-start | bytes 294920 | tf_op jit(solution)/shard_map/ppermute | solution.py:58
  31.9 1.8 %collective-permute-done.4 = f32[3,16,512]{2,1,0:T(8,128)S(1)} collective-permute-done((f32[3,16,512]{2,1,0:T(8,128)S(1)}, f32[3,16,512]{2,1,0:T(8,128)S(1)}, u32[]{:S(2)}, u32[]{:S(2)}) %collective-permute-start.4) | collective-permute-done | bytes 98336 | tf_op jit(solution)/shard_map/ppermute | solution.py:58
  33.8 1.0 fusion.263
  34.8 1.0 fusion.264
  36.3 0.6 divide_select_fusion
  37.0 0.5 divide_select_fusion.2
  37.5 1.9 %divide_select_fusion.1 = f32[22,37,512]{2,1,0:T(8,128)} fusion(f32[22,38,512]{2,1,0:T(8,128)S(1)} %fusion.11), kind=kLoop, calls=%fused_computation.51 | loop fusion | flops 3334144 | bytes 5001216 | tf_op jit(solution)/shard_map/jit(_where)/select_n | solution.py:186
  39.3 1.5 %maximum_maximum_fusion = f32[22,38,512]{2,1,0:T(8,128)} fusion(f32[3,3,512]{2,1,0:T(4,128)S(1)} %get-tuple-element.73, f32[3,32,512]{2,1,0:T(8,128)S(1)} %get-tuple-element.52, f32[3,3,512]{2,1,0:T(4,128)S(1)} %get-tuple-element.74, f32[16,3,512]{2,1,0:T(4,128)S(1)} %get-tuple-element.56, f32[16,32,512]{2,1,0:T(8,128)S(1)} %copy-done.3, ...), kind=kLoop, calls=%fused_computation.146 | loop fusion | flops 3424256 | bytes 3424256 | tf_op jit(solution)/shard_map/concatenate | solution.py:76
  40.9 0.9 slice.505
  41.8 0.9 slice.510
  42.7 1.7 %fusion.73 = f32[22,38,512]{2,1,0:T(8,128)} fusion(f32[2,2,512]{2,1,0:T(2,128)S(1)} %get-tuple-element.66, f32[2,32,512]{2,1,0:T(8,128)S(1)} %slice.510, f32[2,2,512]{2,1,0:T(2,128)S(1)} %get-tuple-element.65, f32[16,2,512]{2,1,0:T(2,128)S(1)} %slice.508, f32[2,2,512]{2,1,0:T(2,128)S(1)} %get-tuple-element.64, f32[16,32,512]{2,1,0:T(8,128)S(1)} %copy-done.1, ...), kind=kLoop, calls=%fused_computation.139 | loop fusion | flops 14125056 | bytes 3186688 | tf_op jit(solution)/shard_map/concatenate | solution.py:76
  44.5 15.7 %and_select_fusion.1 = (f32[22,38,512]{2,1,0:T(8,128)}, f32[22,38,512]{2,1,0:T(8,128)S(1)}, f32[22,38,512]{2,1,0:T(8,128)S(1)}) fusion(f32[22,38,512]{2,1,0:T(8,128)} %maximum_maximum_fusion, f32[22,38,1]{2,1,0:T(8,128)S(1)} %get-tuple-element.36, f32[22,38,511]{2,1,0:T(8,128)S(1)} %divide_select_fusion, f32[22,38,1]{2,1,0:T(8,128)S(1)} %get-tuple-element.35, ...), kind=kLoop, calls=%fused_computation.60 | loop fusion | flops 49223680 | bytes 15052108 | tf_op jit(solution)/shard_map/jit(_where)/select_n | solution.py:213
  60.3 13.2 %and_select_fusion = f32[22,38,512]{2,1,0:T(8,128)S(1)} fusion(f32[22,38,512]{2,1,0:T(8,128)} %get-tuple-element.26, f32[22,38,512]{2,1,0:T(8,128)S(1)} %get-tuple-element.28, f32[22,38,512]{2,1,0:T(8,128)S(1)} %get-tuple-element.27, f32[22,38,1]{2,1,0:T(8,128)S(1)} %get-tuple-element.36, f32[22,38,511]{2,1,0:T(8,128)S(1)} %divide_select_fusion, ...), kind=kLoop, calls=%fused_computation.59 | loop fusion | flops 32958464 | bytes 12139852 | tf_op jit(solution)/shard_map/jit(_where)/select_n | solution.py:213
  73.5 4.4 %fusion.55 = (f32[22,38,512]{2,1,0:T(8,128)S(1)}, f32[22,38,512]{2,1,0:T(8,128)S(1)}, f32[22,38,512]{2,1,0:T(8,128)S(1)}, f32[22,38,512]{2,1,0:T(8,128)S(1)}, f32[22,38,512]{2,1,0:T(8,128)}, /*index=5*/f32[22,38,512]{2,1,0:T(8,128)}) fusion(f32[22,38,512]{2,1,0:T(8,128)S(1)} %and_select_fusion, f32[21,38,512]{2,1,0:T(8,128)S(1)} %divide_select_fusion.2, ...), kind=kLoop, calls=%fused_computation.116 | loop fusion | flops 8132608 | bytes 14086144 | tf_op jit(solution)/shard_map/mul | solution.py:105
  78.0 4.9 %bitcast_reduce_fusion = f32[4,32,512]{2,1,0:T(8,128)S(1)} fusion(f32[22,38,512]{2,1,0:T(8,128)S(1)} %get-tuple-element.32, f32[22,38,1]{2,1,0:T(8,128)S(1)} %get-tuple-element.36, f32[22,38,511]{2,1,0:T(8,128)S(1)} %divide_select_fusion, f32[22,38,512]{2,1,0:T(8,128)S(1)} %get-tuple-element.31, f32[22,38,1]{2,1,0:T(8,128)S(1)} %get-tuple-element.35, ...), kind=kLoop, calls=%fused_computation.222 | loop fusion | flops 4128768 | bytes 12463376 | tf_op jit(solution)/shard_map/reduce_sum | solution.py:117
  82.9 0.5 fusion.231
  83.5 5.3 %collective-permute-start.6 = (f32[2,4,8,128]{3,2,1,0:T(8,128)S(1)}, f32[2,4,8,128]{3,2,1,0:T(8,128)S(1)}, u32[]{:S(2)}, u32[]{:S(2)}) collective-permute-start(f32[2,4,8,128]{3,2,1,0:T(8,128)S(1)} %pad_maximum_fusion.15), channel_id=1, source_target_pairs={{0,16},{8,24},{16,32},{24,40},{32,48},{40,56},{48,64},{56,72},{64,... | collective-permute-start | bytes 98312 | tf_op jit(solution)/shard_map/ppermute | solution.py:25
  88.9 2.9 %collective-permute-start.7 = (f32[2,4,8,128]{3,2,1,0:T(8,128)S(1)}, f32[2,4,8,128]{3,2,1,0:T(8,128)S(1)}, u32[]{:S(2)}, u32[]{:S(2)}) collective-permute-start(f32[2,4,8,128]{3,2,1,0:T(8,128)S(1)} %pad_maximum_fusion.15), channel_id=1, source_target_pairs={{0,8},{8,16},{16,24},{24,32},{32,40},{40,48},{48,56},{56,64},{64,7... | collective-permute-start | bytes 98312 | tf_op jit(solution)/shard_map/ppermute | solution.py:25
  91.8 5.1 %collective-permute-start.8 = (f32[2,4,8,128]{3,2,1,0:T(8,128)S(1)}, f32[2,4,8,128]{3,2,1,0:T(8,128)S(1)}, u32[]{:S(2)}, u32[]{:S(2)}) collective-permute-start(f32[2,4,8,128]{3,2,1,0:T(8,128)S(1)} %pad_maximum_fusion.15), channel_id=1, source_target_pairs={{8,0},{16,8},{24,16},{32,24},{40,32},{48,40},{56,48},{64,56},{72,6... | collective-permute-start | bytes 98312 | tf_op jit(solution)/shard_map/ppermute | solution.py:26
  96.8 2.1 %collective-permute-start.9 = (f32[2,4,8,128]{3,2,1,0:T(8,128)S(1)}, f32[2,4,8,128]{3,2,1,0:T(8,128)S(1)}, u32[]{:S(2)}, u32[]{:S(2)}) collective-permute-start(f32[2,4,8,128]{3,2,1,0:T(8,128)S(1)} %pad_maximum_fusion.15), channel_id=1, source_target_pairs={{16,0},{24,8},{32,16},{40,24},{48,32},{56,40},{64,48},{72,56},{80,... | collective-permute-start | bytes 98312 | tf_op jit(solution)/shard_map/ppermute | solution.py:26
  99.1 5.1 %collective-permute-done.9 = f32[2,4,8,128]{3,2,1,0:T(8,128)S(1)} collective-permute-done((f32[2,4,8,128]{3,2,1,0:T(8,128)S(1)}, f32[2,4,8,128]{3,2,1,0:T(8,128)S(1)}, u32[]{:S(2)}, u32[]{:S(2)}) %collective-permute-start.9) | collective-permute-done | bytes 32800 | tf_op jit(solution)/shard_map/ppermute | solution.py:26
  104.2 4.8 %collective-permute-start.10 = (f32[2,20,8,128]{3,2,1,0:T(8,128)S(1)}, f32[2,20,8,128]{3,2,1,0:T(8,128)S(1)}, u32[]{:S(2)}, u32[]{:S(2)}) collective-permute-start(f32[2,20,8,128]{3,2,1,0:T(8,128)S(1)} %constant_dynamic-update-slice_fusion), channel_id=1, source_target_pairs={{0,1},{1,2},{2,3},{3,4},{4,5},{5,6},{6,7},{8,9},{9,10},{10,11},{11... | collective-permute-start | bytes 491528 | tf_op jit(solution)/shard_map/ppermute | solution.py:25
  109.0 2.1 %collective-permute-start.11 = (f32[2,20,8,128]{3,2,1,0:T(8,128)S(1)}, f32[2,20,8,128]{3,2,1,0:T(8,128)S(1)}, u32[]{:S(2)}, u32[]{:S(2)}) collective-permute-start(f32[2,20,8,128]{3,2,1,0:T(8,128)S(1)} %constant_dynamic-update-slice_fusion), channel_id=1, source_target_pairs={{1,0},{2,1},{3,2},{4,3},{5,4},{6,5},{7,6},{9,8},{10,9},{11,10},{12... | collective-permute-start | bytes 491528 | tf_op jit(solution)/shard_map/ppermute | solution.py:26
  111.1 2.0 %collective-permute-done.10 = f32[2,20,8,128]{3,2,1,0:T(8,128)S(1)} collective-permute-done((f32[2,20,8,128]{3,2,1,0:T(8,128)S(1)}, f32[2,20,8,128]{3,2,1,0:T(8,128)S(1)}, u32[]{:S(2)}, u32[]{:S(2)}) %collective-permute-start.10) | collective-permute-done | bytes 163872 | tf_op jit(solution)/shard_map/ppermute | solution.py:25
  113.1 4.0 %collective-permute-done.11 = f32[2,20,8,128]{3,2,1,0:T(8,128)S(1)} collective-permute-done((f32[2,20,8,128]{3,2,1,0:T(8,128)S(1)}, f32[2,20,8,128]{3,2,1,0:T(8,128)S(1)}, u32[]{:S(2)}, u32[]{:S(2)}) %collective-permute-start.11) | collective-permute-done | bytes 163872 | tf_op jit(solution)/shard_map/ppermute | solution.py:26
  117.1 0.5 fusion.216
  117.7 0.3 fusion.217
  118.5 0.3 multiply_add_fusion.2
  119.1 0.3 multiply_add_fusion
  119.6 0.5 fusion.220
  120.1 0.3 convolution_bitcast_fusion
  120.4 1.2 bitcast_add_fusion
  (97 shorter events, 2.3 us)
Async XLA Ops:
  0.0 10.0 %copy-start = (f32[16,32,512]{2,1,0:T(8,128)S(1)}, f32[16,32,512]{2,1,0:T(8,128)}, u32[]{:S(2)}) copy-start(f32[16,32,512]{2,1,0:T(8,128)} %param.4) | copy-start | bytes 3145732
  1.2 9.9 %copy-start.1 = (f32[16,32,512]{2,1,0:T(8,128)S(1)}, f32[16,32,512]{2,1,0:T(8,128)}, u32[]{:S(2)}) copy-start(f32[16,32,512]{2,1,0:T(8,128)} %param.3) | copy-start | bytes 3145732
  3.4 20.1 %collective-permute-start = (f32[16,8,512]{2,1,0:T(8,128)}, f32[16,8,512]{2,1,0:T(8,128)S(1)}, u32[]{:S(2)}, u32[]{:S(2)}) collective-permute-start(f32[16,8,512]{2,1,0:T(8,128)} %pad_maximum_fusion.11), channel_id=1, source_target_pairs={{0,1},{1,2},{2,3},{3,4},{4,5},{5,6},{6,7},{8,9},{9,10},{10,11},{11... | collective-permute-start | bytes 786440 | tf_op jit(solution)/shard_map/ppermute | solution.py:58
  7.2 16.3 %collective-permute-start.1 = (f32[16,8,512]{2,1,0:T(8,128)}, f32[16,8,512]{2,1,0:T(8,128)S(1)}, u32[]{:S(2)}, u32[]{:S(2)}) collective-permute-start(f32[16,8,512]{2,1,0:T(8,128)} %pad_maximum_fusion.12), channel_id=1, source_target_pairs={{1,0},{2,1},{3,2},{4,3},{5,4},{6,5},{7,6},{9,8},{10,9},{11,10},{12... | collective-permute-start | bytes 786440 | tf_op jit(solution)/shard_map/ppermute | solution.py:58
  12.0 21.7 %collective-permute-start.3 = (f32[8,32,512]{2,1,0:T(8,128)}, f32[8,32,512]{2,1,0:T(8,128)}, u32[]{:S(2)}, u32[]{:S(2)}) collective-permute-start(f32[8,32,512]{2,1,0:T(8,128)} %pad_maximum_fusion.8), channel_id=1, source_target_pairs={{0,8},{8,16},{16,24},{24,32},{32,40},{40,48},{48,56},{56,64},{64,7... | collective-permute-start | bytes 1572872 | tf_op jit(solution)/shard_map/ppermute | solution.py:58
  14.8 20.0 %collective-permute-start.5 = (f32[8,32,512]{2,1,0:T(8,128)}, f32[8,32,512]{2,1,0:T(8,128)}, u32[]{:S(2)}, u32[]{:S(2)}) collective-permute-start(f32[8,32,512]{2,1,0:T(8,128)} %pad_maximum_fusion.9), channel_id=1, source_target_pairs={{8,0},{16,8},{24,16},{32,24},{40,32},{48,40},{56,48},{64,56},{72,6... | collective-permute-start | bytes 1572872 | tf_op jit(solution)/shard_map/ppermute | solution.py:58
  20.8 10.7 %copy-start.13 = (s32[512]{0:T(512)}, s32[512]{0:T(512)S(1)}, u32[]{:S(2)}) copy-start(s32[512]{0:T(512)S(1)} %get-tuple-element.79) | copy-start | bytes 6148
  20.8 10.7 %copy-start.15 = (s32[512]{0:T(512)}, s32[512]{0:T(512)S(1)}, u32[]{:S(2)}) copy-start(s32[512]{0:T(512)S(1)} %get-tuple-element.80) | copy-start | bytes 6148
  20.9 10.7 %copy-start.23 = (pred[512]{0:T(512)(128)(4,1)}, pred[512]{0:T(512)(128)(4,1)S(1)}, u32[]{:S(2)}) copy-start(pred[512]{0:T(512)(128)(4,1)S(1)} %fusion.240) | copy-start | bytes 1540
  20.9 10.7 %copy-start.17 = (s32[32]{0:T(128)}, s32[32]{0:T(128)S(1)}, u32[]{:S(2)}) copy-start(s32[32]{0:T(128)S(1)} %get-tuple-element.81) | copy-start | bytes 388
  20.9 10.7 %copy-start.19 = (s32[32]{0:T(128)}, s32[32]{0:T(128)S(1)}, u32[]{:S(2)}) copy-start(s32[32]{0:T(128)S(1)} %get-tuple-element.82) | copy-start | bytes 388
  20.9 10.6 %copy-start.21 = (pred[32]{0:T(512)(128)(4,1)}, pred[32]{0:T(512)(128)(4,1)S(1)}, u32[]{:S(2)}) copy-start(pred[32]{0:T(512)(128)(4,1)S(1)} %compare_and_fusion.1) | copy-start | bytes 100
  23.5 8.3 %collective-permute-start.2 = (f32[3,16,512]{2,1,0:T(8,128)S(1)}, f32[3,16,512]{2,1,0:T(8,128)S(1)}, u32[]{:S(2)}, u32[]{:S(2)}) collective-permute-start(f32[3,16,512]{2,1,0:T(8,128)S(1)} %pad_maximum_fusion.13), channel_id=1, source_target_pairs={{0,8},{8,16},{16,24},{24,32},{32,40},{40,48},{48,56},{56,64},{64,7... | collective-permute-start | bytes 294920 | tf_op jit(solution)/shard_map/ppermute | solution.py:58
  25.4 8.2 %collective-permute-start.4 = (f32[3,16,512]{2,1,0:T(8,128)S(1)}, f32[3,16,512]{2,1,0:T(8,128)S(1)}, u32[]{:S(2)}, u32[]{:S(2)}) collective-permute-start(f32[3,16,512]{2,1,0:T(8,128)S(1)} %pad_maximum_fusion.14), channel_id=1, source_target_pairs={{8,0},{16,8},{24,16},{32,24},{40,32},{48,40},{56,48},{64,56},{72,6... | collective-permute-start | bytes 294920 | tf_op jit(solution)/shard_map/ppermute | solution.py:58
  31.7 12.8 %copy-start.5 = (f32[16,2,512]{2,1,0:T(2,128)}, f32[16,2,512]{2,1,0:T(2,128)S(1)}, u32[]{:S(2)}) copy-start(f32[16,2,512]{2,1,0:T(2,128)S(1)} %slice.507) | copy-start | bytes 196612
  31.7 12.7 %copy-start.6 = (f32[16,2,512]{2,1,0:T(2,128)}, f32[16,2,512]{2,1,0:T(2,128)S(1)}, u32[]{:S(2)}) copy-start(f32[16,2,512]{2,1,0:T(2,128)S(1)} %slice.508) | copy-start | bytes 196612
  31.9 12.6 %copy-start.10 = (f32[2,2,512]{2,1,0:T(2,128)}, f32[2,2,512]{2,1,0:T(2,128)S(1)}, u32[]{:S(2)}) copy-start(f32[2,2,512]{2,1,0:T(2,128)S(1)} %get-tuple-element.64) | copy-start | bytes 24580
  33.7 9.0 %copy-start.11 = (f32[2,2,512]{2,1,0:T(2,128)}, f32[2,2,512]{2,1,0:T(2,128)S(1)}, u32[]{:S(2)}) copy-start(f32[2,2,512]{2,1,0:T(2,128)S(1)} %get-tuple-element.65) | copy-start | bytes 24580
  33.7 9.0 %copy-start.12 = (f32[2,2,512]{2,1,0:T(2,128)}, f32[2,2,512]{2,1,0:T(2,128)S(1)}, u32[]{:S(2)}) copy-start(f32[2,2,512]{2,1,0:T(2,128)S(1)} %get-tuple-element.66) | copy-start | bytes 24580
  33.7 10.8 %copy-start.7 = (f32[3,3,512]{2,1,0:T(4,128)}, f32[3,3,512]{2,1,0:T(4,128)S(1)}, u32[]{:S(2)}) copy-start(f32[3,3,512]{2,1,0:T(4,128)S(1)} %get-tuple-element.72) | copy-start | bytes 55300
  37.4 1.9 %copy-start.3 = (f32[16,32,512]{2,1,0:T(8,128)S(1)}, f32[16,32,512]{2,1,0:T(8,128)}, u32[]{:S(2)}) copy-start(f32[16,32,512]{2,1,0:T(8,128)} %param.5) | copy-start | bytes 3145732
  41.8 2.7 %copy-start.25 = (pred[22]{0:T(512)(128)(4,1)S(1)}, pred[22]{0:T(512)(128)(4,1)}, u32[]{:S(2)}) copy-start(pred[22]{0:T(512)(128)(4,1)} %compare_and_fusion.3) | copy-start | bytes 70
  41.8 2.7 %copy-start.26 = (pred[38]{0:T(512)(128)(4,1)S(1)}, pred[38]{0:T(512)(128)(4,1)}, u32[]{:S(2)}) copy-start(pred[38]{0:T(512)(128)(4,1)} %compare_and_fusion.2) | copy-start | bytes 118
  42.7 17.6 %copy-start.4 = (f32[2,32,512]{2,1,0:T(8,128)}, f32[2,32,512]{2,1,0:T(8,128)S(1)}, u32[]{:S(2)}) copy-start(f32[2,32,512]{2,1,0:T(8,128)S(1)} %slice.510) | copy-start | bytes 393220
  60.3 13.2 %copy-start.8 = (f32[3,3,512]{2,1,0:T(4,128)S(1)}, f32[3,3,512]{2,1,0:T(4,128)}, u32[]{:S(2)}) copy-start(f32[3,3,512]{2,1,0:T(4,128)} %copy-done.7) | copy-start | bytes 55300
  73.5 4.4 %copy-start.2 = (f32[22,38,512]{2,1,0:T(8,128)S(1)}, f32[22,38,512]{2,1,0:T(8,128)}, u32[]{:S(2)}) copy-start(f32[22,38,512]{2,1,0:T(8,128)} %fusion.73) | copy-start | bytes 5136388
  77.9 4.9 %copy-start.14 = (s32[512]{0:T(512)S(1)}, s32[512]{0:T(512)}, u32[]{:S(2)}) copy-start(s32[512]{0:T(512)} %copy-done.13) | copy-start | bytes 6148
  77.9 4.9 %copy-start.16 = (s32[512]{0:T(512)S(1)}, s32[512]{0:T(512)}, u32[]{:S(2)}) copy-start(s32[512]{0:T(512)} %copy-done.15) | copy-start | bytes 6148
  77.9 4.9 %copy-start.24 = (pred[512]{0:T(512)(128)(4,1)S(1)}, pred[512]{0:T(512)(128)(4,1)}, u32[]{:S(2)}) copy-start(pred[512]{0:T(512)(128)(4,1)} %copy-done.23) | copy-start | bytes 1540
  77.9 5.4 %copy-start.18 = (s32[32]{0:T(128)S(1)}, s32[32]{0:T(128)}, u32[]{:S(2)}) copy-start(s32[32]{0:T(128)} %copy-done.17) | copy-start | bytes 388
  77.9 5.4 %copy-start.20 = (s32[32]{0:T(128)S(1)}, s32[32]{0:T(128)}, u32[]{:S(2)}) copy-start(s32[32]{0:T(128)} %copy-done.19) | copy-start | bytes 388
  78.0 5.4 %copy-start.22 = (pred[32]{0:T(512)(128)(4,1)S(1)}, pred[32]{0:T(512)(128)(4,1)}, u32[]{:S(2)}) copy-start(pred[32]{0:T(512)(128)(4,1)} %copy-done.21) | copy-start | bytes 100
  78.0 5.6 %copy-start.9 = (f32[1,4,8,128]{3,2,1,0:T(8,128)S(1)}, f32[1,4,8,128]{3,2,1,0:T(8,128)}, u32[]{:S(2)}) copy-start(f32[1,4,8,128]{3,2,1,0:T(8,128)} %fusion.79) | copy-start | bytes 49156
  83.5 15.4 %collective-permute-start.6 = (f32[2,4,8,128]{3,2,1,0:T(8,128)S(1)}, f32[2,4,8,128]{3,2,1,0:T(8,128)S(1)}, u32[]{:S(2)}, u32[]{:S(2)}) collective-permute-start(f32[2,4,8,128]{3,2,1,0:T(8,128)S(1)} %pad_maximum_fusion.15), channel_id=1, source_target_pairs={{0,16},{8,24},{16,32},{24,40},{32,48},{40,56},{48,64},{56,72},{64,... | collective-permute-start | bytes 98312 | tf_op jit(solution)/shard_map/ppermute | solution.py:25
  88.9 10.1 %collective-permute-start.7 = (f32[2,4,8,128]{3,2,1,0:T(8,128)S(1)}, f32[2,4,8,128]{3,2,1,0:T(8,128)S(1)}, u32[]{:S(2)}, u32[]{:S(2)}) collective-permute-start(f32[2,4,8,128]{3,2,1,0:T(8,128)S(1)} %pad_maximum_fusion.15), channel_id=1, source_target_pairs={{0,8},{8,16},{16,24},{24,32},{32,40},{40,48},{48,56},{56,64},{64,7... | collective-permute-start | bytes 98312 | tf_op jit(solution)/shard_map/ppermute | solution.py:25
  91.8 7.3 %collective-permute-start.8 = (f32[2,4,8,128]{3,2,1,0:T(8,128)S(1)}, f32[2,4,8,128]{3,2,1,0:T(8,128)S(1)}, u32[]{:S(2)}, u32[]{:S(2)}) collective-permute-start(f32[2,4,8,128]{3,2,1,0:T(8,128)S(1)} %pad_maximum_fusion.15), channel_id=1, source_target_pairs={{8,0},{16,8},{24,16},{32,24},{40,32},{48,40},{56,48},{64,56},{72,6... | collective-permute-start | bytes 98312 | tf_op jit(solution)/shard_map/ppermute | solution.py:26
  96.8 7.3 %collective-permute-start.9 = (f32[2,4,8,128]{3,2,1,0:T(8,128)S(1)}, f32[2,4,8,128]{3,2,1,0:T(8,128)S(1)}, u32[]{:S(2)}, u32[]{:S(2)}) collective-permute-start(f32[2,4,8,128]{3,2,1,0:T(8,128)S(1)} %pad_maximum_fusion.15), channel_id=1, source_target_pairs={{16,0},{24,8},{32,16},{40,24},{48,32},{56,40},{64,48},{72,56},{80,... | collective-permute-start | bytes 98312 | tf_op jit(solution)/shard_map/ppermute | solution.py:26
  104.2 9.0 %collective-permute-start.10 = (f32[2,20,8,128]{3,2,1,0:T(8,128)S(1)}, f32[2,20,8,128]{3,2,1,0:T(8,128)S(1)}, u32[]{:S(2)}, u32[]{:S(2)}) collective-permute-start(f32[2,20,8,128]{3,2,1,0:T(8,128)S(1)} %constant_dynamic-update-slice_fusion), channel_id=1, source_target_pairs={{0,1},{1,2},{2,3},{3,4},{4,5},{5,6},{6,7},{8,9},{9,10},{10,11},{11... | collective-permute-start | bytes 491528 | tf_op jit(solution)/shard_map/ppermute | solution.py:25
  109.0 8.1 %collective-permute-start.11 = (f32[2,20,8,128]{3,2,1,0:T(8,128)S(1)}, f32[2,20,8,128]{3,2,1,0:T(8,128)S(1)}, u32[]{:S(2)}, u32[]{:S(2)}) collective-permute-start(f32[2,20,8,128]{3,2,1,0:T(8,128)S(1)} %constant_dynamic-update-slice_fusion), channel_id=1, source_target_pairs={{1,0},{2,1},{3,2},{4,3},{5,4},{6,5},{7,6},{9,8},{10,9},{11,10},{12... | collective-permute-start | bytes 491528 | tf_op jit(solution)/shard_map/ppermute | solution.py:26

commit v7 on v6

--- a/solution.py
+++ b/solution.py
@@ -204,6 +204,7 @@
     sx, sy, sz = pressure.shape
     rhs_e, b_e, fine = packed_halo([right_side, inv_density, pressure], [depth - 1, depth, depth])
     rhs_e = jnp.pad(rhs_e, ((1, 1), (1, 1), (0, 0)))
+    rhs_e, b_e, fine = lax.optimization_barrier((rhs_e, b_e, fine))
     totals = (sx * lax.axis_size("box"), sy * lax.axis_size("group"))
     inside = grid_mask(fine.shape, depth, ("box", "group"), totals)
     coefs = face_pairs(b_e, low_faces(b_e))

time: 123 us -> 97.7 us (0.79)
  other arithmetic: 53 us -> 24.1 us
  local copies, waits for them, and re-layouts: 8.14 us -> 12.8 us
  starting transfers between devices: 44.1 us -> 45.9 us
  waiting for transfers between devices: 12.9 us -> 11.3 us
    select_n x2, other arithmetic: 29 us -> 8.98 us  [per_device(): fine = jnp.where(inside, fine + step, 0.0)]
    concatenate x3, other arithmetic: 3.53 us -> 1.04 us  [packed_halo(): out.append(jnp.concatenate(rows, axis=0))]
    reduce_sum x2, other arithmetic: 4.94 us -> 2.67 us  [block_mean(): fx = field.reshape(sx // 4, 4, sy, sz).sum(axis=1)]
    slice x2, local copies, waits for them, and re-layouts: 0.07 us -> 2.06 us  [packed_halo(): yh[:, ys]]
    slice x2, local copies, waits for them, and re-layouts: 0.07 us -> 2.06 us  [packed_halo(): yl[:, ys]]
    ppermute x6, waiting for transfers between devices: 1.89 us -> 0.02 us  [send(): return lax.ppermute(msg, axis, pairs)]
    mul x1, other arithmetic: 4.4 us -> 2.66 us  [apply_op(): total = total + coef * (field - near)]
    select_n x3, other arithmetic: 2.98 us -> 1.74 us  [low_faces(): inner = jnp.where((lo > 0) & (hi > 0), 2.0 * hi * lo / (hi + lo), hi + lo)]
  transfers between devices with their start and end apart: 12 -> 12, of which waited for: 5 -> 3; matrix products, arithmetic and copies ran while one was open for 6% -> 11% of each run, Pallas kernels for 0% -> 0%
where the time goes in v7:
time: 97.7 us; the launch traced here: 96.7 us
  starting transfers between devices  45.9 us (47%)
  other arithmetic  24.1 us (25%)
  local copies, waits for them, and re-layouts  12.8 us (13%)
  waiting for transfers between devices  11.3 us (12%)
  matrix products  2.05 us (2%)
    ppermute x6, starting transfers between devices, send(): return lax.ppermute(msg, axis, pairs)  22.4 us
    ppermute x3, starting transfers between devices, halo_from(): lax.ppermute(lax.slice_in_dim(block, n - width, n, axis=dim), axis, forward)  13.4 us
    ppermute x3, starting transfers between devices, halo_from(): lax.ppermute(lax.slice_in_dim(block, 0, width, axis=dim), axis, backward)  10.1 us
    select_n x2, other arithmetic, per_device(): fine = jnp.where(inside, fine + step, 0.0)  8.98 us
    ppermute x3, waiting for transfers between devices, halo_from(): lax.ppermute(lax.slice_in_dim(block, 0, width, axis=dim), axis, backward)  8.75 us
    slice x6, local copies, waits for them, and re-layouts, packed_halo(): lax.slice_in_dim(f, f.shape[dim] - d, f.shape[dim], axis=dim)  4.36 us
    concatenate x6, other arithmetic, send(): msg = jnp.concatenate(pieces, axis=dim)  3.31 us
    reduce_sum x2, other arithmetic, block_mean(): fx = field.reshape(sx // 4, 4, sy, sz).sum(axis=1)  2.67 us
  transfers between devices with their start and end apart: 12, of which 3 were waited for; matrix products, arithmetic and copies ran while one was open for 11% of the time, Pallas kernels for 0%

profile of v7, /device:TPU:34, one launch (start us, length us, event | category | flops | bytes accessed | tf_op | source)
XLA Modules:
  0.0 96.7 jit_solution(16119023921587518056)
XLA Ops:
  0.0 1.2 %fusion.238 = (f32[16,2,512]{2,1,0:T(2,128)S(1)}, f32[16,2,512]{2,1,0:T(2,128)S(1)}) fusion(f32[16,32,512]{2,1,0:T(8,128)} %param.3), kind=kLoop, calls=%fused_computation.382 | loop fusion | bytes 262144 | tf_op jit(solution)/shard_map/slice | solution.py:48
  1.2 1.4 %fusion.239 = (f32[16,3,512]{2,1,0:T(4,128)S(1)}, f32[16,3,512]{2,1,0:T(4,128)S(1)}, f32[16,3,512]{2,1,0:T(4,128)S(1)}, f32[16,3,512]{2,1,0:T(4,128)S(1)}) fusion(f32[16,32,512]{2,1,0:T(8,128)} %param.4, f32[16,32,512]{2,1,0:T(8,128)} %param.5), kind=kLoop, calls=%fused_computation.383 | loop fusion | bytes 786432 | tf_op jit(solution)/shard_map/slice | solution.py:48
  2.6 0.8 pad_maximum_fusion.9
  3.4 3.0 %collective-permute-start = (f32[16,8,512]{2,1,0:T(8,128)}, f32[16,8,512]{2,1,0:T(8,128)}, u32[]{:S(2)}, u32[]{:S(2)}) collective-permute-start(f32[16,8,512]{2,1,0:T(8,128)} %pad_maximum_fusion.9), channel_id=1, source_target_pairs={{0,1},{1,2},{2,3},{3,4},{4,5},{5,6},{6,7},{8,9},{9,10},{10,11},{11... | collective-permute-start | bytes 786440 | tf_op jit(solution)/shard_map/ppermute | solution.py:58
  6.5 0.8 pad_maximum_fusion.10
  7.3 3.5 %collective-permute-start.1 = (f32[16,8,512]{2,1,0:T(8,128)}, f32[16,8,512]{2,1,0:T(8,128)}, u32[]{:S(2)}, u32[]{:S(2)}) collective-permute-start(f32[16,8,512]{2,1,0:T(8,128)} %pad_maximum_fusion.10), channel_id=1, source_target_pairs={{1,0},{2,1},{3,2},{4,3},{5,4},{6,5},{7,6},{9,8},{10,9},{11,10},{12... | collective-permute-start | bytes 786440 | tf_op jit(solution)/shard_map/ppermute | solution.py:58
  10.9 0.8 pad_maximum_fusion.6
  11.7 1.9 %collective-permute-start.3 = (f32[8,32,512]{2,1,0:T(8,128)}, f32[8,32,512]{2,1,0:T(8,128)}, u32[]{:S(2)}, u32[]{:S(2)}) collective-permute-start(f32[8,32,512]{2,1,0:T(8,128)} %pad_maximum_fusion.6), channel_id=1, source_target_pairs={{0,8},{8,16},{16,24},{24,32},{32,40},{40,48},{48,56},{56,64},{64,7... | collective-permute-start | bytes 1572872 | tf_op jit(solution)/shard_map/ppermute | solution.py:58
  13.7 0.8 pad_maximum_fusion.7
  14.5 6.0 %collective-permute-start.5 = (f32[8,32,512]{2,1,0:T(8,128)}, f32[8,32,512]{2,1,0:T(8,128)}, u32[]{:S(2)}, u32[]{:S(2)}) collective-permute-start(f32[8,32,512]{2,1,0:T(8,128)} %pad_maximum_fusion.7), channel_id=1, source_target_pairs={{8,0},{16,8},{24,16},{32,24},{40,32},{48,40},{56,48},{64,56},{72,6... | collective-permute-start | bytes 1572872 | tf_op jit(solution)/shard_map/ppermute | solution.py:58
  20.7 0.5 fusion.211
  21.4 0.8 fusion.245
  22.2 0.8 fusion.246
  23.1 1.9 %collective-permute-start.2 = (f32[3,16,512]{2,1,0:T(8,128)S(1)}, f32[3,16,512]{2,1,0:T(8,128)S(1)}, u32[]{:S(2)}, u32[]{:S(2)}) collective-permute-start(f32[3,16,512]{2,1,0:T(8,128)S(1)} %pad_maximum_fusion.11), channel_id=1, source_target_pairs={{0,8},{8,16},{16,24},{24,32},{32,40},{40,48},{48,56},{56,64},{64,7... | collective-permute-start | bytes 294920 | tf_op jit(solution)/shard_map/ppermute | solution.py:58
  25.0 6.0 %collective-permute-start.4 = (f32[3,16,512]{2,1,0:T(8,128)S(1)}, f32[3,16,512]{2,1,0:T(8,128)S(1)}, u32[]{:S(2)}, u32[]{:S(2)}) collective-permute-start(f32[3,16,512]{2,1,0:T(8,128)S(1)} %pad_maximum_fusion.12), channel_id=1, source_target_pairs={{8,0},{16,8},{24,16},{32,24},{40,32},{48,40},{56,48},{64,56},{72,6... | collective-permute-start | bytes 294920 | tf_op jit(solution)/shard_map/ppermute | solution.py:58
  31.1 1.1 %fusion.243 = (f32[16,3,512]{2,1,0:T(4,128)S(1)}, f32[16,3,512]{2,1,0:T(4,128)S(1)}) fusion(f32[16,8,512]{2,1,0:T(8,128)} %collective-permute-done), kind=kLoop, calls=%fused_computation.387 | loop fusion | bytes 393216 | tf_op jit(solution)/shard_map/slice | solution.py:73
  32.1 1.1 %fusion.244 = (f32[16,3,512]{2,1,0:T(4,128)S(1)}, f32[16,3,512]{2,1,0:T(4,128)S(1)}) fusion(f32[16,8,512]{2,1,0:T(8,128)} %collective-permute-done.1), kind=kLoop, calls=%fused_computation.388 | loop fusion | bytes 393216 | tf_op jit(solution)/shard_map/slice | solution.py:73
  33.2 1.0 %slice.497 = f32[16,2,512]{2,1,0:T(2,128)S(1)} slice(f32[16,8,512]{2,1,0:T(8,128)} %collective-permute-done), slice={[0:16], [0:2], [0:512]} | slice | bytes 131072 | tf_op jit(solution)/shard_map/slice | solution.py:73
  34.2 1.0 %slice.498 = f32[16,2,512]{2,1,0:T(2,128)S(1)} slice(f32[16,8,512]{2,1,0:T(8,128)} %collective-permute-done.1), slice={[0:16], [0:2], [0:512]} | slice | bytes 131072 | tf_op jit(solution)/shard_map/slice | solution.py:73
  35.3 1.0 %fusion.241 = (f32[3,32,512]{2,1,0:T(8,128)S(1)}, f32[3,32,512]{2,1,0:T(8,128)S(1)}) fusion(f32[8,32,512]{2,1,0:T(8,128)} %collective-permute-done.3), kind=kLoop, calls=%fused_computation.385 | loop fusion | bytes 786432 | tf_op jit(solution)/shard_map/slice | solution.py:72
  36.4 1.0 %fusion.242 = (f32[3,32,512]{2,1,0:T(8,128)S(1)}, f32[3,32,512]{2,1,0:T(8,128)S(1)}) fusion(f32[8,32,512]{2,1,0:T(8,128)} %collective-permute-done.5), kind=kLoop, calls=%fused_computation.386 | loop fusion | bytes 786432 | tf_op jit(solution)/shard_map/slice | solution.py:74
  38.0 0.9 slice.495
  38.9 0.9 slice.502
  39.8 0.5 fusion.47
  40.3 0.6 divide_select_fusion
  41.0 0.6 divide_select_fusion.1
  41.6 0.5 divide_select_fusion.2
  42.4 4.5 %and_select_fusion.1 = f32[22,38,512]{2,1,0:T(8,128)S(1)} fusion(f32[22,38,512]{2,1,0:T(8,128)S(1)} %maximum_maximum_fusion.1, f32[22,38,512]{2,1,0:T(8,128)S(1)} %fusion.47, f32[22,1,512]{2,1,0:T(1,128)S(1)} %get-tuple-element.43, f32[22,37,512]{2,1,0:T(8,128)S(1)} %divide_select_fusion.1, f32[22,1,512]{2,1,0:T(1,128)S(1)} %get-tuple-element.42, ...), kind=kLoop, calls=%fused_computation.34 | loop fusion | flops 14553088 | bytes 10399052 | tf_op jit(solution)/shard_map/jit(_where)/select_n | solution.py:214
  46.9 4.5 %and_select_fusion = f32[22,38,512]{2,1,0:T(8,128)S(1)} fusion(f32[22,38,512]{2,1,0:T(8,128)S(1)} %and_select_fusion.1, f32[22,38,512]{2,1,0:T(8,128)S(1)} %fusion.47, f32[22,1,512]{2,1,0:T(1,128)S(1)} %get-tuple-element.43, f32[22,37,512]{2,1,0:T(8,128)S(1)} %divide_select_fusion.1, f32[22,1,512]{2,1,0:T(1,128)S(1)} %get-tuple-element.42, ...), kind=kLoop, calls=%fused_computation.33 | loop fusion | flops 14553088 | bytes 10399052 | tf_op jit(solution)/shard_map/jit(_where)/select_n | solution.py:214
  51.4 2.7 %fusion.43 = (f32[22,38,512]{2,1,0:T(8,128)S(1)}, f32[22,38,512]{2,1,0:T(8,128)S(1)}, f32[22,38,512]{2,1,0:T(8,128)S(1)}, f32[22,38,512]{2,1,0:T(8,128)S(1)}, f3...) fusion(f32[22,38,512]{2,1,0:T(8,128)S(1)} %and_select_fusion, f32[21,38,512]{2,1,0:T(8,128)S(1)} %divide_select_fusion.2, ...), kind=kLoop, calls=%fused_computation.78 | loop fusion | flops 2996224 | bytes 13774848 | tf_op jit(solution)/shard_map/mul | solution.py:105
  54.0 2.6 %bitcast_reduce_fusion = f32[4,32,512]{2,1,0:T(8,128)S(1)} fusion(f32[22,38,512]{2,1,0:T(8,128)S(1)} %get-tuple-element.35, f32[22,38,1]{2,1,0:T(8,128)S(1)} %get-tuple-element.41, f32[22,38,511]{2,1,0:T(8,128)S(1)} %divide_select_fusion, f32[22,38,512]{2,1,0:T(8,128)S(1)} %get-tuple-element.34, f32[22,38,1]{2,1,0:T(8,128)S(1)} %get-tuple-element.40, ...), kind=kLoop, calls=%fused_computation.173 | loop fusion | flops 4653056 | bytes 12123408 | tf_op jit(solution)/shard_map/reduce_sum | solution.py:117
  56.6 0.5 fusion.209
  57.3 7.5 %collective-permute-start.6 = (f32[2,4,8,128]{3,2,1,0:T(8,128)S(1)}, f32[2,4,8,128]{3,2,1,0:T(8,128)S(1)}, u32[]{:S(2)}, u32[]{:S(2)}) collective-permute-start(f32[2,4,8,128]{3,2,1,0:T(8,128)S(1)} %pad_maximum_fusion.13), channel_id=1, source_target_pairs={{0,16},{8,24},{16,32},{24,40},{32,48},{40,56},{48,64},{56,72},{64,... | collective-permute-start | bytes 98312 | tf_op jit(solution)/shard_map/ppermute | solution.py:25
  64.8 1.9 %collective-permute-start.7 = (f32[2,4,8,128]{3,2,1,0:T(8,128)S(1)}, f32[2,4,8,128]{3,2,1,0:T(8,128)S(1)}, u32[]{:S(2)}, u32[]{:S(2)}) collective-permute-start(f32[2,4,8,128]{3,2,1,0:T(8,128)S(1)} %pad_maximum_fusion.13), channel_id=1, source_target_pairs={{0,8},{8,16},{16,24},{24,32},{32,40},{40,48},{48,56},{56,64},{64,7... | collective-permute-start | bytes 98312 | tf_op jit(solution)/shard_map/ppermute | solution.py:25
  66.7 6.0 %collective-permute-start.8 = (f32[2,4,8,128]{3,2,1,0:T(8,128)S(1)}, f32[2,4,8,128]{3,2,1,0:T(8,128)S(1)}, u32[]{:S(2)}, u32[]{:S(2)}) collective-permute-start(f32[2,4,8,128]{3,2,1,0:T(8,128)S(1)} %pad_maximum_fusion.13), channel_id=1, source_target_pairs={{8,0},{16,8},{24,16},{32,24},{40,32},{48,40},{56,48},{64,56},{72,6... | collective-permute-start | bytes 98312 | tf_op jit(solution)/shard_map/ppermute | solution.py:26
  72.8 1.9 %collective-permute-start.9 = (f32[2,4,8,128]{3,2,1,0:T(8,128)S(1)}, f32[2,4,8,128]{3,2,1,0:T(8,128)S(1)}, u32[]{:S(2)}, u32[]{:S(2)}) collective-permute-start(f32[2,4,8,128]{3,2,1,0:T(8,128)S(1)} %pad_maximum_fusion.13), channel_id=1, source_target_pairs={{16,0},{24,8},{32,16},{40,24},{48,32},{56,40},{64,48},{72,56},{80,... | collective-permute-start | bytes 98312 | tf_op jit(solution)/shard_map/ppermute | solution.py:26
  74.8 5.3 %collective-permute-done.9 = f32[2,4,8,128]{3,2,1,0:T(8,128)S(1)} collective-permute-done((f32[2,4,8,128]{3,2,1,0:T(8,128)S(1)}, f32[2,4,8,128]{3,2,1,0:T(8,128)S(1)}, u32[]{:S(2)}, u32[]{:S(2)}) %collective-permute-start.9) | collective-permute-done | bytes 32800 | tf_op jit(solution)/shard_map/ppermute | solution.py:26
  80.1 4.0 %collective-permute-start.10 = (f32[2,20,8,128]{3,2,1,0:T(8,128)S(1)}, f32[2,20,8,128]{3,2,1,0:T(8,128)S(1)}, u32[]{:S(2)}, u32[]{:S(2)}) collective-permute-start(f32[2,20,8,128]{3,2,1,0:T(8,128)S(1)} %constant_dynamic-update-slice_fusion), channel_id=1, source_target_pairs={{0,1},{1,2},{2,3},{3,4},{4,5},{5,6},{6,7},{8,9},{9,10},{10,11},{11... | collective-permute-start | bytes 491528 | tf_op jit(solution)/shard_map/ppermute | solution.py:25
  84.1 2.1 %collective-permute-start.11 = (f32[2,20,8,128]{3,2,1,0:T(8,128)S(1)}, f32[2,20,8,128]{3,2,1,0:T(8,128)S(1)}, u32[]{:S(2)}, u32[]{:S(2)}) collective-permute-start(f32[2,20,8,128]{3,2,1,0:T(8,128)S(1)} %constant_dynamic-update-slice_fusion), channel_id=1, source_target_pairs={{1,0},{2,1},{3,2},{4,3},{5,4},{6,5},{7,6},{9,8},{10,9},{11,10},{12... | collective-permute-start | bytes 491528 | tf_op jit(solution)/shard_map/ppermute | solution.py:26
  86.2 2.5 %collective-permute-done.10 = f32[2,20,8,128]{3,2,1,0:T(8,128)S(1)} collective-permute-done((f32[2,20,8,128]{3,2,1,0:T(8,128)S(1)}, f32[2,20,8,128]{3,2,1,0:T(8,128)S(1)}, u32[]{:S(2)}, u32[]{:S(2)}) %collective-permute-start.10) | collective-permute-done | bytes 163872 | tf_op jit(solution)/shard_map/ppermute | solution.py:25
  88.8 3.4 %collective-permute-done.11 = f32[2,20,8,128]{3,2,1,0:T(8,128)S(1)} collective-permute-done((f32[2,20,8,128]{3,2,1,0:T(8,128)S(1)}, f32[2,20,8,128]{3,2,1,0:T(8,128)S(1)}, u32[]{:S(2)}, u32[]{:S(2)}) %collective-permute-start.11) | collective-permute-done | bytes 163872 | tf_op jit(solution)/shard_map/ppermute | solution.py:26
  92.3 0.5 fusion.194
  92.8 0.3 fusion.195
  93.7 0.3 multiply_add_fusion.2
  94.2 0.3 multiply_add_fusion
  94.7 0.5 fusion.198
  95.2 0.3 convolution_bitcast_fusion
  95.5 1.2 %bitcast_add_fusion = f32[16,32,512]{2,1,0:T(8,128)} fusion(f32[22,38,512]{2,1,0:T(8,128)S(1)} %and_select_fusion, f32[4,32,512]{2,1,0:T(8,128)S(1)} %convolution_bitcast_fusion), kind=kLoop, calls=%fused_computation.172 | loop fusion | flops 262144 | bytes 2359296 | tf_op jit(solution)/shard_map/add | solution.py:221
  (51 shorter events, 2.5 us)
Async XLA Ops:
  0.0 10.8 %copy-start = (f32[16,32,512]{2,1,0:T(8,128)S(1)}, f32[16,32,512]{2,1,0:T(8,128)}, u32[]{:S(2)}) copy-start(f32[16,32,512]{2,1,0:T(8,128)} %param.4) | copy-start | bytes 3145732
  0.0 10.8 %copy-start.1 = (f32[16,32,512]{2,1,0:T(8,128)S(1)}, f32[16,32,512]{2,1,0:T(8,128)}, u32[]{:S(2)}) copy-start(f32[16,32,512]{2,1,0:T(8,128)} %param.5) | copy-start | bytes 3145732
  1.2 9.6 %copy-start.2 = (f32[16,32,512]{2,1,0:T(8,128)S(1)}, f32[16,32,512]{2,1,0:T(8,128)}, u32[]{:S(2)}) copy-start(f32[16,32,512]{2,1,0:T(8,128)} %param.3) | copy-start | bytes 3145732
  3.4 17.9 %collective-permute-start = (f32[16,8,512]{2,1,0:T(8,128)}, f32[16,8,512]{2,1,0:T(8,128)}, u32[]{:S(2)}, u32[]{:S(2)}) collective-permute-start(f32[16,8,512]{2,1,0:T(8,128)} %pad_maximum_fusion.9), channel_id=1, source_target_pairs={{0,1},{1,2},{2,3},{3,4},{4,5},{5,6},{6,7},{8,9},{9,10},{10,11},{11... | collective-permute-start | bytes 786440 | tf_op jit(solution)/shard_map/ppermute | solution.py:58
  7.3 14.9 %collective-permute-start.1 = (f32[16,8,512]{2,1,0:T(8,128)}, f32[16,8,512]{2,1,0:T(8,128)}, u32[]{:S(2)}, u32[]{:S(2)}) collective-permute-start(f32[16,8,512]{2,1,0:T(8,128)} %pad_maximum_fusion.10), channel_id=1, source_target_pairs={{1,0},{2,1},{3,2},{4,3},{5,4},{6,5},{7,6},{9,8},{10,9},{11,10},{12... | collective-permute-start | bytes 786440 | tf_op jit(solution)/shard_map/ppermute | solution.py:58
  11.7 23.6 %collective-permute-start.3 = (f32[8,32,512]{2,1,0:T(8,128)}, f32[8,32,512]{2,1,0:T(8,128)}, u32[]{:S(2)}, u32[]{:S(2)}) collective-permute-start(f32[8,32,512]{2,1,0:T(8,128)} %pad_maximum_fusion.6), channel_id=1, source_target_pairs={{0,8},{8,16},{16,24},{24,32},{32,40},{40,48},{48,56},{56,64},{64,7... | collective-permute-start | bytes 1572872 | tf_op jit(solution)/shard_map/ppermute | solution.py:58
  14.5 21.9 %collective-permute-start.5 = (f32[8,32,512]{2,1,0:T(8,128)}, f32[8,32,512]{2,1,0:T(8,128)}, u32[]{:S(2)}, u32[]{:S(2)}) collective-permute-start(f32[8,32,512]{2,1,0:T(8,128)} %pad_maximum_fusion.7), channel_id=1, source_target_pairs={{8,0},{16,8},{24,16},{32,24},{40,32},{48,40},{56,48},{64,56},{72,6... | collective-permute-start | bytes 1572872 | tf_op jit(solution)/shard_map/ppermute | solution.py:58
  23.1 12.1 %collective-permute-start.2 = (f32[3,16,512]{2,1,0:T(8,128)S(1)}, f32[3,16,512]{2,1,0:T(8,128)S(1)}, u32[]{:S(2)}, u32[]{:S(2)}) collective-permute-start(f32[3,16,512]{2,1,0:T(8,128)S(1)} %pad_maximum_fusion.11), channel_id=1, source_target_pairs={{0,8},{8,16},{16,24},{24,32},{32,40},{40,48},{48,56},{56,64},{64,7... | collective-permute-start | bytes 294920 | tf_op jit(solution)/shard_map/ppermute | solution.py:58
  25.0 10.2 %collective-permute-start.4 = (f32[3,16,512]{2,1,0:T(8,128)S(1)}, f32[3,16,512]{2,1,0:T(8,128)S(1)}, u32[]{:S(2)}, u32[]{:S(2)}) collective-permute-start(f32[3,16,512]{2,1,0:T(8,128)S(1)} %pad_maximum_fusion.12), channel_id=1, source_target_pairs={{8,0},{16,8},{24,16},{32,24},{40,32},{48,40},{56,48},{64,56},{72,6... | collective-permute-start | bytes 294920 | tf_op jit(solution)/shard_map/ppermute | solution.py:58
  57.3 17.4 %collective-permute-start.6 = (f32[2,4,8,128]{3,2,1,0:T(8,128)S(1)}, f32[2,4,8,128]{3,2,1,0:T(8,128)S(1)}, u32[]{:S(2)}, u32[]{:S(2)}) collective-permute-start(f32[2,4,8,128]{3,2,1,0:T(8,128)S(1)} %pad_maximum_fusion.13), channel_id=1, source_target_pairs={{0,16},{8,24},{16,32},{24,40},{32,48},{40,56},{48,64},{56,72},{64,... | collective-permute-start | bytes 98312 | tf_op jit(solution)/shard_map/ppermute | solution.py:25
  64.8 9.9 %collective-permute-start.7 = (f32[2,4,8,128]{3,2,1,0:T(8,128)S(1)}, f32[2,4,8,128]{3,2,1,0:T(8,128)S(1)}, u32[]{:S(2)}, u32[]{:S(2)}) collective-permute-start(f32[2,4,8,128]{3,2,1,0:T(8,128)S(1)} %pad_maximum_fusion.13), channel_id=1, source_target_pairs={{0,8},{8,16},{16,24},{24,32},{32,40},{40,48},{48,56},{56,64},{64,7... | collective-permute-start | bytes 98312 | tf_op jit(solution)/shard_map/ppermute | solution.py:25
  66.7 8.0 %collective-permute-start.8 = (f32[2,4,8,128]{3,2,1,0:T(8,128)S(1)}, f32[2,4,8,128]{3,2,1,0:T(8,128)S(1)}, u32[]{:S(2)}, u32[]{:S(2)}) collective-permute-start(f32[2,4,8,128]{3,2,1,0:T(8,128)S(1)} %pad_maximum_fusion.13), channel_id=1, source_target_pairs={{8,0},{16,8},{24,16},{32,24},{40,32},{48,40},{56,48},{64,56},{72,6... | collective-permute-start | bytes 98312 | tf_op jit(solution)/shard_map/ppermute | solution.py:26
  72.8 7.3 %collective-permute-start.9 = (f32[2,4,8,128]{3,2,1,0:T(8,128)S(1)}, f32[2,4,8,128]{3,2,1,0:T(8,128)S(1)}, u32[]{:S(2)}, u32[]{:S(2)}) collective-permute-start(f32[2,4,8,128]{3,2,1,0:T(8,128)S(1)} %pad_maximum_fusion.13), channel_id=1, source_target_pairs={{16,0},{24,8},{32,16},{40,24},{48,32},{56,40},{64,48},{72,56},{80,... | collective-permute-start | bytes 98312 | tf_op jit(solution)/shard_map/ppermute | solution.py:26
  80.1 8.7 %collective-permute-start.10 = (f32[2,20,8,128]{3,2,1,0:T(8,128)S(1)}, f32[2,20,8,128]{3,2,1,0:T(8,128)S(1)}, u32[]{:S(2)}, u32[]{:S(2)}) collective-permute-start(f32[2,20,8,128]{3,2,1,0:T(8,128)S(1)} %constant_dynamic-update-slice_fusion), channel_id=1, source_target_pairs={{0,1},{1,2},{2,3},{3,4},{4,5},{5,6},{6,7},{8,9},{9,10},{10,11},{11... | collective-permute-start | bytes 491528 | tf_op jit(solution)/shard_map/ppermute | solution.py:25
  84.1 8.1 %collective-permute-start.11 = (f32[2,20,8,128]{3,2,1,0:T(8,128)S(1)}, f32[2,20,8,128]{3,2,1,0:T(8,128)S(1)}, u32[]{:S(2)}, u32[]{:S(2)}) collective-permute-start(f32[2,20,8,128]{3,2,1,0:T(8,128)S(1)} %constant_dynamic-update-slice_fusion), channel_id=1, source_target_pairs={{1,0},{2,1},{3,2},{4,3},{5,4},{6,5},{7,6},{9,8},{10,9},{11,10},{12... | collective-permute-start | bytes 491528 | tf_op jit(solution)/shard_map/ppermute | solution.py:26

commit v8 on v6

--- a/solution.py
+++ b/solution.py
@@ -135,13 +135,14 @@
     return (gx >= 0) & (gx < totals[0]) & (gy >= 0) & (gy < totals[1])
 
 
-def chebyshev_local(rhs_c, b_c):
+def coarse_extend(field):
+    return deep_extend(deep_extend(field, "box", 0, CHEB), "group", 1, CHEB)
+
+
+def chebyshev_local(rhs_c, b_ext):
     depth = CHEB
     cx, cy, cz = rhs_c.shape
-    both = jnp.stack([b_c, rhs_c])
-    both = deep_extend(both, "box", 1, depth)
-    both = deep_extend(both, "group", 2, depth)
-    b_ext, rhs_ext = both[0], both[1]
+    rhs_ext = coarse_extend(rhs_c)
     totals = (cx * lax.axis_size("box"), cy * lax.axis_size("group"))
     inside = inside_mask(b_ext.shape, depth, totals)
     coefs = [c * 0.0625 for c in coefs_of(b_ext, padded_neighbours(jnp.pad(b_ext, 1)))]
@@ -202,8 +203,10 @@
 def per_device(right_side, inv_density, pressure):
     depth = SWEEPS + 1
     sx, sy, sz = pressure.shape
+    coarse_b_ext = coarse_extend(block_mean(inv_density))
     rhs_e, b_e, fine = packed_halo([right_side, inv_density, pressure], [depth - 1, depth, depth])
     rhs_e = jnp.pad(rhs_e, ((1, 1), (1, 1), (0, 0)))
+    rhs_e, b_e, fine, coarse_b_ext = lax.optimization_barrier((rhs_e, b_e, fine, coarse_b_ext))
     totals = (sx * lax.axis_size("box"), sy * lax.axis_size("group"))
     inside = grid_mask(fine.shape, depth, ("box", "group"), totals)
     coefs = face_pairs(b_e, low_faces(b_e))
@@ -215,8 +218,7 @@
     own = (slice(depth, depth + sx), slice(depth, depth + sy))
     fine, res = fine[own], res[own]
     coarse_rhs = block_mean(res)
-    coarse_b = block_mean(inv_density)
-    corr = chebyshev_local(coarse_rhs, coarse_b)
+    corr = chebyshev_local(coarse_rhs, coarse_b_ext)
     return fine + expand(corr, fine.shape)
 
 

time: 123 us -> 119 us (0.967)
  other arithmetic: 53 us -> 28.4 us
  starting transfers between devices: 44.1 us -> 64 us
  local copies, waits for them, and re-layouts: 8.14 us -> 12.1 us
  waiting for transfers between devices: 12.9 us -> 10.9 us
    select_n x2, other arithmetic: 29 us -> 8.96 us  [per_device(): fine = jnp.where(inside, fine + step, 0.0)]
    ppermute x3 -> x6, starting transfers between devices: 9.33 us -> 19.5 us  [halo_from(): lax.ppermute(lax.slice_in_dim(block, 0, width, axis=dim), axis, backward)]
    ppermute x3 -> x6, starting transfers between devices: 13 us -> 23.1 us  [halo_from(): lax.ppermute(lax.slice_in_dim(block, n - width, n, axis=dim), axis, forward)]
    concatenate x6, other arithmetic: 3.3 us -> 6.28 us  [send(): msg = jnp.concatenate(pieces, axis=dim)]
    concatenate x3, other arithmetic: 3.53 us -> 1.03 us  [packed_halo(): out.append(jnp.concatenate(rows, axis=0))]
    slice x6 -> x8, local copies, waits for them, and re-layouts: 3.68 us -> 6.08 us  [packed_halo(): lax.slice_in_dim(f, f.shape[dim] - d, f.shape[dim], axis=dim)]
    unnamed x57 -> x40, local copies, waits for them, and re-layouts: 0.13 us -> 2.24 us
    slice x2, local copies, waits for them, and re-layouts: 0.07 us -> 2.06 us  [packed_halo(): yl[:, ys]]
  transfers between devices with their start and end apart: 12 -> 18, of which waited for: 5 -> 4; matrix products, arithmetic and copies ran while one was open for 6% -> 15% of each run, Pallas kernels for 0% -> 0%
where the time goes in v8:
time: 119 us; the launch traced here: 118 us
  starting transfers between devices  64 us (54%)
  other arithmetic  28.4 us (24%)
  local copies, waits for them, and re-layouts  12.1 us (10%)
  waiting for transfers between devices  10.9 us (9%)
  matrix products  2.05 us (2%)
    ppermute x6, starting transfers between devices, halo_from(): lax.ppermute(lax.slice_in_dim(block, n - width, n, axis=dim), axis, forward)  23.1 us
    ppermute x6, starting transfers between devices, send(): return lax.ppermute(msg, axis, pairs)  21.4 us
    ppermute x6, starting transfers between devices, halo_from(): lax.ppermute(lax.slice_in_dim(block, 0, width, axis=dim), axis, backward)  19.5 us
    ppermute x6, waiting for transfers between devices, halo_from(): lax.ppermute(lax.slice_in_dim(block, 0, width, axis=dim), axis, backward)  9.21 us
    select_n x2, other arithmetic, per_device(): fine = jnp.where(inside, fine + step, 0.0)  8.96 us
    concatenate x6, other arithmetic, send(): msg = jnp.concatenate(pieces, axis=dim)  6.28 us
    slice x8, local copies, waits for them, and re-layouts, packed_halo(): lax.slice_in_dim(f, f.shape[dim] - d, f.shape[dim], axis=dim)  6.08 us
    reduce_sum x2, other arithmetic, block_mean(): fx = field.reshape(sx // 4, 4, sy, sz).sum(axis=1)  4.05 us
  transfers between devices with their start and end apart: 18, of which 4 were waited for; matrix products, arithmetic and copies ran while one was open for 15% of the time, Pallas kernels for 0%

profile of v8, /device:TPU:34, one launch (start us, length us, event | category | flops | bytes accessed | tf_op | source)
XLA Modules:
  0.0 118.2 jit_solution(14634196289179428848)
XLA Ops:
  0.1 1.5 %bitcast_reduce_fusion.1 = f32[4,32,512]{2,1,0:T(8,128)S(1)} fusion(f32[16,32,512]{2,1,0:T(8,128)} %param.4), kind=kLoop, calls=%fused_computation.174 | loop fusion | flops 196608 | bytes 1310720 | tf_op jit(solution)/shard_map/reduce_sum | solution.py:117
  2.3 5.0 %collective-permute-start.6 = (f32[4,8,128]{2,1,0:T(8,128)S(1)}, f32[4,8,128]{2,1,0:T(8,128)}, u32[]{:S(2)}, u32[]{:S(2)}) collective-permute-start(f32[4,8,128]{2,1,0:T(8,128)S(1)} %fusion.53), channel_id=1, source_target_pairs={{0,16},{8,24},{16,32},{24,40},{32,48},{40,56},{48,64},{56,72},{64,... | collective-permute-start | bytes 49160 | tf_op jit(solution)/shard_map/ppermute | solution.py:25
  7.3 1.9 %collective-permute-start.7 = (f32[4,8,128]{2,1,0:T(8,128)S(1)}, f32[4,8,128]{2,1,0:T(8,128)}, u32[]{:S(2)}, u32[]{:S(2)}) collective-permute-start(f32[4,8,128]{2,1,0:T(8,128)S(1)} %fusion.53), channel_id=1, source_target_pairs={{0,8},{8,16},{16,24},{24,32},{32,40},{40,48},{48,56},{56,64},{64,7... | collective-permute-start | bytes 49160 | tf_op jit(solution)/shard_map/ppermute | solution.py:25
  9.2 6.0 %collective-permute-start.8 = (f32[4,8,128]{2,1,0:T(8,128)S(1)}, f32[4,8,128]{2,1,0:T(8,128)}, u32[]{:S(2)}, u32[]{:S(2)}) collective-permute-start(f32[4,8,128]{2,1,0:T(8,128)S(1)} %fusion.53), channel_id=1, source_target_pairs={{8,0},{16,8},{24,16},{32,24},{40,32},{48,40},{56,48},{64,56},{72,6... | collective-permute-start | bytes 49160 | tf_op jit(solution)/shard_map/ppermute | solution.py:26
  15.3 2.5 %collective-permute-start.9 = (f32[4,8,128]{2,1,0:T(8,128)S(1)}, f32[4,8,128]{2,1,0:T(8,128)}, u32[]{:S(2)}, u32[]{:S(2)}) collective-permute-start(f32[4,8,128]{2,1,0:T(8,128)S(1)} %fusion.53), channel_id=1, source_target_pairs={{16,0},{24,8},{32,16},{40,24},{48,32},{56,40},{64,48},{72,56},{80,... | collective-permute-start | bytes 49160 | tf_op jit(solution)/shard_map/ppermute | solution.py:26
  17.7 0.7 fusion.237
  18.4 0.7 fusion.238
  19.1 1.7 %fusion.236 = (f32[16,2,512]{2,1,0:T(2,128)S(1)}, f32[16,2,512]{2,1,0:T(2,128)}) fusion(f32[16,32,512]{2,1,0:T(8,128)} %param.3), kind=kLoop, calls=%fused_computation.384 | loop fusion | bytes 262144 | tf_op jit(solution)/shard_map/slice | solution.py:48
  20.8 0.8 pad_maximum_fusion.8
  21.6 3.4 %collective-permute-start = (f32[16,8,512]{2,1,0:T(8,128)}, f32[16,8,512]{2,1,0:T(8,128)}, u32[]{:S(2)}, u32[]{:S(2)}) collective-permute-start(f32[16,8,512]{2,1,0:T(8,128)} %pad_maximum_fusion.8), channel_id=1, source_target_pairs={{0,1},{1,2},{2,3},{3,4},{4,5},{5,6},{6,7},{8,9},{9,10},{10,11},{11... | collective-permute-start | bytes 786440 | tf_op jit(solution)/shard_map/ppermute | solution.py:58
  25.0 0.7 fusion.234
  25.7 0.7 fusion.235
  26.5 0.7 fusion.233
  27.2 1.8 %pad_maximum_fusion.9 = f32[16,8,512]{2,1,0:T(8,128)} fusion(f32[16,3,512]{2,1,0:T(4,128)} %get-tuple-element.57, f32[16,3,512]{2,1,0:T(4,128)} %get-tuple-element.55, f32[16,2,512]{2,1,0:T(2,128)} %get-tuple-element.53), kind=kLoop, calls=%fused_computation.178 | loop fusion | flops 131072 | bytes 524288 | tf_op jit(solution)/shard_map/concatenate | solution.py:55
  29.0 1.9 %pad_maximum_fusion.6 = f32[8,32,512]{2,1,0:T(8,128)} fusion(f32[3,32,512]{2,1,0:T(8,128)} %get-tuple-element.50, f32[3,32,512]{2,1,0:T(8,128)} %get-tuple-element.48, f32[2,32,512]{2,1,0:T(8,128)} %get-tuple-element.46), kind=kLoop, calls=%fused_computation.175 | loop fusion | flops 262144 | bytes 1048576 | tf_op jit(solution)/shard_map/concatenate | solution.py:55
  30.9 1.7 %pad_maximum_fusion.7 = f32[8,32,512]{2,1,0:T(8,128)} fusion(f32[3,32,512]{2,1,0:T(8,128)S(1)} %get-tuple-element.51, f32[3,32,512]{2,1,0:T(8,128)S(1)} %get-tuple-element.49, f32[2,32,512]{2,1,0:T(8,128)} %get-tuple-element.47), kind=kLoop, calls=%fused_computation.176 | loop fusion | flops 262144 | bytes 1048576 | tf_op jit(solution)/shard_map/concatenate | solution.py:55
  32.7 3.1 %collective-permute-start.1 = (f32[16,8,512]{2,1,0:T(8,128)}, f32[16,8,512]{2,1,0:T(8,128)S(1)}, u32[]{:S(2)}, u32[]{:S(2)}) collective-permute-start(f32[16,8,512]{2,1,0:T(8,128)} %pad_maximum_fusion.9), channel_id=1, source_target_pairs={{1,0},{2,1},{3,2},{4,3},{5,4},{6,5},{7,6},{9,8},{10,9},{11,10},{12... | collective-permute-start | bytes 786440 | tf_op jit(solution)/shard_map/ppermute | solution.py:58
  35.8 0.7 constant_dynamic-update-slice_fusion.4
  36.5 1.9 %collective-permute-start.3 = (f32[8,32,512]{2,1,0:T(8,128)}, f32[8,32,512]{2,1,0:T(8,128)S(1)}, u32[]{:S(2)}, u32[]{:S(2)}) collective-permute-start(f32[8,32,512]{2,1,0:T(8,128)} %pad_maximum_fusion.6), channel_id=1, source_target_pairs={{0,8},{8,16},{16,24},{24,32},{32,40},{40,48},{48,56},{56,64},{64,7... | collective-permute-start | bytes 1572872 | tf_op jit(solution)/shard_map/ppermute | solution.py:58
  38.4 0.7 constant_dynamic-update-slice_fusion.3
  39.2 0.7 constant_dynamic-update-slice_fusion.1
  39.9 0.7 constant_dynamic-update-slice_fusion
  40.6 3.6 %collective-permute-start.10 = (f32[20,8,128]{2,1,0:T(8,128)S(1)}, f32[20,8,128]{2,1,0:T(8,128)S(1)}, u32[]{:S(2)}, u32[]{:S(2)}) collective-permute-start(f32[20,8,128]{2,1,0:T(8,128)S(1)} %constant_dynamic-update-slice_fusion), channel_id=1, source_target_pairs={{0,1},{1,2},{2,3},{3,4},{4,5},{5,6},{6,7},{8,9},{9,10},{10,11},{11... | collective-permute-start | bytes 245768 | tf_op jit(solution)/shard_map/ppermute | solution.py:25
  44.2 2.2 %collective-permute-start.11 = (f32[20,8,128]{2,1,0:T(8,128)S(1)}, f32[20,8,128]{2,1,0:T(8,128)S(1)}, u32[]{:S(2)}, u32[]{:S(2)}) collective-permute-start(f32[20,8,128]{2,1,0:T(8,128)S(1)} %constant_dynamic-update-slice_fusion), channel_id=1, source_target_pairs={{1,0},{2,1},{3,2},{4,3},{5,4},{6,5},{7,6},{9,8},{10,9},{11,10},{12... | collective-permute-start | bytes 245768 | tf_op jit(solution)/shard_map/ppermute | solution.py:26
  46.5 1.4 %collective-permute-done.10 = f32[20,8,128]{2,1,0:T(8,128)S(1)} collective-permute-done((f32[20,8,128]{2,1,0:T(8,128)S(1)}, f32[20,8,128]{2,1,0:T(8,128)S(1)}, u32[]{:S(2)}, u32[]{:S(2)}) %collective-permute-start.10) | collective-permute-done | bytes 81952 | tf_op jit(solution)/shard_map/ppermute | solution.py:25
  47.9 4.8 %collective-permute-start.5 = (f32[8,32,512]{2,1,0:T(8,128)}, f32[8,32,512]{2,1,0:T(8,128)S(1)}, u32[]{:S(2)}, u32[]{:S(2)}) collective-permute-start(f32[8,32,512]{2,1,0:T(8,128)} %pad_maximum_fusion.7), channel_id=1, source_target_pairs={{8,0},{16,8},{24,16},{32,24},{40,32},{48,40},{56,48},{64,56},{72,6... | collective-permute-start | bytes 1572872 | tf_op jit(solution)/shard_map/ppermute | solution.py:58
  52.8 0.8 fusion.243
  53.6 2.9 %collective-permute-start.2 = (f32[3,16,512]{2,1,0:T(8,128)S(1)}, f32[3,16,512]{2,1,0:T(8,128)S(1)}, u32[]{:S(2)}, u32[]{:S(2)}) collective-permute-start(f32[3,16,512]{2,1,0:T(8,128)S(1)} %pad_maximum_fusion.11), channel_id=1, source_target_pairs={{0,8},{8,16},{16,24},{24,32},{32,40},{40,48},{48,56},{56,64},{64,7... | collective-permute-start | bytes 294920 | tf_op jit(solution)/shard_map/ppermute | solution.py:58
  56.6 5.3 %collective-permute-start.4 = (f32[3,16,512]{2,1,0:T(8,128)S(1)}, f32[3,16,512]{2,1,0:T(8,128)S(1)}, u32[]{:S(2)}, u32[]{:S(2)}) collective-permute-start(f32[3,16,512]{2,1,0:T(8,128)S(1)} %pad_maximum_fusion.12), channel_id=1, source_target_pairs={{8,0},{16,8},{24,16},{32,24},{40,32},{48,40},{56,48},{64,56},{72,6... | collective-permute-start | bytes 294920 | tf_op jit(solution)/shard_map/ppermute | solution.py:58
  61.8 1.1 fusion.241
  63.0 1.0 slice.489
  64.8 0.5 slice-done
  65.8 0.6 divide_select_fusion
  66.4 0.6 divide_select_fusion.1
  67.8 4.5 %and_select_fusion.1 = f32[22,38,512]{2,1,0:T(8,128)S(1)} fusion(f32[22,38,512]{2,1,0:T(8,128)S(1)} %maximum_maximum_fusion.1, f32[22,38,512]{2,1,0:T(8,128)S(1)} %fusion.47, f32[22,1,512]{2,1,0:T(1,128)S(1)} %get-tuple-element.45, f32[22,37,512]{2,1,0:T(8,128)S(1)} %divide_select_fusion.1, f32[22,1,512]{2,1,0:T(1,128)S(1)} %get-tuple-element.44, ...), kind=kLoop, calls=%fused_computation.34 | loop fusion | flops 14553088 | bytes 10399052 | tf_op jit(solution)/shard_map/jit(_where)/select_n | solution.py:216
  72.3 4.5 %and_select_fusion = f32[22,38,512]{2,1,0:T(8,128)S(1)} fusion(f32[22,38,512]{2,1,0:T(8,128)S(1)} %and_select_fusion.1, f32[22,38,512]{2,1,0:T(8,128)S(1)} %fusion.47, f32[22,1,512]{2,1,0:T(1,128)S(1)} %get-tuple-element.45, f32[22,37,512]{2,1,0:T(8,128)S(1)} %divide_select_fusion.1, f32[22,1,512]{2,1,0:T(1,128)S(1)} %get-tuple-element.44, ...), kind=kLoop, calls=%fused_computation.33 | loop fusion | flops 14553088 | bytes 10399052 | tf_op jit(solution)/shard_map/jit(_where)/select_n | solution.py:216
  76.8 2.6 %fusion.43 = (f32[22,38,512]{2,1,0:T(8,128)S(1)}, f32[22,38,512]{2,1,0:T(8,128)S(1)}, f32[22,38,512]{2,1,0:T(8,128)S(1)}, f32[22,38,512]{2,1,0:T(8,128)S(1)}, f3...) fusion(f32[22,38,512]{2,1,0:T(8,128)S(1)} %and_select_fusion, f32[21,38,512]{2,1,0:T(8,128)S(1)} %divide_select_fusion.2, ...), kind=kLoop, calls=%fused_computation.78 | loop fusion | flops 2996224 | bytes 13774848 | tf_op jit(solution)/shard_map/mul | solution.py:105
  79.5 2.6 %bitcast_reduce_fusion = f32[4,32,512]{2,1,0:T(8,128)S(1)} fusion(f32[22,38,512]{2,1,0:T(8,128)S(1)} %get-tuple-element.37, f32[22,38,1]{2,1,0:T(8,128)S(1)} %get-tuple-element.43, f32[22,38,511]{2,1,0:T(8,128)S(1)} %divide_select_fusion, f32[22,38,512]{2,1,0:T(8,128)S(1)} %get-tuple-element.36, f32[22,38,1]{2,1,0:T(8,128)S(1)} %get-tuple-element.42, ...), kind=kLoop, calls=%fused_computation.173 | loop fusion | flops 4653056 | bytes 12123408 | tf_op jit(solution)/shard_map/reduce_sum | solution.py:117
  82.8 5.1 %collective-permute-start.12 = (f32[4,8,128]{2,1,0:T(8,128)S(1)}, f32[4,8,128]{2,1,0:T(8,128)S(1)}, u32[]{:S(2)}, u32[]{:S(2)}) collective-permute-start(f32[4,8,128]{2,1,0:T(8,128)S(1)} %fusion.52), channel_id=1, source_target_pairs={{0,16},{8,24},{16,32},{24,40},{32,48},{40,56},{48,64},{56,72},{64,... | collective-permute-start | bytes 49160 | tf_op jit(solution)/shard_map/ppermute | solution.py:25
  87.9 4.0 %collective-permute-start.13 = (f32[4,8,128]{2,1,0:T(8,128)S(1)}, f32[4,8,128]{2,1,0:T(8,128)S(1)}, u32[]{:S(2)}, u32[]{:S(2)}) collective-permute-start(f32[4,8,128]{2,1,0:T(8,128)S(1)} %fusion.52), channel_id=1, source_target_pairs={{0,8},{8,16},{16,24},{24,32},{32,40},{40,48},{48,56},{56,64},{64,7... | collective-permute-start | bytes 49160 | tf_op jit(solution)/shard_map/ppermute | solution.py:25
  92.0 3.9 %collective-permute-start.14 = (f32[4,8,128]{2,1,0:T(8,128)S(1)}, f32[4,8,128]{2,1,0:T(8,128)S(1)}, u32[]{:S(2)}, u32[]{:S(2)}) collective-permute-start(f32[4,8,128]{2,1,0:T(8,128)S(1)} %fusion.52), channel_id=1, source_target_pairs={{8,0},{16,8},{24,16},{32,24},{40,32},{48,40},{56,48},{64,56},{72,6... | collective-permute-start | bytes 49160 | tf_op jit(solution)/shard_map/ppermute | solution.py:26
  95.9 2.2 %collective-permute-start.15 = (f32[4,8,128]{2,1,0:T(8,128)S(1)}, f32[4,8,128]{2,1,0:T(8,128)S(1)}, u32[]{:S(2)}, u32[]{:S(2)}) collective-permute-start(f32[4,8,128]{2,1,0:T(8,128)S(1)} %fusion.52), channel_id=1, source_target_pairs={{16,0},{24,8},{32,16},{40,24},{48,32},{56,40},{64,48},{72,56},{80,... | collective-permute-start | bytes 49160 | tf_op jit(solution)/shard_map/ppermute | solution.py:26
  98.2 4.8 %collective-permute-done.15 = f32[4,8,128]{2,1,0:T(8,128)S(1)} collective-permute-done((f32[4,8,128]{2,1,0:T(8,128)S(1)}, f32[4,8,128]{2,1,0:T(8,128)S(1)}, u32[]{:S(2)}, u32[]{:S(2)}) %collective-permute-start.15) | collective-permute-done | bytes 16416 | tf_op jit(solution)/shard_map/ppermute | solution.py:26
  103.1 3.5 %collective-permute-start.16 = (f32[20,8,128]{2,1,0:T(8,128)S(1)}, f32[20,8,128]{2,1,0:T(8,128)S(1)}, u32[]{:S(2)}, u32[]{:S(2)}) collective-permute-start(f32[20,8,128]{2,1,0:T(8,128)S(1)} %constant_dynamic-update-slice_fusion.5), channel_id=1, source_target_pairs={{0,1},{1,2},{2,3},{3,4},{4,5},{5,6},{6,7},{8,9},{9,10},{10,11},{11... | collective-permute-start | bytes 245768 | tf_op jit(solution)/shard_map/ppermute | solution.py:25
  106.5 2.6 %collective-permute-start.17 = (f32[20,8,128]{2,1,0:T(8,128)S(1)}, f32[20,8,128]{2,1,0:T(8,128)S(1)}, u32[]{:S(2)}, u32[]{:S(2)}) collective-permute-start(f32[20,8,128]{2,1,0:T(8,128)S(1)} %constant_dynamic-update-slice_fusion.5), channel_id=1, source_target_pairs={{1,0},{2,1},{3,2},{4,3},{5,4},{6,5},{7,6},{9,8},{10,9},{11,10},{12... | collective-permute-start | bytes 245768 | tf_op jit(solution)/shard_map/ppermute | solution.py:26
  109.4 4.4 %collective-permute-done.17 = f32[20,8,128]{2,1,0:T(8,128)S(1)} collective-permute-done((f32[20,8,128]{2,1,0:T(8,128)S(1)}, f32[20,8,128]{2,1,0:T(8,128)S(1)}, u32[]{:S(2)}, u32[]{:S(2)}) %collective-permute-start.17) | collective-permute-done | bytes 81952 | tf_op jit(solution)/shard_map/ppermute | solution.py:26
  113.8 0.5 broadcast_multiply_fusion
  117.1 1.2 bitcast_add_fusion
  (95 shorter events, 6.4 us)
Async XLA Ops:
  0.0 17.7 %copy-start = (f32[16,32,512]{2,1,0:T(8,128)S(1)}, f32[16,32,512]{2,1,0:T(8,128)}, u32[]{:S(2)}) copy-start(f32[16,32,512]{2,1,0:T(8,128)} %param.4) | copy-start | bytes 3145732
  0.0 18.4 %copy-start.1 = (f32[16,32,512]{2,1,0:T(8,128)S(1)}, f32[16,32,512]{2,1,0:T(8,128)}, u32[]{:S(2)}) copy-start(f32[16,32,512]{2,1,0:T(8,128)} %param.5) | copy-start | bytes 3145732
  0.0 1.6 %copy-start.4 = (s32[512]{0:T(512)}, s32[512]{0:T(512)S(1)}, u32[]{:S(2)}) copy-start(s32[512]{0:T(512)S(1)} %get-tuple-element.84) | copy-start | bytes 6148
  0.0 1.6 %copy-start.6 = (s32[512]{0:T(512)}, s32[512]{0:T(512)S(1)}, u32[]{:S(2)}) copy-start(s32[512]{0:T(512)S(1)} %get-tuple-element.85) | copy-start | bytes 6148
  0.0 1.6 %copy-start.14 = (pred[512]{0:T(512)(128)(4,1)}, pred[512]{0:T(512)(128)(4,1)S(1)}, u32[]{:S(2)}) copy-start(pred[512]{0:T(512)(128)(4,1)S(1)} %fusion.215) | copy-start | bytes 1540
  0.1 21.6 %copy-start.8 = (s32[32]{0:T(128)}, s32[32]{0:T(128)S(1)}, u32[]{:S(2)}) copy-start(s32[32]{0:T(128)S(1)} %get-tuple-element.86) | copy-start | bytes 388
  0.1 21.6 %copy-start.10 = (s32[32]{0:T(128)}, s32[32]{0:T(128)S(1)}, u32[]{:S(2)}) copy-start(s32[32]{0:T(128)S(1)} %get-tuple-element.87) | copy-start | bytes 388
  0.1 21.5 %copy-start.12 = (pred[32]{0:T(512)(128)(4,1)}, pred[32]{0:T(512)(128)(4,1)S(1)}, u32[]{:S(2)}) copy-start(pred[32]{0:T(512)(128)(4,1)S(1)} %compare_and_fusion.1) | copy-start | bytes 100
  2.1 24.4 %copy-start.2 = (f32[16,32,512]{2,1,0:T(8,128)S(1)}, f32[16,32,512]{2,1,0:T(8,128)}, u32[]{:S(2)}) copy-start(f32[16,32,512]{2,1,0:T(8,128)} %param.3) | copy-start | bytes 3145732
  2.3 30.4 %collective-permute-start.6 = (f32[4,8,128]{2,1,0:T(8,128)S(1)}, f32[4,8,128]{2,1,0:T(8,128)}, u32[]{:S(2)}, u32[]{:S(2)}) collective-permute-start(f32[4,8,128]{2,1,0:T(8,128)S(1)} %fusion.53), channel_id=1, source_target_pairs={{0,16},{8,24},{16,32},{24,40},{32,48},{40,56},{48,64},{56,72},{64,... | collective-permute-start | bytes 49160 | tf_op jit(solution)/shard_map/ppermute | solution.py:25
  7.3 29.3 %collective-permute-start.7 = (f32[4,8,128]{2,1,0:T(8,128)S(1)}, f32[4,8,128]{2,1,0:T(8,128)}, u32[]{:S(2)}, u32[]{:S(2)}) collective-permute-start(f32[4,8,128]{2,1,0:T(8,128)S(1)} %fusion.53), channel_id=1, source_target_pairs={{0,8},{8,16},{16,24},{24,32},{32,40},{40,48},{48,56},{56,64},{64,7... | collective-permute-start | bytes 49160 | tf_op jit(solution)/shard_map/ppermute | solution.py:25
  9.2 30.0 %collective-permute-start.8 = (f32[4,8,128]{2,1,0:T(8,128)S(1)}, f32[4,8,128]{2,1,0:T(8,128)}, u32[]{:S(2)}, u32[]{:S(2)}) collective-permute-start(f32[4,8,128]{2,1,0:T(8,128)S(1)} %fusion.53), channel_id=1, source_target_pairs={{8,0},{16,8},{24,16},{32,24},{40,32},{48,40},{56,48},{64,56},{72,6... | collective-permute-start | bytes 49160 | tf_op jit(solution)/shard_map/ppermute | solution.py:26
  15.3 24.6 %collective-permute-start.9 = (f32[4,8,128]{2,1,0:T(8,128)S(1)}, f32[4,8,128]{2,1,0:T(8,128)}, u32[]{:S(2)}, u32[]{:S(2)}) collective-permute-start(f32[4,8,128]{2,1,0:T(8,128)S(1)} %fusion.53), channel_id=1, source_target_pairs={{16,0},{24,8},{32,16},{40,24},{48,32},{56,40},{64,48},{72,56},{80,... | collective-permute-start | bytes 49160 | tf_op jit(solution)/shard_map/ppermute | solution.py:26
  21.6 31.1 %collective-permute-start = (f32[16,8,512]{2,1,0:T(8,128)}, f32[16,8,512]{2,1,0:T(8,128)}, u32[]{:S(2)}, u32[]{:S(2)}) collective-permute-start(f32[16,8,512]{2,1,0:T(8,128)} %pad_maximum_fusion.8), channel_id=1, source_target_pairs={{0,1},{1,2},{2,3},{3,4},{4,5},{5,6},{6,7},{8,9},{9,10},{10,11},{11... | collective-permute-start | bytes 786440 | tf_op jit(solution)/shard_map/ppermute | solution.py:58
  32.7 20.9 %collective-permute-start.1 = (f32[16,8,512]{2,1,0:T(8,128)}, f32[16,8,512]{2,1,0:T(8,128)S(1)}, u32[]{:S(2)}, u32[]{:S(2)}) collective-permute-start(f32[16,8,512]{2,1,0:T(8,128)} %pad_maximum_fusion.9), channel_id=1, source_target_pairs={{1,0},{2,1},{3,2},{4,3},{5,4},{6,5},{7,6},{9,8},{10,9},{11,10},{12... | collective-permute-start | bytes 786440 | tf_op jit(solution)/shard_map/ppermute | solution.py:58
  36.5 27.5 %collective-permute-start.3 = (f32[8,32,512]{2,1,0:T(8,128)}, f32[8,32,512]{2,1,0:T(8,128)S(1)}, u32[]{:S(2)}, u32[]{:S(2)}) collective-permute-start(f32[8,32,512]{2,1,0:T(8,128)} %pad_maximum_fusion.6), channel_id=1, source_target_pairs={{0,8},{8,16},{16,24},{24,32},{32,40},{40,48},{48,56},{56,64},{64,7... | collective-permute-start | bytes 1572872 | tf_op jit(solution)/shard_map/ppermute | solution.py:58
  40.6 7.3 %collective-permute-start.10 = (f32[20,8,128]{2,1,0:T(8,128)S(1)}, f32[20,8,128]{2,1,0:T(8,128)S(1)}, u32[]{:S(2)}, u32[]{:S(2)}) collective-permute-start(f32[20,8,128]{2,1,0:T(8,128)S(1)} %constant_dynamic-update-slice_fusion), channel_id=1, source_target_pairs={{0,1},{1,2},{2,3},{3,4},{4,5},{5,6},{6,7},{8,9},{9,10},{10,11},{11... | collective-permute-start | bytes 245768 | tf_op jit(solution)/shard_map/ppermute | solution.py:25
  44.2 8.5 %collective-permute-start.11 = (f32[20,8,128]{2,1,0:T(8,128)S(1)}, f32[20,8,128]{2,1,0:T(8,128)S(1)}, u32[]{:S(2)}, u32[]{:S(2)}) collective-permute-start(f32[20,8,128]{2,1,0:T(8,128)S(1)} %constant_dynamic-update-slice_fusion), channel_id=1, source_target_pairs={{1,0},{2,1},{3,2},{4,3},{5,4},{6,5},{7,6},{9,8},{10,9},{11,10},{12... | collective-permute-start | bytes 245768 | tf_op jit(solution)/shard_map/ppermute | solution.py:26
  47.9 16.2 %collective-permute-start.5 = (f32[8,32,512]{2,1,0:T(8,128)}, f32[8,32,512]{2,1,0:T(8,128)S(1)}, u32[]{:S(2)}, u32[]{:S(2)}) collective-permute-start(f32[8,32,512]{2,1,0:T(8,128)} %pad_maximum_fusion.7), channel_id=1, source_target_pairs={{8,0},{16,8},{24,16},{32,24},{40,32},{48,40},{56,48},{64,56},{72,6... | collective-permute-start | bytes 1572872 | tf_op jit(solution)/shard_map/ppermute | solution.py:58
  53.6 10.6 %copy-start.3 = (f32[16,8,512]{2,1,0:T(8,128)}, f32[16,8,512]{2,1,0:T(8,128)S(1)}, u32[]{:S(2)}) copy-start(f32[16,8,512]{2,1,0:T(8,128)S(1)} %collective-permute-done.1) | copy-start | bytes 786436
  53.6 10.3 %collective-permute-start.2 = (f32[3,16,512]{2,1,0:T(8,128)S(1)}, f32[3,16,512]{2,1,0:T(8,128)S(1)}, u32[]{:S(2)}, u32[]{:S(2)}) collective-permute-start(f32[3,16,512]{2,1,0:T(8,128)S(1)} %pad_maximum_fusion.11), channel_id=1, source_target_pairs={{0,8},{8,16},{16,24},{24,32},{32,40},{40,48},{48,56},{56,64},{64,7... | collective-permute-start | bytes 294920 | tf_op jit(solution)/shard_map/ppermute | solution.py:58
  56.6 7.5 %collective-permute-start.4 = (f32[3,16,512]{2,1,0:T(8,128)S(1)}, f32[3,16,512]{2,1,0:T(8,128)S(1)}, u32[]{:S(2)}, u32[]{:S(2)}) collective-permute-start(f32[3,16,512]{2,1,0:T(8,128)S(1)} %pad_maximum_fusion.12), channel_id=1, source_target_pairs={{8,0},{16,8},{24,16},{32,24},{40,32},{48,40},{56,48},{64,56},{72,6... | collective-permute-start | bytes 294920 | tf_op jit(solution)/shard_map/ppermute | solution.py:58
  64.5 0.8 slice-start
  79.4 2.7 %copy-start.5 = (s32[512]{0:T(512)S(1)}, s32[512]{0:T(512)}, u32[]{:S(2)}) copy-start(s32[512]{0:T(512)} %copy-done.4) | copy-start | bytes 6148
  79.5 2.7 %copy-start.7 = (s32[512]{0:T(512)S(1)}, s32[512]{0:T(512)}, u32[]{:S(2)}) copy-start(s32[512]{0:T(512)} %copy-done.6) | copy-start | bytes 6148
  79.5 2.7 %copy-start.15 = (pred[512]{0:T(512)(128)(4,1)S(1)}, pred[512]{0:T(512)(128)(4,1)}, u32[]{:S(2)}) copy-start(pred[512]{0:T(512)(128)(4,1)} %copy-done.14) | copy-start | bytes 1540
  79.5 3.2 %copy-start.9 = (s32[32]{0:T(128)S(1)}, s32[32]{0:T(128)}, u32[]{:S(2)}) copy-start(s32[32]{0:T(128)} %copy-done.8) | copy-start | bytes 388
  79.5 3.2 %copy-start.11 = (s32[32]{0:T(128)S(1)}, s32[32]{0:T(128)}, u32[]{:S(2)}) copy-start(s32[32]{0:T(128)} %copy-done.10) | copy-start | bytes 388
  79.5 3.2 %copy-start.13 = (pred[32]{0:T(512)(128)(4,1)S(1)}, pred[32]{0:T(512)(128)(4,1)}, u32[]{:S(2)}) copy-start(pred[32]{0:T(512)(128)(4,1)} %copy-done.12) | copy-start | bytes 100
  82.8 15.4 %collective-permute-start.12 = (f32[4,8,128]{2,1,0:T(8,128)S(1)}, f32[4,8,128]{2,1,0:T(8,128)S(1)}, u32[]{:S(2)}, u32[]{:S(2)}) collective-permute-start(f32[4,8,128]{2,1,0:T(8,128)S(1)} %fusion.52), channel_id=1, source_target_pairs={{0,16},{8,24},{16,32},{24,40},{32,48},{40,56},{48,64},{56,72},{64,... | collective-permute-start | bytes 49160 | tf_op jit(solution)/shard_map/ppermute | solution.py:25
  87.9 10.2 %collective-permute-start.13 = (f32[4,8,128]{2,1,0:T(8,128)S(1)}, f32[4,8,128]{2,1,0:T(8,128)S(1)}, u32[]{:S(2)}, u32[]{:S(2)}) collective-permute-start(f32[4,8,128]{2,1,0:T(8,128)S(1)} %fusion.52), channel_id=1, source_target_pairs={{0,8},{8,16},{16,24},{24,32},{32,40},{40,48},{48,56},{56,64},{64,7... | collective-permute-start | bytes 49160 | tf_op jit(solution)/shard_map/ppermute | solution.py:25
  92.0 6.3 %collective-permute-start.14 = (f32[4,8,128]{2,1,0:T(8,128)S(1)}, f32[4,8,128]{2,1,0:T(8,128)S(1)}, u32[]{:S(2)}, u32[]{:S(2)}) collective-permute-start(f32[4,8,128]{2,1,0:T(8,128)S(1)} %fusion.52), channel_id=1, source_target_pairs={{8,0},{16,8},{24,16},{32,24},{40,32},{48,40},{56,48},{64,56},{72,6... | collective-permute-start | bytes 49160 | tf_op jit(solution)/shard_map/ppermute | solution.py:26
  95.9 7.1 %collective-permute-start.15 = (f32[4,8,128]{2,1,0:T(8,128)S(1)}, f32[4,8,128]{2,1,0:T(8,128)S(1)}, u32[]{:S(2)}, u32[]{:S(2)}) collective-permute-start(f32[4,8,128]{2,1,0:T(8,128)S(1)} %fusion.52), channel_id=1, source_target_pairs={{16,0},{24,8},{32,16},{40,24},{48,32},{56,40},{64,48},{72,56},{80,... | collective-permute-start | bytes 49160 | tf_op jit(solution)/shard_map/ppermute | solution.py:26
  103.1 6.3 %collective-permute-start.16 = (f32[20,8,128]{2,1,0:T(8,128)S(1)}, f32[20,8,128]{2,1,0:T(8,128)S(1)}, u32[]{:S(2)}, u32[]{:S(2)}) collective-permute-start(f32[20,8,128]{2,1,0:T(8,128)S(1)} %constant_dynamic-update-slice_fusion.5), channel_id=1, source_target_pairs={{0,1},{1,2},{2,3},{3,4},{4,5},{5,6},{6,7},{8,9},{9,10},{10,11},{11... | collective-permute-start | bytes 245768 | tf_op jit(solution)/shard_map/ppermute | solution.py:25
  106.5 7.2 %collective-permute-start.17 = (f32[20,8,128]{2,1,0:T(8,128)S(1)}, f32[20,8,128]{2,1,0:T(8,128)S(1)}, u32[]{:S(2)}, u32[]{:S(2)}) collective-permute-start(f32[20,8,128]{2,1,0:T(8,128)S(1)} %constant_dynamic-update-slice_fusion.5), channel_id=1, source_target_pairs={{1,0},{2,1},{3,2},{4,3},{5,4},{6,5},{7,6},{9,8},{10,9},{11,10},{12... | collective-permute-start | bytes 245768 | tf_op jit(solution)/shard_map/ppermute | solution.py:26

commit v9 on v7

--- a/solution.py
+++ b/solution.py
@@ -1,11 +1,14 @@
 import jax
 import jax.numpy as jnp
 from jax import lax
+from jax.experimental import pallas as pl
+from jax.experimental.pallas import tpu as pltpu
 from jax.sharding import PartitionSpec as P
 
 SWEEPS = 2
 CHEB = 8
 HIGHEST = lax.Precision.HIGHEST
+INTERPRET = False
 
 
 def shifted_pairs(count, hop):
@@ -114,7 +117,11 @@
 
 def block_mean(field):
     sx, sy, sz = field.shape
-    fx = field.reshape(sx // 4, 4, sy, sz).sum(axis=1)
+    return block_mean_x(field.reshape(sx // 4, 4, sy, sz).sum(axis=1))
+
+
+def block_mean_x(fx):
+    sx, sy, sz = fx.shape
     fz = jnp.einsum("xyz,zc->xyc", fx, group_matrix(sz, 4), precision=HIGHEST)
     fy = jnp.einsum("xyc,yb->xbc", fz, group_matrix(sy, 4), precision=HIGHEST)
     return fy * (1.0 / 64.0)
@@ -199,23 +206,131 @@
     return pairs
 
 
+def fine_kernel(bounds, rhs_ref, b_ref, p_ref, fine_out, resx_out,
+                lx_ref, ly_ref, lz_ref, d_ref, f1_ref, f2_ref, plane_ref):
+    ex, ey, nz = b_ref.shape
+    sx, sy = fine_out.shape[0], fine_out.shape[1]
+    depth = (ex - sx) // 2
+    row = lax.broadcasted_iota(jnp.int32, (ey, nz), 0)
+    lane = lax.broadcasted_iota(jnp.int32, (ey, nz), 1)
+    x_lo, x_hi, y_lo, y_hi = bounds[0], bounds[1], bounds[2], bounds[3]
+    rows_in = (row >= y_lo) & (row < y_hi)
+
+    def face(a, n):
+        return jnp.where((a > 0) & (n > 0), 2.0 * a * n / (a + n), a + n)
+
+    def below(ref, x):
+        return jnp.where(x > 0, ref[jnp.maximum(x - 1, 0)], 0.0)
+
+    def above(ref, x):
+        return jnp.where(x < ex - 1, ref[jnp.minimum(x + 1, ex - 1)], 0.0)
+
+    def faces_body(x, carry):
+        b0 = b_ref[x]
+        lx_ref[x] = face(b0, below(b_ref, x))
+        ly_ref[x] = face(b0, pltpu.roll(b0, 1, 0))
+        lz_ref[x] = face(b0, jnp.where(lane == 0, 0.0, pltpu.roll(b0, 1, 1)))
+        return carry
+
+    lax.fori_loop(0, ex, faces_body, 0)
+
+    def coefs(x):
+        b0 = b_ref[x]
+        lx_hi = jnp.where(x < ex - 1, lx_ref[jnp.minimum(x + 1, ex - 1)], b0)
+        ly = ly_ref[x]
+        lz = lz_ref[x]
+        ly_hi = pltpu.roll(ly, ey - 1, 0)
+        lz_hi = jnp.where(lane == nz - 1, b0, pltpu.roll(lz, nz - 1, 1))
+        return [lx_ref[x], lx_hi, ly, ly_hi, lz, lz_hi]
+
+    def diag_body(x, carry):
+        total = jnp.zeros((ey, nz), jnp.float32)
+        for c in coefs(x):
+            total = total + c
+        d_ref[x] = total
+        return carry
+
+    lax.fori_loop(0, ex, diag_body, 0)
+
+    def apply_at(src, x):
+        v = src[x]
+        nears = [
+            below(src, x),
+            above(src, x),
+            pltpu.roll(v, 1, 0),
+            pltpu.roll(v, ey - 1, 0),
+            jnp.where(lane == 0, 0.0, pltpu.roll(v, 1, 1)),
+            jnp.where(lane == nz - 1, 0.0, pltpu.roll(v, nz - 1, 1)),
+        ]
+        total = jnp.zeros((ey, nz), jnp.float32)
+        for c, n in zip(coefs(x), nears):
+            total = total + c * (v - n)
+        return v, total
+
+    def sweep(src, dst):
+        def body(x, carry):
+            v, av = apply_at(src, x)
+            new = v + 2.0 / 3.0 * (rhs_ref[x] - av) / d_ref[x]
+            inside = rows_in & (x >= x_lo) & (x < x_hi)
+            dst[x] = jnp.where(inside, new, 0.0)
+            return carry
+
+        lax.fori_loop(0, ex, body, 0)
+
+    sweep(p_ref, f1_ref)
+    sweep(f1_ref, f2_ref)
+
+    def res_body(xc, carry):
+        acc = jnp.zeros((sy, nz), jnp.float32)
+        for k in range(4):
+            xo = xc * 4 + k
+            x = xo + depth
+            v, av = apply_at(f2_ref, x)
+            plane_ref[...] = rhs_ref[x] - av
+            acc = acc + plane_ref[pl.ds(depth + 1, sy), :]
+            fine_out[xo] = f2_ref[x, pl.ds(depth + 1, sy), :]
+        resx_out[xc] = acc
+        return carry
+
+    lax.fori_loop(0, sx // 4, res_body, 0)
+
+
+def fine_stage(rhs_e, b_e, p_e, bounds, own_shape):
+    sx, sy, sz = own_shape
+    ex, ey, _ = b_e.shape
+    vmem = pl.BlockSpec(memory_space=pltpu.VMEM)
+    plane = jax.ShapeDtypeStruct
+    return pl.pallas_call(
+        fine_kernel,
+        out_shape=(plane((sx, sy, sz), jnp.float32), plane((sx // 4, sy, sz), jnp.float32)),
+        in_specs=[pl.BlockSpec(memory_space=pltpu.SMEM), vmem, vmem, vmem],
+        out_specs=(vmem, vmem),
+        scratch_shapes=[pltpu.VMEM((ex, ey, sz), jnp.float32) for _ in range(6)]
+        + [pltpu.VMEM((ey, sz), jnp.float32)],
+        compiler_params=pltpu.CompilerParams(vmem_limit_bytes=100 * 1024 * 1024),
+        interpret=INTERPRET,
+    )(bounds, rhs_e, b_e, p_e)
+
+
 def per_device(right_side, inv_density, pressure):
     depth = SWEEPS + 1
     sx, sy, sz = pressure.shape
     rhs_e, b_e, fine = packed_halo([right_side, inv_density, pressure], [depth - 1, depth, depth])
-    rhs_e = jnp.pad(rhs_e, ((1, 1), (1, 1), (0, 0)))
+    rows = ((0, 0), (1, 1), (0, 0))
+    rhs_e = jnp.pad(rhs_e, ((1, 1), (2, 2), (0, 0)))
+    b_e, fine = jnp.pad(b_e, rows), jnp.pad(fine, rows)
     rhs_e, b_e, fine = lax.optimization_barrier((rhs_e, b_e, fine))
-    totals = (sx * lax.axis_size("box"), sy * lax.axis_size("group"))
-    inside = grid_mask(fine.shape, depth, ("box", "group"), totals)
-    coefs = face_pairs(b_e, low_faces(b_e))
-    diag = sum(coefs)
-    for sweep in range(SWEEPS):
-        step = 2.0 / 3.0 * (rhs_e - apply_op(fine, padded_neighbours(jnp.pad(fine, 1)), coefs)) / diag
-        fine = jnp.where(inside, fine + step, 0.0)
-    res = rhs_e - apply_op(fine, padded_neighbours(jnp.pad(fine, 1)), coefs)
-    own = (slice(depth, depth + sx), slice(depth, depth + sy))
-    fine, res = fine[own], res[own]
-    coarse_rhs = block_mean(res)
+    ex, ey = b_e.shape[0], b_e.shape[1]
+    bi, gi = lax.axis_index("box"), lax.axis_index("group")
+    nb, ng = lax.axis_size("box"), lax.axis_size("group")
+    bounds = jnp.stack([
+        jnp.maximum(depth - bi * sx, 0),
+        jnp.minimum(nb * sx + depth - bi * sx, ex),
+        jnp.maximum(depth + 1 - gi * sy, 1),
+        jnp.minimum(ng * sy + depth + 1 - gi * sy, ey - 1),
+    ]).astype(jnp.int32)
+    fine, resx = fine_stage(rhs_e, b_e, fine, bounds, pressure.shape)
+    coarse_rhs = block_mean_x(resx)
     coarse_b = block_mean(inv_density)
     corr = chebyshev_local(coarse_rhs, coarse_b)
     return fine + expand(corr, fine.shape)

time: 97.7 us -> 103 us (1.054)
  Pallas kernels: 0 us -> 16.8 us
  other arithmetic: 24.1 us -> 13.7 us
  local copies, waits for them, and re-layouts: 12.8 us -> 10.2 us
  matrix products: 2.05 us -> 4.29 us
    pallas_call x0 -> x1, Pallas kernels: none -> 16.8 us  [fine_stage(): pl.pallas_call(fine_kernel, out_shape=(plane((sx, sy, sz), jnp.float32),...]
    select_n x5 -> x0, other arithmetic: 10.7 us -> none  [the longest x2 8.98 us: per_device(): fine = jnp.where(inside, fine + step, 0.0)]
    concatenate x3, other arithmetic: 1.04 us -> 4.56 us  [packed_halo(): out.append(jnp.concatenate(rows, axis=0))]
    mul x1 -> x0, other arithmetic: 2.66 us -> none  [apply_op(): total = total + coef * (field - near)]
    reduce_sum x2 -> x1, other arithmetic: 2.67 us -> 0.09 us  [block_mean(): return block_mean_x(field.reshape(sx // 4, 4, sy, sz).sum(axis=1))]
    dot_general x4, matrix products: 1.27 us -> 3.51 us  [the longest x2 1.94 us: block_mean_x(): fz = jnp.einsum('xyz,zc->xyc', fx, group_matrix(sz, 4), precision=HIGHEST)]
    slice x2 -> x3, local copies, waits for them, and re-layouts: 2.06 us -> 0.06 us  [packed_halo(): yl[:, ys]]
  transfers between devices with their start and end apart: 12 -> 12, of which waited for: 3 -> 4; matrix products, arithmetic and copies ran while one was open for 11% -> 9% of each run, Pallas kernels for 0% -> 0%
where the time goes in v9:
time: 103 us; the launch traced here: 101 us
  starting transfers between devices  45 us (44%)
  Pallas kernels  16.8 us (16%)
  other arithmetic  13.7 us (13%)
  waiting for transfers between devices  10.9 us (11%)
  local copies, waits for them, and re-layouts  10.2 us (10%)
  matrix products  4.29 us (4%)
    ppermute x6, starting transfers between devices, send(): return lax.ppermute(msg, axis, pairs)  21.7 us
    pallas_call x1, Pallas kernels, fine_stage(): pl.pallas_call(fine_kernel, out_shape=(plane((sx, sy, sz), jnp.float32),...  16.8 us
    ppermute x3, starting transfers between devices, halo_from(): lax.ppermute(lax.slice_in_dim(block, n - width, n, axis=dim), axis, forward)  13.4 us
    ppermute x3, starting transfers between devices, halo_from(): lax.ppermute(lax.slice_in_dim(block, 0, width, axis=dim), axis, backward)  9.89 us
    ppermute x3, waiting for transfers between devices, halo_from(): lax.ppermute(lax.slice_in_dim(block, 0, width, axis=dim), axis, backward)  8.42 us
    concatenate x3, other arithmetic, packed_halo(): out.append(jnp.concatenate(rows, axis=0))  4.56 us
    slice x6, local copies, waits for them, and re-layouts, packed_halo(): lax.slice_in_dim(f, f.shape[dim] - d, f.shape[dim], axis=dim)  3.62 us
    concatenate x6, other arithmetic, send(): msg = jnp.concatenate(pieces, axis=dim)  3.29 us
  transfers between devices with their start and end apart: 12, of which 4 were waited for; matrix products, arithmetic and copies ran while one was open for 9% of the time, Pallas kernels for 0%

profile of v9, /device:TPU:34, one launch (start us, length us, event | category | flops | bytes accessed | tf_op | source)
XLA Modules:
  0.0 101.5 jit_solution(5219893663852528338)
XLA Ops:
  0.0 1.2 %fusion.180 = (f32[16,2,512]{2,1,0:T(2,128)S(1)}, f32[16,2,512]{2,1,0:T(2,128)S(1)}) fusion(f32[16,32,512]{2,1,0:T(8,128)} %param.3), kind=kLoop, calls=%fused_computation.292 | loop fusion | bytes 262144 | tf_op jit(solution)/shard_map/slice | solution.py:51
  1.2 1.4 %fusion.181 = (f32[16,3,512]{2,1,0:T(4,128)S(1)}, f32[16,3,512]{2,1,0:T(4,128)S(1)}, f32[16,3,512]{2,1,0:T(4,128)S(1)}, f32[16,3,512]{2,1,0:T(4,128)S(1)}) fusion(f32[16,32,512]{2,1,0:T(8,128)} %param.4, f32[16,32,512]{2,1,0:T(8,128)} %param.5), kind=kLoop, calls=%fused_computation.293 | loop fusion | bytes 786432 | tf_op jit(solution)/shard_map/slice | solution.py:51
  2.6 0.8 pad_maximum_fusion.3
  3.4 3.0 %collective-permute-start = (f32[16,8,512]{2,1,0:T(8,128)}, f32[16,8,512]{2,1,0:T(8,128)S(1)}, u32[]{:S(2)}, u32[]{:S(2)}) collective-permute-start(f32[16,8,512]{2,1,0:T(8,128)} %pad_maximum_fusion.3), channel_id=1, source_target_pairs={{0,1},{1,2},{2,3},{3,4},{4,5},{5,6},{6,7},{8,9},{9,10},{10,11},{11... | collective-permute-start | bytes 786440 | tf_op jit(solution)/shard_map/ppermute | solution.py:61
  6.5 0.8 pad_maximum_fusion.4
  7.2 2.8 %collective-permute-start.1 = (f32[16,8,512]{2,1,0:T(8,128)}, f32[16,8,512]{2,1,0:T(8,128)}, u32[]{:S(2)}, u32[]{:S(2)}) collective-permute-start(f32[16,8,512]{2,1,0:T(8,128)} %pad_maximum_fusion.4), channel_id=1, source_target_pairs={{1,0},{2,1},{3,2},{4,3},{5,4},{6,5},{7,6},{9,8},{10,9},{11,10},{12... | collective-permute-start | bytes 786440 | tf_op jit(solution)/shard_map/ppermute | solution.py:61
  10.2 0.8 pad_maximum_fusion
  11.0 1.9 %collective-permute-start.3 = (f32[8,32,512]{2,1,0:T(8,128)}, f32[8,32,512]{2,1,0:T(8,128)}, u32[]{:S(2)}, u32[]{:S(2)}) collective-permute-start(f32[8,32,512]{2,1,0:T(8,128)} %pad_maximum_fusion), channel_id=1, source_target_pairs={{0,8},{8,16},{16,24},{24,32},{32,40},{40,48},{48,56},{56,64},{64,7... | collective-permute-start | bytes 1572872 | tf_op jit(solution)/shard_map/ppermute | solution.py:61
  13.0 0.8 pad_maximum_fusion.1
  13.8 6.0 %collective-permute-start.5 = (f32[8,32,512]{2,1,0:T(8,128)}, f32[8,32,512]{2,1,0:T(8,128)}, u32[]{:S(2)}, u32[]{:S(2)}) collective-permute-start(f32[8,32,512]{2,1,0:T(8,128)} %pad_maximum_fusion.1), channel_id=1, source_target_pairs={{8,0},{16,8},{24,16},{32,24},{40,32},{48,40},{56,48},{64,56},{72,6... | collective-permute-start | bytes 1572872 | tf_op jit(solution)/shard_map/ppermute | solution.py:61
  20.0 0.5 fusion.156
  20.6 0.7 fusion.11
  21.3 0.7 pad_add_fusion.bounds
  22.0 0.9 fusion.188
  23.0 1.9 %collective-permute-start.2 = (f32[3,16,512]{2,1,0:T(8,128)S(1)}, f32[3,16,512]{2,1,0:T(8,128)S(1)}, u32[]{:S(2)}, u32[]{:S(2)}) collective-permute-start(f32[3,16,512]{2,1,0:T(8,128)S(1)} %pad_maximum_fusion.5), channel_id=1, source_target_pairs={{0,8},{8,16},{16,24},{24,32},{32,40},{40,48},{48,56},{56,64},{64,7... | collective-permute-start | bytes 294920 | tf_op jit(solution)/shard_map/ppermute | solution.py:61
  24.9 6.0 %collective-permute-start.4 = (f32[3,16,512]{2,1,0:T(8,128)S(1)}, f32[3,16,512]{2,1,0:T(8,128)S(1)}, u32[]{:S(2)}, u32[]{:S(2)}) collective-permute-start(f32[3,16,512]{2,1,0:T(8,128)S(1)} %pad_maximum_fusion.6), channel_id=1, source_target_pairs={{8,0},{16,8},{24,16},{32,24},{40,32},{48,40},{56,48},{64,56},{72,6... | collective-permute-start | bytes 294920 | tf_op jit(solution)/shard_map/ppermute | solution.py:61
  31.0 1.1 %fusion.186 = (f32[16,3,512]{2,1,0:T(4,128)S(1)}, f32[16,3,512]{2,1,0:T(4,128)S(1)}) fusion(f32[16,8,512]{2,1,0:T(8,128)} %collective-permute-done.1), kind=kLoop, calls=%fused_computation.298 | loop fusion | bytes 393216 | tf_op jit(solution)/shard_map/slice | solution.py:76
  32.1 1.0 slice.370
  33.2 0.3 collective-permute-done.4
  33.5 1.0 %fusion.183 = (f32[3,32,512]{2,1,0:T(8,128)S(1)}, f32[3,32,512]{2,1,0:T(8,128)S(1)}) fusion(f32[8,32,512]{2,1,0:T(8,128)} %collective-permute-done.3), kind=kLoop, calls=%fused_computation.295 | loop fusion | bytes 786432 | tf_op jit(solution)/shard_map/slice | solution.py:75
  34.6 1.0 %fusion.184 = (f32[3,32,512]{2,1,0:T(8,128)S(1)}, f32[3,32,512]{2,1,0:T(8,128)S(1)}) fusion(f32[8,32,512]{2,1,0:T(8,128)} %collective-permute-done.5), kind=kLoop, calls=%fused_computation.296 | loop fusion | bytes 786432 | tf_op jit(solution)/shard_map/slice | solution.py:77
  35.7 1.5 %fusion.p_ref = f32[22,40,512]{2,1,0:T(8,128)} fusion(f32[3,3,512]{2,1,0:T(4,128)S(1)} %get-tuple-element.67, f32[3,32,512]{2,1,0:T(8,128)S(1)} %get-tuple-element.50, f32[3,3,512]{2,1,0:T(4,128)S(1)} %get-tuple-element.66, f32[16,3,512]{2,1,0:T(4,128)S(1)} %get-tuple-element.54, f32[3,3,512]{2,1,0:T(4,128)S(1)} %get-tuple-element.63, ...), kind=kLoop, calls=%fused_computation.7 | loop fusion | flops 9011200 | bytes 3514368 | tf_op jit(solution)/shard_map/concatenate | solution.py:79
  37.2 1.5 %fusion.2.b_ref = f32[22,40,512]{2,1,0:T(8,128)} fusion(f32[3,3,512]{2,1,0:T(4,128)S(1)} %get-tuple-element.68, f32[3,32,512]{2,1,0:T(8,128)S(1)} %get-tuple-element.51, f32[3,3,512]{2,1,0:T(4,128)S(1)} %get-tuple-element.69, f32[16,3,512]{2,1,0:T(4,128)S(1)} %get-tuple-element.55, f32[3,3,512]{2,1,0:T(4,128)S(1)} %get-tuple-element.64, ...), kind=kLoop, calls=%fused_computation.15 | loop fusion | flops 9011200 | bytes 3514368 | tf_op jit(solution)/shard_map/concatenate | solution.py:79
  38.7 0.9 slice.367
  39.6 0.9 slice.374
  40.5 1.5 %fusion.4.rhs_ref = f32[22,40,512]{2,1,0:T(8,128)} fusion(f32[2,2,512]{2,1,0:T(2,128)S(1)} %get-tuple-element.73, f32[2,32,512]{2,1,0:T(8,128)S(1)} %slice.374, f32[2,2,512]{2,1,0:T(2,128)S(1)} %get-tuple-element.72, f32[16,2,512]{2,1,0:T(2,128)S(1)} %slice.370, f32[2,2,512]{2,1,0:T(2,128)S(1)} %get-tuple-element.71, f32[16,32,512]{2,1,0:T(8,128)S(1)} %copy-done.2, ...), kind=kLoop, calls=%fused_computation.23 | loop fusion | flops 14868480 | bytes 3276800 | tf_op jit(solution)/shard_map/concatenate | solution.py:79
  42.1 16.8 %shard_map.37 = (f32[16,32,512]{2,1,0:T(8,128)}, f32[4,32,512]{2,1,0:T(8,128)}) custom-call(s32[4]{0:T(128)} %pad_add_fusion.bounds, f32[22,40,512]{2,1,0:T(8,128)} %fusion.4.rhs_ref, f32[22,40,512]{2,1,0:T(8,128)} %fusion.2.b_ref, f32[22,40,512]{2,1,0:T(8,128)} %fusion.p_ref), custom_call_target="tpu_custom_call" | custom-call | tf_op jit(solution)/shard_map/pallas_call | solution.py:303
  58.8 1.4 %fusion.154 = f32[4,32,128]{2,1,0:T(8,128)S(1)} fusion(f32[4,32,512]{2,1,0:T(8,128)} %get-tuple-element.14, s32[512]{0:T(512)} %copy-done.5, s32[512]{0:T(512)} %copy-done.7, pred[512]{0:T(512)(128)(4,1)} %copy-done.15), kind=kOutput, calls=%fused_computation.264 | convolution fusion | flops 100794368 | bytes 332288 | tf_op jit(solution)/shard_map/xyz,zc->xyc/dot_general | solution.py:125
  60.3 0.8 fusion.10
  61.1 0.7 pad_maximum_fusion.7
  61.8 6.5 %collective-permute-start.6 = (f32[2,4,8,128]{3,2,1,0:T(8,128)S(1)}, f32[2,4,8,128]{3,2,1,0:T(8,128)S(1)}, u32[]{:S(2)}, u32[]{:S(2)}) collective-permute-start(f32[2,4,8,128]{3,2,1,0:T(8,128)S(1)} %pad_maximum_fusion.7), channel_id=1, source_target_pairs={{0,16},{8,24},{16,32},{24,40},{32,48},{40,56},{48,64},{56,72},{64,... | collective-permute-start | bytes 98312 | tf_op jit(solution)/shard_map/ppermute | solution.py:28
  68.3 2.1 %collective-permute-start.7 = (f32[2,4,8,128]{3,2,1,0:T(8,128)S(1)}, f32[2,4,8,128]{3,2,1,0:T(8,128)S(1)}, u32[]{:S(2)}, u32[]{:S(2)}) collective-permute-start(f32[2,4,8,128]{3,2,1,0:T(8,128)S(1)} %pad_maximum_fusion.7), channel_id=1, source_target_pairs={{0,8},{8,16},{16,24},{24,32},{32,40},{40,48},{48,56},{56,64},{64,7... | collective-permute-start | bytes 98312 | tf_op jit(solution)/shard_map/ppermute | solution.py:28
  70.4 5.9 %collective-permute-start.8 = (f32[2,4,8,128]{3,2,1,0:T(8,128)S(1)}, f32[2,4,8,128]{3,2,1,0:T(8,128)S(1)}, u32[]{:S(2)}, u32[]{:S(2)}) collective-permute-start(f32[2,4,8,128]{3,2,1,0:T(8,128)S(1)} %pad_maximum_fusion.7), channel_id=1, source_target_pairs={{8,0},{16,8},{24,16},{32,24},{40,32},{48,40},{56,48},{64,56},{72,6... | collective-permute-start | bytes 98312 | tf_op jit(solution)/shard_map/ppermute | solution.py:29
  76.3 2.1 %collective-permute-start.9 = (f32[2,4,8,128]{3,2,1,0:T(8,128)S(1)}, f32[2,4,8,128]{3,2,1,0:T(8,128)S(1)}, u32[]{:S(2)}, u32[]{:S(2)}) collective-permute-start(f32[2,4,8,128]{3,2,1,0:T(8,128)S(1)} %pad_maximum_fusion.7), channel_id=1, source_target_pairs={{16,0},{24,8},{32,16},{40,24},{48,32},{56,40},{64,48},{72,56},{80,... | collective-permute-start | bytes 98312 | tf_op jit(solution)/shard_map/ppermute | solution.py:29
  78.4 0.7 constant_dynamic-update-slice_fusion.2
  79.2 4.4 %collective-permute-done.9 = f32[2,4,8,128]{3,2,1,0:T(8,128)S(1)} collective-permute-done((f32[2,4,8,128]{3,2,1,0:T(8,128)S(1)}, f32[2,4,8,128]{3,2,1,0:T(8,128)S(1)}, u32[]{:S(2)}, u32[]{:S(2)}) %collective-permute-start.9) | collective-permute-done | bytes 32800 | tf_op jit(solution)/shard_map/ppermute | solution.py:29
  83.6 4.8 %collective-permute-start.10 = (f32[2,20,8,128]{3,2,1,0:T(8,128)S(1)}, f32[2,20,8,128]{3,2,1,0:T(8,128)S(1)}, u32[]{:S(2)}, u32[]{:S(2)}) collective-permute-start(f32[2,20,8,128]{3,2,1,0:T(8,128)S(1)} %constant_dynamic-update-slice_fusion), channel_id=1, source_target_pairs={{0,1},{1,2},{2,3},{3,4},{4,5},{5,6},{6,7},{8,9},{9,10},{10,11},{11... | collective-permute-start | bytes 491528 | tf_op jit(solution)/shard_map/ppermute | solution.py:28
  88.4 1.9 %collective-permute-start.11 = (f32[2,20,8,128]{3,2,1,0:T(8,128)S(1)}, f32[2,20,8,128]{3,2,1,0:T(8,128)S(1)}, u32[]{:S(2)}, u32[]{:S(2)}) collective-permute-start(f32[2,20,8,128]{3,2,1,0:T(8,128)S(1)} %constant_dynamic-update-slice_fusion), channel_id=1, source_target_pairs={{1,0},{2,1},{3,2},{4,3},{5,4},{6,5},{7,6},{9,8},{10,9},{11,10},{12... | collective-permute-start | bytes 491528 | tf_op jit(solution)/shard_map/ppermute | solution.py:29
  90.4 2.2 %collective-permute-done.10 = f32[2,20,8,128]{3,2,1,0:T(8,128)S(1)} collective-permute-done((f32[2,20,8,128]{3,2,1,0:T(8,128)S(1)}, f32[2,20,8,128]{3,2,1,0:T(8,128)S(1)}, u32[]{:S(2)}, u32[]{:S(2)}) %collective-permute-start.10) | collective-permute-done | bytes 163872 | tf_op jit(solution)/shard_map/ppermute | solution.py:28
  92.6 4.0 %collective-permute-done.11 = f32[2,20,8,128]{3,2,1,0:T(8,128)S(1)} collective-permute-done((f32[2,20,8,128]{3,2,1,0:T(8,128)S(1)}, f32[2,20,8,128]{3,2,1,0:T(8,128)S(1)}, u32[]{:S(2)}, u32[]{:S(2)}) %collective-permute-start.11) | collective-permute-done | bytes 163872 | tf_op jit(solution)/shard_map/ppermute | solution.py:29
  96.6 0.5 fusion.139
  97.1 0.3 fusion.140
  98.0 0.3 multiply_add_fusion.2
  98.6 0.3 multiply_add_fusion
  99.2 0.4 copy-done.6
  99.5 0.5 fusion.143
  100.0 0.3 convolution_bitcast_fusion
  100.4 1.1 %bitcast_add_fusion = f32[16,32,512]{2,1,0:T(8,128)} fusion(f32[16,32,512]{2,1,0:T(8,128)S(1)} %copy-done.3, f32[4,32,512]{2,1,0:T(8,128)S(1)} %convolution_bitcast_fusion), kind=kLoop, calls=%fused_computation.87 | loop fusion | flops 262144 | bytes 2359296 | tf_op jit(solution)/shard_map/add | solution.py:336
  (70 shorter events, 1.5 us)
Async XLA Ops:
  0.0 10.1 %copy-start = (f32[16,32,512]{2,1,0:T(8,128)S(1)}, f32[16,32,512]{2,1,0:T(8,128)}, u32[]{:S(2)}) copy-start(f32[16,32,512]{2,1,0:T(8,128)} %param.4) | copy-start | bytes 3145732
  0.0 10.1 %copy-start.1 = (f32[16,32,512]{2,1,0:T(8,128)S(1)}, f32[16,32,512]{2,1,0:T(8,128)}, u32[]{:S(2)}) copy-start(f32[16,32,512]{2,1,0:T(8,128)} %param.5) | copy-start | bytes 3145732
  1.2 8.9 %copy-start.2 = (f32[16,32,512]{2,1,0:T(8,128)S(1)}, f32[16,32,512]{2,1,0:T(8,128)}, u32[]{:S(2)}) copy-start(f32[16,32,512]{2,1,0:T(8,128)} %param.3) | copy-start | bytes 3145732
  3.4 18.6 %collective-permute-start = (f32[16,8,512]{2,1,0:T(8,128)}, f32[16,8,512]{2,1,0:T(8,128)S(1)}, u32[]{:S(2)}, u32[]{:S(2)}) collective-permute-start(f32[16,8,512]{2,1,0:T(8,128)} %pad_maximum_fusion.3), channel_id=1, source_target_pairs={{0,1},{1,2},{2,3},{3,4},{4,5},{5,6},{6,7},{8,9},{9,10},{10,11},{11... | collective-permute-start | bytes 786440 | tf_op jit(solution)/shard_map/ppermute | solution.py:61
  7.2 14.8 %collective-permute-start.1 = (f32[16,8,512]{2,1,0:T(8,128)}, f32[16,8,512]{2,1,0:T(8,128)}, u32[]{:S(2)}, u32[]{:S(2)}) collective-permute-start(f32[16,8,512]{2,1,0:T(8,128)} %pad_maximum_fusion.4), channel_id=1, source_target_pairs={{1,0},{2,1},{3,2},{4,3},{5,4},{6,5},{7,6},{9,8},{10,9},{11,10},{12... | collective-permute-start | bytes 786440 | tf_op jit(solution)/shard_map/ppermute | solution.py:61
  11.0 22.5 %collective-permute-start.3 = (f32[8,32,512]{2,1,0:T(8,128)}, f32[8,32,512]{2,1,0:T(8,128)}, u32[]{:S(2)}, u32[]{:S(2)}) collective-permute-start(f32[8,32,512]{2,1,0:T(8,128)} %pad_maximum_fusion), channel_id=1, source_target_pairs={{0,8},{8,16},{16,24},{24,32},{32,40},{40,48},{48,56},{56,64},{64,7... | collective-permute-start | bytes 1572872 | tf_op jit(solution)/shard_map/ppermute | solution.py:61
  13.8 20.8 %collective-permute-start.5 = (f32[8,32,512]{2,1,0:T(8,128)}, f32[8,32,512]{2,1,0:T(8,128)}, u32[]{:S(2)}, u32[]{:S(2)}) collective-permute-start(f32[8,32,512]{2,1,0:T(8,128)} %pad_maximum_fusion.1), channel_id=1, source_target_pairs={{8,0},{16,8},{24,16},{32,24},{40,32},{48,40},{56,48},{64,56},{72,6... | collective-permute-start | bytes 1572872 | tf_op jit(solution)/shard_map/ppermute | solution.py:61
  19.8 0.7 copy-start.5
  19.9 0.7 copy-start.7
  19.9 0.7 copy-start.15
  19.9 12.2 %copy-start.9 = (s32[32]{0:T(128)}, s32[32]{0:T(128)S(1)}, u32[]{:S(2)}) copy-start(s32[32]{0:T(128)S(1)} %get-tuple-element.80) | copy-start | bytes 388
  19.9 12.2 %copy-start.11 = (s32[32]{0:T(128)}, s32[32]{0:T(128)S(1)}, u32[]{:S(2)}) copy-start(s32[32]{0:T(128)S(1)} %get-tuple-element.81) | copy-start | bytes 388
  20.6 15.1 %copy-start.13 = (pred[32]{0:T(512)(128)(4,1)}, pred[32]{0:T(512)(128)(4,1)S(1)}, u32[]{:S(2)}) copy-start(pred[32]{0:T(512)(128)(4,1)S(1)} %compare_and_fusion.1) | copy-start | bytes 100
  22.0 13.7 %copy-start.4 = (f32[16,8,512]{2,1,0:T(8,128)}, f32[16,8,512]{2,1,0:T(8,128)S(1)}, u32[]{:S(2)}) copy-start(f32[16,8,512]{2,1,0:T(8,128)S(1)} %collective-permute-done) | copy-start | bytes 786436
  23.0 10.2 %collective-permute-start.2 = (f32[3,16,512]{2,1,0:T(8,128)S(1)}, f32[3,16,512]{2,1,0:T(8,128)S(1)}, u32[]{:S(2)}, u32[]{:S(2)}) collective-permute-start(f32[3,16,512]{2,1,0:T(8,128)S(1)} %pad_maximum_fusion.5), channel_id=1, source_target_pairs={{0,8},{8,16},{16,24},{24,32},{32,40},{40,48},{48,56},{56,64},{64,7... | collective-permute-start | bytes 294920 | tf_op jit(solution)/shard_map/ppermute | solution.py:61
  24.9 8.6 %collective-permute-start.4 = (f32[3,16,512]{2,1,0:T(8,128)S(1)}, f32[3,16,512]{2,1,0:T(8,128)S(1)}, u32[]{:S(2)}, u32[]{:S(2)}) collective-permute-start(f32[3,16,512]{2,1,0:T(8,128)S(1)} %pad_maximum_fusion.6), channel_id=1, source_target_pairs={{8,0},{16,8},{24,16},{32,24},{40,32},{48,40},{56,48},{64,56},{72,6... | collective-permute-start | bytes 294920 | tf_op jit(solution)/shard_map/ppermute | solution.py:61
  37.2 3.4 %slice-start = ((f32[16,8,512]{2,1,0:T(8,128)}), f32[16,2,512]{2,1,0:T(2,128)S(1)}, s32[]{:S(2)}) async-start(f32[16,8,512]{2,1,0:T(8,128)} %copy-done.4), calls=%async_computation | async-start | bytes 131072 | tf_op jit(solution)/shard_map/slice | solution.py:76
  61.8 16.6 %collective-permute-start.6 = (f32[2,4,8,128]{3,2,1,0:T(8,128)S(1)}, f32[2,4,8,128]{3,2,1,0:T(8,128)S(1)}, u32[]{:S(2)}, u32[]{:S(2)}) collective-permute-start(f32[2,4,8,128]{3,2,1,0:T(8,128)S(1)} %pad_maximum_fusion.7), channel_id=1, source_target_pairs={{0,16},{8,24},{16,32},{24,40},{32,48},{40,56},{48,64},{56,72},{64,... | collective-permute-start | bytes 98312 | tf_op jit(solution)/shard_map/ppermute | solution.py:28
  68.3 10.1 %collective-permute-start.7 = (f32[2,4,8,128]{3,2,1,0:T(8,128)S(1)}, f32[2,4,8,128]{3,2,1,0:T(8,128)S(1)}, u32[]{:S(2)}, u32[]{:S(2)}) collective-permute-start(f32[2,4,8,128]{3,2,1,0:T(8,128)S(1)} %pad_maximum_fusion.7), channel_id=1, source_target_pairs={{0,8},{8,16},{16,24},{24,32},{32,40},{40,48},{48,56},{56,64},{64,7... | collective-permute-start | bytes 98312 | tf_op jit(solution)/shard_map/ppermute | solution.py:28
  70.4 8.8 %collective-permute-start.8 = (f32[2,4,8,128]{3,2,1,0:T(8,128)S(1)}, f32[2,4,8,128]{3,2,1,0:T(8,128)S(1)}, u32[]{:S(2)}, u32[]{:S(2)}) collective-permute-start(f32[2,4,8,128]{3,2,1,0:T(8,128)S(1)} %pad_maximum_fusion.7), channel_id=1, source_target_pairs={{8,0},{16,8},{24,16},{32,24},{40,32},{48,40},{56,48},{64,56},{72,6... | collective-permute-start | bytes 98312 | tf_op jit(solution)/shard_map/ppermute | solution.py:29
  76.3 7.3 %collective-permute-start.9 = (f32[2,4,8,128]{3,2,1,0:T(8,128)S(1)}, f32[2,4,8,128]{3,2,1,0:T(8,128)S(1)}, u32[]{:S(2)}, u32[]{:S(2)}) collective-permute-start(f32[2,4,8,128]{3,2,1,0:T(8,128)S(1)} %pad_maximum_fusion.7), channel_id=1, source_target_pairs={{16,0},{24,8},{32,16},{40,24},{48,32},{56,40},{64,48},{72,56},{80,... | collective-permute-start | bytes 98312 | tf_op jit(solution)/shard_map/ppermute | solution.py:29
  83.6 9.0 %collective-permute-start.10 = (f32[2,20,8,128]{3,2,1,0:T(8,128)S(1)}, f32[2,20,8,128]{3,2,1,0:T(8,128)S(1)}, u32[]{:S(2)}, u32[]{:S(2)}) collective-permute-start(f32[2,20,8,128]{3,2,1,0:T(8,128)S(1)} %constant_dynamic-update-slice_fusion), channel_id=1, source_target_pairs={{0,1},{1,2},{2,3},{3,4},{4,5},{5,6},{6,7},{8,9},{9,10},{10,11},{11... | collective-permute-start | bytes 491528 | tf_op jit(solution)/shard_map/ppermute | solution.py:28
  88.4 8.1 %collective-permute-start.11 = (f32[2,20,8,128]{3,2,1,0:T(8,128)S(1)}, f32[2,20,8,128]{3,2,1,0:T(8,128)S(1)}, u32[]{:S(2)}, u32[]{:S(2)}) collective-permute-start(f32[2,20,8,128]{3,2,1,0:T(8,128)S(1)} %constant_dynamic-update-slice_fusion), channel_id=1, source_target_pairs={{1,0},{2,1},{3,2},{4,3},{5,4},{6,5},{7,6},{9,8},{10,9},{11,10},{12... | collective-permute-start | bytes 491528 | tf_op jit(solution)/shard_map/ppermute | solution.py:29
  98.9 0.7 copy-start.6
  98.9 0.7 copy-start.8
  98.9 0.7 copy-start.16
  98.9 1.1 %copy-start.10 = (s32[32]{0:T(128)S(1)}, s32[32]{0:T(128)}, u32[]{:S(2)}) copy-start(s32[32]{0:T(128)} %copy-done.9) | copy-start | bytes 388
  98.9 1.1 %copy-start.12 = (s32[32]{0:T(128)S(1)}, s32[32]{0:T(128)}, u32[]{:S(2)}) copy-start(s32[32]{0:T(128)} %copy-done.11) | copy-start | bytes 388
  98.9 1.1 %copy-start.14 = (pred[32]{0:T(512)(128)(4,1)S(1)}, pred[32]{0:T(512)(128)(4,1)}, u32[]{:S(2)}) copy-start(pred[32]{0:T(512)(128)(4,1)} %copy-done.13) | copy-start | bytes 100
  98.9 1.4 %copy-start.3 = (f32[16,32,512]{2,1,0:T(8,128)S(1)}, f32[16,32,512]{2,1,0:T(8,128)}, u32[]{:S(2)}) copy-start(f32[16,32,512]{2,1,0:T(8,128)} %get-tuple-element.13) | copy-start | bytes 3145732

commit v10 on v9

--- a/solution.py
+++ b/solution.py
@@ -207,78 +207,78 @@
 
 
 def fine_kernel(bounds, rhs_ref, b_ref, p_ref, fine_out, resx_out,
-                lx_ref, ly_ref, lz_ref, d_ref, f1_ref, f2_ref, plane_ref):
+                lx_ref, ly_ref, lz_ref, w_ref, f1_ref, f2_ref, plane_ref):
     ex, ey, nz = b_ref.shape
     sx, sy = fine_out.shape[0], fine_out.shape[1]
     depth = (ex - sx) // 2
     row = lax.broadcasted_iota(jnp.int32, (ey, nz), 0)
     lane = lax.broadcasted_iota(jnp.int32, (ey, nz), 1)
+    first_z, last_z = lane == 0, lane == nz - 1
     x_lo, x_hi, y_lo, y_hi = bounds[0], bounds[1], bounds[2], bounds[3]
     rows_in = (row >= y_lo) & (row < y_hi)
 
     def face(a, n):
         return jnp.where((a > 0) & (n > 0), 2.0 * a * n / (a + n), a + n)
 
-    def below(ref, x):
-        return jnp.where(x > 0, ref[jnp.maximum(x - 1, 0)], 0.0)
-
-    def above(ref, x):
-        return jnp.where(x < ex - 1, ref[jnp.minimum(x + 1, ex - 1)], 0.0)
+    def faces_at(x, b0, bxm):
+        lx_ref[x] = face(b0, bxm)
+        ly_ref[x] = face(b0, pltpu.roll(b0, 1, 0))
+        lz_ref[x] = face(b0, jnp.where(first_z, 0.0, pltpu.roll(b0, 1, 1)))
+
+    faces_at(0, b_ref[0], jnp.zeros((ey, nz), jnp.float32))
 
     def faces_body(x, carry):
-        b0 = b_ref[x]
-        lx_ref[x] = face(b0, below(b_ref, x))
-        ly_ref[x] = face(b0, pltpu.roll(b0, 1, 0))
-        lz_ref[x] = face(b0, jnp.where(lane == 0, 0.0, pltpu.roll(b0, 1, 1)))
+        faces_at(x, b_ref[x], b_ref[x - 1])
         return carry
 
-    lax.fori_loop(0, ex, faces_body, 0)
+    lax.fori_loop(1, ex, faces_body, 0)
 
     def coefs(x):
         b0 = b_ref[x]
-        lx_hi = jnp.where(x < ex - 1, lx_ref[jnp.minimum(x + 1, ex - 1)], b0)
         ly = ly_ref[x]
         lz = lz_ref[x]
         ly_hi = pltpu.roll(ly, ey - 1, 0)
-        lz_hi = jnp.where(lane == nz - 1, b0, pltpu.roll(lz, nz - 1, 1))
-        return [lx_ref[x], lx_hi, ly, ly_hi, lz, lz_hi]
+        lz_hi = jnp.where(last_z, b0, pltpu.roll(lz, nz - 1, 1))
+        return [lx_ref[x], lx_ref[x + 1], ly, ly_hi, lz, lz_hi]
 
     def diag_body(x, carry):
-        total = jnp.zeros((ey, nz), jnp.float32)
-        for c in coefs(x):
-            total = total + c
-        d_ref[x] = total
+        c = coefs(x)
+        total = ((c[0] + c[1]) + (c[2] + c[3])) + (c[4] + c[5])
+        w_ref[x] = (2.0 / 3.0) / total
         return carry
 
-    lax.fori_loop(0, ex, diag_body, 0)
+    lax.fori_loop(1, ex - 1, diag_body, 0)
 
     def apply_at(src, x):
         v = src[x]
         nears = [
-            below(src, x),
-            above(src, x),
+            src[x - 1],
+            src[x + 1],
             pltpu.roll(v, 1, 0),
             pltpu.roll(v, ey - 1, 0),
-            jnp.where(lane == 0, 0.0, pltpu.roll(v, 1, 1)),
-            jnp.where(lane == nz - 1, 0.0, pltpu.roll(v, nz - 1, 1)),
+            jnp.where(first_z, 0.0, pltpu.roll(v, 1, 1)),
+            jnp.where(last_z, 0.0, pltpu.roll(v, nz - 1, 1)),
         ]
-        total = jnp.zeros((ey, nz), jnp.float32)
-        for c, n in zip(coefs(x), nears):
-            total = total + c * (v - n)
-        return v, total
-
-    def sweep(src, dst):
+        terms = [c * (v - n) for c, n in zip(coefs(x), nears)]
+        return v, ((terms[0] + terms[1]) + (terms[2] + terms[3])) + (terms[4] + terms[5])
+
+    zero_plane = jnp.zeros((ey, nz), jnp.float32)
+
+    def sweep(src, dst, edge):
+        for x in list(range(edge)) + list(range(ex - edge, ex)):
+            dst[x] = zero_plane
+
         def body(x, carry):
             v, av = apply_at(src, x)
-            new = v + 2.0 / 3.0 * (rhs_ref[x] - av) / d_ref[x]
+            new = v + (rhs_ref[x] - av) * w_ref[x]
             inside = rows_in & (x >= x_lo) & (x < x_hi)
             dst[x] = jnp.where(inside, new, 0.0)
             return carry
 
-        lax.fori_loop(0, ex, body, 0)
-
-    sweep(p_ref, f1_ref)
-    sweep(f1_ref, f2_ref)
+        lax.fori_loop(edge, ex - edge, body, 0)
+
+    sweep(p_ref, f1_ref, 1)
+    sweep(f1_ref, f2_ref, 2)
 
     def res_body(xc, carry):
         acc = jnp.zeros((sy, nz), jnp.float32)
@@ -319,7 +319,6 @@
     rows = ((0, 0), (1, 1), (0, 0))
     rhs_e = jnp.pad(rhs_e, ((1, 1), (2, 2), (0, 0)))
     b_e, fine = jnp.pad(b_e, rows), jnp.pad(fine, rows)
-    rhs_e, b_e, fine = lax.optimization_barrier((rhs_e, b_e, fine))
     ex, ey = b_e.shape[0], b_e.shape[1]
     bi, gi = lax.axis_index("box"), lax.axis_index("group")
     nb, ng = lax.axis_size("box"), lax.axis_size("group")

time: 103 us -> 101 us (0.981)
  Pallas kernels: 16.8 us -> 15.6 us
    pallas_call x1, Pallas kernels: 16.8 us -> 15.6 us  [fine_stage(): pl.pallas_call(fine_kernel, out_shape=(plane((sx, sy, sz), jnp.float32),...]
where the time goes in v10:
time: 101 us; the launch traced here: 100 us
  starting transfers between devices  45 us (45%)
  Pallas kernels  15.6 us (15%)
  other arithmetic  13.7 us (14%)
  waiting for transfers between devices  10.9 us (11%)
  local copies, waits for them, and re-layouts  10.2 us (10%)
  matrix products  4.29 us (4%)
    ppermute x6, starting transfers between devices, send(): return lax.ppermute(msg, axis, pairs)  21.7 us
    pallas_call x1, Pallas kernels, fine_stage(): pl.pallas_call(fine_kernel, out_shape=(plane((sx, sy, sz), jnp.float32),...  15.6 us
    ppermute x3, starting transfers between devices, halo_from(): lax.ppermute(lax.slice_in_dim(block, n - width, n, axis=dim), axis, forward)  13.4 us
    ppermute x3, starting transfers between devices, halo_from(): lax.ppermute(lax.slice_in_dim(block, 0, width, axis=dim), axis, backward)  9.89 us
    ppermute x3, waiting for transfers between devices, halo_from(): lax.ppermute(lax.slice_in_dim(block, 0, width, axis=dim), axis, backward)  8.42 us
    concatenate x3, other arithmetic, packed_halo(): out.append(jnp.concatenate(rows, axis=0))  4.56 us
    slice x6, local copies, waits for them, and re-layouts, packed_halo(): lax.slice_in_dim(f, f.shape[dim] - d, f.shape[dim], axis=dim)  3.62 us
    concatenate x6, other arithmetic, send(): msg = jnp.concatenate(pieces, axis=dim)  3.29 us
  transfers between devices with their start and end apart: 12, of which 4 were waited for; matrix products, arithmetic and copies ran while one was open for 9% of the time, Pallas kernels for 0%

profile of v10, /device:TPU:34, one launch (start us, length us, event | category | flops | bytes accessed | tf_op | source)
XLA Modules:
  0.0 100.3 jit_solution(11439050225976465408)
XLA Ops:
  0.0 1.2 %fusion.180 = (f32[16,2,512]{2,1,0:T(2,128)S(1)}, f32[16,2,512]{2,1,0:T(2,128)S(1)}) fusion(f32[16,32,512]{2,1,0:T(8,128)} %param.3), kind=kLoop, calls=%fused_computation.292 | loop fusion | bytes 262144 | tf_op jit(solution)/shard_map/slice | solution.py:51
  1.2 1.4 %fusion.181 = (f32[16,3,512]{2,1,0:T(4,128)S(1)}, f32[16,3,512]{2,1,0:T(4,128)S(1)}, f32[16,3,512]{2,1,0:T(4,128)S(1)}, f32[16,3,512]{2,1,0:T(4,128)S(1)}) fusion(f32[16,32,512]{2,1,0:T(8,128)} %param.4, f32[16,32,512]{2,1,0:T(8,128)} %param.5), kind=kLoop, calls=%fused_computation.293 | loop fusion | bytes 786432 | tf_op jit(solution)/shard_map/slice | solution.py:51
  2.6 0.8 pad_maximum_fusion.3
  3.4 3.0 %collective-permute-start = (f32[16,8,512]{2,1,0:T(8,128)}, f32[16,8,512]{2,1,0:T(8,128)S(1)}, u32[]{:S(2)}, u32[]{:S(2)}) collective-permute-start(f32[16,8,512]{2,1,0:T(8,128)} %pad_maximum_fusion.3), channel_id=1, source_target_pairs={{0,1},{1,2},{2,3},{3,4},{4,5},{5,6},{6,7},{8,9},{9,10},{10,11},{11... | collective-permute-start | bytes 786440 | tf_op jit(solution)/shard_map/ppermute | solution.py:61
  6.5 0.8 pad_maximum_fusion.4
  7.2 2.8 %collective-permute-start.1 = (f32[16,8,512]{2,1,0:T(8,128)}, f32[16,8,512]{2,1,0:T(8,128)}, u32[]{:S(2)}, u32[]{:S(2)}) collective-permute-start(f32[16,8,512]{2,1,0:T(8,128)} %pad_maximum_fusion.4), channel_id=1, source_target_pairs={{1,0},{2,1},{3,2},{4,3},{5,4},{6,5},{7,6},{9,8},{10,9},{11,10},{12... | collective-permute-start | bytes 786440 | tf_op jit(solution)/shard_map/ppermute | solution.py:61
  10.2 0.8 pad_maximum_fusion
  11.0 1.9 %collective-permute-start.3 = (f32[8,32,512]{2,1,0:T(8,128)}, f32[8,32,512]{2,1,0:T(8,128)}, u32[]{:S(2)}, u32[]{:S(2)}) collective-permute-start(f32[8,32,512]{2,1,0:T(8,128)} %pad_maximum_fusion), channel_id=1, source_target_pairs={{0,8},{8,16},{16,24},{24,32},{32,40},{40,48},{48,56},{56,64},{64,7... | collective-permute-start | bytes 1572872 | tf_op jit(solution)/shard_map/ppermute | solution.py:61
  13.0 0.8 pad_maximum_fusion.1
  13.8 6.0 %collective-permute-start.5 = (f32[8,32,512]{2,1,0:T(8,128)}, f32[8,32,512]{2,1,0:T(8,128)}, u32[]{:S(2)}, u32[]{:S(2)}) collective-permute-start(f32[8,32,512]{2,1,0:T(8,128)} %pad_maximum_fusion.1), channel_id=1, source_target_pairs={{8,0},{16,8},{24,16},{32,24},{40,32},{48,40},{56,48},{64,56},{72,6... | collective-permute-start | bytes 1572872 | tf_op jit(solution)/shard_map/ppermute | solution.py:61
  20.0 0.5 fusion.156
  20.6 0.7 fusion.11
  21.3 0.7 pad_add_fusion.bounds
  22.0 0.9 fusion.188
  23.0 1.9 %collective-permute-start.2 = (f32[3,16,512]{2,1,0:T(8,128)S(1)}, f32[3,16,512]{2,1,0:T(8,128)S(1)}, u32[]{:S(2)}, u32[]{:S(2)}) collective-permute-start(f32[3,16,512]{2,1,0:T(8,128)S(1)} %pad_maximum_fusion.5), channel_id=1, source_target_pairs={{0,8},{8,16},{16,24},{24,32},{32,40},{40,48},{48,56},{56,64},{64,7... | collective-permute-start | bytes 294920 | tf_op jit(solution)/shard_map/ppermute | solution.py:61
  24.9 6.0 %collective-permute-start.4 = (f32[3,16,512]{2,1,0:T(8,128)S(1)}, f32[3,16,512]{2,1,0:T(8,128)S(1)}, u32[]{:S(2)}, u32[]{:S(2)}) collective-permute-start(f32[3,16,512]{2,1,0:T(8,128)S(1)} %pad_maximum_fusion.6), channel_id=1, source_target_pairs={{8,0},{16,8},{24,16},{32,24},{40,32},{48,40},{56,48},{64,56},{72,6... | collective-permute-start | bytes 294920 | tf_op jit(solution)/shard_map/ppermute | solution.py:61
  31.0 1.1 %fusion.186 = (f32[16,3,512]{2,1,0:T(4,128)S(1)}, f32[16,3,512]{2,1,0:T(4,128)S(1)}) fusion(f32[16,8,512]{2,1,0:T(8,128)} %collective-permute-done.1), kind=kLoop, calls=%fused_computation.298 | loop fusion | bytes 393216 | tf_op jit(solution)/shard_map/slice | solution.py:76
  32.1 1.0 slice.370
  33.2 0.3 collective-permute-done.4
  33.5 1.0 %fusion.183 = (f32[3,32,512]{2,1,0:T(8,128)S(1)}, f32[3,32,512]{2,1,0:T(8,128)S(1)}) fusion(f32[8,32,512]{2,1,0:T(8,128)} %collective-permute-done.3), kind=kLoop, calls=%fused_computation.295 | loop fusion | bytes 786432 | tf_op jit(solution)/shard_map/slice | solution.py:75
  34.6 1.0 %fusion.184 = (f32[3,32,512]{2,1,0:T(8,128)S(1)}, f32[3,32,512]{2,1,0:T(8,128)S(1)}) fusion(f32[8,32,512]{2,1,0:T(8,128)} %collective-permute-done.5), kind=kLoop, calls=%fused_computation.296 | loop fusion | bytes 786432 | tf_op jit(solution)/shard_map/slice | solution.py:77
  35.7 1.5 %fusion.p_ref = f32[22,40,512]{2,1,0:T(8,128)} fusion(f32[3,3,512]{2,1,0:T(4,128)S(1)} %get-tuple-element.61, f32[3,32,512]{2,1,0:T(8,128)S(1)} %get-tuple-element.44, f32[3,3,512]{2,1,0:T(4,128)S(1)} %get-tuple-element.60, f32[16,3,512]{2,1,0:T(4,128)S(1)} %get-tuple-element.48, f32[3,3,512]{2,1,0:T(4,128)S(1)} %get-tuple-element.57, ...), kind=kLoop, calls=%fused_computation.7 | loop fusion | flops 9011200 | bytes 3514368 | tf_op jit(solution)/shard_map/concatenate | solution.py:79
  37.2 1.5 %fusion.2.b_ref = f32[22,40,512]{2,1,0:T(8,128)} fusion(f32[3,3,512]{2,1,0:T(4,128)S(1)} %get-tuple-element.62, f32[3,32,512]{2,1,0:T(8,128)S(1)} %get-tuple-element.45, f32[3,3,512]{2,1,0:T(4,128)S(1)} %get-tuple-element.63, f32[16,3,512]{2,1,0:T(4,128)S(1)} %get-tuple-element.49, f32[3,3,512]{2,1,0:T(4,128)S(1)} %get-tuple-element.58, ...), kind=kLoop, calls=%fused_computation.15 | loop fusion | flops 9011200 | bytes 3514368 | tf_op jit(solution)/shard_map/concatenate | solution.py:79
  38.7 0.9 slice.367
  39.6 0.9 slice.374
  40.5 1.5 %fusion.4.rhs_ref = f32[22,40,512]{2,1,0:T(8,128)} fusion(f32[2,2,512]{2,1,0:T(2,128)S(1)} %get-tuple-element.67, f32[2,32,512]{2,1,0:T(8,128)S(1)} %slice.374, f32[2,2,512]{2,1,0:T(2,128)S(1)} %get-tuple-element.66, f32[16,2,512]{2,1,0:T(2,128)S(1)} %slice.370, f32[2,2,512]{2,1,0:T(2,128)S(1)} %get-tuple-element.65, f32[16,32,512]{2,1,0:T(8,128)S(1)} %copy-done.2, ...), kind=kLoop, calls=%fused_computation.23 | loop fusion | flops 14868480 | bytes 3276800 | tf_op jit(solution)/shard_map/concatenate | solution.py:79
  42.1 15.6 %shard_map.37 = (f32[16,32,512]{2,1,0:T(8,128)}, f32[4,32,512]{2,1,0:T(8,128)}) custom-call(s32[4]{0:T(128)} %pad_add_fusion.bounds, f32[22,40,512]{2,1,0:T(8,128)} %fusion.4.rhs_ref, f32[22,40,512]{2,1,0:T(8,128)} %fusion.2.b_ref, f32[22,40,512]{2,1,0:T(8,128)} %fusion.p_ref), custom_call_target="tpu_custom_call" | custom-call | tf_op jit(solution)/shard_map/pallas_call | solution.py:303
  57.6 1.4 %fusion.154 = f32[4,32,128]{2,1,0:T(8,128)S(1)} fusion(f32[4,32,512]{2,1,0:T(8,128)} %get-tuple-element.8, s32[512]{0:T(512)} %copy-done.5, s32[512]{0:T(512)} %copy-done.7, pred[512]{0:T(512)(128)(4,1)} %copy-done.15), kind=kOutput, calls=%fused_computation.264 | convolution fusion | flops 100794368 | bytes 332288 | tf_op jit(solution)/shard_map/xyz,zc->xyc/dot_general | solution.py:125
  59.1 0.8 fusion.10
  59.9 0.7 pad_maximum_fusion.7
  60.6 6.5 %collective-permute-start.6 = (f32[2,4,8,128]{3,2,1,0:T(8,128)S(1)}, f32[2,4,8,128]{3,2,1,0:T(8,128)S(1)}, u32[]{:S(2)}, u32[]{:S(2)}) collective-permute-start(f32[2,4,8,128]{3,2,1,0:T(8,128)S(1)} %pad_maximum_fusion.7), channel_id=1, source_target_pairs={{0,16},{8,24},{16,32},{24,40},{32,48},{40,56},{48,64},{56,72},{64,... | collective-permute-start | bytes 98312 | tf_op jit(solution)/shard_map/ppermute | solution.py:28
  67.1 2.1 %collective-permute-start.7 = (f32[2,4,8,128]{3,2,1,0:T(8,128)S(1)}, f32[2,4,8,128]{3,2,1,0:T(8,128)S(1)}, u32[]{:S(2)}, u32[]{:S(2)}) collective-permute-start(f32[2,4,8,128]{3,2,1,0:T(8,128)S(1)} %pad_maximum_fusion.7), channel_id=1, source_target_pairs={{0,8},{8,16},{16,24},{24,32},{32,40},{40,48},{48,56},{56,64},{64,7... | collective-permute-start | bytes 98312 | tf_op jit(solution)/shard_map/ppermute | solution.py:28
  69.2 5.9 %collective-permute-start.8 = (f32[2,4,8,128]{3,2,1,0:T(8,128)S(1)}, f32[2,4,8,128]{3,2,1,0:T(8,128)S(1)}, u32[]{:S(2)}, u32[]{:S(2)}) collective-permute-start(f32[2,4,8,128]{3,2,1,0:T(8,128)S(1)} %pad_maximum_fusion.7), channel_id=1, source_target_pairs={{8,0},{16,8},{24,16},{32,24},{40,32},{48,40},{56,48},{64,56},{72,6... | collective-permute-start | bytes 98312 | tf_op jit(solution)/shard_map/ppermute | solution.py:29
  75.1 2.1 %collective-permute-start.9 = (f32[2,4,8,128]{3,2,1,0:T(8,128)S(1)}, f32[2,4,8,128]{3,2,1,0:T(8,128)S(1)}, u32[]{:S(2)}, u32[]{:S(2)}) collective-permute-start(f32[2,4,8,128]{3,2,1,0:T(8,128)S(1)} %pad_maximum_fusion.7), channel_id=1, source_target_pairs={{16,0},{24,8},{32,16},{40,24},{48,32},{56,40},{64,48},{72,56},{80,... | collective-permute-start | bytes 98312 | tf_op jit(solution)/shard_map/ppermute | solution.py:29
  77.2 0.7 constant_dynamic-update-slice_fusion.2
  78.0 4.4 %collective-permute-done.9 = f32[2,4,8,128]{3,2,1,0:T(8,128)S(1)} collective-permute-done((f32[2,4,8,128]{3,2,1,0:T(8,128)S(1)}, f32[2,4,8,128]{3,2,1,0:T(8,128)S(1)}, u32[]{:S(2)}, u32[]{:S(2)}) %collective-permute-start.9) | collective-permute-done | bytes 32800 | tf_op jit(solution)/shard_map/ppermute | solution.py:29
  82.4 4.8 %collective-permute-start.10 = (f32[2,20,8,128]{3,2,1,0:T(8,128)S(1)}, f32[2,20,8,128]{3,2,1,0:T(8,128)S(1)}, u32[]{:S(2)}, u32[]{:S(2)}) collective-permute-start(f32[2,20,8,128]{3,2,1,0:T(8,128)S(1)} %constant_dynamic-update-slice_fusion), channel_id=1, source_target_pairs={{0,1},{1,2},{2,3},{3,4},{4,5},{5,6},{6,7},{8,9},{9,10},{10,11},{11... | collective-permute-start | bytes 491528 | tf_op jit(solution)/shard_map/ppermute | solution.py:28
  87.2 1.9 %collective-permute-start.11 = (f32[2,20,8,128]{3,2,1,0:T(8,128)S(1)}, f32[2,20,8,128]{3,2,1,0:T(8,128)S(1)}, u32[]{:S(2)}, u32[]{:S(2)}) collective-permute-start(f32[2,20,8,128]{3,2,1,0:T(8,128)S(1)} %constant_dynamic-update-slice_fusion), channel_id=1, source_target_pairs={{1,0},{2,1},{3,2},{4,3},{5,4},{6,5},{7,6},{9,8},{10,9},{11,10},{12... | collective-permute-start | bytes 491528 | tf_op jit(solution)/shard_map/ppermute | solution.py:29
  89.2 2.2 %collective-permute-done.10 = f32[2,20,8,128]{3,2,1,0:T(8,128)S(1)} collective-permute-done((f32[2,20,8,128]{3,2,1,0:T(8,128)S(1)}, f32[2,20,8,128]{3,2,1,0:T(8,128)S(1)}, u32[]{:S(2)}, u32[]{:S(2)}) %collective-permute-start.10) | collective-permute-done | bytes 163872 | tf_op jit(solution)/shard_map/ppermute | solution.py:28
  91.4 4.0 %collective-permute-done.11 = f32[2,20,8,128]{3,2,1,0:T(8,128)S(1)} collective-permute-done((f32[2,20,8,128]{3,2,1,0:T(8,128)S(1)}, f32[2,20,8,128]{3,2,1,0:T(8,128)S(1)}, u32[]{:S(2)}, u32[]{:S(2)}) %collective-permute-start.11) | collective-permute-done | bytes 163872 | tf_op jit(solution)/shard_map/ppermute | solution.py:29
  95.4 0.5 fusion.139
  95.9 0.3 fusion.140
  96.8 0.3 multiply_add_fusion.2
  97.4 0.3 multiply_add_fusion
  98.0 0.4 copy-done.6
  98.3 0.5 fusion.143
  98.8 0.3 convolution_bitcast_fusion
  99.2 1.1 %bitcast_add_fusion = f32[16,32,512]{2,1,0:T(8,128)} fusion(f32[16,32,512]{2,1,0:T(8,128)S(1)} %copy-done.3, f32[4,32,512]{2,1,0:T(8,128)S(1)} %convolution_bitcast_fusion), kind=kLoop, calls=%fused_computation.87 | loop fusion | flops 262144 | bytes 2359296 | tf_op jit(solution)/shard_map/add | solution.py:335
  (70 shorter events, 1.5 us)
Async XLA Ops:
  0.0 10.1 %copy-start = (f32[16,32,512]{2,1,0:T(8,128)S(1)}, f32[16,32,512]{2,1,0:T(8,128)}, u32[]{:S(2)}) copy-start(f32[16,32,512]{2,1,0:T(8,128)} %param.4) | copy-start | bytes 3145732
  0.0 10.1 %copy-start.1 = (f32[16,32,512]{2,1,0:T(8,128)S(1)}, f32[16,32,512]{2,1,0:T(8,128)}, u32[]{:S(2)}) copy-start(f32[16,32,512]{2,1,0:T(8,128)} %param.5) | copy-start | bytes 3145732
  1.2 8.9 %copy-start.2 = (f32[16,32,512]{2,1,0:T(8,128)S(1)}, f32[16,32,512]{2,1,0:T(8,128)}, u32[]{:S(2)}) copy-start(f32[16,32,512]{2,1,0:T(8,128)} %param.3) | copy-start | bytes 3145732
  3.4 18.6 %collective-permute-start = (f32[16,8,512]{2,1,0:T(8,128)}, f32[16,8,512]{2,1,0:T(8,128)S(1)}, u32[]{:S(2)}, u32[]{:S(2)}) collective-permute-start(f32[16,8,512]{2,1,0:T(8,128)} %pad_maximum_fusion.3), channel_id=1, source_target_pairs={{0,1},{1,2},{2,3},{3,4},{4,5},{5,6},{6,7},{8,9},{9,10},{10,11},{11... | collective-permute-start | bytes 786440 | tf_op jit(solution)/shard_map/ppermute | solution.py:61
  7.2 14.8 %collective-permute-start.1 = (f32[16,8,512]{2,1,0:T(8,128)}, f32[16,8,512]{2,1,0:T(8,128)}, u32[]{:S(2)}, u32[]{:S(2)}) collective-permute-start(f32[16,8,512]{2,1,0:T(8,128)} %pad_maximum_fusion.4), channel_id=1, source_target_pairs={{1,0},{2,1},{3,2},{4,3},{5,4},{6,5},{7,6},{9,8},{10,9},{11,10},{12... | collective-permute-start | bytes 786440 | tf_op jit(solution)/shard_map/ppermute | solution.py:61
  11.0 22.5 %collective-permute-start.3 = (f32[8,32,512]{2,1,0:T(8,128)}, f32[8,32,512]{2,1,0:T(8,128)}, u32[]{:S(2)}, u32[]{:S(2)}) collective-permute-start(f32[8,32,512]{2,1,0:T(8,128)} %pad_maximum_fusion), channel_id=1, source_target_pairs={{0,8},{8,16},{16,24},{24,32},{32,40},{40,48},{48,56},{56,64},{64,7... | collective-permute-start | bytes 1572872 | tf_op jit(solution)/shard_map/ppermute | solution.py:61
  13.8 20.8 %collective-permute-start.5 = (f32[8,32,512]{2,1,0:T(8,128)}, f32[8,32,512]{2,1,0:T(8,128)}, u32[]{:S(2)}, u32[]{:S(2)}) collective-permute-start(f32[8,32,512]{2,1,0:T(8,128)} %pad_maximum_fusion.1), channel_id=1, source_target_pairs={{8,0},{16,8},{24,16},{32,24},{40,32},{48,40},{56,48},{64,56},{72,6... | collective-permute-start | bytes 1572872 | tf_op jit(solution)/shard_map/ppermute | solution.py:61
  19.8 0.7 copy-start.5
  19.9 0.7 copy-start.7
  19.9 0.7 copy-start.15
  19.9 12.2 %copy-start.9 = (s32[32]{0:T(128)}, s32[32]{0:T(128)S(1)}, u32[]{:S(2)}) copy-start(s32[32]{0:T(128)S(1)} %get-tuple-element.74) | copy-start | bytes 388
  19.9 12.2 %copy-start.11 = (s32[32]{0:T(128)}, s32[32]{0:T(128)S(1)}, u32[]{:S(2)}) copy-start(s32[32]{0:T(128)S(1)} %get-tuple-element.75) | copy-start | bytes 388
  20.6 15.1 %copy-start.13 = (pred[32]{0:T(512)(128)(4,1)}, pred[32]{0:T(512)(128)(4,1)S(1)}, u32[]{:S(2)}) copy-start(pred[32]{0:T(512)(128)(4,1)S(1)} %compare_and_fusion.1) | copy-start | bytes 100
  22.0 13.7 %copy-start.4 = (f32[16,8,512]{2,1,0:T(8,128)}, f32[16,8,512]{2,1,0:T(8,128)S(1)}, u32[]{:S(2)}) copy-start(f32[16,8,512]{2,1,0:T(8,128)S(1)} %collective-permute-done) | copy-start | bytes 786436
  23.0 10.2 %collective-permute-start.2 = (f32[3,16,512]{2,1,0:T(8,128)S(1)}, f32[3,16,512]{2,1,0:T(8,128)S(1)}, u32[]{:S(2)}, u32[]{:S(2)}) collective-permute-start(f32[3,16,512]{2,1,0:T(8,128)S(1)} %pad_maximum_fusion.5), channel_id=1, source_target_pairs={{0,8},{8,16},{16,24},{24,32},{32,40},{40,48},{48,56},{56,64},{64,7... | collective-permute-start | bytes 294920 | tf_op jit(solution)/shard_map/ppermute | solution.py:61
  24.9 8.6 %collective-permute-start.4 = (f32[3,16,512]{2,1,0:T(8,128)S(1)}, f32[3,16,512]{2,1,0:T(8,128)S(1)}, u32[]{:S(2)}, u32[]{:S(2)}) collective-permute-start(f32[3,16,512]{2,1,0:T(8,128)S(1)} %pad_maximum_fusion.6), channel_id=1, source_target_pairs={{8,0},{16,8},{24,16},{32,24},{40,32},{48,40},{56,48},{64,56},{72,6... | collective-permute-start | bytes 294920 | tf_op jit(solution)/shard_map/ppermute | solution.py:61
  37.2 3.4 %slice-start = ((f32[16,8,512]{2,1,0:T(8,128)}), f32[16,2,512]{2,1,0:T(2,128)S(1)}, s32[]{:S(2)}) async-start(f32[16,8,512]{2,1,0:T(8,128)} %copy-done.4), calls=%async_computation | async-start | bytes 131072 | tf_op jit(solution)/shard_map/slice | solution.py:76
  60.6 16.6 %collective-permute-start.6 = (f32[2,4,8,128]{3,2,1,0:T(8,128)S(1)}, f32[2,4,8,128]{3,2,1,0:T(8,128)S(1)}, u32[]{:S(2)}, u32[]{:S(2)}) collective-permute-start(f32[2,4,8,128]{3,2,1,0:T(8,128)S(1)} %pad_maximum_fusion.7), channel_id=1, source_target_pairs={{0,16},{8,24},{16,32},{24,40},{32,48},{40,56},{48,64},{56,72},{64,... | collective-permute-start | bytes 98312 | tf_op jit(solution)/shard_map/ppermute | solution.py:28
  67.1 10.1 %collective-permute-start.7 = (f32[2,4,8,128]{3,2,1,0:T(8,128)S(1)}, f32[2,4,8,128]{3,2,1,0:T(8,128)S(1)}, u32[]{:S(2)}, u32[]{:S(2)}) collective-permute-start(f32[2,4,8,128]{3,2,1,0:T(8,128)S(1)} %pad_maximum_fusion.7), channel_id=1, source_target_pairs={{0,8},{8,16},{16,24},{24,32},{32,40},{40,48},{48,56},{56,64},{64,7... | collective-permute-start | bytes 98312 | tf_op jit(solution)/shard_map/ppermute | solution.py:28
  69.2 8.8 %collective-permute-start.8 = (f32[2,4,8,128]{3,2,1,0:T(8,128)S(1)}, f32[2,4,8,128]{3,2,1,0:T(8,128)S(1)}, u32[]{:S(2)}, u32[]{:S(2)}) collective-permute-start(f32[2,4,8,128]{3,2,1,0:T(8,128)S(1)} %pad_maximum_fusion.7), channel_id=1, source_target_pairs={{8,0},{16,8},{24,16},{32,24},{40,32},{48,40},{56,48},{64,56},{72,6... | collective-permute-start | bytes 98312 | tf_op jit(solution)/shard_map/ppermute | solution.py:29
  75.1 7.3 %collective-permute-start.9 = (f32[2,4,8,128]{3,2,1,0:T(8,128)S(1)}, f32[2,4,8,128]{3,2,1,0:T(8,128)S(1)}, u32[]{:S(2)}, u32[]{:S(2)}) collective-permute-start(f32[2,4,8,128]{3,2,1,0:T(8,128)S(1)} %pad_maximum_fusion.7), channel_id=1, source_target_pairs={{16,0},{24,8},{32,16},{40,24},{48,32},{56,40},{64,48},{72,56},{80,... | collective-permute-start | bytes 98312 | tf_op jit(solution)/shard_map/ppermute | solution.py:29
  82.4 9.0 %collective-permute-start.10 = (f32[2,20,8,128]{3,2,1,0:T(8,128)S(1)}, f32[2,20,8,128]{3,2,1,0:T(8,128)S(1)}, u32[]{:S(2)}, u32[]{:S(2)}) collective-permute-start(f32[2,20,8,128]{3,2,1,0:T(8,128)S(1)} %constant_dynamic-update-slice_fusion), channel_id=1, source_target_pairs={{0,1},{1,2},{2,3},{3,4},{4,5},{5,6},{6,7},{8,9},{9,10},{10,11},{11... | collective-permute-start | bytes 491528 | tf_op jit(solution)/shard_map/ppermute | solution.py:28
  87.2 8.1 %collective-permute-start.11 = (f32[2,20,8,128]{3,2,1,0:T(8,128)S(1)}, f32[2,20,8,128]{3,2,1,0:T(8,128)S(1)}, u32[]{:S(2)}, u32[]{:S(2)}) collective-permute-start(f32[2,20,8,128]{3,2,1,0:T(8,128)S(1)} %constant_dynamic-update-slice_fusion), channel_id=1, source_target_pairs={{1,0},{2,1},{3,2},{4,3},{5,4},{6,5},{7,6},{9,8},{10,9},{11,10},{12... | collective-permute-start | bytes 491528 | tf_op jit(solution)/shard_map/ppermute | solution.py:29
  97.7 0.7 copy-start.6
  97.7 0.7 copy-start.8
  97.7 0.7 copy-start.16
  97.7 1.1 %copy-start.10 = (s32[32]{0:T(128)S(1)}, s32[32]{0:T(128)}, u32[]{:S(2)}) copy-start(s32[32]{0:T(128)} %copy-done.9) | copy-start | bytes 388
  97.7 1.1 %copy-start.12 = (s32[32]{0:T(128)S(1)}, s32[32]{0:T(128)}, u32[]{:S(2)}) copy-start(s32[32]{0:T(128)} %copy-done.11) | copy-start | bytes 388
  97.7 1.1 %copy-start.14 = (pred[32]{0:T(512)(128)(4,1)S(1)}, pred[32]{0:T(512)(128)(4,1)}, u32[]{:S(2)}) copy-start(pred[32]{0:T(512)(128)(4,1)} %copy-done.13) | copy-start | bytes 100
  97.7 1.4 %copy-start.3 = (f32[16,32,512]{2,1,0:T(8,128)S(1)}, f32[16,32,512]{2,1,0:T(8,128)}, u32[]{:S(2)}) copy-start(f32[16,32,512]{2,1,0:T(8,128)} %get-tuple-element.7) | copy-start | bytes 3145732

commit v11 on v7

--- a/solution.py
+++ b/solution.py
@@ -177,6 +177,19 @@
     return inside
 
 
+def shared_faces(b):
+    def face(a, n):
+        return jnp.where((a > 0) & (n > 0), 2.0 * a * n / (a + n), a + n)
+
+    nears = padded_neighbours(jnp.pad(b, 1))
+    lx, ly, lz = face(b, nears[0]), face(b, nears[2]), face(b, nears[4])
+    hx = jnp.pad(lx, ((0, 1), (0, 0), (0, 0)))[1:]
+    hy = jnp.pad(ly, ((0, 0), (0, 1), (0, 0)))[:, 1:]
+    hz = jnp.pad(lz, ((0, 0), (0, 0), (0, 1)))[:, :, 1:]
+    top = lax.broadcasted_iota(jnp.int32, b.shape, 2) == b.shape[2] - 1
+    return [lx, hx, ly, hy, lz, jnp.where(top, b, hz)]
+
+
 def low_faces(b):
     faces = []
     for dim in range(3):
@@ -207,7 +220,7 @@
     rhs_e, b_e, fine = lax.optimization_barrier((rhs_e, b_e, fine))
     totals = (sx * lax.axis_size("box"), sy * lax.axis_size("group"))
     inside = grid_mask(fine.shape, depth, ("box", "group"), totals)
-    coefs = face_pairs(b_e, low_faces(b_e))
+    coefs = shared_faces(b_e)
     diag = sum(coefs)
     for sweep in range(SWEEPS):
         step = 2.0 / 3.0 * (rhs_e - apply_op(fine, padded_neighbours(jnp.pad(fine, 1)), coefs)) / diag

time: 97.7 us -> 96.4 us (0.987)
  local copies, waits for them, and re-layouts: 12.8 us -> 7.8 us
  waiting for transfers between devices: 11.3 us -> 13.8 us
  other arithmetic: 24.1 us -> 26.1 us
    select_n x2 -> x1, other arithmetic: 8.98 us -> 4.11 us  [per_device(): fine = jnp.where(inside, fine + step, 0.0)]
    slice x0 -> x1, other arithmetic: none -> 4 us  [shared_faces(): hy = jnp.pad(ly, ((0, 0), (0, 1), (0, 0)))[:, 1:]]
    ppermute x6, waiting for transfers between devices: 0.02 us -> 2.75 us  [send(): return lax.ppermute(msg, axis, pairs)]
    slice x2 -> x3, local copies, waits for them, and re-layouts: 2.06 us -> 0.06 us  [packed_halo(): yh[:, ys]]
    slice x2 -> x3, local copies, waits for them, and re-layouts: 2.06 us -> 0.06 us  [packed_halo(): yl[:, ys]]
    reduce_sum x2, other arithmetic: 2.67 us -> 4.65 us  [block_mean(): fx = field.reshape(sx // 4, 4, sy, sz).sum(axis=1)]
    select_n x3 -> x1, other arithmetic: 1.74 us -> 2.14 us  [face(): return jnp.where((a > 0) & (n > 0), 2.0 * a * n / (a + n), a + n)]
  transfers between devices with their start and end apart: 12 -> 12, of which waited for: 3 -> 5; matrix products, arithmetic and copies ran while one was open for 11% -> 6% of each run, Pallas kernels for 0% -> 0%
where the time goes in v11:
time: 96.4 us; the launch traced here: 95.5 us
  starting transfers between devices  45.1 us (47%)
  other arithmetic  26.1 us (27%)
  waiting for transfers between devices  13.8 us (14%)
  local copies, waits for them, and re-layouts  7.8 us (8%)
  matrix products  2.05 us (2%)
    ppermute x6, starting transfers between devices, send(): return lax.ppermute(msg, axis, pairs)  21.7 us
    ppermute x3, starting transfers between devices, halo_from(): lax.ppermute(lax.slice_in_dim(block, n - width, n, axis=dim), axis, forward)  13.3 us
    ppermute x3, starting transfers between devices, halo_from(): lax.ppermute(lax.slice_in_dim(block, 0, width, axis=dim), axis, backward)  10.1 us
    ppermute x3, waiting for transfers between devices, halo_from(): lax.ppermute(lax.slice_in_dim(block, 0, width, axis=dim), axis, backward)  9.04 us
    reduce_sum x2, other arithmetic, block_mean(): fx = field.reshape(sx // 4, 4, sy, sz).sum(axis=1)  4.65 us
    select_n x1, other arithmetic, per_device(): fine = jnp.where(inside, fine + step, 0.0)  4.11 us
    slice x1, other arithmetic, shared_faces(): hy = jnp.pad(ly, ((0, 0), (0, 1), (0, 0)))[:, 1:]  4 us
    slice x6, local copies, waits for them, and re-layouts, packed_halo(): lax.slice_in_dim(f, f.shape[dim] - d, f.shape[dim], axis=dim)  3.6 us
  transfers between devices with their start and end apart: 12, of which 5 were waited for; matrix products, arithmetic and copies ran while one was open for 6% of the time, Pallas kernels for 0%

profile of v11, /device:TPU:34, one launch (start us, length us, event | category | flops | bytes accessed | tf_op | source)
XLA Modules:
  0.0 95.5 jit_solution(8464191939742797526)
XLA Ops:
  0.0 1.2 %fusion.228 = (f32[16,2,512]{2,1,0:T(2,128)S(1)}, f32[16,2,512]{2,1,0:T(2,128)S(1)}) fusion(f32[16,32,512]{2,1,0:T(8,128)} %param.3), kind=kLoop, calls=%fused_computation.370 | loop fusion | bytes 262144 | tf_op jit(solution)/shard_map/slice | solution.py:48
  1.2 1.3 %fusion.229 = (f32[16,3,512]{2,1,0:T(4,128)S(1)}, f32[16,3,512]{2,1,0:T(4,128)S(1)}, f32[16,3,512]{2,1,0:T(4,128)S(1)}, f32[16,3,512]{2,1,0:T(4,128)S(1)}) fusion(f32[16,32,512]{2,1,0:T(8,128)} %param.4, f32[16,32,512]{2,1,0:T(8,128)} %param.5), kind=kLoop, calls=%fused_computation.371 | loop fusion | bytes 786432 | tf_op jit(solution)/shard_map/slice | solution.py:48
  2.5 0.8 pad_maximum_fusion.3
  3.3 3.0 %collective-permute-start = (f32[16,8,512]{2,1,0:T(8,128)}, f32[16,8,512]{2,1,0:T(8,128)S(1)}, u32[]{:S(2)}, u32[]{:S(2)}) collective-permute-start(f32[16,8,512]{2,1,0:T(8,128)} %pad_maximum_fusion.3), channel_id=1, source_target_pairs={{0,1},{1,2},{2,3},{3,4},{4,5},{5,6},{6,7},{8,9},{9,10},{10,11},{11... | collective-permute-start | bytes 786440 | tf_op jit(solution)/shard_map/ppermute | solution.py:58
  6.4 0.8 pad_maximum_fusion.4
  7.1 2.8 %collective-permute-start.1 = (f32[16,8,512]{2,1,0:T(8,128)}, f32[16,8,512]{2,1,0:T(8,128)S(1)}, u32[]{:S(2)}, u32[]{:S(2)}) collective-permute-start(f32[16,8,512]{2,1,0:T(8,128)} %pad_maximum_fusion.4), channel_id=1, source_target_pairs={{1,0},{2,1},{3,2},{4,3},{5,4},{6,5},{7,6},{9,8},{10,9},{11,10},{12... | collective-permute-start | bytes 786440 | tf_op jit(solution)/shard_map/ppermute | solution.py:58
  10.0 1.0 %fusion.225 = (f32[2,32,512]{2,1,0:T(8,128)S(1)}, f32[2,32,512]{2,1,0:T(8,128)S(1)}) fusion(f32[16,32,512]{2,1,0:T(8,128)} %param.3), kind=kLoop, calls=%fused_computation.367 | loop fusion | bytes 524288 | tf_op jit(solution)/shard_map/slice | solution.py:48
  11.0 0.9 pad_maximum_fusion
  11.9 1.9 %collective-permute-start.3 = (f32[8,32,512]{2,1,0:T(8,128)}, f32[8,32,512]{2,1,0:T(8,128)}, u32[]{:S(2)}, u32[]{:S(2)}) collective-permute-start(f32[8,32,512]{2,1,0:T(8,128)} %pad_maximum_fusion), channel_id=1, source_target_pairs={{0,8},{8,16},{16,24},{24,32},{32,40},{40,48},{48,56},{56,64},{64,7... | collective-permute-start | bytes 1572872 | tf_op jit(solution)/shard_map/ppermute | solution.py:58
  13.8 0.8 pad_maximum_fusion.1
  14.6 6.0 %collective-permute-start.5 = (f32[8,32,512]{2,1,0:T(8,128)}, f32[8,32,512]{2,1,0:T(8,128)}, u32[]{:S(2)}, u32[]{:S(2)}) collective-permute-start(f32[8,32,512]{2,1,0:T(8,128)} %pad_maximum_fusion.1), channel_id=1, source_target_pairs={{8,0},{16,8},{24,16},{32,24},{40,32},{48,40},{56,48},{64,56},{72,6... | collective-permute-start | bytes 1572872 | tf_op jit(solution)/shard_map/ppermute | solution.py:58
  20.9 0.5 fusion.203
  21.6 1.9 %collective-permute-start.2 = (f32[3,16,512]{2,1,0:T(8,128)S(1)}, f32[3,16,512]{2,1,0:T(8,128)S(1)}, u32[]{:S(2)}, u32[]{:S(2)}) collective-permute-start(f32[3,16,512]{2,1,0:T(8,128)S(1)} %pad_maximum_fusion.5), channel_id=1, source_target_pairs={{0,8},{8,16},{16,24},{24,32},{32,40},{40,48},{48,56},{56,64},{64,7... | collective-permute-start | bytes 294920 | tf_op jit(solution)/shard_map/ppermute | solution.py:58
  23.6 6.0 %collective-permute-start.4 = (f32[3,16,512]{2,1,0:T(8,128)S(1)}, f32[3,16,512]{2,1,0:T(8,128)S(1)}, u32[]{:S(2)}, u32[]{:S(2)}) collective-permute-start(f32[3,16,512]{2,1,0:T(8,128)S(1)} %pad_maximum_fusion.6), channel_id=1, source_target_pairs={{8,0},{16,8},{24,16},{32,24},{40,32},{48,40},{56,48},{64,56},{72,6... | collective-permute-start | bytes 294920 | tf_op jit(solution)/shard_map/ppermute | solution.py:58
  29.7 0.3 collective-permute-done.2
  30.1 2.4 %collective-permute-done.4 = f32[3,16,512]{2,1,0:T(8,128)S(1)} collective-permute-done((f32[3,16,512]{2,1,0:T(8,128)S(1)}, f32[3,16,512]{2,1,0:T(8,128)S(1)}, u32[]{:S(2)}, u32[]{:S(2)}) %collective-permute-start.4) | collective-permute-done | bytes 98336 | tf_op jit(solution)/shard_map/ppermute | solution.py:58
  32.6 1.0 %fusion.231 = (f32[3,32,512]{2,1,0:T(8,128)S(1)}, f32[3,32,512]{2,1,0:T(8,128)S(1)}) fusion(f32[8,32,512]{2,1,0:T(8,128)} %collective-permute-done.3), kind=kLoop, calls=%fused_computation.373 | loop fusion | bytes 786432 | tf_op jit(solution)/shard_map/slice | solution.py:72
  33.6 1.0 %fusion.232 = (f32[3,32,512]{2,1,0:T(8,128)S(1)}, f32[3,32,512]{2,1,0:T(8,128)S(1)}) fusion(f32[8,32,512]{2,1,0:T(8,128)} %collective-permute-done.5), kind=kLoop, calls=%fused_computation.374 | loop fusion | bytes 786432 | tf_op jit(solution)/shard_map/slice | solution.py:74
  34.7 0.3 maximum_maximum_fusion.1
  35.0 0.3 maximum_maximum_fusion
  35.3 1.0 %slice.471 = f32[2,32,512]{2,1,0:T(8,128)S(1)} slice(f32[8,32,512]{2,1,0:T(8,128)} %collective-permute-done.3), slice={[0:2], [0:32], [0:512]} | slice | bytes 262144 | tf_op jit(solution)/shard_map/slice | solution.py:72
  36.3 0.9 slice.478
  37.2 0.5 fusion.48
  37.7 2.1 %divide_select_fusion.2 = (f32[22,38,512]{2,1,0:T(8,128)S(1)}, f32[22,38,512]{2,1,0:T(8,128)S(1)}, f32[22,38,512]{2,1,0:T(8,128)S(1)}) fusion(f32[22,38,512]{2,1,0:T(8,128)S(1)} %maximum_maximum_fusion), kind=kLoop, calls=%fused_computation.27 | loop fusion | flops 8560640 | bytes 6848512 | tf_op jit(solution)/shard_map/jit(_where)/select_n | solution.py:182
  39.8 4.1 %and_select_fusion.1 = (f32[22,38,512]{2,1,0:T(8,128)S(1)}, f32[22,38,512]{2,1,0:T(8,128)S(1)}) fusion(f32[22,38,512]{2,1,0:T(8,128)S(1)} %maximum_maximum_fusion.1, f32[22,38,512]{2,1,0:T(8,128)S(1)} %get-tuple-element.43, f32[22,38,512]{2,1,0:T(8,128)S(1)} %get-tuple-element.44, f32[22,38,512]{2,1,0:T(8,128)S(1)} %get-tuple-element.42, ...), kind=kLoop, calls=%fused_computation.29 | loop fusion | flops 12412928 | bytes 13697596 | tf_op jit(solution)/shard_map/jit(_where)/select_n | solution.py:227
  44.0 4.0 %pad_slice_fusion.23 = (f32[22,38,512]{2,1,0:T(8,128)S(1)}, f32[22,38,512]{2,1,0:T(8,128)S(1)}) fusion(f32[22,38,512]{2,1,0:T(8,128)S(1)} %get-tuple-element.44, f32[22,38,512]{2,1,0:T(8,128)S(1)} %get-tuple-element.32, f32[22,38,512]{2,1,0:T(8,128)S(1)} %get-tuple-element.33, f32[22,38,512]{2,1,0:T(8,128)S(1)} %get-tuple-element.43, ...), kind=kLoop, calls=%fused_computation.91 | loop fusion | flops 11984896 | bytes 13697084 | tf_op jit(solution)/shard_map/slice | solution.py:187
  48.0 3.1 %fusion.44 = (f32[22,38,512]{2,1,0:T(8,128)S(1)}, f32[22,38,512]{2,1,0:T(8,128)S(1)}, f32[22,38,512]{2,1,0:T(8,128)S(1)}, f32[22,38,512]{2,1,0:T(8,128)S(1)}, f3...) fusion(f32[22,38,512]{2,1,0:T(8,128)S(1)} %get-tuple-element.42, f32[22,38,512]{2,1,0:T(8,128)S(1)} %get-tuple-element.41), kind=kLoop, calls=%fused_computation.76 | loop fusion | flops 2140160 | bytes 13697024 | tf_op jit(solution)/shard_map/mul | solution.py:105
  51.1 4.6 %bitcast_reduce_fusion = f32[4,32,512]{2,1,0:T(8,128)S(1)} fusion(f32[22,38,512]{2,1,0:T(8,128)S(1)} %get-tuple-element.37, f32[22,38,512]{2,1,0:T(8,128)S(1)} %get-tuple-element.33, f32[22,38,512]{2,1,0:T(8,128)S(1)} %get-tuple-element.36, f32[22,38,512]{2,1,0:T(8,128)S(1)} %get-tuple-element.43, f32[22,38,512]{2,1,0:T(8,128)} %get-tuple-element.39, ...), kind=kLoop, calls=%fused_computation.162 | loop fusion | flops 3604480 | bytes 12845056 | tf_op jit(solution)/shard_map/reduce_sum | solution.py:117
  55.7 0.5 fusion.201
  56.3 6.4 %collective-permute-start.6 = (f32[2,4,8,128]{3,2,1,0:T(8,128)S(1)}, f32[2,4,8,128]{3,2,1,0:T(8,128)S(1)}, u32[]{:S(2)}, u32[]{:S(2)}) collective-permute-start(f32[2,4,8,128]{3,2,1,0:T(8,128)S(1)} %pad_maximum_fusion.7), channel_id=1, source_target_pairs={{0,16},{8,24},{16,32},{24,40},{32,48},{40,56},{48,64},{56,72},{64,... | collective-permute-start | bytes 98312 | tf_op jit(solution)/shard_map/ppermute | solution.py:25
  62.8 2.1 %collective-permute-start.7 = (f32[2,4,8,128]{3,2,1,0:T(8,128)S(1)}, f32[2,4,8,128]{3,2,1,0:T(8,128)S(1)}, u32[]{:S(2)}, u32[]{:S(2)}) collective-permute-start(f32[2,4,8,128]{3,2,1,0:T(8,128)S(1)} %pad_maximum_fusion.7), channel_id=1, source_target_pairs={{0,8},{8,16},{16,24},{24,32},{32,40},{40,48},{48,56},{56,64},{64,7... | collective-permute-start | bytes 98312 | tf_op jit(solution)/shard_map/ppermute | solution.py:25
  64.9 5.8 %collective-permute-start.8 = (f32[2,4,8,128]{3,2,1,0:T(8,128)S(1)}, f32[2,4,8,128]{3,2,1,0:T(8,128)S(1)}, u32[]{:S(2)}, u32[]{:S(2)}) collective-permute-start(f32[2,4,8,128]{3,2,1,0:T(8,128)S(1)} %pad_maximum_fusion.7), channel_id=1, source_target_pairs={{8,0},{16,8},{24,16},{32,24},{40,32},{48,40},{56,48},{64,56},{72,6... | collective-permute-start | bytes 98312 | tf_op jit(solution)/shard_map/ppermute | solution.py:26
  70.7 2.1 %collective-permute-start.9 = (f32[2,4,8,128]{3,2,1,0:T(8,128)S(1)}, f32[2,4,8,128]{3,2,1,0:T(8,128)S(1)}, u32[]{:S(2)}, u32[]{:S(2)}) collective-permute-start(f32[2,4,8,128]{3,2,1,0:T(8,128)S(1)} %pad_maximum_fusion.7), channel_id=1, source_target_pairs={{16,0},{24,8},{32,16},{40,24},{48,32},{56,40},{64,48},{72,56},{80,... | collective-permute-start | bytes 98312 | tf_op jit(solution)/shard_map/ppermute | solution.py:26
  73.0 5.1 %collective-permute-done.9 = f32[2,4,8,128]{3,2,1,0:T(8,128)S(1)} collective-permute-done((f32[2,4,8,128]{3,2,1,0:T(8,128)S(1)}, f32[2,4,8,128]{3,2,1,0:T(8,128)S(1)}, u32[]{:S(2)}, u32[]{:S(2)}) %collective-permute-start.9) | collective-permute-done | bytes 32800 | tf_op jit(solution)/shard_map/ppermute | solution.py:26
  78.1 4.8 %collective-permute-start.10 = (f32[2,20,8,128]{3,2,1,0:T(8,128)S(1)}, f32[2,20,8,128]{3,2,1,0:T(8,128)S(1)}, u32[]{:S(2)}, u32[]{:S(2)}) collective-permute-start(f32[2,20,8,128]{3,2,1,0:T(8,128)S(1)} %constant_dynamic-update-slice_fusion), channel_id=1, source_target_pairs={{0,1},{1,2},{2,3},{3,4},{4,5},{5,6},{6,7},{8,9},{9,10},{10,11},{11... | collective-permute-start | bytes 491528 | tf_op jit(solution)/shard_map/ppermute | solution.py:25
  82.8 2.1 %collective-permute-start.11 = (f32[2,20,8,128]{3,2,1,0:T(8,128)S(1)}, f32[2,20,8,128]{3,2,1,0:T(8,128)S(1)}, u32[]{:S(2)}, u32[]{:S(2)}) collective-permute-start(f32[2,20,8,128]{3,2,1,0:T(8,128)S(1)} %constant_dynamic-update-slice_fusion), channel_id=1, source_target_pairs={{1,0},{2,1},{3,2},{4,3},{5,4},{6,5},{7,6},{9,8},{10,9},{11,10},{12... | collective-permute-start | bytes 491528 | tf_op jit(solution)/shard_map/ppermute | solution.py:26
  85.0 2.0 %collective-permute-done.10 = f32[2,20,8,128]{3,2,1,0:T(8,128)S(1)} collective-permute-done((f32[2,20,8,128]{3,2,1,0:T(8,128)S(1)}, f32[2,20,8,128]{3,2,1,0:T(8,128)S(1)}, u32[]{:S(2)}, u32[]{:S(2)}) %collective-permute-start.10) | collective-permute-done | bytes 163872 | tf_op jit(solution)/shard_map/ppermute | solution.py:25
  87.0 3.9 %collective-permute-done.11 = f32[2,20,8,128]{3,2,1,0:T(8,128)S(1)} collective-permute-done((f32[2,20,8,128]{3,2,1,0:T(8,128)S(1)}, f32[2,20,8,128]{3,2,1,0:T(8,128)S(1)}, u32[]{:S(2)}, u32[]{:S(2)}) %collective-permute-start.11) | collective-permute-done | bytes 163872 | tf_op jit(solution)/shard_map/ppermute | solution.py:26
  91.0 0.5 fusion.186
  91.5 0.3 fusion.187
  91.9 0.3 multiply_add_fusion.4
  92.1 0.3 multiply_add_fusion.3
  92.4 0.3 multiply_add_fusion.2
  92.7 0.3 multiply_add_fusion.1
  93.0 0.3 multiply_add_fusion
  93.5 0.5 fusion.190
  94.0 0.3 convolution_bitcast_fusion
  94.3 1.2 %bitcast_add_fusion = f32[16,32,512]{2,1,0:T(8,128)} fusion(f32[22,38,512]{2,1,0:T(8,128)S(1)} %get-tuple-element.41, f32[4,32,512]{2,1,0:T(8,128)S(1)} %convolution_bitcast_fusion), kind=kLoop, calls=%fused_computation.161 | loop fusion | flops 262144 | bytes 2359296 | tf_op jit(solution)/shard_map/add | solution.py:234
  (53 shorter events, 1.0 us)
Async XLA Ops:
  0.0 10.0 %copy-start = (f32[16,32,512]{2,1,0:T(8,128)S(1)}, f32[16,32,512]{2,1,0:T(8,128)}, u32[]{:S(2)}) copy-start(f32[16,32,512]{2,1,0:T(8,128)} %param.4) | copy-start | bytes 3145732
  0.0 10.0 %copy-start.1 = (f32[16,32,512]{2,1,0:T(8,128)S(1)}, f32[16,32,512]{2,1,0:T(8,128)}, u32[]{:S(2)}) copy-start(f32[16,32,512]{2,1,0:T(8,128)} %param.5) | copy-start | bytes 3145732
  3.3 18.2 %collective-permute-start = (f32[16,8,512]{2,1,0:T(8,128)}, f32[16,8,512]{2,1,0:T(8,128)S(1)}, u32[]{:S(2)}, u32[]{:S(2)}) collective-permute-start(f32[16,8,512]{2,1,0:T(8,128)} %pad_maximum_fusion.3), channel_id=1, source_target_pairs={{0,1},{1,2},{2,3},{3,4},{4,5},{5,6},{6,7},{8,9},{9,10},{10,11},{11... | collective-permute-start | bytes 786440 | tf_op jit(solution)/shard_map/ppermute | solution.py:58
  7.1 14.4 %collective-permute-start.1 = (f32[16,8,512]{2,1,0:T(8,128)}, f32[16,8,512]{2,1,0:T(8,128)S(1)}, u32[]{:S(2)}, u32[]{:S(2)}) collective-permute-start(f32[16,8,512]{2,1,0:T(8,128)} %pad_maximum_fusion.4), channel_id=1, source_target_pairs={{1,0},{2,1},{3,2},{4,3},{5,4},{6,5},{7,6},{9,8},{10,9},{11,10},{12... | collective-permute-start | bytes 786440 | tf_op jit(solution)/shard_map/ppermute | solution.py:58
  11.9 20.7 %collective-permute-start.3 = (f32[8,32,512]{2,1,0:T(8,128)}, f32[8,32,512]{2,1,0:T(8,128)}, u32[]{:S(2)}, u32[]{:S(2)}) collective-permute-start(f32[8,32,512]{2,1,0:T(8,128)} %pad_maximum_fusion), channel_id=1, source_target_pairs={{0,8},{8,16},{16,24},{24,32},{32,40},{40,48},{48,56},{56,64},{64,7... | collective-permute-start | bytes 1572872 | tf_op jit(solution)/shard_map/ppermute | solution.py:58
  14.6 19.0 %collective-permute-start.5 = (f32[8,32,512]{2,1,0:T(8,128)}, f32[8,32,512]{2,1,0:T(8,128)}, u32[]{:S(2)}, u32[]{:S(2)}) collective-permute-start(f32[8,32,512]{2,1,0:T(8,128)} %pad_maximum_fusion.1), channel_id=1, source_target_pairs={{8,0},{16,8},{24,16},{32,24},{40,32},{48,40},{56,48},{64,56},{72,6... | collective-permute-start | bytes 1572872 | tf_op jit(solution)/shard_map/ppermute | solution.py:58
  21.5 13.1 %copy-start.3 = (f32[16,8,512]{2,1,0:T(8,128)}, f32[16,8,512]{2,1,0:T(8,128)S(1)}, u32[]{:S(2)}) copy-start(f32[16,8,512]{2,1,0:T(8,128)S(1)} %collective-permute-done) | copy-start | bytes 786436
  21.6 13.1 %copy-start.4 = (f32[16,8,512]{2,1,0:T(8,128)}, f32[16,8,512]{2,1,0:T(8,128)S(1)}, u32[]{:S(2)}) copy-start(f32[16,8,512]{2,1,0:T(8,128)S(1)} %collective-permute-done.1) | copy-start | bytes 786436
  21.6 8.4 %collective-permute-start.2 = (f32[3,16,512]{2,1,0:T(8,128)S(1)}, f32[3,16,512]{2,1,0:T(8,128)S(1)}, u32[]{:S(2)}, u32[]{:S(2)}) collective-permute-start(f32[3,16,512]{2,1,0:T(8,128)S(1)} %pad_maximum_fusion.5), channel_id=1, source_target_pairs={{0,8},{8,16},{16,24},{24,32},{32,40},{40,48},{48,56},{56,64},{64,7... | collective-permute-start | bytes 294920 | tf_op jit(solution)/shard_map/ppermute | solution.py:58
  23.6 9.0 %collective-permute-start.4 = (f32[3,16,512]{2,1,0:T(8,128)S(1)}, f32[3,16,512]{2,1,0:T(8,128)S(1)}, u32[]{:S(2)}, u32[]{:S(2)}) collective-permute-start(f32[3,16,512]{2,1,0:T(8,128)S(1)} %pad_maximum_fusion.6), channel_id=1, source_target_pairs={{8,0},{16,8},{24,16},{32,24},{40,32},{48,40},{56,48},{64,56},{72,6... | collective-permute-start | bytes 294920 | tf_op jit(solution)/shard_map/ppermute | solution.py:58
  35.0 2.2 %copy-start.2 = (f32[16,32,512]{2,1,0:T(8,128)S(1)}, f32[16,32,512]{2,1,0:T(8,128)}, u32[]{:S(2)}) copy-start(f32[16,32,512]{2,1,0:T(8,128)} %param.3) | copy-start | bytes 3145732
  35.0 2.2 %slice-start = ((f32[16,8,512]{2,1,0:T(8,128)}), f32[16,2,512]{2,1,0:T(2,128)S(1)}, s32[]{:S(2)}) async-start(f32[16,8,512]{2,1,0:T(8,128)} %copy-done.3), calls=%async_computation | async-start | bytes 131072 | tf_op jit(solution)/shard_map/slice | solution.py:73
  35.0 2.2 %slice-start.1 = ((f32[16,8,512]{2,1,0:T(8,128)}), f32[16,2,512]{2,1,0:T(2,128)S(1)}, s32[]{:S(2)}) async-start(f32[16,8,512]{2,1,0:T(8,128)} %copy-done.4), calls=%async_computation.1 | async-start | bytes 131072 | tf_op jit(solution)/shard_map/slice | solution.py:73
  56.3 16.6 %collective-permute-start.6 = (f32[2,4,8,128]{3,2,1,0:T(8,128)S(1)}, f32[2,4,8,128]{3,2,1,0:T(8,128)S(1)}, u32[]{:S(2)}, u32[]{:S(2)}) collective-permute-start(f32[2,4,8,128]{3,2,1,0:T(8,128)S(1)} %pad_maximum_fusion.7), channel_id=1, source_target_pairs={{0,16},{8,24},{16,32},{24,40},{32,48},{40,56},{48,64},{56,72},{64,... | collective-permute-start | bytes 98312 | tf_op jit(solution)/shard_map/ppermute | solution.py:25
  62.8 10.1 %collective-permute-start.7 = (f32[2,4,8,128]{3,2,1,0:T(8,128)S(1)}, f32[2,4,8,128]{3,2,1,0:T(8,128)S(1)}, u32[]{:S(2)}, u32[]{:S(2)}) collective-permute-start(f32[2,4,8,128]{3,2,1,0:T(8,128)S(1)} %pad_maximum_fusion.7), channel_id=1, source_target_pairs={{0,8},{8,16},{16,24},{24,32},{32,40},{40,48},{48,56},{56,64},{64,7... | collective-permute-start | bytes 98312 | tf_op jit(solution)/shard_map/ppermute | solution.py:25
  64.9 8.0 %collective-permute-start.8 = (f32[2,4,8,128]{3,2,1,0:T(8,128)S(1)}, f32[2,4,8,128]{3,2,1,0:T(8,128)S(1)}, u32[]{:S(2)}, u32[]{:S(2)}) collective-permute-start(f32[2,4,8,128]{3,2,1,0:T(8,128)S(1)} %pad_maximum_fusion.7), channel_id=1, source_target_pairs={{8,0},{16,8},{24,16},{32,24},{40,32},{48,40},{56,48},{64,56},{72,6... | collective-permute-start | bytes 98312 | tf_op jit(solution)/shard_map/ppermute | solution.py:26
  70.7 7.3 %collective-permute-start.9 = (f32[2,4,8,128]{3,2,1,0:T(8,128)S(1)}, f32[2,4,8,128]{3,2,1,0:T(8,128)S(1)}, u32[]{:S(2)}, u32[]{:S(2)}) collective-permute-start(f32[2,4,8,128]{3,2,1,0:T(8,128)S(1)} %pad_maximum_fusion.7), channel_id=1, source_target_pairs={{16,0},{24,8},{32,16},{40,24},{48,32},{56,40},{64,48},{72,56},{80,... | collective-permute-start | bytes 98312 | tf_op jit(solution)/shard_map/ppermute | solution.py:26
  78.1 9.0 %collective-permute-start.10 = (f32[2,20,8,128]{3,2,1,0:T(8,128)S(1)}, f32[2,20,8,128]{3,2,1,0:T(8,128)S(1)}, u32[]{:S(2)}, u32[]{:S(2)}) collective-permute-start(f32[2,20,8,128]{3,2,1,0:T(8,128)S(1)} %constant_dynamic-update-slice_fusion), channel_id=1, source_target_pairs={{0,1},{1,2},{2,3},{3,4},{4,5},{5,6},{6,7},{8,9},{9,10},{10,11},{11... | collective-permute-start | bytes 491528 | tf_op jit(solution)/shard_map/ppermute | solution.py:25
  82.8 8.1 %collective-permute-start.11 = (f32[2,20,8,128]{3,2,1,0:T(8,128)S(1)}, f32[2,20,8,128]{3,2,1,0:T(8,128)S(1)}, u32[]{:S(2)}, u32[]{:S(2)}) collective-permute-start(f32[2,20,8,128]{3,2,1,0:T(8,128)S(1)} %constant_dynamic-update-slice_fusion), channel_id=1, source_target_pairs={{1,0},{2,1},{3,2},{4,3},{5,4},{6,5},{7,6},{9,8},{10,9},{11,10},{12... | collective-permute-start | bytes 491528 | tf_op jit(solution)/shard_map/ppermute | solution.py:26

commit v12 on v11

--- a/solution.py
+++ b/solution.py
@@ -139,8 +139,8 @@
     depth = CHEB
     cx, cy, cz = rhs_c.shape
     both = jnp.stack([b_c, rhs_c])
+    both = deep_extend(both, "group", 2, depth)
     both = deep_extend(both, "box", 1, depth)
-    both = deep_extend(both, "group", 2, depth)
     b_ext, rhs_ext = both[0], both[1]
     totals = (cx * lax.axis_size("box"), cy * lax.axis_size("group"))
     inside = inside_mask(b_ext.shape, depth, totals)

time: 96.4 us -> 98.7 us (1.024)
  local copies, waits for them, and re-layouts: 7.8 us -> 12.5 us
  waiting for transfers between devices: 13.8 us -> 9.9 us
    ppermute x6, waiting for transfers between devices: 2.75 us -> 0.02 us  [send(): return lax.ppermute(msg, axis, pairs)]
    ppermute x3, waiting for transfers between devices: 2.05 us -> 0.01 us  [halo_from(): lax.ppermute(lax.slice_in_dim(block, n - width, n, axis=dim), axis, forward)]
    slice x3 -> x2, local copies, waits for them, and re-layouts: 0.06 us -> 2.06 us  [packed_halo(): yl[:, ys]]
    slice x3 -> x2, local copies, waits for them, and re-layouts: 0.06 us -> 2.06 us  [packed_halo(): yh[:, ys]]
  transfers between devices with their start and end apart: 12 -> 12, of which waited for: 5 -> 2; matrix products, arithmetic and copies ran while one was open for 6% -> 11% of each run, Pallas kernels for 0% -> 0%
where the time goes in v12:
time: 98.7 us; the launch traced here: 97.8 us
  starting transfers between devices  46 us (47%)
  other arithmetic  26.9 us (27%)
  local copies, waits for them, and re-layouts  12.5 us (13%)
  waiting for transfers between devices  9.9 us (10%)
  matrix products  2.05 us (2%)
    ppermute x6, starting transfers between devices, send(): return lax.ppermute(msg, axis, pairs)  22.4 us
    ppermute x3, starting transfers between devices, halo_from(): lax.ppermute(lax.slice_in_dim(block, n - width, n, axis=dim), axis, forward)  12.8 us
    ppermute x3, starting transfers between devices, halo_from(): lax.ppermute(lax.slice_in_dim(block, 0, width, axis=dim), axis, backward)  10.8 us
    ppermute x3, waiting for transfers between devices, halo_from(): lax.ppermute(lax.slice_in_dim(block, 0, width, axis=dim), axis, backward)  9.88 us
    reduce_sum x2, other arithmetic, block_mean(): fx = field.reshape(sx // 4, 4, sy, sz).sum(axis=1)  5.04 us
    slice x6, local copies, waits for them, and re-layouts, packed_halo(): lax.slice_in_dim(f, f.shape[dim] - d, f.shape[dim], axis=dim)  4.36 us
    select_n x1, other arithmetic, per_device(): fine = jnp.where(inside, fine + step, 0.0)  4.11 us
    slice x1, other arithmetic, shared_faces(): hy = jnp.pad(ly, ((0, 0), (0, 1), (0, 0)))[:, 1:]  4 us
  transfers between devices with their start and end apart: 12, of which 2 were waited for; matrix products, arithmetic and copies ran while one was open for 11% of the time, Pallas kernels for 0%

profile of v12, /device:TPU:34, one launch (start us, length us, event | category | flops | bytes accessed | tf_op | source)
XLA Modules:
  0.0 97.8 jit_solution(14984299683471161330)
XLA Ops:
  0.0 1.2 %fusion.229 = (f32[16,2,512]{2,1,0:T(2,128)S(1)}, f32[16,2,512]{2,1,0:T(2,128)S(1)}) fusion(f32[16,32,512]{2,1,0:T(8,128)} %param.3), kind=kLoop, calls=%fused_computation.373 | loop fusion | bytes 262144 | tf_op jit(solution)/shard_map/slice | solution.py:48
  1.2 1.4 %fusion.230 = (f32[16,3,512]{2,1,0:T(4,128)S(1)}, f32[16,3,512]{2,1,0:T(4,128)S(1)}, f32[16,3,512]{2,1,0:T(4,128)S(1)}, f32[16,3,512]{2,1,0:T(4,128)S(1)}) fusion(f32[16,32,512]{2,1,0:T(8,128)} %param.4, f32[16,32,512]{2,1,0:T(8,128)} %param.5), kind=kLoop, calls=%fused_computation.374 | loop fusion | bytes 786432 | tf_op jit(solution)/shard_map/slice | solution.py:48
  2.6 0.8 pad_maximum_fusion.2
  3.4 3.0 %collective-permute-start = (f32[16,8,512]{2,1,0:T(8,128)}, f32[16,8,512]{2,1,0:T(8,128)}, u32[]{:S(2)}, u32[]{:S(2)}) collective-permute-start(f32[16,8,512]{2,1,0:T(8,128)} %pad_maximum_fusion.2), channel_id=1, source_target_pairs={{0,1},{1,2},{2,3},{3,4},{4,5},{5,6},{6,7},{8,9},{9,10},{10,11},{11... | collective-permute-start | bytes 786440 | tf_op jit(solution)/shard_map/ppermute | solution.py:58
  6.5 0.8 pad_maximum_fusion.3
  7.3 3.5 %collective-permute-start.1 = (f32[16,8,512]{2,1,0:T(8,128)}, f32[16,8,512]{2,1,0:T(8,128)}, u32[]{:S(2)}, u32[]{:S(2)}) collective-permute-start(f32[16,8,512]{2,1,0:T(8,128)} %pad_maximum_fusion.3), channel_id=1, source_target_pairs={{1,0},{2,1},{3,2},{4,3},{5,4},{6,5},{7,6},{9,8},{10,9},{11,10},{12... | collective-permute-start | bytes 786440 | tf_op jit(solution)/shard_map/ppermute | solution.py:58
  10.9 0.8 pad_maximum_fusion
  11.7 1.9 %collective-permute-start.3 = (f32[8,32,512]{2,1,0:T(8,128)}, f32[8,32,512]{2,1,0:T(8,128)}, u32[]{:S(2)}, u32[]{:S(2)}) collective-permute-start(f32[8,32,512]{2,1,0:T(8,128)} %pad_maximum_fusion), channel_id=1, source_target_pairs={{0,8},{8,16},{16,24},{24,32},{32,40},{40,48},{48,56},{56,64},{64,7... | collective-permute-start | bytes 1572872 | tf_op jit(solution)/shard_map/ppermute | solution.py:58
  13.7 0.8 pad_maximum_fusion.1
  14.5 6.0 %collective-permute-start.5 = (f32[8,32,512]{2,1,0:T(8,128)}, f32[8,32,512]{2,1,0:T(8,128)}, u32[]{:S(2)}, u32[]{:S(2)}) collective-permute-start(f32[8,32,512]{2,1,0:T(8,128)} %pad_maximum_fusion.1), channel_id=1, source_target_pairs={{8,0},{16,8},{24,16},{32,24},{40,32},{48,40},{56,48},{64,56},{72,6... | collective-permute-start | bytes 1572872 | tf_op jit(solution)/shard_map/ppermute | solution.py:58
  20.7 0.5 fusion.204
  21.4 0.8 fusion.236
  22.2 0.8 fusion.237
  23.1 1.9 %collective-permute-start.2 = (f32[3,16,512]{2,1,0:T(8,128)S(1)}, f32[3,16,512]{2,1,0:T(8,128)S(1)}, u32[]{:S(2)}, u32[]{:S(2)}) collective-permute-start(f32[3,16,512]{2,1,0:T(8,128)S(1)} %pad_maximum_fusion.8), channel_id=1, source_target_pairs={{0,8},{8,16},{16,24},{24,32},{32,40},{40,48},{48,56},{56,64},{64,7... | collective-permute-start | bytes 294920 | tf_op jit(solution)/shard_map/ppermute | solution.py:58
  25.0 6.0 %collective-permute-start.4 = (f32[3,16,512]{2,1,0:T(8,128)S(1)}, f32[3,16,512]{2,1,0:T(8,128)S(1)}, u32[]{:S(2)}, u32[]{:S(2)}) collective-permute-start(f32[3,16,512]{2,1,0:T(8,128)S(1)} %pad_maximum_fusion.9), channel_id=1, source_target_pairs={{8,0},{16,8},{24,16},{32,24},{40,32},{48,40},{56,48},{64,56},{72,6... | collective-permute-start | bytes 294920 | tf_op jit(solution)/shard_map/ppermute | solution.py:58
  31.1 1.1 %fusion.234 = (f32[16,3,512]{2,1,0:T(4,128)S(1)}, f32[16,3,512]{2,1,0:T(4,128)S(1)}) fusion(f32[16,8,512]{2,1,0:T(8,128)} %collective-permute-done), kind=kLoop, calls=%fused_computation.378 | loop fusion | bytes 393216 | tf_op jit(solution)/shard_map/slice | solution.py:73
  32.2 1.1 %fusion.235 = (f32[16,3,512]{2,1,0:T(4,128)S(1)}, f32[16,3,512]{2,1,0:T(4,128)S(1)}) fusion(f32[16,8,512]{2,1,0:T(8,128)} %collective-permute-done.1), kind=kLoop, calls=%fused_computation.379 | loop fusion | bytes 393216 | tf_op jit(solution)/shard_map/slice | solution.py:73
  33.3 1.0 slice.473
  34.2 1.0 slice.474
  35.3 1.0 %fusion.232 = (f32[3,32,512]{2,1,0:T(8,128)S(1)}, f32[3,32,512]{2,1,0:T(8,128)S(1)}) fusion(f32[8,32,512]{2,1,0:T(8,128)} %collective-permute-done.3), kind=kLoop, calls=%fused_computation.376 | loop fusion | bytes 786432 | tf_op jit(solution)/shard_map/slice | solution.py:72
  36.4 1.0 %fusion.233 = (f32[3,32,512]{2,1,0:T(8,128)S(1)}, f32[3,32,512]{2,1,0:T(8,128)S(1)}) fusion(f32[8,32,512]{2,1,0:T(8,128)} %collective-permute-done.5), kind=kLoop, calls=%fused_computation.377 | loop fusion | bytes 786432 | tf_op jit(solution)/shard_map/slice | solution.py:74
  37.4 0.3 maximum_maximum_fusion.1
  37.7 0.3 maximum_maximum_fusion
  38.0 0.9 slice.471
  39.0 0.9 slice.478
  39.9 0.5 fusion.48
  40.4 2.1 %divide_select_fusion.2 = (f32[22,38,512]{2,1,0:T(8,128)S(1)}, f32[22,38,512]{2,1,0:T(8,128)S(1)}, f32[22,38,512]{2,1,0:T(8,128)S(1)}) fusion(f32[22,38,512]{2,1,0:T(8,128)S(1)} %maximum_maximum_fusion), kind=kLoop, calls=%fused_computation.27 | loop fusion | flops 8560640 | bytes 6848512 | tf_op jit(solution)/shard_map/jit(_where)/select_n | solution.py:182
  42.5 4.1 %and_select_fusion.1 = (f32[22,38,512]{2,1,0:T(8,128)S(1)}, f32[22,38,512]{2,1,0:T(8,128)S(1)}) fusion(f32[22,38,512]{2,1,0:T(8,128)S(1)} %maximum_maximum_fusion.1, f32[22,38,512]{2,1,0:T(8,128)S(1)} %get-tuple-element.43, f32[22,38,512]{2,1,0:T(8,128)S(1)} %get-tuple-element.44, f32[22,38,512]{2,1,0:T(8,128)S(1)} %get-tuple-element.42, ...), kind=kLoop, calls=%fused_computation.29 | loop fusion | flops 12412928 | bytes 13697596 | tf_op jit(solution)/shard_map/jit(_where)/select_n | solution.py:227
  46.6 4.0 %pad_slice_fusion.23 = (f32[22,38,512]{2,1,0:T(8,128)S(1)}, f32[22,38,512]{2,1,0:T(8,128)S(1)}) fusion(f32[22,38,512]{2,1,0:T(8,128)S(1)} %get-tuple-element.44, f32[22,38,512]{2,1,0:T(8,128)S(1)} %get-tuple-element.32, f32[22,38,512]{2,1,0:T(8,128)S(1)} %get-tuple-element.33, f32[22,38,512]{2,1,0:T(8,128)S(1)} %get-tuple-element.43, ...), kind=kLoop, calls=%fused_computation.91 | loop fusion | flops 11984896 | bytes 13697084 | tf_op jit(solution)/shard_map/slice | solution.py:187
  50.6 3.5 %fusion.44 = (f32[22,38,512]{2,1,0:T(8,128)S(1)}, f32[22,38,512]{2,1,0:T(8,128)S(1)}, f32[22,38,512]{2,1,0:T(8,128)S(1)}, f32[22,38,512]{2,1,0:T(8,128)S(1)}, f32[22,38,512]{2,1,0:T(8,128)}, /*index=5*/f32[22,38,512]{2,1,0:T(8,128)}) fusion(f32[22,38,512]{2,1,0:T(8,128)S(1)} %get-tuple-element.42, f32[22,38,512]{2,1,0:T(8,128)S(1)} %get-tuple-element.41), kind=kLoop, calls=%fused_computation.76 | loop fusion | flops 2140160 | bytes 13697024 | tf_op jit(solution)/shard_map/mul | solution.py:105
  54.1 5.0 %bitcast_reduce_fusion = f32[4,32,512]{2,1,0:T(8,128)S(1)} fusion(f32[22,38,512]{2,1,0:T(8,128)S(1)} %get-tuple-element.37, f32[22,38,512]{2,1,0:T(8,128)S(1)} %get-tuple-element.33, f32[22,38,512]{2,1,0:T(8,128)S(1)} %get-tuple-element.36, f32[22,38,512]{2,1,0:T(8,128)S(1)} %get-tuple-element.43, f32[22,38,512]{2,1,0:T(8,128)} %get-tuple-element.39, ...), kind=kLoop, calls=%fused_computation.162 | loop fusion | flops 3604480 | bytes 12845056 | tf_op jit(solution)/shard_map/reduce_sum | solution.py:117
  59.1 0.5 fusion.202
  59.7 3.2 %collective-permute-start.6 = (f32[2,4,8,128]{3,2,1,0:T(8,128)S(1)}, f32[2,4,8,128]{3,2,1,0:T(8,128)S(1)}, u32[]{:S(2)}, u32[]{:S(2)}) collective-permute-start(f32[2,4,8,128]{3,2,1,0:T(8,128)S(1)} %pad_maximum_fusion.10), channel_id=1, source_target_pairs={{0,1},{1,2},{2,3},{3,4},{4,5},{5,6},{6,7},{8,9},{9,10},{10,11},{11... | collective-permute-start | bytes 98312 | tf_op jit(solution)/shard_map/ppermute | solution.py:25
  62.9 2.6 %collective-permute-start.7 = (f32[2,4,8,128]{3,2,1,0:T(8,128)S(1)}, f32[2,4,8,128]{3,2,1,0:T(8,128)S(1)}, u32[]{:S(2)}, u32[]{:S(2)}) collective-permute-start(f32[2,4,8,128]{3,2,1,0:T(8,128)S(1)} %pad_maximum_fusion.10), channel_id=1, source_target_pairs={{1,0},{2,1},{3,2},{4,3},{5,4},{6,5},{7,6},{9,8},{10,9},{11,10},{12... | collective-permute-start | bytes 98312 | tf_op jit(solution)/shard_map/ppermute | solution.py:26
  65.6 4.1 %collective-permute-done.7 = f32[2,4,8,128]{3,2,1,0:T(8,128)S(1)} collective-permute-done((f32[2,4,8,128]{3,2,1,0:T(8,128)S(1)}, f32[2,4,8,128]{3,2,1,0:T(8,128)S(1)}, u32[]{:S(2)}, u32[]{:S(2)}) %collective-permute-start.7) | collective-permute-done | bytes 32800 | tf_op jit(solution)/shard_map/ppermute | solution.py:26
  69.7 7.7 %collective-permute-start.8 = (f32[2,4,24,128]{3,2,1,0:T(8,128)S(1)}, f32[2,4,24,128]{3,2,1,0:T(8,128)S(1)}, u32[]{:S(2)}, u32[]{:S(2)}) collective-permute-start(f32[2,4,24,128]{3,2,1,0:T(8,128)S(1)} %pad_maximum_fusion.5), channel_id=1, source_target_pairs={{0,16},{8,24},{16,32},{24,40},{32,48},{40,56},{48,64},{56,72},{64,... | collective-permute-start | bytes 294920 | tf_op jit(solution)/shard_map/ppermute | solution.py:25
  77.3 1.9 %collective-permute-start.9 = (f32[2,4,24,128]{3,2,1,0:T(8,128)S(1)}, f32[2,4,24,128]{3,2,1,0:T(8,128)S(1)}, u32[]{:S(2)}, u32[]{:S(2)}) collective-permute-start(f32[2,4,24,128]{3,2,1,0:T(8,128)S(1)} %pad_maximum_fusion.5), channel_id=1, source_target_pairs={{0,8},{8,16},{16,24},{24,32},{32,40},{40,48},{48,56},{56,64},{64,7... | collective-permute-start | bytes 294920 | tf_op jit(solution)/shard_map/ppermute | solution.py:25
  79.3 6.0 %collective-permute-start.10 = (f32[2,4,24,128]{3,2,1,0:T(8,128)S(1)}, f32[2,4,24,128]{3,2,1,0:T(8,128)S(1)}, u32[]{:S(2)}, u32[]{:S(2)}) collective-permute-start(f32[2,4,24,128]{3,2,1,0:T(8,128)S(1)} %pad_maximum_fusion.5), channel_id=1, source_target_pairs={{8,0},{16,8},{24,16},{32,24},{40,32},{48,40},{56,48},{64,56},{72,6... | collective-permute-start | bytes 294920 | tf_op jit(solution)/shard_map/ppermute | solution.py:26
  85.3 2.1 %collective-permute-start.11 = (f32[2,4,24,128]{3,2,1,0:T(8,128)S(1)}, f32[2,4,24,128]{3,2,1,0:T(8,128)S(1)}, u32[]{:S(2)}, u32[]{:S(2)}) collective-permute-start(f32[2,4,24,128]{3,2,1,0:T(8,128)S(1)} %pad_maximum_fusion.5), channel_id=1, source_target_pairs={{16,0},{24,8},{32,16},{40,24},{48,32},{56,40},{64,48},{72,56},{80,... | collective-permute-start | bytes 294920 | tf_op jit(solution)/shard_map/ppermute | solution.py:26
  87.5 5.8 %collective-permute-done.11 = f32[2,4,24,128]{3,2,1,0:T(8,128)S(1)} collective-permute-done((f32[2,4,24,128]{3,2,1,0:T(8,128)S(1)}, f32[2,4,24,128]{3,2,1,0:T(8,128)S(1)}, u32[]{:S(2)}, u32[]{:S(2)}) %collective-permute-start.11) | collective-permute-done | bytes 98336 | tf_op jit(solution)/shard_map/ppermute | solution.py:26
  93.4 0.5 fusion.186
  93.9 0.3 fusion.187
  94.5 0.3 multiply_add_fusion.3
  94.8 0.3 multiply_add_fusion.2
  95.3 0.3 multiply_add_fusion
  95.9 0.5 fusion.191
  96.3 0.3 convolution_bitcast_fusion
  96.6 1.2 %bitcast_add_fusion = f32[16,32,512]{2,1,0:T(8,128)} fusion(f32[22,38,512]{2,1,0:T(8,128)S(1)} %get-tuple-element.41, f32[4,32,512]{2,1,0:T(8,128)S(1)} %convolution_bitcast_fusion), kind=kLoop, calls=%fused_computation.161 | loop fusion | flops 262144 | bytes 2359296 | tf_op jit(solution)/shard_map/add | solution.py:234
  (47 shorter events, 1.5 us)
Async XLA Ops:
  0.0 10.8 %copy-start = (f32[16,32,512]{2,1,0:T(8,128)S(1)}, f32[16,32,512]{2,1,0:T(8,128)}, u32[]{:S(2)}) copy-start(f32[16,32,512]{2,1,0:T(8,128)} %param.4) | copy-start | bytes 3145732
  0.0 10.8 %copy-start.1 = (f32[16,32,512]{2,1,0:T(8,128)S(1)}, f32[16,32,512]{2,1,0:T(8,128)}, u32[]{:S(2)}) copy-start(f32[16,32,512]{2,1,0:T(8,128)} %param.5) | copy-start | bytes 3145732
  1.2 9.6 %copy-start.2 = (f32[16,32,512]{2,1,0:T(8,128)S(1)}, f32[16,32,512]{2,1,0:T(8,128)}, u32[]{:S(2)}) copy-start(f32[16,32,512]{2,1,0:T(8,128)} %param.3) | copy-start | bytes 3145732
  3.4 18.0 %collective-permute-start = (f32[16,8,512]{2,1,0:T(8,128)}, f32[16,8,512]{2,1,0:T(8,128)}, u32[]{:S(2)}, u32[]{:S(2)}) collective-permute-start(f32[16,8,512]{2,1,0:T(8,128)} %pad_maximum_fusion.2), channel_id=1, source_target_pairs={{0,1},{1,2},{2,3},{3,4},{4,5},{5,6},{6,7},{8,9},{9,10},{10,11},{11... | collective-permute-start | bytes 786440 | tf_op jit(solution)/shard_map/ppermute | solution.py:58
  7.3 15.0 %collective-permute-start.1 = (f32[16,8,512]{2,1,0:T(8,128)}, f32[16,8,512]{2,1,0:T(8,128)}, u32[]{:S(2)}, u32[]{:S(2)}) collective-permute-start(f32[16,8,512]{2,1,0:T(8,128)} %pad_maximum_fusion.3), channel_id=1, source_target_pairs={{1,0},{2,1},{3,2},{4,3},{5,4},{6,5},{7,6},{9,8},{10,9},{11,10},{12... | collective-permute-start | bytes 786440 | tf_op jit(solution)/shard_map/ppermute | solution.py:58
  11.7 23.6 %collective-permute-start.3 = (f32[8,32,512]{2,1,0:T(8,128)}, f32[8,32,512]{2,1,0:T(8,128)}, u32[]{:S(2)}, u32[]{:S(2)}) collective-permute-start(f32[8,32,512]{2,1,0:T(8,128)} %pad_maximum_fusion), channel_id=1, source_target_pairs={{0,8},{8,16},{16,24},{24,32},{32,40},{40,48},{48,56},{56,64},{64,7... | collective-permute-start | bytes 1572872 | tf_op jit(solution)/shard_map/ppermute | solution.py:58
  14.5 21.9 %collective-permute-start.5 = (f32[8,32,512]{2,1,0:T(8,128)}, f32[8,32,512]{2,1,0:T(8,128)}, u32[]{:S(2)}, u32[]{:S(2)}) collective-permute-start(f32[8,32,512]{2,1,0:T(8,128)} %pad_maximum_fusion.1), channel_id=1, source_target_pairs={{8,0},{16,8},{24,16},{32,24},{40,32},{48,40},{56,48},{64,56},{72,6... | collective-permute-start | bytes 1572872 | tf_op jit(solution)/shard_map/ppermute | solution.py:58
  23.1 12.1 %collective-permute-start.2 = (f32[3,16,512]{2,1,0:T(8,128)S(1)}, f32[3,16,512]{2,1,0:T(8,128)S(1)}, u32[]{:S(2)}, u32[]{:S(2)}) collective-permute-start(f32[3,16,512]{2,1,0:T(8,128)S(1)} %pad_maximum_fusion.8), channel_id=1, source_target_pairs={{0,8},{8,16},{16,24},{24,32},{32,40},{40,48},{48,56},{56,64},{64,7... | collective-permute-start | bytes 294920 | tf_op jit(solution)/shard_map/ppermute | solution.py:58
  25.0 10.2 %collective-permute-start.4 = (f32[3,16,512]{2,1,0:T(8,128)S(1)}, f32[3,16,512]{2,1,0:T(8,128)S(1)}, u32[]{:S(2)}, u32[]{:S(2)}) collective-permute-start(f32[3,16,512]{2,1,0:T(8,128)S(1)} %pad_maximum_fusion.9), channel_id=1, source_target_pairs={{8,0},{16,8},{24,16},{32,24},{40,32},{48,40},{56,48},{64,56},{72,6... | collective-permute-start | bytes 294920 | tf_op jit(solution)/shard_map/ppermute | solution.py:58
  59.7 5.9 %collective-permute-start.6 = (f32[2,4,8,128]{3,2,1,0:T(8,128)S(1)}, f32[2,4,8,128]{3,2,1,0:T(8,128)S(1)}, u32[]{:S(2)}, u32[]{:S(2)}) collective-permute-start(f32[2,4,8,128]{3,2,1,0:T(8,128)S(1)} %pad_maximum_fusion.10), channel_id=1, source_target_pairs={{0,1},{1,2},{2,3},{3,4},{4,5},{5,6},{6,7},{8,9},{9,10},{10,11},{11... | collective-permute-start | bytes 98312 | tf_op jit(solution)/shard_map/ppermute | solution.py:25
  62.9 6.7 %collective-permute-start.7 = (f32[2,4,8,128]{3,2,1,0:T(8,128)S(1)}, f32[2,4,8,128]{3,2,1,0:T(8,128)S(1)}, u32[]{:S(2)}, u32[]{:S(2)}) collective-permute-start(f32[2,4,8,128]{3,2,1,0:T(8,128)S(1)} %pad_maximum_fusion.10), channel_id=1, source_target_pairs={{1,0},{2,1},{3,2},{4,3},{5,4},{6,5},{7,6},{9,8},{10,9},{11,10},{12... | collective-permute-start | bytes 98312 | tf_op jit(solution)/shard_map/ppermute | solution.py:26
  69.7 17.8 %collective-permute-start.8 = (f32[2,4,24,128]{3,2,1,0:T(8,128)S(1)}, f32[2,4,24,128]{3,2,1,0:T(8,128)S(1)}, u32[]{:S(2)}, u32[]{:S(2)}) collective-permute-start(f32[2,4,24,128]{3,2,1,0:T(8,128)S(1)} %pad_maximum_fusion.5), channel_id=1, source_target_pairs={{0,16},{8,24},{16,32},{24,40},{32,48},{40,56},{48,64},{56,72},{64,... | collective-permute-start | bytes 294920 | tf_op jit(solution)/shard_map/ppermute | solution.py:25
  77.3 10.1 %collective-permute-start.9 = (f32[2,4,24,128]{3,2,1,0:T(8,128)S(1)}, f32[2,4,24,128]{3,2,1,0:T(8,128)S(1)}, u32[]{:S(2)}, u32[]{:S(2)}) collective-permute-start(f32[2,4,24,128]{3,2,1,0:T(8,128)S(1)} %pad_maximum_fusion.5), channel_id=1, source_target_pairs={{0,8},{8,16},{16,24},{24,32},{32,40},{40,48},{48,56},{56,64},{64,7... | collective-permute-start | bytes 294920 | tf_op jit(solution)/shard_map/ppermute | solution.py:25
  79.3 8.2 %collective-permute-start.10 = (f32[2,4,24,128]{3,2,1,0:T(8,128)S(1)}, f32[2,4,24,128]{3,2,1,0:T(8,128)S(1)}, u32[]{:S(2)}, u32[]{:S(2)}) collective-permute-start(f32[2,4,24,128]{3,2,1,0:T(8,128)S(1)} %pad_maximum_fusion.5), channel_id=1, source_target_pairs={{8,0},{16,8},{24,16},{32,24},{40,32},{48,40},{56,48},{64,56},{72,6... | collective-permute-start | bytes 294920 | tf_op jit(solution)/shard_map/ppermute | solution.py:26
  85.3 8.0 %collective-permute-start.11 = (f32[2,4,24,128]{3,2,1,0:T(8,128)S(1)}, f32[2,4,24,128]{3,2,1,0:T(8,128)S(1)}, u32[]{:S(2)}, u32[]{:S(2)}) collective-permute-start(f32[2,4,24,128]{3,2,1,0:T(8,128)S(1)} %pad_maximum_fusion.5), channel_id=1, source_target_pairs={{16,0},{24,8},{32,16},{40,24},{48,32},{56,40},{64,48},{72,56},{80,... | collective-permute-start | bytes 294920 | tf_op jit(solution)/shard_map/ppermute | solution.py:26

commit v13 on v11

--- a/solution.py
+++ b/solution.py
@@ -225,9 +225,18 @@
     for sweep in range(SWEEPS):
         step = 2.0 / 3.0 * (rhs_e - apply_op(fine, padded_neighbours(jnp.pad(fine, 1)), coefs)) / diag
         fine = jnp.where(inside, fine + step, 0.0)
-    res = rhs_e - apply_op(fine, padded_neighbours(jnp.pad(fine, 1)), coefs)
     own = (slice(depth, depth + sx), slice(depth, depth + sy))
-    fine, res = fine[own], res[own]
+    core = fine[own]
+    nears = [
+        fine[depth - 1:depth - 1 + sx, depth:depth + sy],
+        fine[depth + 1:depth + 1 + sx, depth:depth + sy],
+        fine[depth:depth + sx, depth - 1:depth - 1 + sy],
+        fine[depth:depth + sx, depth + 1:depth + 1 + sy],
+        shift_z(core, -1),
+        shift_z(core, 1),
+    ]
+    res = right_side - apply_op(core, nears, [c[own] for c in coefs])
+    fine, res = lax.optimization_barrier((core, res))
     coarse_rhs = block_mean(res)
     coarse_b = block_mean(inv_density)
     corr = chebyshev_local(coarse_rhs, coarse_b)

time: 96.4 us -> 93.8 us (0.973)
  other arithmetic: 26.1 us -> 20.1 us
  local copies, waits for them, and re-layouts: 7.8 us -> 13 us
  waiting for transfers between devices: 13.8 us -> 11.3 us
    reduce_sum x2, other arithmetic: 4.65 us -> 0.17 us  [block_mean(): fx = field.reshape(sx // 4, 4, sy, sz).sum(axis=1)]
    slice x1 -> x0, other arithmetic: 4 us -> none  [shared_faces(): hy = jnp.pad(ly, ((0, 0), (0, 1), (0, 0)))[:, 1:]]
    select_n x1 -> x2, other arithmetic: 4.11 us -> 7.91 us  [per_device(): fine = jnp.where(inside, fine + step, 0.0)]
    mul x1 -> x0, other arithmetic: 3.12 us -> none  [apply_op(): total = total + coef * (field - near)]
    ppermute x6, waiting for transfers between devices: 2.75 us -> 0.02 us  [send(): return lax.ppermute(msg, axis, pairs)]
    slice x3 -> x2, local copies, waits for them, and re-layouts: 0.06 us -> 2.06 us  [packed_halo(): yl[:, ys]]
    slice x3 -> x2, local copies, waits for them, and re-layouts: 0.06 us -> 2.06 us  [packed_halo(): yh[:, ys]]
    sub x0 -> x1, other arithmetic: none -> 1.8 us  [per_device(): res = right_side - apply_op(core, nears, [c[own] for c in coefs])]
  transfers between devices with their start and end apart: 12 -> 12, of which waited for: 5 -> 3; matrix products, arithmetic and copies ran while one was open for 6% -> 11% of each run, Pallas kernels for 0% -> 0%
where the time goes in v13:
time: 93.8 us; the launch traced here: 92.8 us
  starting transfers between devices  45.9 us (49%)
  other arithmetic  20.1 us (21%)
  local copies, waits for them, and re-layouts  13 us (14%)
  waiting for transfers between devices  11.3 us (12%)
  matrix products  2.05 us (2%)
    ppermute x6, starting transfers between devices, send(): return lax.ppermute(msg, axis, pairs)  22.4 us
    ppermute x3, starting transfers between devices, halo_from(): lax.ppermute(lax.slice_in_dim(block, n - width, n, axis=dim), axis, forward)  13.4 us
    ppermute x3, starting transfers between devices, halo_from(): lax.ppermute(lax.slice_in_dim(block, 0, width, axis=dim), axis, backward)  10.1 us
    ppermute x3, waiting for transfers between devices, halo_from(): lax.ppermute(lax.slice_in_dim(block, 0, width, axis=dim), axis, backward)  8.75 us
    select_n x2, other arithmetic, per_device(): fine = jnp.where(inside, fine + step, 0.0)  7.91 us
    slice x6, local copies, waits for them, and re-layouts, packed_halo(): lax.slice_in_dim(f, f.shape[dim] - d, f.shape[dim], axis=dim)  4.36 us
    concatenate x6, other arithmetic, send(): msg = jnp.concatenate(pieces, axis=dim)  3.31 us
    ppermute x3, waiting for transfers between devices, halo_from(): lax.ppermute(lax.slice_in_dim(block, n - width, n, axis=dim), axis, forward)  2.53 us
  transfers between devices with their start and end apart: 12, of which 3 were waited for; matrix products, arithmetic and copies ran while one was open for 11% of the time, Pallas kernels for 0%

profile of v13, /device:TPU:34, one launch (start us, length us, event | category | flops | bytes accessed | tf_op | source)
XLA Modules:
  0.0 92.8 jit_solution(4371031338966826803)
XLA Ops:
  0.0 1.2 %fusion.230 = (f32[16,2,512]{2,1,0:T(2,128)S(1)}, f32[16,2,512]{2,1,0:T(2,128)S(1)}) fusion(f32[16,32,512]{2,1,0:T(8,128)} %param.3), kind=kLoop, calls=%fused_computation.363 | loop fusion | bytes 262144 | tf_op jit(solution)/shard_map/slice | solution.py:48
  1.2 1.4 %fusion.231 = (f32[16,3,512]{2,1,0:T(4,128)S(1)}, f32[16,3,512]{2,1,0:T(4,128)S(1)}, f32[16,3,512]{2,1,0:T(4,128)S(1)}, f32[16,3,512]{2,1,0:T(4,128)S(1)}) fusion(f32[16,32,512]{2,1,0:T(8,128)} %param.4, f32[16,32,512]{2,1,0:T(8,128)} %param.5), kind=kLoop, calls=%fused_computation.364 | loop fusion | bytes 786432 | tf_op jit(solution)/shard_map/slice | solution.py:48
  2.6 0.8 pad_maximum_fusion.3
  3.4 3.0 %collective-permute-start = (f32[16,8,512]{2,1,0:T(8,128)}, f32[16,8,512]{2,1,0:T(8,128)}, u32[]{:S(2)}, u32[]{:S(2)}) collective-permute-start(f32[16,8,512]{2,1,0:T(8,128)} %pad_maximum_fusion.3), channel_id=1, source_target_pairs={{0,1},{1,2},{2,3},{3,4},{4,5},{5,6},{6,7},{8,9},{9,10},{10,11},{11... | collective-permute-start | bytes 786440 | tf_op jit(solution)/shard_map/ppermute | solution.py:58
  6.5 0.8 pad_maximum_fusion.4
  7.3 3.5 %collective-permute-start.1 = (f32[16,8,512]{2,1,0:T(8,128)}, f32[16,8,512]{2,1,0:T(8,128)}, u32[]{:S(2)}, u32[]{:S(2)}) collective-permute-start(f32[16,8,512]{2,1,0:T(8,128)} %pad_maximum_fusion.4), channel_id=1, source_target_pairs={{1,0},{2,1},{3,2},{4,3},{5,4},{6,5},{7,6},{9,8},{10,9},{11,10},{12... | collective-permute-start | bytes 786440 | tf_op jit(solution)/shard_map/ppermute | solution.py:58
  10.9 0.8 pad_maximum_fusion
  11.7 1.9 %collective-permute-start.3 = (f32[8,32,512]{2,1,0:T(8,128)}, f32[8,32,512]{2,1,0:T(8,128)}, u32[]{:S(2)}, u32[]{:S(2)}) collective-permute-start(f32[8,32,512]{2,1,0:T(8,128)} %pad_maximum_fusion), channel_id=1, source_target_pairs={{0,8},{8,16},{16,24},{24,32},{32,40},{40,48},{48,56},{56,64},{64,7... | collective-permute-start | bytes 1572872 | tf_op jit(solution)/shard_map/ppermute | solution.py:58
  13.7 0.8 pad_maximum_fusion.1
  14.5 6.0 %collective-permute-start.5 = (f32[8,32,512]{2,1,0:T(8,128)}, f32[8,32,512]{2,1,0:T(8,128)}, u32[]{:S(2)}, u32[]{:S(2)}) collective-permute-start(f32[8,32,512]{2,1,0:T(8,128)} %pad_maximum_fusion.1), channel_id=1, source_target_pairs={{8,0},{16,8},{24,16},{32,24},{40,32},{48,40},{56,48},{64,56},{72,6... | collective-permute-start | bytes 1572872 | tf_op jit(solution)/shard_map/ppermute | solution.py:58
  20.7 0.5 fusion.204
  21.4 0.8 fusion.237
  22.2 0.8 fusion.238
  23.1 1.9 %collective-permute-start.2 = (f32[3,16,512]{2,1,0:T(8,128)S(1)}, f32[3,16,512]{2,1,0:T(8,128)S(1)}, u32[]{:S(2)}, u32[]{:S(2)}) collective-permute-start(f32[3,16,512]{2,1,0:T(8,128)S(1)} %pad_maximum_fusion.5), channel_id=1, source_target_pairs={{0,8},{8,16},{16,24},{24,32},{32,40},{40,48},{48,56},{56,64},{64,7... | collective-permute-start | bytes 294920 | tf_op jit(solution)/shard_map/ppermute | solution.py:58
  25.0 6.0 %collective-permute-start.4 = (f32[3,16,512]{2,1,0:T(8,128)S(1)}, f32[3,16,512]{2,1,0:T(8,128)S(1)}, u32[]{:S(2)}, u32[]{:S(2)}) collective-permute-start(f32[3,16,512]{2,1,0:T(8,128)S(1)} %pad_maximum_fusion.6), channel_id=1, source_target_pairs={{8,0},{16,8},{24,16},{32,24},{40,32},{48,40},{56,48},{64,56},{72,6... | collective-permute-start | bytes 294920 | tf_op jit(solution)/shard_map/ppermute | solution.py:58
  31.1 1.1 %fusion.235 = (f32[16,3,512]{2,1,0:T(4,128)S(1)}, f32[16,3,512]{2,1,0:T(4,128)S(1)}) fusion(f32[16,8,512]{2,1,0:T(8,128)} %collective-permute-done), kind=kLoop, calls=%fused_computation.368 | loop fusion | bytes 393216 | tf_op jit(solution)/shard_map/slice | solution.py:73
  32.2 1.1 %fusion.236 = (f32[16,3,512]{2,1,0:T(4,128)S(1)}, f32[16,3,512]{2,1,0:T(4,128)S(1)}) fusion(f32[16,8,512]{2,1,0:T(8,128)} %collective-permute-done.1), kind=kLoop, calls=%fused_computation.369 | loop fusion | bytes 393216 | tf_op jit(solution)/shard_map/slice | solution.py:73
  33.3 1.0 %slice.499 = f32[16,2,512]{2,1,0:T(2,128)S(1)} slice(f32[16,8,512]{2,1,0:T(8,128)} %collective-permute-done), slice={[0:16], [0:2], [0:512]} | slice | bytes 131072 | tf_op jit(solution)/shard_map/slice | solution.py:73
  34.2 1.0 %slice.500 = f32[16,2,512]{2,1,0:T(2,128)S(1)} slice(f32[16,8,512]{2,1,0:T(8,128)} %collective-permute-done.1), slice={[0:16], [0:2], [0:512]} | slice | bytes 131072 | tf_op jit(solution)/shard_map/slice | solution.py:73
  35.3 1.0 %fusion.233 = (f32[3,32,512]{2,1,0:T(8,128)S(1)}, f32[3,32,512]{2,1,0:T(8,128)S(1)}) fusion(f32[8,32,512]{2,1,0:T(8,128)} %collective-permute-done.3), kind=kLoop, calls=%fused_computation.366 | loop fusion | bytes 786432 | tf_op jit(solution)/shard_map/slice | solution.py:72
  36.4 1.0 %fusion.234 = (f32[3,32,512]{2,1,0:T(8,128)S(1)}, f32[3,32,512]{2,1,0:T(8,128)S(1)}) fusion(f32[8,32,512]{2,1,0:T(8,128)} %collective-permute-done.5), kind=kLoop, calls=%fused_computation.367 | loop fusion | bytes 786432 | tf_op jit(solution)/shard_map/slice | solution.py:74
  37.4 0.3 maximum_maximum_fusion.1
  37.7 0.3 maximum_maximum_fusion
  38.0 0.9 slice.497
  38.9 0.9 slice.504
  39.9 0.5 fusion.43
  40.4 2.1 %divide_select_fusion.2 = (f32[22,38,512]{2,1,0:T(8,128)S(1)}, f32[22,38,512]{2,1,0:T(8,128)S(1)}, f32[22,38,512]{2,1,0:T(8,128)S(1)}) fusion(f32[22,38,512]{2,1,0:T(8,128)S(1)} %maximum_maximum_fusion), kind=kLoop, calls=%fused_computation.21 | loop fusion | flops 8560640 | bytes 6848512 | tf_op jit(solution)/shard_map/jit(_where)/select_n | solution.py:182
  42.5 4.1 %and_select_fusion.1 = (f32[22,38,512]{2,1,0:T(8,128)S(1)}, f32[22,38,512]{2,1,0:T(8,128)S(1)}) fusion(f32[22,38,512]{2,1,0:T(8,128)S(1)} %maximum_maximum_fusion.1, f32[22,38,512]{2,1,0:T(8,128)S(1)} %get-tuple-element.43, f32[22,38,512]{2,1,0:T(8,128)S(1)} %get-tuple-element.44, f32[22,38,512]{2,1,0:T(8,128)S(1)} %get-tuple-element.42, ...), kind=kLoop, calls=%fused_computation.23 | loop fusion | flops 12412928 | bytes 13697596 | tf_op jit(solution)/shard_map/jit(_where)/select_n | solution.py:227
  46.6 3.8 %and_select_fusion = f32[22,38,512]{2,1,0:T(8,128)S(1)} fusion(f32[22,38,512]{2,1,0:T(8,128)S(1)} %get-tuple-element.36, f32[22,38,512]{2,1,0:T(8,128)S(1)} %get-tuple-element.37, f32[22,38,512]{2,1,0:T(8,128)S(1)} %get-tuple-element.43, f32[22,38,512]{2,1,0:T(8,128)S(1)} %get-tuple-element.44, f32[22,38,512]{2,1,0:T(8,128)S(1)} %get-tuple-element.42, ...), kind=kLoop, calls=%fused_computation.22 | loop fusion | flops 11984896 | bytes 11984956 | tf_op jit(solution)/shard_map/jit(_where)/select_n | solution.py:227
  50.4 0.5 fusion.226
  50.9 1.8 %fusion.51 = (f32[16,32,512]{2,1,0:T(8,128)S(1)}, f32[16,32,512]{2,1,0:T(8,128)S(1)}) fusion(f32[16,32,512]{2,1,0:T(8,128)S(1)} %copy-done.1, f32[22,38,512]{2,1,0:T(8,128)S(1)} %get-tuple-element.37, f32[22,38,512]{2,1,0:T(8,128)S(1)} %get-tuple-element.43, f32[22,38,512]{2,1,0:T(8,128)S(1)} %and_select_fusion, f32[22,38,512]{2,1,0:T(8,128)S(1)} %get-tuple-element.44, ...), kind=kLoop, calls=%fused_computation.139 | loop fusion | flops 4718592 | bytes 16773120 | tf_op jit(solution)/shard_map/sub | solution.py:238
  52.8 0.5 fusion.202
  53.4 7.5 %collective-permute-start.6 = (f32[2,4,8,128]{3,2,1,0:T(8,128)S(1)}, f32[2,4,8,128]{3,2,1,0:T(8,128)S(1)}, u32[]{:S(2)}, u32[]{:S(2)}) collective-permute-start(f32[2,4,8,128]{3,2,1,0:T(8,128)S(1)} %pad_maximum_fusion.7), channel_id=1, source_target_pairs={{0,16},{8,24},{16,32},{24,40},{32,48},{40,56},{48,64},{56,72},{64,... | collective-permute-start | bytes 98312 | tf_op jit(solution)/shard_map/ppermute | solution.py:25
  61.0 1.9 %collective-permute-start.7 = (f32[2,4,8,128]{3,2,1,0:T(8,128)S(1)}, f32[2,4,8,128]{3,2,1,0:T(8,128)S(1)}, u32[]{:S(2)}, u32[]{:S(2)}) collective-permute-start(f32[2,4,8,128]{3,2,1,0:T(8,128)S(1)} %pad_maximum_fusion.7), channel_id=1, source_target_pairs={{0,8},{8,16},{16,24},{24,32},{32,40},{40,48},{48,56},{56,64},{64,7... | collective-permute-start | bytes 98312 | tf_op jit(solution)/shard_map/ppermute | solution.py:25
  62.9 6.0 %collective-permute-start.8 = (f32[2,4,8,128]{3,2,1,0:T(8,128)S(1)}, f32[2,4,8,128]{3,2,1,0:T(8,128)S(1)}, u32[]{:S(2)}, u32[]{:S(2)}) collective-permute-start(f32[2,4,8,128]{3,2,1,0:T(8,128)S(1)} %pad_maximum_fusion.7), channel_id=1, source_target_pairs={{8,0},{16,8},{24,16},{32,24},{40,32},{48,40},{56,48},{64,56},{72,6... | collective-permute-start | bytes 98312 | tf_op jit(solution)/shard_map/ppermute | solution.py:26
  68.9 1.9 %collective-permute-start.9 = (f32[2,4,8,128]{3,2,1,0:T(8,128)S(1)}, f32[2,4,8,128]{3,2,1,0:T(8,128)S(1)}, u32[]{:S(2)}, u32[]{:S(2)}) collective-permute-start(f32[2,4,8,128]{3,2,1,0:T(8,128)S(1)} %pad_maximum_fusion.7), channel_id=1, source_target_pairs={{16,0},{24,8},{32,16},{40,24},{48,32},{56,40},{64,48},{72,56},{80,... | collective-permute-start | bytes 98312 | tf_op jit(solution)/shard_map/ppermute | solution.py:26
  71.0 5.3 %collective-permute-done.9 = f32[2,4,8,128]{3,2,1,0:T(8,128)S(1)} collective-permute-done((f32[2,4,8,128]{3,2,1,0:T(8,128)S(1)}, f32[2,4,8,128]{3,2,1,0:T(8,128)S(1)}, u32[]{:S(2)}, u32[]{:S(2)}) %collective-permute-start.9) | collective-permute-done | bytes 32800 | tf_op jit(solution)/shard_map/ppermute | solution.py:26
  76.3 4.0 %collective-permute-start.10 = (f32[2,20,8,128]{3,2,1,0:T(8,128)S(1)}, f32[2,20,8,128]{3,2,1,0:T(8,128)S(1)}, u32[]{:S(2)}, u32[]{:S(2)}) collective-permute-start(f32[2,20,8,128]{3,2,1,0:T(8,128)S(1)} %constant_dynamic-update-slice_fusion), channel_id=1, source_target_pairs={{0,1},{1,2},{2,3},{3,4},{4,5},{5,6},{6,7},{8,9},{9,10},{10,11},{11... | collective-permute-start | bytes 491528 | tf_op jit(solution)/shard_map/ppermute | solution.py:25
  80.2 2.1 %collective-permute-start.11 = (f32[2,20,8,128]{3,2,1,0:T(8,128)S(1)}, f32[2,20,8,128]{3,2,1,0:T(8,128)S(1)}, u32[]{:S(2)}, u32[]{:S(2)}) collective-permute-start(f32[2,20,8,128]{3,2,1,0:T(8,128)S(1)} %constant_dynamic-update-slice_fusion), channel_id=1, source_target_pairs={{1,0},{2,1},{3,2},{4,3},{5,4},{6,5},{7,6},{9,8},{10,9},{11,10},{12... | collective-permute-start | bytes 491528 | tf_op jit(solution)/shard_map/ppermute | solution.py:26
  82.4 2.5 %collective-permute-done.10 = f32[2,20,8,128]{3,2,1,0:T(8,128)S(1)} collective-permute-done((f32[2,20,8,128]{3,2,1,0:T(8,128)S(1)}, f32[2,20,8,128]{3,2,1,0:T(8,128)S(1)}, u32[]{:S(2)}, u32[]{:S(2)}) %collective-permute-start.10) | collective-permute-done | bytes 163872 | tf_op jit(solution)/shard_map/ppermute | solution.py:25
  84.9 3.4 %collective-permute-done.11 = f32[2,20,8,128]{3,2,1,0:T(8,128)S(1)} collective-permute-done((f32[2,20,8,128]{3,2,1,0:T(8,128)S(1)}, f32[2,20,8,128]{3,2,1,0:T(8,128)S(1)}, u32[]{:S(2)}, u32[]{:S(2)}) %collective-permute-start.11) | collective-permute-done | bytes 163872 | tf_op jit(solution)/shard_map/ppermute | solution.py:26
  88.4 0.5 fusion.187
  89.0 0.3 fusion.188
  89.8 0.3 multiply_add_fusion.2
  90.4 0.3 multiply_add_fusion
  90.9 0.5 fusion.191
  91.4 0.3 convolution_bitcast_fusion
  91.7 1.1 %bitcast_add_fusion = f32[16,32,512]{2,1,0:T(8,128)} fusion(f32[16,32,512]{2,1,0:T(8,128)S(1)} %get-tuple-element.13, f32[4,32,512]{2,1,0:T(8,128)S(1)} %convolution_bitcast_fusion), kind=kLoop, calls=%fused_computation.153 | loop fusion | flops 262144 | bytes 2359296 | tf_op jit(solution)/shard_map/add | solution.py:243
  (48 shorter events, 1.8 us)
Async XLA Ops:
  0.0 10.8 %copy-start = (f32[16,32,512]{2,1,0:T(8,128)S(1)}, f32[16,32,512]{2,1,0:T(8,128)}, u32[]{:S(2)}) copy-start(f32[16,32,512]{2,1,0:T(8,128)} %param.4) | copy-start | bytes 3145732
  0.0 10.8 %copy-start.2 = (f32[16,32,512]{2,1,0:T(8,128)S(1)}, f32[16,32,512]{2,1,0:T(8,128)}, u32[]{:S(2)}) copy-start(f32[16,32,512]{2,1,0:T(8,128)} %param.5) | copy-start | bytes 3145732
  1.2 9.6 %copy-start.1 = (f32[16,32,512]{2,1,0:T(8,128)S(1)}, f32[16,32,512]{2,1,0:T(8,128)}, u32[]{:S(2)}) copy-start(f32[16,32,512]{2,1,0:T(8,128)} %param.3) | copy-start | bytes 3145732
  3.4 17.9 %collective-permute-start = (f32[16,8,512]{2,1,0:T(8,128)}, f32[16,8,512]{2,1,0:T(8,128)}, u32[]{:S(2)}, u32[]{:S(2)}) collective-permute-start(f32[16,8,512]{2,1,0:T(8,128)} %pad_maximum_fusion.3), channel_id=1, source_target_pairs={{0,1},{1,2},{2,3},{3,4},{4,5},{5,6},{6,7},{8,9},{9,10},{10,11},{11... | collective-permute-start | bytes 786440 | tf_op jit(solution)/shard_map/ppermute | solution.py:58
  7.3 15.0 %collective-permute-start.1 = (f32[16,8,512]{2,1,0:T(8,128)}, f32[16,8,512]{2,1,0:T(8,128)}, u32[]{:S(2)}, u32[]{:S(2)}) collective-permute-start(f32[16,8,512]{2,1,0:T(8,128)} %pad_maximum_fusion.4), channel_id=1, source_target_pairs={{1,0},{2,1},{3,2},{4,3},{5,4},{6,5},{7,6},{9,8},{10,9},{11,10},{12... | collective-permute-start | bytes 786440 | tf_op jit(solution)/shard_map/ppermute | solution.py:58
  11.7 23.6 %collective-permute-start.3 = (f32[8,32,512]{2,1,0:T(8,128)}, f32[8,32,512]{2,1,0:T(8,128)}, u32[]{:S(2)}, u32[]{:S(2)}) collective-permute-start(f32[8,32,512]{2,1,0:T(8,128)} %pad_maximum_fusion), channel_id=1, source_target_pairs={{0,8},{8,16},{16,24},{24,32},{32,40},{40,48},{48,56},{56,64},{64,7... | collective-permute-start | bytes 1572872 | tf_op jit(solution)/shard_map/ppermute | solution.py:58
  14.5 21.9 %collective-permute-start.5 = (f32[8,32,512]{2,1,0:T(8,128)}, f32[8,32,512]{2,1,0:T(8,128)}, u32[]{:S(2)}, u32[]{:S(2)}) collective-permute-start(f32[8,32,512]{2,1,0:T(8,128)} %pad_maximum_fusion.1), channel_id=1, source_target_pairs={{8,0},{16,8},{24,16},{32,24},{40,32},{48,40},{56,48},{64,56},{72,6... | collective-permute-start | bytes 1572872 | tf_op jit(solution)/shard_map/ppermute | solution.py:58
  23.1 12.1 %collective-permute-start.2 = (f32[3,16,512]{2,1,0:T(8,128)S(1)}, f32[3,16,512]{2,1,0:T(8,128)S(1)}, u32[]{:S(2)}, u32[]{:S(2)}) collective-permute-start(f32[3,16,512]{2,1,0:T(8,128)S(1)} %pad_maximum_fusion.5), channel_id=1, source_target_pairs={{0,8},{8,16},{16,24},{24,32},{32,40},{40,48},{48,56},{56,64},{64,7... | collective-permute-start | bytes 294920 | tf_op jit(solution)/shard_map/ppermute | solution.py:58
  25.0 10.2 %collective-permute-start.4 = (f32[3,16,512]{2,1,0:T(8,128)S(1)}, f32[3,16,512]{2,1,0:T(8,128)S(1)}, u32[]{:S(2)}, u32[]{:S(2)}) collective-permute-start(f32[3,16,512]{2,1,0:T(8,128)S(1)} %pad_maximum_fusion.6), channel_id=1, source_target_pairs={{8,0},{16,8},{24,16},{32,24},{40,32},{48,40},{56,48},{64,56},{72,6... | collective-permute-start | bytes 294920 | tf_op jit(solution)/shard_map/ppermute | solution.py:58
  53.4 17.4 %collective-permute-start.6 = (f32[2,4,8,128]{3,2,1,0:T(8,128)S(1)}, f32[2,4,8,128]{3,2,1,0:T(8,128)S(1)}, u32[]{:S(2)}, u32[]{:S(2)}) collective-permute-start(f32[2,4,8,128]{3,2,1,0:T(8,128)S(1)} %pad_maximum_fusion.7), channel_id=1, source_target_pairs={{0,16},{8,24},{16,32},{24,40},{32,48},{40,56},{48,64},{56,72},{64,... | collective-permute-start | bytes 98312 | tf_op jit(solution)/shard_map/ppermute | solution.py:25
  61.0 9.9 %collective-permute-start.7 = (f32[2,4,8,128]{3,2,1,0:T(8,128)S(1)}, f32[2,4,8,128]{3,2,1,0:T(8,128)S(1)}, u32[]{:S(2)}, u32[]{:S(2)}) collective-permute-start(f32[2,4,8,128]{3,2,1,0:T(8,128)S(1)} %pad_maximum_fusion.7), channel_id=1, source_target_pairs={{0,8},{8,16},{16,24},{24,32},{32,40},{40,48},{48,56},{56,64},{64,7... | collective-permute-start | bytes 98312 | tf_op jit(solution)/shard_map/ppermute | solution.py:25
  62.9 8.0 %collective-permute-start.8 = (f32[2,4,8,128]{3,2,1,0:T(8,128)S(1)}, f32[2,4,8,128]{3,2,1,0:T(8,128)S(1)}, u32[]{:S(2)}, u32[]{:S(2)}) collective-permute-start(f32[2,4,8,128]{3,2,1,0:T(8,128)S(1)} %pad_maximum_fusion.7), channel_id=1, source_target_pairs={{8,0},{16,8},{24,16},{32,24},{40,32},{48,40},{56,48},{64,56},{72,6... | collective-permute-start | bytes 98312 | tf_op jit(solution)/shard_map/ppermute | solution.py:26
  68.9 7.3 %collective-permute-start.9 = (f32[2,4,8,128]{3,2,1,0:T(8,128)S(1)}, f32[2,4,8,128]{3,2,1,0:T(8,128)S(1)}, u32[]{:S(2)}, u32[]{:S(2)}) collective-permute-start(f32[2,4,8,128]{3,2,1,0:T(8,128)S(1)} %pad_maximum_fusion.7), channel_id=1, source_target_pairs={{16,0},{24,8},{32,16},{40,24},{48,32},{56,40},{64,48},{72,56},{80,... | collective-permute-start | bytes 98312 | tf_op jit(solution)/shard_map/ppermute | solution.py:26
  76.3 8.7 %collective-permute-start.10 = (f32[2,20,8,128]{3,2,1,0:T(8,128)S(1)}, f32[2,20,8,128]{3,2,1,0:T(8,128)S(1)}, u32[]{:S(2)}, u32[]{:S(2)}) collective-permute-start(f32[2,20,8,128]{3,2,1,0:T(8,128)S(1)} %constant_dynamic-update-slice_fusion), channel_id=1, source_target_pairs={{0,1},{1,2},{2,3},{3,4},{4,5},{5,6},{6,7},{8,9},{9,10},{10,11},{11... | collective-permute-start | bytes 491528 | tf_op jit(solution)/shard_map/ppermute | solution.py:25
  80.2 8.1 %collective-permute-start.11 = (f32[2,20,8,128]{3,2,1,0:T(8,128)S(1)}, f32[2,20,8,128]{3,2,1,0:T(8,128)S(1)}, u32[]{:S(2)}, u32[]{:S(2)}) collective-permute-start(f32[2,20,8,128]{3,2,1,0:T(8,128)S(1)} %constant_dynamic-update-slice_fusion), channel_id=1, source_target_pairs={{1,0},{2,1},{3,2},{4,3},{5,4},{6,5},{7,6},{9,8},{10,9},{11,10},{12... | collective-permute-start | bytes 491528 | tf_op jit(solution)/shard_map/ppermute | solution.py:26

commit v14 on v13

--- a/solution.py
+++ b/solution.py
@@ -61,17 +61,19 @@
     xh = send([down(f, d, 0) for f, d in zip(fields, depths)], "box", bb, 0)
     yl = send([up(f, d, 1) for f, d in zip(fields, depths)], "group", fg, 1)
     yh = send([down(f, d, 1) for f, d in zip(fields, depths)], "group", bg, 1)
-    width = yl.shape[1]
     low = send([up(yl, top, 0), up(yh, top, 0)], "box", fb, 1)
     high = send([down(yl, top, 0), down(yh, top, 0)], "box", bb, 1)
+    total = sum(depths)
     out = []
     for f, d, o in zip(fields, depths, offs):
-        ys = slice(o, o + d)
-        ys2 = slice(width + o, width + o + d)
+        lo_win = slice(o + d - top, o + d)
+        hi_win = slice(o, o + top)
+        assert lo_win.start >= 0 and hi_win.stop <= total
+        hi_win2 = slice(total + hi_win.start, total + hi_win.stop)
         rows = [
-            jnp.concatenate([low[top - d:, ys], xl[o:o + d], low[top - d:, ys2]], axis=1),
-            jnp.concatenate([yl[:, ys], f, yh[:, ys]], axis=1),
-            jnp.concatenate([high[:d, ys], xh[o:o + d], high[:d, ys2]], axis=1),
+            jnp.concatenate([low[:, lo_win], xl[lo_win], low[:, hi_win2]], axis=1),
+            jnp.concatenate([yl[:, lo_win], f, yh[:, hi_win]], axis=1),
+            jnp.concatenate([high[:, lo_win], xh[hi_win], high[:, hi_win2]], axis=1),
         ]
         out.append(jnp.concatenate(rows, axis=0))
     return out
@@ -215,8 +217,7 @@
 def per_device(right_side, inv_density, pressure):
     depth = SWEEPS + 1
     sx, sy, sz = pressure.shape
-    rhs_e, b_e, fine = packed_halo([right_side, inv_density, pressure], [depth - 1, depth, depth])
-    rhs_e = jnp.pad(rhs_e, ((1, 1), (1, 1), (0, 0)))
+    b_e, rhs_e, fine = packed_halo([inv_density, right_side, pressure], [depth, depth - 1, depth])
     rhs_e, b_e, fine = lax.optimization_barrier((rhs_e, b_e, fine))
     totals = (sx * lax.axis_size("box"), sy * lax.axis_size("group"))
     inside = grid_mask(fine.shape, depth, ("box", "group"), totals)

time: 93.8 us -> 90.3 us (0.963)
  local copies, waits for them, and re-layouts: 13 us -> 9.76 us
    slice x12 -> x6, local copies, waits for them, and re-layouts: 8.11 us -> 4.89 us  [the longest x1 1.34 us: packed_halo(): yh[:, hi_win]]
  transfers between devices with their start and end apart: 12 -> 12, of which waited for: 3 -> 4; matrix products, arithmetic and copies ran while one was open for 11% -> 10% of each run, Pallas kernels for 0% -> 0%
where the time goes in v14:
time: 90.3 us; the launch traced here: 89.4 us
  starting transfers between devices  45.3 us (50%)
  other arithmetic  19.9 us (22%)
  waiting for transfers between devices  11.9 us (13%)
  local copies, waits for them, and re-layouts  9.76 us (11%)
  matrix products  2.05 us (2%)
    ppermute x6, starting transfers between devices, send(): return lax.ppermute(msg, axis, pairs)  22.4 us
    ppermute x3, starting transfers between devices, halo_from(): lax.ppermute(lax.slice_in_dim(block, n - width, n, axis=dim), axis, forward)  12.8 us
    ppermute x3, starting transfers between devices, halo_from(): lax.ppermute(lax.slice_in_dim(block, 0, width, axis=dim), axis, backward)  10.1 us
    ppermute x3, waiting for transfers between devices, halo_from(): lax.ppermute(lax.slice_in_dim(block, 0, width, axis=dim), axis, backward)  8.75 us
    select_n x2, other arithmetic, per_device(): fine = jnp.where(inside, fine + step, 0.0)  7.91 us
    slice x6, local copies, waits for them, and re-layouts, packed_halo(): lax.slice_in_dim(f, f.shape[dim] - d, f.shape[dim], axis=dim)  4.36 us
    concatenate x6, other arithmetic, send(): msg = jnp.concatenate(pieces, axis=dim)  3.31 us
    ppermute x3, waiting for transfers between devices, halo_from(): lax.ppermute(lax.slice_in_dim(block, n - width, n, axis=dim), axis, forward)  2.53 us
  transfers between devices with their start and end apart: 12, of which 4 were waited for; matrix products, arithmetic and copies ran while one was open for 10% of the time, Pallas kernels for 0%

profile of v14, /device:TPU:34, one launch (start us, length us, event | category | flops | bytes accessed | tf_op | source)
XLA Modules:
  0.0 89.4 jit_solution(6965200524565251365)
XLA Ops:
  0.0 1.2 %fusion.226 = (f32[16,2,512]{2,1,0:T(2,128)S(1)}, f32[16,2,512]{2,1,0:T(2,128)S(1)}) fusion(f32[16,32,512]{2,1,0:T(8,128)} %param.3), kind=kLoop, calls=%fused_computation.350 | loop fusion | bytes 262144 | tf_op jit(solution)/shard_map/slice | solution.py:48
  1.2 1.4 %fusion.225 = (f32[16,3,512]{2,1,0:T(4,128)S(1)}, f32[16,3,512]{2,1,0:T(4,128)S(1)}, f32[16,3,512]{2,1,0:T(4,128)S(1)}, f32[16,3,512]{2,1,0:T(4,128)S(1)}) fusion(f32[16,32,512]{2,1,0:T(8,128)} %param.4, f32[16,32,512]{2,1,0:T(8,128)} %param.5), kind=kLoop, calls=%fused_computation.349 | loop fusion | bytes 786432 | tf_op jit(solution)/shard_map/slice | solution.py:48
  2.6 0.8 pad_maximum_fusion.3
  3.4 3.0 %collective-permute-start = (f32[16,8,512]{2,1,0:T(8,128)}, f32[16,8,512]{2,1,0:T(8,128)}, u32[]{:S(2)}, u32[]{:S(2)}) collective-permute-start(f32[16,8,512]{2,1,0:T(8,128)} %pad_maximum_fusion.3), channel_id=1, source_target_pairs={{0,1},{1,2},{2,3},{3,4},{4,5},{5,6},{6,7},{8,9},{9,10},{10,11},{11... | collective-permute-start | bytes 786440 | tf_op jit(solution)/shard_map/ppermute | solution.py:58
  6.5 0.8 pad_maximum_fusion.4
  7.3 3.5 %collective-permute-start.1 = (f32[16,8,512]{2,1,0:T(8,128)}, f32[16,8,512]{2,1,0:T(8,128)}, u32[]{:S(2)}, u32[]{:S(2)}) collective-permute-start(f32[16,8,512]{2,1,0:T(8,128)} %pad_maximum_fusion.4), channel_id=1, source_target_pairs={{1,0},{2,1},{3,2},{4,3},{5,4},{6,5},{7,6},{9,8},{10,9},{11,10},{12... | collective-permute-start | bytes 786440 | tf_op jit(solution)/shard_map/ppermute | solution.py:58
  10.9 0.9 pad_maximum_fusion
  11.8 1.9 %collective-permute-start.3 = (f32[8,32,512]{2,1,0:T(8,128)}, f32[8,32,512]{2,1,0:T(8,128)}, u32[]{:S(2)}, u32[]{:S(2)}) collective-permute-start(f32[8,32,512]{2,1,0:T(8,128)} %pad_maximum_fusion), channel_id=1, source_target_pairs={{0,8},{8,16},{16,24},{24,32},{32,40},{40,48},{48,56},{56,64},{64,7... | collective-permute-start | bytes 1572872 | tf_op jit(solution)/shard_map/ppermute | solution.py:58
  13.7 0.8 pad_maximum_fusion.1
  14.5 6.0 %collective-permute-start.5 = (f32[8,32,512]{2,1,0:T(8,128)}, f32[8,32,512]{2,1,0:T(8,128)}, u32[]{:S(2)}, u32[]{:S(2)}) collective-permute-start(f32[8,32,512]{2,1,0:T(8,128)} %pad_maximum_fusion.1), channel_id=1, source_target_pairs={{8,0},{16,8},{24,16},{32,24},{40,32},{48,40},{56,48},{64,56},{72,6... | collective-permute-start | bytes 1572872 | tf_op jit(solution)/shard_map/ppermute | solution.py:58
  20.7 0.5 fusion.199
  21.4 0.8 fusion.232
  22.2 0.8 fusion.233
  23.1 1.9 %collective-permute-start.2 = (f32[3,16,512]{2,1,0:T(8,128)S(1)}, f32[3,16,512]{2,1,0:T(8,128)S(1)}, u32[]{:S(2)}, u32[]{:S(2)}) collective-permute-start(f32[3,16,512]{2,1,0:T(8,128)S(1)} %pad_maximum_fusion.5), channel_id=1, source_target_pairs={{0,8},{8,16},{16,24},{24,32},{32,40},{40,48},{48,56},{56,64},{64,7... | collective-permute-start | bytes 294920 | tf_op jit(solution)/shard_map/ppermute | solution.py:58
  25.0 6.0 %collective-permute-start.4 = (f32[3,16,512]{2,1,0:T(8,128)S(1)}, f32[3,16,512]{2,1,0:T(8,128)S(1)}, u32[]{:S(2)}, u32[]{:S(2)}) collective-permute-start(f32[3,16,512]{2,1,0:T(8,128)S(1)} %pad_maximum_fusion.6), channel_id=1, source_target_pairs={{8,0},{16,8},{24,16},{32,24},{40,32},{48,40},{56,48},{64,56},{72,6... | collective-permute-start | bytes 294920 | tf_op jit(solution)/shard_map/ppermute | solution.py:58
  31.1 1.2 %fusion.230 = (f32[16,3,512]{2,1,0:T(4,128)S(1)}, f32[16,3,512]{2,1,0:T(4,128)S(1)}, f32[16,3,512]{2,1,0:T(4,128)S(1)}) fusion(f32[16,8,512]{2,1,0:T(8,128)} %collective-permute-done), kind=kLoop, calls=%fused_computation.354 | loop fusion | bytes 589824 | tf_op jit(solution)/shard_map/slice | solution.py:75
  32.3 1.3 %fusion.231 = (f32[16,3,512]{2,1,0:T(4,128)S(1)}, f32[16,3,512]{2,1,0:T(4,128)S(1)}, f32[16,3,512]{2,1,0:T(4,128)S(1)}) fusion(f32[16,8,512]{2,1,0:T(8,128)} %collective-permute-done.1), kind=kLoop, calls=%fused_computation.355 | loop fusion | bytes 589824 | tf_op jit(solution)/shard_map/slice | solution.py:75
  33.7 0.6 collective-permute-done.4
  34.3 1.2 %fusion.228 = (f32[3,32,512]{2,1,0:T(8,128)S(1)}, f32[3,32,512]{2,1,0:T(8,128)S(1)}, f32[3,32,512]{2,1,0:T(8,128)S(1)}) fusion(f32[8,32,512]{2,1,0:T(8,128)} %collective-permute-done.3), kind=kLoop, calls=%fused_computation.352 | loop fusion | bytes 1179648 | tf_op jit(solution)/shard_map/slice | solution.py:74
  35.5 1.2 %fusion.229 = (f32[3,32,512]{2,1,0:T(8,128)S(1)}, f32[3,32,512]{2,1,0:T(8,128)S(1)}, f32[3,32,512]{2,1,0:T(8,128)S(1)}) fusion(f32[8,32,512]{2,1,0:T(8,128)} %collective-permute-done.5), kind=kLoop, calls=%fused_computation.353 | loop fusion | bytes 1179648 | tf_op jit(solution)/shard_map/slice | solution.py:76
  36.7 0.3 maximum_maximum_fusion.2
  37.0 0.3 maximum_maximum_fusion.1
  37.3 0.3 maximum_maximum_fusion
  37.6 2.1 %divide_select_fusion.2 = (f32[22,38,512]{2,1,0:T(8,128)S(1)}, f32[22,38,512]{2,1,0:T(8,128)S(1)}, f32[22,38,512]{2,1,0:T(8,128)S(1)}) fusion(f32[22,38,512]{2,1,0:T(8,128)S(1)} %maximum_maximum_fusion.1), kind=kLoop, calls=%fused_computation.17 | loop fusion | flops 8560640 | bytes 6848512 | tf_op jit(solution)/shard_map/jit(_where)/select_n | solution.py:184
  39.7 4.1 %and_select_fusion.1 = (f32[22,38,512]{2,1,0:T(8,128)S(1)}, f32[22,38,512]{2,1,0:T(8,128)S(1)}) fusion(f32[22,38,512]{2,1,0:T(8,128)S(1)} %maximum_maximum_fusion.2, f32[22,38,512]{2,1,0:T(8,128)S(1)} %get-tuple-element.43, f32[22,38,512]{2,1,0:T(8,128)S(1)} %get-tuple-element.44, f32[22,38,512]{2,1,0:T(8,128)S(1)} %get-tuple-element.42, ...), kind=kLoop, calls=%fused_computation.19 | loop fusion | flops 12412928 | bytes 13697596 | tf_op jit(solution)/shard_map/jit(_where)/select_n | solution.py:228
  43.8 3.8 %and_select_fusion = f32[22,38,512]{2,1,0:T(8,128)S(1)} fusion(f32[22,38,512]{2,1,0:T(8,128)S(1)} %get-tuple-element.36, f32[22,38,512]{2,1,0:T(8,128)S(1)} %get-tuple-element.37, f32[22,38,512]{2,1,0:T(8,128)S(1)} %get-tuple-element.43, f32[22,38,512]{2,1,0:T(8,128)S(1)} %get-tuple-element.44, f32[22,38,512]{2,1,0:T(8,128)S(1)} %get-tuple-element.42, ...), kind=kLoop, calls=%fused_computation.18 | loop fusion | flops 11984896 | bytes 11984956 | tf_op jit(solution)/shard_map/jit(_where)/select_n | solution.py:228
  47.6 0.5 fusion.221
  48.1 1.8 %fusion.46 = (f32[16,32,512]{2,1,0:T(8,128)S(1)}, f32[16,32,512]{2,1,0:T(8,128)S(1)}) fusion(f32[16,32,512]{2,1,0:T(8,128)S(1)} %copy-done.1, f32[22,38,512]{2,1,0:T(8,128)S(1)} %get-tuple-element.37, f32[22,38,512]{2,1,0:T(8,128)S(1)} %get-tuple-element.43, f32[22,38,512]{2,1,0:T(8,128)S(1)} %and_select_fusion, f32[22,38,512]{2,1,0:T(8,128)S(1)} %get-tuple-element.44, ...), kind=kLoop, calls=%fused_computation.125 | loop fusion | flops 4718592 | bytes 16773120 | tf_op jit(solution)/shard_map/sub | solution.py:239
  50.0 0.5 fusion.197
  50.7 6.9 %collective-permute-start.6 = (f32[2,4,8,128]{3,2,1,0:T(8,128)S(1)}, f32[2,4,8,128]{3,2,1,0:T(8,128)S(1)}, u32[]{:S(2)}, u32[]{:S(2)}) collective-permute-start(f32[2,4,8,128]{3,2,1,0:T(8,128)S(1)} %pad_maximum_fusion.7), channel_id=1, source_target_pairs={{0,16},{8,24},{16,32},{24,40},{32,48},{40,56},{48,64},{56,72},{64,... | collective-permute-start | bytes 98312 | tf_op jit(solution)/shard_map/ppermute | solution.py:25
  57.5 1.9 %collective-permute-start.7 = (f32[2,4,8,128]{3,2,1,0:T(8,128)S(1)}, f32[2,4,8,128]{3,2,1,0:T(8,128)S(1)}, u32[]{:S(2)}, u32[]{:S(2)}) collective-permute-start(f32[2,4,8,128]{3,2,1,0:T(8,128)S(1)} %pad_maximum_fusion.7), channel_id=1, source_target_pairs={{0,8},{8,16},{16,24},{24,32},{32,40},{40,48},{48,56},{56,64},{64,7... | collective-permute-start | bytes 98312 | tf_op jit(solution)/shard_map/ppermute | solution.py:25
  59.5 6.0 %collective-permute-start.8 = (f32[2,4,8,128]{3,2,1,0:T(8,128)S(1)}, f32[2,4,8,128]{3,2,1,0:T(8,128)S(1)}, u32[]{:S(2)}, u32[]{:S(2)}) collective-permute-start(f32[2,4,8,128]{3,2,1,0:T(8,128)S(1)} %pad_maximum_fusion.7), channel_id=1, source_target_pairs={{8,0},{16,8},{24,16},{32,24},{40,32},{48,40},{56,48},{64,56},{72,6... | collective-permute-start | bytes 98312 | tf_op jit(solution)/shard_map/ppermute | solution.py:26
  65.5 1.9 %collective-permute-start.9 = (f32[2,4,8,128]{3,2,1,0:T(8,128)S(1)}, f32[2,4,8,128]{3,2,1,0:T(8,128)S(1)}, u32[]{:S(2)}, u32[]{:S(2)}) collective-permute-start(f32[2,4,8,128]{3,2,1,0:T(8,128)S(1)} %pad_maximum_fusion.7), channel_id=1, source_target_pairs={{16,0},{24,8},{32,16},{40,24},{48,32},{56,40},{64,48},{72,56},{80,... | collective-permute-start | bytes 98312 | tf_op jit(solution)/shard_map/ppermute | solution.py:26
  67.5 5.3 %collective-permute-done.9 = f32[2,4,8,128]{3,2,1,0:T(8,128)S(1)} collective-permute-done((f32[2,4,8,128]{3,2,1,0:T(8,128)S(1)}, f32[2,4,8,128]{3,2,1,0:T(8,128)S(1)}, u32[]{:S(2)}, u32[]{:S(2)}) %collective-permute-start.9) | collective-permute-done | bytes 32800 | tf_op jit(solution)/shard_map/ppermute | solution.py:26
  72.8 4.0 %collective-permute-start.10 = (f32[2,20,8,128]{3,2,1,0:T(8,128)S(1)}, f32[2,20,8,128]{3,2,1,0:T(8,128)S(1)}, u32[]{:S(2)}, u32[]{:S(2)}) collective-permute-start(f32[2,20,8,128]{3,2,1,0:T(8,128)S(1)} %constant_dynamic-update-slice_fusion), channel_id=1, source_target_pairs={{0,1},{1,2},{2,3},{3,4},{4,5},{5,6},{6,7},{8,9},{9,10},{10,11},{11... | collective-permute-start | bytes 491528 | tf_op jit(solution)/shard_map/ppermute | solution.py:25
  76.8 2.1 %collective-permute-start.11 = (f32[2,20,8,128]{3,2,1,0:T(8,128)S(1)}, f32[2,20,8,128]{3,2,1,0:T(8,128)S(1)}, u32[]{:S(2)}, u32[]{:S(2)}) collective-permute-start(f32[2,20,8,128]{3,2,1,0:T(8,128)S(1)} %constant_dynamic-update-slice_fusion), channel_id=1, source_target_pairs={{1,0},{2,1},{3,2},{4,3},{5,4},{6,5},{7,6},{9,8},{10,9},{11,10},{12... | collective-permute-start | bytes 491528 | tf_op jit(solution)/shard_map/ppermute | solution.py:26
  78.9 2.5 %collective-permute-done.10 = f32[2,20,8,128]{3,2,1,0:T(8,128)S(1)} collective-permute-done((f32[2,20,8,128]{3,2,1,0:T(8,128)S(1)}, f32[2,20,8,128]{3,2,1,0:T(8,128)S(1)}, u32[]{:S(2)}, u32[]{:S(2)}) %collective-permute-start.10) | collective-permute-done | bytes 163872 | tf_op jit(solution)/shard_map/ppermute | solution.py:25
  81.5 3.4 %collective-permute-done.11 = f32[2,20,8,128]{3,2,1,0:T(8,128)S(1)} collective-permute-done((f32[2,20,8,128]{3,2,1,0:T(8,128)S(1)}, f32[2,20,8,128]{3,2,1,0:T(8,128)S(1)}, u32[]{:S(2)}, u32[]{:S(2)}) %collective-permute-start.11) | collective-permute-done | bytes 163872 | tf_op jit(solution)/shard_map/ppermute | solution.py:26
  85.0 0.5 fusion.182
  85.5 0.3 fusion.183
  85.8 0.3 multiply_add_fusion.4
  86.1 0.3 multiply_add_fusion.3
  86.4 0.3 multiply_add_fusion.2
  86.7 0.3 multiply_add_fusion.1
  86.9 0.3 multiply_add_fusion
  87.5 0.5 fusion.186
  88.0 0.3 convolution_bitcast_fusion
  88.3 1.1 %bitcast_add_fusion = f32[16,32,512]{2,1,0:T(8,128)} fusion(f32[16,32,512]{2,1,0:T(8,128)S(1)} %get-tuple-element.13, f32[4,32,512]{2,1,0:T(8,128)S(1)} %convolution_bitcast_fusion), kind=kLoop, calls=%fused_computation.139 | loop fusion | flops 262144 | bytes 2359296 | tf_op jit(solution)/shard_map/add | solution.py:244
  (42 shorter events, 1.0 us)
Async XLA Ops:
  0.0 10.8 %copy-start = (f32[16,32,512]{2,1,0:T(8,128)S(1)}, f32[16,32,512]{2,1,0:T(8,128)}, u32[]{:S(2)}) copy-start(f32[16,32,512]{2,1,0:T(8,128)} %param.4) | copy-start | bytes 3145732
  0.0 10.8 %copy-start.2 = (f32[16,32,512]{2,1,0:T(8,128)S(1)}, f32[16,32,512]{2,1,0:T(8,128)}, u32[]{:S(2)}) copy-start(f32[16,32,512]{2,1,0:T(8,128)} %param.5) | copy-start | bytes 3145732
  1.2 9.6 %copy-start.1 = (f32[16,32,512]{2,1,0:T(8,128)S(1)}, f32[16,32,512]{2,1,0:T(8,128)}, u32[]{:S(2)}) copy-start(f32[16,32,512]{2,1,0:T(8,128)} %param.3) | copy-start | bytes 3145732
  3.4 18.0 %collective-permute-start = (f32[16,8,512]{2,1,0:T(8,128)}, f32[16,8,512]{2,1,0:T(8,128)}, u32[]{:S(2)}, u32[]{:S(2)}) collective-permute-start(f32[16,8,512]{2,1,0:T(8,128)} %pad_maximum_fusion.3), channel_id=1, source_target_pairs={{0,1},{1,2},{2,3},{3,4},{4,5},{5,6},{6,7},{8,9},{9,10},{10,11},{11... | collective-permute-start | bytes 786440 | tf_op jit(solution)/shard_map/ppermute | solution.py:58
  7.3 15.0 %collective-permute-start.1 = (f32[16,8,512]{2,1,0:T(8,128)}, f32[16,8,512]{2,1,0:T(8,128)}, u32[]{:S(2)}, u32[]{:S(2)}) collective-permute-start(f32[16,8,512]{2,1,0:T(8,128)} %pad_maximum_fusion.4), channel_id=1, source_target_pairs={{1,0},{2,1},{3,2},{4,3},{5,4},{6,5},{7,6},{9,8},{10,9},{11,10},{12... | collective-permute-start | bytes 786440 | tf_op jit(solution)/shard_map/ppermute | solution.py:58
  11.8 22.6 %collective-permute-start.3 = (f32[8,32,512]{2,1,0:T(8,128)}, f32[8,32,512]{2,1,0:T(8,128)}, u32[]{:S(2)}, u32[]{:S(2)}) collective-permute-start(f32[8,32,512]{2,1,0:T(8,128)} %pad_maximum_fusion), channel_id=1, source_target_pairs={{0,8},{8,16},{16,24},{24,32},{32,40},{40,48},{48,56},{56,64},{64,7... | collective-permute-start | bytes 1572872 | tf_op jit(solution)/shard_map/ppermute | solution.py:58
  14.5 21.0 %collective-permute-start.5 = (f32[8,32,512]{2,1,0:T(8,128)}, f32[8,32,512]{2,1,0:T(8,128)}, u32[]{:S(2)}, u32[]{:S(2)}) collective-permute-start(f32[8,32,512]{2,1,0:T(8,128)} %pad_maximum_fusion.1), channel_id=1, source_target_pairs={{8,0},{16,8},{24,16},{32,24},{40,32},{48,40},{56,48},{64,56},{72,6... | collective-permute-start | bytes 1572872 | tf_op jit(solution)/shard_map/ppermute | solution.py:58
  23.1 10.5 %collective-permute-start.2 = (f32[3,16,512]{2,1,0:T(8,128)S(1)}, f32[3,16,512]{2,1,0:T(8,128)S(1)}, u32[]{:S(2)}, u32[]{:S(2)}) collective-permute-start(f32[3,16,512]{2,1,0:T(8,128)S(1)} %pad_maximum_fusion.5), channel_id=1, source_target_pairs={{0,8},{8,16},{16,24},{24,32},{32,40},{40,48},{48,56},{56,64},{64,7... | collective-permute-start | bytes 294920 | tf_op jit(solution)/shard_map/ppermute | solution.py:58
  25.0 9.3 %collective-permute-start.4 = (f32[3,16,512]{2,1,0:T(8,128)S(1)}, f32[3,16,512]{2,1,0:T(8,128)S(1)}, u32[]{:S(2)}, u32[]{:S(2)}) collective-permute-start(f32[3,16,512]{2,1,0:T(8,128)S(1)} %pad_maximum_fusion.6), channel_id=1, source_target_pairs={{8,0},{16,8},{24,16},{32,24},{40,32},{48,40},{56,48},{64,56},{72,6... | collective-permute-start | bytes 294920 | tf_op jit(solution)/shard_map/ppermute | solution.py:58
  50.7 16.8 %collective-permute-start.6 = (f32[2,4,8,128]{3,2,1,0:T(8,128)S(1)}, f32[2,4,8,128]{3,2,1,0:T(8,128)S(1)}, u32[]{:S(2)}, u32[]{:S(2)}) collective-permute-start(f32[2,4,8,128]{3,2,1,0:T(8,128)S(1)} %pad_maximum_fusion.7), channel_id=1, source_target_pairs={{0,16},{8,24},{16,32},{24,40},{32,48},{40,56},{48,64},{56,72},{64,... | collective-permute-start | bytes 98312 | tf_op jit(solution)/shard_map/ppermute | solution.py:25
  57.5 9.9 %collective-permute-start.7 = (f32[2,4,8,128]{3,2,1,0:T(8,128)S(1)}, f32[2,4,8,128]{3,2,1,0:T(8,128)S(1)}, u32[]{:S(2)}, u32[]{:S(2)}) collective-permute-start(f32[2,4,8,128]{3,2,1,0:T(8,128)S(1)} %pad_maximum_fusion.7), channel_id=1, source_target_pairs={{0,8},{8,16},{16,24},{24,32},{32,40},{40,48},{48,56},{56,64},{64,7... | collective-permute-start | bytes 98312 | tf_op jit(solution)/shard_map/ppermute | solution.py:25
  59.5 8.0 %collective-permute-start.8 = (f32[2,4,8,128]{3,2,1,0:T(8,128)S(1)}, f32[2,4,8,128]{3,2,1,0:T(8,128)S(1)}, u32[]{:S(2)}, u32[]{:S(2)}) collective-permute-start(f32[2,4,8,128]{3,2,1,0:T(8,128)S(1)} %pad_maximum_fusion.7), channel_id=1, source_target_pairs={{8,0},{16,8},{24,16},{32,24},{40,32},{48,40},{56,48},{64,56},{72,6... | collective-permute-start | bytes 98312 | tf_op jit(solution)/shard_map/ppermute | solution.py:26
  65.5 7.3 %collective-permute-start.9 = (f32[2,4,8,128]{3,2,1,0:T(8,128)S(1)}, f32[2,4,8,128]{3,2,1,0:T(8,128)S(1)}, u32[]{:S(2)}, u32[]{:S(2)}) collective-permute-start(f32[2,4,8,128]{3,2,1,0:T(8,128)S(1)} %pad_maximum_fusion.7), channel_id=1, source_target_pairs={{16,0},{24,8},{32,16},{40,24},{48,32},{56,40},{64,48},{72,56},{80,... | collective-permute-start | bytes 98312 | tf_op jit(solution)/shard_map/ppermute | solution.py:26
  72.8 8.7 %collective-permute-start.10 = (f32[2,20,8,128]{3,2,1,0:T(8,128)S(1)}, f32[2,20,8,128]{3,2,1,0:T(8,128)S(1)}, u32[]{:S(2)}, u32[]{:S(2)}) collective-permute-start(f32[2,20,8,128]{3,2,1,0:T(8,128)S(1)} %constant_dynamic-update-slice_fusion), channel_id=1, source_target_pairs={{0,1},{1,2},{2,3},{3,4},{4,5},{5,6},{6,7},{8,9},{9,10},{10,11},{11... | collective-permute-start | bytes 491528 | tf_op jit(solution)/shard_map/ppermute | solution.py:25
  76.8 8.1 %collective-permute-start.11 = (f32[2,20,8,128]{3,2,1,0:T(8,128)S(1)}, f32[2,20,8,128]{3,2,1,0:T(8,128)S(1)}, u32[]{:S(2)}, u32[]{:S(2)}) collective-permute-start(f32[2,20,8,128]{3,2,1,0:T(8,128)S(1)} %constant_dynamic-update-slice_fusion), channel_id=1, source_target_pairs={{1,0},{2,1},{3,2},{4,3},{5,4},{6,5},{7,6},{9,8},{10,9},{11,10},{12... | collective-permute-start | bytes 491528 | tf_op jit(solution)/shard_map/ppermute | solution.py:26

commit v15 on v14

--- a/solution.py
+++ b/solution.py
@@ -223,16 +223,24 @@
     inside = grid_mask(fine.shape, depth, ("box", "group"), totals)
     coefs = shared_faces(b_e)
     diag = sum(coefs)
+    ex = fine.shape[0]
     for sweep in range(SWEEPS):
-        step = 2.0 / 3.0 * (rhs_e - apply_op(fine, padded_neighbours(jnp.pad(fine, 1)), coefs)) / diag
-        fine = jnp.where(inside, fine + step, 0.0)
+        part = slice(sweep + 1, ex - sweep - 1)
+        prev = fine
+        centre = prev[1:-1]
+        rows = jnp.pad(centre, ((0, 0), (1, 1), (0, 0)))
+        nears = [prev[:-2], prev[2:], rows[:, :-2], rows[:, 2:], shift_z(centre, -1), shift_z(centre, 1)]
+        cut = [c[part] for c in coefs]
+        step = 2.0 / 3.0 * (rhs_e[part] - apply_op(centre, nears, cut)) / diag[part]
+        fine = jnp.where(inside[part], centre + step, 0.0)
+    first = depth - SWEEPS
     own = (slice(depth, depth + sx), slice(depth, depth + sy))
-    core = fine[own]
+    core = fine[first:first + sx, depth:depth + sy]
     nears = [
-        fine[depth - 1:depth - 1 + sx, depth:depth + sy],
-        fine[depth + 1:depth + 1 + sx, depth:depth + sy],
-        fine[depth:depth + sx, depth - 1:depth - 1 + sy],
-        fine[depth:depth + sx, depth + 1:depth + 1 + sy],
+        fine[first - 1:first - 1 + sx, depth:depth + sy],
+        fine[first + 1:first + 1 + sx, depth:depth + sy],
+        fine[first:first + sx, depth - 1:depth - 1 + sy],
+        fine[first:first + sx, depth + 1:depth + 1 + sy],
         shift_z(core, -1),
         shift_z(core, 1),
     ]

time: 90.3 us -> 92 us (1.019)
  local copies, waits for them, and re-layouts: 9.76 us -> 12 us
    select_n x2, other arithmetic: 7.91 us -> 6.24 us  [per_device(): fine = jnp.where(inside[part], centre + step, 0.0)]
    add x0 -> x1, other arithmetic: none -> 1.09 us  [per_device(): diag = sum(coefs)]
    slice x1 -> x3, local copies, waits for them, and re-layouts: 0.46 us -> 1.55 us  [shift_z(): return jnp.concatenate([zeros, field[:, :, :-1]], axis=2)]
where the time goes in v15:
time: 92 us; the launch traced here: 91.1 us
  starting transfers between devices  45.3 us (49%)
  other arithmetic  19.5 us (21%)
  local copies, waits for them, and re-layouts  12 us (13%)
  waiting for transfers between devices  11.7 us (13%)
  matrix products  2.05 us (2%)
    ppermute x6, starting transfers between devices, send(): return lax.ppermute(msg, axis, pairs)  22.4 us
    ppermute x3, starting transfers between devices, halo_from(): lax.ppermute(lax.slice_in_dim(block, n - width, n, axis=dim), axis, forward)  12.8 us
    ppermute x3, starting transfers between devices, halo_from(): lax.ppermute(lax.slice_in_dim(block, 0, width, axis=dim), axis, backward)  10.1 us
    ppermute x3, waiting for transfers between devices, halo_from(): lax.ppermute(lax.slice_in_dim(block, 0, width, axis=dim), axis, backward)  8.75 us
    select_n x2, other arithmetic, per_device(): fine = jnp.where(inside[part], centre + step, 0.0)  6.24 us
    slice x6, local copies, waits for them, and re-layouts, packed_halo(): lax.slice_in_dim(f, f.shape[dim] - d, f.shape[dim], axis=dim)  4.36 us
    concatenate x6, other arithmetic, send(): msg = jnp.concatenate(pieces, axis=dim)  3.33 us
    ppermute x3, waiting for transfers between devices, halo_from(): lax.ppermute(lax.slice_in_dim(block, n - width, n, axis=dim), axis, forward)  2.53 us
  transfers between devices with their start and end apart: 12, of which 4 were waited for; matrix products, arithmetic and copies ran while one was open for 10% of the time, Pallas kernels for 0%

profile of v15, /device:TPU:34, one launch (start us, length us, event | category | flops | bytes accessed | tf_op | source)
XLA Modules:
  0.0 91.1 jit_solution(11168603638749720846)
XLA Ops:
  0.0 1.2 %fusion.212 = (f32[16,2,512]{2,1,0:T(2,128)S(1)}, f32[16,2,512]{2,1,0:T(2,128)S(1)}) fusion(f32[16,32,512]{2,1,0:T(8,128)} %param.3), kind=kLoop, calls=%fused_computation.334 | loop fusion | bytes 262144 | tf_op jit(solution)/shard_map/slice | solution.py:48
  1.2 1.4 %fusion.211 = (f32[16,3,512]{2,1,0:T(4,128)S(1)}, f32[16,3,512]{2,1,0:T(4,128)S(1)}, f32[16,3,512]{2,1,0:T(4,128)S(1)}, f32[16,3,512]{2,1,0:T(4,128)S(1)}) fusion(f32[16,32,512]{2,1,0:T(8,128)} %param.4, f32[16,32,512]{2,1,0:T(8,128)} %param.5), kind=kLoop, calls=%fused_computation.333 | loop fusion | bytes 786432 | tf_op jit(solution)/shard_map/slice | solution.py:48
  2.6 0.8 pad_maximum_fusion.3
  3.4 3.0 %collective-permute-start = (f32[16,8,512]{2,1,0:T(8,128)}, f32[16,8,512]{2,1,0:T(8,128)}, u32[]{:S(2)}, u32[]{:S(2)}) collective-permute-start(f32[16,8,512]{2,1,0:T(8,128)} %pad_maximum_fusion.3), channel_id=1, source_target_pairs={{0,1},{1,2},{2,3},{3,4},{4,5},{5,6},{6,7},{8,9},{9,10},{10,11},{11... | collective-permute-start | bytes 786440 | tf_op jit(solution)/shard_map/ppermute | solution.py:58
  6.5 0.8 pad_maximum_fusion.4
  7.3 3.5 %collective-permute-start.1 = (f32[16,8,512]{2,1,0:T(8,128)}, f32[16,8,512]{2,1,0:T(8,128)}, u32[]{:S(2)}, u32[]{:S(2)}) collective-permute-start(f32[16,8,512]{2,1,0:T(8,128)} %pad_maximum_fusion.4), channel_id=1, source_target_pairs={{1,0},{2,1},{3,2},{4,3},{5,4},{6,5},{7,6},{9,8},{10,9},{11,10},{12... | collective-permute-start | bytes 786440 | tf_op jit(solution)/shard_map/ppermute | solution.py:58
  10.9 0.9 pad_maximum_fusion
  11.8 1.9 %collective-permute-start.3 = (f32[8,32,512]{2,1,0:T(8,128)}, f32[8,32,512]{2,1,0:T(8,128)}, u32[]{:S(2)}, u32[]{:S(2)}) collective-permute-start(f32[8,32,512]{2,1,0:T(8,128)} %pad_maximum_fusion), channel_id=1, source_target_pairs={{0,8},{8,16},{16,24},{24,32},{32,40},{40,48},{48,56},{56,64},{64,7... | collective-permute-start | bytes 1572872 | tf_op jit(solution)/shard_map/ppermute | solution.py:58
  13.7 0.8 pad_maximum_fusion.1
  14.5 6.0 %collective-permute-start.5 = (f32[8,32,512]{2,1,0:T(8,128)}, f32[8,32,512]{2,1,0:T(8,128)}, u32[]{:S(2)}, u32[]{:S(2)}) collective-permute-start(f32[8,32,512]{2,1,0:T(8,128)} %pad_maximum_fusion.1), channel_id=1, source_target_pairs={{8,0},{16,8},{24,16},{32,24},{40,32},{48,40},{56,48},{64,56},{72,6... | collective-permute-start | bytes 1572872 | tf_op jit(solution)/shard_map/ppermute | solution.py:58
  20.9 0.5 fusion.183
  21.6 0.8 fusion.218
  22.4 0.8 fusion.219
  23.3 1.9 %collective-permute-start.2 = (f32[3,16,512]{2,1,0:T(8,128)S(1)}, f32[3,16,512]{2,1,0:T(8,128)S(1)}, u32[]{:S(2)}, u32[]{:S(2)}) collective-permute-start(f32[3,16,512]{2,1,0:T(8,128)S(1)} %pad_maximum_fusion.5), channel_id=1, source_target_pairs={{0,8},{8,16},{16,24},{24,32},{32,40},{40,48},{48,56},{56,64},{64,7... | collective-permute-start | bytes 294920 | tf_op jit(solution)/shard_map/ppermute | solution.py:58
  25.2 6.0 %collective-permute-start.4 = (f32[3,16,512]{2,1,0:T(8,128)S(1)}, f32[3,16,512]{2,1,0:T(8,128)S(1)}, u32[]{:S(2)}, u32[]{:S(2)}) collective-permute-start(f32[3,16,512]{2,1,0:T(8,128)S(1)} %pad_maximum_fusion.6), channel_id=1, source_target_pairs={{8,0},{16,8},{24,16},{32,24},{40,32},{48,40},{56,48},{64,56},{72,6... | collective-permute-start | bytes 294920 | tf_op jit(solution)/shard_map/ppermute | solution.py:58
  31.3 1.2 %fusion.216 = (f32[16,3,512]{2,1,0:T(4,128)S(1)}, f32[16,3,512]{2,1,0:T(4,128)S(1)}, f32[16,3,512]{2,1,0:T(4,128)S(1)}) fusion(f32[16,8,512]{2,1,0:T(8,128)} %collective-permute-done), kind=kLoop, calls=%fused_computation.338 | loop fusion | bytes 589824 | tf_op jit(solution)/shard_map/slice | solution.py:75
  32.5 1.4 %fusion.217 = (f32[16,3,512]{2,1,0:T(4,128)S(1)}, f32[16,3,512]{2,1,0:T(4,128)S(1)}, f32[16,3,512]{2,1,0:T(4,128)S(1)}) fusion(f32[16,8,512]{2,1,0:T(8,128)} %collective-permute-done.1), kind=kLoop, calls=%fused_computation.339 | loop fusion | bytes 589824 | tf_op jit(solution)/shard_map/slice | solution.py:75
  33.9 0.4 collective-permute-done.4
  34.4 1.2 %fusion.214 = (f32[3,32,512]{2,1,0:T(8,128)S(1)}, f32[3,32,512]{2,1,0:T(8,128)S(1)}, f32[3,32,512]{2,1,0:T(8,128)S(1)}) fusion(f32[8,32,512]{2,1,0:T(8,128)} %collective-permute-done.3), kind=kLoop, calls=%fused_computation.336 | loop fusion | bytes 1179648 | tf_op jit(solution)/shard_map/slice | solution.py:74
  35.5 1.2 %fusion.215 = (f32[3,32,512]{2,1,0:T(8,128)S(1)}, f32[3,32,512]{2,1,0:T(8,128)S(1)}, f32[3,32,512]{2,1,0:T(8,128)S(1)}) fusion(f32[8,32,512]{2,1,0:T(8,128)} %collective-permute-done.5), kind=kLoop, calls=%fused_computation.337 | loop fusion | bytes 1179648 | tf_op jit(solution)/shard_map/slice | solution.py:76
  36.7 0.3 maximum_maximum_fusion.2
  37.6 0.6 fusion.205
  38.2 2.1 %divide_select_fusion.2 = (f32[22,38,512]{2,1,0:T(8,128)S(1)}, f32[22,38,512]{2,1,0:T(8,128)S(1)}, f32[22,38,512]{2,1,0:T(8,128)S(1)}) fusion(f32[22,38,512]{2,1,0:T(8,128)S(1)} %maximum_maximum_fusion.1), kind=kLoop, calls=%fused_computation.5 | loop fusion | flops 8560640 | bytes 6848512 | tf_op jit(solution)/shard_map/jit(_where)/select_n | solution.py:184
  40.4 1.1 %fusion.4 = (f32[22,38,512]{2,1,0:T(8,128)S(1)}, f32[22,38,512]{2,1,0:T(8,128)S(1)}) fusion(f32[22,38,512]{2,1,0:T(8,128)S(1)} %get-tuple-element.41, f32[22,38,512]{2,1,0:T(8,128)S(1)} %get-tuple-element.42, f32[22,38,512]{2,1,0:T(8,128)S(1)} %get-tuple-element.40, f32[22,38,512]{2,1,0:T(8,128)S(1)} %maximum_maximum_fusion.1, ...), kind=kLoop, calls=%fused_computation.12 | loop fusion | flops 2568192 | bytes 10273280 | tf_op jit(solution)/shard_map/add | solution.py:225
  41.5 0.4 copy-done.1
  41.9 0.5 slice-done
  42.4 3.4 %fusion.7 = f32[20,38,512]{2,1,0:T(8,128)S(1)} fusion(f32[20,38,512]{2,1,0:T(8,128)S(1)} %slice-done, f32[22,38,512]{2,1,0:T(8,128)S(1)} %get-tuple-element.36, f32[22,38,512]{2,1,0:T(8,128)S(1)} %get-tuple-element.37, f32[22,38,512]{2,1,0:T(8,128)S(1)} %get-tuple-element.41, f32[22,38,512]{2,1,0:T(8,128)S(1)} %get-tuple-element.42, ...), kind=kLoop, calls=%fused_computation.67 | loop fusion | flops 8560640 | bytes 23429120 | tf_op jit(solution)/shard_map/jit(_where)/select_n | solution.py:235
  45.7 0.5 fusion.206
  46.4 2.9 %slice_select_fusion = f32[18,38,512]{2,1,0:T(8,128)S(1)} fusion(pred[22,38,512]{2,1,0:T(8,128)(4,1)S(1)} %broadcast_and_fusion, f32[18,38,512]{2,1,0:T(8,128)S(1)} %slice.620, f32[22,38,512]{2,1,0:T(8,128)S(1)} %get-tuple-element.36, f32[18,38,511]{2,1,0:T(8,128)S(1)} %get-tuple-element.44, f32[22,38,512]{2,1,0:T(8,128)S(1)} %get-tuple-element.37, ...), kind=kLoop, calls=%fused_computation.98 | loop fusion | flops 7704576 | bytes 21266432 | tf_op jit(solution)/shard_map/jit(_where)/select_n | solution.py:235
  49.3 0.5 fusion.207
  49.7 1.8 %fusion.30 = (f32[16,32,512]{2,1,0:T(8,128)S(1)}, f32[16,32,512]{2,1,0:T(8,128)S(1)}) fusion(f32[16,32,512]{2,1,0:T(8,128)S(1)} %copy-done.3, f32[22,38,512]{2,1,0:T(8,128)S(1)} %get-tuple-element.37, f32[22,38,512]{2,1,0:T(8,128)S(1)} %get-tuple-element.41, f32[18,38,512]{2,1,0:T(8,128)S(1)} %slice_select_fusion, f32[22,38,512]{2,1,0:T(8,128)S(1)} %get-tuple-element.42, ...), kind=kLoop, calls=%fused_computation.106 | loop fusion | flops 4718592 | bytes 16773120 | tf_op jit(solution)/shard_map/sub | solution.py:247
  51.6 0.5 fusion.181
  52.3 6.9 %collective-permute-start.6 = (f32[2,4,8,128]{3,2,1,0:T(8,128)S(1)}, f32[2,4,8,128]{3,2,1,0:T(8,128)S(1)}, u32[]{:S(2)}, u32[]{:S(2)}) collective-permute-start(f32[2,4,8,128]{3,2,1,0:T(8,128)S(1)} %pad_maximum_fusion.7), channel_id=1, source_target_pairs={{0,16},{8,24},{16,32},{24,40},{32,48},{40,56},{48,64},{56,72},{64,... | collective-permute-start | bytes 98312 | tf_op jit(solution)/shard_map/ppermute | solution.py:25
  59.2 1.9 %collective-permute-start.7 = (f32[2,4,8,128]{3,2,1,0:T(8,128)S(1)}, f32[2,4,8,128]{3,2,1,0:T(8,128)S(1)}, u32[]{:S(2)}, u32[]{:S(2)}) collective-permute-start(f32[2,4,8,128]{3,2,1,0:T(8,128)S(1)} %pad_maximum_fusion.7), channel_id=1, source_target_pairs={{0,8},{8,16},{16,24},{24,32},{32,40},{40,48},{48,56},{56,64},{64,7... | collective-permute-start | bytes 98312 | tf_op jit(solution)/shard_map/ppermute | solution.py:25
  61.1 6.0 %collective-permute-start.8 = (f32[2,4,8,128]{3,2,1,0:T(8,128)S(1)}, f32[2,4,8,128]{3,2,1,0:T(8,128)S(1)}, u32[]{:S(2)}, u32[]{:S(2)}) collective-permute-start(f32[2,4,8,128]{3,2,1,0:T(8,128)S(1)} %pad_maximum_fusion.7), channel_id=1, source_target_pairs={{8,0},{16,8},{24,16},{32,24},{40,32},{48,40},{56,48},{64,56},{72,6... | collective-permute-start | bytes 98312 | tf_op jit(solution)/shard_map/ppermute | solution.py:26
  67.2 1.9 %collective-permute-start.9 = (f32[2,4,8,128]{3,2,1,0:T(8,128)S(1)}, f32[2,4,8,128]{3,2,1,0:T(8,128)S(1)}, u32[]{:S(2)}, u32[]{:S(2)}) collective-permute-start(f32[2,4,8,128]{3,2,1,0:T(8,128)S(1)} %pad_maximum_fusion.7), channel_id=1, source_target_pairs={{16,0},{24,8},{32,16},{40,24},{48,32},{56,40},{64,48},{72,56},{80,... | collective-permute-start | bytes 98312 | tf_op jit(solution)/shard_map/ppermute | solution.py:26
  69.2 5.3 %collective-permute-done.9 = f32[2,4,8,128]{3,2,1,0:T(8,128)S(1)} collective-permute-done((f32[2,4,8,128]{3,2,1,0:T(8,128)S(1)}, f32[2,4,8,128]{3,2,1,0:T(8,128)S(1)}, u32[]{:S(2)}, u32[]{:S(2)}) %collective-permute-start.9) | collective-permute-done | bytes 32800 | tf_op jit(solution)/shard_map/ppermute | solution.py:26
  74.5 4.0 %collective-permute-start.10 = (f32[2,20,8,128]{3,2,1,0:T(8,128)S(1)}, f32[2,20,8,128]{3,2,1,0:T(8,128)S(1)}, u32[]{:S(2)}, u32[]{:S(2)}) collective-permute-start(f32[2,20,8,128]{3,2,1,0:T(8,128)S(1)} %constant_dynamic-update-slice_fusion), channel_id=1, source_target_pairs={{0,1},{1,2},{2,3},{3,4},{4,5},{5,6},{6,7},{8,9},{9,10},{10,11},{11... | collective-permute-start | bytes 491528 | tf_op jit(solution)/shard_map/ppermute | solution.py:25
  78.5 2.1 %collective-permute-start.11 = (f32[2,20,8,128]{3,2,1,0:T(8,128)S(1)}, f32[2,20,8,128]{3,2,1,0:T(8,128)S(1)}, u32[]{:S(2)}, u32[]{:S(2)}) collective-permute-start(f32[2,20,8,128]{3,2,1,0:T(8,128)S(1)} %constant_dynamic-update-slice_fusion), channel_id=1, source_target_pairs={{1,0},{2,1},{3,2},{4,3},{5,4},{6,5},{7,6},{9,8},{10,9},{11,10},{12... | collective-permute-start | bytes 491528 | tf_op jit(solution)/shard_map/ppermute | solution.py:26
  80.6 2.5 %collective-permute-done.10 = f32[2,20,8,128]{3,2,1,0:T(8,128)S(1)} collective-permute-done((f32[2,20,8,128]{3,2,1,0:T(8,128)S(1)}, f32[2,20,8,128]{3,2,1,0:T(8,128)S(1)}, u32[]{:S(2)}, u32[]{:S(2)}) %collective-permute-start.10) | collective-permute-done | bytes 163872 | tf_op jit(solution)/shard_map/ppermute | solution.py:25
  83.1 3.4 %collective-permute-done.11 = f32[2,20,8,128]{3,2,1,0:T(8,128)S(1)} collective-permute-done((f32[2,20,8,128]{3,2,1,0:T(8,128)S(1)}, f32[2,20,8,128]{3,2,1,0:T(8,128)S(1)}, u32[]{:S(2)}, u32[]{:S(2)}) %collective-permute-start.11) | collective-permute-done | bytes 163872 | tf_op jit(solution)/shard_map/ppermute | solution.py:26
  86.7 0.5 fusion.166
  87.2 0.3 fusion.167
  88.0 0.3 multiply_add_fusion.2
  88.6 0.3 multiply_add_fusion
  89.1 0.5 fusion.170
  89.6 0.3 convolution_bitcast_fusion
  89.9 1.1 %bitcast_add_fusion = f32[16,32,512]{2,1,0:T(8,128)} fusion(f32[16,32,512]{2,1,0:T(8,128)S(1)} %get-tuple-element.13, f32[4,32,512]{2,1,0:T(8,128)S(1)} %convolution_bitcast_fusion), kind=kLoop, calls=%fused_computation.120 | loop fusion | flops 262144 | bytes 2359296 | tf_op jit(solution)/shard_map/add | solution.py:252
  (53 shorter events, 2.7 us)
Async XLA Ops:
  0.0 10.8 %copy-start.2 = (f32[16,32,512]{2,1,0:T(8,128)S(1)}, f32[16,32,512]{2,1,0:T(8,128)}, u32[]{:S(2)}) copy-start(f32[16,32,512]{2,1,0:T(8,128)} %param.4) | copy-start | bytes 3145732
  0.0 10.8 %copy-start.4 = (f32[16,32,512]{2,1,0:T(8,128)S(1)}, f32[16,32,512]{2,1,0:T(8,128)}, u32[]{:S(2)}) copy-start(f32[16,32,512]{2,1,0:T(8,128)} %param.5) | copy-start | bytes 3145732
  1.2 9.6 %copy-start.3 = (f32[16,32,512]{2,1,0:T(8,128)S(1)}, f32[16,32,512]{2,1,0:T(8,128)}, u32[]{:S(2)}) copy-start(f32[16,32,512]{2,1,0:T(8,128)} %param.3) | copy-start | bytes 3145732
  3.4 18.2 %collective-permute-start = (f32[16,8,512]{2,1,0:T(8,128)}, f32[16,8,512]{2,1,0:T(8,128)}, u32[]{:S(2)}, u32[]{:S(2)}) collective-permute-start(f32[16,8,512]{2,1,0:T(8,128)} %pad_maximum_fusion.3), channel_id=1, source_target_pairs={{0,1},{1,2},{2,3},{3,4},{4,5},{5,6},{6,7},{8,9},{9,10},{10,11},{11... | collective-permute-start | bytes 786440 | tf_op jit(solution)/shard_map/ppermute | solution.py:58
  7.3 15.2 %collective-permute-start.1 = (f32[16,8,512]{2,1,0:T(8,128)}, f32[16,8,512]{2,1,0:T(8,128)}, u32[]{:S(2)}, u32[]{:S(2)}) collective-permute-start(f32[16,8,512]{2,1,0:T(8,128)} %pad_maximum_fusion.4), channel_id=1, source_target_pairs={{1,0},{2,1},{3,2},{4,3},{5,4},{6,5},{7,6},{9,8},{10,9},{11,10},{12... | collective-permute-start | bytes 786440 | tf_op jit(solution)/shard_map/ppermute | solution.py:58
  11.8 22.6 %collective-permute-start.3 = (f32[8,32,512]{2,1,0:T(8,128)}, f32[8,32,512]{2,1,0:T(8,128)}, u32[]{:S(2)}, u32[]{:S(2)}) collective-permute-start(f32[8,32,512]{2,1,0:T(8,128)} %pad_maximum_fusion), channel_id=1, source_target_pairs={{0,8},{8,16},{16,24},{24,32},{32,40},{40,48},{48,56},{56,64},{64,7... | collective-permute-start | bytes 1572872 | tf_op jit(solution)/shard_map/ppermute | solution.py:58
  14.5 21.0 %collective-permute-start.5 = (f32[8,32,512]{2,1,0:T(8,128)}, f32[8,32,512]{2,1,0:T(8,128)}, u32[]{:S(2)}, u32[]{:S(2)}) collective-permute-start(f32[8,32,512]{2,1,0:T(8,128)} %pad_maximum_fusion.1), channel_id=1, source_target_pairs={{8,0},{16,8},{24,16},{32,24},{40,32},{48,40},{56,48},{64,56},{72,6... | collective-permute-start | bytes 1572872 | tf_op jit(solution)/shard_map/ppermute | solution.py:58
  23.3 10.6 %collective-permute-start.2 = (f32[3,16,512]{2,1,0:T(8,128)S(1)}, f32[3,16,512]{2,1,0:T(8,128)S(1)}, u32[]{:S(2)}, u32[]{:S(2)}) collective-permute-start(f32[3,16,512]{2,1,0:T(8,128)S(1)} %pad_maximum_fusion.5), channel_id=1, source_target_pairs={{0,8},{8,16},{16,24},{24,32},{32,40},{40,48},{48,56},{56,64},{64,7... | collective-permute-start | bytes 294920 | tf_op jit(solution)/shard_map/ppermute | solution.py:58
  25.2 9.1 %collective-permute-start.4 = (f32[3,16,512]{2,1,0:T(8,128)S(1)}, f32[3,16,512]{2,1,0:T(8,128)S(1)}, u32[]{:S(2)}, u32[]{:S(2)}) collective-permute-start(f32[3,16,512]{2,1,0:T(8,128)S(1)} %pad_maximum_fusion.6), channel_id=1, source_target_pairs={{8,0},{16,8},{24,16},{32,24},{40,32},{48,40},{56,48},{64,56},{72,6... | collective-permute-start | bytes 294920 | tf_op jit(solution)/shard_map/ppermute | solution.py:58
  37.0 1.3 %copy-start = (f32[22,38,512]{2,1,0:T(8,128)}, f32[22,38,512]{2,1,0:T(8,128)S(1)}, u32[]{:S(2)}) copy-start(f32[22,38,512]{2,1,0:T(8,128)S(1)} %maximum_maximum_fusion.2) | copy-start | bytes 5136388
  40.4 1.5 %copy-start.1 = (f32[22,38,512]{2,1,0:T(8,128)S(1)}, f32[22,38,512]{2,1,0:T(8,128)}, u32[]{:S(2)}) copy-start(f32[22,38,512]{2,1,0:T(8,128)} %copy-done) | copy-start | bytes 5136388
  40.4 2.0 %slice-start = ((f32[22,38,512]{2,1,0:T(8,128)}), f32[20,38,512]{2,1,0:T(8,128)S(1)}, s32[]{:S(2)}) async-start(f32[22,38,512]{2,1,0:T(8,128)} %copy-done), calls=%async_computation | async-start | bytes 3276800 | tf_op jit(solution)/shard_map/slice | solution.py:230
  52.3 16.8 %collective-permute-start.6 = (f32[2,4,8,128]{3,2,1,0:T(8,128)S(1)}, f32[2,4,8,128]{3,2,1,0:T(8,128)S(1)}, u32[]{:S(2)}, u32[]{:S(2)}) collective-permute-start(f32[2,4,8,128]{3,2,1,0:T(8,128)S(1)} %pad_maximum_fusion.7), channel_id=1, source_target_pairs={{0,16},{8,24},{16,32},{24,40},{32,48},{40,56},{48,64},{56,72},{64,... | collective-permute-start | bytes 98312 | tf_op jit(solution)/shard_map/ppermute | solution.py:25
  59.2 9.9 %collective-permute-start.7 = (f32[2,4,8,128]{3,2,1,0:T(8,128)S(1)}, f32[2,4,8,128]{3,2,1,0:T(8,128)S(1)}, u32[]{:S(2)}, u32[]{:S(2)}) collective-permute-start(f32[2,4,8,128]{3,2,1,0:T(8,128)S(1)} %pad_maximum_fusion.7), channel_id=1, source_target_pairs={{0,8},{8,16},{16,24},{24,32},{32,40},{40,48},{48,56},{56,64},{64,7... | collective-permute-start | bytes 98312 | tf_op jit(solution)/shard_map/ppermute | solution.py:25
  61.1 8.0 %collective-permute-start.8 = (f32[2,4,8,128]{3,2,1,0:T(8,128)S(1)}, f32[2,4,8,128]{3,2,1,0:T(8,128)S(1)}, u32[]{:S(2)}, u32[]{:S(2)}) collective-permute-start(f32[2,4,8,128]{3,2,1,0:T(8,128)S(1)} %pad_maximum_fusion.7), channel_id=1, source_target_pairs={{8,0},{16,8},{24,16},{32,24},{40,32},{48,40},{56,48},{64,56},{72,6... | collective-permute-start | bytes 98312 | tf_op jit(solution)/shard_map/ppermute | solution.py:26
  67.2 7.3 %collective-permute-start.9 = (f32[2,4,8,128]{3,2,1,0:T(8,128)S(1)}, f32[2,4,8,128]{3,2,1,0:T(8,128)S(1)}, u32[]{:S(2)}, u32[]{:S(2)}) collective-permute-start(f32[2,4,8,128]{3,2,1,0:T(8,128)S(1)} %pad_maximum_fusion.7), channel_id=1, source_target_pairs={{16,0},{24,8},{32,16},{40,24},{48,32},{56,40},{64,48},{72,56},{80,... | collective-permute-start | bytes 98312 | tf_op jit(solution)/shard_map/ppermute | solution.py:26
  74.5 8.7 %collective-permute-start.10 = (f32[2,20,8,128]{3,2,1,0:T(8,128)S(1)}, f32[2,20,8,128]{3,2,1,0:T(8,128)S(1)}, u32[]{:S(2)}, u32[]{:S(2)}) collective-permute-start(f32[2,20,8,128]{3,2,1,0:T(8,128)S(1)} %constant_dynamic-update-slice_fusion), channel_id=1, source_target_pairs={{0,1},{1,2},{2,3},{3,4},{4,5},{5,6},{6,7},{8,9},{9,10},{10,11},{11... | collective-permute-start | bytes 491528 | tf_op jit(solution)/shard_map/ppermute | solution.py:25
  78.5 8.1 %collective-permute-start.11 = (f32[2,20,8,128]{3,2,1,0:T(8,128)S(1)}, f32[2,20,8,128]{3,2,1,0:T(8,128)S(1)}, u32[]{:S(2)}, u32[]{:S(2)}) collective-permute-start(f32[2,20,8,128]{3,2,1,0:T(8,128)S(1)} %constant_dynamic-update-slice_fusion), channel_id=1, source_target_pairs={{1,0},{2,1},{3,2},{4,3},{5,4},{6,5},{7,6},{9,8},{10,9},{11,10},{12... | collective-permute-start | bytes 491528 | tf_op jit(solution)/shard_map/ppermute | solution.py:26

commit v16 on v14

--- a/solution.py
+++ b/solution.py
@@ -223,9 +223,11 @@
     inside = grid_mask(fine.shape, depth, ("box", "group"), totals)
     coefs = shared_faces(b_e)
     diag = sum(coefs)
+    weight = jnp.where(inside, 2.0 / 3.0 / jnp.where(inside, diag, 1.0), 0.0)
+    lift = weight * rhs_e
     for sweep in range(SWEEPS):
-        step = 2.0 / 3.0 * (rhs_e - apply_op(fine, padded_neighbours(jnp.pad(fine, 1)), coefs)) / diag
-        fine = jnp.where(inside, fine + step, 0.0)
+        pull = sum(c * n for c, n in zip(coefs, padded_neighbours(jnp.pad(fine, 1))))
+        fine = jnp.where(inside, fine * (1.0 / 3.0) + lift + weight * pull, 0.0)
     own = (slice(depth, depth + sx), slice(depth, depth + sy))
     core = fine[own]
     nears = [

time: 90.3 us -> 90.2 us (level)
  no operation moved by 1% of the time
where the time goes in v16:
time: 90.2 us; the launch traced here: 89.3 us
  starting transfers between devices  45.2 us (50%)
  other arithmetic  19.8 us (22%)
  waiting for transfers between devices  11.9 us (13%)
  local copies, waits for them, and re-layouts  9.76 us (11%)
  matrix products  2.05 us (2%)
    ppermute x6, starting transfers between devices, send(): return lax.ppermute(msg, axis, pairs)  22.4 us
    ppermute x3, starting transfers between devices, halo_from(): lax.ppermute(lax.slice_in_dim(block, n - width, n, axis=dim), axis, forward)  12.7 us
    ppermute x3, starting transfers between devices, halo_from(): lax.ppermute(lax.slice_in_dim(block, 0, width, axis=dim), axis, backward)  10.1 us
    ppermute x3, waiting for transfers between devices, halo_from(): lax.ppermute(lax.slice_in_dim(block, 0, width, axis=dim), axis, backward)  8.75 us
    select_n x2, other arithmetic, per_device(): fine = jnp.where(inside, fine * (1.0 / 3.0) + lift + weight * pull, 0.0)  7.83 us
    slice x6, local copies, waits for them, and re-layouts, packed_halo(): lax.slice_in_dim(f, f.shape[dim] - d, f.shape[dim], axis=dim)  4.36 us
    concatenate x6, other arithmetic, send(): msg = jnp.concatenate(pieces, axis=dim)  3.31 us
    ppermute x3, waiting for transfers between devices, halo_from(): lax.ppermute(lax.slice_in_dim(block, n - width, n, axis=dim), axis, forward)  2.53 us
  transfers between devices with their start and end apart: 12, of which 4 were waited for; matrix products, arithmetic and copies ran while one was open for 10% of the time, Pallas kernels for 0%

profile of v16, /device:TPU:34, one launch (start us, length us, event | category | flops | bytes accessed | tf_op | source)
XLA Modules:
  0.0 89.3 jit_solution(3874844463868350371)
XLA Ops:
  0.0 1.2 %fusion.212 = (f32[16,2,512]{2,1,0:T(2,128)S(1)}, f32[16,2,512]{2,1,0:T(2,128)S(1)}) fusion(f32[16,32,512]{2,1,0:T(8,128)} %param.3), kind=kLoop, calls=%fused_computation.337 | loop fusion | bytes 262144 | tf_op jit(solution)/shard_map/slice | solution.py:48
  1.2 1.4 %fusion.211 = (f32[16,3,512]{2,1,0:T(4,128)S(1)}, f32[16,3,512]{2,1,0:T(4,128)S(1)}, f32[16,3,512]{2,1,0:T(4,128)S(1)}, f32[16,3,512]{2,1,0:T(4,128)S(1)}) fusion(f32[16,32,512]{2,1,0:T(8,128)} %param.4, f32[16,32,512]{2,1,0:T(8,128)} %param.5), kind=kLoop, calls=%fused_computation.336 | loop fusion | bytes 786432 | tf_op jit(solution)/shard_map/slice | solution.py:48
  2.6 0.8 pad_maximum_fusion.3
  3.4 3.0 %collective-permute-start = (f32[16,8,512]{2,1,0:T(8,128)}, f32[16,8,512]{2,1,0:T(8,128)}, u32[]{:S(2)}, u32[]{:S(2)}) collective-permute-start(f32[16,8,512]{2,1,0:T(8,128)} %pad_maximum_fusion.3), channel_id=1, source_target_pairs={{0,1},{1,2},{2,3},{3,4},{4,5},{5,6},{6,7},{8,9},{9,10},{10,11},{11... | collective-permute-start | bytes 786440 | tf_op jit(solution)/shard_map/ppermute | solution.py:58
  6.5 0.8 pad_maximum_fusion.4
  7.3 3.5 %collective-permute-start.1 = (f32[16,8,512]{2,1,0:T(8,128)}, f32[16,8,512]{2,1,0:T(8,128)}, u32[]{:S(2)}, u32[]{:S(2)}) collective-permute-start(f32[16,8,512]{2,1,0:T(8,128)} %pad_maximum_fusion.4), channel_id=1, source_target_pairs={{1,0},{2,1},{3,2},{4,3},{5,4},{6,5},{7,6},{9,8},{10,9},{11,10},{12... | collective-permute-start | bytes 786440 | tf_op jit(solution)/shard_map/ppermute | solution.py:58
  10.9 0.9 pad_maximum_fusion
  11.8 1.9 %collective-permute-start.3 = (f32[8,32,512]{2,1,0:T(8,128)}, f32[8,32,512]{2,1,0:T(8,128)}, u32[]{:S(2)}, u32[]{:S(2)}) collective-permute-start(f32[8,32,512]{2,1,0:T(8,128)} %pad_maximum_fusion), channel_id=1, source_target_pairs={{0,8},{8,16},{16,24},{24,32},{32,40},{40,48},{48,56},{56,64},{64,7... | collective-permute-start | bytes 1572872 | tf_op jit(solution)/shard_map/ppermute | solution.py:58
  13.7 0.8 pad_maximum_fusion.1
  14.5 6.0 %collective-permute-start.5 = (f32[8,32,512]{2,1,0:T(8,128)}, f32[8,32,512]{2,1,0:T(8,128)}, u32[]{:S(2)}, u32[]{:S(2)}) collective-permute-start(f32[8,32,512]{2,1,0:T(8,128)} %pad_maximum_fusion.1), channel_id=1, source_target_pairs={{8,0},{16,8},{24,16},{32,24},{40,32},{48,40},{56,48},{64,56},{72,6... | collective-permute-start | bytes 1572872 | tf_op jit(solution)/shard_map/ppermute | solution.py:58
  20.7 0.5 fusion.184
  21.4 0.8 fusion.218
  22.2 0.8 fusion.219
  23.1 1.9 %collective-permute-start.2 = (f32[3,16,512]{2,1,0:T(8,128)S(1)}, f32[3,16,512]{2,1,0:T(8,128)S(1)}, u32[]{:S(2)}, u32[]{:S(2)}) collective-permute-start(f32[3,16,512]{2,1,0:T(8,128)S(1)} %pad_maximum_fusion.5), channel_id=1, source_target_pairs={{0,8},{8,16},{16,24},{24,32},{32,40},{40,48},{48,56},{56,64},{64,7... | collective-permute-start | bytes 294920 | tf_op jit(solution)/shard_map/ppermute | solution.py:58
  25.0 6.0 %collective-permute-start.4 = (f32[3,16,512]{2,1,0:T(8,128)S(1)}, f32[3,16,512]{2,1,0:T(8,128)S(1)}, u32[]{:S(2)}, u32[]{:S(2)}) collective-permute-start(f32[3,16,512]{2,1,0:T(8,128)S(1)} %pad_maximum_fusion.6), channel_id=1, source_target_pairs={{8,0},{16,8},{24,16},{32,24},{40,32},{48,40},{56,48},{64,56},{72,6... | collective-permute-start | bytes 294920 | tf_op jit(solution)/shard_map/ppermute | solution.py:58
  31.1 1.2 %fusion.216 = (f32[16,3,512]{2,1,0:T(4,128)S(1)}, f32[16,3,512]{2,1,0:T(4,128)S(1)}, f32[16,3,512]{2,1,0:T(4,128)S(1)}) fusion(f32[16,8,512]{2,1,0:T(8,128)} %collective-permute-done), kind=kLoop, calls=%fused_computation.341 | loop fusion | bytes 589824 | tf_op jit(solution)/shard_map/slice | solution.py:75
  32.3 1.3 %fusion.217 = (f32[16,3,512]{2,1,0:T(4,128)S(1)}, f32[16,3,512]{2,1,0:T(4,128)S(1)}, f32[16,3,512]{2,1,0:T(4,128)S(1)}) fusion(f32[16,8,512]{2,1,0:T(8,128)} %collective-permute-done.1), kind=kLoop, calls=%fused_computation.342 | loop fusion | bytes 589824 | tf_op jit(solution)/shard_map/slice | solution.py:75
  33.7 0.6 collective-permute-done.4
  34.3 1.2 %fusion.214 = (f32[3,32,512]{2,1,0:T(8,128)S(1)}, f32[3,32,512]{2,1,0:T(8,128)S(1)}, f32[3,32,512]{2,1,0:T(8,128)S(1)}) fusion(f32[8,32,512]{2,1,0:T(8,128)} %collective-permute-done.3), kind=kLoop, calls=%fused_computation.339 | loop fusion | bytes 1179648 | tf_op jit(solution)/shard_map/slice | solution.py:74
  35.5 1.2 %fusion.215 = (f32[3,32,512]{2,1,0:T(8,128)S(1)}, f32[3,32,512]{2,1,0:T(8,128)S(1)}, f32[3,32,512]{2,1,0:T(8,128)S(1)}) fusion(f32[8,32,512]{2,1,0:T(8,128)} %collective-permute-done.5), kind=kLoop, calls=%fused_computation.340 | loop fusion | bytes 1179648 | tf_op jit(solution)/shard_map/slice | solution.py:76
  36.7 0.3 maximum_maximum_fusion.2
  37.0 0.3 maximum_maximum_fusion.1
  37.3 0.3 maximum_maximum_fusion
  37.6 2.1 %divide_select_fusion = (f32[22,38,512]{2,1,0:T(8,128)S(1)}, f32[22,38,512]{2,1,0:T(8,128)S(1)}, f32[22,38,512]{2,1,0:T(8,128)S(1)}) fusion(f32[22,38,512]{2,1,0:T(8,128)S(1)} %maximum_maximum_fusion.1), kind=kLoop, calls=%fused_computation.19 | loop fusion | flops 8560640 | bytes 6848512 | tf_op jit(solution)/shard_map/jit(_where)/select_n | solution.py:184
  39.7 4.1 %and_select_fusion.1 = (f32[22,38,512]{2,1,0:T(8,128)S(1)}, f32[22,38,512]{2,1,0:T(8,128)S(1)}) fusion(f32[22,38,512]{2,1,0:T(8,128)S(1)} %get-tuple-element.43, f32[22,38,512]{2,1,0:T(8,128)S(1)} %maximum_maximum_fusion.2, f32[22,38,512]{2,1,0:T(8,128)S(1)} %get-tuple-element.44, f32[22,38,512]{2,1,0:T(8,128)S(1)} %get-tuple-element.42, ...), kind=kLoop, calls=%fused_computation.13 | loop fusion | flops 11556864 | bytes 13697596 | tf_op jit(solution)/shard_map/jit(_where)/select_n | solution.py:230
  43.8 3.8 %and_select_fusion = f32[22,38,512]{2,1,0:T(8,128)S(1)} fusion(f32[22,38,512]{2,1,0:T(8,128)S(1)} %get-tuple-element.43, f32[22,38,512]{2,1,0:T(8,128)S(1)} %get-tuple-element.36, f32[22,38,512]{2,1,0:T(8,128)S(1)} %get-tuple-element.44, f32[22,38,512]{2,1,0:T(8,128)S(1)} %get-tuple-element.42, f32[22,38,512]{2,1,0:T(8,128)S(1)} %get-tuple-element.37, ...), kind=kLoop, calls=%fused_computation.12 | loop fusion | flops 11128832 | bytes 11984956 | tf_op jit(solution)/shard_map/jit(_where)/select_n | solution.py:230
  47.6 0.5 fusion.207
  48.0 1.8 %fusion.31 = (f32[16,32,512]{2,1,0:T(8,128)S(1)}, f32[16,32,512]{2,1,0:T(8,128)S(1)}) fusion(f32[16,32,512]{2,1,0:T(8,128)S(1)} %copy-done.1, f32[22,38,512]{2,1,0:T(8,128)S(1)} %get-tuple-element.37, f32[22,38,512]{2,1,0:T(8,128)S(1)} %get-tuple-element.42, f32[22,38,512]{2,1,0:T(8,128)S(1)} %and_select_fusion, f32[22,38,512]{2,1,0:T(8,128)S(1)} %get-tuple-element.44, ...), kind=kLoop, calls=%fused_computation.111 | loop fusion | flops 4718592 | bytes 16773120 | tf_op jit(solution)/shard_map/sub | solution.py:241
  49.9 0.5 fusion.182
  50.6 6.9 %collective-permute-start.6 = (f32[2,4,8,128]{3,2,1,0:T(8,128)S(1)}, f32[2,4,8,128]{3,2,1,0:T(8,128)S(1)}, u32[]{:S(2)}, u32[]{:S(2)}) collective-permute-start(f32[2,4,8,128]{3,2,1,0:T(8,128)S(1)} %pad_maximum_fusion.7), channel_id=1, source_target_pairs={{0,16},{8,24},{16,32},{24,40},{32,48},{40,56},{48,64},{56,72},{64,... | collective-permute-start | bytes 98312 | tf_op jit(solution)/shard_map/ppermute | solution.py:25
  57.4 1.9 %collective-permute-start.7 = (f32[2,4,8,128]{3,2,1,0:T(8,128)S(1)}, f32[2,4,8,128]{3,2,1,0:T(8,128)S(1)}, u32[]{:S(2)}, u32[]{:S(2)}) collective-permute-start(f32[2,4,8,128]{3,2,1,0:T(8,128)S(1)} %pad_maximum_fusion.7), channel_id=1, source_target_pairs={{0,8},{8,16},{16,24},{24,32},{32,40},{40,48},{48,56},{56,64},{64,7... | collective-permute-start | bytes 98312 | tf_op jit(solution)/shard_map/ppermute | solution.py:25
  59.4 6.0 %collective-permute-start.8 = (f32[2,4,8,128]{3,2,1,0:T(8,128)S(1)}, f32[2,4,8,128]{3,2,1,0:T(8,128)S(1)}, u32[]{:S(2)}, u32[]{:S(2)}) collective-permute-start(f32[2,4,8,128]{3,2,1,0:T(8,128)S(1)} %pad_maximum_fusion.7), channel_id=1, source_target_pairs={{8,0},{16,8},{24,16},{32,24},{40,32},{48,40},{56,48},{64,56},{72,6... | collective-permute-start | bytes 98312 | tf_op jit(solution)/shard_map/ppermute | solution.py:26
  65.4 1.9 %collective-permute-start.9 = (f32[2,4,8,128]{3,2,1,0:T(8,128)S(1)}, f32[2,4,8,128]{3,2,1,0:T(8,128)S(1)}, u32[]{:S(2)}, u32[]{:S(2)}) collective-permute-start(f32[2,4,8,128]{3,2,1,0:T(8,128)S(1)} %pad_maximum_fusion.7), channel_id=1, source_target_pairs={{16,0},{24,8},{32,16},{40,24},{48,32},{56,40},{64,48},{72,56},{80,... | collective-permute-start | bytes 98312 | tf_op jit(solution)/shard_map/ppermute | solution.py:26
  67.4 5.3 %collective-permute-done.9 = f32[2,4,8,128]{3,2,1,0:T(8,128)S(1)} collective-permute-done((f32[2,4,8,128]{3,2,1,0:T(8,128)S(1)}, f32[2,4,8,128]{3,2,1,0:T(8,128)S(1)}, u32[]{:S(2)}, u32[]{:S(2)}) %collective-permute-start.9) | collective-permute-done | bytes 32800 | tf_op jit(solution)/shard_map/ppermute | solution.py:26
  72.7 4.0 %collective-permute-start.10 = (f32[2,20,8,128]{3,2,1,0:T(8,128)S(1)}, f32[2,20,8,128]{3,2,1,0:T(8,128)S(1)}, u32[]{:S(2)}, u32[]{:S(2)}) collective-permute-start(f32[2,20,8,128]{3,2,1,0:T(8,128)S(1)} %constant_dynamic-update-slice_fusion), channel_id=1, source_target_pairs={{0,1},{1,2},{2,3},{3,4},{4,5},{5,6},{6,7},{8,9},{9,10},{10,11},{11... | collective-permute-start | bytes 491528 | tf_op jit(solution)/shard_map/ppermute | solution.py:25
  76.7 2.1 %collective-permute-start.11 = (f32[2,20,8,128]{3,2,1,0:T(8,128)S(1)}, f32[2,20,8,128]{3,2,1,0:T(8,128)S(1)}, u32[]{:S(2)}, u32[]{:S(2)}) collective-permute-start(f32[2,20,8,128]{3,2,1,0:T(8,128)S(1)} %constant_dynamic-update-slice_fusion), channel_id=1, source_target_pairs={{1,0},{2,1},{3,2},{4,3},{5,4},{6,5},{7,6},{9,8},{10,9},{11,10},{12... | collective-permute-start | bytes 491528 | tf_op jit(solution)/shard_map/ppermute | solution.py:26
  78.9 2.5 %collective-permute-done.10 = f32[2,20,8,128]{3,2,1,0:T(8,128)S(1)} collective-permute-done((f32[2,20,8,128]{3,2,1,0:T(8,128)S(1)}, f32[2,20,8,128]{3,2,1,0:T(8,128)S(1)}, u32[]{:S(2)}, u32[]{:S(2)}) %collective-permute-start.10) | collective-permute-done | bytes 163872 | tf_op jit(solution)/shard_map/ppermute | solution.py:25
  81.4 3.4 %collective-permute-done.11 = f32[2,20,8,128]{3,2,1,0:T(8,128)S(1)} collective-permute-done((f32[2,20,8,128]{3,2,1,0:T(8,128)S(1)}, f32[2,20,8,128]{3,2,1,0:T(8,128)S(1)}, u32[]{:S(2)}, u32[]{:S(2)}) %collective-permute-start.11) | collective-permute-done | bytes 163872 | tf_op jit(solution)/shard_map/ppermute | solution.py:26
  84.9 0.5 fusion.167
  85.4 0.3 fusion.168
  85.8 0.3 multiply_add_fusion.4
  86.0 0.3 multiply_add_fusion.3
  86.3 0.3 multiply_add_fusion.2
  86.6 0.3 multiply_add_fusion.1
  86.9 0.3 multiply_add_fusion
  87.4 0.5 fusion.171
  87.9 0.3 convolution_bitcast_fusion
  88.2 1.1 %bitcast_add_fusion = f32[16,32,512]{2,1,0:T(8,128)} fusion(f32[16,32,512]{2,1,0:T(8,128)S(1)} %get-tuple-element.13, f32[4,32,512]{2,1,0:T(8,128)S(1)} %convolution_bitcast_fusion), kind=kLoop, calls=%fused_computation.125 | loop fusion | flops 262144 | bytes 2359296 | tf_op jit(solution)/shard_map/add | solution.py:246
  (42 shorter events, 1.0 us)
Async XLA Ops:
  0.0 10.8 %copy-start = (f32[16,32,512]{2,1,0:T(8,128)S(1)}, f32[16,32,512]{2,1,0:T(8,128)}, u32[]{:S(2)}) copy-start(f32[16,32,512]{2,1,0:T(8,128)} %param.4) | copy-start | bytes 3145732
  0.0 10.8 %copy-start.2 = (f32[16,32,512]{2,1,0:T(8,128)S(1)}, f32[16,32,512]{2,1,0:T(8,128)}, u32[]{:S(2)}) copy-start(f32[16,32,512]{2,1,0:T(8,128)} %param.5) | copy-start | bytes 3145732
  1.2 9.6 %copy-start.1 = (f32[16,32,512]{2,1,0:T(8,128)S(1)}, f32[16,32,512]{2,1,0:T(8,128)}, u32[]{:S(2)}) copy-start(f32[16,32,512]{2,1,0:T(8,128)} %param.3) | copy-start | bytes 3145732
  3.4 18.0 %collective-permute-start = (f32[16,8,512]{2,1,0:T(8,128)}, f32[16,8,512]{2,1,0:T(8,128)}, u32[]{:S(2)}, u32[]{:S(2)}) collective-permute-start(f32[16,8,512]{2,1,0:T(8,128)} %pad_maximum_fusion.3), channel_id=1, source_target_pairs={{0,1},{1,2},{2,3},{3,4},{4,5},{5,6},{6,7},{8,9},{9,10},{10,11},{11... | collective-permute-start | bytes 786440 | tf_op jit(solution)/shard_map/ppermute | solution.py:58
  7.3 15.0 %collective-permute-start.1 = (f32[16,8,512]{2,1,0:T(8,128)}, f32[16,8,512]{2,1,0:T(8,128)}, u32[]{:S(2)}, u32[]{:S(2)}) collective-permute-start(f32[16,8,512]{2,1,0:T(8,128)} %pad_maximum_fusion.4), channel_id=1, source_target_pairs={{1,0},{2,1},{3,2},{4,3},{5,4},{6,5},{7,6},{9,8},{10,9},{11,10},{12... | collective-permute-start | bytes 786440 | tf_op jit(solution)/shard_map/ppermute | solution.py:58
  11.8 22.6 %collective-permute-start.3 = (f32[8,32,512]{2,1,0:T(8,128)}, f32[8,32,512]{2,1,0:T(8,128)}, u32[]{:S(2)}, u32[]{:S(2)}) collective-permute-start(f32[8,32,512]{2,1,0:T(8,128)} %pad_maximum_fusion), channel_id=1, source_target_pairs={{0,8},{8,16},{16,24},{24,32},{32,40},{40,48},{48,56},{56,64},{64,7... | collective-permute-start | bytes 1572872 | tf_op jit(solution)/shard_map/ppermute | solution.py:58
  14.5 21.0 %collective-permute-start.5 = (f32[8,32,512]{2,1,0:T(8,128)}, f32[8,32,512]{2,1,0:T(8,128)}, u32[]{:S(2)}, u32[]{:S(2)}) collective-permute-start(f32[8,32,512]{2,1,0:T(8,128)} %pad_maximum_fusion.1), channel_id=1, source_target_pairs={{8,0},{16,8},{24,16},{32,24},{40,32},{48,40},{56,48},{64,56},{72,6... | collective-permute-start | bytes 1572872 | tf_op jit(solution)/shard_map/ppermute | solution.py:58
  23.1 10.5 %collective-permute-start.2 = (f32[3,16,512]{2,1,0:T(8,128)S(1)}, f32[3,16,512]{2,1,0:T(8,128)S(1)}, u32[]{:S(2)}, u32[]{:S(2)}) collective-permute-start(f32[3,16,512]{2,1,0:T(8,128)S(1)} %pad_maximum_fusion.5), channel_id=1, source_target_pairs={{0,8},{8,16},{16,24},{24,32},{32,40},{40,48},{48,56},{56,64},{64,7... | collective-permute-start | bytes 294920 | tf_op jit(solution)/shard_map/ppermute | solution.py:58
  25.0 9.3 %collective-permute-start.4 = (f32[3,16,512]{2,1,0:T(8,128)S(1)}, f32[3,16,512]{2,1,0:T(8,128)S(1)}, u32[]{:S(2)}, u32[]{:S(2)}) collective-permute-start(f32[3,16,512]{2,1,0:T(8,128)S(1)} %pad_maximum_fusion.6), channel_id=1, source_target_pairs={{8,0},{16,8},{24,16},{32,24},{40,32},{48,40},{56,48},{64,56},{72,6... | collective-permute-start | bytes 294920 | tf_op jit(solution)/shard_map/ppermute | solution.py:58
  50.6 16.8 %collective-permute-start.6 = (f32[2,4,8,128]{3,2,1,0:T(8,128)S(1)}, f32[2,4,8,128]{3,2,1,0:T(8,128)S(1)}, u32[]{:S(2)}, u32[]{:S(2)}) collective-permute-start(f32[2,4,8,128]{3,2,1,0:T(8,128)S(1)} %pad_maximum_fusion.7), channel_id=1, source_target_pairs={{0,16},{8,24},{16,32},{24,40},{32,48},{40,56},{48,64},{56,72},{64,... | collective-permute-start | bytes 98312 | tf_op jit(solution)/shard_map/ppermute | solution.py:25
  57.4 9.9 %collective-permute-start.7 = (f32[2,4,8,128]{3,2,1,0:T(8,128)S(1)}, f32[2,4,8,128]{3,2,1,0:T(8,128)S(1)}, u32[]{:S(2)}, u32[]{:S(2)}) collective-permute-start(f32[2,4,8,128]{3,2,1,0:T(8,128)S(1)} %pad_maximum_fusion.7), channel_id=1, source_target_pairs={{0,8},{8,16},{16,24},{24,32},{32,40},{40,48},{48,56},{56,64},{64,7... | collective-permute-start | bytes 98312 | tf_op jit(solution)/shard_map/ppermute | solution.py:25
  59.4 8.0 %collective-permute-start.8 = (f32[2,4,8,128]{3,2,1,0:T(8,128)S(1)}, f32[2,4,8,128]{3,2,1,0:T(8,128)S(1)}, u32[]{:S(2)}, u32[]{:S(2)}) collective-permute-start(f32[2,4,8,128]{3,2,1,0:T(8,128)S(1)} %pad_maximum_fusion.7), channel_id=1, source_target_pairs={{8,0},{16,8},{24,16},{32,24},{40,32},{48,40},{56,48},{64,56},{72,6... | collective-permute-start | bytes 98312 | tf_op jit(solution)/shard_map/ppermute | solution.py:26
  65.4 7.3 %collective-permute-start.9 = (f32[2,4,8,128]{3,2,1,0:T(8,128)S(1)}, f32[2,4,8,128]{3,2,1,0:T(8,128)S(1)}, u32[]{:S(2)}, u32[]{:S(2)}) collective-permute-start(f32[2,4,8,128]{3,2,1,0:T(8,128)S(1)} %pad_maximum_fusion.7), channel_id=1, source_target_pairs={{16,0},{24,8},{32,16},{40,24},{48,32},{56,40},{64,48},{72,56},{80,... | collective-permute-start | bytes 98312 | tf_op jit(solution)/shard_map/ppermute | solution.py:26
  72.7 8.7 %collective-permute-start.10 = (f32[2,20,8,128]{3,2,1,0:T(8,128)S(1)}, f32[2,20,8,128]{3,2,1,0:T(8,128)S(1)}, u32[]{:S(2)}, u32[]{:S(2)}) collective-permute-start(f32[2,20,8,128]{3,2,1,0:T(8,128)S(1)} %constant_dynamic-update-slice_fusion), channel_id=1, source_target_pairs={{0,1},{1,2},{2,3},{3,4},{4,5},{5,6},{6,7},{8,9},{9,10},{10,11},{11... | collective-permute-start | bytes 491528 | tf_op jit(solution)/shard_map/ppermute | solution.py:25
  76.7 8.1 %collective-permute-start.11 = (f32[2,20,8,128]{3,2,1,0:T(8,128)S(1)}, f32[2,20,8,128]{3,2,1,0:T(8,128)S(1)}, u32[]{:S(2)}, u32[]{:S(2)}) collective-permute-start(f32[2,20,8,128]{3,2,1,0:T(8,128)S(1)} %constant_dynamic-update-slice_fusion), channel_id=1, source_target_pairs={{1,0},{2,1},{3,2},{4,3},{5,4},{6,5},{7,6},{9,8},{10,9},{11,10},{12... | collective-permute-start | bytes 491528 | tf_op jit(solution)/shard_map/ppermute | solution.py:26

commit v17 on v16

--- a/solution.py
+++ b/solution.py
@@ -225,8 +225,9 @@
     diag = sum(coefs)
     weight = jnp.where(inside, 2.0 / 3.0 / jnp.where(inside, diag, 1.0), 0.0)
     lift = weight * rhs_e
+    plain = coefs[:5] + [jnp.pad(coefs[4], ((0, 0), (0, 0), (0, 1)))[:, :, 1:]]
     for sweep in range(SWEEPS):
-        pull = sum(c * n for c, n in zip(coefs, padded_neighbours(jnp.pad(fine, 1))))
+        pull = sum(c * n for c, n in zip(plain, padded_neighbours(jnp.pad(fine, 1))))
         fine = jnp.where(inside, fine * (1.0 / 3.0) + lift + weight * pull, 0.0)
     own = (slice(depth, depth + sx), slice(depth, depth + sy))
     core = fine[own]

time: 90.2 us -> 90.2 us (level)
  no operation moved by 1% of the time
where the time goes in v17:
time: 90.2 us; the launch traced here: 89.4 us
  starting transfers between devices  45.3 us (50%)
  other arithmetic  19.8 us (22%)
  waiting for transfers between devices  11.9 us (13%)
  local copies, waits for them, and re-layouts  9.78 us (11%)
  matrix products  2.06 us (2%)
    ppermute x6, starting transfers between devices, send(): return lax.ppermute(msg, axis, pairs)  22.4 us
    ppermute x3, starting transfers between devices, halo_from(): lax.ppermute(lax.slice_in_dim(block, n - width, n, axis=dim), axis, forward)  12.8 us
    ppermute x3, starting transfers between devices, halo_from(): lax.ppermute(lax.slice_in_dim(block, 0, width, axis=dim), axis, backward)  10.1 us
    ppermute x3, waiting for transfers between devices, halo_from(): lax.ppermute(lax.slice_in_dim(block, 0, width, axis=dim), axis, backward)  8.75 us
    select_n x2, other arithmetic, per_device(): fine = jnp.where(inside, fine * (1.0 / 3.0) + lift + weight * pull, 0.0)  7.84 us
    slice x6, local copies, waits for them, and re-layouts, packed_halo(): lax.slice_in_dim(f, f.shape[dim] - d, f.shape[dim], axis=dim)  4.36 us
    concatenate x6, other arithmetic, send(): msg = jnp.concatenate(pieces, axis=dim)  3.31 us
    ppermute x3, waiting for transfers between devices, halo_from(): lax.ppermute(lax.slice_in_dim(block, n - width, n, axis=dim), axis, forward)  2.53 us
  transfers between devices with their start and end apart: 12, of which 4 were waited for; matrix products, arithmetic and copies ran while one was open for 10% of the time, Pallas kernels for 0%

profile of v17, /device:TPU:34, one launch (start us, length us, event | category | flops | bytes accessed | tf_op | source)
XLA Modules:
  0.0 89.4 jit_solution(4501383966365181655)
XLA Ops:
  0.0 1.2 %fusion.212 = (f32[16,2,512]{2,1,0:T(2,128)S(1)}, f32[16,2,512]{2,1,0:T(2,128)S(1)}) fusion(f32[16,32,512]{2,1,0:T(8,128)} %param.3), kind=kLoop, calls=%fused_computation.337 | loop fusion | bytes 262144 | tf_op jit(solution)/shard_map/slice | solution.py:48
  1.2 1.4 %fusion.211 = (f32[16,3,512]{2,1,0:T(4,128)S(1)}, f32[16,3,512]{2,1,0:T(4,128)S(1)}, f32[16,3,512]{2,1,0:T(4,128)S(1)}, f32[16,3,512]{2,1,0:T(4,128)S(1)}) fusion(f32[16,32,512]{2,1,0:T(8,128)} %param.4, f32[16,32,512]{2,1,0:T(8,128)} %param.5), kind=kLoop, calls=%fused_computation.336 | loop fusion | bytes 786432 | tf_op jit(solution)/shard_map/slice | solution.py:48
  2.6 0.8 pad_maximum_fusion.3
  3.4 3.0 %collective-permute-start = (f32[16,8,512]{2,1,0:T(8,128)}, f32[16,8,512]{2,1,0:T(8,128)}, u32[]{:S(2)}, u32[]{:S(2)}) collective-permute-start(f32[16,8,512]{2,1,0:T(8,128)} %pad_maximum_fusion.3), channel_id=1, source_target_pairs={{0,1},{1,2},{2,3},{3,4},{4,5},{5,6},{6,7},{8,9},{9,10},{10,11},{11... | collective-permute-start | bytes 786440 | tf_op jit(solution)/shard_map/ppermute | solution.py:58
  6.5 0.8 pad_maximum_fusion.4
  7.3 3.5 %collective-permute-start.1 = (f32[16,8,512]{2,1,0:T(8,128)}, f32[16,8,512]{2,1,0:T(8,128)}, u32[]{:S(2)}, u32[]{:S(2)}) collective-permute-start(f32[16,8,512]{2,1,0:T(8,128)} %pad_maximum_fusion.4), channel_id=1, source_target_pairs={{1,0},{2,1},{3,2},{4,3},{5,4},{6,5},{7,6},{9,8},{10,9},{11,10},{12... | collective-permute-start | bytes 786440 | tf_op jit(solution)/shard_map/ppermute | solution.py:58
  10.9 0.9 pad_maximum_fusion
  11.8 1.9 %collective-permute-start.3 = (f32[8,32,512]{2,1,0:T(8,128)}, f32[8,32,512]{2,1,0:T(8,128)}, u32[]{:S(2)}, u32[]{:S(2)}) collective-permute-start(f32[8,32,512]{2,1,0:T(8,128)} %pad_maximum_fusion), channel_id=1, source_target_pairs={{0,8},{8,16},{16,24},{24,32},{32,40},{40,48},{48,56},{56,64},{64,7... | collective-permute-start | bytes 1572872 | tf_op jit(solution)/shard_map/ppermute | solution.py:58
  13.7 0.8 pad_maximum_fusion.1
  14.5 6.0 %collective-permute-start.5 = (f32[8,32,512]{2,1,0:T(8,128)}, f32[8,32,512]{2,1,0:T(8,128)}, u32[]{:S(2)}, u32[]{:S(2)}) collective-permute-start(f32[8,32,512]{2,1,0:T(8,128)} %pad_maximum_fusion.1), channel_id=1, source_target_pairs={{8,0},{16,8},{24,16},{32,24},{40,32},{48,40},{56,48},{64,56},{72,6... | collective-permute-start | bytes 1572872 | tf_op jit(solution)/shard_map/ppermute | solution.py:58
  20.7 0.5 fusion.184
  21.4 0.8 fusion.218
  22.2 0.8 fusion.219
  23.1 1.9 %collective-permute-start.2 = (f32[3,16,512]{2,1,0:T(8,128)S(1)}, f32[3,16,512]{2,1,0:T(8,128)S(1)}, u32[]{:S(2)}, u32[]{:S(2)}) collective-permute-start(f32[3,16,512]{2,1,0:T(8,128)S(1)} %pad_maximum_fusion.5), channel_id=1, source_target_pairs={{0,8},{8,16},{16,24},{24,32},{32,40},{40,48},{48,56},{56,64},{64,7... | collective-permute-start | bytes 294920 | tf_op jit(solution)/shard_map/ppermute | solution.py:58
  25.0 6.0 %collective-permute-start.4 = (f32[3,16,512]{2,1,0:T(8,128)S(1)}, f32[3,16,512]{2,1,0:T(8,128)S(1)}, u32[]{:S(2)}, u32[]{:S(2)}) collective-permute-start(f32[3,16,512]{2,1,0:T(8,128)S(1)} %pad_maximum_fusion.6), channel_id=1, source_target_pairs={{8,0},{16,8},{24,16},{32,24},{40,32},{48,40},{56,48},{64,56},{72,6... | collective-permute-start | bytes 294920 | tf_op jit(solution)/shard_map/ppermute | solution.py:58
  31.1 1.2 %fusion.216 = (f32[16,3,512]{2,1,0:T(4,128)S(1)}, f32[16,3,512]{2,1,0:T(4,128)S(1)}, f32[16,3,512]{2,1,0:T(4,128)S(1)}) fusion(f32[16,8,512]{2,1,0:T(8,128)} %collective-permute-done), kind=kLoop, calls=%fused_computation.341 | loop fusion | bytes 589824 | tf_op jit(solution)/shard_map/slice | solution.py:75
  32.3 1.3 %fusion.217 = (f32[16,3,512]{2,1,0:T(4,128)S(1)}, f32[16,3,512]{2,1,0:T(4,128)S(1)}, f32[16,3,512]{2,1,0:T(4,128)S(1)}) fusion(f32[16,8,512]{2,1,0:T(8,128)} %collective-permute-done.1), kind=kLoop, calls=%fused_computation.342 | loop fusion | bytes 589824 | tf_op jit(solution)/shard_map/slice | solution.py:75
  33.7 0.6 collective-permute-done.4
  34.3 1.2 %fusion.214 = (f32[3,32,512]{2,1,0:T(8,128)S(1)}, f32[3,32,512]{2,1,0:T(8,128)S(1)}, f32[3,32,512]{2,1,0:T(8,128)S(1)}) fusion(f32[8,32,512]{2,1,0:T(8,128)} %collective-permute-done.3), kind=kLoop, calls=%fused_computation.339 | loop fusion | bytes 1179648 | tf_op jit(solution)/shard_map/slice | solution.py:74
  35.5 1.2 %fusion.215 = (f32[3,32,512]{2,1,0:T(8,128)S(1)}, f32[3,32,512]{2,1,0:T(8,128)S(1)}, f32[3,32,512]{2,1,0:T(8,128)S(1)}) fusion(f32[8,32,512]{2,1,0:T(8,128)} %collective-permute-done.5), kind=kLoop, calls=%fused_computation.340 | loop fusion | bytes 1179648 | tf_op jit(solution)/shard_map/slice | solution.py:76
  36.7 0.3 maximum_maximum_fusion.2
  37.0 0.3 maximum_maximum_fusion.1
  37.3 0.3 maximum_maximum_fusion
  37.6 2.1 %divide_select_fusion = (f32[22,38,512]{2,1,0:T(8,128)S(1)}, f32[22,38,512]{2,1,0:T(8,128)S(1)}, f32[22,38,512]{2,1,0:T(8,128)S(1)}) fusion(f32[22,38,512]{2,1,0:T(8,128)S(1)} %maximum_maximum_fusion.1), kind=kLoop, calls=%fused_computation.19 | loop fusion | flops 8560640 | bytes 6848512 | tf_op jit(solution)/shard_map/jit(_where)/select_n | solution.py:184
  39.7 4.0 %and_select_fusion.1 = (f32[22,38,512]{2,1,0:T(8,128)S(1)}, f32[22,38,512]{2,1,0:T(8,128)S(1)}) fusion(f32[22,38,512]{2,1,0:T(8,128)S(1)} %get-tuple-element.43, f32[22,38,512]{2,1,0:T(8,128)S(1)} %maximum_maximum_fusion.2, f32[22,38,512]{2,1,0:T(8,128)S(1)} %get-tuple-element.44, f32[22,38,512]{2,1,0:T(8,128)S(1)} %get-tuple-element.42, ...), kind=kLoop, calls=%fused_computation.13 | loop fusion | flops 11556864 | bytes 13697596 | tf_op jit(solution)/shard_map/jit(_where)/select_n | solution.py:231
  43.8 3.8 %and_select_fusion = f32[22,38,512]{2,1,0:T(8,128)S(1)} fusion(f32[22,38,512]{2,1,0:T(8,128)S(1)} %get-tuple-element.43, f32[22,38,512]{2,1,0:T(8,128)S(1)} %get-tuple-element.36, f32[22,38,512]{2,1,0:T(8,128)S(1)} %get-tuple-element.44, f32[22,38,512]{2,1,0:T(8,128)S(1)} %get-tuple-element.42, pred[38]{0:T(512)(128)(4,1)S(1)} %compare_and_fusion.2, ...), kind=kLoop, calls=%fused_computation.12 | loop fusion | flops 11128832 | bytes 11984956 | tf_op jit(solution)/shard_map/jit(_where)/select_n | solution.py:231
  47.6 0.5 fusion.207
  48.1 1.8 %fusion.31 = (f32[16,32,512]{2,1,0:T(8,128)S(1)}, f32[16,32,512]{2,1,0:T(8,128)S(1)}) fusion(f32[16,32,512]{2,1,0:T(8,128)S(1)} %copy-done.1, f32[22,38,512]{2,1,0:T(8,128)S(1)} %get-tuple-element.37, f32[22,38,512]{2,1,0:T(8,128)S(1)} %get-tuple-element.42, f32[22,38,512]{2,1,0:T(8,128)S(1)} %and_select_fusion, f32[22,38,512]{2,1,0:T(8,128)S(1)} %get-tuple-element.44, ...), kind=kLoop, calls=%fused_computation.111 | loop fusion | flops 4718592 | bytes 16773120 | tf_op jit(solution)/shard_map/sub | solution.py:242
  50.0 0.5 fusion.182
  50.6 6.9 %collective-permute-start.6 = (f32[2,4,8,128]{3,2,1,0:T(8,128)S(1)}, f32[2,4,8,128]{3,2,1,0:T(8,128)S(1)}, u32[]{:S(2)}, u32[]{:S(2)}) collective-permute-start(f32[2,4,8,128]{3,2,1,0:T(8,128)S(1)} %pad_maximum_fusion.7), channel_id=1, source_target_pairs={{0,16},{8,24},{16,32},{24,40},{32,48},{40,56},{48,64},{56,72},{64,... | collective-permute-start | bytes 98312 | tf_op jit(solution)/shard_map/ppermute | solution.py:25
  57.5 1.9 %collective-permute-start.7 = (f32[2,4,8,128]{3,2,1,0:T(8,128)S(1)}, f32[2,4,8,128]{3,2,1,0:T(8,128)S(1)}, u32[]{:S(2)}, u32[]{:S(2)}) collective-permute-start(f32[2,4,8,128]{3,2,1,0:T(8,128)S(1)} %pad_maximum_fusion.7), channel_id=1, source_target_pairs={{0,8},{8,16},{16,24},{24,32},{32,40},{40,48},{48,56},{56,64},{64,7... | collective-permute-start | bytes 98312 | tf_op jit(solution)/shard_map/ppermute | solution.py:25
  59.4 6.0 %collective-permute-start.8 = (f32[2,4,8,128]{3,2,1,0:T(8,128)S(1)}, f32[2,4,8,128]{3,2,1,0:T(8,128)S(1)}, u32[]{:S(2)}, u32[]{:S(2)}) collective-permute-start(f32[2,4,8,128]{3,2,1,0:T(8,128)S(1)} %pad_maximum_fusion.7), channel_id=1, source_target_pairs={{8,0},{16,8},{24,16},{32,24},{40,32},{48,40},{56,48},{64,56},{72,6... | collective-permute-start | bytes 98312 | tf_op jit(solution)/shard_map/ppermute | solution.py:26
  65.5 1.9 %collective-permute-start.9 = (f32[2,4,8,128]{3,2,1,0:T(8,128)S(1)}, f32[2,4,8,128]{3,2,1,0:T(8,128)S(1)}, u32[]{:S(2)}, u32[]{:S(2)}) collective-permute-start(f32[2,4,8,128]{3,2,1,0:T(8,128)S(1)} %pad_maximum_fusion.7), channel_id=1, source_target_pairs={{16,0},{24,8},{32,16},{40,24},{48,32},{56,40},{64,48},{72,56},{80,... | collective-permute-start | bytes 98312 | tf_op jit(solution)/shard_map/ppermute | solution.py:26
  67.5 5.3 %collective-permute-done.9 = f32[2,4,8,128]{3,2,1,0:T(8,128)S(1)} collective-permute-done((f32[2,4,8,128]{3,2,1,0:T(8,128)S(1)}, f32[2,4,8,128]{3,2,1,0:T(8,128)S(1)}, u32[]{:S(2)}, u32[]{:S(2)}) %collective-permute-start.9) | collective-permute-done | bytes 32800 | tf_op jit(solution)/shard_map/ppermute | solution.py:26
  72.8 4.0 %collective-permute-start.10 = (f32[2,20,8,128]{3,2,1,0:T(8,128)S(1)}, f32[2,20,8,128]{3,2,1,0:T(8,128)S(1)}, u32[]{:S(2)}, u32[]{:S(2)}) collective-permute-start(f32[2,20,8,128]{3,2,1,0:T(8,128)S(1)} %constant_dynamic-update-slice_fusion), channel_id=1, source_target_pairs={{0,1},{1,2},{2,3},{3,4},{4,5},{5,6},{6,7},{8,9},{9,10},{10,11},{11... | collective-permute-start | bytes 491528 | tf_op jit(solution)/shard_map/ppermute | solution.py:25
  76.8 2.1 %collective-permute-start.11 = (f32[2,20,8,128]{3,2,1,0:T(8,128)S(1)}, f32[2,20,8,128]{3,2,1,0:T(8,128)S(1)}, u32[]{:S(2)}, u32[]{:S(2)}) collective-permute-start(f32[2,20,8,128]{3,2,1,0:T(8,128)S(1)} %constant_dynamic-update-slice_fusion), channel_id=1, source_target_pairs={{1,0},{2,1},{3,2},{4,3},{5,4},{6,5},{7,6},{9,8},{10,9},{11,10},{12... | collective-permute-start | bytes 491528 | tf_op jit(solution)/shard_map/ppermute | solution.py:26
  78.9 2.5 %collective-permute-done.10 = f32[2,20,8,128]{3,2,1,0:T(8,128)S(1)} collective-permute-done((f32[2,20,8,128]{3,2,1,0:T(8,128)S(1)}, f32[2,20,8,128]{3,2,1,0:T(8,128)S(1)}, u32[]{:S(2)}, u32[]{:S(2)}) %collective-permute-start.10) | collective-permute-done | bytes 163872 | tf_op jit(solution)/shard_map/ppermute | solution.py:25
  81.4 3.4 %collective-permute-done.11 = f32[2,20,8,128]{3,2,1,0:T(8,128)S(1)} collective-permute-done((f32[2,20,8,128]{3,2,1,0:T(8,128)S(1)}, f32[2,20,8,128]{3,2,1,0:T(8,128)S(1)}, u32[]{:S(2)}, u32[]{:S(2)}) %collective-permute-start.11) | collective-permute-done | bytes 163872 | tf_op jit(solution)/shard_map/ppermute | solution.py:26
  84.9 0.5 fusion.167
  85.5 0.3 fusion.168
  85.8 0.3 multiply_add_fusion.4
  86.1 0.3 multiply_add_fusion.3
  86.3 0.3 multiply_add_fusion.2
  86.6 0.3 multiply_add_fusion.1
  86.9 0.3 multiply_add_fusion
  87.4 0.5 fusion.171
  87.9 0.3 convolution_bitcast_fusion
  88.2 1.1 %bitcast_add_fusion = f32[16,32,512]{2,1,0:T(8,128)} fusion(f32[16,32,512]{2,1,0:T(8,128)S(1)} %get-tuple-element.13, f32[4,32,512]{2,1,0:T(8,128)S(1)} %convolution_bitcast_fusion), kind=kLoop, calls=%fused_computation.125 | loop fusion | flops 262144 | bytes 2359296 | tf_op jit(solution)/shard_map/add | solution.py:247
  (42 shorter events, 1.0 us)
Async XLA Ops:
  0.0 10.8 %copy-start = (f32[16,32,512]{2,1,0:T(8,128)S(1)}, f32[16,32,512]{2,1,0:T(8,128)}, u32[]{:S(2)}) copy-start(f32[16,32,512]{2,1,0:T(8,128)} %param.4) | copy-start | bytes 3145732
  0.0 10.8 %copy-start.2 = (f32[16,32,512]{2,1,0:T(8,128)S(1)}, f32[16,32,512]{2,1,0:T(8,128)}, u32[]{:S(2)}) copy-start(f32[16,32,512]{2,1,0:T(8,128)} %param.5) | copy-start | bytes 3145732
  1.2 9.6 %copy-start.1 = (f32[16,32,512]{2,1,0:T(8,128)S(1)}, f32[16,32,512]{2,1,0:T(8,128)}, u32[]{:S(2)}) copy-start(f32[16,32,512]{2,1,0:T(8,128)} %param.3) | copy-start | bytes 3145732
  3.4 18.0 %collective-permute-start = (f32[16,8,512]{2,1,0:T(8,128)}, f32[16,8,512]{2,1,0:T(8,128)}, u32[]{:S(2)}, u32[]{:S(2)}) collective-permute-start(f32[16,8,512]{2,1,0:T(8,128)} %pad_maximum_fusion.3), channel_id=1, source_target_pairs={{0,1},{1,2},{2,3},{3,4},{4,5},{5,6},{6,7},{8,9},{9,10},{10,11},{11... | collective-permute-start | bytes 786440 | tf_op jit(solution)/shard_map/ppermute | solution.py:58
  7.3 15.0 %collective-permute-start.1 = (f32[16,8,512]{2,1,0:T(8,128)}, f32[16,8,512]{2,1,0:T(8,128)}, u32[]{:S(2)}, u32[]{:S(2)}) collective-permute-start(f32[16,8,512]{2,1,0:T(8,128)} %pad_maximum_fusion.4), channel_id=1, source_target_pairs={{1,0},{2,1},{3,2},{4,3},{5,4},{6,5},{7,6},{9,8},{10,9},{11,10},{12... | collective-permute-start | bytes 786440 | tf_op jit(solution)/shard_map/ppermute | solution.py:58
  11.8 22.6 %collective-permute-start.3 = (f32[8,32,512]{2,1,0:T(8,128)}, f32[8,32,512]{2,1,0:T(8,128)}, u32[]{:S(2)}, u32[]{:S(2)}) collective-permute-start(f32[8,32,512]{2,1,0:T(8,128)} %pad_maximum_fusion), channel_id=1, source_target_pairs={{0,8},{8,16},{16,24},{24,32},{32,40},{40,48},{48,56},{56,64},{64,7... | collective-permute-start | bytes 1572872 | tf_op jit(solution)/shard_map/ppermute | solution.py:58
  14.5 21.0 %collective-permute-start.5 = (f32[8,32,512]{2,1,0:T(8,128)}, f32[8,32,512]{2,1,0:T(8,128)}, u32[]{:S(2)}, u32[]{:S(2)}) collective-permute-start(f32[8,32,512]{2,1,0:T(8,128)} %pad_maximum_fusion.1), channel_id=1, source_target_pairs={{8,0},{16,8},{24,16},{32,24},{40,32},{48,40},{56,48},{64,56},{72,6... | collective-permute-start | bytes 1572872 | tf_op jit(solution)/shard_map/ppermute | solution.py:58
  23.1 10.5 %collective-permute-start.2 = (f32[3,16,512]{2,1,0:T(8,128)S(1)}, f32[3,16,512]{2,1,0:T(8,128)S(1)}, u32[]{:S(2)}, u32[]{:S(2)}) collective-permute-start(f32[3,16,512]{2,1,0:T(8,128)S(1)} %pad_maximum_fusion.5), channel_id=1, source_target_pairs={{0,8},{8,16},{16,24},{24,32},{32,40},{40,48},{48,56},{56,64},{64,7... | collective-permute-start | bytes 294920 | tf_op jit(solution)/shard_map/ppermute | solution.py:58
  25.0 9.3 %collective-permute-start.4 = (f32[3,16,512]{2,1,0:T(8,128)S(1)}, f32[3,16,512]{2,1,0:T(8,128)S(1)}, u32[]{:S(2)}, u32[]{:S(2)}) collective-permute-start(f32[3,16,512]{2,1,0:T(8,128)S(1)} %pad_maximum_fusion.6), channel_id=1, source_target_pairs={{8,0},{16,8},{24,16},{32,24},{40,32},{48,40},{56,48},{64,56},{72,6... | collective-permute-start | bytes 294920 | tf_op jit(solution)/shard_map/ppermute | solution.py:58
  50.6 16.8 %collective-permute-start.6 = (f32[2,4,8,128]{3,2,1,0:T(8,128)S(1)}, f32[2,4,8,128]{3,2,1,0:T(8,128)S(1)}, u32[]{:S(2)}, u32[]{:S(2)}) collective-permute-start(f32[2,4,8,128]{3,2,1,0:T(8,128)S(1)} %pad_maximum_fusion.7), channel_id=1, source_target_pairs={{0,16},{8,24},{16,32},{24,40},{32,48},{40,56},{48,64},{56,72},{64,... | collective-permute-start | bytes 98312 | tf_op jit(solution)/shard_map/ppermute | solution.py:25
  57.5 9.9 %collective-permute-start.7 = (f32[2,4,8,128]{3,2,1,0:T(8,128)S(1)}, f32[2,4,8,128]{3,2,1,0:T(8,128)S(1)}, u32[]{:S(2)}, u32[]{:S(2)}) collective-permute-start(f32[2,4,8,128]{3,2,1,0:T(8,128)S(1)} %pad_maximum_fusion.7), channel_id=1, source_target_pairs={{0,8},{8,16},{16,24},{24,32},{32,40},{40,48},{48,56},{56,64},{64,7... | collective-permute-start | bytes 98312 | tf_op jit(solution)/shard_map/ppermute | solution.py:25
  59.4 8.0 %collective-permute-start.8 = (f32[2,4,8,128]{3,2,1,0:T(8,128)S(1)}, f32[2,4,8,128]{3,2,1,0:T(8,128)S(1)}, u32[]{:S(2)}, u32[]{:S(2)}) collective-permute-start(f32[2,4,8,128]{3,2,1,0:T(8,128)S(1)} %pad_maximum_fusion.7), channel_id=1, source_target_pairs={{8,0},{16,8},{24,16},{32,24},{40,32},{48,40},{56,48},{64,56},{72,6... | collective-permute-start | bytes 98312 | tf_op jit(solution)/shard_map/ppermute | solution.py:26
  65.5 7.3 %collective-permute-start.9 = (f32[2,4,8,128]{3,2,1,0:T(8,128)S(1)}, f32[2,4,8,128]{3,2,1,0:T(8,128)S(1)}, u32[]{:S(2)}, u32[]{:S(2)}) collective-permute-start(f32[2,4,8,128]{3,2,1,0:T(8,128)S(1)} %pad_maximum_fusion.7), channel_id=1, source_target_pairs={{16,0},{24,8},{32,16},{40,24},{48,32},{56,40},{64,48},{72,56},{80,... | collective-permute-start | bytes 98312 | tf_op jit(solution)/shard_map/ppermute | solution.py:26
  72.8 8.7 %collective-permute-start.10 = (f32[2,20,8,128]{3,2,1,0:T(8,128)S(1)}, f32[2,20,8,128]{3,2,1,0:T(8,128)S(1)}, u32[]{:S(2)}, u32[]{:S(2)}) collective-permute-start(f32[2,20,8,128]{3,2,1,0:T(8,128)S(1)} %constant_dynamic-update-slice_fusion), channel_id=1, source_target_pairs={{0,1},{1,2},{2,3},{3,4},{4,5},{5,6},{6,7},{8,9},{9,10},{10,11},{11... | collective-permute-start | bytes 491528 | tf_op jit(solution)/shard_map/ppermute | solution.py:25
  76.8 8.1 %collective-permute-start.11 = (f32[2,20,8,128]{3,2,1,0:T(8,128)S(1)}, f32[2,20,8,128]{3,2,1,0:T(8,128)S(1)}, u32[]{:S(2)}, u32[]{:S(2)}) collective-permute-start(f32[2,20,8,128]{3,2,1,0:T(8,128)S(1)} %constant_dynamic-update-slice_fusion), channel_id=1, source_target_pairs={{1,0},{2,1},{3,2},{4,3},{5,4},{6,5},{7,6},{9,8},{10,9},{11,10},{12... | collective-permute-start | bytes 491528 | tf_op jit(solution)/shard_map/ppermute | solution.py:26

commit v18 on v14

--- a/solution.py
+++ b/solution.py
@@ -137,11 +137,29 @@
     return (gx >= 0) & (gx < totals[0]) & (gy >= 0) & (gy < totals[1])
 
 
+def pair_extend(block, depth):
+    nb = lax.axis_size("box")
+    n = block.shape[1]
+    odd = lax.axis_index("box") % 2
+    partner = lax.ppermute(block, "box", [(i, i ^ 1) for i in range(nb)])
+    pair = jnp.where(odd == 0, jnp.concatenate([block, partner], axis=1),
+                     jnp.concatenate([partner, block], axis=1))
+    low = lax.ppermute(pair, "box", shifted_pairs(nb, 2))
+    high = lax.ppermute(pair, "box", [(t, s) for s, t in shifted_pairs(nb, 2)])
+    span = jnp.concatenate([low, pair, high], axis=1)
+    start = 2 * n - depth + odd * n
+    return lax.dynamic_slice_in_dim(span, start, n + 2 * depth, axis=1)
+
+
 def chebyshev_local(rhs_c, b_c):
     depth = CHEB
     cx, cy, cz = rhs_c.shape
     both = jnp.stack([b_c, rhs_c])
-    both = deep_extend(both, "box", 1, depth)
+    nb = lax.axis_size("box")
+    if nb % 2 == 0 and nb > 2 and cx < depth <= 2 * cx:
+        both = pair_extend(both, depth)
+    else:
+        both = deep_extend(both, "box", 1, depth)
     both = deep_extend(both, "group", 2, depth)
     b_ext, rhs_ext = both[0], both[1]
     totals = (cx * lax.axis_size("box"), cy * lax.axis_size("group"))

time: 90.3 us -> 85.3 us (0.945)
  the two profiles are of different devices: /device:TPU:34 before, /device:TPU:88 now
where the time goes in v18:
time: 85.3 us; the launch traced here: 84.7 us
  starting transfers between devices  39.3 us (46%)
  other arithmetic  20 us (23%)
  waiting for transfers between devices  13.2 us (15%)
  local copies, waits for them, and re-layouts  9.73 us (11%)
  matrix products  2.05 us (2%)
    ppermute x6, starting transfers between devices, send(): return lax.ppermute(msg, axis, pairs)  20.8 us
    ppermute x1, starting transfers between devices, pair_extend(): low = lax.ppermute(pair, 'box', shifted_pairs(nb, 2))  8.25 us
    select_n x2, other arithmetic, per_device(): fine = jnp.where(inside, fine + step, 0.0)  7.91 us
    ppermute x1, waiting for transfers between devices, pair_extend(): high = lax.ppermute(pair, 'box', [(t, s) for s, t in shifted_pairs(nb, 2)])  6.61 us
    ppermute x1, waiting for transfers between devices, halo_from(): lax.ppermute(lax.slice_in_dim(block, n - width, n, axis=dim), axis, forward)  4.56 us
    slice x6, local copies, waits for them, and re-layouts, packed_halo(): lax.slice_in_dim(f, f.shape[dim] - d, f.shape[dim], axis=dim)  4.36 us
    ppermute x1, starting transfers between devices, halo_from(): lax.ppermute(lax.slice_in_dim(block, 0, width, axis=dim), axis, backward)  3.65 us
    concatenate x6, other arithmetic, send(): msg = jnp.concatenate(pieces, axis=dim)  3.32 us
  transfers between devices with their start and end apart: 11, of which 4 were waited for; matrix products, arithmetic and copies ran while one was open for 10% of the time, Pallas kernels for 0%

profile of v18, /device:TPU:88, one launch (start us, length us, event | category | flops | bytes accessed | tf_op | source)
XLA Modules:
  0.0 84.7 jit_solution(16767715173451372393)
XLA Ops:
  0.0 1.2 %fusion.228 = (f32[16,2,512]{2,1,0:T(2,128)S(1)}, f32[16,2,512]{2,1,0:T(2,128)S(1)}) fusion(f32[16,32,512]{2,1,0:T(8,128)} %param.3), kind=kLoop, calls=%fused_computation.351 | loop fusion | bytes 262144 | tf_op jit(solution)/shard_map/slice | solution.py:48
  1.2 1.4 %fusion.227 = (f32[16,3,512]{2,1,0:T(4,128)S(1)}, f32[16,3,512]{2,1,0:T(4,128)S(1)}, f32[16,3,512]{2,1,0:T(4,128)S(1)}, f32[16,3,512]{2,1,0:T(4,128)S(1)}) fusion(f32[16,32,512]{2,1,0:T(8,128)} %param.4, f32[16,32,512]{2,1,0:T(8,128)} %param.5), kind=kLoop, calls=%fused_computation.350 | loop fusion | bytes 786432 | tf_op jit(solution)/shard_map/slice | solution.py:48
  2.6 0.8 pad_maximum_fusion.3
  3.4 3.5 %collective-permute-start = (f32[16,8,512]{2,1,0:T(8,128)}, f32[16,8,512]{2,1,0:T(8,128)}, u32[]{:S(2)}, u32[]{:S(2)}) collective-permute-start(f32[16,8,512]{2,1,0:T(8,128)} %pad_maximum_fusion.3), channel_id=1, source_target_pairs={{0,1},{1,2},{2,3},{3,4},{4,5},{5,6},{6,7},{8,9},{9,10},{10,11},{11... | collective-permute-start | bytes 786440 | tf_op jit(solution)/shard_map/ppermute | solution.py:58
  7.0 0.8 pad_maximum_fusion.4
  7.8 3.2 %collective-permute-start.1 = (f32[16,8,512]{2,1,0:T(8,128)}, f32[16,8,512]{2,1,0:T(8,128)}, u32[]{:S(2)}, u32[]{:S(2)}) collective-permute-start(f32[16,8,512]{2,1,0:T(8,128)} %pad_maximum_fusion.4), channel_id=1, source_target_pairs={{1,0},{2,1},{3,2},{4,3},{5,4},{6,5},{7,6},{9,8},{10,9},{11,10},{12... | collective-permute-start | bytes 786440 | tf_op jit(solution)/shard_map/ppermute | solution.py:58
  11.1 0.9 %pad_maximum_fusion = f32[8,32,512]{2,1,0:T(8,128)} fusion(f32[3,32,512]{2,1,0:T(8,128)S(1)} %get-tuple-element.90, f32[2,32,512]{2,1,0:T(8,128)S(1)} %get-tuple-element.47, f32[3,32,512]{2,1,0:T(8,128)S(1)} %get-tuple-element.45), kind=kLoop, calls=%fused_computation.143 | loop fusion | flops 262144 | bytes 1048576 | tf_op jit(solution)/shard_map/concatenate | solution.py:55
  12.0 1.9 %collective-permute-start.3 = (f32[8,32,512]{2,1,0:T(8,128)}, f32[8,32,512]{2,1,0:T(8,128)}, u32[]{:S(2)}, u32[]{:S(2)}) collective-permute-start(f32[8,32,512]{2,1,0:T(8,128)} %pad_maximum_fusion), channel_id=1, source_target_pairs={{0,8},{8,16},{16,24},{24,32},{32,40},{40,48},{48,56},{56,64},{64,7... | collective-permute-start | bytes 1572872 | tf_op jit(solution)/shard_map/ppermute | solution.py:58
  13.9 0.8 pad_maximum_fusion.1
  14.7 5.1 %collective-permute-start.5 = (f32[8,32,512]{2,1,0:T(8,128)}, f32[8,32,512]{2,1,0:T(8,128)}, u32[]{:S(2)}, u32[]{:S(2)}) collective-permute-start(f32[8,32,512]{2,1,0:T(8,128)} %pad_maximum_fusion.1), channel_id=1, source_target_pairs={{8,0},{16,8},{24,16},{32,24},{40,32},{48,40},{56,48},{64,56},{72,6... | collective-permute-start | bytes 1572872 | tf_op jit(solution)/shard_map/ppermute | solution.py:58
  20.0 0.5 fusion.201
  20.7 0.8 fusion.234
  21.5 0.8 fusion.235
  22.4 1.9 %collective-permute-start.2 = (f32[3,16,512]{2,1,0:T(8,128)S(1)}, f32[3,16,512]{2,1,0:T(8,128)S(1)}, u32[]{:S(2)}, u32[]{:S(2)}) collective-permute-start(f32[3,16,512]{2,1,0:T(8,128)S(1)} %pad_maximum_fusion.5), channel_id=1, source_target_pairs={{0,8},{8,16},{16,24},{24,32},{32,40},{40,48},{48,56},{56,64},{64,7... | collective-permute-start | bytes 294920 | tf_op jit(solution)/shard_map/ppermute | solution.py:58
  24.3 5.1 %collective-permute-start.4 = (f32[3,16,512]{2,1,0:T(8,128)S(1)}, f32[3,16,512]{2,1,0:T(8,128)S(1)}, u32[]{:S(2)}, u32[]{:S(2)}) collective-permute-start(f32[3,16,512]{2,1,0:T(8,128)S(1)} %pad_maximum_fusion.6), channel_id=1, source_target_pairs={{8,0},{16,8},{24,16},{32,24},{40,32},{48,40},{56,48},{64,56},{72,6... | collective-permute-start | bytes 294920 | tf_op jit(solution)/shard_map/ppermute | solution.py:58
  29.5 1.3 %fusion.232 = (f32[16,3,512]{2,1,0:T(4,128)S(1)}, f32[16,3,512]{2,1,0:T(4,128)S(1)}, f32[16,3,512]{2,1,0:T(4,128)S(1)}) fusion(f32[16,8,512]{2,1,0:T(8,128)} %collective-permute-done), kind=kLoop, calls=%fused_computation.355 | loop fusion | bytes 589824 | tf_op jit(solution)/shard_map/slice | solution.py:75
  30.8 1.2 %fusion.233 = (f32[16,3,512]{2,1,0:T(4,128)S(1)}, f32[16,3,512]{2,1,0:T(4,128)S(1)}, f32[16,3,512]{2,1,0:T(4,128)S(1)}) fusion(f32[16,8,512]{2,1,0:T(8,128)} %collective-permute-done.1), kind=kLoop, calls=%fused_computation.356 | loop fusion | bytes 589824 | tf_op jit(solution)/shard_map/slice | solution.py:75
  32.1 1.2 %fusion.230 = (f32[3,32,512]{2,1,0:T(8,128)S(1)}, f32[3,32,512]{2,1,0:T(8,128)S(1)}, f32[3,32,512]{2,1,0:T(8,128)S(1)}) fusion(f32[8,32,512]{2,1,0:T(8,128)} %collective-permute-done.3), kind=kLoop, calls=%fused_computation.353 | loop fusion | bytes 1179648 | tf_op jit(solution)/shard_map/slice | solution.py:74
  33.3 1.2 %fusion.231 = (f32[3,32,512]{2,1,0:T(8,128)S(1)}, f32[3,32,512]{2,1,0:T(8,128)S(1)}, f32[3,32,512]{2,1,0:T(8,128)S(1)}) fusion(f32[8,32,512]{2,1,0:T(8,128)} %collective-permute-done.5), kind=kLoop, calls=%fused_computation.354 | loop fusion | bytes 1179648 | tf_op jit(solution)/shard_map/slice | solution.py:76
  34.4 0.3 maximum_maximum_fusion.2
  34.7 0.3 maximum_maximum_fusion.1
  35.0 0.3 maximum_maximum_fusion
  35.3 2.1 %divide_select_fusion.2 = (f32[22,38,512]{2,1,0:T(8,128)S(1)}, f32[22,38,512]{2,1,0:T(8,128)S(1)}, f32[22,38,512]{2,1,0:T(8,128)S(1)}) fusion(f32[22,38,512]{2,1,0:T(8,128)S(1)} %maximum_maximum_fusion.1), kind=kLoop, calls=%fused_computation.17 | loop fusion | flops 8560640 | bytes 6848512 | tf_op jit(solution)/shard_map/jit(_where)/select_n | solution.py:202
  37.5 4.1 %and_select_fusion.1 = (f32[22,38,512]{2,1,0:T(8,128)S(1)}, f32[22,38,512]{2,1,0:T(8,128)S(1)}) fusion(f32[22,38,512]{2,1,0:T(8,128)S(1)} %maximum_maximum_fusion.2, f32[22,38,512]{2,1,0:T(8,128)S(1)} %get-tuple-element.43, f32[22,38,512]{2,1,0:T(8,128)S(1)} %get-tuple-element.44, f32[22,38,512]{2,1,0:T(8,128)S(1)} %get-tuple-element.42, ...), kind=kLoop, calls=%fused_computation.19 | loop fusion | flops 12412928 | bytes 13697596 | tf_op jit(solution)/shard_map/jit(_where)/select_n | solution.py:246
  41.6 3.8 %and_select_fusion = f32[22,38,512]{2,1,0:T(8,128)S(1)} fusion(f32[22,38,512]{2,1,0:T(8,128)S(1)} %get-tuple-element.36, f32[22,38,512]{2,1,0:T(8,128)S(1)} %get-tuple-element.37, f32[22,38,512]{2,1,0:T(8,128)S(1)} %get-tuple-element.43, f32[22,38,512]{2,1,0:T(8,128)S(1)} %get-tuple-element.44, f32[22,38,512]{2,1,0:T(8,128)S(1)} %get-tuple-element.42, ...), kind=kLoop, calls=%fused_computation.18 | loop fusion | flops 11984896 | bytes 11984956 | tf_op jit(solution)/shard_map/jit(_where)/select_n | solution.py:246
  45.4 0.5 fusion.223
  45.9 1.8 %fusion.46 = (f32[16,32,512]{2,1,0:T(8,128)S(1)}, f32[16,32,512]{2,1,0:T(8,128)S(1)}) fusion(f32[16,32,512]{2,1,0:T(8,128)S(1)} %copy-done.1, f32[22,38,512]{2,1,0:T(8,128)S(1)} %get-tuple-element.37, f32[22,38,512]{2,1,0:T(8,128)S(1)} %get-tuple-element.43, f32[22,38,512]{2,1,0:T(8,128)S(1)} %and_select_fusion, f32[22,38,512]{2,1,0:T(8,128)S(1)} %get-tuple-element.44, ...), kind=kLoop, calls=%fused_computation.125 | loop fusion | flops 4718592 | bytes 16773120 | tf_op jit(solution)/shard_map/sub | solution.py:257
  47.8 0.5 fusion.199
  48.4 2.3 %collective-permute-start.6 = (f32[2,4,8,128]{3,2,1,0:T(8,128)S(1)}, f32[2,4,8,128]{3,2,1,0:T(8,128)S(1)}, u32[]{:S(2)}, u32[]{:S(2)}) collective-permute-start(f32[2,4,8,128]{3,2,1,0:T(8,128)S(1)} %pad_maximum_fusion.7), channel_id=1, source_target_pairs={{0,8},{8,0},{16,24},{24,16},{32,40},{40,32},{48,56},{56,48},{64,72... | collective-permute-start | bytes 98312 | tf_op jit(solution)/shard_map/ppermute | solution.py:144
  50.7 0.9 %collective-permute-done.6 = f32[2,4,8,128]{3,2,1,0:T(8,128)S(1)} collective-permute-done((f32[2,4,8,128]{3,2,1,0:T(8,128)S(1)}, f32[2,4,8,128]{3,2,1,0:T(8,128)S(1)}, u32[]{:S(2)}, u32[]{:S(2)}) %collective-permute-start.6) | collective-permute-done | bytes 32800 | tf_op jit(solution)/shard_map/ppermute | solution.py:144
  51.5 8.3 %collective-permute-start.7 = (f32[2,8,8,128]{3,2,1,0:T(8,128)S(1)}, f32[2,8,8,128]{3,2,1,0:T(8,128)S(1)}, u32[]{:S(2)}, u32[]{:S(2)}) collective-permute-start(f32[2,8,8,128]{3,2,1,0:T(8,128)S(1)} %maximum_select_fusion), channel_id=1, source_target_pairs={{0,16},{8,24},{16,32},{24,40},{32,48},{40,56},{48,64},{56,72},{64,... | collective-permute-start | bytes 196616 | tf_op jit(solution)/shard_map/ppermute | solution.py:147
  59.8 1.9 %collective-permute-start.8 = (f32[2,8,8,128]{3,2,1,0:T(8,128)S(1)}, f32[2,8,8,128]{3,2,1,0:T(8,128)S(1)}, u32[]{:S(2)}, u32[]{:S(2)}) collective-permute-start(f32[2,8,8,128]{3,2,1,0:T(8,128)S(1)} %maximum_select_fusion), channel_id=1, source_target_pairs={{16,0},{24,8},{32,16},{40,24},{48,32},{56,40},{64,48},{72,56},{80,... | collective-permute-start | bytes 196616 | tf_op jit(solution)/shard_map/ppermute | solution.py:148
  61.8 6.6 %collective-permute-done.8 = f32[2,8,8,128]{3,2,1,0:T(8,128)S(1)} collective-permute-done((f32[2,8,8,128]{3,2,1,0:T(8,128)S(1)}, f32[2,8,8,128]{3,2,1,0:T(8,128)S(1)}, u32[]{:S(2)}, u32[]{:S(2)}) %collective-permute-start.8) | collective-permute-done | bytes 65568 | tf_op jit(solution)/shard_map/ppermute | solution.py:148
  68.4 3.7 %collective-permute-start.10 = (f32[2,20,8,128]{3,2,1,0:T(8,128)S(1)}, f32[2,20,8,128]{3,2,1,0:T(8,128)S(1)}, u32[]{:S(2)}, u32[]{:S(2)}) collective-permute-start(f32[2,20,8,128]{3,2,1,0:T(8,128)S(1)} %fusion.185), channel_id=1, source_target_pairs={{1,0},{2,1},{3,2},{4,3},{5,4},{6,5},{7,6},{9,8},{10,9},{11,10},{12... | collective-permute-start | bytes 491528 | tf_op jit(solution)/shard_map/ppermute | solution.py:26
  72.1 2.4 %collective-permute-start.9 = (f32[2,20,8,128]{3,2,1,0:T(8,128)S(1)}, f32[2,20,8,128]{3,2,1,0:T(8,128)S(1)}, u32[]{:S(2)}, u32[]{:S(2)}) collective-permute-start(f32[2,20,8,128]{3,2,1,0:T(8,128)S(1)} %fusion.185), channel_id=1, source_target_pairs={{0,1},{1,2},{2,3},{3,4},{4,5},{5,6},{6,7},{8,9},{9,10},{10,11},{11... | collective-permute-start | bytes 491528 | tf_op jit(solution)/shard_map/ppermute | solution.py:25
  74.5 1.1 %collective-permute-done.10 = f32[2,20,8,128]{3,2,1,0:T(8,128)S(1)} collective-permute-done((f32[2,20,8,128]{3,2,1,0:T(8,128)S(1)}, f32[2,20,8,128]{3,2,1,0:T(8,128)S(1)}, u32[]{:S(2)}, u32[]{:S(2)}) %collective-permute-start.10) | collective-permute-done | bytes 163872 | tf_op jit(solution)/shard_map/ppermute | solution.py:26
  75.6 4.6 %collective-permute-done.9 = f32[2,20,8,128]{3,2,1,0:T(8,128)S(1)} collective-permute-done((f32[2,20,8,128]{3,2,1,0:T(8,128)S(1)}, f32[2,20,8,128]{3,2,1,0:T(8,128)S(1)}, u32[]{:S(2)}, u32[]{:S(2)}) %collective-permute-start.9) | collective-permute-done | bytes 163872 | tf_op jit(solution)/shard_map/ppermute | solution.py:25
  80.3 0.5 fusion.182
  80.8 0.3 fusion.183
  81.1 0.3 multiply_add_fusion.4
  81.4 0.3 multiply_add_fusion.3
  81.7 0.3 multiply_add_fusion.2
  82.0 0.3 multiply_add_fusion.1
  82.2 0.3 multiply_add_fusion
  82.5 0.2 fusion.169
  82.8 0.5 fusion.188
  83.2 0.3 convolution_bitcast_fusion
  83.6 1.1 %bitcast_add_fusion = f32[16,32,512]{2,1,0:T(8,128)} fusion(f32[16,32,512]{2,1,0:T(8,128)S(1)} %get-tuple-element.13, f32[4,32,512]{2,1,0:T(8,128)S(1)} %convolution_bitcast_fusion), kind=kLoop, calls=%fused_computation.139 | loop fusion | flops 262144 | bytes 2359296 | tf_op jit(solution)/shard_map/add | solution.py:262
  (37 shorter events, 0.8 us)
Async XLA Ops:
  0.0 11.0 %copy-start = (f32[16,32,512]{2,1,0:T(8,128)S(1)}, f32[16,32,512]{2,1,0:T(8,128)}, u32[]{:S(2)}) copy-start(f32[16,32,512]{2,1,0:T(8,128)} %param.4) | copy-start | bytes 3145732
  0.0 11.0 %copy-start.2 = (f32[16,32,512]{2,1,0:T(8,128)S(1)}, f32[16,32,512]{2,1,0:T(8,128)}, u32[]{:S(2)}) copy-start(f32[16,32,512]{2,1,0:T(8,128)} %param.5) | copy-start | bytes 3145732
  1.2 9.8 %copy-start.1 = (f32[16,32,512]{2,1,0:T(8,128)S(1)}, f32[16,32,512]{2,1,0:T(8,128)}, u32[]{:S(2)}) copy-start(f32[16,32,512]{2,1,0:T(8,128)} %param.3) | copy-start | bytes 3145732
  3.4 17.3 %collective-permute-start = (f32[16,8,512]{2,1,0:T(8,128)}, f32[16,8,512]{2,1,0:T(8,128)}, u32[]{:S(2)}, u32[]{:S(2)}) collective-permute-start(f32[16,8,512]{2,1,0:T(8,128)} %pad_maximum_fusion.3), channel_id=1, source_target_pairs={{0,1},{1,2},{2,3},{3,4},{4,5},{5,6},{6,7},{8,9},{9,10},{10,11},{11... | collective-permute-start | bytes 786440 | tf_op jit(solution)/shard_map/ppermute | solution.py:58
  7.8 13.8 %collective-permute-start.1 = (f32[16,8,512]{2,1,0:T(8,128)}, f32[16,8,512]{2,1,0:T(8,128)}, u32[]{:S(2)}, u32[]{:S(2)}) collective-permute-start(f32[16,8,512]{2,1,0:T(8,128)} %pad_maximum_fusion.4), channel_id=1, source_target_pairs={{1,0},{2,1},{3,2},{4,3},{5,4},{6,5},{7,6},{9,8},{10,9},{11,10},{12... | collective-permute-start | bytes 786440 | tf_op jit(solution)/shard_map/ppermute | solution.py:58
  12.0 20.1 %collective-permute-start.3 = (f32[8,32,512]{2,1,0:T(8,128)}, f32[8,32,512]{2,1,0:T(8,128)}, u32[]{:S(2)}, u32[]{:S(2)}) collective-permute-start(f32[8,32,512]{2,1,0:T(8,128)} %pad_maximum_fusion), channel_id=1, source_target_pairs={{0,8},{8,16},{16,24},{24,32},{32,40},{40,48},{48,56},{56,64},{64,7... | collective-permute-start | bytes 1572872 | tf_op jit(solution)/shard_map/ppermute | solution.py:58
  14.7 18.5 %collective-permute-start.5 = (f32[8,32,512]{2,1,0:T(8,128)}, f32[8,32,512]{2,1,0:T(8,128)}, u32[]{:S(2)}, u32[]{:S(2)}) collective-permute-start(f32[8,32,512]{2,1,0:T(8,128)} %pad_maximum_fusion.1), channel_id=1, source_target_pairs={{8,0},{16,8},{24,16},{32,24},{40,32},{48,40},{56,48},{64,56},{72,6... | collective-permute-start | bytes 1572872 | tf_op jit(solution)/shard_map/ppermute | solution.py:58
  22.4 9.6 %collective-permute-start.2 = (f32[3,16,512]{2,1,0:T(8,128)S(1)}, f32[3,16,512]{2,1,0:T(8,128)S(1)}, u32[]{:S(2)}, u32[]{:S(2)}) collective-permute-start(f32[3,16,512]{2,1,0:T(8,128)S(1)} %pad_maximum_fusion.5), channel_id=1, source_target_pairs={{0,8},{8,16},{16,24},{24,32},{32,40},{40,48},{48,56},{56,64},{64,7... | collective-permute-start | bytes 294920 | tf_op jit(solution)/shard_map/ppermute | solution.py:58
  24.3 7.7 %collective-permute-start.4 = (f32[3,16,512]{2,1,0:T(8,128)S(1)}, f32[3,16,512]{2,1,0:T(8,128)S(1)}, u32[]{:S(2)}, u32[]{:S(2)}) collective-permute-start(f32[3,16,512]{2,1,0:T(8,128)S(1)} %pad_maximum_fusion.6), channel_id=1, source_target_pairs={{8,0},{16,8},{24,16},{32,24},{40,32},{48,40},{56,48},{64,56},{72,6... | collective-permute-start | bytes 294920 | tf_op jit(solution)/shard_map/ppermute | solution.py:58
  48.4 3.1 %collective-permute-start.6 = (f32[2,4,8,128]{3,2,1,0:T(8,128)S(1)}, f32[2,4,8,128]{3,2,1,0:T(8,128)S(1)}, u32[]{:S(2)}, u32[]{:S(2)}) collective-permute-start(f32[2,4,8,128]{3,2,1,0:T(8,128)S(1)} %pad_maximum_fusion.7), channel_id=1, source_target_pairs={{0,8},{8,0},{16,24},{24,16},{32,40},{40,32},{48,56},{56,48},{64,72... | collective-permute-start | bytes 98312 | tf_op jit(solution)/shard_map/ppermute | solution.py:144
  51.5 10.2 %collective-permute-start.7 = (f32[2,8,8,128]{3,2,1,0:T(8,128)S(1)}, f32[2,8,8,128]{3,2,1,0:T(8,128)S(1)}, u32[]{:S(2)}, u32[]{:S(2)}) collective-permute-start(f32[2,8,8,128]{3,2,1,0:T(8,128)S(1)} %maximum_select_fusion), channel_id=1, source_target_pairs={{0,16},{8,24},{16,32},{24,40},{32,48},{40,56},{48,64},{56,72},{64,... | collective-permute-start | bytes 196616 | tf_op jit(solution)/shard_map/ppermute | solution.py:147
  59.8 8.6 %collective-permute-start.8 = (f32[2,8,8,128]{3,2,1,0:T(8,128)S(1)}, f32[2,8,8,128]{3,2,1,0:T(8,128)S(1)}, u32[]{:S(2)}, u32[]{:S(2)}) collective-permute-start(f32[2,8,8,128]{3,2,1,0:T(8,128)S(1)} %maximum_select_fusion), channel_id=1, source_target_pairs={{16,0},{24,8},{32,16},{40,24},{48,32},{56,40},{64,48},{72,56},{80,... | collective-permute-start | bytes 196616 | tf_op jit(solution)/shard_map/ppermute | solution.py:148
  68.4 7.2 %collective-permute-start.10 = (f32[2,20,8,128]{3,2,1,0:T(8,128)S(1)}, f32[2,20,8,128]{3,2,1,0:T(8,128)S(1)}, u32[]{:S(2)}, u32[]{:S(2)}) collective-permute-start(f32[2,20,8,128]{3,2,1,0:T(8,128)S(1)} %fusion.185), channel_id=1, source_target_pairs={{1,0},{2,1},{3,2},{4,3},{5,4},{6,5},{7,6},{9,8},{10,9},{11,10},{12... | collective-permute-start | bytes 491528 | tf_op jit(solution)/shard_map/ppermute | solution.py:26
  72.1 8.1 %collective-permute-start.9 = (f32[2,20,8,128]{3,2,1,0:T(8,128)S(1)}, f32[2,20,8,128]{3,2,1,0:T(8,128)S(1)}, u32[]{:S(2)}, u32[]{:S(2)}) collective-permute-start(f32[2,20,8,128]{3,2,1,0:T(8,128)S(1)} %fusion.185), channel_id=1, source_target_pairs={{0,1},{1,2},{2,3},{3,4},{4,5},{5,6},{6,7},{8,9},{9,10},{10,11},{11... | collective-permute-start | bytes 491528 | tf_op jit(solution)/shard_map/ppermute | solution.py:25

commit v19 on v18

--- a/solution.py
+++ b/solution.py
@@ -241,9 +241,12 @@
     inside = grid_mask(fine.shape, depth, ("box", "group"), totals)
     coefs = shared_faces(b_e)
     diag = sum(coefs)
+    weight = jnp.where(inside, 2.0 / 3.0 / jnp.where(inside, diag, 1.0), 0.0)
+    lift = weight * rhs_e
+    plain = coefs[:5] + [jnp.pad(coefs[4], ((0, 0), (0, 0), (0, 1)))[:, :, 1:]]
     for sweep in range(SWEEPS):
-        step = 2.0 / 3.0 * (rhs_e - apply_op(fine, padded_neighbours(jnp.pad(fine, 1)), coefs)) / diag
-        fine = jnp.where(inside, fine + step, 0.0)
+        pull = sum(c * n for c, n in zip(plain, padded_neighbours(jnp.pad(fine, 1))))
+        fine = jnp.where(inside, fine * (1.0 / 3.0) + lift + weight * pull, 0.0)
     own = (slice(depth, depth + sx), slice(depth, depth + sy))
     core = fine[own]
     nears = [

time: 85.3 us -> 85.2 us (level)
  the two profiles are of different devices: /device:TPU:88 before, /device:TPU:90 now
where the time goes in v19:
time: 85.2 us; the launch traced here: 84.6 us
  starting transfers between devices  35 us (41%)
  other arithmetic  19.9 us (23%)
  waiting for transfers between devices  17.5 us (21%)
  local copies, waits for them, and re-layouts  9.74 us (11%)
  matrix products  2.06 us (2%)
    ppermute x6, starting transfers between devices, send(): return lax.ppermute(msg, axis, pairs)  20.8 us
    select_n x2, other arithmetic, per_device(): fine = jnp.where(inside, fine * (1.0 / 3.0) + lift + weight * pull, 0.0)  7.84 us
    ppermute x1, waiting for transfers between devices, pair_extend(): high = lax.ppermute(pair, 'box', [(t, s) for s, t in shifted_pairs(nb, 2)])  6.38 us
    ppermute x1, starting transfers between devices, pair_extend(): low = lax.ppermute(pair, 'box', shifted_pairs(nb, 2))  5.55 us
    ppermute x1, waiting for transfers between devices, halo_from(): lax.ppermute(lax.slice_in_dim(block, n - width, n, axis=dim), axis, forward)  4.56 us
    slice x6, local copies, waits for them, and re-layouts, packed_halo(): lax.slice_in_dim(f, f.shape[dim] - d, f.shape[dim], axis=dim)  4.35 us
    ppermute x6, waiting for transfers between devices, send(): return lax.ppermute(msg, axis, pairs)  4.29 us
    ppermute x1, starting transfers between devices, halo_from(): lax.ppermute(lax.slice_in_dim(block, 0, width, axis=dim), axis, backward)  3.65 us
  transfers between devices with their start and end apart: 11, of which 6 were waited for; matrix products, arithmetic and copies ran while one was open for 10% of the time, Pallas kernels for 0%

profile of v19, /device:TPU:90, one launch (start us, length us, event | category | flops | bytes accessed | tf_op | source)
XLA Modules:
  0.0 84.6 jit_solution(953268215858453170)
XLA Ops:
  0.0 1.2 %fusion.214 = (f32[16,2,512]{2,1,0:T(2,128)S(1)}, f32[16,2,512]{2,1,0:T(2,128)S(1)}) fusion(f32[16,32,512]{2,1,0:T(8,128)} %param.3), kind=kLoop, calls=%fused_computation.338 | loop fusion | bytes 262144 | tf_op jit(solution)/shard_map/slice | solution.py:48
  1.2 1.4 %fusion.213 = (f32[16,3,512]{2,1,0:T(4,128)S(1)}, f32[16,3,512]{2,1,0:T(4,128)S(1)}, f32[16,3,512]{2,1,0:T(4,128)S(1)}, f32[16,3,512]{2,1,0:T(4,128)S(1)}) fusion(f32[16,32,512]{2,1,0:T(8,128)} %param.4, f32[16,32,512]{2,1,0:T(8,128)} %param.5), kind=kLoop, calls=%fused_computation.337 | loop fusion | bytes 786432 | tf_op jit(solution)/shard_map/slice | solution.py:48
  2.6 0.8 pad_maximum_fusion.3
  3.4 3.5 %collective-permute-start = (f32[16,8,512]{2,1,0:T(8,128)}, f32[16,8,512]{2,1,0:T(8,128)}, u32[]{:S(2)}, u32[]{:S(2)}) collective-permute-start(f32[16,8,512]{2,1,0:T(8,128)} %pad_maximum_fusion.3), channel_id=1, source_target_pairs={{0,1},{1,2},{2,3},{3,4},{4,5},{5,6},{6,7},{8,9},{9,10},{10,11},{11... | collective-permute-start | bytes 786440 | tf_op jit(solution)/shard_map/ppermute | solution.py:58
  7.0 0.8 pad_maximum_fusion.4
  7.8 3.2 %collective-permute-start.1 = (f32[16,8,512]{2,1,0:T(8,128)}, f32[16,8,512]{2,1,0:T(8,128)}, u32[]{:S(2)}, u32[]{:S(2)}) collective-permute-start(f32[16,8,512]{2,1,0:T(8,128)} %pad_maximum_fusion.4), channel_id=1, source_target_pairs={{1,0},{2,1},{3,2},{4,3},{5,4},{6,5},{7,6},{9,8},{10,9},{11,10},{12... | collective-permute-start | bytes 786440 | tf_op jit(solution)/shard_map/ppermute | solution.py:58
  11.1 0.9 %pad_maximum_fusion = f32[8,32,512]{2,1,0:T(8,128)} fusion(f32[3,32,512]{2,1,0:T(8,128)S(1)} %get-tuple-element.90, f32[2,32,512]{2,1,0:T(8,128)S(1)} %get-tuple-element.47, f32[3,32,512]{2,1,0:T(8,128)S(1)} %get-tuple-element.45), kind=kLoop, calls=%fused_computation.129 | loop fusion | flops 262144 | bytes 1048576 | tf_op jit(solution)/shard_map/concatenate | solution.py:55
  12.0 1.9 %collective-permute-start.3 = (f32[8,32,512]{2,1,0:T(8,128)}, f32[8,32,512]{2,1,0:T(8,128)}, u32[]{:S(2)}, u32[]{:S(2)}) collective-permute-start(f32[8,32,512]{2,1,0:T(8,128)} %pad_maximum_fusion), channel_id=1, source_target_pairs={{0,8},{8,16},{16,24},{24,32},{32,40},{40,48},{48,56},{56,64},{64,7... | collective-permute-start | bytes 1572872 | tf_op jit(solution)/shard_map/ppermute | solution.py:58
  13.9 0.8 pad_maximum_fusion.1
  14.7 5.1 %collective-permute-start.5 = (f32[8,32,512]{2,1,0:T(8,128)}, f32[8,32,512]{2,1,0:T(8,128)}, u32[]{:S(2)}, u32[]{:S(2)}) collective-permute-start(f32[8,32,512]{2,1,0:T(8,128)} %pad_maximum_fusion.1), channel_id=1, source_target_pairs={{8,0},{16,8},{24,16},{32,24},{40,32},{48,40},{56,48},{64,56},{72,6... | collective-permute-start | bytes 1572872 | tf_op jit(solution)/shard_map/ppermute | solution.py:58
  20.0 0.5 fusion.186
  20.7 0.8 fusion.220
  21.5 4.3 %collective-permute-done.1 = f32[16,8,512]{2,1,0:T(8,128)} collective-permute-done((f32[16,8,512]{2,1,0:T(8,128)}, f32[16,8,512]{2,1,0:T(8,128)}, u32[]{:S(2)}, u32[]{:S(2)}) %collective-permute-start.1) | collective-permute-done | bytes 262176 | tf_op jit(solution)/shard_map/ppermute | solution.py:58
  25.8 0.8 fusion.221
  26.6 1.9 %collective-permute-start.2 = (f32[3,16,512]{2,1,0:T(8,128)S(1)}, f32[3,16,512]{2,1,0:T(8,128)S(1)}, u32[]{:S(2)}, u32[]{:S(2)}) collective-permute-start(f32[3,16,512]{2,1,0:T(8,128)S(1)} %pad_maximum_fusion.5), channel_id=1, source_target_pairs={{0,8},{8,16},{16,24},{24,32},{32,40},{40,48},{48,56},{56,64},{64,7... | collective-permute-start | bytes 294920 | tf_op jit(solution)/shard_map/ppermute | solution.py:58
  28.6 5.1 %collective-permute-start.4 = (f32[3,16,512]{2,1,0:T(8,128)S(1)}, f32[3,16,512]{2,1,0:T(8,128)S(1)}, u32[]{:S(2)}, u32[]{:S(2)}) collective-permute-start(f32[3,16,512]{2,1,0:T(8,128)S(1)} %pad_maximum_fusion.6), channel_id=1, source_target_pairs={{8,0},{16,8},{24,16},{32,24},{40,32},{48,40},{56,48},{64,56},{72,6... | collective-permute-start | bytes 294920 | tf_op jit(solution)/shard_map/ppermute | solution.py:58
  33.7 1.3 %fusion.218 = (f32[16,3,512]{2,1,0:T(4,128)S(1)}, f32[16,3,512]{2,1,0:T(4,128)S(1)}, f32[16,3,512]{2,1,0:T(4,128)S(1)}) fusion(f32[16,8,512]{2,1,0:T(8,128)} %collective-permute-done), kind=kLoop, calls=%fused_computation.342 | loop fusion | bytes 589824 | tf_op jit(solution)/shard_map/slice | solution.py:75
  35.0 1.2 %fusion.219 = (f32[16,3,512]{2,1,0:T(4,128)S(1)}, f32[16,3,512]{2,1,0:T(4,128)S(1)}, f32[16,3,512]{2,1,0:T(4,128)S(1)}) fusion(f32[16,8,512]{2,1,0:T(8,128)} %collective-permute-done.1), kind=kLoop, calls=%fused_computation.343 | loop fusion | bytes 589824 | tf_op jit(solution)/shard_map/slice | solution.py:75
  36.4 1.2 %fusion.216 = (f32[3,32,512]{2,1,0:T(8,128)S(1)}, f32[3,32,512]{2,1,0:T(8,128)S(1)}, f32[3,32,512]{2,1,0:T(8,128)S(1)}) fusion(f32[8,32,512]{2,1,0:T(8,128)} %collective-permute-done.3), kind=kLoop, calls=%fused_computation.340 | loop fusion | bytes 1179648 | tf_op jit(solution)/shard_map/slice | solution.py:74
  37.5 1.2 %fusion.217 = (f32[3,32,512]{2,1,0:T(8,128)S(1)}, f32[3,32,512]{2,1,0:T(8,128)S(1)}, f32[3,32,512]{2,1,0:T(8,128)S(1)}) fusion(f32[8,32,512]{2,1,0:T(8,128)} %collective-permute-done.5), kind=kLoop, calls=%fused_computation.341 | loop fusion | bytes 1179648 | tf_op jit(solution)/shard_map/slice | solution.py:76
  38.7 0.3 maximum_maximum_fusion.2
  39.0 0.3 maximum_maximum_fusion.1
  39.3 0.3 maximum_maximum_fusion
  39.6 2.1 %divide_select_fusion = (f32[22,38,512]{2,1,0:T(8,128)S(1)}, f32[22,38,512]{2,1,0:T(8,128)S(1)}, f32[22,38,512]{2,1,0:T(8,128)S(1)}) fusion(f32[22,38,512]{2,1,0:T(8,128)S(1)} %maximum_maximum_fusion.1), kind=kLoop, calls=%fused_computation.19 | loop fusion | flops 8560640 | bytes 6848512 | tf_op jit(solution)/shard_map/jit(_where)/select_n | solution.py:202
  41.7 4.0 %and_select_fusion.1 = (f32[22,38,512]{2,1,0:T(8,128)S(1)}, f32[22,38,512]{2,1,0:T(8,128)S(1)}) fusion(f32[22,38,512]{2,1,0:T(8,128)S(1)} %get-tuple-element.43, f32[22,38,512]{2,1,0:T(8,128)S(1)} %maximum_maximum_fusion.2, f32[22,38,512]{2,1,0:T(8,128)S(1)} %get-tuple-element.44, f32[22,38,512]{2,1,0:T(8,128)S(1)} %get-tuple-element.42, ...), kind=kLoop, calls=%fused_computation.13 | loop fusion | flops 11556864 | bytes 13697596 | tf_op jit(solution)/shard_map/jit(_where)/select_n | solution.py:249
  45.8 3.8 %and_select_fusion = f32[22,38,512]{2,1,0:T(8,128)S(1)} fusion(f32[22,38,512]{2,1,0:T(8,128)S(1)} %get-tuple-element.43, f32[22,38,512]{2,1,0:T(8,128)S(1)} %get-tuple-element.36, f32[22,38,512]{2,1,0:T(8,128)S(1)} %get-tuple-element.44, f32[22,38,512]{2,1,0:T(8,128)S(1)} %get-tuple-element.42, pred[38]{0:T(512)(128)(4,1)S(1)} %compare_and_fusion.2, ...), kind=kLoop, calls=%fused_computation.12 | loop fusion | flops 11128832 | bytes 11984956 | tf_op jit(solution)/shard_map/jit(_where)/select_n | solution.py:249
  49.6 0.5 fusion.209
  50.1 1.8 %fusion.31 = (f32[16,32,512]{2,1,0:T(8,128)S(1)}, f32[16,32,512]{2,1,0:T(8,128)S(1)}) fusion(f32[16,32,512]{2,1,0:T(8,128)S(1)} %copy-done.1, f32[22,38,512]{2,1,0:T(8,128)S(1)} %get-tuple-element.37, f32[22,38,512]{2,1,0:T(8,128)S(1)} %get-tuple-element.42, f32[22,38,512]{2,1,0:T(8,128)S(1)} %and_select_fusion, f32[22,38,512]{2,1,0:T(8,128)S(1)} %get-tuple-element.44, ...), kind=kLoop, calls=%fused_computation.111 | loop fusion | flops 4718592 | bytes 16773120 | tf_op jit(solution)/shard_map/sub | solution.py:260
  52.0 0.5 fusion.184
  52.6 0.7 collective-permute-start.6
  53.3 0.9 %collective-permute-done.6 = f32[2,4,8,128]{3,2,1,0:T(8,128)S(1)} collective-permute-done((f32[2,4,8,128]{3,2,1,0:T(8,128)S(1)}, f32[2,4,8,128]{3,2,1,0:T(8,128)S(1)}, u32[]{:S(2)}, u32[]{:S(2)}) %collective-permute-start.6) | collective-permute-done | bytes 32800 | tf_op jit(solution)/shard_map/ppermute | solution.py:144
  54.2 5.6 %collective-permute-start.7 = (f32[2,8,8,128]{3,2,1,0:T(8,128)S(1)}, f32[2,8,8,128]{3,2,1,0:T(8,128)S(1)}, u32[]{:S(2)}, u32[]{:S(2)}) collective-permute-start(f32[2,8,8,128]{3,2,1,0:T(8,128)S(1)} %maximum_select_fusion), channel_id=1, source_target_pairs={{0,16},{8,24},{16,32},{24,40},{32,48},{40,56},{48,64},{56,72},{64,... | collective-permute-start | bytes 196616 | tf_op jit(solution)/shard_map/ppermute | solution.py:147
  59.8 1.9 %collective-permute-start.8 = (f32[2,8,8,128]{3,2,1,0:T(8,128)S(1)}, f32[2,8,8,128]{3,2,1,0:T(8,128)S(1)}, u32[]{:S(2)}, u32[]{:S(2)}) collective-permute-start(f32[2,8,8,128]{3,2,1,0:T(8,128)S(1)} %maximum_select_fusion), channel_id=1, source_target_pairs={{16,0},{24,8},{32,16},{40,24},{48,32},{56,40},{64,48},{72,56},{80,... | collective-permute-start | bytes 196616 | tf_op jit(solution)/shard_map/ppermute | solution.py:148
  61.9 6.4 %collective-permute-done.8 = f32[2,8,8,128]{3,2,1,0:T(8,128)S(1)} collective-permute-done((f32[2,8,8,128]{3,2,1,0:T(8,128)S(1)}, f32[2,8,8,128]{3,2,1,0:T(8,128)S(1)}, u32[]{:S(2)}, u32[]{:S(2)}) %collective-permute-start.8) | collective-permute-done | bytes 65568 | tf_op jit(solution)/shard_map/ppermute | solution.py:148
  68.4 3.7 %collective-permute-start.10 = (f32[2,20,8,128]{3,2,1,0:T(8,128)S(1)}, f32[2,20,8,128]{3,2,1,0:T(8,128)S(1)}, u32[]{:S(2)}, u32[]{:S(2)}) collective-permute-start(f32[2,20,8,128]{3,2,1,0:T(8,128)S(1)} %fusion.170), channel_id=1, source_target_pairs={{1,0},{2,1},{3,2},{4,3},{5,4},{6,5},{7,6},{9,8},{10,9},{11,10},{12... | collective-permute-start | bytes 491528 | tf_op jit(solution)/shard_map/ppermute | solution.py:26
  72.0 2.4 %collective-permute-start.9 = (f32[2,20,8,128]{3,2,1,0:T(8,128)S(1)}, f32[2,20,8,128]{3,2,1,0:T(8,128)S(1)}, u32[]{:S(2)}, u32[]{:S(2)}) collective-permute-start(f32[2,20,8,128]{3,2,1,0:T(8,128)S(1)} %fusion.170), channel_id=1, source_target_pairs={{0,1},{1,2},{2,3},{3,4},{4,5},{5,6},{6,7},{8,9},{9,10},{10,11},{11... | collective-permute-start | bytes 491528 | tf_op jit(solution)/shard_map/ppermute | solution.py:25
  74.5 1.1 %collective-permute-done.10 = f32[2,20,8,128]{3,2,1,0:T(8,128)S(1)} collective-permute-done((f32[2,20,8,128]{3,2,1,0:T(8,128)S(1)}, f32[2,20,8,128]{3,2,1,0:T(8,128)S(1)}, u32[]{:S(2)}, u32[]{:S(2)}) %collective-permute-start.10) | collective-permute-done | bytes 163872 | tf_op jit(solution)/shard_map/ppermute | solution.py:26
  75.6 4.6 %collective-permute-done.9 = f32[2,20,8,128]{3,2,1,0:T(8,128)S(1)} collective-permute-done((f32[2,20,8,128]{3,2,1,0:T(8,128)S(1)}, f32[2,20,8,128]{3,2,1,0:T(8,128)S(1)}, u32[]{:S(2)}, u32[]{:S(2)}) %collective-permute-start.9) | collective-permute-done | bytes 163872 | tf_op jit(solution)/shard_map/ppermute | solution.py:25
  80.2 0.5 fusion.167
  80.7 0.3 fusion.168
  81.1 0.3 multiply_add_fusion.4
  81.3 0.3 multiply_add_fusion.3
  81.6 0.3 multiply_add_fusion.2
  81.9 0.3 multiply_add_fusion.1
  82.2 0.3 multiply_add_fusion
  82.7 0.5 fusion.173
  83.2 0.3 convolution_bitcast_fusion
  83.5 1.1 %bitcast_add_fusion = f32[16,32,512]{2,1,0:T(8,128)} fusion(f32[16,32,512]{2,1,0:T(8,128)S(1)} %get-tuple-element.13, f32[4,32,512]{2,1,0:T(8,128)S(1)} %convolution_bitcast_fusion), kind=kLoop, calls=%fused_computation.125 | loop fusion | flops 262144 | bytes 2359296 | tf_op jit(solution)/shard_map/add | solution.py:265
  (37 shorter events, 1.3 us)
Async XLA Ops:
  0.0 11.0 %copy-start = (f32[16,32,512]{2,1,0:T(8,128)S(1)}, f32[16,32,512]{2,1,0:T(8,128)}, u32[]{:S(2)}) copy-start(f32[16,32,512]{2,1,0:T(8,128)} %param.4) | copy-start | bytes 3145732
  0.0 11.0 %copy-start.2 = (f32[16,32,512]{2,1,0:T(8,128)S(1)}, f32[16,32,512]{2,1,0:T(8,128)}, u32[]{:S(2)}) copy-start(f32[16,32,512]{2,1,0:T(8,128)} %param.5) | copy-start | bytes 3145732
  1.2 9.8 %copy-start.1 = (f32[16,32,512]{2,1,0:T(8,128)S(1)}, f32[16,32,512]{2,1,0:T(8,128)}, u32[]{:S(2)}) copy-start(f32[16,32,512]{2,1,0:T(8,128)} %param.3) | copy-start | bytes 3145732
  3.4 17.3 %collective-permute-start = (f32[16,8,512]{2,1,0:T(8,128)}, f32[16,8,512]{2,1,0:T(8,128)}, u32[]{:S(2)}, u32[]{:S(2)}) collective-permute-start(f32[16,8,512]{2,1,0:T(8,128)} %pad_maximum_fusion.3), channel_id=1, source_target_pairs={{0,1},{1,2},{2,3},{3,4},{4,5},{5,6},{6,7},{8,9},{9,10},{10,11},{11... | collective-permute-start | bytes 786440 | tf_op jit(solution)/shard_map/ppermute | solution.py:58
  7.8 18.0 %collective-permute-start.1 = (f32[16,8,512]{2,1,0:T(8,128)}, f32[16,8,512]{2,1,0:T(8,128)}, u32[]{:S(2)}, u32[]{:S(2)}) collective-permute-start(f32[16,8,512]{2,1,0:T(8,128)} %pad_maximum_fusion.4), channel_id=1, source_target_pairs={{1,0},{2,1},{3,2},{4,3},{5,4},{6,5},{7,6},{9,8},{10,9},{11,10},{12... | collective-permute-start | bytes 786440 | tf_op jit(solution)/shard_map/ppermute | solution.py:58
  12.0 24.4 %collective-permute-start.3 = (f32[8,32,512]{2,1,0:T(8,128)}, f32[8,32,512]{2,1,0:T(8,128)}, u32[]{:S(2)}, u32[]{:S(2)}) collective-permute-start(f32[8,32,512]{2,1,0:T(8,128)} %pad_maximum_fusion), channel_id=1, source_target_pairs={{0,8},{8,16},{16,24},{24,32},{32,40},{40,48},{48,56},{56,64},{64,7... | collective-permute-start | bytes 1572872 | tf_op jit(solution)/shard_map/ppermute | solution.py:58
  14.7 22.8 %collective-permute-start.5 = (f32[8,32,512]{2,1,0:T(8,128)}, f32[8,32,512]{2,1,0:T(8,128)}, u32[]{:S(2)}, u32[]{:S(2)}) collective-permute-start(f32[8,32,512]{2,1,0:T(8,128)} %pad_maximum_fusion.1), channel_id=1, source_target_pairs={{8,0},{16,8},{24,16},{32,24},{40,32},{48,40},{56,48},{64,56},{72,6... | collective-permute-start | bytes 1572872 | tf_op jit(solution)/shard_map/ppermute | solution.py:58
  26.6 9.6 %collective-permute-start.2 = (f32[3,16,512]{2,1,0:T(8,128)S(1)}, f32[3,16,512]{2,1,0:T(8,128)S(1)}, u32[]{:S(2)}, u32[]{:S(2)}) collective-permute-start(f32[3,16,512]{2,1,0:T(8,128)S(1)} %pad_maximum_fusion.5), channel_id=1, source_target_pairs={{0,8},{8,16},{16,24},{24,32},{32,40},{40,48},{48,56},{56,64},{64,7... | collective-permute-start | bytes 294920 | tf_op jit(solution)/shard_map/ppermute | solution.py:58
  28.6 7.7 %collective-permute-start.4 = (f32[3,16,512]{2,1,0:T(8,128)S(1)}, f32[3,16,512]{2,1,0:T(8,128)S(1)}, u32[]{:S(2)}, u32[]{:S(2)}) collective-permute-start(f32[3,16,512]{2,1,0:T(8,128)S(1)} %pad_maximum_fusion.6), channel_id=1, source_target_pairs={{8,0},{16,8},{24,16},{32,24},{40,32},{48,40},{56,48},{64,56},{72,6... | collective-permute-start | bytes 294920 | tf_op jit(solution)/shard_map/ppermute | solution.py:58
  52.6 1.6 %collective-permute-start.6 = (f32[2,4,8,128]{3,2,1,0:T(8,128)S(1)}, f32[2,4,8,128]{3,2,1,0:T(8,128)S(1)}, u32[]{:S(2)}, u32[]{:S(2)}) collective-permute-start(f32[2,4,8,128]{3,2,1,0:T(8,128)S(1)} %pad_maximum_fusion.7), channel_id=1, source_target_pairs={{0,8},{8,0},{16,24},{24,16},{32,40},{40,32},{48,56},{56,48},{64,72... | collective-permute-start | bytes 98312 | tf_op jit(solution)/shard_map/ppermute | solution.py:144
  54.2 7.7 %collective-permute-start.7 = (f32[2,8,8,128]{3,2,1,0:T(8,128)S(1)}, f32[2,8,8,128]{3,2,1,0:T(8,128)S(1)}, u32[]{:S(2)}, u32[]{:S(2)}) collective-permute-start(f32[2,8,8,128]{3,2,1,0:T(8,128)S(1)} %maximum_select_fusion), channel_id=1, source_target_pairs={{0,16},{8,24},{16,32},{24,40},{32,48},{40,56},{48,64},{56,72},{64,... | collective-permute-start | bytes 196616 | tf_op jit(solution)/shard_map/ppermute | solution.py:147
  59.8 8.6 %collective-permute-start.8 = (f32[2,8,8,128]{3,2,1,0:T(8,128)S(1)}, f32[2,8,8,128]{3,2,1,0:T(8,128)S(1)}, u32[]{:S(2)}, u32[]{:S(2)}) collective-permute-start(f32[2,8,8,128]{3,2,1,0:T(8,128)S(1)} %maximum_select_fusion), channel_id=1, source_target_pairs={{16,0},{24,8},{32,16},{40,24},{48,32},{56,40},{64,48},{72,56},{80,... | collective-permute-start | bytes 196616 | tf_op jit(solution)/shard_map/ppermute | solution.py:148
  68.4 7.2 %collective-permute-start.10 = (f32[2,20,8,128]{3,2,1,0:T(8,128)S(1)}, f32[2,20,8,128]{3,2,1,0:T(8,128)S(1)}, u32[]{:S(2)}, u32[]{:S(2)}) collective-permute-start(f32[2,20,8,128]{3,2,1,0:T(8,128)S(1)} %fusion.170), channel_id=1, source_target_pairs={{1,0},{2,1},{3,2},{4,3},{5,4},{6,5},{7,6},{9,8},{10,9},{11,10},{12... | collective-permute-start | bytes 491528 | tf_op jit(solution)/shard_map/ppermute | solution.py:26
  72.0 8.1 %collective-permute-start.9 = (f32[2,20,8,128]{3,2,1,0:T(8,128)S(1)}, f32[2,20,8,128]{3,2,1,0:T(8,128)S(1)}, u32[]{:S(2)}, u32[]{:S(2)}) collective-permute-start(f32[2,20,8,128]{3,2,1,0:T(8,128)S(1)} %fusion.170), channel_id=1, source_target_pairs={{0,1},{1,2},{2,3},{3,4},{4,5},{5,6},{6,7},{8,9},{9,10},{10,11},{11... | collective-permute-start | bytes 491528 | tf_op jit(solution)/shard_map/ppermute | solution.py:25

commit v20 on v18

--- a/solution.py
+++ b/solution.py
@@ -144,6 +144,7 @@
     partner = lax.ppermute(block, "box", [(i, i ^ 1) for i in range(nb)])
     pair = jnp.where(odd == 0, jnp.concatenate([block, partner], axis=1),
                      jnp.concatenate([partner, block], axis=1))
+    pair = deep_extend(pair, "group", 2, depth)
     low = lax.ppermute(pair, "box", shifted_pairs(nb, 2))
     high = lax.ppermute(pair, "box", [(t, s) for s, t in shifted_pairs(nb, 2)])
     span = jnp.concatenate([low, pair, high], axis=1)
@@ -159,8 +160,7 @@
     if nb % 2 == 0 and nb > 2 and cx < depth <= 2 * cx:
         both = pair_extend(both, depth)
     else:
-        both = deep_extend(both, "box", 1, depth)
-    both = deep_extend(both, "group", 2, depth)
+        both = deep_extend(deep_extend(both, "box", 1, depth), "group", 2, depth)
     b_ext, rhs_ext = both[0], both[1]
     totals = (cx * lax.axis_size("box"), cy * lax.axis_size("group"))
     inside = inside_mask(b_ext.shape, depth, totals)

time: 85.3 us -> 85.9 us (level)
  the two profiles are of different devices: /device:TPU:88 before, /device:TPU:34 now
where the time goes in v20:
time: 85.9 us; the launch traced here: 85.3 us
  starting transfers between devices  40.7 us (47%)
  other arithmetic  20 us (23%)
  waiting for transfers between devices  12.4 us (14%)
  local copies, waits for them, and re-layouts  9.73 us (11%)
  matrix products  2.05 us (2%)
    ppermute x6, starting transfers between devices, send(): return lax.ppermute(msg, axis, pairs)  22.4 us
    select_n x2, other arithmetic, per_device(): fine = jnp.where(inside, fine + step, 0.0)  7.91 us
    ppermute x1, waiting for transfers between devices, pair_extend(): high = lax.ppermute(pair, 'box', [(t, s) for s, t in shifted_pairs(nb, 2)])  5.76 us
    ppermute x1, starting transfers between devices, pair_extend(): low = lax.ppermute(pair, 'box', shifted_pairs(nb, 2))  5.61 us
    ppermute x1, starting transfers between devices, pair_extend(): partner = lax.ppermute(block, 'box', [(i, i ^ 1) for i in range(nb)])  4.82 us
    ppermute x1, waiting for transfers between devices, halo_from(): lax.ppermute(lax.slice_in_dim(block, 0, width, axis=dim), axis, backward)  4.81 us
    slice x6, local copies, waits for them, and re-layouts, packed_halo(): lax.slice_in_dim(f, f.shape[dim] - d, f.shape[dim], axis=dim)  4.36 us
    ppermute x1, starting transfers between devices, halo_from(): lax.ppermute(lax.slice_in_dim(block, n - width, n, axis=dim), axis, forward)  3.99 us
  transfers between devices with their start and end apart: 11, of which 5 were waited for; matrix products, arithmetic and copies ran while one was open for 10% of the time, Pallas kernels for 0%

profile of v20, /device:TPU:34, one launch (start us, length us, event | category | flops | bytes accessed | tf_op | source)
XLA Modules:
  0.0 85.3 jit_solution(9598965951512460420)
XLA Ops:
  0.0 1.2 %fusion.230 = (f32[16,2,512]{2,1,0:T(2,128)S(1)}, f32[16,2,512]{2,1,0:T(2,128)S(1)}) fusion(f32[16,32,512]{2,1,0:T(8,128)} %param.3), kind=kLoop, calls=%fused_computation.355 | loop fusion | bytes 262144 | tf_op jit(solution)/shard_map/slice | solution.py:48
  1.2 1.4 %fusion.229 = (f32[16,3,512]{2,1,0:T(4,128)S(1)}, f32[16,3,512]{2,1,0:T(4,128)S(1)}, f32[16,3,512]{2,1,0:T(4,128)S(1)}, f32[16,3,512]{2,1,0:T(4,128)S(1)}) fusion(f32[16,32,512]{2,1,0:T(8,128)} %param.4, f32[16,32,512]{2,1,0:T(8,128)} %param.5), kind=kLoop, calls=%fused_computation.354 | loop fusion | bytes 786432 | tf_op jit(solution)/shard_map/slice | solution.py:48
  2.6 0.8 pad_maximum_fusion.2
  3.4 3.0 %collective-permute-start = (f32[16,8,512]{2,1,0:T(8,128)}, f32[16,8,512]{2,1,0:T(8,128)}, u32[]{:S(2)}, u32[]{:S(2)}) collective-permute-start(f32[16,8,512]{2,1,0:T(8,128)} %pad_maximum_fusion.2), channel_id=1, source_target_pairs={{0,1},{1,2},{2,3},{3,4},{4,5},{5,6},{6,7},{8,9},{9,10},{10,11},{11... | collective-permute-start | bytes 786440 | tf_op jit(solution)/shard_map/ppermute | solution.py:58
  6.5 0.8 pad_maximum_fusion.3
  7.3 3.5 %collective-permute-start.1 = (f32[16,8,512]{2,1,0:T(8,128)}, f32[16,8,512]{2,1,0:T(8,128)}, u32[]{:S(2)}, u32[]{:S(2)}) collective-permute-start(f32[16,8,512]{2,1,0:T(8,128)} %pad_maximum_fusion.3), channel_id=1, source_target_pairs={{1,0},{2,1},{3,2},{4,3},{5,4},{6,5},{7,6},{9,8},{10,9},{11,10},{12... | collective-permute-start | bytes 786440 | tf_op jit(solution)/shard_map/ppermute | solution.py:58
  10.9 0.9 %pad_maximum_fusion = f32[8,32,512]{2,1,0:T(8,128)} fusion(f32[3,32,512]{2,1,0:T(8,128)S(1)} %get-tuple-element.90, f32[2,32,512]{2,1,0:T(8,128)S(1)} %get-tuple-element.47, f32[3,32,512]{2,1,0:T(8,128)S(1)} %get-tuple-element.45), kind=kLoop, calls=%fused_computation.148 | loop fusion | flops 262144 | bytes 1048576 | tf_op jit(solution)/shard_map/concatenate | solution.py:55
  11.8 1.9 %collective-permute-start.3 = (f32[8,32,512]{2,1,0:T(8,128)}, f32[8,32,512]{2,1,0:T(8,128)}, u32[]{:S(2)}, u32[]{:S(2)}) collective-permute-start(f32[8,32,512]{2,1,0:T(8,128)} %pad_maximum_fusion), channel_id=1, source_target_pairs={{0,8},{8,16},{16,24},{24,32},{32,40},{40,48},{48,56},{56,64},{64,7... | collective-permute-start | bytes 1572872 | tf_op jit(solution)/shard_map/ppermute | solution.py:58
  13.7 0.8 pad_maximum_fusion.1
  14.5 6.0 %collective-permute-start.5 = (f32[8,32,512]{2,1,0:T(8,128)}, f32[8,32,512]{2,1,0:T(8,128)}, u32[]{:S(2)}, u32[]{:S(2)}) collective-permute-start(f32[8,32,512]{2,1,0:T(8,128)} %pad_maximum_fusion.1), channel_id=1, source_target_pairs={{8,0},{16,8},{24,16},{32,24},{40,32},{48,40},{56,48},{64,56},{72,6... | collective-permute-start | bytes 1572872 | tf_op jit(solution)/shard_map/ppermute | solution.py:58
  20.7 0.5 fusion.203
  21.4 0.8 fusion.236
  22.3 0.8 fusion.237
  23.1 1.9 %collective-permute-start.2 = (f32[3,16,512]{2,1,0:T(8,128)S(1)}, f32[3,16,512]{2,1,0:T(8,128)S(1)}, u32[]{:S(2)}, u32[]{:S(2)}) collective-permute-start(f32[3,16,512]{2,1,0:T(8,128)S(1)} %pad_maximum_fusion.5), channel_id=1, source_target_pairs={{0,8},{8,16},{16,24},{24,32},{32,40},{40,48},{48,56},{56,64},{64,7... | collective-permute-start | bytes 294920 | tf_op jit(solution)/shard_map/ppermute | solution.py:58
  25.0 6.0 %collective-permute-start.4 = (f32[3,16,512]{2,1,0:T(8,128)S(1)}, f32[3,16,512]{2,1,0:T(8,128)S(1)}, u32[]{:S(2)}, u32[]{:S(2)}) collective-permute-start(f32[3,16,512]{2,1,0:T(8,128)S(1)} %pad_maximum_fusion.6), channel_id=1, source_target_pairs={{8,0},{16,8},{24,16},{32,24},{40,32},{48,40},{56,48},{64,56},{72,6... | collective-permute-start | bytes 294920 | tf_op jit(solution)/shard_map/ppermute | solution.py:58
  31.1 1.3 %fusion.234 = (f32[16,3,512]{2,1,0:T(4,128)S(1)}, f32[16,3,512]{2,1,0:T(4,128)S(1)}, f32[16,3,512]{2,1,0:T(4,128)S(1)}) fusion(f32[16,8,512]{2,1,0:T(8,128)} %collective-permute-done), kind=kLoop, calls=%fused_computation.359 | loop fusion | bytes 589824 | tf_op jit(solution)/shard_map/slice | solution.py:75
  32.4 1.2 %fusion.235 = (f32[16,3,512]{2,1,0:T(4,128)S(1)}, f32[16,3,512]{2,1,0:T(4,128)S(1)}, f32[16,3,512]{2,1,0:T(4,128)S(1)}) fusion(f32[16,8,512]{2,1,0:T(8,128)} %collective-permute-done.1), kind=kLoop, calls=%fused_computation.360 | loop fusion | bytes 589824 | tf_op jit(solution)/shard_map/slice | solution.py:75
  33.7 0.7 collective-permute-done.4
  34.4 1.2 %fusion.232 = (f32[3,32,512]{2,1,0:T(8,128)S(1)}, f32[3,32,512]{2,1,0:T(8,128)S(1)}, f32[3,32,512]{2,1,0:T(8,128)S(1)}) fusion(f32[8,32,512]{2,1,0:T(8,128)} %collective-permute-done.3), kind=kLoop, calls=%fused_computation.357 | loop fusion | bytes 1179648 | tf_op jit(solution)/shard_map/slice | solution.py:74
  35.5 1.2 %fusion.233 = (f32[3,32,512]{2,1,0:T(8,128)S(1)}, f32[3,32,512]{2,1,0:T(8,128)S(1)}, f32[3,32,512]{2,1,0:T(8,128)S(1)}) fusion(f32[8,32,512]{2,1,0:T(8,128)} %collective-permute-done.5), kind=kLoop, calls=%fused_computation.358 | loop fusion | bytes 1179648 | tf_op jit(solution)/shard_map/slice | solution.py:76
  36.7 0.3 maximum_maximum_fusion.2
  37.0 0.3 maximum_maximum_fusion.1
  37.3 0.3 maximum_maximum_fusion
  37.6 2.1 %divide_select_fusion.2 = (f32[22,38,512]{2,1,0:T(8,128)S(1)}, f32[22,38,512]{2,1,0:T(8,128)S(1)}, f32[22,38,512]{2,1,0:T(8,128)S(1)}) fusion(f32[22,38,512]{2,1,0:T(8,128)S(1)} %maximum_maximum_fusion.1), kind=kLoop, calls=%fused_computation.17 | loop fusion | flops 8560640 | bytes 6848512 | tf_op jit(solution)/shard_map/jit(_where)/select_n | solution.py:202
  39.7 4.1 %and_select_fusion.1 = (f32[22,38,512]{2,1,0:T(8,128)S(1)}, f32[22,38,512]{2,1,0:T(8,128)S(1)}) fusion(f32[22,38,512]{2,1,0:T(8,128)S(1)} %maximum_maximum_fusion.2, f32[22,38,512]{2,1,0:T(8,128)S(1)} %get-tuple-element.43, f32[22,38,512]{2,1,0:T(8,128)S(1)} %get-tuple-element.44, f32[22,38,512]{2,1,0:T(8,128)S(1)} %get-tuple-element.42, ...), kind=kLoop, calls=%fused_computation.19 | loop fusion | flops 12412928 | bytes 13697596 | tf_op jit(solution)/shard_map/jit(_where)/select_n | solution.py:246
  43.8 3.8 %and_select_fusion = f32[22,38,512]{2,1,0:T(8,128)S(1)} fusion(f32[22,38,512]{2,1,0:T(8,128)S(1)} %get-tuple-element.36, f32[22,38,512]{2,1,0:T(8,128)S(1)} %get-tuple-element.37, f32[22,38,512]{2,1,0:T(8,128)S(1)} %get-tuple-element.43, f32[22,38,512]{2,1,0:T(8,128)S(1)} %get-tuple-element.44, f32[22,38,512]{2,1,0:T(8,128)S(1)} %get-tuple-element.42, ...), kind=kLoop, calls=%fused_computation.18 | loop fusion | flops 11984896 | bytes 11984956 | tf_op jit(solution)/shard_map/jit(_where)/select_n | solution.py:246
  47.6 0.5 fusion.225
  48.1 1.8 %fusion.46 = (f32[16,32,512]{2,1,0:T(8,128)S(1)}, f32[16,32,512]{2,1,0:T(8,128)S(1)}) fusion(f32[16,32,512]{2,1,0:T(8,128)S(1)} %copy-done.1, f32[22,38,512]{2,1,0:T(8,128)S(1)} %get-tuple-element.37, f32[22,38,512]{2,1,0:T(8,128)S(1)} %get-tuple-element.43, f32[22,38,512]{2,1,0:T(8,128)S(1)} %and_select_fusion, f32[22,38,512]{2,1,0:T(8,128)S(1)} %get-tuple-element.44, ...), kind=kLoop, calls=%fused_computation.125 | loop fusion | flops 4718592 | bytes 16773120 | tf_op jit(solution)/shard_map/sub | solution.py:257
  50.0 0.5 fusion.201
  50.7 4.8 %collective-permute-start.6 = (f32[2,4,8,128]{3,2,1,0:T(8,128)S(1)}, f32[2,4,8,128]{3,2,1,0:T(8,128)S(1)}, u32[]{:S(2)}, u32[]{:S(2)}) collective-permute-start(f32[2,4,8,128]{3,2,1,0:T(8,128)S(1)} %pad_maximum_fusion.7), channel_id=1, source_target_pairs={{0,8},{8,0},{16,24},{24,16},{32,40},{40,32},{48,56},{56,48},{64,72... | collective-permute-start | bytes 98312 | tf_op jit(solution)/shard_map/ppermute | solution.py:144
  55.5 0.9 %collective-permute-done.6 = f32[2,4,8,128]{3,2,1,0:T(8,128)S(1)} collective-permute-done((f32[2,4,8,128]{3,2,1,0:T(8,128)S(1)}, f32[2,4,8,128]{3,2,1,0:T(8,128)S(1)}, u32[]{:S(2)}, u32[]{:S(2)}) %collective-permute-start.6) | collective-permute-done | bytes 32800 | tf_op jit(solution)/shard_map/ppermute | solution.py:144
  56.3 4.0 %collective-permute-start.7 = (f32[2,8,8,128]{3,2,1,0:T(8,128)S(1)}, f32[2,8,8,128]{3,2,1,0:T(8,128)S(1)}, u32[]{:S(2)}, u32[]{:S(2)}) collective-permute-start(f32[2,8,8,128]{3,2,1,0:T(8,128)S(1)} %maximum_select_fusion), channel_id=1, source_target_pairs={{0,1},{1,2},{2,3},{3,4},{4,5},{5,6},{6,7},{8,9},{9,10},{10,11},{11... | collective-permute-start | bytes 196616 | tf_op jit(solution)/shard_map/ppermute | solution.py:25
  60.3 1.9 %collective-permute-start.8 = (f32[2,8,8,128]{3,2,1,0:T(8,128)S(1)}, f32[2,8,8,128]{3,2,1,0:T(8,128)S(1)}, u32[]{:S(2)}, u32[]{:S(2)}) collective-permute-start(f32[2,8,8,128]{3,2,1,0:T(8,128)S(1)} %maximum_select_fusion), channel_id=1, source_target_pairs={{1,0},{2,1},{3,2},{4,3},{5,4},{6,5},{7,6},{9,8},{10,9},{11,10},{12... | collective-permute-start | bytes 196616 | tf_op jit(solution)/shard_map/ppermute | solution.py:26
  62.3 0.3 collective-permute-done.7
  62.6 4.8 %collective-permute-done.8 = f32[2,8,8,128]{3,2,1,0:T(8,128)S(1)} collective-permute-done((f32[2,8,8,128]{3,2,1,0:T(8,128)S(1)}, f32[2,8,8,128]{3,2,1,0:T(8,128)S(1)}, u32[]{:S(2)}, u32[]{:S(2)}) %collective-permute-start.8) | collective-permute-done | bytes 65568 | tf_op jit(solution)/shard_map/ppermute | solution.py:26
  67.4 1.9 %collective-permute-start.10 = (f32[2,8,24,128]{3,2,1,0:T(8,128)S(1)}, f32[2,8,24,128]{3,2,1,0:T(8,128)S(1)}, u32[]{:S(2)}, u32[]{:S(2)}) collective-permute-start(f32[2,8,24,128]{3,2,1,0:T(8,128)S(1)} %pad_maximum_fusion.4), channel_id=1, source_target_pairs={{16,0},{24,8},{32,16},{40,24},{48,32},{56,40},{64,48},{72,56},{80,... | collective-permute-start | bytes 589832 | tf_op jit(solution)/shard_map/ppermute | solution.py:149
  69.4 5.6 %collective-permute-start.9 = (f32[2,8,24,128]{3,2,1,0:T(8,128)S(1)}, f32[2,8,24,128]{3,2,1,0:T(8,128)S(1)}, u32[]{:S(2)}, u32[]{:S(2)}) collective-permute-start(f32[2,8,24,128]{3,2,1,0:T(8,128)S(1)} %pad_maximum_fusion.4), channel_id=1, source_target_pairs={{0,16},{8,24},{16,32},{24,40},{32,48},{40,56},{48,64},{56,72},{64,... | collective-permute-start | bytes 589832 | tf_op jit(solution)/shard_map/ppermute | solution.py:148
  75.0 5.8 %collective-permute-done.10 = f32[2,8,24,128]{3,2,1,0:T(8,128)S(1)} collective-permute-done((f32[2,8,24,128]{3,2,1,0:T(8,128)S(1)}, f32[2,8,24,128]{3,2,1,0:T(8,128)S(1)}, u32[]{:S(2)}, u32[]{:S(2)}) %collective-permute-start.10) | collective-permute-done | bytes 196640 | tf_op jit(solution)/shard_map/ppermute | solution.py:149
  80.9 0.5 fusion.186
  81.4 0.3 fusion.187
  81.8 0.3 multiply_add_fusion.4
  82.0 0.3 multiply_add_fusion.3
  82.3 0.3 multiply_add_fusion.2
  82.6 0.3 multiply_add_fusion.1
  82.9 0.3 multiply_add_fusion
  83.4 0.5 fusion.190
  83.9 0.3 convolution_bitcast_fusion
  84.2 1.1 %bitcast_add_fusion = f32[16,32,512]{2,1,0:T(8,128)} fusion(f32[16,32,512]{2,1,0:T(8,128)S(1)} %get-tuple-element.13, f32[4,32,512]{2,1,0:T(8,128)S(1)} %convolution_bitcast_fusion), kind=kLoop, calls=%fused_computation.139 | loop fusion | flops 262144 | bytes 2359296 | tf_op jit(solution)/shard_map/add | solution.py:262
  (37 shorter events, 1.1 us)
Async XLA Ops:
  0.0 10.8 %copy-start = (f32[16,32,512]{2,1,0:T(8,128)S(1)}, f32[16,32,512]{2,1,0:T(8,128)}, u32[]{:S(2)}) copy-start(f32[16,32,512]{2,1,0:T(8,128)} %param.4) | copy-start | bytes 3145732
  0.0 10.8 %copy-start.2 = (f32[16,32,512]{2,1,0:T(8,128)S(1)}, f32[16,32,512]{2,1,0:T(8,128)}, u32[]{:S(2)}) copy-start(f32[16,32,512]{2,1,0:T(8,128)} %param.5) | copy-start | bytes 3145732
  1.2 9.6 %copy-start.1 = (f32[16,32,512]{2,1,0:T(8,128)S(1)}, f32[16,32,512]{2,1,0:T(8,128)}, u32[]{:S(2)}) copy-start(f32[16,32,512]{2,1,0:T(8,128)} %param.3) | copy-start | bytes 3145732
  3.4 18.0 %collective-permute-start = (f32[16,8,512]{2,1,0:T(8,128)}, f32[16,8,512]{2,1,0:T(8,128)}, u32[]{:S(2)}, u32[]{:S(2)}) collective-permute-start(f32[16,8,512]{2,1,0:T(8,128)} %pad_maximum_fusion.2), channel_id=1, source_target_pairs={{0,1},{1,2},{2,3},{3,4},{4,5},{5,6},{6,7},{8,9},{9,10},{10,11},{11... | collective-permute-start | bytes 786440 | tf_op jit(solution)/shard_map/ppermute | solution.py:58
  7.3 15.0 %collective-permute-start.1 = (f32[16,8,512]{2,1,0:T(8,128)}, f32[16,8,512]{2,1,0:T(8,128)}, u32[]{:S(2)}, u32[]{:S(2)}) collective-permute-start(f32[16,8,512]{2,1,0:T(8,128)} %pad_maximum_fusion.3), channel_id=1, source_target_pairs={{1,0},{2,1},{3,2},{4,3},{5,4},{6,5},{7,6},{9,8},{10,9},{11,10},{12... | collective-permute-start | bytes 786440 | tf_op jit(solution)/shard_map/ppermute | solution.py:58
  11.8 22.6 %collective-permute-start.3 = (f32[8,32,512]{2,1,0:T(8,128)}, f32[8,32,512]{2,1,0:T(8,128)}, u32[]{:S(2)}, u32[]{:S(2)}) collective-permute-start(f32[8,32,512]{2,1,0:T(8,128)} %pad_maximum_fusion), channel_id=1, source_target_pairs={{0,8},{8,16},{16,24},{24,32},{32,40},{40,48},{48,56},{56,64},{64,7... | collective-permute-start | bytes 1572872 | tf_op jit(solution)/shard_map/ppermute | solution.py:58
  14.5 21.0 %collective-permute-start.5 = (f32[8,32,512]{2,1,0:T(8,128)}, f32[8,32,512]{2,1,0:T(8,128)}, u32[]{:S(2)}, u32[]{:S(2)}) collective-permute-start(f32[8,32,512]{2,1,0:T(8,128)} %pad_maximum_fusion.1), channel_id=1, source_target_pairs={{8,0},{16,8},{24,16},{32,24},{40,32},{48,40},{56,48},{64,56},{72,6... | collective-permute-start | bytes 1572872 | tf_op jit(solution)/shard_map/ppermute | solution.py:58
  23.1 10.5 %collective-permute-start.2 = (f32[3,16,512]{2,1,0:T(8,128)S(1)}, f32[3,16,512]{2,1,0:T(8,128)S(1)}, u32[]{:S(2)}, u32[]{:S(2)}) collective-permute-start(f32[3,16,512]{2,1,0:T(8,128)S(1)} %pad_maximum_fusion.5), channel_id=1, source_target_pairs={{0,8},{8,16},{16,24},{24,32},{32,40},{40,48},{48,56},{56,64},{64,7... | collective-permute-start | bytes 294920 | tf_op jit(solution)/shard_map/ppermute | solution.py:58
  25.0 9.3 %collective-permute-start.4 = (f32[3,16,512]{2,1,0:T(8,128)S(1)}, f32[3,16,512]{2,1,0:T(8,128)S(1)}, u32[]{:S(2)}, u32[]{:S(2)}) collective-permute-start(f32[3,16,512]{2,1,0:T(8,128)S(1)} %pad_maximum_fusion.6), channel_id=1, source_target_pairs={{8,0},{16,8},{24,16},{32,24},{40,32},{48,40},{56,48},{64,56},{72,6... | collective-permute-start | bytes 294920 | tf_op jit(solution)/shard_map/ppermute | solution.py:58
  50.7 5.7 %collective-permute-start.6 = (f32[2,4,8,128]{3,2,1,0:T(8,128)S(1)}, f32[2,4,8,128]{3,2,1,0:T(8,128)S(1)}, u32[]{:S(2)}, u32[]{:S(2)}) collective-permute-start(f32[2,4,8,128]{3,2,1,0:T(8,128)S(1)} %pad_maximum_fusion.7), channel_id=1, source_target_pairs={{0,8},{8,0},{16,24},{24,16},{32,40},{40,32},{48,56},{56,48},{64,72... | collective-permute-start | bytes 98312 | tf_op jit(solution)/shard_map/ppermute | solution.py:144
  56.3 6.2 %collective-permute-start.7 = (f32[2,8,8,128]{3,2,1,0:T(8,128)S(1)}, f32[2,8,8,128]{3,2,1,0:T(8,128)S(1)}, u32[]{:S(2)}, u32[]{:S(2)}) collective-permute-start(f32[2,8,8,128]{3,2,1,0:T(8,128)S(1)} %maximum_select_fusion), channel_id=1, source_target_pairs={{0,1},{1,2},{2,3},{3,4},{4,5},{5,6},{6,7},{8,9},{9,10},{10,11},{11... | collective-permute-start | bytes 196616 | tf_op jit(solution)/shard_map/ppermute | solution.py:25
  60.3 7.1 %collective-permute-start.8 = (f32[2,8,8,128]{3,2,1,0:T(8,128)S(1)}, f32[2,8,8,128]{3,2,1,0:T(8,128)S(1)}, u32[]{:S(2)}, u32[]{:S(2)}) collective-permute-start(f32[2,8,8,128]{3,2,1,0:T(8,128)S(1)} %maximum_select_fusion), channel_id=1, source_target_pairs={{1,0},{2,1},{3,2},{4,3},{5,4},{6,5},{7,6},{9,8},{10,9},{11,10},{12... | collective-permute-start | bytes 196616 | tf_op jit(solution)/shard_map/ppermute | solution.py:26
  67.4 13.3 %collective-permute-start.10 = (f32[2,8,24,128]{3,2,1,0:T(8,128)S(1)}, f32[2,8,24,128]{3,2,1,0:T(8,128)S(1)}, u32[]{:S(2)}, u32[]{:S(2)}) collective-permute-start(f32[2,8,24,128]{3,2,1,0:T(8,128)S(1)} %pad_maximum_fusion.4), channel_id=1, source_target_pairs={{16,0},{24,8},{32,16},{40,24},{48,32},{56,40},{64,48},{72,56},{80,... | collective-permute-start | bytes 589832 | tf_op jit(solution)/shard_map/ppermute | solution.py:149
  69.4 11.4 %collective-permute-start.9 = (f32[2,8,24,128]{3,2,1,0:T(8,128)S(1)}, f32[2,8,24,128]{3,2,1,0:T(8,128)S(1)}, u32[]{:S(2)}, u32[]{:S(2)}) collective-permute-start(f32[2,8,24,128]{3,2,1,0:T(8,128)S(1)} %pad_maximum_fusion.4), channel_id=1, source_target_pairs={{0,16},{8,24},{16,32},{24,40},{32,48},{40,56},{48,64},{56,72},{64,... | collective-permute-start | bytes 589832 | tf_op jit(solution)/shard_map/ppermute | solution.py:148

commit v21 on v18

--- a/solution.py
+++ b/solution.py
@@ -57,8 +57,14 @@
             return jnp.zeros_like(msg)
         return lax.ppermute(msg, axis, pairs)
 
-    xl = send([up(f, d, 0) for f, d in zip(fields, depths)], "box", fb, 0)
-    xh = send([down(f, d, 0) for f, d in zip(fields, depths)], "box", bb, 0)
+    def send_split(pieces, axis, pairs, dim):
+        msg = jnp.concatenate(pieces, axis=dim)
+        half = msg.shape[2] // 2
+        parts = [msg[:, :, :half], msg[:, :, half:]]
+        return jnp.concatenate([send([p], axis, pairs, dim) for p in parts], axis=2)
+
+    xl = send_split([up(f, d, 0) for f, d in zip(fields, depths)], "box", fb, 0)
+    xh = send_split([down(f, d, 0) for f, d in zip(fields, depths)], "box", bb, 0)
     yl = send([up(f, d, 1) for f, d in zip(fields, depths)], "group", fg, 1)
     yh = send([down(f, d, 1) for f, d in zip(fields, depths)], "group", bg, 1)
     low = send([up(yl, top, 0), up(yh, top, 0)], "box", fb, 1)

time: 85.3 us -> 87.1 us (1.021)
  the two profiles are of different devices: /device:TPU:88 before, /device:TPU:34 now
where the time goes in v21:
time: 87.1 us; the launch traced here: 85.5 us
  starting transfers between devices  40.4 us (46%)
  other arithmetic  18.3 us (21%)
  local copies, waits for them, and re-layouts  12.1 us (14%)
  waiting for transfers between devices  12.1 us (14%)
  matrix products  2.05 us (2%)
    ppermute x8, starting transfers between devices, send(): return lax.ppermute(msg, axis, pairs)  26.7 us
    select_n x2, other arithmetic, per_device(): fine = jnp.where(inside, fine + step, 0.0)  7.87 us
    ppermute x1, waiting for transfers between devices, halo_from(): lax.ppermute(lax.slice_in_dim(block, 0, width, axis=dim), axis, backward)  5.05 us
    ppermute x1, waiting for transfers between devices, pair_extend(): low = lax.ppermute(pair, 'box', shifted_pairs(nb, 2))  4.65 us
    slice x7, local copies, waits for them, and re-layouts, packed_halo(): lax.slice_in_dim(f, f.shape[dim] - d, f.shape[dim], axis=dim)  4.36 us
    ppermute x1, starting transfers between devices, halo_from(): lax.ppermute(lax.slice_in_dim(block, n - width, n, axis=dim), axis, forward)  4.14 us
    ppermute x1, starting transfers between devices, pair_extend(): high = lax.ppermute(pair, 'box', [(t, s) for s, t in shifted_pairs(nb, 2)])  3.75 us
    ppermute x1, starting transfers between devices, pair_extend(): low = lax.ppermute(pair, 'box', shifted_pairs(nb, 2))  3.6 us
  transfers between devices with their start and end apart: 13, of which 5 were waited for; matrix products, arithmetic and copies ran while one was open for 12% of the time, Pallas kernels for 0%

profile of v21, /device:TPU:34, one launch (start us, length us, event | category | flops | bytes accessed | tf_op | source)
XLA Modules:
  0.0 85.5 jit_solution(841099373194616524)
XLA Ops:
  0.0 1.2 %fusion.228 = (f32[16,2,512]{2,1,0:T(2,128)S(1)}, f32[16,2,512]{2,1,0:T(2,128)S(1)}) fusion(f32[16,32,512]{2,1,0:T(8,128)} %param.3), kind=kLoop, calls=%fused_computation.355 | loop fusion | bytes 262144 | tf_op jit(solution)/shard_map/slice | solution.py:48
  1.2 1.4 %fusion.227 = (f32[16,3,512]{2,1,0:T(4,128)S(1)}, f32[16,3,512]{2,1,0:T(4,128)S(1)}, f32[16,3,512]{2,1,0:T(4,128)S(1)}, f32[16,3,512]{2,1,0:T(4,128)S(1)}) fusion(f32[16,32,512]{2,1,0:T(8,128)} %param.4, f32[16,32,512]{2,1,0:T(8,128)} %param.5), kind=kLoop, calls=%fused_computation.354 | loop fusion | bytes 786432 | tf_op jit(solution)/shard_map/slice | solution.py:48
  2.6 0.8 pad_maximum_fusion.3
  3.4 3.0 %collective-permute-start = (f32[16,8,512]{2,1,0:T(8,128)}, f32[16,8,512]{2,1,0:T(8,128)}, u32[]{:S(2)}, u32[]{:S(2)}) collective-permute-start(f32[16,8,512]{2,1,0:T(8,128)} %pad_maximum_fusion.3), channel_id=1, source_target_pairs={{0,1},{1,2},{2,3},{3,4},{4,5},{5,6},{6,7},{8,9},{9,10},{10,11},{11... | collective-permute-start | bytes 786440 | tf_op jit(solution)/shard_map/ppermute | solution.py:58
  6.5 0.8 pad_maximum_fusion.4
  7.2 3.5 %collective-permute-start.1 = (f32[16,8,512]{2,1,0:T(8,128)}, f32[16,8,512]{2,1,0:T(8,128)}, u32[]{:S(2)}, u32[]{:S(2)}) collective-permute-start(f32[16,8,512]{2,1,0:T(8,128)} %pad_maximum_fusion.4), channel_id=1, source_target_pairs={{1,0},{2,1},{3,2},{4,3},{5,4},{6,5},{7,6},{9,8},{10,9},{11,10},{12... | collective-permute-start | bytes 786440 | tf_op jit(solution)/shard_map/ppermute | solution.py:58
  11.0 0.9 %fusion.232 = (f32[8,32,256]{2,1,0:T(8,128)}, f32[8,32,256]{2,1,0:T(8,128)}) fusion(f32[8,32,512]{2,1,0:T(8,128)S(1)} %get-tuple-element.93), kind=kLoop, calls=%fused_computation.359 | loop fusion | bytes 1048576 | tf_op jit(solution)/shard_map/slice | solution.py:63
  11.8 1.9 %collective-permute-start.3 = (f32[8,32,256]{2,1,0:T(8,128)}, f32[8,32,256]{2,1,0:T(8,128)}, u32[]{:S(2)}, u32[]{:S(2)}) collective-permute-start(f32[8,32,256]{2,1,0:T(8,128)} %get-tuple-element.64), channel_id=1, source_target_pairs={{0,8},{8,16},{16,24},{24,32},{32,40},{40,48},{48,56},{56,64},{64,7... | collective-permute-start | bytes 786440 | tf_op jit(solution)/shard_map/ppermute | solution.py:58
  13.7 5.0 %collective-permute-start.4 = (f32[8,32,256]{2,1,0:T(8,128)}, f32[8,32,256]{2,1,0:T(8,128)}, u32[]{:S(2)}, u32[]{:S(2)}) collective-permute-start(f32[8,32,256]{2,1,0:T(8,128)} %get-tuple-element.63), channel_id=1, source_target_pairs={{0,8},{8,16},{16,24},{24,32},{32,40},{40,48},{48,56},{56,64},{64,7... | collective-permute-start | bytes 786440 | tf_op jit(solution)/shard_map/ppermute | solution.py:58
  18.7 0.9 %fusion.233 = (f32[8,32,256]{2,1,0:T(8,128)}, f32[8,32,256]{2,1,0:T(8,128)}) fusion(f32[8,32,512]{2,1,0:T(8,128)S(1)} %get-tuple-element.94), kind=kLoop, calls=%fused_computation.360 | loop fusion | bytes 1048576 | tf_op jit(solution)/shard_map/slice | solution.py:63
  19.6 3.0 %collective-permute-start.6 = (f32[8,32,256]{2,1,0:T(8,128)}, f32[8,32,256]{2,1,0:T(8,128)}, u32[]{:S(2)}, u32[]{:S(2)}) collective-permute-start(f32[8,32,256]{2,1,0:T(8,128)} %get-tuple-element.66), channel_id=1, source_target_pairs={{8,0},{16,8},{24,16},{32,24},{40,32},{48,40},{56,48},{64,56},{72,6... | collective-permute-start | bytes 786440 | tf_op jit(solution)/shard_map/ppermute | solution.py:58
  22.7 0.5 fusion.201
  23.4 2.4 %collective-permute-start.7 = (f32[8,32,256]{2,1,0:T(8,128)}, f32[8,32,256]{2,1,0:T(8,128)S(1)}, u32[]{:S(2)}, u32[]{:S(2)}) collective-permute-start(f32[8,32,256]{2,1,0:T(8,128)} %get-tuple-element.65), channel_id=1, source_target_pairs={{8,0},{16,8},{24,16},{32,24},{40,32},{48,40},{56,48},{64,56},{72,6... | collective-permute-start | bytes 786440 | tf_op jit(solution)/shard_map/ppermute | solution.py:58
  25.8 0.8 fusion.236
  26.7 0.8 fusion.237
  27.5 1.9 %collective-permute-start.2 = (f32[3,16,512]{2,1,0:T(8,128)S(1)}, f32[3,16,512]{2,1,0:T(8,128)S(1)}, u32[]{:S(2)}, u32[]{:S(2)}) collective-permute-start(f32[3,16,512]{2,1,0:T(8,128)S(1)} %pad_maximum_fusion.5), channel_id=1, source_target_pairs={{0,8},{8,16},{16,24},{24,32},{32,40},{40,48},{48,56},{56,64},{64,7... | collective-permute-start | bytes 294920 | tf_op jit(solution)/shard_map/ppermute | solution.py:58
  29.5 6.0 %collective-permute-start.5 = (f32[3,16,512]{2,1,0:T(8,128)S(1)}, f32[3,16,512]{2,1,0:T(8,128)S(1)}, u32[]{:S(2)}, u32[]{:S(2)}) collective-permute-start(f32[3,16,512]{2,1,0:T(8,128)S(1)} %pad_maximum_fusion.6), channel_id=1, source_target_pairs={{8,0},{16,8},{24,16},{32,24},{40,32},{48,40},{56,48},{64,56},{72,6... | collective-permute-start | bytes 294920 | tf_op jit(solution)/shard_map/ppermute | solution.py:58
  35.5 1.0 %constant_dynamic-update-slice_fusion.1 = f32[8,32,512]{2,1,0:T(8,128)S(1)} fusion(f32[8,32,256]{2,1,0:T(8,128)} %collective-permute-done.3), kind=kLoop, calls=%fused_computation.320 | loop fusion | bytes 524288
  36.5 1.0 %constant_dynamic-update-slice_fusion.3 = f32[8,32,512]{2,1,0:T(8,128)S(1)} fusion(f32[8,32,256]{2,1,0:T(8,128)} %collective-permute-done.6), kind=kLoop, calls=%fused_computation.322 | loop fusion | bytes 524288
  37.5 1.0 %constant_dynamic-update-slice_fusion = f32[8,32,512]{2,1,0:T(8,128)S(1)} fusion(f32[8,32,512]{2,1,0:T(8,128)S(1)} %constant_dynamic-update-slice_fusion.1, f32[8,32,256]{2,1,0:T(8,128)} %collective-permute-done.4), kind=kLoop, calls=%fused_computation.319 | loop fusion | bytes 524288 | tf_op jit(solution)/shard_map/concatenate | solution.py:64
  38.6 1.2 %fusion.234 = (f32[16,3,512]{2,1,0:T(4,128)S(1)}, f32[16,3,512]{2,1,0:T(4,128)S(1)}, f32[16,3,512]{2,1,0:T(4,128)S(1)}) fusion(f32[16,8,512]{2,1,0:T(8,128)} %collective-permute-done), kind=kLoop, calls=%fused_computation.361 | loop fusion | bytes 589824 | tf_op jit(solution)/shard_map/slice | solution.py:81
  39.8 1.2 %fusion.235 = (f32[16,3,512]{2,1,0:T(4,128)S(1)}, f32[16,3,512]{2,1,0:T(4,128)S(1)}, f32[16,3,512]{2,1,0:T(4,128)S(1)}) fusion(f32[16,8,512]{2,1,0:T(8,128)} %collective-permute-done.1), kind=kLoop, calls=%fused_computation.362 | loop fusion | bytes 589824 | tf_op jit(solution)/shard_map/slice | solution.py:81
  41.2 0.3 maximum_maximum_fusion.2
  41.5 0.3 maximum_maximum_fusion.1
  41.7 0.3 maximum_maximum_fusion
  42.0 2.1 %divide_select_fusion.2 = (f32[22,38,512]{2,1,0:T(8,128)S(1)}, f32[22,38,512]{2,1,0:T(8,128)S(1)}, f32[22,38,512]{2,1,0:T(8,128)S(1)}) fusion(f32[22,38,512]{2,1,0:T(8,128)S(1)} %maximum_maximum_fusion.1), kind=kLoop, calls=%fused_computation.17 | loop fusion | flops 8560640 | bytes 6848512 | tf_op jit(solution)/shard_map/jit(_where)/select_n | solution.py:208
  44.2 4.1 %and_select_fusion.1 = (f32[22,38,512]{2,1,0:T(8,128)S(1)}, f32[22,38,512]{2,1,0:T(8,128)S(1)}) fusion(f32[22,38,512]{2,1,0:T(8,128)S(1)} %maximum_maximum_fusion.2, f32[22,38,512]{2,1,0:T(8,128)S(1)} %get-tuple-element.43, f32[22,38,512]{2,1,0:T(8,128)S(1)} %get-tuple-element.44, f32[22,38,512]{2,1,0:T(8,128)S(1)} %get-tuple-element.42, ...), kind=kLoop, calls=%fused_computation.19 | loop fusion | flops 12412928 | bytes 13697596 | tf_op jit(solution)/shard_map/jit(_where)/select_n | solution.py:252
  48.3 3.8 %and_select_fusion = f32[22,38,512]{2,1,0:T(8,128)S(1)} fusion(f32[22,38,512]{2,1,0:T(8,128)S(1)} %get-tuple-element.36, f32[22,38,512]{2,1,0:T(8,128)S(1)} %get-tuple-element.37, f32[22,38,512]{2,1,0:T(8,128)S(1)} %get-tuple-element.43, f32[22,38,512]{2,1,0:T(8,128)S(1)} %get-tuple-element.44, f32[22,38,512]{2,1,0:T(8,128)S(1)} %get-tuple-element.42, ...), kind=kLoop, calls=%fused_computation.18 | loop fusion | flops 11984896 | bytes 11984956 | tf_op jit(solution)/shard_map/jit(_where)/select_n | solution.py:252
  52.1 0.5 fusion.223
  52.5 1.8 %fusion.46 = (f32[16,32,512]{2,1,0:T(8,128)S(1)}, f32[16,32,512]{2,1,0:T(8,128)S(1)}) fusion(f32[16,32,512]{2,1,0:T(8,128)S(1)} %copy-done.1, f32[22,38,512]{2,1,0:T(8,128)S(1)} %get-tuple-element.37, f32[22,38,512]{2,1,0:T(8,128)S(1)} %get-tuple-element.43, f32[22,38,512]{2,1,0:T(8,128)S(1)} %and_select_fusion, f32[22,38,512]{2,1,0:T(8,128)S(1)} %get-tuple-element.44, ...), kind=kLoop, calls=%fused_computation.125 | loop fusion | flops 4718592 | bytes 16773120 | tf_op jit(solution)/shard_map/sub | solution.py:263
  54.4 0.5 fusion.199
  55.2 1.2 %collective-permute-done.8 = f32[2,4,8,128]{3,2,1,0:T(8,128)S(1)} collective-permute-done((f32[2,4,8,128]{3,2,1,0:T(8,128)S(1)}, f32[2,4,8,128]{3,2,1,0:T(8,128)S(1)}, u32[]{:S(2)}, u32[]{:S(2)}) %collective-permute-start.8) | collective-permute-done | bytes 32800 | tf_op jit(solution)/shard_map/ppermute | solution.py:150
  56.4 3.7 %collective-permute-start.10 = (f32[2,8,8,128]{3,2,1,0:T(8,128)S(1)}, f32[2,8,8,128]{3,2,1,0:T(8,128)S(1)}, u32[]{:S(2)}, u32[]{:S(2)}) collective-permute-start(f32[2,8,8,128]{3,2,1,0:T(8,128)S(1)} %maximum_select_fusion), channel_id=1, source_target_pairs={{16,0},{24,8},{32,16},{40,24},{48,32},{56,40},{64,48},{72,56},{80,... | collective-permute-start | bytes 196616 | tf_op jit(solution)/shard_map/ppermute | solution.py:154
  60.1 3.6 %collective-permute-start.9 = (f32[2,8,8,128]{3,2,1,0:T(8,128)S(1)}, f32[2,8,8,128]{3,2,1,0:T(8,128)S(1)}, u32[]{:S(2)}, u32[]{:S(2)}) collective-permute-start(f32[2,8,8,128]{3,2,1,0:T(8,128)S(1)} %maximum_select_fusion), channel_id=1, source_target_pairs={{0,16},{8,24},{16,32},{24,40},{32,48},{40,56},{48,64},{56,72},{64,... | collective-permute-start | bytes 196616 | tf_op jit(solution)/shard_map/ppermute | solution.py:153
  63.7 0.3 collective-permute-done.10
  64.0 4.7 %collective-permute-done.9 = f32[2,8,8,128]{3,2,1,0:T(8,128)S(1)} collective-permute-done((f32[2,8,8,128]{3,2,1,0:T(8,128)S(1)}, f32[2,8,8,128]{3,2,1,0:T(8,128)S(1)}, u32[]{:S(2)}, u32[]{:S(2)}) %collective-permute-start.9) | collective-permute-done | bytes 65568 | tf_op jit(solution)/shard_map/ppermute | solution.py:153
  68.8 4.1 %collective-permute-start.11 = (f32[2,20,8,128]{3,2,1,0:T(8,128)S(1)}, f32[2,20,8,128]{3,2,1,0:T(8,128)S(1)}, u32[]{:S(2)}, u32[]{:S(2)}) collective-permute-start(f32[2,20,8,128]{3,2,1,0:T(8,128)S(1)} %fusion.185), channel_id=1, source_target_pairs={{0,1},{1,2},{2,3},{3,4},{4,5},{5,6},{6,7},{8,9},{9,10},{10,11},{11... | collective-permute-start | bytes 491528 | tf_op jit(solution)/shard_map/ppermute | solution.py:25
  72.9 2.1 %collective-permute-start.12 = (f32[2,20,8,128]{3,2,1,0:T(8,128)S(1)}, f32[2,20,8,128]{3,2,1,0:T(8,128)S(1)}, u32[]{:S(2)}, u32[]{:S(2)}) collective-permute-start(f32[2,20,8,128]{3,2,1,0:T(8,128)S(1)} %fusion.185), channel_id=1, source_target_pairs={{1,0},{2,1},{3,2},{4,3},{5,4},{6,5},{7,6},{9,8},{10,9},{11,10},{12... | collective-permute-start | bytes 491528 | tf_op jit(solution)/shard_map/ppermute | solution.py:26
  75.0 0.9 %collective-permute-done.11 = f32[2,20,8,128]{3,2,1,0:T(8,128)S(1)} collective-permute-done((f32[2,20,8,128]{3,2,1,0:T(8,128)S(1)}, f32[2,20,8,128]{3,2,1,0:T(8,128)S(1)}, u32[]{:S(2)}, u32[]{:S(2)}) %collective-permute-start.11) | collective-permute-done | bytes 163872 | tf_op jit(solution)/shard_map/ppermute | solution.py:25
  76.0 5.0 %collective-permute-done.12 = f32[2,20,8,128]{3,2,1,0:T(8,128)S(1)} collective-permute-done((f32[2,20,8,128]{3,2,1,0:T(8,128)S(1)}, f32[2,20,8,128]{3,2,1,0:T(8,128)S(1)}, u32[]{:S(2)}, u32[]{:S(2)}) %collective-permute-start.12) | collective-permute-done | bytes 163872 | tf_op jit(solution)/shard_map/ppermute | solution.py:26
  81.1 0.5 fusion.182
  81.6 0.3 fusion.183
  82.2 0.3 multiply_add_fusion.3
  82.5 0.3 multiply_add_fusion.2
  83.0 0.3 multiply_add_fusion
  83.6 0.5 fusion.188
  84.0 0.3 convolution_bitcast_fusion
  84.4 1.1 %bitcast_add_fusion = f32[16,32,512]{2,1,0:T(8,128)} fusion(f32[16,32,512]{2,1,0:T(8,128)S(1)} %get-tuple-element.13, f32[4,32,512]{2,1,0:T(8,128)S(1)} %convolution_bitcast_fusion), kind=kLoop, calls=%fused_computation.139 | loop fusion | flops 262144 | bytes 2359296 | tf_op jit(solution)/shard_map/add | solution.py:268
  (47 shorter events, 1.9 us)
Async XLA Ops:
  0.0 10.7 %copy-start = (f32[16,32,512]{2,1,0:T(8,128)S(1)}, f32[16,32,512]{2,1,0:T(8,128)}, u32[]{:S(2)}) copy-start(f32[16,32,512]{2,1,0:T(8,128)} %param.4) | copy-start | bytes 3145732
  0.0 10.8 %copy-start.2 = (f32[16,32,512]{2,1,0:T(8,128)S(1)}, f32[16,32,512]{2,1,0:T(8,128)}, u32[]{:S(2)}) copy-start(f32[16,32,512]{2,1,0:T(8,128)} %param.5) | copy-start | bytes 3145732
  1.2 9.6 %copy-start.1 = (f32[16,32,512]{2,1,0:T(8,128)S(1)}, f32[16,32,512]{2,1,0:T(8,128)}, u32[]{:S(2)}) copy-start(f32[16,32,512]{2,1,0:T(8,128)} %param.3) | copy-start | bytes 3145732
  3.4 20.0 %collective-permute-start = (f32[16,8,512]{2,1,0:T(8,128)}, f32[16,8,512]{2,1,0:T(8,128)}, u32[]{:S(2)}, u32[]{:S(2)}) collective-permute-start(f32[16,8,512]{2,1,0:T(8,128)} %pad_maximum_fusion.3), channel_id=1, source_target_pairs={{0,1},{1,2},{2,3},{3,4},{4,5},{5,6},{6,7},{8,9},{9,10},{10,11},{11... | collective-permute-start | bytes 786440 | tf_op jit(solution)/shard_map/ppermute | solution.py:58
  7.2 19.4 %collective-permute-start.1 = (f32[16,8,512]{2,1,0:T(8,128)}, f32[16,8,512]{2,1,0:T(8,128)}, u32[]{:S(2)}, u32[]{:S(2)}) collective-permute-start(f32[16,8,512]{2,1,0:T(8,128)} %pad_maximum_fusion.4), channel_id=1, source_target_pairs={{1,0},{2,1},{3,2},{4,3},{5,4},{6,5},{7,6},{9,8},{10,9},{11,10},{12... | collective-permute-start | bytes 786440 | tf_op jit(solution)/shard_map/ppermute | solution.py:58
  11.8 17.6 %collective-permute-start.3 = (f32[8,32,256]{2,1,0:T(8,128)}, f32[8,32,256]{2,1,0:T(8,128)}, u32[]{:S(2)}, u32[]{:S(2)}) collective-permute-start(f32[8,32,256]{2,1,0:T(8,128)} %get-tuple-element.64), channel_id=1, source_target_pairs={{0,8},{8,16},{16,24},{24,32},{32,40},{40,48},{48,56},{56,64},{64,7... | collective-permute-start | bytes 786440 | tf_op jit(solution)/shard_map/ppermute | solution.py:58
  13.7 23.7 %collective-permute-start.4 = (f32[8,32,256]{2,1,0:T(8,128)}, f32[8,32,256]{2,1,0:T(8,128)}, u32[]{:S(2)}, u32[]{:S(2)}) collective-permute-start(f32[8,32,256]{2,1,0:T(8,128)} %get-tuple-element.63), channel_id=1, source_target_pairs={{0,8},{8,16},{16,24},{24,32},{32,40},{40,48},{48,56},{56,64},{64,7... | collective-permute-start | bytes 786440 | tf_op jit(solution)/shard_map/ppermute | solution.py:58
  19.6 16.9 %collective-permute-start.6 = (f32[8,32,256]{2,1,0:T(8,128)}, f32[8,32,256]{2,1,0:T(8,128)}, u32[]{:S(2)}, u32[]{:S(2)}) collective-permute-start(f32[8,32,256]{2,1,0:T(8,128)} %get-tuple-element.66), channel_id=1, source_target_pairs={{8,0},{16,8},{24,16},{32,24},{40,32},{48,40},{56,48},{64,56},{72,6... | collective-permute-start | bytes 786440 | tf_op jit(solution)/shard_map/ppermute | solution.py:58
  23.4 15.1 %collective-permute-start.7 = (f32[8,32,256]{2,1,0:T(8,128)}, f32[8,32,256]{2,1,0:T(8,128)S(1)}, u32[]{:S(2)}, u32[]{:S(2)}) collective-permute-start(f32[8,32,256]{2,1,0:T(8,128)} %get-tuple-element.65), channel_id=1, source_target_pairs={{8,0},{16,8},{24,16},{32,24},{40,32},{48,40},{56,48},{64,56},{72,6... | collective-permute-start | bytes 786440 | tf_op jit(solution)/shard_map/ppermute | solution.py:58
  27.5 13.6 %collective-permute-start.2 = (f32[3,16,512]{2,1,0:T(8,128)S(1)}, f32[3,16,512]{2,1,0:T(8,128)S(1)}, u32[]{:S(2)}, u32[]{:S(2)}) collective-permute-start(f32[3,16,512]{2,1,0:T(8,128)S(1)} %pad_maximum_fusion.5), channel_id=1, source_target_pairs={{0,8},{8,16},{16,24},{24,32},{32,40},{40,48},{48,56},{56,64},{64,7... | collective-permute-start | bytes 294920 | tf_op jit(solution)/shard_map/ppermute | solution.py:58
  29.5 11.6 %collective-permute-start.5 = (f32[3,16,512]{2,1,0:T(8,128)S(1)}, f32[3,16,512]{2,1,0:T(8,128)S(1)}, u32[]{:S(2)}, u32[]{:S(2)}) collective-permute-start(f32[3,16,512]{2,1,0:T(8,128)S(1)} %pad_maximum_fusion.6), channel_id=1, source_target_pairs={{8,0},{16,8},{24,16},{32,24},{40,32},{48,40},{56,48},{64,56},{72,6... | collective-permute-start | bytes 294920 | tf_op jit(solution)/shard_map/ppermute | solution.py:58
  55.1 1.3 %collective-permute-start.8 = (f32[2,4,8,128]{3,2,1,0:T(8,128)S(1)}, f32[2,4,8,128]{3,2,1,0:T(8,128)S(1)}, u32[]{:S(2)}, u32[]{:S(2)}) collective-permute-start(f32[2,4,8,128]{3,2,1,0:T(8,128)S(1)} %pad_maximum_fusion.7), channel_id=1, source_target_pairs={{0,8},{8,0},{16,24},{24,16},{32,40},{40,32},{48,56},{56,48},{64,72... | collective-permute-start | bytes 98312 | tf_op jit(solution)/shard_map/ppermute | solution.py:150
  56.4 7.7 %collective-permute-start.10 = (f32[2,8,8,128]{3,2,1,0:T(8,128)S(1)}, f32[2,8,8,128]{3,2,1,0:T(8,128)S(1)}, u32[]{:S(2)}, u32[]{:S(2)}) collective-permute-start(f32[2,8,8,128]{3,2,1,0:T(8,128)S(1)} %maximum_select_fusion), channel_id=1, source_target_pairs={{16,0},{24,8},{32,16},{40,24},{48,32},{56,40},{64,48},{72,56},{80,... | collective-permute-start | bytes 196616 | tf_op jit(solution)/shard_map/ppermute | solution.py:154
  60.1 8.6 %collective-permute-start.9 = (f32[2,8,8,128]{3,2,1,0:T(8,128)S(1)}, f32[2,8,8,128]{3,2,1,0:T(8,128)S(1)}, u32[]{:S(2)}, u32[]{:S(2)}) collective-permute-start(f32[2,8,8,128]{3,2,1,0:T(8,128)S(1)} %maximum_select_fusion), channel_id=1, source_target_pairs={{0,16},{8,24},{16,32},{24,40},{32,48},{40,56},{48,64},{56,72},{64,... | collective-permute-start | bytes 196616 | tf_op jit(solution)/shard_map/ppermute | solution.py:153
  68.8 7.2 %collective-permute-start.11 = (f32[2,20,8,128]{3,2,1,0:T(8,128)S(1)}, f32[2,20,8,128]{3,2,1,0:T(8,128)S(1)}, u32[]{:S(2)}, u32[]{:S(2)}) collective-permute-start(f32[2,20,8,128]{3,2,1,0:T(8,128)S(1)} %fusion.185), channel_id=1, source_target_pairs={{0,1},{1,2},{2,3},{3,4},{4,5},{5,6},{6,7},{8,9},{9,10},{10,11},{11... | collective-permute-start | bytes 491528 | tf_op jit(solution)/shard_map/ppermute | solution.py:25
  72.9 8.1 %collective-permute-start.12 = (f32[2,20,8,128]{3,2,1,0:T(8,128)S(1)}, f32[2,20,8,128]{3,2,1,0:T(8,128)S(1)}, u32[]{:S(2)}, u32[]{:S(2)}) collective-permute-start(f32[2,20,8,128]{3,2,1,0:T(8,128)S(1)} %fusion.185), channel_id=1, source_target_pairs={{1,0},{2,1},{3,2},{4,3},{5,4},{6,5},{7,6},{9,8},{10,9},{11,10},{12... | collective-permute-start | bytes 491528 | tf_op jit(solution)/shard_map/ppermute | solution.py:26

commit v22 on v18

--- a/solution.py
+++ b/solution.py
@@ -160,7 +160,13 @@
         both = pair_extend(both, depth)
     else:
         both = deep_extend(both, "box", 1, depth)
-    both = deep_extend(both, "group", 2, depth)
+    edge = jnp.zeros_like(both[:, :1, :depth])
+    inner = deep_extend(both[:, 1:-1], "group", 2, depth)
+    both = jnp.concatenate([
+        jnp.concatenate([edge, both[:, :1], edge], axis=2),
+        inner,
+        jnp.concatenate([edge, both[:, -1:], edge], axis=2),
+    ], axis=1)
     b_ext, rhs_ext = both[0], both[1]
     totals = (cx * lax.axis_size("box"), cy * lax.axis_size("group"))
     inside = inside_mask(b_ext.shape, depth, totals)

time: 85.3 us -> 85.1 us (level)
  the two profiles are of different devices: /device:TPU:88 before, /device:TPU:90 now
where the time goes in v22:
time: 85.1 us; the launch traced here: 84.5 us
  starting transfers between devices  35 us (41%)
  other arithmetic  20 us (24%)
  waiting for transfers between devices  17.3 us (20%)
  local copies, waits for them, and re-layouts  9.76 us (11%)
  matrix products  2.05 us (2%)
    ppermute x6, starting transfers between devices, send(): return lax.ppermute(msg, axis, pairs)  20.8 us
    select_n x2, other arithmetic, per_device(): fine = jnp.where(inside, fine + step, 0.0)  7.91 us
    ppermute x1, waiting for transfers between devices, pair_extend(): high = lax.ppermute(pair, 'box', [(t, s) for s, t in shifted_pairs(nb, 2)])  6.38 us
    ppermute x1, starting transfers between devices, pair_extend(): low = lax.ppermute(pair, 'box', shifted_pairs(nb, 2))  5.55 us
    ppermute x1, waiting for transfers between devices, halo_from(): lax.ppermute(lax.slice_in_dim(block, n - width, n, axis=dim), axis, forward)  4.56 us
    slice x6, local copies, waits for them, and re-layouts, packed_halo(): lax.slice_in_dim(f, f.shape[dim] - d, f.shape[dim], axis=dim)  4.35 us
    ppermute x6, waiting for transfers between devices, send(): return lax.ppermute(msg, axis, pairs)  4.28 us
    ppermute x1, starting transfers between devices, halo_from(): lax.ppermute(lax.slice_in_dim(block, 0, width, axis=dim), axis, backward)  3.65 us
  transfers between devices with their start and end apart: 11, of which 6 were waited for; matrix products, arithmetic and copies ran while one was open for 10% of the time, Pallas kernels for 0%

profile of v22, /device:TPU:90, one launch (start us, length us, event | category | flops | bytes accessed | tf_op | source)
XLA Modules:
  0.0 84.5 jit_solution(13451216541100411038)
XLA Ops:
  0.0 1.2 %fusion.228 = (f32[16,2,512]{2,1,0:T(2,128)S(1)}, f32[16,2,512]{2,1,0:T(2,128)S(1)}) fusion(f32[16,32,512]{2,1,0:T(8,128)} %param.3), kind=kLoop, calls=%fused_computation.351 | loop fusion | bytes 262144 | tf_op jit(solution)/shard_map/slice | solution.py:48
  1.2 1.4 %fusion.227 = (f32[16,3,512]{2,1,0:T(4,128)S(1)}, f32[16,3,512]{2,1,0:T(4,128)S(1)}, f32[16,3,512]{2,1,0:T(4,128)S(1)}, f32[16,3,512]{2,1,0:T(4,128)S(1)}) fusion(f32[16,32,512]{2,1,0:T(8,128)} %param.4, f32[16,32,512]{2,1,0:T(8,128)} %param.5), kind=kLoop, calls=%fused_computation.350 | loop fusion | bytes 786432 | tf_op jit(solution)/shard_map/slice | solution.py:48
  2.6 0.8 pad_maximum_fusion.2
  3.4 3.5 %collective-permute-start = (f32[16,8,512]{2,1,0:T(8,128)}, f32[16,8,512]{2,1,0:T(8,128)}, u32[]{:S(2)}, u32[]{:S(2)}) collective-permute-start(f32[16,8,512]{2,1,0:T(8,128)} %pad_maximum_fusion.2), channel_id=1, source_target_pairs={{0,1},{1,2},{2,3},{3,4},{4,5},{5,6},{6,7},{8,9},{9,10},{10,11},{11... | collective-permute-start | bytes 786440 | tf_op jit(solution)/shard_map/ppermute | solution.py:58
  7.0 0.8 pad_maximum_fusion.3
  7.8 3.2 %collective-permute-start.1 = (f32[16,8,512]{2,1,0:T(8,128)}, f32[16,8,512]{2,1,0:T(8,128)}, u32[]{:S(2)}, u32[]{:S(2)}) collective-permute-start(f32[16,8,512]{2,1,0:T(8,128)} %pad_maximum_fusion.3), channel_id=1, source_target_pairs={{1,0},{2,1},{3,2},{4,3},{5,4},{6,5},{7,6},{9,8},{10,9},{11,10},{12... | collective-permute-start | bytes 786440 | tf_op jit(solution)/shard_map/ppermute | solution.py:58
  11.1 0.9 %pad_maximum_fusion = f32[8,32,512]{2,1,0:T(8,128)} fusion(f32[3,32,512]{2,1,0:T(8,128)S(1)} %get-tuple-element.92, f32[2,32,512]{2,1,0:T(8,128)S(1)} %get-tuple-element.47, f32[3,32,512]{2,1,0:T(8,128)S(1)} %get-tuple-element.45), kind=kLoop, calls=%fused_computation.143 | loop fusion | flops 262144 | bytes 1048576 | tf_op jit(solution)/shard_map/concatenate | solution.py:55
  12.0 1.9 %collective-permute-start.3 = (f32[8,32,512]{2,1,0:T(8,128)}, f32[8,32,512]{2,1,0:T(8,128)}, u32[]{:S(2)}, u32[]{:S(2)}) collective-permute-start(f32[8,32,512]{2,1,0:T(8,128)} %pad_maximum_fusion), channel_id=1, source_target_pairs={{0,8},{8,16},{16,24},{24,32},{32,40},{40,48},{48,56},{56,64},{64,7... | collective-permute-start | bytes 1572872 | tf_op jit(solution)/shard_map/ppermute | solution.py:58
  13.9 0.8 pad_maximum_fusion.1
  14.7 5.1 %collective-permute-start.5 = (f32[8,32,512]{2,1,0:T(8,128)}, f32[8,32,512]{2,1,0:T(8,128)}, u32[]{:S(2)}, u32[]{:S(2)}) collective-permute-start(f32[8,32,512]{2,1,0:T(8,128)} %pad_maximum_fusion.1), channel_id=1, source_target_pairs={{8,0},{16,8},{24,16},{32,24},{40,32},{48,40},{56,48},{64,56},{72,6... | collective-permute-start | bytes 1572872 | tf_op jit(solution)/shard_map/ppermute | solution.py:58
  20.0 0.5 fusion.201
  20.7 0.8 fusion.234
  21.5 4.3 %collective-permute-done.1 = f32[16,8,512]{2,1,0:T(8,128)} collective-permute-done((f32[16,8,512]{2,1,0:T(8,128)}, f32[16,8,512]{2,1,0:T(8,128)}, u32[]{:S(2)}, u32[]{:S(2)}) %collective-permute-start.1) | collective-permute-done | bytes 262176 | tf_op jit(solution)/shard_map/ppermute | solution.py:58
  25.8 0.8 fusion.235
  26.6 1.9 %collective-permute-start.2 = (f32[3,16,512]{2,1,0:T(8,128)S(1)}, f32[3,16,512]{2,1,0:T(8,128)S(1)}, u32[]{:S(2)}, u32[]{:S(2)}) collective-permute-start(f32[3,16,512]{2,1,0:T(8,128)S(1)} %pad_maximum_fusion.4), channel_id=1, source_target_pairs={{0,8},{8,16},{16,24},{24,32},{32,40},{40,48},{48,56},{56,64},{64,7... | collective-permute-start | bytes 294920 | tf_op jit(solution)/shard_map/ppermute | solution.py:58
  28.6 5.1 %collective-permute-start.4 = (f32[3,16,512]{2,1,0:T(8,128)S(1)}, f32[3,16,512]{2,1,0:T(8,128)S(1)}, u32[]{:S(2)}, u32[]{:S(2)}) collective-permute-start(f32[3,16,512]{2,1,0:T(8,128)S(1)} %pad_maximum_fusion.5), channel_id=1, source_target_pairs={{8,0},{16,8},{24,16},{32,24},{40,32},{48,40},{56,48},{64,56},{72,6... | collective-permute-start | bytes 294920 | tf_op jit(solution)/shard_map/ppermute | solution.py:58
  33.7 1.2 %fusion.232 = (f32[16,3,512]{2,1,0:T(4,128)S(1)}, f32[16,3,512]{2,1,0:T(4,128)S(1)}, f32[16,3,512]{2,1,0:T(4,128)S(1)}) fusion(f32[16,8,512]{2,1,0:T(8,128)} %collective-permute-done), kind=kLoop, calls=%fused_computation.355 | loop fusion | bytes 589824 | tf_op jit(solution)/shard_map/slice | solution.py:75
  34.9 1.3 %fusion.233 = (f32[16,3,512]{2,1,0:T(4,128)S(1)}, f32[16,3,512]{2,1,0:T(4,128)S(1)}, f32[16,3,512]{2,1,0:T(4,128)S(1)}) fusion(f32[16,8,512]{2,1,0:T(8,128)} %collective-permute-done.1), kind=kLoop, calls=%fused_computation.356 | loop fusion | bytes 589824 | tf_op jit(solution)/shard_map/slice | solution.py:75
  36.4 1.2 %fusion.230 = (f32[3,32,512]{2,1,0:T(8,128)S(1)}, f32[3,32,512]{2,1,0:T(8,128)S(1)}, f32[3,32,512]{2,1,0:T(8,128)S(1)}) fusion(f32[8,32,512]{2,1,0:T(8,128)} %collective-permute-done.3), kind=kLoop, calls=%fused_computation.353 | loop fusion | bytes 1179648 | tf_op jit(solution)/shard_map/slice | solution.py:74
  37.6 1.2 %fusion.231 = (f32[3,32,512]{2,1,0:T(8,128)S(1)}, f32[3,32,512]{2,1,0:T(8,128)S(1)}, f32[3,32,512]{2,1,0:T(8,128)S(1)}) fusion(f32[8,32,512]{2,1,0:T(8,128)} %collective-permute-done.5), kind=kLoop, calls=%fused_computation.354 | loop fusion | bytes 1179648 | tf_op jit(solution)/shard_map/slice | solution.py:76
  38.7 0.3 maximum_maximum_fusion.2
  39.0 0.3 maximum_maximum_fusion.1
  39.3 0.3 maximum_maximum_fusion
  39.6 2.1 %divide_select_fusion.2 = (f32[22,38,512]{2,1,0:T(8,128)S(1)}, f32[22,38,512]{2,1,0:T(8,128)S(1)}, f32[22,38,512]{2,1,0:T(8,128)S(1)}) fusion(f32[22,38,512]{2,1,0:T(8,128)S(1)} %maximum_maximum_fusion.1), kind=kLoop, calls=%fused_computation.17 | loop fusion | flops 8560640 | bytes 6848512 | tf_op jit(solution)/shard_map/jit(_where)/select_n | solution.py:208
  41.7 4.1 %and_select_fusion.1 = (f32[22,38,512]{2,1,0:T(8,128)S(1)}, f32[22,38,512]{2,1,0:T(8,128)S(1)}) fusion(f32[22,38,512]{2,1,0:T(8,128)S(1)} %maximum_maximum_fusion.2, f32[22,38,512]{2,1,0:T(8,128)S(1)} %get-tuple-element.43, f32[22,38,512]{2,1,0:T(8,128)S(1)} %get-tuple-element.44, f32[22,38,512]{2,1,0:T(8,128)S(1)} %get-tuple-element.42, ...), kind=kLoop, calls=%fused_computation.19 | loop fusion | flops 12412928 | bytes 13697596 | tf_op jit(solution)/shard_map/jit(_where)/select_n | solution.py:252
  45.9 3.8 %and_select_fusion = f32[22,38,512]{2,1,0:T(8,128)S(1)} fusion(f32[22,38,512]{2,1,0:T(8,128)S(1)} %get-tuple-element.36, f32[22,38,512]{2,1,0:T(8,128)S(1)} %get-tuple-element.37, f32[22,38,512]{2,1,0:T(8,128)S(1)} %get-tuple-element.43, f32[22,38,512]{2,1,0:T(8,128)S(1)} %get-tuple-element.44, f32[22,38,512]{2,1,0:T(8,128)S(1)} %get-tuple-element.42, ...), kind=kLoop, calls=%fused_computation.18 | loop fusion | flops 11984896 | bytes 11984956 | tf_op jit(solution)/shard_map/jit(_where)/select_n | solution.py:252
  49.7 0.5 fusion.223
  50.2 1.8 %fusion.46 = (f32[16,32,512]{2,1,0:T(8,128)S(1)}, f32[16,32,512]{2,1,0:T(8,128)S(1)}) fusion(f32[16,32,512]{2,1,0:T(8,128)S(1)} %copy-done.1, f32[22,38,512]{2,1,0:T(8,128)S(1)} %get-tuple-element.37, f32[22,38,512]{2,1,0:T(8,128)S(1)} %get-tuple-element.43, f32[22,38,512]{2,1,0:T(8,128)S(1)} %and_select_fusion, f32[22,38,512]{2,1,0:T(8,128)S(1)} %get-tuple-element.44, ...), kind=kLoop, calls=%fused_computation.125 | loop fusion | flops 4718592 | bytes 16773120 | tf_op jit(solution)/shard_map/sub | solution.py:263
  52.0 0.5 fusion.199
  52.7 0.7 collective-permute-start.6
  53.4 0.9 %collective-permute-done.6 = f32[2,4,8,128]{3,2,1,0:T(8,128)S(1)} collective-permute-done((f32[2,4,8,128]{3,2,1,0:T(8,128)S(1)}, f32[2,4,8,128]{3,2,1,0:T(8,128)S(1)}, u32[]{:S(2)}, u32[]{:S(2)}) %collective-permute-start.6) | collective-permute-done | bytes 32800 | tf_op jit(solution)/shard_map/ppermute | solution.py:144
  54.2 5.6 %collective-permute-start.7 = (f32[2,8,8,128]{3,2,1,0:T(8,128)S(1)}, f32[2,8,8,128]{3,2,1,0:T(8,128)S(1)}, u32[]{:S(2)}, u32[]{:S(2)}) collective-permute-start(f32[2,8,8,128]{3,2,1,0:T(8,128)S(1)} %maximum_select_fusion), channel_id=1, source_target_pairs={{0,16},{8,24},{16,32},{24,40},{32,48},{40,56},{48,64},{56,72},{64,... | collective-permute-start | bytes 196616 | tf_op jit(solution)/shard_map/ppermute | solution.py:147
  59.8 1.9 %collective-permute-start.8 = (f32[2,8,8,128]{3,2,1,0:T(8,128)S(1)}, f32[2,8,8,128]{3,2,1,0:T(8,128)S(1)}, u32[]{:S(2)}, u32[]{:S(2)}) collective-permute-start(f32[2,8,8,128]{3,2,1,0:T(8,128)S(1)} %maximum_select_fusion), channel_id=1, source_target_pairs={{16,0},{24,8},{32,16},{40,24},{48,32},{56,40},{64,48},{72,56},{80,... | collective-permute-start | bytes 196616 | tf_op jit(solution)/shard_map/ppermute | solution.py:148
  62.0 6.4 %collective-permute-done.8 = f32[2,8,8,128]{3,2,1,0:T(8,128)S(1)} collective-permute-done((f32[2,8,8,128]{3,2,1,0:T(8,128)S(1)}, f32[2,8,8,128]{3,2,1,0:T(8,128)S(1)}, u32[]{:S(2)}, u32[]{:S(2)}) %collective-permute-start.8) | collective-permute-done | bytes 65568 | tf_op jit(solution)/shard_map/ppermute | solution.py:148
  68.5 3.7 %collective-permute-start.10 = (f32[2,18,8,128]{3,2,1,0:T(8,128)S(1)}, f32[2,18,8,128]{3,2,1,0:T(8,128)S(1)}, u32[]{:S(2)}, u32[]{:S(2)}) collective-permute-start(f32[2,18,8,128]{3,2,1,0:T(8,128)S(1)} %slice.548), channel_id=1, source_target_pairs={{1,0},{2,1},{3,2},{4,3},{5,4},{6,5},{7,6},{9,8},{10,9},{11,10},{12... | collective-permute-start | bytes 442376 | tf_op jit(solution)/shard_map/ppermute | solution.py:26
  72.1 2.4 %collective-permute-start.9 = (f32[2,18,8,128]{3,2,1,0:T(8,128)S(1)}, f32[2,18,8,128]{3,2,1,0:T(8,128)S(1)}, u32[]{:S(2)}, u32[]{:S(2)}) collective-permute-start(f32[2,18,8,128]{3,2,1,0:T(8,128)S(1)} %slice.548), channel_id=1, source_target_pairs={{0,1},{1,2},{2,3},{3,4},{4,5},{5,6},{6,7},{8,9},{9,10},{10,11},{11... | collective-permute-start | bytes 442376 | tf_op jit(solution)/shard_map/ppermute | solution.py:25
  74.5 1.0 %collective-permute-done.10 = f32[2,18,8,128]{3,2,1,0:T(8,128)S(1)} collective-permute-done((f32[2,18,8,128]{3,2,1,0:T(8,128)S(1)}, f32[2,18,8,128]{3,2,1,0:T(8,128)S(1)}, u32[]{:S(2)}, u32[]{:S(2)}) %collective-permute-start.10) | collective-permute-done | bytes 147488 | tf_op jit(solution)/shard_map/ppermute | solution.py:26
  75.5 4.6 %collective-permute-done.9 = f32[2,18,8,128]{3,2,1,0:T(8,128)S(1)} collective-permute-done((f32[2,18,8,128]{3,2,1,0:T(8,128)S(1)}, f32[2,18,8,128]{3,2,1,0:T(8,128)S(1)}, u32[]{:S(2)}, u32[]{:S(2)}) %collective-permute-start.9) | collective-permute-done | bytes 147488 | tf_op jit(solution)/shard_map/ppermute | solution.py:25
  80.1 0.5 fusion.182
  80.6 0.3 fusion.183
  81.0 0.3 multiply_add_fusion.4
  81.2 0.3 multiply_add_fusion.3
  81.5 0.3 multiply_add_fusion.2
  81.8 0.3 multiply_add_fusion.1
  82.1 0.3 multiply_add_fusion
  82.6 0.5 fusion.188
  83.1 0.3 convolution_bitcast_fusion
  83.4 1.1 %bitcast_add_fusion = f32[16,32,512]{2,1,0:T(8,128)} fusion(f32[16,32,512]{2,1,0:T(8,128)S(1)} %get-tuple-element.13, f32[4,32,512]{2,1,0:T(8,128)S(1)} %convolution_bitcast_fusion), kind=kLoop, calls=%fused_computation.139 | loop fusion | flops 262144 | bytes 2359296 | tf_op jit(solution)/shard_map/add | solution.py:268
  (40 shorter events, 1.3 us)
Async XLA Ops:
  0.0 11.0 %copy-start = (f32[16,32,512]{2,1,0:T(8,128)S(1)}, f32[16,32,512]{2,1,0:T(8,128)}, u32[]{:S(2)}) copy-start(f32[16,32,512]{2,1,0:T(8,128)} %param.4) | copy-start | bytes 3145732
  0.0 11.0 %copy-start.2 = (f32[16,32,512]{2,1,0:T(8,128)S(1)}, f32[16,32,512]{2,1,0:T(8,128)}, u32[]{:S(2)}) copy-start(f32[16,32,512]{2,1,0:T(8,128)} %param.5) | copy-start | bytes 3145732
  1.2 9.8 %copy-start.1 = (f32[16,32,512]{2,1,0:T(8,128)S(1)}, f32[16,32,512]{2,1,0:T(8,128)}, u32[]{:S(2)}) copy-start(f32[16,32,512]{2,1,0:T(8,128)} %param.3) | copy-start | bytes 3145732
  3.4 17.3 %collective-permute-start = (f32[16,8,512]{2,1,0:T(8,128)}, f32[16,8,512]{2,1,0:T(8,128)}, u32[]{:S(2)}, u32[]{:S(2)}) collective-permute-start(f32[16,8,512]{2,1,0:T(8,128)} %pad_maximum_fusion.2), channel_id=1, source_target_pairs={{0,1},{1,2},{2,3},{3,4},{4,5},{5,6},{6,7},{8,9},{9,10},{10,11},{11... | collective-permute-start | bytes 786440 | tf_op jit(solution)/shard_map/ppermute | solution.py:58
  7.8 18.0 %collective-permute-start.1 = (f32[16,8,512]{2,1,0:T(8,128)}, f32[16,8,512]{2,1,0:T(8,128)}, u32[]{:S(2)}, u32[]{:S(2)}) collective-permute-start(f32[16,8,512]{2,1,0:T(8,128)} %pad_maximum_fusion.3), channel_id=1, source_target_pairs={{1,0},{2,1},{3,2},{4,3},{5,4},{6,5},{7,6},{9,8},{10,9},{11,10},{12... | collective-permute-start | bytes 786440 | tf_op jit(solution)/shard_map/ppermute | solution.py:58
  12.0 24.4 %collective-permute-start.3 = (f32[8,32,512]{2,1,0:T(8,128)}, f32[8,32,512]{2,1,0:T(8,128)}, u32[]{:S(2)}, u32[]{:S(2)}) collective-permute-start(f32[8,32,512]{2,1,0:T(8,128)} %pad_maximum_fusion), channel_id=1, source_target_pairs={{0,8},{8,16},{16,24},{24,32},{32,40},{40,48},{48,56},{56,64},{64,7... | collective-permute-start | bytes 1572872 | tf_op jit(solution)/shard_map/ppermute | solution.py:58
  14.7 22.8 %collective-permute-start.5 = (f32[8,32,512]{2,1,0:T(8,128)}, f32[8,32,512]{2,1,0:T(8,128)}, u32[]{:S(2)}, u32[]{:S(2)}) collective-permute-start(f32[8,32,512]{2,1,0:T(8,128)} %pad_maximum_fusion.1), channel_id=1, source_target_pairs={{8,0},{16,8},{24,16},{32,24},{40,32},{48,40},{56,48},{64,56},{72,6... | collective-permute-start | bytes 1572872 | tf_op jit(solution)/shard_map/ppermute | solution.py:58
  26.6 9.6 %collective-permute-start.2 = (f32[3,16,512]{2,1,0:T(8,128)S(1)}, f32[3,16,512]{2,1,0:T(8,128)S(1)}, u32[]{:S(2)}, u32[]{:S(2)}) collective-permute-start(f32[3,16,512]{2,1,0:T(8,128)S(1)} %pad_maximum_fusion.4), channel_id=1, source_target_pairs={{0,8},{8,16},{16,24},{24,32},{32,40},{40,48},{48,56},{56,64},{64,7... | collective-permute-start | bytes 294920 | tf_op jit(solution)/shard_map/ppermute | solution.py:58
  28.6 7.7 %collective-permute-start.4 = (f32[3,16,512]{2,1,0:T(8,128)S(1)}, f32[3,16,512]{2,1,0:T(8,128)S(1)}, u32[]{:S(2)}, u32[]{:S(2)}) collective-permute-start(f32[3,16,512]{2,1,0:T(8,128)S(1)} %pad_maximum_fusion.5), channel_id=1, source_target_pairs={{8,0},{16,8},{24,16},{32,24},{40,32},{48,40},{56,48},{64,56},{72,6... | collective-permute-start | bytes 294920 | tf_op jit(solution)/shard_map/ppermute | solution.py:58
  52.7 1.5 %collective-permute-start.6 = (f32[2,4,8,128]{3,2,1,0:T(8,128)S(1)}, f32[2,4,8,128]{3,2,1,0:T(8,128)S(1)}, u32[]{:S(2)}, u32[]{:S(2)}) collective-permute-start(f32[2,4,8,128]{3,2,1,0:T(8,128)S(1)} %pad_maximum_fusion.6), channel_id=1, source_target_pairs={{0,8},{8,0},{16,24},{24,16},{32,40},{40,32},{48,56},{56,48},{64,72... | collective-permute-start | bytes 98312 | tf_op jit(solution)/shard_map/ppermute | solution.py:144
  54.2 7.7 %collective-permute-start.7 = (f32[2,8,8,128]{3,2,1,0:T(8,128)S(1)}, f32[2,8,8,128]{3,2,1,0:T(8,128)S(1)}, u32[]{:S(2)}, u32[]{:S(2)}) collective-permute-start(f32[2,8,8,128]{3,2,1,0:T(8,128)S(1)} %maximum_select_fusion), channel_id=1, source_target_pairs={{0,16},{8,24},{16,32},{24,40},{32,48},{40,56},{48,64},{56,72},{64,... | collective-permute-start | bytes 196616 | tf_op jit(solution)/shard_map/ppermute | solution.py:147
  59.8 8.6 %collective-permute-start.8 = (f32[2,8,8,128]{3,2,1,0:T(8,128)S(1)}, f32[2,8,8,128]{3,2,1,0:T(8,128)S(1)}, u32[]{:S(2)}, u32[]{:S(2)}) collective-permute-start(f32[2,8,8,128]{3,2,1,0:T(8,128)S(1)} %maximum_select_fusion), channel_id=1, source_target_pairs={{16,0},{24,8},{32,16},{40,24},{48,32},{56,40},{64,48},{72,56},{80,... | collective-permute-start | bytes 196616 | tf_op jit(solution)/shard_map/ppermute | solution.py:148
  68.5 7.0 %collective-permute-start.10 = (f32[2,18,8,128]{3,2,1,0:T(8,128)S(1)}, f32[2,18,8,128]{3,2,1,0:T(8,128)S(1)}, u32[]{:S(2)}, u32[]{:S(2)}) collective-permute-start(f32[2,18,8,128]{3,2,1,0:T(8,128)S(1)} %slice.548), channel_id=1, source_target_pairs={{1,0},{2,1},{3,2},{4,3},{5,4},{6,5},{7,6},{9,8},{10,9},{11,10},{12... | collective-permute-start | bytes 442376 | tf_op jit(solution)/shard_map/ppermute | solution.py:26
  72.1 7.9 %collective-permute-start.9 = (f32[2,18,8,128]{3,2,1,0:T(8,128)S(1)}, f32[2,18,8,128]{3,2,1,0:T(8,128)S(1)}, u32[]{:S(2)}, u32[]{:S(2)}) collective-permute-start(f32[2,18,8,128]{3,2,1,0:T(8,128)S(1)} %slice.548), channel_id=1, source_target_pairs={{0,1},{1,2},{2,3},{3,4},{4,5},{5,6},{6,7},{8,9},{9,10},{10,11},{11... | collective-permute-start | bytes 442376 | tf_op jit(solution)/shard_map/ppermute | solution.py:25

commit v23 on v18

--- a/solution.py
+++ b/solution.py
@@ -255,7 +255,7 @@
         shift_z(core, 1),
     ]
     res = right_side - apply_op(core, nears, [c[own] for c in coefs])
-    fine, res = lax.optimization_barrier((core, res))
+    fine, res = core, lax.optimization_barrier(res)
     coarse_rhs = block_mean(res)
     coarse_b = block_mean(inv_density)
     corr = chebyshev_local(coarse_rhs, coarse_b)

time: 85.3 us -> 82.5 us (0.967)
  the two profiles are of different devices: /device:TPU:88 before, /device:TPU:34 now
where the time goes in v23:
time: 82.5 us; the launch traced here: 81.1 us
  starting transfers between devices  41.7 us (51%)
  other arithmetic  19.3 us (23%)
  waiting for transfers between devices  10.8 us (13%)
  local copies, waits for them, and re-layouts  6.64 us (8%)
  matrix products  2.05 us (2%)
    ppermute x6, starting transfers between devices, send(): return lax.ppermute(msg, axis, pairs)  21.8 us
    select_n x2, other arithmetic, per_device(): fine = jnp.where(inside, fine + step, 0.0)  7.9 us
    ppermute x1, starting transfers between devices, pair_extend(): high = lax.ppermute(pair, 'box', [(t, s) for s, t in shifted_pairs(nb, 2)])  6.19 us
    ppermute x1, starting transfers between devices, halo_from(): lax.ppermute(lax.slice_in_dim(block, n - width, n, axis=dim), axis, forward)  4.84 us
    ppermute x1, starting transfers between devices, pair_extend(): partner = lax.ppermute(block, 'box', [(i, i ^ 1) for i in range(nb)])  4.82 us
    slice x6, local copies, waits for them, and re-layouts, packed_halo(): lax.slice_in_dim(f, f.shape[dim] - d, f.shape[dim], axis=dim)  3.68 us
    ppermute x1, waiting for transfers between devices, halo_from(): lax.ppermute(lax.slice_in_dim(block, n - width, n, axis=dim), axis, forward)  3.41 us
    concatenate x6, other arithmetic, send(): msg = jnp.concatenate(pieces, axis=dim)  2.61 us
  transfers between devices with their start and end apart: 11, of which 7 were waited for; matrix products, arithmetic and copies ran while one was open for 7% of the time, Pallas kernels for 0%

profile of v23, /device:TPU:34, one launch (start us, length us, event | category | flops | bytes accessed | tf_op | source)
XLA Modules:
  0.0 81.1 jit_solution(4579032391893396052)
XLA Ops:
  0.0 1.2 %fusion.228 = (f32[16,2,512]{2,1,0:T(2,128)S(1)}, f32[16,2,512]{2,1,0:T(2,128)S(1)}) fusion(f32[16,32,512]{2,1,0:T(8,128)} %param.3), kind=kLoop, calls=%fused_computation.351 | loop fusion | bytes 262144 | tf_op jit(solution)/shard_map/slice | solution.py:48
  1.2 1.4 %fusion.227 = (f32[16,3,512]{2,1,0:T(4,128)S(1)}, f32[16,3,512]{2,1,0:T(4,128)S(1)}, f32[16,3,512]{2,1,0:T(4,128)S(1)}, f32[16,3,512]{2,1,0:T(4,128)S(1)}) fusion(f32[16,32,512]{2,1,0:T(8,128)} %param.4, f32[16,32,512]{2,1,0:T(8,128)} %param.5), kind=kLoop, calls=%fused_computation.350 | loop fusion | bytes 786432 | tf_op jit(solution)/shard_map/slice | solution.py:48
  2.7 3.0 %collective-permute-start = (f32[16,8,512]{2,1,0:T(8,128)S(1)}, f32[16,8,512]{2,1,0:T(8,128)S(1)}, u32[]{:S(2)}, u32[]{:S(2)}) collective-permute-start(f32[16,8,512]{2,1,0:T(8,128)S(1)} %pad_maximum_fusion.3), channel_id=1, source_target_pairs={{0,1},{1,2},{2,3},{3,4},{4,5},{5,6},{6,7},{8,9},{9,10},{10,11},{11... | collective-permute-start | bytes 786440 | tf_op jit(solution)/shard_map/ppermute | solution.py:58
  5.7 0.8 %pad_maximum_fusion.4 = f32[16,8,512]{2,1,0:T(8,128)} fusion(f32[16,3,512]{2,1,0:T(4,128)S(1)} %get-tuple-element.81, f32[16,2,512]{2,1,0:T(2,128)S(1)} %get-tuple-element.48, f32[16,3,512]{2,1,0:T(4,128)S(1)} %get-tuple-element.46), kind=kLoop, calls=%fused_computation.147 | loop fusion | flops 131072 | bytes 524288 | tf_op jit(solution)/shard_map/concatenate | solution.py:55
  6.5 2.8 %collective-permute-start.1 = (f32[16,8,512]{2,1,0:T(8,128)}, f32[16,8,512]{2,1,0:T(8,128)S(1)}, u32[]{:S(2)}, u32[]{:S(2)}) collective-permute-start(f32[16,8,512]{2,1,0:T(8,128)} %pad_maximum_fusion.4), channel_id=1, source_target_pairs={{1,0},{2,1},{3,2},{4,3},{5,4},{6,5},{7,6},{9,8},{10,9},{11,10},{12... | collective-permute-start | bytes 786440 | tf_op jit(solution)/shard_map/ppermute | solution.py:58
  9.4 1.1 %fusion.224 = (f32[3,32,512]{2,1,0:T(8,128)S(1)}, f32[3,32,512]{2,1,0:T(8,128)S(1)}, f32[3,32,512]{2,1,0:T(8,128)S(1)}, f32[3,32,512]{2,1,0:T(8,128)S(1)}) fusion(f32[16,32,512]{2,1,0:T(8,128)S(1)} %copy-done, f32[16,32,512]{2,1,0:T(8,128)} %param.5), kind=kLoop, calls=%fused_computation.347 | loop fusion | bytes 1572864 | tf_op jit(solution)/shard_map/slice | solution.py:48
  10.5 0.8 %pad_maximum_fusion = f32[8,32,512]{2,1,0:T(8,128)} fusion(f32[3,32,512]{2,1,0:T(8,128)S(1)} %get-tuple-element.84, f32[2,32,512]{2,1,0:T(8,128)S(1)} %get-tuple-element.41, f32[3,32,512]{2,1,0:T(8,128)S(1)} %get-tuple-element.39), kind=kLoop, calls=%fused_computation.143 | loop fusion | flops 262144 | bytes 1048576 | tf_op jit(solution)/shard_map/concatenate | solution.py:55
  11.3 1.9 %collective-permute-start.3 = (f32[8,32,512]{2,1,0:T(8,128)}, f32[8,32,512]{2,1,0:T(8,128)}, u32[]{:S(2)}, u32[]{:S(2)}) collective-permute-start(f32[8,32,512]{2,1,0:T(8,128)} %pad_maximum_fusion), channel_id=1, source_target_pairs={{0,8},{8,16},{16,24},{24,32},{32,40},{40,48},{48,56},{56,64},{64,7... | collective-permute-start | bytes 1572872 | tf_op jit(solution)/shard_map/ppermute | solution.py:58
  13.2 0.8 %pad_maximum_fusion.1 = f32[8,32,512]{2,1,0:T(8,128)} fusion(f32[3,32,512]{2,1,0:T(8,128)S(1)} %get-tuple-element.83, f32[2,32,512]{2,1,0:T(8,128)S(1)} %get-tuple-element.42, f32[3,32,512]{2,1,0:T(8,128)S(1)} %get-tuple-element.40), kind=kLoop, calls=%fused_computation.144 | loop fusion | flops 262144 | bytes 1048576 | tf_op jit(solution)/shard_map/concatenate | solution.py:55
  14.1 6.0 %collective-permute-start.5 = (f32[8,32,512]{2,1,0:T(8,128)}, f32[8,32,512]{2,1,0:T(8,128)}, u32[]{:S(2)}, u32[]{:S(2)}) collective-permute-start(f32[8,32,512]{2,1,0:T(8,128)} %pad_maximum_fusion.1), channel_id=1, source_target_pairs={{8,0},{16,8},{24,16},{32,24},{40,32},{48,40},{56,48},{64,56},{72,6... | collective-permute-start | bytes 1572872 | tf_op jit(solution)/shard_map/ppermute | solution.py:58
  20.3 0.5 fusion.201
  20.8 0.1 fusion.44
  21.0 1.9 %collective-permute-start.2 = (f32[3,16,512]{2,1,0:T(8,128)S(1)}, f32[3,16,512]{2,1,0:T(8,128)S(1)}, u32[]{:S(2)}, u32[]{:S(2)}) collective-permute-start(f32[3,16,512]{2,1,0:T(8,128)S(1)} %pad_maximum_fusion.5), channel_id=1, source_target_pairs={{0,8},{8,16},{16,24},{24,32},{32,40},{40,48},{48,56},{56,64},{64,7... | collective-permute-start | bytes 294920 | tf_op jit(solution)/shard_map/ppermute | solution.py:58
  23.0 6.0 %collective-permute-start.4 = (f32[3,16,512]{2,1,0:T(8,128)S(1)}, f32[3,16,512]{2,1,0:T(8,128)S(1)}, u32[]{:S(2)}, u32[]{:S(2)}) collective-permute-start(f32[3,16,512]{2,1,0:T(8,128)S(1)} %pad_maximum_fusion.6), channel_id=1, source_target_pairs={{8,0},{16,8},{24,16},{32,24},{40,32},{48,40},{56,48},{64,56},{72,6... | collective-permute-start | bytes 294920 | tf_op jit(solution)/shard_map/ppermute | solution.py:58
  29.2 0.3 collective-permute-done.2
  29.5 2.1 %collective-permute-done.4 = f32[3,16,512]{2,1,0:T(8,128)S(1)} collective-permute-done((f32[3,16,512]{2,1,0:T(8,128)S(1)}, f32[3,16,512]{2,1,0:T(8,128)S(1)}, u32[]{:S(2)}, u32[]{:S(2)}) %collective-permute-start.4) | collective-permute-done | bytes 98336 | tf_op jit(solution)/shard_map/ppermute | solution.py:58
  31.7 1.2 %fusion.230 = (f32[3,32,512]{2,1,0:T(8,128)S(1)}, f32[3,32,512]{2,1,0:T(8,128)S(1)}, f32[3,32,512]{2,1,0:T(8,128)S(1)}) fusion(f32[8,32,512]{2,1,0:T(8,128)} %collective-permute-done.3), kind=kLoop, calls=%fused_computation.353 | loop fusion | bytes 1179648 | tf_op jit(solution)/shard_map/slice | solution.py:74
  32.8 1.2 %fusion.231 = (f32[3,32,512]{2,1,0:T(8,128)S(1)}, f32[3,32,512]{2,1,0:T(8,128)S(1)}, f32[3,32,512]{2,1,0:T(8,128)S(1)}) fusion(f32[8,32,512]{2,1,0:T(8,128)} %collective-permute-done.5), kind=kLoop, calls=%fused_computation.354 | loop fusion | bytes 1179648 | tf_op jit(solution)/shard_map/slice | solution.py:76
  34.0 0.3 maximum_maximum_fusion.2
  34.3 0.3 maximum_maximum_fusion.1
  34.6 0.3 maximum_maximum_fusion
  34.9 2.1 %divide_select_fusion.2 = (f32[22,38,512]{2,1,0:T(8,128)S(1)}, f32[22,38,512]{2,1,0:T(8,128)S(1)}, f32[22,38,512]{2,1,0:T(8,128)S(1)}) fusion(f32[22,38,512]{2,1,0:T(8,128)S(1)} %maximum_maximum_fusion.1), kind=kLoop, calls=%fused_computation.17 | loop fusion | flops 8560640 | bytes 6848512 | tf_op jit(solution)/shard_map/jit(_where)/select_n | solution.py:202
  37.1 4.1 %and_select_fusion.1 = (f32[22,38,512]{2,1,0:T(8,128)S(1)}, f32[22,38,512]{2,1,0:T(8,128)S(1)}) fusion(f32[22,38,512]{2,1,0:T(8,128)S(1)} %maximum_maximum_fusion.2, f32[22,38,512]{2,1,0:T(8,128)S(1)} %get-tuple-element.37, f32[22,38,512]{2,1,0:T(8,128)S(1)} %get-tuple-element.38, f32[22,38,512]{2,1,0:T(8,128)S(1)} %get-tuple-element.36, ...), kind=kLoop, calls=%fused_computation.19 | loop fusion | flops 12412928 | bytes 13697596 | tf_op jit(solution)/shard_map/jit(_where)/select_n | solution.py:246
  41.2 3.8 %and_select_fusion = f32[22,38,512]{2,1,0:T(8,128)S(1)} fusion(f32[22,38,512]{2,1,0:T(8,128)S(1)} %get-tuple-element.32, f32[22,38,512]{2,1,0:T(8,128)S(1)} %get-tuple-element.33, f32[22,38,512]{2,1,0:T(8,128)S(1)} %get-tuple-element.37, f32[22,38,512]{2,1,0:T(8,128)S(1)} %get-tuple-element.38, f32[22,38,512]{2,1,0:T(8,128)S(1)} %get-tuple-element.36, ...), kind=kLoop, calls=%fused_computation.18 | loop fusion | flops 11984896 | bytes 11984956 | tf_op jit(solution)/shard_map/jit(_where)/select_n | solution.py:246
  45.0 0.4 fusion.223
  45.4 1.8 %fusion.46 = f32[16,32,512]{2,1,0:T(8,128)S(1)} fusion(f32[16,32,512]{2,1,0:T(8,128)S(1)} %copy-done.1, f32[22,38,512]{2,1,0:T(8,128)S(1)} %get-tuple-element.33, f32[22,38,512]{2,1,0:T(8,128)S(1)} %get-tuple-element.37, f32[22,38,512]{2,1,0:T(8,128)S(1)} %and_select_fusion, f32[22,38,512]{2,1,0:T(8,128)S(1)} %get-tuple-element.38, ...), kind=kLoop, calls=%fused_computation.125 | loop fusion | flops 4718592 | bytes 15724544 | tf_op jit(solution)/shard_map/sub | solution.py:257
  47.3 0.5 fusion.199
  48.0 4.8 %collective-permute-start.6 = (f32[2,4,8,128]{3,2,1,0:T(8,128)S(1)}, f32[2,4,8,128]{3,2,1,0:T(8,128)S(1)}, u32[]{:S(2)}, u32[]{:S(2)}) collective-permute-start(f32[2,4,8,128]{3,2,1,0:T(8,128)S(1)} %pad_maximum_fusion.7), channel_id=1, source_target_pairs={{0,8},{8,0},{16,24},{24,16},{32,40},{40,32},{48,56},{56,48},{64,72... | collective-permute-start | bytes 98312 | tf_op jit(solution)/shard_map/ppermute | solution.py:144
  52.8 0.9 %collective-permute-done.6 = f32[2,4,8,128]{3,2,1,0:T(8,128)S(1)} collective-permute-done((f32[2,4,8,128]{3,2,1,0:T(8,128)S(1)}, f32[2,4,8,128]{3,2,1,0:T(8,128)S(1)}, u32[]{:S(2)}, u32[]{:S(2)}) %collective-permute-start.6) | collective-permute-done | bytes 32800 | tf_op jit(solution)/shard_map/ppermute | solution.py:144
  53.6 2.1 %collective-permute-start.7 = (f32[2,8,8,128]{3,2,1,0:T(8,128)S(1)}, f32[2,8,8,128]{3,2,1,0:T(8,128)S(1)}, u32[]{:S(2)}, u32[]{:S(2)}) collective-permute-start(f32[2,8,8,128]{3,2,1,0:T(8,128)S(1)} %maximum_select_fusion), channel_id=1, source_target_pairs={{0,16},{8,24},{16,32},{24,40},{32,48},{40,56},{48,64},{56,72},{64,... | collective-permute-start | bytes 196616 | tf_op jit(solution)/shard_map/ppermute | solution.py:147
  55.7 6.2 %collective-permute-start.8 = (f32[2,8,8,128]{3,2,1,0:T(8,128)S(1)}, f32[2,8,8,128]{3,2,1,0:T(8,128)S(1)}, u32[]{:S(2)}, u32[]{:S(2)}) collective-permute-start(f32[2,8,8,128]{3,2,1,0:T(8,128)S(1)} %maximum_select_fusion), channel_id=1, source_target_pairs={{16,0},{24,8},{32,16},{40,24},{48,32},{56,40},{64,48},{72,56},{80,... | collective-permute-start | bytes 196616 | tf_op jit(solution)/shard_map/ppermute | solution.py:148
  61.9 0.4 collective-permute-done.7
  62.3 2.0 %collective-permute-done.8 = f32[2,8,8,128]{3,2,1,0:T(8,128)S(1)} collective-permute-done((f32[2,8,8,128]{3,2,1,0:T(8,128)S(1)}, f32[2,8,8,128]{3,2,1,0:T(8,128)S(1)}, u32[]{:S(2)}, u32[]{:S(2)}) %collective-permute-start.8) | collective-permute-done | bytes 65568 | tf_op jit(solution)/shard_map/ppermute | solution.py:148
  64.3 2.1 %collective-permute-start.10 = (f32[2,20,8,128]{3,2,1,0:T(8,128)S(1)}, f32[2,20,8,128]{3,2,1,0:T(8,128)S(1)}, u32[]{:S(2)}, u32[]{:S(2)}) collective-permute-start(f32[2,20,8,128]{3,2,1,0:T(8,128)S(1)} %fusion.185), channel_id=1, source_target_pairs={{1,0},{2,1},{3,2},{4,3},{5,4},{6,5},{7,6},{9,8},{10,9},{11,10},{12... | collective-permute-start | bytes 491528 | tf_op jit(solution)/shard_map/ppermute | solution.py:26
  66.4 4.8 %collective-permute-start.9 = (f32[2,20,8,128]{3,2,1,0:T(8,128)S(1)}, f32[2,20,8,128]{3,2,1,0:T(8,128)S(1)}, u32[]{:S(2)}, u32[]{:S(2)}) collective-permute-start(f32[2,20,8,128]{3,2,1,0:T(8,128)S(1)} %fusion.185), channel_id=1, source_target_pairs={{0,1},{1,2},{2,3},{3,4},{4,5},{5,6},{6,7},{8,9},{9,10},{10,11},{11... | collective-permute-start | bytes 491528 | tf_op jit(solution)/shard_map/ppermute | solution.py:25
  71.3 1.8 %collective-permute-done.10 = f32[2,20,8,128]{3,2,1,0:T(8,128)S(1)} collective-permute-done((f32[2,20,8,128]{3,2,1,0:T(8,128)S(1)}, f32[2,20,8,128]{3,2,1,0:T(8,128)S(1)}, u32[]{:S(2)}, u32[]{:S(2)}) %collective-permute-start.10) | collective-permute-done | bytes 163872 | tf_op jit(solution)/shard_map/ppermute | solution.py:26
  73.1 3.4 %collective-permute-done.9 = f32[2,20,8,128]{3,2,1,0:T(8,128)S(1)} collective-permute-done((f32[2,20,8,128]{3,2,1,0:T(8,128)S(1)}, f32[2,20,8,128]{3,2,1,0:T(8,128)S(1)}, u32[]{:S(2)}, u32[]{:S(2)}) %collective-permute-start.9) | collective-permute-done | bytes 163872 | tf_op jit(solution)/shard_map/ppermute | solution.py:25
  76.6 0.5 fusion.182
  77.1 0.3 fusion.183
  77.5 0.3 multiply_add_fusion.4
  77.7 0.3 multiply_add_fusion.3
  78.0 0.3 multiply_add_fusion.2
  78.3 0.3 multiply_add_fusion.1
  78.5 0.3 multiply_add_fusion
  78.8 0.2 fusion.169
  79.1 0.5 fusion.188
  79.6 0.3 convolution_bitcast_fusion
  79.9 1.2 %bitcast_add_fusion = f32[16,32,512]{2,1,0:T(8,128)} fusion(f32[22,38,512]{2,1,0:T(8,128)S(1)} %and_select_fusion, f32[4,32,512]{2,1,0:T(8,128)S(1)} %convolution_bitcast_fusion), kind=kLoop, calls=%fused_computation.139 | loop fusion | flops 262144 | bytes 2359296 | tf_op jit(solution)/shard_map/add | solution.py:262
  (37 shorter events, 0.8 us)
Async XLA Ops:
  0.0 9.3 %copy-start = (f32[16,32,512]{2,1,0:T(8,128)S(1)}, f32[16,32,512]{2,1,0:T(8,128)}, u32[]{:S(2)}) copy-start(f32[16,32,512]{2,1,0:T(8,128)} %param.4) | copy-start | bytes 3145732
  1.2 9.3 %copy-start.1 = (f32[16,32,512]{2,1,0:T(8,128)S(1)}, f32[16,32,512]{2,1,0:T(8,128)}, u32[]{:S(2)}) copy-start(f32[16,32,512]{2,1,0:T(8,128)} %param.3) | copy-start | bytes 3145732
  2.7 18.3 %collective-permute-start = (f32[16,8,512]{2,1,0:T(8,128)S(1)}, f32[16,8,512]{2,1,0:T(8,128)S(1)}, u32[]{:S(2)}, u32[]{:S(2)}) collective-permute-start(f32[16,8,512]{2,1,0:T(8,128)S(1)} %pad_maximum_fusion.3), channel_id=1, source_target_pairs={{0,1},{1,2},{2,3},{3,4},{4,5},{5,6},{6,7},{8,9},{9,10},{10,11},{11... | collective-permute-start | bytes 786440 | tf_op jit(solution)/shard_map/ppermute | solution.py:58
  6.5 14.5 %collective-permute-start.1 = (f32[16,8,512]{2,1,0:T(8,128)}, f32[16,8,512]{2,1,0:T(8,128)S(1)}, u32[]{:S(2)}, u32[]{:S(2)}) collective-permute-start(f32[16,8,512]{2,1,0:T(8,128)} %pad_maximum_fusion.4), channel_id=1, source_target_pairs={{1,0},{2,1},{3,2},{4,3},{5,4},{6,5},{7,6},{9,8},{10,9},{11,10},{12... | collective-permute-start | bytes 786440 | tf_op jit(solution)/shard_map/ppermute | solution.py:58
  11.3 20.3 %collective-permute-start.3 = (f32[8,32,512]{2,1,0:T(8,128)}, f32[8,32,512]{2,1,0:T(8,128)}, u32[]{:S(2)}, u32[]{:S(2)}) collective-permute-start(f32[8,32,512]{2,1,0:T(8,128)} %pad_maximum_fusion), channel_id=1, source_target_pairs={{0,8},{8,16},{16,24},{24,32},{32,40},{40,48},{48,56},{56,64},{64,7... | collective-permute-start | bytes 1572872 | tf_op jit(solution)/shard_map/ppermute | solution.py:58
  14.1 18.7 %collective-permute-start.5 = (f32[8,32,512]{2,1,0:T(8,128)}, f32[8,32,512]{2,1,0:T(8,128)}, u32[]{:S(2)}, u32[]{:S(2)}) collective-permute-start(f32[8,32,512]{2,1,0:T(8,128)} %pad_maximum_fusion.1), channel_id=1, source_target_pairs={{8,0},{16,8},{24,16},{32,24},{40,32},{48,40},{56,48},{64,56},{72,6... | collective-permute-start | bytes 1572872 | tf_op jit(solution)/shard_map/ppermute | solution.py:58
  21.0 8.4 %collective-permute-start.2 = (f32[3,16,512]{2,1,0:T(8,128)S(1)}, f32[3,16,512]{2,1,0:T(8,128)S(1)}, u32[]{:S(2)}, u32[]{:S(2)}) collective-permute-start(f32[3,16,512]{2,1,0:T(8,128)S(1)} %pad_maximum_fusion.5), channel_id=1, source_target_pairs={{0,8},{8,16},{16,24},{24,32},{32,40},{40,48},{48,56},{56,64},{64,7... | collective-permute-start | bytes 294920 | tf_op jit(solution)/shard_map/ppermute | solution.py:58
  23.0 8.6 %collective-permute-start.4 = (f32[3,16,512]{2,1,0:T(8,128)S(1)}, f32[3,16,512]{2,1,0:T(8,128)S(1)}, u32[]{:S(2)}, u32[]{:S(2)}) collective-permute-start(f32[3,16,512]{2,1,0:T(8,128)S(1)} %pad_maximum_fusion.6), channel_id=1, source_target_pairs={{8,0},{16,8},{24,16},{32,24},{40,32},{48,40},{56,48},{64,56},{72,6... | collective-permute-start | bytes 294920 | tf_op jit(solution)/shard_map/ppermute | solution.py:58
  29.1 4.9 %copy-start.2 = (f32[16,32,512]{2,1,0:T(8,128)S(1)}, f32[16,32,512]{2,1,0:T(8,128)}, u32[]{:S(2)}) copy-start(f32[16,32,512]{2,1,0:T(8,128)} %param.5) | copy-start | bytes 3145732
  48.0 5.7 %collective-permute-start.6 = (f32[2,4,8,128]{3,2,1,0:T(8,128)S(1)}, f32[2,4,8,128]{3,2,1,0:T(8,128)S(1)}, u32[]{:S(2)}, u32[]{:S(2)}) collective-permute-start(f32[2,4,8,128]{3,2,1,0:T(8,128)S(1)} %pad_maximum_fusion.7), channel_id=1, source_target_pairs={{0,8},{8,0},{16,24},{24,16},{32,40},{40,32},{48,56},{56,48},{64,72... | collective-permute-start | bytes 98312 | tf_op jit(solution)/shard_map/ppermute | solution.py:144
  53.6 8.6 %collective-permute-start.7 = (f32[2,8,8,128]{3,2,1,0:T(8,128)S(1)}, f32[2,8,8,128]{3,2,1,0:T(8,128)S(1)}, u32[]{:S(2)}, u32[]{:S(2)}) collective-permute-start(f32[2,8,8,128]{3,2,1,0:T(8,128)S(1)} %maximum_select_fusion), channel_id=1, source_target_pairs={{0,16},{8,24},{16,32},{24,40},{32,48},{40,56},{48,64},{56,72},{64,... | collective-permute-start | bytes 196616 | tf_op jit(solution)/shard_map/ppermute | solution.py:147
  55.7 8.5 %collective-permute-start.8 = (f32[2,8,8,128]{3,2,1,0:T(8,128)S(1)}, f32[2,8,8,128]{3,2,1,0:T(8,128)S(1)}, u32[]{:S(2)}, u32[]{:S(2)}) collective-permute-start(f32[2,8,8,128]{3,2,1,0:T(8,128)S(1)} %maximum_select_fusion), channel_id=1, source_target_pairs={{16,0},{24,8},{32,16},{40,24},{48,32},{56,40},{64,48},{72,56},{80,... | collective-permute-start | bytes 196616 | tf_op jit(solution)/shard_map/ppermute | solution.py:148
  64.3 8.8 %collective-permute-start.10 = (f32[2,20,8,128]{3,2,1,0:T(8,128)S(1)}, f32[2,20,8,128]{3,2,1,0:T(8,128)S(1)}, u32[]{:S(2)}, u32[]{:S(2)}) collective-permute-start(f32[2,20,8,128]{3,2,1,0:T(8,128)S(1)} %fusion.185), channel_id=1, source_target_pairs={{1,0},{2,1},{3,2},{4,3},{5,4},{6,5},{7,6},{9,8},{10,9},{11,10},{12... | collective-permute-start | bytes 491528 | tf_op jit(solution)/shard_map/ppermute | solution.py:26
  66.4 10.1 %collective-permute-start.9 = (f32[2,20,8,128]{3,2,1,0:T(8,128)S(1)}, f32[2,20,8,128]{3,2,1,0:T(8,128)S(1)}, u32[]{:S(2)}, u32[]{:S(2)}) collective-permute-start(f32[2,20,8,128]{3,2,1,0:T(8,128)S(1)} %fusion.185), channel_id=1, source_target_pairs={{0,1},{1,2},{2,3},{3,4},{4,5},{5,6},{6,7},{8,9},{9,10},{10,11},{11... | collective-permute-start | bytes 491528 | tf_op jit(solution)/shard_map/ppermute | solution.py:25

commit v24 on v23

--- a/solution.py
+++ b/solution.py
@@ -255,7 +255,7 @@
         shift_z(core, 1),
     ]
     res = right_side - apply_op(core, nears, [c[own] for c in coefs])
-    fine, res = core, lax.optimization_barrier(res)
+    fine = core
     coarse_rhs = block_mean(res)
     coarse_b = block_mean(inv_density)
     corr = chebyshev_local(coarse_rhs, coarse_b)

time: 82.5 us -> 82.6 us (level)
    reduce_sum x2, other arithmetic: 0.17 us -> 2.06 us  [block_mean(): fx = field.reshape(sx // 4, 4, sy, sz).sum(axis=1)]
    sub x1 -> x0, other arithmetic: 1.8 us -> none  [per_device(): res = right_side - apply_op(core, nears, [c[own] for c in coefs])]
where the time goes in v24:
time: 82.6 us; the launch traced here: 81.1 us
  starting transfers between devices  41.7 us (50%)
  other arithmetic  19.4 us (23%)
  waiting for transfers between devices  10.8 us (13%)
  local copies, waits for them, and re-layouts  6.64 us (8%)
  matrix products  2.05 us (2%)
    ppermute x6, starting transfers between devices, send(): return lax.ppermute(msg, axis, pairs)  21.8 us
    select_n x2, other arithmetic, per_device(): fine = jnp.where(inside, fine + step, 0.0)  7.9 us
    ppermute x1, starting transfers between devices, pair_extend(): high = lax.ppermute(pair, 'box', [(t, s) for s, t in shifted_pairs(nb, 2)])  6.19 us
    ppermute x1, starting transfers between devices, halo_from(): lax.ppermute(lax.slice_in_dim(block, n - width, n, axis=dim), axis, forward)  4.84 us
    ppermute x1, starting transfers between devices, pair_extend(): partner = lax.ppermute(block, 'box', [(i, i ^ 1) for i in range(nb)])  4.81 us
    slice x6, local copies, waits for them, and re-layouts, packed_halo(): lax.slice_in_dim(f, f.shape[dim] - d, f.shape[dim], axis=dim)  3.68 us
    ppermute x1, waiting for transfers between devices, halo_from(): lax.ppermute(lax.slice_in_dim(block, n - width, n, axis=dim), axis, forward)  3.41 us
    concatenate x6, other arithmetic, send(): msg = jnp.concatenate(pieces, axis=dim)  2.61 us
  transfers between devices with their start and end apart: 11, of which 7 were waited for; matrix products, arithmetic and copies ran while one was open for 7% of the time, Pallas kernels for 0%

profile of v24, /device:TPU:34, one launch (start us, length us, event | category | flops | bytes accessed | tf_op | source)
XLA Modules:
  0.0 81.1 jit_solution(14351344364518343849)
XLA Ops:
  0.0 1.2 %fusion.228 = (f32[16,2,512]{2,1,0:T(2,128)S(1)}, f32[16,2,512]{2,1,0:T(2,128)S(1)}) fusion(f32[16,32,512]{2,1,0:T(8,128)} %param.3), kind=kLoop, calls=%fused_computation.351 | loop fusion | bytes 262144 | tf_op jit(solution)/shard_map/slice | solution.py:48
  1.2 1.4 %fusion.227 = (f32[16,3,512]{2,1,0:T(4,128)S(1)}, f32[16,3,512]{2,1,0:T(4,128)S(1)}, f32[16,3,512]{2,1,0:T(4,128)S(1)}, f32[16,3,512]{2,1,0:T(4,128)S(1)}) fusion(f32[16,32,512]{2,1,0:T(8,128)} %param.4, f32[16,32,512]{2,1,0:T(8,128)} %param.5), kind=kLoop, calls=%fused_computation.350 | loop fusion | bytes 786432 | tf_op jit(solution)/shard_map/slice | solution.py:48
  2.7 3.0 %collective-permute-start = (f32[16,8,512]{2,1,0:T(8,128)S(1)}, f32[16,8,512]{2,1,0:T(8,128)S(1)}, u32[]{:S(2)}, u32[]{:S(2)}) collective-permute-start(f32[16,8,512]{2,1,0:T(8,128)S(1)} %pad_maximum_fusion.3), channel_id=1, source_target_pairs={{0,1},{1,2},{2,3},{3,4},{4,5},{5,6},{6,7},{8,9},{9,10},{10,11},{11... | collective-permute-start | bytes 786440 | tf_op jit(solution)/shard_map/ppermute | solution.py:58
  5.7 0.8 %pad_maximum_fusion.4 = f32[16,8,512]{2,1,0:T(8,128)} fusion(f32[16,3,512]{2,1,0:T(4,128)S(1)} %get-tuple-element.81, f32[16,2,512]{2,1,0:T(2,128)S(1)} %get-tuple-element.48, f32[16,3,512]{2,1,0:T(4,128)S(1)} %get-tuple-element.46), kind=kLoop, calls=%fused_computation.147 | loop fusion | flops 131072 | bytes 524288 | tf_op jit(solution)/shard_map/concatenate | solution.py:55
  6.5 2.8 %collective-permute-start.1 = (f32[16,8,512]{2,1,0:T(8,128)}, f32[16,8,512]{2,1,0:T(8,128)S(1)}, u32[]{:S(2)}, u32[]{:S(2)}) collective-permute-start(f32[16,8,512]{2,1,0:T(8,128)} %pad_maximum_fusion.4), channel_id=1, source_target_pairs={{1,0},{2,1},{3,2},{4,3},{5,4},{6,5},{7,6},{9,8},{10,9},{11,10},{12... | collective-permute-start | bytes 786440 | tf_op jit(solution)/shard_map/ppermute | solution.py:58
  9.4 1.1 %fusion.224 = (f32[3,32,512]{2,1,0:T(8,128)S(1)}, f32[3,32,512]{2,1,0:T(8,128)S(1)}, f32[3,32,512]{2,1,0:T(8,128)S(1)}, f32[3,32,512]{2,1,0:T(8,128)S(1)}) fusion(f32[16,32,512]{2,1,0:T(8,128)S(1)} %copy-done, f32[16,32,512]{2,1,0:T(8,128)} %param.5), kind=kLoop, calls=%fused_computation.347 | loop fusion | bytes 1572864 | tf_op jit(solution)/shard_map/slice | solution.py:48
  10.5 0.8 %pad_maximum_fusion = f32[8,32,512]{2,1,0:T(8,128)} fusion(f32[3,32,512]{2,1,0:T(8,128)S(1)} %get-tuple-element.84, f32[2,32,512]{2,1,0:T(8,128)S(1)} %get-tuple-element.41, f32[3,32,512]{2,1,0:T(8,128)S(1)} %get-tuple-element.39), kind=kLoop, calls=%fused_computation.143 | loop fusion | flops 262144 | bytes 1048576 | tf_op jit(solution)/shard_map/concatenate | solution.py:55
  11.3 1.9 %collective-permute-start.3 = (f32[8,32,512]{2,1,0:T(8,128)}, f32[8,32,512]{2,1,0:T(8,128)}, u32[]{:S(2)}, u32[]{:S(2)}) collective-permute-start(f32[8,32,512]{2,1,0:T(8,128)} %pad_maximum_fusion), channel_id=1, source_target_pairs={{0,8},{8,16},{16,24},{24,32},{32,40},{40,48},{48,56},{56,64},{64,7... | collective-permute-start | bytes 1572872 | tf_op jit(solution)/shard_map/ppermute | solution.py:58
  13.2 0.8 %pad_maximum_fusion.1 = f32[8,32,512]{2,1,0:T(8,128)} fusion(f32[3,32,512]{2,1,0:T(8,128)S(1)} %get-tuple-element.83, f32[2,32,512]{2,1,0:T(8,128)S(1)} %get-tuple-element.42, f32[3,32,512]{2,1,0:T(8,128)S(1)} %get-tuple-element.40), kind=kLoop, calls=%fused_computation.144 | loop fusion | flops 262144 | bytes 1048576 | tf_op jit(solution)/shard_map/concatenate | solution.py:55
  14.1 6.0 %collective-permute-start.5 = (f32[8,32,512]{2,1,0:T(8,128)}, f32[8,32,512]{2,1,0:T(8,128)}, u32[]{:S(2)}, u32[]{:S(2)}) collective-permute-start(f32[8,32,512]{2,1,0:T(8,128)} %pad_maximum_fusion.1), channel_id=1, source_target_pairs={{8,0},{16,8},{24,16},{32,24},{40,32},{48,40},{56,48},{64,56},{72,6... | collective-permute-start | bytes 1572872 | tf_op jit(solution)/shard_map/ppermute | solution.py:58
  20.3 0.5 fusion.201
  20.8 0.1 fusion.44
  21.0 1.9 %collective-permute-start.2 = (f32[3,16,512]{2,1,0:T(8,128)S(1)}, f32[3,16,512]{2,1,0:T(8,128)S(1)}, u32[]{:S(2)}, u32[]{:S(2)}) collective-permute-start(f32[3,16,512]{2,1,0:T(8,128)S(1)} %pad_maximum_fusion.5), channel_id=1, source_target_pairs={{0,8},{8,16},{16,24},{24,32},{32,40},{40,48},{48,56},{56,64},{64,7... | collective-permute-start | bytes 294920 | tf_op jit(solution)/shard_map/ppermute | solution.py:58
  23.0 6.0 %collective-permute-start.4 = (f32[3,16,512]{2,1,0:T(8,128)S(1)}, f32[3,16,512]{2,1,0:T(8,128)S(1)}, u32[]{:S(2)}, u32[]{:S(2)}) collective-permute-start(f32[3,16,512]{2,1,0:T(8,128)S(1)} %pad_maximum_fusion.6), channel_id=1, source_target_pairs={{8,0},{16,8},{24,16},{32,24},{40,32},{48,40},{56,48},{64,56},{72,6... | collective-permute-start | bytes 294920 | tf_op jit(solution)/shard_map/ppermute | solution.py:58
  29.2 0.3 collective-permute-done.2
  29.5 2.1 %collective-permute-done.4 = f32[3,16,512]{2,1,0:T(8,128)S(1)} collective-permute-done((f32[3,16,512]{2,1,0:T(8,128)S(1)}, f32[3,16,512]{2,1,0:T(8,128)S(1)}, u32[]{:S(2)}, u32[]{:S(2)}) %collective-permute-start.4) | collective-permute-done | bytes 98336 | tf_op jit(solution)/shard_map/ppermute | solution.py:58
  31.7 1.2 %fusion.230 = (f32[3,32,512]{2,1,0:T(8,128)S(1)}, f32[3,32,512]{2,1,0:T(8,128)S(1)}, f32[3,32,512]{2,1,0:T(8,128)S(1)}) fusion(f32[8,32,512]{2,1,0:T(8,128)} %collective-permute-done.3), kind=kLoop, calls=%fused_computation.353 | loop fusion | bytes 1179648 | tf_op jit(solution)/shard_map/slice | solution.py:74
  32.8 1.2 %fusion.231 = (f32[3,32,512]{2,1,0:T(8,128)S(1)}, f32[3,32,512]{2,1,0:T(8,128)S(1)}, f32[3,32,512]{2,1,0:T(8,128)S(1)}) fusion(f32[8,32,512]{2,1,0:T(8,128)} %collective-permute-done.5), kind=kLoop, calls=%fused_computation.354 | loop fusion | bytes 1179648 | tf_op jit(solution)/shard_map/slice | solution.py:76
  34.0 0.3 maximum_maximum_fusion.2
  34.3 0.3 maximum_maximum_fusion.1
  34.6 0.3 maximum_maximum_fusion
  34.9 2.1 %divide_select_fusion.2 = (f32[22,38,512]{2,1,0:T(8,128)S(1)}, f32[22,38,512]{2,1,0:T(8,128)S(1)}, f32[22,38,512]{2,1,0:T(8,128)S(1)}) fusion(f32[22,38,512]{2,1,0:T(8,128)S(1)} %maximum_maximum_fusion.1), kind=kLoop, calls=%fused_computation.17 | loop fusion | flops 8560640 | bytes 6848512 | tf_op jit(solution)/shard_map/jit(_where)/select_n | solution.py:202
  37.1 4.1 %and_select_fusion.1 = (f32[22,38,512]{2,1,0:T(8,128)S(1)}, f32[22,38,512]{2,1,0:T(8,128)S(1)}) fusion(f32[22,38,512]{2,1,0:T(8,128)S(1)} %maximum_maximum_fusion.2, f32[22,38,512]{2,1,0:T(8,128)S(1)} %get-tuple-element.37, f32[22,38,512]{2,1,0:T(8,128)S(1)} %get-tuple-element.38, f32[22,38,512]{2,1,0:T(8,128)S(1)} %get-tuple-element.36, ...), kind=kLoop, calls=%fused_computation.19 | loop fusion | flops 12412928 | bytes 13697596 | tf_op jit(solution)/shard_map/jit(_where)/select_n | solution.py:246
  41.2 3.8 %and_select_fusion = f32[22,38,512]{2,1,0:T(8,128)S(1)} fusion(f32[22,38,512]{2,1,0:T(8,128)S(1)} %get-tuple-element.32, f32[22,38,512]{2,1,0:T(8,128)S(1)} %get-tuple-element.33, f32[22,38,512]{2,1,0:T(8,128)S(1)} %get-tuple-element.37, f32[22,38,512]{2,1,0:T(8,128)S(1)} %get-tuple-element.38, f32[22,38,512]{2,1,0:T(8,128)S(1)} %get-tuple-element.36, ...), kind=kLoop, calls=%fused_computation.18 | loop fusion | flops 11984896 | bytes 11984956 | tf_op jit(solution)/shard_map/jit(_where)/select_n | solution.py:246
  45.0 0.4 fusion.223
  45.4 2.0 %bitcast_reduce_fusion = f32[4,32,512]{2,1,0:T(8,128)S(1)} fusion(f32[16,32,512]{2,1,0:T(8,128)S(1)} %copy-done.1, f32[16,32,511]{2,1,0:T(8,128)S(1)} %get-tuple-element.35, f32[22,38,512]{2,1,0:T(8,128)S(1)} %get-tuple-element.33, f32[16,32,511]{2,1,0:T(8,128)S(1)} %get-tuple-element.34, f32[22,38,512]{2,1,0:T(8,128)S(1)} %get-tuple-element.37, ...), kind=kLoop, calls=%fused_computation.140 | loop fusion | flops 4915200 | bytes 14938112 | tf_op jit(solution)/shard_map/reduce_sum | solution.py:119
  47.4 0.5 fusion.199
  48.0 4.8 %collective-permute-start.6 = (f32[2,4,8,128]{3,2,1,0:T(8,128)S(1)}, f32[2,4,8,128]{3,2,1,0:T(8,128)S(1)}, u32[]{:S(2)}, u32[]{:S(2)}) collective-permute-start(f32[2,4,8,128]{3,2,1,0:T(8,128)S(1)} %pad_maximum_fusion.7), channel_id=1, source_target_pairs={{0,8},{8,0},{16,24},{24,16},{32,40},{40,32},{48,56},{56,48},{64,72... | collective-permute-start | bytes 98312 | tf_op jit(solution)/shard_map/ppermute | solution.py:144
  52.9 0.9 %collective-permute-done.6 = f32[2,4,8,128]{3,2,1,0:T(8,128)S(1)} collective-permute-done((f32[2,4,8,128]{3,2,1,0:T(8,128)S(1)}, f32[2,4,8,128]{3,2,1,0:T(8,128)S(1)}, u32[]{:S(2)}, u32[]{:S(2)}) %collective-permute-start.6) | collective-permute-done | bytes 32800 | tf_op jit(solution)/shard_map/ppermute | solution.py:144
  53.7 2.1 %collective-permute-start.7 = (f32[2,8,8,128]{3,2,1,0:T(8,128)S(1)}, f32[2,8,8,128]{3,2,1,0:T(8,128)S(1)}, u32[]{:S(2)}, u32[]{:S(2)}) collective-permute-start(f32[2,8,8,128]{3,2,1,0:T(8,128)S(1)} %maximum_select_fusion), channel_id=1, source_target_pairs={{0,16},{8,24},{16,32},{24,40},{32,48},{40,56},{48,64},{56,72},{64,... | collective-permute-start | bytes 196616 | tf_op jit(solution)/shard_map/ppermute | solution.py:147
  55.8 6.2 %collective-permute-start.8 = (f32[2,8,8,128]{3,2,1,0:T(8,128)S(1)}, f32[2,8,8,128]{3,2,1,0:T(8,128)S(1)}, u32[]{:S(2)}, u32[]{:S(2)}) collective-permute-start(f32[2,8,8,128]{3,2,1,0:T(8,128)S(1)} %maximum_select_fusion), channel_id=1, source_target_pairs={{16,0},{24,8},{32,16},{40,24},{48,32},{56,40},{64,48},{72,56},{80,... | collective-permute-start | bytes 196616 | tf_op jit(solution)/shard_map/ppermute | solution.py:148
  62.0 0.4 collective-permute-done.7
  62.4 2.0 %collective-permute-done.8 = f32[2,8,8,128]{3,2,1,0:T(8,128)S(1)} collective-permute-done((f32[2,8,8,128]{3,2,1,0:T(8,128)S(1)}, f32[2,8,8,128]{3,2,1,0:T(8,128)S(1)}, u32[]{:S(2)}, u32[]{:S(2)}) %collective-permute-start.8) | collective-permute-done | bytes 65568 | tf_op jit(solution)/shard_map/ppermute | solution.py:148
  64.4 2.1 %collective-permute-start.10 = (f32[2,20,8,128]{3,2,1,0:T(8,128)S(1)}, f32[2,20,8,128]{3,2,1,0:T(8,128)S(1)}, u32[]{:S(2)}, u32[]{:S(2)}) collective-permute-start(f32[2,20,8,128]{3,2,1,0:T(8,128)S(1)} %fusion.185), channel_id=1, source_target_pairs={{1,0},{2,1},{3,2},{4,3},{5,4},{6,5},{7,6},{9,8},{10,9},{11,10},{12... | collective-permute-start | bytes 491528 | tf_op jit(solution)/shard_map/ppermute | solution.py:26
  66.5 4.8 %collective-permute-start.9 = (f32[2,20,8,128]{3,2,1,0:T(8,128)S(1)}, f32[2,20,8,128]{3,2,1,0:T(8,128)S(1)}, u32[]{:S(2)}, u32[]{:S(2)}) collective-permute-start(f32[2,20,8,128]{3,2,1,0:T(8,128)S(1)} %fusion.185), channel_id=1, source_target_pairs={{0,1},{1,2},{2,3},{3,4},{4,5},{5,6},{6,7},{8,9},{9,10},{10,11},{11... | collective-permute-start | bytes 491528 | tf_op jit(solution)/shard_map/ppermute | solution.py:25
  71.4 1.8 %collective-permute-done.10 = f32[2,20,8,128]{3,2,1,0:T(8,128)S(1)} collective-permute-done((f32[2,20,8,128]{3,2,1,0:T(8,128)S(1)}, f32[2,20,8,128]{3,2,1,0:T(8,128)S(1)}, u32[]{:S(2)}, u32[]{:S(2)}) %collective-permute-start.10) | collective-permute-done | bytes 163872 | tf_op jit(solution)/shard_map/ppermute | solution.py:26
  73.2 3.4 %collective-permute-done.9 = f32[2,20,8,128]{3,2,1,0:T(8,128)S(1)} collective-permute-done((f32[2,20,8,128]{3,2,1,0:T(8,128)S(1)}, f32[2,20,8,128]{3,2,1,0:T(8,128)S(1)}, u32[]{:S(2)}, u32[]{:S(2)}) %collective-permute-start.9) | collective-permute-done | bytes 163872 | tf_op jit(solution)/shard_map/ppermute | solution.py:25
  76.7 0.5 fusion.182
  77.2 0.3 fusion.183
  77.5 0.3 multiply_add_fusion.4
  77.8 0.3 multiply_add_fusion.3
  78.1 0.3 multiply_add_fusion.2
  78.4 0.3 multiply_add_fusion.1
  78.6 0.3 multiply_add_fusion
  78.9 0.2 fusion.169
  79.1 0.5 fusion.188
  79.6 0.3 convolution_bitcast_fusion
  79.9 1.2 %bitcast_add_fusion = f32[16,32,512]{2,1,0:T(8,128)} fusion(f32[22,38,512]{2,1,0:T(8,128)S(1)} %and_select_fusion, f32[4,32,512]{2,1,0:T(8,128)S(1)} %convolution_bitcast_fusion), kind=kLoop, calls=%fused_computation.139 | loop fusion | flops 262144 | bytes 2359296 | tf_op jit(solution)/shard_map/add | solution.py:262
  (36 shorter events, 0.8 us)
Async XLA Ops:
  0.0 9.3 %copy-start = (f32[16,32,512]{2,1,0:T(8,128)S(1)}, f32[16,32,512]{2,1,0:T(8,128)}, u32[]{:S(2)}) copy-start(f32[16,32,512]{2,1,0:T(8,128)} %param.4) | copy-start | bytes 3145732
  1.2 9.3 %copy-start.1 = (f32[16,32,512]{2,1,0:T(8,128)S(1)}, f32[16,32,512]{2,1,0:T(8,128)}, u32[]{:S(2)}) copy-start(f32[16,32,512]{2,1,0:T(8,128)} %param.3) | copy-start | bytes 3145732
  2.7 18.3 %collective-permute-start = (f32[16,8,512]{2,1,0:T(8,128)S(1)}, f32[16,8,512]{2,1,0:T(8,128)S(1)}, u32[]{:S(2)}, u32[]{:S(2)}) collective-permute-start(f32[16,8,512]{2,1,0:T(8,128)S(1)} %pad_maximum_fusion.3), channel_id=1, source_target_pairs={{0,1},{1,2},{2,3},{3,4},{4,5},{5,6},{6,7},{8,9},{9,10},{10,11},{11... | collective-permute-start | bytes 786440 | tf_op jit(solution)/shard_map/ppermute | solution.py:58
  6.5 14.5 %collective-permute-start.1 = (f32[16,8,512]{2,1,0:T(8,128)}, f32[16,8,512]{2,1,0:T(8,128)S(1)}, u32[]{:S(2)}, u32[]{:S(2)}) collective-permute-start(f32[16,8,512]{2,1,0:T(8,128)} %pad_maximum_fusion.4), channel_id=1, source_target_pairs={{1,0},{2,1},{3,2},{4,3},{5,4},{6,5},{7,6},{9,8},{10,9},{11,10},{12... | collective-permute-start | bytes 786440 | tf_op jit(solution)/shard_map/ppermute | solution.py:58
  11.3 20.3 %collective-permute-start.3 = (f32[8,32,512]{2,1,0:T(8,128)}, f32[8,32,512]{2,1,0:T(8,128)}, u32[]{:S(2)}, u32[]{:S(2)}) collective-permute-start(f32[8,32,512]{2,1,0:T(8,128)} %pad_maximum_fusion), channel_id=1, source_target_pairs={{0,8},{8,16},{16,24},{24,32},{32,40},{40,48},{48,56},{56,64},{64,7... | collective-permute-start | bytes 1572872 | tf_op jit(solution)/shard_map/ppermute | solution.py:58
  14.1 18.7 %collective-permute-start.5 = (f32[8,32,512]{2,1,0:T(8,128)}, f32[8,32,512]{2,1,0:T(8,128)}, u32[]{:S(2)}, u32[]{:S(2)}) collective-permute-start(f32[8,32,512]{2,1,0:T(8,128)} %pad_maximum_fusion.1), channel_id=1, source_target_pairs={{8,0},{16,8},{24,16},{32,24},{40,32},{48,40},{56,48},{64,56},{72,6... | collective-permute-start | bytes 1572872 | tf_op jit(solution)/shard_map/ppermute | solution.py:58
  21.0 8.4 %collective-permute-start.2 = (f32[3,16,512]{2,1,0:T(8,128)S(1)}, f32[3,16,512]{2,1,0:T(8,128)S(1)}, u32[]{:S(2)}, u32[]{:S(2)}) collective-permute-start(f32[3,16,512]{2,1,0:T(8,128)S(1)} %pad_maximum_fusion.5), channel_id=1, source_target_pairs={{0,8},{8,16},{16,24},{24,32},{32,40},{40,48},{48,56},{56,64},{64,7... | collective-permute-start | bytes 294920 | tf_op jit(solution)/shard_map/ppermute | solution.py:58
  23.0 8.6 %collective-permute-start.4 = (f32[3,16,512]{2,1,0:T(8,128)S(1)}, f32[3,16,512]{2,1,0:T(8,128)S(1)}, u32[]{:S(2)}, u32[]{:S(2)}) collective-permute-start(f32[3,16,512]{2,1,0:T(8,128)S(1)} %pad_maximum_fusion.6), channel_id=1, source_target_pairs={{8,0},{16,8},{24,16},{32,24},{40,32},{48,40},{56,48},{64,56},{72,6... | collective-permute-start | bytes 294920 | tf_op jit(solution)/shard_map/ppermute | solution.py:58
  29.1 4.9 %copy-start.2 = (f32[16,32,512]{2,1,0:T(8,128)S(1)}, f32[16,32,512]{2,1,0:T(8,128)}, u32[]{:S(2)}) copy-start(f32[16,32,512]{2,1,0:T(8,128)} %param.5) | copy-start | bytes 3145732
  48.0 5.7 %collective-permute-start.6 = (f32[2,4,8,128]{3,2,1,0:T(8,128)S(1)}, f32[2,4,8,128]{3,2,1,0:T(8,128)S(1)}, u32[]{:S(2)}, u32[]{:S(2)}) collective-permute-start(f32[2,4,8,128]{3,2,1,0:T(8,128)S(1)} %pad_maximum_fusion.7), channel_id=1, source_target_pairs={{0,8},{8,0},{16,24},{24,16},{32,40},{40,32},{48,56},{56,48},{64,72... | collective-permute-start | bytes 98312 | tf_op jit(solution)/shard_map/ppermute | solution.py:144
  53.7 8.6 %collective-permute-start.7 = (f32[2,8,8,128]{3,2,1,0:T(8,128)S(1)}, f32[2,8,8,128]{3,2,1,0:T(8,128)S(1)}, u32[]{:S(2)}, u32[]{:S(2)}) collective-permute-start(f32[2,8,8,128]{3,2,1,0:T(8,128)S(1)} %maximum_select_fusion), channel_id=1, source_target_pairs={{0,16},{8,24},{16,32},{24,40},{32,48},{40,56},{48,64},{56,72},{64,... | collective-permute-start | bytes 196616 | tf_op jit(solution)/shard_map/ppermute | solution.py:147
  55.8 8.5 %collective-permute-start.8 = (f32[2,8,8,128]{3,2,1,0:T(8,128)S(1)}, f32[2,8,8,128]{3,2,1,0:T(8,128)S(1)}, u32[]{:S(2)}, u32[]{:S(2)}) collective-permute-start(f32[2,8,8,128]{3,2,1,0:T(8,128)S(1)} %maximum_select_fusion), channel_id=1, source_target_pairs={{16,0},{24,8},{32,16},{40,24},{48,32},{56,40},{64,48},{72,56},{80,... | collective-permute-start | bytes 196616 | tf_op jit(solution)/shard_map/ppermute | solution.py:148
  64.4 8.8 %collective-permute-start.10 = (f32[2,20,8,128]{3,2,1,0:T(8,128)S(1)}, f32[2,20,8,128]{3,2,1,0:T(8,128)S(1)}, u32[]{:S(2)}, u32[]{:S(2)}) collective-permute-start(f32[2,20,8,128]{3,2,1,0:T(8,128)S(1)} %fusion.185), channel_id=1, source_target_pairs={{1,0},{2,1},{3,2},{4,3},{5,4},{6,5},{7,6},{9,8},{10,9},{11,10},{12... | collective-permute-start | bytes 491528 | tf_op jit(solution)/shard_map/ppermute | solution.py:26
  66.5 10.1 %collective-permute-start.9 = (f32[2,20,8,128]{3,2,1,0:T(8,128)S(1)}, f32[2,20,8,128]{3,2,1,0:T(8,128)S(1)}, u32[]{:S(2)}, u32[]{:S(2)}) collective-permute-start(f32[2,20,8,128]{3,2,1,0:T(8,128)S(1)} %fusion.185), channel_id=1, source_target_pairs={{0,1},{1,2},{2,3},{3,4},{4,5},{5,6},{6,7},{8,9},{9,10},{10,11},{11... | collective-permute-start | bytes 491528 | tf_op jit(solution)/shard_map/ppermute | solution.py:25

commit v25 on v23

--- a/solution.py
+++ b/solution.py
@@ -257,7 +257,7 @@
     res = right_side - apply_op(core, nears, [c[own] for c in coefs])
     fine, res = core, lax.optimization_barrier(res)
     coarse_rhs = block_mean(res)
-    coarse_b = block_mean(inv_density)
+    coarse_b = block_mean(b_e[own])
     corr = chebyshev_local(coarse_rhs, coarse_b)
     return fine + expand(corr, fine.shape)
 

time: 82.5 us -> 84.8 us (1.028)
  waiting for transfers between devices: 10.8 us -> 12.6 us
    ppermute x6, waiting for transfers between devices: 2.42 us -> 4.44 us  [send(): return lax.ppermute(msg, axis, pairs)]
    slice x1, local copies, waits for them, and re-layouts: 1.16 us -> 0.04 us  [packed_halo(): xl[lo_win]]
    unnamed x6, local copies, waits for them, and re-layouts: 0.02 us -> 0.94 us
  transfers between devices with their start and end apart: 11 -> 11, of which waited for: 7 -> 7; matrix products, arithmetic and copies ran while one was open for 7% -> 5% of each run, Pallas kernels for 0% -> 0%
where the time goes in v25:
time: 84.8 us; the launch traced here: 83.4 us
  starting transfers between devices  41.7 us (49%)
  other arithmetic  20.1 us (24%)
  waiting for transfers between devices  12.6 us (15%)
  local copies, waits for them, and re-layouts  6.45 us (8%)
  matrix products  2.05 us (2%)
    ppermute x6, starting transfers between devices, send(): return lax.ppermute(msg, axis, pairs)  21.7 us
    select_n x2, other arithmetic, per_device(): fine = jnp.where(inside, fine + step, 0.0)  7.9 us
    ppermute x1, starting transfers between devices, pair_extend(): high = lax.ppermute(pair, 'box', [(t, s) for s, t in shifted_pairs(nb, 2)])  6.19 us
    ppermute x1, starting transfers between devices, pair_extend(): partner = lax.ppermute(block, 'box', [(i, i ^ 1) for i in range(nb)])  4.82 us
    ppermute x1, starting transfers between devices, halo_from(): lax.ppermute(lax.slice_in_dim(block, n - width, n, axis=dim), axis, forward)  4.77 us
    ppermute x6, waiting for transfers between devices, send(): return lax.ppermute(msg, axis, pairs)  4.44 us
    slice x6, local copies, waits for them, and re-layouts, packed_halo(): lax.slice_in_dim(f, f.shape[dim] - d, f.shape[dim], axis=dim)  3.68 us
    ppermute x1, waiting for transfers between devices, halo_from(): lax.ppermute(lax.slice_in_dim(block, n - width, n, axis=dim), axis, forward)  3.41 us
  transfers between devices with their start and end apart: 11, of which 7 were waited for; matrix products, arithmetic and copies ran while one was open for 5% of the time, Pallas kernels for 0%

profile of v25, /device:TPU:34, one launch (start us, length us, event | category | flops | bytes accessed | tf_op | source)
XLA Modules:
  0.0 83.4 jit_solution(2297130903768669342)
XLA Ops:
  0.0 1.2 %fusion.228 = (f32[16,2,512]{2,1,0:T(2,128)S(1)}, f32[16,2,512]{2,1,0:T(2,128)S(1)}) fusion(f32[16,32,512]{2,1,0:T(8,128)} %param.3), kind=kLoop, calls=%fused_computation.351 | loop fusion | bytes 262144 | tf_op jit(solution)/shard_map/slice | solution.py:48
  1.2 1.4 %fusion.227 = (f32[16,3,512]{2,1,0:T(4,128)S(1)}, f32[16,3,512]{2,1,0:T(4,128)S(1)}, f32[16,3,512]{2,1,0:T(4,128)S(1)}, f32[16,3,512]{2,1,0:T(4,128)S(1)}) fusion(f32[16,32,512]{2,1,0:T(8,128)} %param.4, f32[16,32,512]{2,1,0:T(8,128)} %param.5), kind=kLoop, calls=%fused_computation.350 | loop fusion | bytes 786432 | tf_op jit(solution)/shard_map/slice | solution.py:48
  2.6 0.8 pad_maximum_fusion.3
  3.4 3.0 %collective-permute-start = (f32[16,8,512]{2,1,0:T(8,128)}, f32[16,8,512]{2,1,0:T(8,128)S(1)}, u32[]{:S(2)}, u32[]{:S(2)}) collective-permute-start(f32[16,8,512]{2,1,0:T(8,128)} %pad_maximum_fusion.3), channel_id=1, source_target_pairs={{0,1},{1,2},{2,3},{3,4},{4,5},{5,6},{6,7},{8,9},{9,10},{10,11},{11... | collective-permute-start | bytes 786440 | tf_op jit(solution)/shard_map/ppermute | solution.py:58
  6.4 0.8 pad_maximum_fusion.4
  7.2 2.8 %collective-permute-start.1 = (f32[16,8,512]{2,1,0:T(8,128)}, f32[16,8,512]{2,1,0:T(8,128)S(1)}, u32[]{:S(2)}, u32[]{:S(2)}) collective-permute-start(f32[16,8,512]{2,1,0:T(8,128)} %pad_maximum_fusion.4), channel_id=1, source_target_pairs={{1,0},{2,1},{3,2},{4,3},{5,4},{6,5},{7,6},{9,8},{10,9},{11,10},{12... | collective-permute-start | bytes 786440 | tf_op jit(solution)/shard_map/ppermute | solution.py:58
  10.0 1.1 %fusion.224 = (f32[3,32,512]{2,1,0:T(8,128)S(1)}, f32[3,32,512]{2,1,0:T(8,128)S(1)}, f32[3,32,512]{2,1,0:T(8,128)S(1)}, f32[3,32,512]{2,1,0:T(8,128)S(1)}) fusion(f32[16,32,512]{2,1,0:T(8,128)} %param.4, f32[16,32,512]{2,1,0:T(8,128)S(1)} %copy-done.1), kind=kLoop, calls=%fused_computation.347 | loop fusion | bytes 1572864 | tf_op jit(solution)/shard_map/slice | solution.py:48
  11.1 0.8 %pad_maximum_fusion = f32[8,32,512]{2,1,0:T(8,128)} fusion(f32[3,32,512]{2,1,0:T(8,128)S(1)} %get-tuple-element.84, f32[2,32,512]{2,1,0:T(8,128)S(1)} %get-tuple-element.41, f32[3,32,512]{2,1,0:T(8,128)S(1)} %get-tuple-element.39), kind=kLoop, calls=%fused_computation.143 | loop fusion | flops 262144 | bytes 1048576 | tf_op jit(solution)/shard_map/concatenate | solution.py:55
  12.0 1.9 %collective-permute-start.3 = (f32[8,32,512]{2,1,0:T(8,128)}, f32[8,32,512]{2,1,0:T(8,128)S(1)}, u32[]{:S(2)}, u32[]{:S(2)}) collective-permute-start(f32[8,32,512]{2,1,0:T(8,128)} %pad_maximum_fusion), channel_id=1, source_target_pairs={{0,8},{8,16},{16,24},{24,32},{32,40},{40,48},{48,56},{56,64},{64,7... | collective-permute-start | bytes 1572872 | tf_op jit(solution)/shard_map/ppermute | solution.py:58
  13.9 0.8 %pad_maximum_fusion.1 = f32[8,32,512]{2,1,0:T(8,128)} fusion(f32[3,32,512]{2,1,0:T(8,128)S(1)} %get-tuple-element.83, f32[2,32,512]{2,1,0:T(8,128)S(1)} %get-tuple-element.42, f32[3,32,512]{2,1,0:T(8,128)S(1)} %get-tuple-element.40), kind=kLoop, calls=%fused_computation.144 | loop fusion | flops 262144 | bytes 1048576 | tf_op jit(solution)/shard_map/concatenate | solution.py:55
  14.7 6.0 %collective-permute-start.5 = (f32[8,32,512]{2,1,0:T(8,128)}, f32[8,32,512]{2,1,0:T(8,128)}, u32[]{:S(2)}, u32[]{:S(2)}) collective-permute-start(f32[8,32,512]{2,1,0:T(8,128)} %pad_maximum_fusion.1), channel_id=1, source_target_pairs={{8,0},{16,8},{24,16},{32,24},{40,32},{48,40},{56,48},{64,56},{72,6... | collective-permute-start | bytes 1572872 | tf_op jit(solution)/shard_map/ppermute | solution.py:58
  21.0 1.9 %collective-permute-start.2 = (f32[3,16,512]{2,1,0:T(8,128)S(1)}, f32[3,16,512]{2,1,0:T(8,128)S(1)}, u32[]{:S(2)}, u32[]{:S(2)}) collective-permute-start(f32[3,16,512]{2,1,0:T(8,128)S(1)} %pad_maximum_fusion.5), channel_id=1, source_target_pairs={{0,8},{8,16},{16,24},{24,32},{32,40},{40,48},{48,56},{56,64},{64,7... | collective-permute-start | bytes 294920 | tf_op jit(solution)/shard_map/ppermute | solution.py:58
  22.9 6.0 %collective-permute-start.4 = (f32[3,16,512]{2,1,0:T(8,128)S(1)}, f32[3,16,512]{2,1,0:T(8,128)S(1)}, u32[]{:S(2)}, u32[]{:S(2)}) collective-permute-start(f32[3,16,512]{2,1,0:T(8,128)S(1)} %pad_maximum_fusion.6), channel_id=1, source_target_pairs={{8,0},{16,8},{24,16},{32,24},{40,32},{48,40},{56,48},{64,56},{72,6... | collective-permute-start | bytes 294920 | tf_op jit(solution)/shard_map/ppermute | solution.py:58
  29.1 0.3 collective-permute-done.2
  29.4 4.1 %collective-permute-done.4 = f32[3,16,512]{2,1,0:T(8,128)S(1)} collective-permute-done((f32[3,16,512]{2,1,0:T(8,128)S(1)}, f32[3,16,512]{2,1,0:T(8,128)S(1)}, u32[]{:S(2)}, u32[]{:S(2)}) %collective-permute-start.4) | collective-permute-done | bytes 98336 | tf_op jit(solution)/shard_map/ppermute | solution.py:58
  33.7 1.2 %fusion.231 = (f32[3,32,512]{2,1,0:T(8,128)S(1)}, f32[3,32,512]{2,1,0:T(8,128)S(1)}, f32[3,32,512]{2,1,0:T(8,128)S(1)}) fusion(f32[8,32,512]{2,1,0:T(8,128)} %collective-permute-done.5), kind=kLoop, calls=%fused_computation.354 | loop fusion | bytes 1179648 | tf_op jit(solution)/shard_map/slice | solution.py:76
  34.8 0.3 maximum_maximum_fusion.2
  35.1 0.9 %copy-done.2 = f32[16,32,512]{2,1,0:T(8,128)S(1)} copy-done((f32[16,32,512]{2,1,0:T(8,128)S(1)}, f32[16,32,512]{2,1,0:T(8,128)}, u32[]{:S(2)}) %copy-start.2) | copy-done | bytes 1048600
  36.1 0.3 maximum_maximum_fusion.1
  36.4 0.3 maximum_maximum_fusion
  36.7 2.1 %divide_select_fusion.2 = (f32[22,38,512]{2,1,0:T(8,128)S(1)}, f32[22,38,512]{2,1,0:T(8,128)S(1)}, f32[22,38,512]{2,1,0:T(8,128)S(1)}) fusion(f32[22,38,512]{2,1,0:T(8,128)S(1)} %maximum_maximum_fusion.1), kind=kLoop, calls=%fused_computation.17 | loop fusion | flops 8560640 | bytes 6848512 | tf_op jit(solution)/shard_map/jit(_where)/select_n | solution.py:202
  39.0 4.1 %and_select_fusion.1 = (f32[22,38,512]{2,1,0:T(8,128)S(1)}, f32[22,38,512]{2,1,0:T(8,128)S(1)}) fusion(f32[22,38,512]{2,1,0:T(8,128)S(1)} %maximum_maximum_fusion.2, f32[22,38,512]{2,1,0:T(8,128)S(1)} %get-tuple-element.38, f32[22,38,512]{2,1,0:T(8,128)S(1)} %get-tuple-element.37, f32[22,38,512]{2,1,0:T(8,128)S(1)} %get-tuple-element.36, ...), kind=kLoop, calls=%fused_computation.19 | loop fusion | flops 12412928 | bytes 13697596 | tf_op jit(solution)/shard_map/jit(_where)/select_n | solution.py:246
  43.1 3.8 %and_select_fusion = f32[22,38,512]{2,1,0:T(8,128)S(1)} fusion(f32[22,38,512]{2,1,0:T(8,128)S(1)} %get-tuple-element.32, f32[22,38,512]{2,1,0:T(8,128)S(1)} %get-tuple-element.33, f32[22,38,512]{2,1,0:T(8,128)S(1)} %get-tuple-element.38, f32[22,38,512]{2,1,0:T(8,128)S(1)} %get-tuple-element.37, f32[22,38,512]{2,1,0:T(8,128)S(1)} %get-tuple-element.36, ...), kind=kLoop, calls=%fused_computation.18 | loop fusion | flops 11984896 | bytes 11984956 | tf_op jit(solution)/shard_map/jit(_where)/select_n | solution.py:246
  46.9 0.4 fusion.223
  47.4 1.8 %fusion.46 = f32[16,32,512]{2,1,0:T(8,128)S(1)} fusion(f32[16,32,512]{2,1,0:T(8,128)S(1)} %copy-done, f32[22,38,512]{2,1,0:T(8,128)S(1)} %get-tuple-element.33, f32[22,38,512]{2,1,0:T(8,128)S(1)} %get-tuple-element.38, f32[22,38,512]{2,1,0:T(8,128)S(1)} %and_select_fusion, f32[22,38,512]{2,1,0:T(8,128)S(1)} %get-tuple-element.37, ...), kind=kLoop, calls=%fused_computation.125 | loop fusion | flops 4718592 | bytes 15724544 | tf_op jit(solution)/shard_map/sub | solution.py:257
  49.2 0.5 fusion.199
  49.7 0.5 fusion.201
  50.5 4.8 %collective-permute-start.6 = (f32[2,4,8,128]{3,2,1,0:T(8,128)S(1)}, f32[2,4,8,128]{3,2,1,0:T(8,128)S(1)}, u32[]{:S(2)}, u32[]{:S(2)}) collective-permute-start(f32[2,4,8,128]{3,2,1,0:T(8,128)S(1)} %pad_maximum_fusion.7), channel_id=1, source_target_pairs={{0,8},{8,0},{16,24},{24,16},{32,40},{40,32},{48,56},{56,48},{64,72... | collective-permute-start | bytes 98312 | tf_op jit(solution)/shard_map/ppermute | solution.py:144
  55.3 0.9 %collective-permute-done.6 = f32[2,4,8,128]{3,2,1,0:T(8,128)S(1)} collective-permute-done((f32[2,4,8,128]{3,2,1,0:T(8,128)S(1)}, f32[2,4,8,128]{3,2,1,0:T(8,128)S(1)}, u32[]{:S(2)}, u32[]{:S(2)}) %collective-permute-start.6) | collective-permute-done | bytes 32800 | tf_op jit(solution)/shard_map/ppermute | solution.py:144
  56.2 2.1 %collective-permute-start.7 = (f32[2,8,8,128]{3,2,1,0:T(8,128)S(1)}, f32[2,8,8,128]{3,2,1,0:T(8,128)S(1)}, u32[]{:S(2)}, u32[]{:S(2)}) collective-permute-start(f32[2,8,8,128]{3,2,1,0:T(8,128)S(1)} %maximum_select_fusion), channel_id=1, source_target_pairs={{0,16},{8,24},{16,32},{24,40},{32,48},{40,56},{48,64},{56,72},{64,... | collective-permute-start | bytes 196616 | tf_op jit(solution)/shard_map/ppermute | solution.py:147
  58.3 6.2 %collective-permute-start.8 = (f32[2,8,8,128]{3,2,1,0:T(8,128)S(1)}, f32[2,8,8,128]{3,2,1,0:T(8,128)S(1)}, u32[]{:S(2)}, u32[]{:S(2)}) collective-permute-start(f32[2,8,8,128]{3,2,1,0:T(8,128)S(1)} %maximum_select_fusion), channel_id=1, source_target_pairs={{16,0},{24,8},{32,16},{40,24},{48,32},{56,40},{64,48},{72,56},{80,... | collective-permute-start | bytes 196616 | tf_op jit(solution)/shard_map/ppermute | solution.py:148
  64.5 0.4 collective-permute-done.7
  64.9 2.0 %collective-permute-done.8 = f32[2,8,8,128]{3,2,1,0:T(8,128)S(1)} collective-permute-done((f32[2,8,8,128]{3,2,1,0:T(8,128)S(1)}, f32[2,8,8,128]{3,2,1,0:T(8,128)S(1)}, u32[]{:S(2)}, u32[]{:S(2)}) %collective-permute-start.8) | collective-permute-done | bytes 65568 | tf_op jit(solution)/shard_map/ppermute | solution.py:148
  66.9 2.2 %collective-permute-start.10 = (f32[2,20,8,128]{3,2,1,0:T(8,128)S(1)}, f32[2,20,8,128]{3,2,1,0:T(8,128)S(1)}, u32[]{:S(2)}, u32[]{:S(2)}) collective-permute-start(f32[2,20,8,128]{3,2,1,0:T(8,128)S(1)} %fusion.185), channel_id=1, source_target_pairs={{1,0},{2,1},{3,2},{4,3},{5,4},{6,5},{7,6},{9,8},{10,9},{11,10},{12... | collective-permute-start | bytes 491528 | tf_op jit(solution)/shard_map/ppermute | solution.py:26
  69.0 4.8 %collective-permute-start.9 = (f32[2,20,8,128]{3,2,1,0:T(8,128)S(1)}, f32[2,20,8,128]{3,2,1,0:T(8,128)S(1)}, u32[]{:S(2)}, u32[]{:S(2)}) collective-permute-start(f32[2,20,8,128]{3,2,1,0:T(8,128)S(1)} %fusion.185), channel_id=1, source_target_pairs={{0,1},{1,2},{2,3},{3,4},{4,5},{5,6},{6,7},{8,9},{9,10},{10,11},{11... | collective-permute-start | bytes 491528 | tf_op jit(solution)/shard_map/ppermute | solution.py:25
  73.9 1.6 %collective-permute-done.10 = f32[2,20,8,128]{3,2,1,0:T(8,128)S(1)} collective-permute-done((f32[2,20,8,128]{3,2,1,0:T(8,128)S(1)}, f32[2,20,8,128]{3,2,1,0:T(8,128)S(1)}, u32[]{:S(2)}, u32[]{:S(2)}) %collective-permute-start.10) | collective-permute-done | bytes 163872 | tf_op jit(solution)/shard_map/ppermute | solution.py:26
  75.4 3.4 %collective-permute-done.9 = f32[2,20,8,128]{3,2,1,0:T(8,128)S(1)} collective-permute-done((f32[2,20,8,128]{3,2,1,0:T(8,128)S(1)}, f32[2,20,8,128]{3,2,1,0:T(8,128)S(1)}, u32[]{:S(2)}, u32[]{:S(2)}) %collective-permute-start.9) | collective-permute-done | bytes 163872 | tf_op jit(solution)/shard_map/ppermute | solution.py:25
  78.9 0.5 fusion.182
  79.4 0.3 fusion.183
  79.8 0.3 multiply_add_fusion.4
  80.0 0.3 multiply_add_fusion.3
  80.3 0.3 multiply_add_fusion.2
  80.6 0.3 multiply_add_fusion.1
  80.9 0.3 multiply_add_fusion
  81.2 0.2 fusion.169
  81.4 0.5 fusion.188
  81.9 0.3 convolution_bitcast_fusion
  82.2 1.2 %bitcast_add_fusion = f32[16,32,512]{2,1,0:T(8,128)} fusion(f32[22,38,512]{2,1,0:T(8,128)S(1)} %and_select_fusion, f32[4,32,512]{2,1,0:T(8,128)S(1)} %convolution_bitcast_fusion), kind=kLoop, calls=%fused_computation.139 | loop fusion | flops 262144 | bytes 2359296 | tf_op jit(solution)/shard_map/add | solution.py:262
  (37 shorter events, 1.0 us)
Async XLA Ops:
  0.0 10.0 %copy-start.1 = (f32[16,32,512]{2,1,0:T(8,128)S(1)}, f32[16,32,512]{2,1,0:T(8,128)}, u32[]{:S(2)}) copy-start(f32[16,32,512]{2,1,0:T(8,128)} %param.5) | copy-start | bytes 3145732
  1.2 9.9 %copy-start = (f32[16,32,512]{2,1,0:T(8,128)S(1)}, f32[16,32,512]{2,1,0:T(8,128)}, u32[]{:S(2)}) copy-start(f32[16,32,512]{2,1,0:T(8,128)} %param.3) | copy-start | bytes 3145732
  3.4 17.5 %collective-permute-start = (f32[16,8,512]{2,1,0:T(8,128)}, f32[16,8,512]{2,1,0:T(8,128)S(1)}, u32[]{:S(2)}, u32[]{:S(2)}) collective-permute-start(f32[16,8,512]{2,1,0:T(8,128)} %pad_maximum_fusion.3), channel_id=1, source_target_pairs={{0,1},{1,2},{2,3},{3,4},{4,5},{5,6},{6,7},{8,9},{9,10},{10,11},{11... | collective-permute-start | bytes 786440 | tf_op jit(solution)/shard_map/ppermute | solution.py:58
  7.2 13.7 %collective-permute-start.1 = (f32[16,8,512]{2,1,0:T(8,128)}, f32[16,8,512]{2,1,0:T(8,128)S(1)}, u32[]{:S(2)}, u32[]{:S(2)}) collective-permute-start(f32[16,8,512]{2,1,0:T(8,128)} %pad_maximum_fusion.4), channel_id=1, source_target_pairs={{1,0},{2,1},{3,2},{4,3},{5,4},{6,5},{7,6},{9,8},{10,9},{11,10},{12... | collective-permute-start | bytes 786440 | tf_op jit(solution)/shard_map/ppermute | solution.py:58
  12.0 21.6 %collective-permute-start.3 = (f32[8,32,512]{2,1,0:T(8,128)}, f32[8,32,512]{2,1,0:T(8,128)S(1)}, u32[]{:S(2)}, u32[]{:S(2)}) collective-permute-start(f32[8,32,512]{2,1,0:T(8,128)} %pad_maximum_fusion), channel_id=1, source_target_pairs={{0,8},{8,16},{16,24},{24,32},{32,40},{40,48},{48,56},{56,64},{64,7... | collective-permute-start | bytes 1572872 | tf_op jit(solution)/shard_map/ppermute | solution.py:58
  14.7 18.9 %collective-permute-start.5 = (f32[8,32,512]{2,1,0:T(8,128)}, f32[8,32,512]{2,1,0:T(8,128)}, u32[]{:S(2)}, u32[]{:S(2)}) collective-permute-start(f32[8,32,512]{2,1,0:T(8,128)} %pad_maximum_fusion.1), channel_id=1, source_target_pairs={{8,0},{16,8},{24,16},{32,24},{40,32},{48,40},{56,48},{64,56},{72,6... | collective-permute-start | bytes 1572872 | tf_op jit(solution)/shard_map/ppermute | solution.py:58
  21.0 8.4 %collective-permute-start.2 = (f32[3,16,512]{2,1,0:T(8,128)S(1)}, f32[3,16,512]{2,1,0:T(8,128)S(1)}, u32[]{:S(2)}, u32[]{:S(2)}) collective-permute-start(f32[3,16,512]{2,1,0:T(8,128)S(1)} %pad_maximum_fusion.5), channel_id=1, source_target_pairs={{0,8},{8,16},{16,24},{24,32},{32,40},{40,48},{48,56},{56,64},{64,7... | collective-permute-start | bytes 294920 | tf_op jit(solution)/shard_map/ppermute | solution.py:58
  22.9 10.7 %collective-permute-start.4 = (f32[3,16,512]{2,1,0:T(8,128)S(1)}, f32[3,16,512]{2,1,0:T(8,128)S(1)}, u32[]{:S(2)}, u32[]{:S(2)}) collective-permute-start(f32[3,16,512]{2,1,0:T(8,128)S(1)} %pad_maximum_fusion.6), channel_id=1, source_target_pairs={{8,0},{16,8},{24,16},{32,24},{40,32},{48,40},{56,48},{64,56},{72,6... | collective-permute-start | bytes 294920 | tf_op jit(solution)/shard_map/ppermute | solution.py:58
  34.8 1.2 %copy-start.2 = (f32[16,32,512]{2,1,0:T(8,128)S(1)}, f32[16,32,512]{2,1,0:T(8,128)}, u32[]{:S(2)}) copy-start(f32[16,32,512]{2,1,0:T(8,128)} %param.4) | copy-start | bytes 3145732
  50.5 5.7 %collective-permute-start.6 = (f32[2,4,8,128]{3,2,1,0:T(8,128)S(1)}, f32[2,4,8,128]{3,2,1,0:T(8,128)S(1)}, u32[]{:S(2)}, u32[]{:S(2)}) collective-permute-start(f32[2,4,8,128]{3,2,1,0:T(8,128)S(1)} %pad_maximum_fusion.7), channel_id=1, source_target_pairs={{0,8},{8,0},{16,24},{24,16},{32,40},{40,32},{48,56},{56,48},{64,72... | collective-permute-start | bytes 98312 | tf_op jit(solution)/shard_map/ppermute | solution.py:144
  56.2 8.6 %collective-permute-start.7 = (f32[2,8,8,128]{3,2,1,0:T(8,128)S(1)}, f32[2,8,8,128]{3,2,1,0:T(8,128)S(1)}, u32[]{:S(2)}, u32[]{:S(2)}) collective-permute-start(f32[2,8,8,128]{3,2,1,0:T(8,128)S(1)} %maximum_select_fusion), channel_id=1, source_target_pairs={{0,16},{8,24},{16,32},{24,40},{32,48},{40,56},{48,64},{56,72},{64,... | collective-permute-start | bytes 196616 | tf_op jit(solution)/shard_map/ppermute | solution.py:147
  58.3 8.5 %collective-permute-start.8 = (f32[2,8,8,128]{3,2,1,0:T(8,128)S(1)}, f32[2,8,8,128]{3,2,1,0:T(8,128)S(1)}, u32[]{:S(2)}, u32[]{:S(2)}) collective-permute-start(f32[2,8,8,128]{3,2,1,0:T(8,128)S(1)} %maximum_select_fusion), channel_id=1, source_target_pairs={{16,0},{24,8},{32,16},{40,24},{48,32},{56,40},{64,48},{72,56},{80,... | collective-permute-start | bytes 196616 | tf_op jit(solution)/shard_map/ppermute | solution.py:148
  66.9 8.5 %collective-permute-start.10 = (f32[2,20,8,128]{3,2,1,0:T(8,128)S(1)}, f32[2,20,8,128]{3,2,1,0:T(8,128)S(1)}, u32[]{:S(2)}, u32[]{:S(2)}) collective-permute-start(f32[2,20,8,128]{3,2,1,0:T(8,128)S(1)} %fusion.185), channel_id=1, source_target_pairs={{1,0},{2,1},{3,2},{4,3},{5,4},{6,5},{7,6},{9,8},{10,9},{11,10},{12... | collective-permute-start | bytes 491528 | tf_op jit(solution)/shard_map/ppermute | solution.py:26
  69.0 9.8 %collective-permute-start.9 = (f32[2,20,8,128]{3,2,1,0:T(8,128)S(1)}, f32[2,20,8,128]{3,2,1,0:T(8,128)S(1)}, u32[]{:S(2)}, u32[]{:S(2)}) collective-permute-start(f32[2,20,8,128]{3,2,1,0:T(8,128)S(1)} %fusion.185), channel_id=1, source_target_pairs={{0,1},{1,2},{2,3},{3,4},{4,5},{5,6},{6,7},{8,9},{9,10},{10,11},{11... | collective-permute-start | bytes 491528 | tf_op jit(solution)/shard_map/ppermute | solution.py:25

commit v26 on v22

--- a/solution.py
+++ b/solution.py
@@ -261,7 +261,7 @@
         shift_z(core, 1),
     ]
     res = right_side - apply_op(core, nears, [c[own] for c in coefs])
-    fine, res = lax.optimization_barrier((core, res))
+    fine, res = core, lax.optimization_barrier(res)
     coarse_rhs = block_mean(res)
     coarse_b = block_mean(inv_density)
     corr = chebyshev_local(coarse_rhs, coarse_b)

time: 85.1 us -> 82.3 us (0.967)
  the two profiles are of different devices: /device:TPU:90 before, /device:TPU:88 now
where the time goes in v26:
time: 82.3 us; the launch traced here: 81.9 us
  starting transfers between devices  38.4 us (47%)
  other arithmetic  19.3 us (23%)
  waiting for transfers between devices  15 us (18%)
  local copies, waits for them, and re-layouts  6.66 us (8%)
  matrix products  2.05 us (2%)
    ppermute x6, starting transfers between devices, send(): return lax.ppermute(msg, axis, pairs)  20.8 us
    select_n x2, other arithmetic, per_device(): fine = jnp.where(inside, fine + step, 0.0)  7.9 us
    ppermute x1, starting transfers between devices, pair_extend(): low = lax.ppermute(pair, 'box', shifted_pairs(nb, 2))  7.73 us
    ppermute x1, waiting for transfers between devices, pair_extend(): high = lax.ppermute(pair, 'box', [(t, s) for s, t in shifted_pairs(nb, 2)])  6.61 us
    slice x6, local copies, waits for them, and re-layouts, packed_halo(): lax.slice_in_dim(f, f.shape[dim] - d, f.shape[dim], axis=dim)  3.68 us
    ppermute x1, starting transfers between devices, halo_from(): lax.ppermute(lax.slice_in_dim(block, n - width, n, axis=dim), axis, forward)  3.19 us
    ppermute x1, starting transfers between devices, halo_from(): lax.ppermute(lax.slice_in_dim(block, 0, width, axis=dim), axis, backward)  2.84 us
    ppermute x6, waiting for transfers between devices, send(): return lax.ppermute(msg, axis, pairs)  2.81 us
  transfers between devices with their start and end apart: 11, of which 5 were waited for; matrix products, arithmetic and copies ran while one was open for 7% of the time, Pallas kernels for 0%

profile of v26, /device:TPU:88, one launch (start us, length us, event | category | flops | bytes accessed | tf_op | source)
XLA Modules:
  0.0 81.9 jit_solution(911462680447374466)
XLA Ops:
  0.0 1.2 %fusion.228 = (f32[16,2,512]{2,1,0:T(2,128)S(1)}, f32[16,2,512]{2,1,0:T(2,128)S(1)}) fusion(f32[16,32,512]{2,1,0:T(8,128)} %param.3), kind=kLoop, calls=%fused_computation.351 | loop fusion | bytes 262144 | tf_op jit(solution)/shard_map/slice | solution.py:48
  1.2 1.4 %fusion.227 = (f32[16,3,512]{2,1,0:T(4,128)S(1)}, f32[16,3,512]{2,1,0:T(4,128)S(1)}, f32[16,3,512]{2,1,0:T(4,128)S(1)}, f32[16,3,512]{2,1,0:T(4,128)S(1)}) fusion(f32[16,32,512]{2,1,0:T(8,128)} %param.4, f32[16,32,512]{2,1,0:T(8,128)} %param.5), kind=kLoop, calls=%fused_computation.350 | loop fusion | bytes 786432 | tf_op jit(solution)/shard_map/slice | solution.py:48
  2.6 0.1 pad_maximum_fusion.2
  2.7 3.5 %collective-permute-start = (f32[16,8,512]{2,1,0:T(8,128)S(1)}, f32[16,8,512]{2,1,0:T(8,128)S(1)}, u32[]{:S(2)}, u32[]{:S(2)}) collective-permute-start(f32[16,8,512]{2,1,0:T(8,128)S(1)} %pad_maximum_fusion.2), channel_id=1, source_target_pairs={{0,1},{1,2},{2,3},{3,4},{4,5},{5,6},{6,7},{8,9},{9,10},{10,11},{11... | collective-permute-start | bytes 786440 | tf_op jit(solution)/shard_map/ppermute | solution.py:58
  6.2 0.8 pad_maximum_fusion.3
  7.0 3.2 %collective-permute-start.1 = (f32[16,8,512]{2,1,0:T(8,128)}, f32[16,8,512]{2,1,0:T(8,128)S(1)}, u32[]{:S(2)}, u32[]{:S(2)}) collective-permute-start(f32[16,8,512]{2,1,0:T(8,128)} %pad_maximum_fusion.3), channel_id=1, source_target_pairs={{1,0},{2,1},{3,2},{4,3},{5,4},{6,5},{7,6},{9,8},{10,9},{11,10},{12... | collective-permute-start | bytes 786440 | tf_op jit(solution)/shard_map/ppermute | solution.py:58
  10.2 1.1 %fusion.224 = (f32[3,32,512]{2,1,0:T(8,128)S(1)}, f32[3,32,512]{2,1,0:T(8,128)S(1)}, f32[3,32,512]{2,1,0:T(8,128)S(1)}, f32[3,32,512]{2,1,0:T(8,128)S(1)}) fusion(f32[16,32,512]{2,1,0:T(8,128)S(1)} %copy-done, f32[16,32,512]{2,1,0:T(8,128)} %param.5), kind=kLoop, calls=%fused_computation.347 | loop fusion | bytes 1572864 | tf_op jit(solution)/shard_map/slice | solution.py:48
  11.4 0.9 %pad_maximum_fusion = f32[8,32,512]{2,1,0:T(8,128)} fusion(f32[3,32,512]{2,1,0:T(8,128)S(1)} %get-tuple-element.86, f32[2,32,512]{2,1,0:T(8,128)S(1)} %get-tuple-element.41, f32[3,32,512]{2,1,0:T(8,128)S(1)} %get-tuple-element.39), kind=kLoop, calls=%fused_computation.143 | loop fusion | flops 262144 | bytes 1048576 | tf_op jit(solution)/shard_map/concatenate | solution.py:55
  12.2 1.9 %collective-permute-start.3 = (f32[8,32,512]{2,1,0:T(8,128)}, f32[8,32,512]{2,1,0:T(8,128)}, u32[]{:S(2)}, u32[]{:S(2)}) collective-permute-start(f32[8,32,512]{2,1,0:T(8,128)} %pad_maximum_fusion), channel_id=1, source_target_pairs={{0,8},{8,16},{16,24},{24,32},{32,40},{40,48},{48,56},{56,64},{64,7... | collective-permute-start | bytes 1572872 | tf_op jit(solution)/shard_map/ppermute | solution.py:58
  14.1 0.8 %pad_maximum_fusion.1 = f32[8,32,512]{2,1,0:T(8,128)} fusion(f32[3,32,512]{2,1,0:T(8,128)S(1)} %get-tuple-element.85, f32[2,32,512]{2,1,0:T(8,128)S(1)} %get-tuple-element.42, f32[3,32,512]{2,1,0:T(8,128)S(1)} %get-tuple-element.40), kind=kLoop, calls=%fused_computation.144 | loop fusion | flops 262144 | bytes 1048576 | tf_op jit(solution)/shard_map/concatenate | solution.py:55
  15.0 5.1 %collective-permute-start.5 = (f32[8,32,512]{2,1,0:T(8,128)}, f32[8,32,512]{2,1,0:T(8,128)}, u32[]{:S(2)}, u32[]{:S(2)}) collective-permute-start(f32[8,32,512]{2,1,0:T(8,128)} %pad_maximum_fusion.1), channel_id=1, source_target_pairs={{8,0},{16,8},{24,16},{32,24},{40,32},{48,40},{56,48},{64,56},{72,6... | collective-permute-start | bytes 1572872 | tf_op jit(solution)/shard_map/ppermute | solution.py:58
  20.3 0.5 fusion.201
  20.8 0.1 fusion.44
  21.0 1.9 %collective-permute-start.2 = (f32[3,16,512]{2,1,0:T(8,128)S(1)}, f32[3,16,512]{2,1,0:T(8,128)S(1)}, u32[]{:S(2)}, u32[]{:S(2)}) collective-permute-start(f32[3,16,512]{2,1,0:T(8,128)S(1)} %pad_maximum_fusion.4), channel_id=1, source_target_pairs={{0,8},{8,16},{16,24},{24,32},{32,40},{40,48},{48,56},{56,64},{64,7... | collective-permute-start | bytes 294920 | tf_op jit(solution)/shard_map/ppermute | solution.py:58
  23.0 5.1 %collective-permute-start.4 = (f32[3,16,512]{2,1,0:T(8,128)S(1)}, f32[3,16,512]{2,1,0:T(8,128)S(1)}, u32[]{:S(2)}, u32[]{:S(2)}) collective-permute-start(f32[3,16,512]{2,1,0:T(8,128)S(1)} %pad_maximum_fusion.5), channel_id=1, source_target_pairs={{8,0},{16,8},{24,16},{32,24},{40,32},{48,40},{56,48},{64,56},{72,6... | collective-permute-start | bytes 294920 | tf_op jit(solution)/shard_map/ppermute | solution.py:58
  28.3 2.8 %collective-permute-done.2 = f32[3,16,512]{2,1,0:T(8,128)S(1)} collective-permute-done((f32[3,16,512]{2,1,0:T(8,128)S(1)}, f32[3,16,512]{2,1,0:T(8,128)S(1)}, u32[]{:S(2)}, u32[]{:S(2)}) %collective-permute-start.2) | collective-permute-done | bytes 98336 | tf_op jit(solution)/shard_map/ppermute | solution.py:58
  31.2 1.2 %fusion.230 = (f32[3,32,512]{2,1,0:T(8,128)S(1)}, f32[3,32,512]{2,1,0:T(8,128)S(1)}, f32[3,32,512]{2,1,0:T(8,128)S(1)}) fusion(f32[8,32,512]{2,1,0:T(8,128)} %collective-permute-done.3), kind=kLoop, calls=%fused_computation.353 | loop fusion | bytes 1179648 | tf_op jit(solution)/shard_map/slice | solution.py:74
  32.4 1.2 %fusion.231 = (f32[3,32,512]{2,1,0:T(8,128)S(1)}, f32[3,32,512]{2,1,0:T(8,128)S(1)}, f32[3,32,512]{2,1,0:T(8,128)S(1)}) fusion(f32[8,32,512]{2,1,0:T(8,128)} %collective-permute-done.5), kind=kLoop, calls=%fused_computation.354 | loop fusion | bytes 1179648 | tf_op jit(solution)/shard_map/slice | solution.py:76
  33.5 0.3 maximum_maximum_fusion.2
  33.9 0.3 maximum_maximum_fusion.1
  34.1 0.3 maximum_maximum_fusion
  34.4 2.1 %divide_select_fusion.2 = (f32[22,38,512]{2,1,0:T(8,128)S(1)}, f32[22,38,512]{2,1,0:T(8,128)S(1)}, f32[22,38,512]{2,1,0:T(8,128)S(1)}) fusion(f32[22,38,512]{2,1,0:T(8,128)S(1)} %maximum_maximum_fusion.1), kind=kLoop, calls=%fused_computation.17 | loop fusion | flops 8560640 | bytes 6848512 | tf_op jit(solution)/shard_map/jit(_where)/select_n | solution.py:208
  36.6 4.1 %and_select_fusion.1 = (f32[22,38,512]{2,1,0:T(8,128)S(1)}, f32[22,38,512]{2,1,0:T(8,128)S(1)}) fusion(f32[22,38,512]{2,1,0:T(8,128)S(1)} %maximum_maximum_fusion.2, f32[22,38,512]{2,1,0:T(8,128)S(1)} %get-tuple-element.37, f32[22,38,512]{2,1,0:T(8,128)S(1)} %get-tuple-element.38, f32[22,38,512]{2,1,0:T(8,128)S(1)} %get-tuple-element.36, ...), kind=kLoop, calls=%fused_computation.19 | loop fusion | flops 12412928 | bytes 13697596 | tf_op jit(solution)/shard_map/jit(_where)/select_n | solution.py:252
  40.7 3.8 %and_select_fusion = f32[22,38,512]{2,1,0:T(8,128)S(1)} fusion(f32[22,38,512]{2,1,0:T(8,128)S(1)} %get-tuple-element.32, f32[22,38,512]{2,1,0:T(8,128)S(1)} %get-tuple-element.33, f32[22,38,512]{2,1,0:T(8,128)S(1)} %get-tuple-element.37, f32[22,38,512]{2,1,0:T(8,128)S(1)} %get-tuple-element.38, f32[22,38,512]{2,1,0:T(8,128)S(1)} %get-tuple-element.36, ...), kind=kLoop, calls=%fused_computation.18 | loop fusion | flops 11984896 | bytes 11984956 | tf_op jit(solution)/shard_map/jit(_where)/select_n | solution.py:252
  44.5 0.4 fusion.223
  44.9 1.8 %fusion.46 = f32[16,32,512]{2,1,0:T(8,128)S(1)} fusion(f32[16,32,512]{2,1,0:T(8,128)S(1)} %copy-done.1, f32[22,38,512]{2,1,0:T(8,128)S(1)} %get-tuple-element.33, f32[22,38,512]{2,1,0:T(8,128)S(1)} %get-tuple-element.37, f32[22,38,512]{2,1,0:T(8,128)S(1)} %and_select_fusion, f32[22,38,512]{2,1,0:T(8,128)S(1)} %get-tuple-element.38, ...), kind=kLoop, calls=%fused_computation.125 | loop fusion | flops 4718592 | bytes 15724544 | tf_op jit(solution)/shard_map/sub | solution.py:263
  46.8 0.5 fusion.199
  47.3 0.1 fusion.43
  47.5 1.8 %collective-permute-start.6 = (f32[2,4,8,128]{3,2,1,0:T(8,128)S(1)}, f32[2,4,8,128]{3,2,1,0:T(8,128)S(1)}, u32[]{:S(2)}, u32[]{:S(2)}) collective-permute-start(f32[2,4,8,128]{3,2,1,0:T(8,128)S(1)} %pad_maximum_fusion.6), channel_id=1, source_target_pairs={{0,8},{8,0},{16,24},{24,16},{32,40},{40,32},{48,56},{56,48},{64,72... | collective-permute-start | bytes 98312 | tf_op jit(solution)/shard_map/ppermute | solution.py:144
  49.3 0.9 %collective-permute-done.6 = f32[2,4,8,128]{3,2,1,0:T(8,128)S(1)} collective-permute-done((f32[2,4,8,128]{3,2,1,0:T(8,128)S(1)}, f32[2,4,8,128]{3,2,1,0:T(8,128)S(1)}, u32[]{:S(2)}, u32[]{:S(2)}) %collective-permute-start.6) | collective-permute-done | bytes 32800 | tf_op jit(solution)/shard_map/ppermute | solution.py:144
  50.2 7.7 %collective-permute-start.7 = (f32[2,8,8,128]{3,2,1,0:T(8,128)S(1)}, f32[2,8,8,128]{3,2,1,0:T(8,128)S(1)}, u32[]{:S(2)}, u32[]{:S(2)}) collective-permute-start(f32[2,8,8,128]{3,2,1,0:T(8,128)S(1)} %maximum_select_fusion), channel_id=1, source_target_pairs={{0,16},{8,24},{16,32},{24,40},{32,48},{40,56},{48,64},{56,72},{64,... | collective-permute-start | bytes 196616 | tf_op jit(solution)/shard_map/ppermute | solution.py:147
  57.9 1.9 %collective-permute-start.8 = (f32[2,8,8,128]{3,2,1,0:T(8,128)S(1)}, f32[2,8,8,128]{3,2,1,0:T(8,128)S(1)}, u32[]{:S(2)}, u32[]{:S(2)}) collective-permute-start(f32[2,8,8,128]{3,2,1,0:T(8,128)S(1)} %maximum_select_fusion), channel_id=1, source_target_pairs={{16,0},{24,8},{32,16},{40,24},{48,32},{56,40},{64,48},{72,56},{80,... | collective-permute-start | bytes 196616 | tf_op jit(solution)/shard_map/ppermute | solution.py:148
  59.9 6.6 %collective-permute-done.8 = f32[2,8,8,128]{3,2,1,0:T(8,128)S(1)} collective-permute-done((f32[2,8,8,128]{3,2,1,0:T(8,128)S(1)}, f32[2,8,8,128]{3,2,1,0:T(8,128)S(1)}, u32[]{:S(2)}, u32[]{:S(2)}) %collective-permute-start.8) | collective-permute-done | bytes 65568 | tf_op jit(solution)/shard_map/ppermute | solution.py:148
  66.6 2.8 %collective-permute-start.10 = (f32[2,18,8,128]{3,2,1,0:T(8,128)S(1)}, f32[2,18,8,128]{3,2,1,0:T(8,128)S(1)}, u32[]{:S(2)}, u32[]{:S(2)}) collective-permute-start(f32[2,18,8,128]{3,2,1,0:T(8,128)S(1)} %slice.548), channel_id=1, source_target_pairs={{1,0},{2,1},{3,2},{4,3},{5,4},{6,5},{7,6},{9,8},{10,9},{11,10},{12... | collective-permute-start | bytes 442376 | tf_op jit(solution)/shard_map/ppermute | solution.py:26
  69.4 3.2 %collective-permute-start.9 = (f32[2,18,8,128]{3,2,1,0:T(8,128)S(1)}, f32[2,18,8,128]{3,2,1,0:T(8,128)S(1)}, u32[]{:S(2)}, u32[]{:S(2)}) collective-permute-start(f32[2,18,8,128]{3,2,1,0:T(8,128)S(1)} %slice.548), channel_id=1, source_target_pairs={{0,1},{1,2},{2,3},{3,4},{4,5},{5,6},{6,7},{8,9},{9,10},{10,11},{11... | collective-permute-start | bytes 442376 | tf_op jit(solution)/shard_map/ppermute | solution.py:25
  72.6 2.6 %collective-permute-done.10 = f32[2,18,8,128]{3,2,1,0:T(8,128)S(1)} collective-permute-done((f32[2,18,8,128]{3,2,1,0:T(8,128)S(1)}, f32[2,18,8,128]{3,2,1,0:T(8,128)S(1)}, u32[]{:S(2)}, u32[]{:S(2)}) %collective-permute-start.10) | collective-permute-done | bytes 147488 | tf_op jit(solution)/shard_map/ppermute | solution.py:26
  75.2 2.2 %collective-permute-done.9 = f32[2,18,8,128]{3,2,1,0:T(8,128)S(1)} collective-permute-done((f32[2,18,8,128]{3,2,1,0:T(8,128)S(1)}, f32[2,18,8,128]{3,2,1,0:T(8,128)S(1)}, u32[]{:S(2)}, u32[]{:S(2)}) %collective-permute-start.9) | collective-permute-done | bytes 147488 | tf_op jit(solution)/shard_map/ppermute | solution.py:25
  77.4 0.5 fusion.182
  77.9 0.3 fusion.183
  78.3 0.3 multiply_add_fusion.4
  78.5 0.3 multiply_add_fusion.3
  78.8 0.3 multiply_add_fusion.2
  79.1 0.3 multiply_add_fusion.1
  79.4 0.3 multiply_add_fusion
  79.7 0.2 fusion.169
  79.9 0.5 fusion.188
  80.4 0.3 convolution_bitcast_fusion
  80.7 1.2 %bitcast_add_fusion = f32[16,32,512]{2,1,0:T(8,128)} fusion(f32[22,38,512]{2,1,0:T(8,128)S(1)} %and_select_fusion, f32[4,32,512]{2,1,0:T(8,128)S(1)} %convolution_bitcast_fusion), kind=kLoop, calls=%fused_computation.139 | loop fusion | flops 262144 | bytes 2359296 | tf_op jit(solution)/shard_map/add | solution.py:268
  (40 shorter events, 0.6 us)
Async XLA Ops:
  0.0 10.2 %copy-start = (f32[16,32,512]{2,1,0:T(8,128)S(1)}, f32[16,32,512]{2,1,0:T(8,128)}, u32[]{:S(2)}) copy-start(f32[16,32,512]{2,1,0:T(8,128)} %param.4) | copy-start | bytes 3145732
  1.2 10.2 %copy-start.1 = (f32[16,32,512]{2,1,0:T(8,128)S(1)}, f32[16,32,512]{2,1,0:T(8,128)}, u32[]{:S(2)}) copy-start(f32[16,32,512]{2,1,0:T(8,128)} %param.3) | copy-start | bytes 3145732
  2.7 18.3 %collective-permute-start = (f32[16,8,512]{2,1,0:T(8,128)S(1)}, f32[16,8,512]{2,1,0:T(8,128)S(1)}, u32[]{:S(2)}, u32[]{:S(2)}) collective-permute-start(f32[16,8,512]{2,1,0:T(8,128)S(1)} %pad_maximum_fusion.2), channel_id=1, source_target_pairs={{0,1},{1,2},{2,3},{3,4},{4,5},{5,6},{6,7},{8,9},{9,10},{10,11},{11... | collective-permute-start | bytes 786440 | tf_op jit(solution)/shard_map/ppermute | solution.py:58
  7.0 14.0 %collective-permute-start.1 = (f32[16,8,512]{2,1,0:T(8,128)}, f32[16,8,512]{2,1,0:T(8,128)S(1)}, u32[]{:S(2)}, u32[]{:S(2)}) collective-permute-start(f32[16,8,512]{2,1,0:T(8,128)} %pad_maximum_fusion.3), channel_id=1, source_target_pairs={{1,0},{2,1},{3,2},{4,3},{5,4},{6,5},{7,6},{9,8},{10,9},{11,10},{12... | collective-permute-start | bytes 786440 | tf_op jit(solution)/shard_map/ppermute | solution.py:58
  12.2 19.0 %collective-permute-start.3 = (f32[8,32,512]{2,1,0:T(8,128)}, f32[8,32,512]{2,1,0:T(8,128)}, u32[]{:S(2)}, u32[]{:S(2)}) collective-permute-start(f32[8,32,512]{2,1,0:T(8,128)} %pad_maximum_fusion), channel_id=1, source_target_pairs={{0,8},{8,16},{16,24},{24,32},{32,40},{40,48},{48,56},{56,64},{64,7... | collective-permute-start | bytes 1572872 | tf_op jit(solution)/shard_map/ppermute | solution.py:58
  15.0 17.4 %collective-permute-start.5 = (f32[8,32,512]{2,1,0:T(8,128)}, f32[8,32,512]{2,1,0:T(8,128)}, u32[]{:S(2)}, u32[]{:S(2)}) collective-permute-start(f32[8,32,512]{2,1,0:T(8,128)} %pad_maximum_fusion.1), channel_id=1, source_target_pairs={{8,0},{16,8},{24,16},{32,24},{40,32},{48,40},{56,48},{64,56},{72,6... | collective-permute-start | bytes 1572872 | tf_op jit(solution)/shard_map/ppermute | solution.py:58
  21.0 10.1 %collective-permute-start.2 = (f32[3,16,512]{2,1,0:T(8,128)S(1)}, f32[3,16,512]{2,1,0:T(8,128)S(1)}, u32[]{:S(2)}, u32[]{:S(2)}) collective-permute-start(f32[3,16,512]{2,1,0:T(8,128)S(1)} %pad_maximum_fusion.4), channel_id=1, source_target_pairs={{0,8},{8,16},{16,24},{24,32},{32,40},{40,48},{48,56},{56,64},{64,7... | collective-permute-start | bytes 294920 | tf_op jit(solution)/shard_map/ppermute | solution.py:58
  23.0 8.1 %collective-permute-start.4 = (f32[3,16,512]{2,1,0:T(8,128)S(1)}, f32[3,16,512]{2,1,0:T(8,128)S(1)}, u32[]{:S(2)}, u32[]{:S(2)}) collective-permute-start(f32[3,16,512]{2,1,0:T(8,128)S(1)} %pad_maximum_fusion.5), channel_id=1, source_target_pairs={{8,0},{16,8},{24,16},{32,24},{40,32},{48,40},{56,48},{64,56},{72,6... | collective-permute-start | bytes 294920 | tf_op jit(solution)/shard_map/ppermute | solution.py:58
  28.2 5.3 %copy-start.2 = (f32[16,32,512]{2,1,0:T(8,128)S(1)}, f32[16,32,512]{2,1,0:T(8,128)}, u32[]{:S(2)}) copy-start(f32[16,32,512]{2,1,0:T(8,128)} %param.5) | copy-start | bytes 3145732
  47.5 2.7 %collective-permute-start.6 = (f32[2,4,8,128]{3,2,1,0:T(8,128)S(1)}, f32[2,4,8,128]{3,2,1,0:T(8,128)S(1)}, u32[]{:S(2)}, u32[]{:S(2)}) collective-permute-start(f32[2,4,8,128]{3,2,1,0:T(8,128)S(1)} %pad_maximum_fusion.6), channel_id=1, source_target_pairs={{0,8},{8,0},{16,24},{24,16},{32,40},{40,32},{48,56},{56,48},{64,72... | collective-permute-start | bytes 98312 | tf_op jit(solution)/shard_map/ppermute | solution.py:144
  50.2 9.7 %collective-permute-start.7 = (f32[2,8,8,128]{3,2,1,0:T(8,128)S(1)}, f32[2,8,8,128]{3,2,1,0:T(8,128)S(1)}, u32[]{:S(2)}, u32[]{:S(2)}) collective-permute-start(f32[2,8,8,128]{3,2,1,0:T(8,128)S(1)} %maximum_select_fusion), channel_id=1, source_target_pairs={{0,16},{8,24},{16,32},{24,40},{32,48},{40,56},{48,64},{56,72},{64,... | collective-permute-start | bytes 196616 | tf_op jit(solution)/shard_map/ppermute | solution.py:147
  57.9 8.6 %collective-permute-start.8 = (f32[2,8,8,128]{3,2,1,0:T(8,128)S(1)}, f32[2,8,8,128]{3,2,1,0:T(8,128)S(1)}, u32[]{:S(2)}, u32[]{:S(2)}) collective-permute-start(f32[2,8,8,128]{3,2,1,0:T(8,128)S(1)} %maximum_select_fusion), channel_id=1, source_target_pairs={{16,0},{24,8},{32,16},{40,24},{48,32},{56,40},{64,48},{72,56},{80,... | collective-permute-start | bytes 196616 | tf_op jit(solution)/shard_map/ppermute | solution.py:148
  66.6 8.6 %collective-permute-start.10 = (f32[2,18,8,128]{3,2,1,0:T(8,128)S(1)}, f32[2,18,8,128]{3,2,1,0:T(8,128)S(1)}, u32[]{:S(2)}, u32[]{:S(2)}) collective-permute-start(f32[2,18,8,128]{3,2,1,0:T(8,128)S(1)} %slice.548), channel_id=1, source_target_pairs={{1,0},{2,1},{3,2},{4,3},{5,4},{6,5},{7,6},{9,8},{10,9},{11,10},{12... | collective-permute-start | bytes 442376 | tf_op jit(solution)/shard_map/ppermute | solution.py:26
  69.4 7.9 %collective-permute-start.9 = (f32[2,18,8,128]{3,2,1,0:T(8,128)S(1)}, f32[2,18,8,128]{3,2,1,0:T(8,128)S(1)}, u32[]{:S(2)}, u32[]{:S(2)}) collective-permute-start(f32[2,18,8,128]{3,2,1,0:T(8,128)S(1)} %slice.548), channel_id=1, source_target_pairs={{0,1},{1,2},{2,3},{3,4},{4,5},{5,6},{6,7},{8,9},{9,10},{10,11},{11... | collective-permute-start | bytes 442376 | tf_op jit(solution)/shard_map/ppermute | solution.py:25
